TPU v7x, 32 devices: a whole 2x2x4 slice. The times are simulated.
32 devices in a mesh: blk: 8 (over z, core), grp: 4 (over y, x).
Axes of the slice: x: 2, y: 2, z: 4, core: 2. Of those that a mesh axis runs over, the one named last changes fastest.
Arguments:
- block_values: bfloat16 [1536, 16, 64, 64], P('blk', 'grp'), may hold values from -1.5 to 1.5
- block_columns: int32 [1536, 16], P('blk', 'grp'), may hold values from 0 to 1535, as said below
- row_counts: int32 [1536], P('blk'), may hold values from 6 to 16
- prolong_blocks: bfloat16 [1536, 64, 64], P(('blk', 'grp')), may hold values from -0.75 to 0.75
- aggregates: int32 [1536], P(('blk', 'grp')), may hold values from 0 to 31, as said below
Outputs:
- coarse_blocks: float32 [32, 32, 64, 64], P('grp', 'blk')
Inputs may be any that keep to these rules, and one draw needn't show every extreme that they name: `aggregates`: the aggregate of a fine block row of panel p, rows p * 192 to (p + 1) * 192 - 1, lies in p * 4 to (p + 1) * 4 - 1. `block_columns`: A block column of a row of panel p lies in a panel p + d modulo the number of panels, for some d of -2 to 2; slot 0 of each row holds the row itself.
All inputs are finite; a program needn't handle non-finite values.
Results may differ from a plain program's by a relative error of at most 0.0029.
Values may be sent and summed in bfloat16 or wider, within the bound.
No kernel may reach another device: no remote copies, remote signals or barrier semaphores. Data moves between devices by JAX's collectives and lax.ppermute only.
A program may use at most 192 MiB of HBM per device.

v0:
```python
import jax
import jax.numpy as jnp
from jax import lax
from jax.sharding import PartitionSpec as P

CB = 4


def passed_along(block, axis, distance):
    devices = range(lax.axis_size(axis))
    route = [((i - distance) % len(devices), i) for i in devices]
    return lax.ppermute(block, axis, route)


def local(block_values, block_columns, row_counts, prolong_blocks, aggregates):
    panel_length = row_counts.shape[0]
    slots_here = block_values.shape[1]
    slot_total = panel_length * slots_here
    block_size = block_values.shape[2]
    group_size = lax.axis_size("grp")
    panel_total = lax.axis_size("blk")
    coarse_count = CB * panel_total
    panel_blocks, panel_aggs = (
        lax.all_gather(prolong_blocks, "grp", axis=0, tiled=True),
        lax.all_gather(aggregates, "grp", axis=0, tiled=True),
    )
    lower = []
    upper = []
    going_down = (panel_blocks, panel_aggs)
    going_up = (panel_blocks, panel_aggs)
    for hop in range(2):
        going_down = passed_along((going_down[0], going_down[1]), "blk", 1)
        lower.insert(0, going_down)
        going_up = passed_along((going_up[0], going_up[1]), "blk", -1)
        upper.append(going_up)
    pieces = lower + [(panel_blocks, panel_aggs)] + upper
    window_blocks = jnp.concatenate([piece[0] for piece in pieces], axis=0)
    window_aggs = jnp.concatenate([piece[1] for piece in pieces], axis=0)
    own_blocks = window_blocks[2 * panel_length : 3 * panel_length]
    own_aggs = window_aggs[2 * panel_length : 3 * panel_length]
    wanted = block_columns.reshape(slot_total)
    column_panel = wanted // panel_length
    distance = jnp.mod(column_panel - lax.axis_index("blk") + 2, panel_total)
    local_rows = distance * panel_length + wanted % panel_length
    fetched = jnp.take(window_blocks, local_rows, axis=0)
    fetched_aggs = jnp.take(window_aggs, local_rows, axis=0)
    prolong_picked = fetched.reshape(panel_length, slots_here, block_size, block_size)
    product = jnp.einsum(
        "rkab,rkbc->rkac", block_values, prolong_picked, preferred_element_type=jnp.float32
    )
    slot_ids = lax.axis_index("grp") * slots_here + jnp.arange(slots_here, dtype=jnp.int32)
    live = slot_ids[None, :] < row_counts[:, None]
    product = jnp.where(live[:, :, None, None], product, 0.0).astype(jnp.bfloat16)
    restricted = jnp.einsum(
        "rba,rkbc->rkac", own_blocks, product, preferred_element_type=jnp.float32
    ).reshape(slot_total, block_size, block_size)
    local_coarse = own_aggs - lax.axis_index("blk") * CB
    target = fetched_aggs * CB + jnp.broadcast_to(
        local_coarse[:, None], (panel_length, slots_here)
    ).reshape(slot_total)
    share = coarse_count // group_size
    wanted_targets = jnp.arange(share * lax.axis_size("grp") * CB, dtype=jnp.int32)
    selector = (wanted_targets[:, None] == target[None, :]).astype(jnp.float32)
    summed = jnp.einsum(
        "ts,sab->tab",
        selector,
        restricted,
        precision=lax.Precision.HIGHEST,
        preferred_element_type=jnp.float32,
    )
    return lax.psum_scatter(
        summed.reshape(share * lax.axis_size("grp"), CB, block_size, block_size),
        "grp",
        scatter_dimension=0,
        tiled=True,
    )


def solution(mesh):
    return jax.shard_map(
        local,
        mesh=mesh,
        in_specs=(
            P("blk", "grp", None, None),
            P("blk", "grp"),
            P("blk"),
            P(("blk", "grp"), None, None),
            P(("blk", "grp")),
        ),
        out_specs=P("grp", "blk", None, None),
        check_vma=False,
    )
```

profile of v0, /device:TPU:26, one launch (start us, length us, event | category | flops | bytes accessed | tf_op | source)
XLA Modules:
  0.0 357.0 jit_solution(9059910426823162043)
XLA Ops:
  6.5 0.0 all-gather.2.cloned.1.call-start
  6.5 0.7 all-gather.2.cloned.1.call-update
  7.3 0.0 reduce-scatter.2.cloned.1.call-start
  7.3 46.7 %all-gather.2.cloned.1.call-done = bf16[192,64,64]{2,1,0:T(8,128)(2,1)} async-done(((bf16[48,64,64]{2,1,0:T(8,128)(2,1)}), bf16[192,64,64]{2,1,0:T(8,128)(2,1)}) %all-gather.2.cloned.1.call-update) | async-done | bytes 1572880 | tf_op jit(solution)/shard_map/all_gather | solution.py:24
  54.0 4.2 %copy.25 = bf16[192,64,64]{0,2,1:T(8,128)(2,1)S(1)} copy(bf16[192,64,64]{2,1,0:T(8,128)(2,1)} %all-gather.2.cloned.1.call-done) | data formatting | bytes 3145728 | tf_op jit(solution)/shard_map/all_gather | solution.py:24
  58.2 0.1 collective-permute-start.4
  58.3 1.7 collective-permute-start.6
  60.0 1.2 dynamic-slice
  61.9 0.9 dynamic-update-slice
  62.8 6.4 %all-reduce = s32[192]{0:T(256)S(1)} all-reduce(s32[192]{0:T(256)S(1)} %dynamic-update-slice), channel_id=1, replica_groups=mesh['blk'=8,'grp'=4] {'grp'}, use_global_device_ids=true, to_apply=%add | all-reduce | flops 192 | bytes 1536
  69.2 0.0 collective-permute-start
  69.2 1.7 collective-permute-start.2
  71.0 32.8 %collective-permute-done.4 = bf16[192,64,64]{0,2,1:T(8,128)(2,1)} collective-permute-done((bf16[192,64,64]{0,2,1:T(8,128)(2,1)S(1)}, bf16[192,64,64]{0,2,1:T(8,128)(2,1)}, u32[]{:S(2)}, u32[]{:S(2)}) %collective-permute-start.4) | collective-permute-done | bytes 1572896 | tf_op jit(solution)/shard_map/ppermute | solution.py:12
  103.7 0.0 collective-permute-start.5
  103.7 0.7 compare_and_fusion
  104.4 0.7 broadcast_divide_fusion
  105.1 0.0 collective-permute-done.6
  105.1 1.8 collective-permute-start.7
  106.9 0.2 copy.18
  107.1 0.1 ne.125
  107.2 0.1 copy.20
  107.4 0.1 div.28
  107.5 0.1 copy.19
  107.6 0.1 rem.106
  107.8 0.8 broadcast_compare_fusion
  108.6 0.0 collective-permute-done
  108.6 1.5 collective-permute-start.1
  110.1 0.0 collective-permute-done.2
  110.1 0.3 collective-permute-start.3
  110.4 0.1 ne.121
  110.5 0.1 div.27
  110.6 0.1 rem.96
  110.7 0.1 broadcast_in_dim.40
  110.8 0.1 reshape.243
  110.9 0.2 copy.24
  111.1 17.1 %copy.32 = bf16[192,4,64,64]{3,2,1,0:T(8,128)(2,1)} copy(bf16[192,4,64,64]{0,3,2,1:T(8,128)(2,1)} %param.5) | data formatting | bytes 12582912 | tf_op args[0]
  128.1 17.1 %collective-permute-done.1 = s32[192]{0:T(256)S(1)} collective-permute-done((s32[192]{0:T(256)S(1)}, s32[192]{0:T(256)S(1)}, u32[]{:S(2)}, u32[]{:S(2)}) %collective-permute-start.1) | collective-permute-done | bytes 800 | tf_op jit(solution)/shard_map/ppermute | solution.py:12
  145.3 7.3 %collective-permute-done.3 = s32[192]{0:T(256)S(1)} collective-permute-done((s32[192]{0:T(256)S(1)}, s32[192]{0:T(256)S(1)}, u32[]{:S(2)}, u32[]{:S(2)}) %collective-permute-start.3) | collective-permute-done | bytes 800 | tf_op jit(solution)/shard_map/ppermute | solution.py:12
  152.6 0.1 concatenate.6
  152.7 3.2 gather_fusion
  155.9 5.3 %copy.28 = bf16[192,64,64]{2,1,0:T(8,128)(2,1)} copy(bf16[192,64,64]{0,2,1:T(8,128)(2,1)} %collective-permute-done.4) | data formatting | bytes 3145728 | tf_op jit(solution)/shard_map/ppermute | solution.py:12
  161.2 0.0 copy-start
  161.2 5.3 %copy.29 = bf16[192,64,64]{2,1,0:T(8,128)(2,1)} copy(bf16[192,64,64]{0,2,1:T(8,128)(2,1)} %collective-permute-done.6) | data formatting | bytes 3145728 | tf_op jit(solution)/shard_map/ppermute | solution.py:12
  166.5 0.0 collective-permute-done.5
  166.5 5.2 %copy.27 = bf16[192,64,64]{2,1,0:T(8,128)(2,1)} copy(bf16[192,64,64]{0,2,1:T(8,128)(2,1)} %collective-permute-done.5) | data formatting | bytes 3145728 | tf_op jit(solution)/shard_map/ppermute | solution.py:12
  171.6 0.0 copy-start.1
  171.6 4.4 %constant_dynamic-update-slice_fusion.4 = bf16[960,64,64]{2,1,0:T(8,128)(2,1)} fusion(bf16[192,64,64]{2,1,0:T(8,128)(2,1)} %copy.27), kind=kLoop, calls=%fused_computation.31 | loop fusion | bytes 4718592
  176.0 4.3 %constant_dynamic-update-slice_fusion.3 = bf16[960,64,64]{2,1,0:T(8,128)(2,1)} fusion(bf16[960,64,64]{2,1,0:T(8,128)(2,1)} %constant_dynamic-update-slice_fusion.4, bf16[192,64,64]{2,1,0:T(8,128)(2,1)} %copy.28), kind=kLoop, calls=%fused_computation.30 | loop fusion | bytes 6291456
  180.3 0.0 copy-done
  180.3 2.4 constant_dynamic-update-slice_fusion.2
  182.7 0.0 copy-done.1
  182.7 2.4 constant_dynamic-update-slice_fusion.1
  185.0 0.0 collective-permute-done.7
  185.0 5.3 %copy.30 = bf16[192,64,64]{2,1,0:T(8,128)(2,1)} copy(bf16[192,64,64]{0,2,1:T(8,128)(2,1)} %collective-permute-done.7) | data formatting | bytes 3145728 | tf_op jit(solution)/shard_map/ppermute | solution.py:12
  190.3 4.2 %constant_dynamic-update-slice_fusion = bf16[960,64,64]{2,1,0:T(8,128)(2,1)} fusion(bf16[960,64,64]{2,1,0:T(8,128)(2,1)} %constant_dynamic-update-slice_fusion.1, bf16[192,64,64]{2,1,0:T(8,128)(2,1)} %copy.30), kind=kLoop, calls=%fused_computation.27 | loop fusion | bytes 6291456 | tf_op jit(solution)/shard_map/concatenate | solution.py:37
  194.5 25.3 %gather_fusion.1 = bf16[768,64,64]{2,1,0:T(8,128)(2,1)} fusion(bf16[960,64,64]{2,1,0:T(8,128)(2,1)} %constant_dynamic-update-slice_fusion, s32[1024]{0:T(1024)S(1)} %pad_clamp_fusion), kind=kCustom, calls=%fused_computation.1 | custom fusion | bytes 12585984 | tf_op jit(solution)/shard_map/jit(_take)/gather | solution.py:45
  219.8 16.6 %copy.31 = bf16[192,4,64,64]{2,3,1,0:T(8,128)(2,1)} copy(bf16[192,4,64,64]{3,2,1,0:T(8,128)(2,1)} %bitcast.23) | data formatting | bytes 12582912 | tf_op jit(solution)/shard_map/jit(_take)/gather | solution.py:45
  236.4 22.3 %fusion.1 = f32[192,4,64,64]{3,2,1,0:T(8,128)} fusion(pred[192,4]{1,0:T(8,128)(4,1)S(1)} %broadcast_compare_fusion, bf16[192,4,64,64]{3,2,1,0:T(8,128)(2,1)} %copy.32, bf16[192,4,64,64]{2,3,1,0:T(8,128)(2,1)} %copy.31, pred[192,4]{1,0:T(8,128)(4,1)S(1)} %copy.24, bf16[192,64,64]{2,1,0:T(8,128)(2,1)S(1)} %copy-done), kind=kOutput, calls=%fused_computation.4 | convolution fusion | flops 814743552 | bytes 26740224 | tf_op jit(solution)/shard_map/rba,rkbc->rkac/dot_general | solution.py:54
  258.8 22.3 %copy.33 = f32[768,64,64]{0,2,1:T(8,128)} copy(f32[768,64,64]{1,2,0:T(8,128)} %bitcast.22) | data formatting | bytes 25165824 | tf_op jit(solution)/shard_map/reshape | solution.py:56
  281.1 13.4 %fusion.3 = f32[32,4,64,64]{3,0,2,1:T(8,128)} fusion(f32[768,64,64]{0,2,1:T(8,128)} %copy.33, s32[768]{0:T(1024)S(1)} %multiply_add_fusion, s32[32,4]{0,1:T(4,128)S(1)} %multiply_add_fusion.1), kind=kOutput, calls=%fused_computation.5 | convolution fusion | flops 4831936512 | bytes 14683648 | tf_op jit(solution)/shard_map/ts,sab->tab/dot_general | solution.py:64
  294.5 0.0 reduce-scatter.2.cloned.1.call-update
  294.5 53.2 %reduce-scatter.2.cloned.1.call-done = f32[8,4,64,64]{3,0,2,1:T(8,128)} async-done(((f32[32,4,64,64]{3,0,2,1:T(8,128)}), f32[8,4,64,64]{3,0,2,1:T(8,128)}) %reduce-scatter.2.cloned.1.call-update) | async-done | bytes 524304 | tf_op jit(solution)/shard_map/reduce_scatter | solution.py:71
  347.7 2.4 copy.34
  (7 shorter events, 0.1 us)
Async XLA Ops:
  6.5 47.5 %all-gather.2.cloned.1.call-start = ((), (), s32[]{:S(2)}) async-start(), calls=%async_computation.1 | async-start | bytes 3932160 | tf_op jit(solution)/shard_map/all_gather | solution.py:24
  7.3 340.5 %reduce-scatter.2.cloned.1.call-start = ((), (), s32[]{:S(2)}) async-start(), calls=%async_computation.2 | async-start | bytes 5242880 | tf_op jit(solution)/shard_map/reduce_scatter | solution.py:71
  58.2 45.5 %collective-permute-start.4 = (bf16[192,64,64]{0,2,1:T(8,128)(2,1)S(1)}, bf16[192,64,64]{0,2,1:T(8,128)(2,1)}, u32[]{:S(2)}, u32[]{:S(2)}) collective-permute-start(bf16[192,64,64]{0,2,1:T(8,128)(2,1)S(1)} %copy.25), channel_id=1, source_target_pairs={{28,0},{0,4},{4,8},{8,12},{12,16},{16,20},{20,24},{24,28},{29,1},{... | collective-permute-start | bytes 4718600 | tf_op jit(solution)/shard_map/ppermute | solution.py:12
  58.3 46.8 %collective-permute-start.6 = (bf16[192,64,64]{0,2,1:T(8,128)(2,1)S(1)}, bf16[192,64,64]{0,2,1:T(8,128)(2,1)}, u32[]{:S(2)}, u32[]{:S(2)}) collective-permute-start(bf16[192,64,64]{0,2,1:T(8,128)(2,1)S(1)} %copy.25), channel_id=1, source_target_pairs={{4,0},{8,4},{12,8},{16,12},{20,16},{24,20},{28,24},{0,28},{5,1},{9... | collective-permute-start | bytes 4718600 | tf_op jit(solution)/shard_map/ppermute | solution.py:12
  69.2 39.4 %collective-permute-start = (s32[192]{0:T(256)S(1)}, s32[192]{0:T(256)S(1)}, u32[]{:S(2)}, u32[]{:S(2)}) collective-permute-start(s32[192]{0:T(256)S(1)} %all-reduce), channel_id=1, source_target_pairs={{28,0},{0,4},{4,8},{8,12},{12,16},{16,20},{20,24},{24,28},{29,1},{... | collective-permute-start | bytes 2312 | tf_op jit(solution)/shard_map/ppermute | solution.py:12
  69.2 40.9 %collective-permute-start.2 = (s32[192]{0:T(256)S(1)}, s32[192]{0:T(256)S(1)}, u32[]{:S(2)}, u32[]{:S(2)}) collective-permute-start(s32[192]{0:T(256)S(1)} %all-reduce), channel_id=1, source_target_pairs={{4,0},{8,4},{12,8},{16,12},{20,16},{24,20},{28,24},{0,28},{5,1},{9... | collective-permute-start | bytes 2312 | tf_op jit(solution)/shard_map/ppermute | solution.py:12
  103.7 62.8 %collective-permute-start.5 = (bf16[192,64,64]{0,2,1:T(8,128)(2,1)}, bf16[192,64,64]{0,2,1:T(8,128)(2,1)}, u32[]{:S(2)}, u32[]{:S(2)}) collective-permute-start(bf16[192,64,64]{0,2,1:T(8,128)(2,1)} %collective-permute-done.4), channel_id=1, source_target_pairs={{28,0},{0,4},{4,8},{8,12},{12,16},{16,20},{20,24},{24,28},{29,1},{... | collective-permute-start | bytes 4718600 | tf_op jit(solution)/shard_map/ppermute | solution.py:12
  105.1 79.9 %collective-permute-start.7 = (bf16[192,64,64]{0,2,1:T(8,128)(2,1)}, bf16[192,64,64]{0,2,1:T(8,128)(2,1)}, u32[]{:S(2)}, u32[]{:S(2)}) collective-permute-start(bf16[192,64,64]{0,2,1:T(8,128)(2,1)} %collective-permute-done.6), channel_id=1, source_target_pairs={{4,0},{8,4},{12,8},{16,12},{20,16},{24,20},{28,24},{0,28},{5,1},{9... | collective-permute-start | bytes 4718600 | tf_op jit(solution)/shard_map/ppermute | solution.py:12
  108.6 36.7 %collective-permute-start.1 = (s32[192]{0:T(256)S(1)}, s32[192]{0:T(256)S(1)}, u32[]{:S(2)}, u32[]{:S(2)}) collective-permute-start(s32[192]{0:T(256)S(1)} %collective-permute-done), channel_id=1, source_target_pairs={{28,0},{0,4},{4,8},{8,12},{12,16},{16,20},{20,24},{24,28},{29,1},{... | collective-permute-start | bytes 2312 | tf_op jit(solution)/shard_map/ppermute | solution.py:12
  110.1 42.5 %collective-permute-start.3 = (s32[192]{0:T(256)S(1)}, s32[192]{0:T(256)S(1)}, u32[]{:S(2)}, u32[]{:S(2)}) collective-permute-start(s32[192]{0:T(256)S(1)} %collective-permute-done.2), channel_id=1, source_target_pairs={{4,0},{8,4},{12,8},{16,12},{20,16},{24,20},{28,24},{0,28},{5,1},{9... | collective-permute-start | bytes 2312 | tf_op jit(solution)/shard_map/ppermute | solution.py:12
  161.2 19.1 %copy-start = (bf16[192,64,64]{2,1,0:T(8,128)(2,1)S(1)}, bf16[192,64,64]{2,1,0:T(8,128)(2,1)}, u32[]{:S(2)}) copy-start(bf16[192,64,64]{2,1,0:T(8,128)(2,1)} %all-gather.2.cloned.1.call-done) | copy-start | bytes 4718596
  171.6 11.0 %copy-start.1 = (bf16[192,64,64]{2,1,0:T(8,128)(2,1)S(1)}, bf16[192,64,64]{2,1,0:T(8,128)(2,1)}, u32[]{:S(2)}) copy-start(bf16[192,64,64]{2,1,0:T(8,128)(2,1)} %copy.29) | copy-start | bytes 4718596
Sparse Core Ops, SparseCore 0:
  9.2 44.7 all-gather.1
  294.6 53.0 reduce-scatter.1
where the time goes:
time: 361 us; the launch traced here: 357 us
  waiting for transfers between devices  158 us (44%)
  local copies, waits for them, and re-layouts  133 us (37%)
  matrix products  35.7 us (10%)
  between operations  14.2 us (4%)
  starting transfers between devices  7.17 us (2%)
  blocking collectives  6.41 us (2%)
    ppermute x8, waiting for transfers between devices, passed_along(): return lax.ppermute(block, axis, route)  57.2 us
    reduce_scatter x1, waiting for transfers between devices, local(): lax.psum_scatter(summed.reshape(share * lax.axis_size('grp'), CB, block_s...  53.2 us
    all_gather x1, waiting for transfers between devices, local(): lax.all_gather(prolong_blocks, 'grp', axis=0, tiled=True)  46.7 us
    gather x2, local copies, waits for them, and re-layouts, local(): fetched = jnp.take(window_blocks, local_rows, axis=0)  41.9 us
    unnamed x12, local copies, waits for them, and re-layouts  32.5 us
    dot_general x1, matrix products, local(): jnp.einsum('rba,rkbc->rkac', own_blocks, product, preferred_element_type=...  22.3 us
    reshape x1, local copies, waits for them, and re-layouts, local(): restricted = jnp.einsum('rba,rkbc->rkac', own_blocks, product, preferred_...  22.3 us
    ppermute x4, local copies, waits for them, and re-layouts, passed_along(): return lax.ppermute(block, axis, route)  21 us
  transfers between devices with their start and end apart: 10, of which 5 were waited for; matrix products, arithmetic and copies ran while one was open for 15% of the time, Pallas kernels for 0%

commit v1 on v0

v1 whole, which is shorter than its diff:
```python
import functools

import jax
import jax.numpy as jnp
from jax import lax
from jax.experimental import pallas as pl
from jax.experimental.pallas import tpu as pltpu
from jax.sharding import PartitionSpec as P

CB = 4
ROWS_PER_STEP = 16


def passed_along(block, axis, distance):
    devices = range(lax.axis_size(axis))
    route = [((i - distance) % len(devices), i) for i in devices]
    return lax.ppermute(block, axis, route)


def coarse_kernel(rows_ref, target_ref, live_ref, values_ref, own_t_ref, *rest):
    pieces = rest[:5]
    acc_ref, window, sems = rest[5:]
    step = pl.program_id(0)
    rows_here, slots, bs, _ = values_ref.shape
    panel_length = pieces[0].shape[0]

    @pl.when(step == 0)
    def _():
        copies = []
        for k, piece in enumerate(pieces):
            cp = pltpu.make_async_copy(
                piece, window.at[pl.ds(k * panel_length, panel_length)], sems.at[k]
            )
            cp.start()
            copies.append(cp)
        for cp in copies:
            cp.wait()
        acc_ref[...] = jnp.zeros_like(acc_ref)

    def row_body(r, carry):
        row = step * rows_here + r
        own_t = own_t_ref[row]
        for s in range(slots):
            n = row * slots + s
            picked = window[rows_ref[n]]
            product = jnp.dot(
                values_ref[r, s], picked, preferred_element_type=jnp.float32
            )
            product = jnp.where(live_ref[n] > 0, product, 0.0).astype(jnp.bfloat16)
            restricted = jnp.dot(own_t, product, preferred_element_type=jnp.float32)
            t = target_ref[n]
            acc_ref[t] = acc_ref[t] + restricted
        return carry

    lax.fori_loop(0, rows_here, row_body, 0)


def coarse_partial(rows, target, live, values, own_t, pieces, n_targets):
    panel_length, slots, bs, _ = values.shape
    rows_per_step = min(ROWS_PER_STEP, panel_length)
    grid = (panel_length // rows_per_step,)
    window_rows = 5 * pieces[0].shape[0]
    return pl.pallas_call(
        coarse_kernel,
        out_shape=jax.ShapeDtypeStruct((n_targets, bs, bs), jnp.float32),
        grid_spec=pltpu.PrefetchScalarGridSpec(
            num_scalar_prefetch=3,
            grid=grid,
            in_specs=[
                pl.BlockSpec((rows_per_step, slots, bs, bs), lambda i, *_: (i, 0, 0, 0)),
                pl.BlockSpec(memory_space=pltpu.VMEM),
            ]
            + [pl.BlockSpec(memory_space=pl.ANY)] * 5,
            out_specs=pl.BlockSpec((n_targets, bs, bs), lambda i, *_: (0, 0, 0)),
            scratch_shapes=[
                pltpu.VMEM((window_rows, bs, bs), jnp.bfloat16),
                pltpu.SemaphoreType.DMA((5,)),
            ],
        ),
        compiler_params=pltpu.CompilerParams(
            dimension_semantics=("arbitrary",),
            vmem_limit_bytes=56 * 1024 * 1024,
        ),
    )(rows, target, live, values, own_t, *pieces)


def local(block_values, block_columns, row_counts, prolong_blocks, aggregates):
    panel_length = row_counts.shape[0]
    slots_here = block_values.shape[1]
    slot_total = panel_length * slots_here
    block_size = block_values.shape[2]
    group_size = lax.axis_size("grp")
    panel_total = lax.axis_size("blk")
    coarse_count = CB * panel_total
    me = lax.axis_index("blk")
    panel_blocks, panel_aggs = (
        lax.all_gather(prolong_blocks, "grp", axis=0, tiled=True),
        lax.all_gather(aggregates, "grp", axis=0, tiled=True),
    )
    lower = []
    upper = []
    going_down = (panel_blocks, panel_aggs)
    going_up = (panel_blocks, panel_aggs)
    for hop in range(2):
        going_down = passed_along((going_down[0], going_down[1]), "blk", 1)
        lower.insert(0, going_down)
        going_up = passed_along((going_up[0], going_up[1]), "blk", -1)
        upper.append(going_up)
    pieces = lower + [(panel_blocks, panel_aggs)] + upper
    window_aggs = jnp.concatenate([piece[1] for piece in pieces], axis=0)
    wanted = block_columns.reshape(slot_total)
    column_panel = wanted // panel_length
    distance = jnp.mod(column_panel - me + 2, panel_total)
    local_rows = distance * panel_length + wanted % panel_length
    fetched_aggs = jnp.take(window_aggs, local_rows, axis=0)
    slot_ids = lax.axis_index("grp") * slots_here + jnp.arange(slots_here, dtype=jnp.int32)
    live = (slot_ids[None, :] < row_counts[:, None]).astype(jnp.int32).reshape(slot_total)
    local_coarse = panel_aggs - me * CB
    target = fetched_aggs * CB + jnp.broadcast_to(
        local_coarse[:, None], (panel_length, slots_here)
    ).reshape(slot_total)
    own_t = jnp.swapaxes(panel_blocks, 1, 2)
    summed = coarse_partial(
        local_rows.astype(jnp.int32),
        target.astype(jnp.int32),
        live,
        block_values,
        own_t,
        [piece[0] for piece in pieces],
        coarse_count * CB,
    )
    return lax.psum_scatter(
        summed.reshape(coarse_count, CB, block_size, block_size),
        "grp",
        scatter_dimension=0,
        tiled=True,
    )


def solution(mesh):
    return jax.shard_map(
        local,
        mesh=mesh,
        in_specs=(
            P("blk", "grp", None, None),
            P("blk", "grp"),
            P("blk"),
            P(("blk", "grp"), None, None),
            P(("blk", "grp")),
        ),
        out_specs=P("grp", "blk", None, None),
        check_vma=False,
    )
```

time: 361 us -> 330 us (0.914)
  local copies, waits for them, and re-layouts: 133 us -> 51.1 us
  Pallas kernels: 0 us -> 66.1 us
  matrix products: 35.7 us -> 0 us
  waiting for transfers between devices: 158 us -> 177 us
  starting transfers between devices: 7.17 us -> 12.3 us
    pallas_call x0 -> x1, Pallas kernels: none -> 66.1 us  [coarse_partial(): pl.pallas_call(coarse_kernel, out_shape=jax.ShapeDtypeStruct((n_targets,...]
    gather x2 -> x0, local copies, waits for them, and re-layouts: 41.9 us -> none  [local(): fetched = jnp.take(window_blocks, local_rows, axis=0)]
    dot_general x2 -> x0, matrix products: 35.7 us -> none  [the longest x1 22.3 us: local(): jnp.einsum('rba,rkbc->rkac', own_blocks, product, preferred_element_type=...]
    reshape x1 -> x0, local copies, waits for them, and re-layouts: 22.3 us -> none  [local(): restricted = jnp.einsum('rba,rkbc->rkac', own_blocks, product, preferred_...]
    ppermute x8, waiting for transfers between devices: 57.2 us -> 73.5 us  [passed_along(): return lax.ppermute(block, axis, route)]
    unnamed x12 -> x14, local copies, waits for them, and re-layouts: 32.5 us -> 17.9 us
    ppermute x8, starting transfers between devices: 7.13 us -> 12.2 us  [passed_along(): return lax.ppermute(block, axis, route)]
    concatenate x1 -> x0, local copies, waits for them, and re-layouts: 4.21 us -> none  [local(): window_blocks = jnp.concatenate([piece[0] for piece in pieces], axis=0)]
  transfers between devices with their start and end apart: 10 -> 10, of which waited for: 5 -> 6; matrix products, arithmetic and copies ran while one was open for 15% -> 13% of each run, Pallas kernels for 0% -> 0%
where the time goes in v1:
time: 330 us; the launch traced here: 328 us
  waiting for transfers between devices  177 us (54%)
  Pallas kernels  66.1 us (20%)
  local copies, waits for them, and re-layouts  51.1 us (15%)
  between operations  14.2 us (4%)
  starting transfers between devices  12.3 us (4%)
  blocking collectives  6.41 us (2%)
    ppermute x8, waiting for transfers between devices, passed_along(): return lax.ppermute(block, axis, route)  73.5 us
    pallas_call x1, Pallas kernels, coarse_partial(): pl.pallas_call(coarse_kernel, out_shape=jax.ShapeDtypeStruct((n_targets,...  66.1 us
    reduce_scatter x1, waiting for transfers between devices, local(): lax.psum_scatter(summed.reshape(coarse_count, CB, block_size, block_size)...  55.9 us
    all_gather x1, waiting for transfers between devices, local(): lax.all_gather(prolong_blocks, 'grp', axis=0, tiled=True)  46.7 us
    ppermute x4, local copies, waits for them, and re-layouts, passed_along(): return lax.ppermute(block, axis, route)  21 us
    unnamed x14, local copies, waits for them, and re-layouts  17.9 us
    ppermute x8, starting transfers between devices, passed_along(): return lax.ppermute(block, axis, route)  12.2 us
    all_gather x2, local copies, waits for them, and re-layouts, local(): lax.all_gather(prolong_blocks, 'grp', axis=0, tiled=True)  7.02 us
  transfers between devices with their start and end apart: 10, of which 6 were waited for; matrix products, arithmetic and copies ran while one was open for 13% of the time, Pallas kernels for 0%

profile of v1, /device:TPU:26, one launch (start us, length us, event | category | flops | bytes accessed | tf_op | source)
XLA Modules:
  0.0 327.8 jit_solution(9538361694804617098)
XLA Ops:
  6.5 0.0 copy-start.4
  6.5 0.0 copy-start.3
  6.5 0.0 copy-start.1
  6.5 0.0 copy-start.2
  6.5 0.0 all-gather.2.cloned.1.call-start
  6.6 0.7 all-gather.2.cloned.1.call-update
  7.3 0.0 reduce-scatter.2.cloned.1.call-start
  7.3 46.7 %all-gather.2.cloned.1.call-done.rest_2_ = bf16[192,64,64]{2,1,0:T(8,128)(2,1)} async-done(((bf16[48,64,64]{2,1,0:T(8,128)(2,1)}), bf16[192,64,64]{2,1,0:T(8,128)(2,1)}) %all-gather.2.cloned.1.call-update) | async-done | bytes 1572880 | tf_op jit(solution)/shard_map/all_gather | solution.py:97
  54.0 4.2 %copy.23 = bf16[192,64,64]{0,2,1:T(8,128)(2,1)S(1)} copy(bf16[192,64,64]{2,1,0:T(8,128)(2,1)} %all-gather.2.cloned.1.call-done.rest_2_) | data formatting | bytes 3145728 | tf_op jit(solution)/shard_map/all_gather | solution.py:97
  58.3 0.1 collective-permute-start.6
  58.3 0.5 collective-permute-start.4
  58.8 43.0 %collective-permute-done.6 = bf16[192,64,64]{0,2,1:T(8,128)(2,1)} collective-permute-done((bf16[192,64,64]{0,2,1:T(8,128)(2,1)S(1)}, bf16[192,64,64]{0,2,1:T(8,128)(2,1)}, u32[]{:S(2)}, u32[]{:S(2)}) %collective-permute-start.6) | collective-permute-done | bytes 1572896 | tf_op jit(solution)/shard_map/ppermute | solution.py:17
  101.8 2.3 collective-permute-start.7
  104.1 0.7 collective-permute-done.4
  104.8 1.4 collective-permute-start.5
  106.2 0.0 copy-done.4
  106.2 0.6 dynamic-slice
  107.5 0.0 copy-done.3
  107.5 0.2 dynamic-update-slice
  107.7 6.4 %all-reduce = s32[192]{0:T(256)S(1)} all-reduce(s32[192]{0:T(256)S(1)} %dynamic-update-slice), channel_id=1, replica_groups=mesh['blk'=8,'grp'=4] {'grp'}, use_global_device_ids=true, to_apply=%add | all-reduce | flops 192 | bytes 1536
  114.2 0.0 collective-permute-start.2
  114.2 2.4 collective-permute-start
  116.5 0.0 copy-done.1
  116.5 0.2 copy.16
  116.7 0.1 ne.93
  116.8 0.1 copy.18
  117.0 0.1 div.23
  117.1 0.1 copy.17
  117.2 0.1 rem.83
  117.3 0.0 copy-done.2
  117.4 0.1 compare_convert_fusion
  117.5 28.0 %collective-permute-done.2 = s32[192]{0:T(256)S(1)} collective-permute-done((s32[192]{0:T(256)S(1)}, s32[192]{0:T(256)S(1)}, u32[]{:S(2)}, u32[]{:S(2)}) %collective-permute-start.2) | collective-permute-done | bytes 800 | tf_op jit(solution)/shard_map/ppermute | solution.py:17
  145.5 2.2 collective-permute-start.3
  147.7 1.9 collective-permute-done
  149.6 3.3 %collective-permute-start.1 = (s32[192]{0:T(256)S(1)}, s32[192]{0:T(256)S(1)}, u32[]{:S(2)}, u32[]{:S(2)}) collective-permute-start(s32[192]{0:T(256)S(1)} %collective-permute-done), channel_id=1, source_target_pairs={{28,0},{0,4},{4,8},{8,12},{12,16},{16,20},{20,24},{24,28},{29,1},{... | collective-permute-start | bytes 2312 | tf_op jit(solution)/shard_map/ppermute | solution.py:17
  152.9 0.1 ne.89
  153.0 0.1 div.22
  153.1 0.1 rem.73
  153.2 0.1 broadcast_in_dim.9
  153.3 0.1 reshape.148
  153.4 0.7 reshape.150.live_ref
  154.1 17.0 %copy.25.values_ref = bf16[192,4,64,64]{3,2,1,0:T(8,128)(2,1)} copy(bf16[192,4,64,64]{0,3,2,1:T(8,128)(2,1)} %param.5) | data formatting | bytes 12582912 | tf_op args[0]
  171.1 0.0 copy-start
  171.1 0.0 collective-permute-done.3
  171.2 0.0 collective-permute-done.1
  171.2 0.1 concatenate.3
  171.2 3.2 gather_fusion
  174.4 0.6 multiply_add_fusion
  175.0 0.0 copy-done
  175.0 2.8 copy.22
  177.8 5.2 %copy.27.rest_1_ = bf16[192,64,64]{2,1,0:T(8,128)(2,1)} copy(bf16[192,64,64]{0,2,1:T(8,128)(2,1)} %collective-permute-done.4) | data formatting | bytes 3145728 | tf_op jit(solution)/shard_map/ppermute | solution.py:17
  183.1 5.2 %copy.28.rest_3_ = bf16[192,64,64]{2,1,0:T(8,128)(2,1)} copy(bf16[192,64,64]{0,2,1:T(8,128)(2,1)} %collective-permute-done.6) | data formatting | bytes 3145728 | tf_op jit(solution)/shard_map/ppermute | solution.py:17
  188.3 0.0 collective-permute-done.7
  188.3 5.3 %copy.29.rest_4_ = bf16[192,64,64]{2,1,0:T(8,128)(2,1)} copy(bf16[192,64,64]{0,2,1:T(8,128)(2,1)} %collective-permute-done.7) | data formatting | bytes 3145728 | tf_op jit(solution)/shard_map/ppermute | solution.py:17
  193.6 0.0 collective-permute-done.5
  193.6 5.2 %copy.26.rest_0_ = bf16[192,64,64]{2,1,0:T(8,128)(2,1)} copy(bf16[192,64,64]{0,2,1:T(8,128)(2,1)} %collective-permute-done.5) | data formatting | bytes 3145728 | tf_op jit(solution)/shard_map/ppermute | solution.py:17
  198.8 66.1 %shard_map.55 = f32[128,64,64]{2,1,0:T(8,128)} custom-call(s32[768]{0:T(1024)} %get-tuple-element.6.rows_ref, s32[768]{0:T(1024)} %get-tuple-element.5.target_ref, s32[768]{0:T(1024)} %reshape.150.live_ref, bf16[192,4,64,64]{3,2,1,0:T(8,128)(2,1)} %copy.25.values_ref, bf16[192,64,64]{2,1,0:T(8,128)(2,1)} %bitcast.4, bf16[192,64,64]{2,1,0:T(8,128)(2,1)} %copy.26.rest_0_, ...), custom_call_target="tpu_custom_call" | custom-call | tf_op jit(solution)/shard_map/pallas_call | solution.py:63
  265.0 0.0 reduce-scatter.2.cloned.1.call-update
  265.0 55.9 %reduce-scatter.2.cloned.1.call-done = f32[8,4,64,64]{3,2,1,0:T(8,128)} async-done(((f32[32,4,64,64]{3,2,1,0:T(8,128)}), f32[8,4,64,64]{3,2,1,0:T(8,128)}) %reduce-scatter.2.cloned.1.call-update) | async-done | bytes 524304 | tf_op jit(solution)/shard_map/reduce_scatter | solution.py:132
  (7 shorter events, 0.1 us)
Async XLA Ops:
  6.5 99.7 %copy-start.4 = (u32[32]{0:T(128)S(1)}, u32[32]{0:T(128)}, u32[]{:S(2)}) copy-start(u32[32]{0:T(128)} %constant.67) | copy-start | bytes 388
  6.5 101.0 %copy-start.3 = (s32[48]{0:T(128)S(1)}, s32[48]{0:T(128)}, u32[]{:S(2)}) copy-start(s32[48]{0:T(128)} %param.9) | copy-start | bytes 580
  6.5 110.0 %copy-start.1 = (s32[192,4]{0,1:T(4,128)S(1)}, s32[192,4]{0,1:T(4,128)}, u32[]{:S(2)}) copy-start(s32[192,4]{0,1:T(4,128)} %param.6) | copy-start | bytes 9220
  6.5 110.8 %copy-start.2 = (s32[192]{0:T(256)S(1)}, s32[192]{0:T(256)}, u32[]{:S(2)}) copy-start(s32[192]{0:T(256)} %param.7) | copy-start | bytes 2308
  6.5 47.5 %all-gather.2.cloned.1.call-start = ((), (), s32[]{:S(2)}) async-start(), calls=%async_computation.1 | async-start | bytes 3932160 | tf_op jit(solution)/shard_map/all_gather | solution.py:97
  7.3 313.6 %reduce-scatter.2.cloned.1.call-start = ((), (), s32[]{:S(2)}) async-start(), calls=%async_computation.2 | async-start | bytes 5242880 | tf_op jit(solution)/shard_map/reduce_scatter | solution.py:132
  58.3 43.6 %collective-permute-start.6 = (bf16[192,64,64]{0,2,1:T(8,128)(2,1)S(1)}, bf16[192,64,64]{0,2,1:T(8,128)(2,1)}, u32[]{:S(2)}, u32[]{:S(2)}) collective-permute-start(bf16[192,64,64]{0,2,1:T(8,128)(2,1)S(1)} %copy.23), channel_id=1, source_target_pairs={{4,0},{8,4},{12,8},{16,12},{20,16},{24,20},{28,24},{0,28},{5,1},{9... | collective-permute-start | bytes 4718600 | tf_op jit(solution)/shard_map/ppermute | solution.py:17
  58.3 46.5 %collective-permute-start.4 = (bf16[192,64,64]{0,2,1:T(8,128)(2,1)S(1)}, bf16[192,64,64]{0,2,1:T(8,128)(2,1)}, u32[]{:S(2)}, u32[]{:S(2)}) collective-permute-start(bf16[192,64,64]{0,2,1:T(8,128)(2,1)S(1)} %copy.23), channel_id=1, source_target_pairs={{28,0},{0,4},{4,8},{8,12},{12,16},{16,20},{20,24},{24,28},{29,1},{... | collective-permute-start | bytes 4718600 | tf_op jit(solution)/shard_map/ppermute | solution.py:17
  101.8 86.5 %collective-permute-start.7 = (bf16[192,64,64]{0,2,1:T(8,128)(2,1)}, bf16[192,64,64]{0,2,1:T(8,128)(2,1)}, u32[]{:S(2)}, u32[]{:S(2)}) collective-permute-start(bf16[192,64,64]{0,2,1:T(8,128)(2,1)} %collective-permute-done.6), channel_id=1, source_target_pairs={{4,0},{8,4},{12,8},{16,12},{20,16},{24,20},{28,24},{0,28},{5,1},{9... | collective-permute-start | bytes 4718600 | tf_op jit(solution)/shard_map/ppermute | solution.py:17
  104.8 88.8 %collective-permute-start.5 = (bf16[192,64,64]{0,2,1:T(8,128)(2,1)}, bf16[192,64,64]{0,2,1:T(8,128)(2,1)}, u32[]{:S(2)}, u32[]{:S(2)}) collective-permute-start(bf16[192,64,64]{0,2,1:T(8,128)(2,1)} %collective-permute-done.4), channel_id=1, source_target_pairs={{28,0},{0,4},{4,8},{8,12},{12,16},{16,20},{20,24},{24,28},{29,1},{... | collective-permute-start | bytes 4718600 | tf_op jit(solution)/shard_map/ppermute | solution.py:17
  114.2 31.3 %collective-permute-start.2 = (s32[192]{0:T(256)S(1)}, s32[192]{0:T(256)S(1)}, u32[]{:S(2)}, u32[]{:S(2)}) collective-permute-start(s32[192]{0:T(256)S(1)} %all-reduce), channel_id=1, source_target_pairs={{4,0},{8,4},{12,8},{16,12},{20,16},{24,20},{28,24},{0,28},{5,1},{9... | collective-permute-start | bytes 2312 | tf_op jit(solution)/shard_map/ppermute | solution.py:17
  114.2 35.4 %collective-permute-start = (s32[192]{0:T(256)S(1)}, s32[192]{0:T(256)S(1)}, u32[]{:S(2)}, u32[]{:S(2)}) collective-permute-start(s32[192]{0:T(256)S(1)} %all-reduce), channel_id=1, source_target_pairs={{28,0},{0,4},{4,8},{8,12},{12,16},{16,20},{20,24},{24,28},{29,1},{... | collective-permute-start | bytes 2312 | tf_op jit(solution)/shard_map/ppermute | solution.py:17
  145.5 25.6 %collective-permute-start.3 = (s32[192]{0:T(256)S(1)}, s32[192]{0:T(256)S(1)}, u32[]{:S(2)}, u32[]{:S(2)}) collective-permute-start(s32[192]{0:T(256)S(1)} %collective-permute-done.2), channel_id=1, source_target_pairs={{4,0},{8,4},{12,8},{16,12},{20,16},{24,20},{28,24},{0,28},{5,1},{9... | collective-permute-start | bytes 2312 | tf_op jit(solution)/shard_map/ppermute | solution.py:17
  149.6 21.6 %collective-permute-start.1 = (s32[192]{0:T(256)S(1)}, s32[192]{0:T(256)S(1)}, u32[]{:S(2)}, u32[]{:S(2)}) collective-permute-start(s32[192]{0:T(256)S(1)} %collective-permute-done), channel_id=1, source_target_pairs={{28,0},{0,4},{4,8},{8,12},{12,16},{16,20},{20,24},{24,28},{29,1},{... | collective-permute-start | bytes 2312 | tf_op jit(solution)/shard_map/ppermute | solution.py:17
  171.1 3.9 %copy-start = (bf16[192,64,64]{2,1,0:T(8,128)(2,1)S(1)}, bf16[192,64,64]{2,1,0:T(8,128)(2,1)}, u32[]{:S(2)}) copy-start(bf16[192,64,64]{2,1,0:T(8,128)(2,1)} %all-gather.2.cloned.1.call-done.rest_2_) | copy-start | bytes 4718596
Sparse Core Ops, SparseCore 0:
  9.2 44.7 all-gather.1
  265.1 55.7 reduce-scatter.1

commit v2 on v1

--- a/solution.py
+++ b/solution.py
@@ -93,10 +93,23 @@
     panel_total = lax.axis_size("blk")
     coarse_count = CB * panel_total
     me = lax.axis_index("blk")
-    panel_blocks, panel_aggs = (
-        lax.all_gather(prolong_blocks, "grp", axis=0, tiled=True),
-        lax.all_gather(aggregates, "grp", axis=0, tiled=True),
-    )
+    group_me = lax.axis_index("grp")
+    received = [(prolong_blocks, aggregates)]
+    for k in range(1, group_size):
+        received.append(
+            lax.ppermute(
+                (prolong_blocks, aggregates),
+                "grp",
+                [(i, (i + k) % group_size) for i in range(group_size)],
+            )
+        )
+    order = jnp.mod(group_me - jnp.arange(group_size, dtype=jnp.int32), group_size)
+    panel_blocks = jnp.take(
+        jnp.stack([piece[0] for piece in received]), order, axis=0
+    ).reshape(panel_length, block_size, block_size)
+    panel_aggs = jnp.take(
+        jnp.stack([piece[1] for piece in received]), order, axis=0
+    ).reshape(panel_length)
     lower = []
     upper = []
     going_down = (panel_blocks, panel_aggs)
@@ -129,12 +142,15 @@
         [piece[0] for piece in pieces],
         coarse_count * CB,
     )
-    return lax.psum_scatter(
-        summed.reshape(coarse_count, CB, block_size, block_size),
-        "grp",
-        scatter_dimension=0,
-        tiled=True,
-    )
+    share = coarse_count // group_size
+    summed = summed.reshape(group_size, share, CB, block_size, block_size)
+    total = jnp.take(summed, group_me, axis=0)
+    for k in range(1, group_size):
+        outgoing = jnp.take(summed, jnp.mod(group_me + k, group_size), axis=0)
+        total = total + lax.ppermute(
+            outgoing, "grp", [(i, (i + k) % group_size) for i in range(group_size)]
+        )
+    return total
 
 
 def solution(mesh):

time: 330 us -> 316 us (0.958)
  between operations: 14.2 us -> 0.31 us
  waiting for transfers between devices: 177 us -> 165 us
  other arithmetic: 0.79 us -> 11.4 us
  blocking collectives: 6.41 us -> 0 us
  starting transfers between devices: 12.3 us -> 15.7 us
    ppermute x0 -> x9, waiting for transfers between devices: none -> 78.6 us  [the longest x3 44.8 us: local(): lax.ppermute(outgoing, 'grp', [(i, (i + k) % group_size) for i in range(g...]
    reduce_scatter x1 -> x0, waiting for transfers between devices: 55.9 us -> none  [local(): lax.psum_scatter(summed.reshape(coarse_count, CB, block_size, block_size)...]
    all_gather x1 -> x0, waiting for transfers between devices: 46.7 us -> none  [local(): lax.all_gather(prolong_blocks, 'grp', axis=0, tiled=True)]
    ppermute x8, waiting for transfers between devices: 73.5 us -> 86.7 us  [passed_along(): return lax.ppermute(block, axis, route)]
    ppermute x0 -> x9, starting transfers between devices: none -> 8.68 us  [the longest x6 6.08 us: local(): lax.ppermute((prolong_blocks, aggregates), 'grp', [(i, (i + k) % group_si...]
    all_gather x2 -> x0, local copies, waits for them, and re-layouts: 7.02 us -> none  [local(): lax.all_gather(prolong_blocks, 'grp', axis=0, tiled=True)]
    unnamed x1 -> x0, blocking collectives: 6.41 us -> none
    ppermute x8, starting transfers between devices: 12.2 us -> 6.99 us  [passed_along(): return lax.ppermute(block, axis, route)]
  transfers between devices with their start and end apart: 10 -> 17, of which waited for: 6 -> 6; matrix products, arithmetic and copies ran while one was open for 13% -> 14% of each run, Pallas kernels for 0% -> 0%
where the time goes in v2:
time: 316 us; the launch traced here: 313 us
  waiting for transfers between devices  165 us (52%)
  Pallas kernels  66.1 us (21%)
  local copies, waits for them, and re-layouts  54.4 us (17%)
  starting transfers between devices  15.7 us (5%)
  other arithmetic  11.4 us (4%)
    ppermute x8, waiting for transfers between devices, passed_along(): return lax.ppermute(block, axis, route)  86.7 us
    pallas_call x1, Pallas kernels, coarse_partial(): pl.pallas_call(coarse_kernel, out_shape=jax.ShapeDtypeStruct((n_targets,...  66.1 us
    ppermute x3, waiting for transfers between devices, local(): lax.ppermute(outgoing, 'grp', [(i, (i + k) % group_size) for i in range(g...  44.8 us
    ppermute x6, waiting for transfers between devices, local(): lax.ppermute((prolong_blocks, aggregates), 'grp', [(i, (i + k) % group_si...  33.8 us
    ppermute x4, local copies, waits for them, and re-layouts, passed_along(): return lax.ppermute(block, axis, route)  20.9 us
    unnamed x15, local copies, waits for them, and re-layouts  18.2 us
    ppermute x8, starting transfers between devices, passed_along(): return lax.ppermute(block, axis, route)  6.99 us
  transfers between devices with their start and end apart: 17, of which 6 were waited for; matrix products, arithmetic and copies ran while one was open for 14% of the time, Pallas kernels for 0%

profile of v2, /device:TPU:26, one launch (start us, length us, event | category | flops | bytes accessed | tf_op | source)
XLA Modules:
  0.0 313.1 jit_solution(17771439289474301973)
XLA Ops:
  0.0 1.5 collective-permute-start.7
  1.5 0.5 collective-permute-start.8
  2.0 1.5 collective-permute-start.9
  3.6 0.1 broadcast_in_dim.45
  3.6 0.1 broadcast_in_dim.46
  3.8 16.9 %collective-permute-done.7 = bf16[48,64,64]{2,1,0:T(8,128)(2,1)S(1)} collective-permute-done((bf16[48,64,64]{2,1,0:T(8,128)(2,1)}, bf16[48,64,64]{2,1,0:T(8,128)(2,1)S(1)}, u32[]{:S(2)}, u32[]{:S(2)}) %collective-permute-start.7) | collective-permute-done | bytes 393248 | tf_op jit(solution)/shard_map/ppermute | solution.py:100
  20.6 16.9 %collective-permute-done.8 = bf16[48,64,64]{2,1,0:T(8,128)(2,1)S(1)} collective-permute-done((bf16[48,64,64]{2,1,0:T(8,128)(2,1)}, bf16[48,64,64]{2,1,0:T(8,128)(2,1)S(1)}, u32[]{:S(2)}, u32[]{:S(2)}) %collective-permute-start.8) | collective-permute-done | bytes 393248 | tf_op jit(solution)/shard_map/ppermute | solution.py:100
  37.6 0.9 copy-done.2
  38.4 0.3 copy-done.3
  38.7 2.3 pad_maximum_fusion
  41.0 2.6 gather_fusion.2
  43.5 2.3 bitcast_select_fusion.rest_2_
  45.8 0.0 copy-start.6
  45.8 0.0 copy-start.4
  45.9 0.0 copy-start.5
  45.9 3.8 %copy.22 = bf16[192,64,64]{0,2,1:T(8,128)(2,1)} copy(bf16[192,64,64]{2,1,0:T(8,128)(2,1)S(1)} %bitcast_select_fusion.rest_2_) | data formatting | bytes 3145728 | tf_op jit(solution)/shard_map/jit(_take)/select_n | solution.py:107
  49.7 1.7 collective-permute-start.12
  51.5 1.2 collective-permute-start
  52.6 0.5 collective-permute-start.1
  53.2 0.8 collective-permute-start.2
  54.0 44.0 %collective-permute-done.10 = bf16[192,64,64]{0,2,1:T(8,128)(2,1)} collective-permute-done((bf16[192,64,64]{0,2,1:T(8,128)(2,1)}, bf16[192,64,64]{0,2,1:T(8,128)(2,1)}, u32[]{:S(2)}, u32[]{:S(2)}) %collective-permute-start.10) | collective-permute-done | bytes 1572896 | tf_op jit(solution)/shard_map/ppermute | solution.py:17
  98.0 0.0 collective-permute-start.11
  98.0 0.0 collective-permute-done.12
  98.0 1.7 collective-permute-start.13
  99.7 0.1 copy.18
  99.8 0.1 div.23
  100.0 0.1 div.22
  100.1 0.1 copy.17
  100.2 0.1 rem.178
  100.3 0.1 rem.152
  100.4 0.2 copy.16
  100.6 0.1 ne.137
  100.7 0.1 ne.131
  101.0 0.1 compare_convert_fusion
  101.1 0.0 collective-permute-done.1
  101.1 0.0 collective-permute-done.2
  101.1 0.6 gather_fusion
  101.7 0.1 gather.20
  101.8 0.0 collective-permute-start.3
  101.8 1.7 collective-permute-start.5
  103.5 42.7 %collective-permute-done.3 = s32[192]{0:T(256)S(1)} collective-permute-done((s32[192]{0:T(256)S(1)}, s32[192]{0:T(256)S(1)}, u32[]{:S(2)}, u32[]{:S(2)}) %collective-permute-start.3) | collective-permute-done | bytes 800 | tf_op jit(solution)/shard_map/ppermute | solution.py:17
  146.2 1.7 collective-permute-start.6
  148.0 0.7 reshape.283.live_ref
  148.7 17.0 %copy.24.values_ref = bf16[192,4,64,64]{3,2,1,0:T(8,128)(2,1)} copy(bf16[192,4,64,64]{0,3,2,1:T(8,128)(2,1)} %param.7) | data formatting | bytes 12582912 | tf_op args[0]
  165.7 0.1 broadcast_in_dim.49
  165.8 0.1 reshape.218
  165.9 0.0 collective-permute-done.6
  165.9 0.1 concatenate.3
  166.0 3.2 %gather_fusion.1 = s32[768]{0:T(1024)S(1)} fusion(s32[960]{0:T(1024)S(1)} %concatenate.3, s32[1024]{0:T(1024)S(1)} %pad_clamp_fusion), kind=kCustom, calls=%fused_computation.1 | custom fusion | bytes 9216 | tf_op jit(solution)/shard_map/jit(_take)/gather | solution.py:128
  169.2 0.6 multiply_add_fusion
  169.8 2.8 copy.25.own_t_ref
  172.6 5.2 %copy.27.rest_1_ = bf16[192,64,64]{2,1,0:T(8,128)(2,1)} copy(bf16[192,64,64]{0,2,1:T(8,128)(2,1)} %collective-permute-done.10) | data formatting | bytes 3145728 | tf_op jit(solution)/shard_map/ppermute | solution.py:17
  177.8 5.2 %copy.28.rest_3_ = bf16[192,64,64]{2,1,0:T(8,128)(2,1)} copy(bf16[192,64,64]{0,2,1:T(8,128)(2,1)} %collective-permute-done.12) | data formatting | bytes 3145728 | tf_op jit(solution)/shard_map/ppermute | solution.py:17
  183.0 0.0 collective-permute-done.11
  183.0 5.3 %copy.26.rest_0_ = bf16[192,64,64]{2,1,0:T(8,128)(2,1)} copy(bf16[192,64,64]{0,2,1:T(8,128)(2,1)} %collective-permute-done.11) | data formatting | bytes 3145728 | tf_op jit(solution)/shard_map/ppermute | solution.py:17
  188.3 5.3 %copy.29.rest_4_ = bf16[192,64,64]{2,1,0:T(8,128)(2,1)} copy(bf16[192,64,64]{0,2,1:T(8,128)(2,1)} %collective-permute-done.13) | data formatting | bytes 3145728 | tf_op jit(solution)/shard_map/ppermute | solution.py:17
  193.5 66.1 %shard_map.55 = f32[128,64,64]{2,1,0:T(8,128)} custom-call(s32[768]{0:T(1024)} %get-tuple-element.18.rows_ref, s32[768]{0:T(1024)} %get-tuple-element.17.target_ref, s32[768]{0:T(1024)} %reshape.283.live_ref, bf16[192,4,64,64]{3,2,1,0:T(8,128)(2,1)} %copy.24.values_ref, bf16[192,64,64]{2,1,0:T(8,128)(2,1)} %copy.25.own_t_ref, ...), custom_call_target="tpu_custom_call" | custom-call | tf_op jit(solution)/shard_map/pallas_call | solution.py:63
  259.7 2.4 select_bitcast_fusion.2
  262.1 1.2 collective-permute-start.14
  263.3 0.5 collective-permute-start.15
  263.9 0.9 collective-permute-start.16
  264.7 23.6 %collective-permute-done.14 = f32[8,4,64,64]{3,2,1,0:T(8,128)} collective-permute-done((f32[8,4,64,64]{3,2,1,0:T(8,128)S(1)}, f32[8,4,64,64]{3,2,1,0:T(8,128)}, u32[]{:S(2)}, u32[]{:S(2)}) %collective-permute-start.14) | collective-permute-done | bytes 524320 | tf_op jit(solution)/shard_map/ppermute | solution.py:150
  288.3 21.2 %collective-permute-done.15 = f32[8,4,64,64]{3,2,1,0:T(8,128)} collective-permute-done((f32[8,4,64,64]{3,2,1,0:T(8,128)S(1)}, f32[8,4,64,64]{3,2,1,0:T(8,128)}, u32[]{:S(2)}, u32[]{:S(2)}) %collective-permute-start.15) | collective-permute-done | bytes 524320 | tf_op jit(solution)/shard_map/ppermute | solution.py:150
  309.5 3.6 %fusion.1 = f32[8,4,64,64]{3,2,1,0:T(8,128)} fusion(f32[8,4,64,64]{3,2,1,0:T(8,128)} %collective-permute-done.16, f32[8,4,64,64]{3,2,1,0:T(8,128)} %collective-permute-done.15, f32[8,4,64,64]{3,2,1,0:T(8,128)} %collective-permute-done.14, f32[4,8,4,64,64]{4,3,2,1,0:T(8,128)} %bitcast.28, s32[]{:T(128)S(6)} %select_n.165, pred[]{:T(512)S(6)} %and.129), kind=kLoop, calls=%fused_computation.7 | loop fusion | flops 524288 | bytes 2621445 | tf_op jit(solution)/shard_map/add | solution.py:150
  (27 shorter events, 0.2 us)
Async XLA Ops:
  0.0 20.6 %collective-permute-start.7 = (bf16[48,64,64]{2,1,0:T(8,128)(2,1)}, bf16[48,64,64]{2,1,0:T(8,128)(2,1)S(1)}, u32[]{:S(2)}, u32[]{:S(2)}) collective-permute-start(bf16[48,64,64]{2,1,0:T(8,128)(2,1)} %param.10), channel_id=1, source_target_pairs={{0,1},{1,2},{2,3},{3,0},{4,5},{5,6},{6,7},{7,4},{8,9},{9,10},{10,1... | collective-permute-start | bytes 1179656 | tf_op jit(solution)/shard_map/ppermute | solution.py:100
  1.5 36.1 %collective-permute-start.8 = (bf16[48,64,64]{2,1,0:T(8,128)(2,1)}, bf16[48,64,64]{2,1,0:T(8,128)(2,1)S(1)}, u32[]{:S(2)}, u32[]{:S(2)}) collective-permute-start(bf16[48,64,64]{2,1,0:T(8,128)(2,1)} %param.10), channel_id=1, source_target_pairs={{0,2},{1,3},{2,0},{3,1},{4,6},{5,7},{6,4},{7,5},{8,10},{9,11},{10,... | collective-permute-start | bytes 1179656 | tf_op jit(solution)/shard_map/ppermute | solution.py:100
  2.0 35.6 %collective-permute-start.9 = (bf16[48,64,64]{2,1,0:T(8,128)(2,1)}, bf16[48,64,64]{2,1,0:T(8,128)(2,1)S(1)}, u32[]{:S(2)}, u32[]{:S(2)}) collective-permute-start(bf16[48,64,64]{2,1,0:T(8,128)(2,1)} %param.10), channel_id=1, source_target_pairs={{0,3},{1,0},{2,1},{3,2},{4,7},{5,4},{6,5},{7,6},{8,11},{9,8},{10,9... | collective-permute-start | bytes 1179656 | tf_op jit(solution)/shard_map/ppermute | solution.py:100
  20.6 16.9 %copy-start.1 = (bf16[48,64,64]{2,1,0:T(8,128)(2,1)}, bf16[48,64,64]{2,1,0:T(8,128)(2,1)S(1)}, u32[]{:S(2)}) copy-start(bf16[48,64,64]{2,1,0:T(8,128)(2,1)S(1)} %collective-permute-done.7) | copy-start | bytes 1179652
  37.6 0.9 copy-start.2
  37.6 1.1 copy-start.3
  45.8 124.0 %copy-start = (bf16[192,64,64]{2,1,0:T(8,128)(2,1)}, bf16[192,64,64]{2,1,0:T(8,128)(2,1)S(1)}, u32[]{:S(2)}) copy-start(bf16[192,64,64]{2,1,0:T(8,128)(2,1)S(1)} %bitcast_select_fusion.rest_2_) | copy-start | bytes 4718596
  45.8 5.6 %copy-start.6 = (s32[48]{0:T(128)S(1)}, s32[48]{0:T(128)}, u32[]{:S(2)}) copy-start(s32[48]{0:T(128)} %param.11) | copy-start | bytes 580
  45.8 53.9 %copy-start.4 = (s32[192,4]{0,1:T(4,128)S(1)}, s32[192,4]{0,1:T(4,128)}, u32[]{:S(2)}) copy-start(s32[192,4]{0,1:T(4,128)} %param.8) | copy-start | bytes 9220
  45.9 55.1 %copy-start.5 = (s32[192]{0:T(256)S(1)}, s32[192]{0:T(256)}, u32[]{:S(2)}) copy-start(s32[192]{0:T(256)} %param.9) | copy-start | bytes 2308
  49.7 48.2 %collective-permute-start.10 = (bf16[192,64,64]{0,2,1:T(8,128)(2,1)}, bf16[192,64,64]{0,2,1:T(8,128)(2,1)}, u32[]{:S(2)}, u32[]{:S(2)}) collective-permute-start(bf16[192,64,64]{0,2,1:T(8,128)(2,1)} %copy.22), channel_id=1, source_target_pairs={{28,0},{0,4},{4,8},{8,12},{12,16},{16,20},{20,24},{24,28},{29,1},{... | collective-permute-start | bytes 4718600 | tf_op jit(solution)/shard_map/ppermute | solution.py:17
  49.7 48.2 %collective-permute-start.12 = (bf16[192,64,64]{0,2,1:T(8,128)(2,1)}, bf16[192,64,64]{0,2,1:T(8,128)(2,1)}, u32[]{:S(2)}, u32[]{:S(2)}) collective-permute-start(bf16[192,64,64]{0,2,1:T(8,128)(2,1)} %copy.22), channel_id=1, source_target_pairs={{4,0},{8,4},{12,8},{16,12},{20,16},{24,20},{28,24},{0,28},{5,1},{9... | collective-permute-start | bytes 4718600 | tf_op jit(solution)/shard_map/ppermute | solution.py:17
  51.5 49.6 %collective-permute-start = (s32[48]{0:T(128)S(1)}, s32[48]{0:T(128)S(1)}, u32[]{:S(2)}, u32[]{:S(2)}) collective-permute-start(s32[48]{0:T(128)S(1)} %copy-done.6), channel_id=1, source_target_pairs={{0,1},{1,2},{2,3},{3,0},{4,5},{5,6},{6,7},{7,4},{8,9},{9,10},{10,1... | collective-permute-start | bytes 584 | tf_op jit(solution)/shard_map/ppermute | solution.py:100
  52.6 48.5 %collective-permute-start.1 = (s32[48]{0:T(128)S(1)}, s32[48]{0:T(128)S(1)}, u32[]{:S(2)}, u32[]{:S(2)}) collective-permute-start(s32[48]{0:T(128)S(1)} %copy-done.6), channel_id=1, source_target_pairs={{0,2},{1,3},{2,0},{3,1},{4,6},{5,7},{6,4},{7,5},{8,10},{9,11},{10,... | collective-permute-start | bytes 584 | tf_op jit(solution)/shard_map/ppermute | solution.py:100
  53.2 48.0 %collective-permute-start.2 = (s32[48]{0:T(128)S(1)}, s32[48]{0:T(128)S(1)}, u32[]{:S(2)}, u32[]{:S(2)}) collective-permute-start(s32[48]{0:T(128)S(1)} %copy-done.6), channel_id=1, source_target_pairs={{0,3},{1,0},{2,1},{3,2},{4,7},{5,4},{6,5},{7,6},{8,11},{9,8},{10,9... | collective-permute-start | bytes 584 | tf_op jit(solution)/shard_map/ppermute | solution.py:100
  98.0 85.0 %collective-permute-start.11 = (bf16[192,64,64]{0,2,1:T(8,128)(2,1)}, bf16[192,64,64]{0,2,1:T(8,128)(2,1)}, u32[]{:S(2)}, u32[]{:S(2)}) collective-permute-start(bf16[192,64,64]{0,2,1:T(8,128)(2,1)} %collective-permute-done.10), channel_id=1, source_target_pairs={{28,0},{0,4},{4,8},{8,12},{12,16},{16,20},{20,24},{24,28},{29,1},{... | collective-permute-start | bytes 4718600 | tf_op jit(solution)/shard_map/ppermute | solution.py:17
  98.0 90.3 %collective-permute-start.13 = (bf16[192,64,64]{0,2,1:T(8,128)(2,1)}, bf16[192,64,64]{0,2,1:T(8,128)(2,1)}, u32[]{:S(2)}, u32[]{:S(2)}) collective-permute-start(bf16[192,64,64]{0,2,1:T(8,128)(2,1)} %collective-permute-done.12), channel_id=1, source_target_pairs={{4,0},{8,4},{12,8},{16,12},{20,16},{24,20},{28,24},{0,28},{5,1},{9... | collective-permute-start | bytes 4718600 | tf_op jit(solution)/shard_map/ppermute | solution.py:17
  101.8 44.4 %collective-permute-start.3 = (s32[192]{0:T(256)S(1)}, s32[192]{0:T(256)S(1)}, u32[]{:S(2)}, u32[]{:S(2)}) collective-permute-start(s32[192]{0:T(256)S(1)} %get-tuple-element.20), channel_id=1, source_target_pairs={{28,0},{0,4},{4,8},{8,12},{12,16},{16,20},{20,24},{24,28},{29,1},{... | collective-permute-start | bytes 2312 | tf_op jit(solution)/shard_map/ppermute | solution.py:17
  101.8 44.4 %collective-permute-start.5 = (s32[192]{0:T(256)S(1)}, s32[192]{0:T(256)S(1)}, u32[]{:S(2)}, u32[]{:S(2)}) collective-permute-start(s32[192]{0:T(256)S(1)} %get-tuple-element.20), channel_id=1, source_target_pairs={{4,0},{8,4},{12,8},{16,12},{20,16},{24,20},{28,24},{0,28},{5,1},{9... | collective-permute-start | bytes 2312 | tf_op jit(solution)/shard_map/ppermute | solution.py:17
  146.2 19.7 %collective-permute-start.4 = (s32[192]{0:T(256)S(1)}, s32[192]{0:T(256)S(1)}, u32[]{:S(2)}, u32[]{:S(2)}) collective-permute-start(s32[192]{0:T(256)S(1)} %collective-permute-done.3), channel_id=1, source_target_pairs={{28,0},{0,4},{4,8},{8,12},{12,16},{16,20},{20,24},{24,28},{29,1},{... | collective-permute-start | bytes 2312 | tf_op jit(solution)/shard_map/ppermute | solution.py:17
  146.2 19.7 %collective-permute-start.6 = (s32[192]{0:T(256)S(1)}, s32[192]{0:T(256)S(1)}, u32[]{:S(2)}, u32[]{:S(2)}) collective-permute-start(s32[192]{0:T(256)S(1)} %collective-permute-done.5), channel_id=1, source_target_pairs={{4,0},{8,4},{12,8},{16,12},{20,16},{24,20},{28,24},{0,28},{5,1},{9... | collective-permute-start | bytes 2312 | tf_op jit(solution)/shard_map/ppermute | solution.py:17
  262.1 26.2 %collective-permute-start.14 = (f32[8,4,64,64]{3,2,1,0:T(8,128)S(1)}, f32[8,4,64,64]{3,2,1,0:T(8,128)}, u32[]{:S(2)}, u32[]{:S(2)}) collective-permute-start(f32[8,4,64,64]{3,2,1,0:T(8,128)S(1)} %get-tuple-element.21), channel_id=1, source_target_pairs={{0,1},{1,2},{2,3},{3,0},{4,5},{5,6},{6,7},{7,4},{8,9},{9,10},{10,1... | collective-permute-start | bytes 1572872 | tf_op jit(solution)/shard_map/ppermute | solution.py:150
  263.3 46.1 %collective-permute-start.15 = (f32[8,4,64,64]{3,2,1,0:T(8,128)S(1)}, f32[8,4,64,64]{3,2,1,0:T(8,128)}, u32[]{:S(2)}, u32[]{:S(2)}) collective-permute-start(f32[8,4,64,64]{3,2,1,0:T(8,128)S(1)} %get-tuple-element.23), channel_id=1, source_target_pairs={{0,2},{1,3},{2,0},{3,1},{4,6},{5,7},{6,4},{7,5},{8,10},{9,11},{10,... | collective-permute-start | bytes 1572872 | tf_op jit(solution)/shard_map/ppermute | solution.py:150
  263.9 45.6 %collective-permute-start.16 = (f32[8,4,64,64]{3,2,1,0:T(8,128)S(1)}, f32[8,4,64,64]{3,2,1,0:T(8,128)}, u32[]{:S(2)}, u32[]{:S(2)}) collective-permute-start(f32[8,4,64,64]{3,2,1,0:T(8,128)S(1)} %get-tuple-element.22), channel_id=1, source_target_pairs={{0,3},{1,0},{2,1},{3,2},{4,7},{5,4},{6,5},{7,6},{8,11},{9,8},{10,9... | collective-permute-start | bytes 1572872 | tf_op jit(solution)/shard_map/ppermute | solution.py:150

commit v3 on v2

--- a/solution.py
+++ b/solution.py
@@ -17,71 +17,92 @@
     return lax.ppermute(block, axis, route)
 
 
-def coarse_kernel(rows_ref, target_ref, live_ref, values_ref, own_t_ref, *rest):
+def coarse_kernel(pair_ref, half_ref, target_ref, live_ref, values_ref, own_t_ref, *rest):
     pieces = rest[:5]
-    acc_ref, window, sems = rest[5:]
+    out_ref, acc_ref, window, sems = rest[5:]
     step = pl.program_id(0)
     rows_here, slots, bs, _ = values_ref.shape
-    panel_length = pieces[0].shape[0]
+    piece_rows = pieces[0].shape[0]
+    lanes = window.shape[2]
 
     @pl.when(step == 0)
     def _():
         copies = []
         for k, piece in enumerate(pieces):
             cp = pltpu.make_async_copy(
-                piece, window.at[pl.ds(k * panel_length, panel_length)], sems.at[k]
+                piece, window.at[pl.ds(k * piece_rows, piece_rows)], sems.at[k]
             )
             cp.start()
             copies.append(cp)
+        acc_ref[...] = jnp.zeros_like(acc_ref)
         for cp in copies:
             cp.wait()
-        acc_ref[...] = jnp.zeros_like(acc_ref)
+
+    lane_half = lax.broadcasted_iota(jnp.int32, (bs, lanes), 1) // bs
 
     def row_body(r, carry):
         row = step * rows_here + r
         own_t = own_t_ref[row]
+        results = []
         for s in range(slots):
             n = row * slots + s
-            picked = window[rows_ref[n]]
+            pair = window[pair_ref[n]]
+            picked = jnp.where(lane_half == half_ref[n], pair, jnp.zeros_like(pair))
             product = jnp.dot(
                 values_ref[r, s], picked, preferred_element_type=jnp.float32
             )
             product = jnp.where(live_ref[n] > 0, product, 0.0).astype(jnp.bfloat16)
-            restricted = jnp.dot(own_t, product, preferred_element_type=jnp.float32)
-            t = target_ref[n]
-            acc_ref[t] = acc_ref[t] + restricted
+            results.append(
+                jnp.dot(own_t, product, preferred_element_type=jnp.float32)
+            )
+        for s in range(slots):
+            t = target_ref[row * slots + s]
+            acc_ref[t] = acc_ref[t] + results[s]
         return carry
 
-    lax.fori_loop(0, rows_here, row_body, 0)
+    lax.fori_loop(0, rows_here, row_body, 0, unroll=2)
+
+    @pl.when(step == pl.num_programs(0) - 1)
+    def _():
+        def pack(m, carry):
+            first = acc_ref[2 * m]
+            second = acc_ref[2 * m + 1]
+            first = first + pltpu.roll(first, bs, 1)
+            second = second + pltpu.roll(second, bs, 1)
+            out_ref[m] = jnp.where(lane_half == 0, first, second)
+            return carry
+
+        lax.fori_loop(0, out_ref.shape[0], pack, 0)
 
 
-def coarse_partial(rows, target, live, values, own_t, pieces, n_targets):
+def coarse_partial(pair, half, target, live, values, own_t, pieces, n_targets):
     panel_length, slots, bs, _ = values.shape
     rows_per_step = min(ROWS_PER_STEP, panel_length)
     grid = (panel_length // rows_per_step,)
-    window_rows = 5 * pieces[0].shape[0]
+    piece_rows, _, lanes = pieces[0].shape
     return pl.pallas_call(
         coarse_kernel,
-        out_shape=jax.ShapeDtypeStruct((n_targets, bs, bs), jnp.float32),
+        out_shape=jax.ShapeDtypeStruct((n_targets // 2, bs, lanes), jnp.float32),
         grid_spec=pltpu.PrefetchScalarGridSpec(
-            num_scalar_prefetch=3,
+            num_scalar_prefetch=4,
             grid=grid,
             in_specs=[
                 pl.BlockSpec((rows_per_step, slots, bs, bs), lambda i, *_: (i, 0, 0, 0)),
                 pl.BlockSpec(memory_space=pltpu.VMEM),
             ]
             + [pl.BlockSpec(memory_space=pl.ANY)] * 5,
-            out_specs=pl.BlockSpec((n_targets, bs, bs), lambda i, *_: (0, 0, 0)),
+            out_specs=pl.BlockSpec((n_targets // 2, bs, lanes), lambda i, *_: (0, 0, 0)),
             scratch_shapes=[
-                pltpu.VMEM((window_rows, bs, bs), jnp.bfloat16),
+                pltpu.VMEM((n_targets, bs, lanes), jnp.float32),
+                pltpu.VMEM((5 * piece_rows, bs, lanes), jnp.bfloat16),
                 pltpu.SemaphoreType.DMA((5,)),
             ],
         ),
         compiler_params=pltpu.CompilerParams(
             dimension_semantics=("arbitrary",),
-            vmem_limit_bytes=56 * 1024 * 1024,
+            vmem_limit_bytes=60 * 1024 * 1024,
         ),
-    )(rows, target, live, values, own_t, *pieces)
+    )(pair, half, target, live, values, own_t, *pieces)
 
 
 def local(block_values, block_columns, row_counts, prolong_blocks, aggregates):
@@ -110,16 +131,21 @@
     panel_aggs = jnp.take(
         jnp.stack([piece[1] for piece in received]), order, axis=0
     ).reshape(panel_length)
+    paired = (
+        panel_blocks.reshape(panel_length // 2, 2, block_size, block_size)
+        .transpose(0, 2, 1, 3)
+        .reshape(panel_length // 2, block_size, 2 * block_size)
+    )
     lower = []
     upper = []
-    going_down = (panel_blocks, panel_aggs)
-    going_up = (panel_blocks, panel_aggs)
+    going_down = (paired, panel_aggs)
+    going_up = (paired, panel_aggs)
     for hop in range(2):
         going_down = passed_along((going_down[0], going_down[1]), "blk", 1)
         lower.insert(0, going_down)
         going_up = passed_along((going_up[0], going_up[1]), "blk", -1)
         upper.append(going_up)
-    pieces = lower + [(panel_blocks, panel_aggs)] + upper
+    pieces = lower + [(paired, panel_aggs)] + upper
     window_aggs = jnp.concatenate([piece[1] for piece in pieces], axis=0)
     wanted = block_columns.reshape(slot_total)
     column_panel = wanted // panel_length
@@ -134,7 +160,8 @@
     ).reshape(slot_total)
     own_t = jnp.swapaxes(panel_blocks, 1, 2)
     summed = coarse_partial(
-        local_rows.astype(jnp.int32),
+        (local_rows // 2).astype(jnp.int32),
+        (local_rows % 2).astype(jnp.int32),
         target.astype(jnp.int32),
         live,
         block_values,
@@ -143,14 +170,15 @@
         coarse_count * CB,
     )
     share = coarse_count // group_size
-    summed = summed.reshape(group_size, share, CB, block_size, block_size)
+    summed = summed.reshape(group_size, share, CB // 2, block_size, 2 * block_size)
     total = jnp.take(summed, group_me, axis=0)
     for k in range(1, group_size):
         outgoing = jnp.take(summed, jnp.mod(group_me + k, group_size), axis=0)
         total = total + lax.ppermute(
             outgoing, "grp", [(i, (i + k) % group_size) for i in range(group_size)]
         )
-    return total
+    total = total.reshape(share, CB // 2, block_size, 2, block_size)
+    return total.transpose(0, 1, 3, 2, 4).reshape(share, CB, block_size, block_size)
 
 
 def solution(mesh):

time: 316 us -> 235 us (0.74)
  waiting for transfers between devices: 165 us -> 120 us
  Pallas kernels: 66.1 us -> 44.4 us
  local copies, waits for them, and re-layouts: 54.4 us -> 37.4 us
  other arithmetic: 11.4 us -> 14.9 us
    ppermute x8, waiting for transfers between devices: 86.7 us -> 64.1 us  [passed_along(): return lax.ppermute(block, axis, route)]
    ppermute x3, waiting for transfers between devices: 44.8 us -> 22.2 us  [local(): lax.ppermute(outgoing, 'grp', [(i, (i + k) % group_size) for i in range(g...]
    pallas_call x1, Pallas kernels: 66.1 us -> 44.4 us  [coarse_partial(): pl.pallas_call(coarse_kernel, out_shape=jax.ShapeDtypeStruct((n_targets /...]
    ppermute x4 -> x0, local copies, waits for them, and re-layouts: 20.9 us -> none  [passed_along(): return lax.ppermute(block, axis, route)]
    gather x1 -> x3, local copies, waits for them, and re-layouts: 2.58 us -> 10 us  [local(): jnp.take(jnp.stack([piece[0] for piece in received]), order, axis=0)]
    select_n x1 -> x2, other arithmetic: 2.27 us -> 6.56 us  [local(): jnp.take(jnp.stack([piece[0] for piece in received]), order, axis=0)]
    reshape x0 -> x1, local copies, waits for them, and re-layouts: none -> 3.89 us  [local(): paired = panel_blocks.reshape(panel_length // 2, 2, block_size, block_siz...]
    select_n x1 -> x0, local copies, waits for them, and re-layouts: 3.85 us -> none  [local(): jnp.take(jnp.stack([piece[0] for piece in received]), order, axis=0)]
  transfers between devices with their start and end apart: 17 -> 17, of which waited for: 6 -> 6; matrix products, arithmetic and copies ran while one was open for 14% -> 13% of each run, Pallas kernels for 0% -> 0%
where the time goes in v3:
time: 235 us; the launch traced here: 233 us
  waiting for transfers between devices  120 us (51%)
  Pallas kernels  44.4 us (19%)
  local copies, waits for them, and re-layouts  37.4 us (16%)
  starting transfers between devices  15.7 us (7%)
  other arithmetic  14.9 us (6%)
    ppermute x8, waiting for transfers between devices, passed_along(): return lax.ppermute(block, axis, route)  64.1 us
    pallas_call x1, Pallas kernels, coarse_partial(): pl.pallas_call(coarse_kernel, out_shape=jax.ShapeDtypeStruct((n_targets /...  44.4 us
    ppermute x6, waiting for transfers between devices, local(): lax.ppermute((prolong_blocks, aggregates), 'grp', [(i, (i + k) % group_si...  33.8 us
    ppermute x3, waiting for transfers between devices, local(): lax.ppermute(outgoing, 'grp', [(i, (i + k) % group_size) for i in range(g...  22.2 us
    unnamed x7, local copies, waits for them, and re-layouts  17 us
    gather x3, local copies, waits for them, and re-layouts, local(): jnp.take(jnp.stack([piece[0] for piece in received]), order, axis=0)  10 us
    ppermute x8, starting transfers between devices, passed_along(): return lax.ppermute(block, axis, route)  6.99 us
    select_n x2, other arithmetic, local(): jnp.take(jnp.stack([piece[0] for piece in received]), order, axis=0)  6.56 us
  transfers between devices with their start and end apart: 17, of which 6 were waited for; matrix products, arithmetic and copies ran while one was open for 13% of the time, Pallas kernels for 0%

profile of v3, /device:TPU:26, one launch (start us, length us, event | category | flops | bytes accessed | tf_op | source)
XLA Modules:
  0.0 232.6 jit_solution(6818349532123140121)
XLA Ops:
  0.0 1.5 collective-permute-start.7
  1.5 0.5 collective-permute-start.8
  2.0 1.5 collective-permute-start.9
  3.6 0.1 broadcast_in_dim.60
  3.6 0.1 broadcast_in_dim.61
  3.8 16.9 %collective-permute-done.7 = bf16[48,64,64]{2,1,0:T(8,128)(2,1)S(1)} collective-permute-done((bf16[48,64,64]{2,1,0:T(8,128)(2,1)}, bf16[48,64,64]{2,1,0:T(8,128)(2,1)S(1)}, u32[]{:S(2)}, u32[]{:S(2)}) %collective-permute-start.7) | collective-permute-done | bytes 393248 | tf_op jit(solution)/shard_map/ppermute | solution.py:121
  20.6 16.9 %collective-permute-done.8 = bf16[48,64,64]{2,1,0:T(8,128)(2,1)S(1)} collective-permute-done((bf16[48,64,64]{2,1,0:T(8,128)(2,1)}, bf16[48,64,64]{2,1,0:T(8,128)(2,1)S(1)}, u32[]{:S(2)}, u32[]{:S(2)}) %collective-permute-start.8) | collective-permute-done | bytes 393248 | tf_op jit(solution)/shard_map/ppermute | solution.py:121
  37.6 0.0 collective-permute-done.9
  37.6 3.0 %pad_maximum_fusion = bf16[4,48,64,64]{3,2,1,0:T(8,128)(2,1)} fusion(bf16[1,48,64,64]{3,2,1,0:T(8,128)(2,1)S(1)} %bitcast.39, bf16[1,48,64,64]{3,2,1,0:T(8,128)(2,1)S(1)} %bitcast.38, bf16[1,48,64,64]{3,2,1,0:T(8,128)(2,1)S(1)} %bitcast.37, bf16[1,48,64,64]{3,2,1,0:T(8,128)(2,1)} %bitcast.36), kind=kLoop, calls=%fused_computation.3 | loop fusion | flops 2359296 | bytes 3145728 | tf_op jit(solution)/shard_map/stack | solution.py:129
  40.6 3.0 %gather_fusion.2 = bf16[4,48,64,64]{3,2,1,0:T(8,128)(2,1)S(1)} fusion(bf16[4,48,64,64]{3,2,1,0:T(8,128)(2,1)} %pad_maximum_fusion, s32[1024]{0:T(1024)S(1)} %pad_clamp_fusion.1), kind=kCustom, calls=%fused_computation.2 | custom fusion | bytes 3145744 | tf_op jit(solution)/shard_map/jit(_take)/gather | solution.py:128
  43.7 4.2 %copy.16 = bf16[96,2,64,64]{0,3,1,2:T(8,128)(2,1)} copy(bf16[96,2,64,64]{3,2,1,0:T(8,128)(2,1)S(1)} %bitcast.31) | data formatting | bytes 3145728 | tf_op jit(solution)/shard_map/jit(_take)/gather | solution.py:128
  47.9 3.1 %broadcast_select_fusion = bf16[96,2,64,64]{0,3,1,2:T(8,128)(2,1)} fusion(bf16[96,2,64,64]{0,3,1,2:T(8,128)(2,1)} %copy.16, pred[96]{0:T(512)(128)(4,1)S(1)} %broadcast_in_dim.61), kind=kLoop, calls=%fused_computation.5 | loop fusion | flops 786432 | bytes 3145824 | tf_op jit(solution)/shard_map/jit(_take)/select_n | solution.py:128
  51.0 3.9 %copy.17.rest_2_ = bf16[96,64,128]{2,1,0:T(8,128)(2,1)} copy(bf16[96,64,128]{0,2,1:T(8,128)(2,1)} %bitcast.33) | data formatting | bytes 3145728 | tf_op jit(solution)/shard_map/reshape | solution.py:137
  54.9 0.0 collective-permute-start.10
  54.9 1.7 collective-permute-start.12
  56.7 1.2 collective-permute-start
  57.8 0.6 collective-permute-start.1
  58.4 0.8 collective-permute-start.2
  59.2 0.1 copy.11
  59.3 0.1 div.34
  59.4 0.1 div.30
  59.6 0.1 copy.10
  59.7 0.1 rem.200
  59.8 0.1 rem.168
  59.9 0.2 copy.9
  60.1 0.1 ne.153
  60.2 0.1 ne.144
  60.4 31.5 %collective-permute-done.10.rest_1_ = bf16[96,64,128]{2,1,0:T(8,128)(2,1)} collective-permute-done((bf16[96,64,128]{2,1,0:T(8,128)(2,1)}, bf16[96,64,128]{2,1,0:T(8,128)(2,1)}, u32[]{:S(2)}, u32[]{:S(2)}) %collective-permute-start.10) | collective-permute-done | bytes 1572896 | tf_op jit(solution)/shard_map/ppermute | solution.py:17
  91.9 1.7 collective-permute-start.13
  93.7 0.1 compare_convert_fusion
  93.8 0.1 broadcast_in_dim.53
  93.9 0.1 broadcast_in_dim.54
  94.0 0.0 collective-permute-done
  94.0 0.0 collective-permute-done.1
  94.0 0.0 collective-permute-done.2
  94.0 0.6 gather_fusion
  94.5 0.1 gather.22
  94.6 0.0 collective-permute-start.3
  94.7 1.7 collective-permute-start.5
  96.4 32.5 %collective-permute-done.3 = s32[192]{0:T(256)S(1)} collective-permute-done((s32[192]{0:T(256)S(1)}, s32[192]{0:T(256)S(1)}, u32[]{:S(2)}, u32[]{:S(2)}) %collective-permute-start.3) | collective-permute-done | bytes 800 | tf_op jit(solution)/shard_map/ppermute | solution.py:17
  128.9 0.0 collective-permute-start.4
  128.9 0.0 collective-permute-done.5
  128.9 1.7 collective-permute-start.6
  130.7 0.7 reshape.294.live_ref
  131.4 17.0 %copy.19.values_ref = bf16[192,4,64,64]{3,2,1,0:T(8,128)(2,1)} copy(bf16[192,4,64,64]{0,3,2,1:T(8,128)(2,1)} %param.7) | data formatting | bytes 12582912 | tf_op args[0]
  148.4 0.1 broadcast_in_dim.57
  148.5 0.1 reshape.227
  148.6 0.0 collective-permute-done.4
  148.6 0.1 concatenate.6
  148.7 3.2 %gather_fusion.1 = s32[768]{0:T(1024)S(1)} fusion(s32[960]{0:T(1024)S(1)} %concatenate.6, s32[1024]{0:T(1024)S(1)} %pad_clamp_fusion), kind=kCustom, calls=%fused_computation.1 | custom fusion | bytes 9216 | tf_op jit(solution)/shard_map/jit(_take)/gather | solution.py:154
  151.9 0.6 multiply_add_fusion
  152.5 0.6 add_select_fusion.1
  153.1 2.8 %copy.15 = bf16[4,48,64,64]{2,3,1,0:T(8,128)(2,1)} copy(bf16[4,48,64,64]{3,2,1,0:T(8,128)(2,1)S(1)} %gather_fusion.2) | data formatting | bytes 3145728 | tf_op jit(solution)/shard_map/jit(_take)/gather | solution.py:128
  155.9 3.4 %bitcast_select_fusion = bf16[192,64,64]{1,2,0:T(8,128)(2,1)} fusion(bf16[4,48,64,64]{2,3,1,0:T(8,128)(2,1)} %copy.15, pred[192]{0:T(512)(128)(4,1)S(1)} %broadcast_in_dim.54), kind=kLoop, calls=%fused_computation.4 | loop fusion | flops 786432 | bytes 3145920 | tf_op jit(solution)/shard_map/jit(_take)/select_n | solution.py:128
  159.3 44.4 %shard_map.55 = f32[64,64,128]{2,1,0:T(8,128)} custom-call(s32[768]{0:T(1024)} %get-tuple-element.27.pair_ref, s32[768]{0:T(1024)} %get-tuple-element.26.half_ref, s32[768]{0:T(1024)} %get-tuple-element.17.target_ref, s32[768]{0:T(1024)} %reshape.294.live_ref, bf16[192,4,64,64]{3,2,1,0:T(8,128)(2,1)} %copy.19.values_ref, bf16[192,64,64]{2,1,0:T(8,128)(2,1)} %bitcast.32, ...), custom_call_target="tpu_custom_call" | custom-call | tf_op jit(solution)/shard_map/pallas_call | solution.py:83
  203.7 1.6 select_bitcast_fusion.2
  205.3 1.2 collective-permute-start.14
  206.5 0.6 collective-permute-start.15
  207.1 0.8 collective-permute-start.16
  207.9 12.3 %collective-permute-done.14 = f32[8,2,64,128]{3,2,1,0:T(8,128)S(1)} collective-permute-done((f32[8,2,64,128]{3,2,1,0:T(8,128)S(1)}, f32[8,2,64,128]{3,2,1,0:T(8,128)S(1)}, u32[]{:S(2)}, u32[]{:S(2)}) %collective-permute-start.14) | collective-permute-done | bytes 524320 | tf_op jit(solution)/shard_map/ppermute | solution.py:177
  220.2 9.9 %collective-permute-done.15 = f32[8,2,64,128]{3,2,1,0:T(8,128)S(1)} collective-permute-done((f32[8,2,64,128]{3,2,1,0:T(8,128)S(1)}, f32[8,2,64,128]{3,2,1,0:T(8,128)S(1)}, u32[]{:S(2)}, u32[]{:S(2)}) %collective-permute-start.15) | collective-permute-done | bytes 524320 | tf_op jit(solution)/shard_map/ppermute | solution.py:177
  230.1 1.2 fusion.1
  231.3 0.2 fusion.17
  231.5 1.1 pad_maximum_fusion.1
  (22 shorter events, 0.2 us)
Async XLA Ops:
  0.0 20.6 %collective-permute-start.7 = (bf16[48,64,64]{2,1,0:T(8,128)(2,1)}, bf16[48,64,64]{2,1,0:T(8,128)(2,1)S(1)}, u32[]{:S(2)}, u32[]{:S(2)}) collective-permute-start(bf16[48,64,64]{2,1,0:T(8,128)(2,1)} %param.10), channel_id=1, source_target_pairs={{0,1},{1,2},{2,3},{3,0},{4,5},{5,6},{6,7},{7,4},{8,9},{9,10},{10,1... | collective-permute-start | bytes 1179656 | tf_op jit(solution)/shard_map/ppermute | solution.py:121
  1.5 36.1 %collective-permute-start.8 = (bf16[48,64,64]{2,1,0:T(8,128)(2,1)}, bf16[48,64,64]{2,1,0:T(8,128)(2,1)S(1)}, u32[]{:S(2)}, u32[]{:S(2)}) collective-permute-start(bf16[48,64,64]{2,1,0:T(8,128)(2,1)} %param.10), channel_id=1, source_target_pairs={{0,2},{1,3},{2,0},{3,1},{4,6},{5,7},{6,4},{7,5},{8,10},{9,11},{10,... | collective-permute-start | bytes 1179656 | tf_op jit(solution)/shard_map/ppermute | solution.py:121
  2.0 35.6 %collective-permute-start.9 = (bf16[48,64,64]{2,1,0:T(8,128)(2,1)}, bf16[48,64,64]{2,1,0:T(8,128)(2,1)S(1)}, u32[]{:S(2)}, u32[]{:S(2)}) collective-permute-start(bf16[48,64,64]{2,1,0:T(8,128)(2,1)} %param.10), channel_id=1, source_target_pairs={{0,3},{1,0},{2,1},{3,2},{4,7},{5,4},{6,5},{7,6},{8,11},{9,8},{10,9... | collective-permute-start | bytes 1179656 | tf_op jit(solution)/shard_map/ppermute | solution.py:121
  47.9 8.8 %copy-start.2 = (s32[48]{0:T(128)S(1)}, s32[48]{0:T(128)}, u32[]{:S(2)}) copy-start(s32[48]{0:T(128)} %param.11) | copy-start | bytes 580
  47.9 11.3 %copy-start = (s32[192,4]{0,1:T(4,128)S(1)}, s32[192,4]{0,1:T(4,128)}, u32[]{:S(2)}) copy-start(s32[192,4]{0,1:T(4,128)} %param.8) | copy-start | bytes 9220
  51.0 42.7 %copy-start.1 = (s32[192]{0:T(256)S(1)}, s32[192]{0:T(256)}, u32[]{:S(2)}) copy-start(s32[192]{0:T(256)} %param.9) | copy-start | bytes 2308
  54.9 37.0 %collective-permute-start.10 = (bf16[96,64,128]{2,1,0:T(8,128)(2,1)}, bf16[96,64,128]{2,1,0:T(8,128)(2,1)}, u32[]{:S(2)}, u32[]{:S(2)}) collective-permute-start(bf16[96,64,128]{2,1,0:T(8,128)(2,1)} %copy.17.rest_2_), channel_id=1, source_target_pairs={{28,0},{0,4},{4,8},{8,12},{12,16},{16,20},{20,24},{24,28},{29,1},{... | collective-permute-start | bytes 4718600 | tf_op jit(solution)/shard_map/ppermute | solution.py:17
  54.9 37.0 %collective-permute-start.12 = (bf16[96,64,128]{2,1,0:T(8,128)(2,1)}, bf16[96,64,128]{2,1,0:T(8,128)(2,1)}, u32[]{:S(2)}, u32[]{:S(2)}) collective-permute-start(bf16[96,64,128]{2,1,0:T(8,128)(2,1)} %copy.17.rest_2_), channel_id=1, source_target_pairs={{4,0},{8,4},{12,8},{16,12},{20,16},{24,20},{28,24},{0,28},{5,1},{9... | collective-permute-start | bytes 4718600 | tf_op jit(solution)/shard_map/ppermute | solution.py:17
  56.7 37.3 %collective-permute-start = (s32[48]{0:T(128)S(1)}, s32[48]{0:T(128)S(1)}, u32[]{:S(2)}, u32[]{:S(2)}) collective-permute-start(s32[48]{0:T(128)S(1)} %copy-done.2), channel_id=1, source_target_pairs={{0,1},{1,2},{2,3},{3,0},{4,5},{5,6},{6,7},{7,4},{8,9},{9,10},{10,1... | collective-permute-start | bytes 584 | tf_op jit(solution)/shard_map/ppermute | solution.py:121
  57.8 36.1 %collective-permute-start.1 = (s32[48]{0:T(128)S(1)}, s32[48]{0:T(128)S(1)}, u32[]{:S(2)}, u32[]{:S(2)}) collective-permute-start(s32[48]{0:T(128)S(1)} %copy-done.2), channel_id=1, source_target_pairs={{0,2},{1,3},{2,0},{3,1},{4,6},{5,7},{6,4},{7,5},{8,10},{9,11},{10,... | collective-permute-start | bytes 584 | tf_op jit(solution)/shard_map/ppermute | solution.py:121
  58.4 35.5 %collective-permute-start.2 = (s32[48]{0:T(128)S(1)}, s32[48]{0:T(128)S(1)}, u32[]{:S(2)}, u32[]{:S(2)}) collective-permute-start(s32[48]{0:T(128)S(1)} %copy-done.2), channel_id=1, source_target_pairs={{0,3},{1,0},{2,1},{3,2},{4,7},{5,4},{6,5},{7,6},{8,11},{9,8},{10,9... | collective-permute-start | bytes 584 | tf_op jit(solution)/shard_map/ppermute | solution.py:121
  91.9 67.4 %collective-permute-start.11 = (bf16[96,64,128]{2,1,0:T(8,128)(2,1)}, bf16[96,64,128]{2,1,0:T(8,128)(2,1)}, u32[]{:S(2)}, u32[]{:S(2)}) collective-permute-start(bf16[96,64,128]{2,1,0:T(8,128)(2,1)} %collective-permute-done.10.rest_1_), channel_id=1, source_target_pairs={{28,0},{0,4},{4,8},{8,12},{12,16},{16,20},{20,24},{24,28},{29,1},{... | collective-permute-start | bytes 4718600 | tf_op jit(solution)/shard_map/ppermute | solution.py:17
  91.9 67.4 %collective-permute-start.13 = (bf16[96,64,128]{2,1,0:T(8,128)(2,1)}, bf16[96,64,128]{2,1,0:T(8,128)(2,1)}, u32[]{:S(2)}, u32[]{:S(2)}) collective-permute-start(bf16[96,64,128]{2,1,0:T(8,128)(2,1)} %collective-permute-done.12.rest_3_), channel_id=1, source_target_pairs={{4,0},{8,4},{12,8},{16,12},{20,16},{24,20},{28,24},{0,28},{5,1},{9... | collective-permute-start | bytes 4718600 | tf_op jit(solution)/shard_map/ppermute | solution.py:17
  94.6 34.3 %collective-permute-start.3 = (s32[192]{0:T(256)S(1)}, s32[192]{0:T(256)S(1)}, u32[]{:S(2)}, u32[]{:S(2)}) collective-permute-start(s32[192]{0:T(256)S(1)} %get-tuple-element.20), channel_id=1, source_target_pairs={{28,0},{0,4},{4,8},{8,12},{12,16},{16,20},{20,24},{24,28},{29,1},{... | collective-permute-start | bytes 2312 | tf_op jit(solution)/shard_map/ppermute | solution.py:17
  94.7 34.3 %collective-permute-start.5 = (s32[192]{0:T(256)S(1)}, s32[192]{0:T(256)S(1)}, u32[]{:S(2)}, u32[]{:S(2)}) collective-permute-start(s32[192]{0:T(256)S(1)} %get-tuple-element.20), channel_id=1, source_target_pairs={{4,0},{8,4},{12,8},{16,12},{20,16},{24,20},{28,24},{0,28},{5,1},{9... | collective-permute-start | bytes 2312 | tf_op jit(solution)/shard_map/ppermute | solution.py:17
  128.9 19.7 %collective-permute-start.4 = (s32[192]{0:T(256)S(1)}, s32[192]{0:T(256)S(1)}, u32[]{:S(2)}, u32[]{:S(2)}) collective-permute-start(s32[192]{0:T(256)S(1)} %collective-permute-done.3), channel_id=1, source_target_pairs={{28,0},{0,4},{4,8},{8,12},{12,16},{16,20},{20,24},{24,28},{29,1},{... | collective-permute-start | bytes 2312 | tf_op jit(solution)/shard_map/ppermute | solution.py:17
  128.9 19.7 %collective-permute-start.6 = (s32[192]{0:T(256)S(1)}, s32[192]{0:T(256)S(1)}, u32[]{:S(2)}, u32[]{:S(2)}) collective-permute-start(s32[192]{0:T(256)S(1)} %collective-permute-done.5), channel_id=1, source_target_pairs={{4,0},{8,4},{12,8},{16,12},{20,16},{24,20},{28,24},{0,28},{5,1},{9... | collective-permute-start | bytes 2312 | tf_op jit(solution)/shard_map/ppermute | solution.py:17
  205.3 14.8 %collective-permute-start.14 = (f32[8,2,64,128]{3,2,1,0:T(8,128)S(1)}, f32[8,2,64,128]{3,2,1,0:T(8,128)S(1)}, u32[]{:S(2)}, u32[]{:S(2)}) collective-permute-start(f32[8,2,64,128]{3,2,1,0:T(8,128)S(1)} %get-tuple-element.21), channel_id=1, source_target_pairs={{0,1},{1,2},{2,3},{3,0},{4,5},{5,6},{6,7},{7,4},{8,9},{9,10},{10,1... | collective-permute-start | bytes 1572872 | tf_op jit(solution)/shard_map/ppermute | solution.py:177
  206.5 23.6 %collective-permute-start.15 = (f32[8,2,64,128]{3,2,1,0:T(8,128)S(1)}, f32[8,2,64,128]{3,2,1,0:T(8,128)S(1)}, u32[]{:S(2)}, u32[]{:S(2)}) collective-permute-start(f32[8,2,64,128]{3,2,1,0:T(8,128)S(1)} %get-tuple-element.23), channel_id=1, source_target_pairs={{0,2},{1,3},{2,0},{3,1},{4,6},{5,7},{6,4},{7,5},{8,10},{9,11},{10,... | collective-permute-start | bytes 1572872 | tf_op jit(solution)/shard_map/ppermute | solution.py:177
  207.1 23.0 %collective-permute-start.16 = (f32[8,2,64,128]{3,2,1,0:T(8,128)S(1)}, f32[8,2,64,128]{3,2,1,0:T(8,128)S(1)}, u32[]{:S(2)}, u32[]{:S(2)}) collective-permute-start(f32[8,2,64,128]{3,2,1,0:T(8,128)S(1)} %get-tuple-element.22), channel_id=1, source_target_pairs={{0,3},{1,0},{2,1},{3,2},{4,7},{5,4},{6,5},{7,6},{8,11},{9,8},{10,9... | collective-permute-start | bytes 1572872 | tf_op jit(solution)/shard_map/ppermute | solution.py:177

commit v4 on v3

--- a/solution.py
+++ b/solution.py
@@ -17,7 +17,7 @@
     return lax.ppermute(block, axis, route)
 
 
-def coarse_kernel(pair_ref, half_ref, target_ref, live_ref, values_ref, own_t_ref, *rest):
+def coarse_kernel(pair_ref, half_ref, target_ref, live_ref, own_pos_ref, values_ref, own_t_ref, *rest):
     pieces = rest[:5]
     out_ref, acc_ref, window, sems = rest[5:]
     step = pl.program_id(0)
@@ -42,7 +42,7 @@
 
     def row_body(r, carry):
         row = step * rows_here + r
-        own_t = own_t_ref[row]
+        own_t = own_t_ref[own_pos_ref[row]]
         results = []
         for s in range(slots):
             n = row * slots + s
@@ -75,7 +75,7 @@
         lax.fori_loop(0, out_ref.shape[0], pack, 0)
 
 
-def coarse_partial(pair, half, target, live, values, own_t, pieces, n_targets):
+def coarse_partial(pair, half, target, live, own_pos, values, own_t, pieces, n_targets):
     panel_length, slots, bs, _ = values.shape
     rows_per_step = min(ROWS_PER_STEP, panel_length)
     grid = (panel_length // rows_per_step,)
@@ -84,7 +84,7 @@
         coarse_kernel,
         out_shape=jax.ShapeDtypeStruct((n_targets // 2, bs, lanes), jnp.float32),
         grid_spec=pltpu.PrefetchScalarGridSpec(
-            num_scalar_prefetch=4,
+            num_scalar_prefetch=5,
             grid=grid,
             in_specs=[
                 pl.BlockSpec((rows_per_step, slots, bs, bs), lambda i, *_: (i, 0, 0, 0)),
@@ -102,7 +102,7 @@
             dimension_semantics=("arbitrary",),
             vmem_limit_bytes=60 * 1024 * 1024,
         ),
-    )(pair, half, target, live, values, own_t, *pieces)
+    )(pair, half, target, live, own_pos, values, own_t, *pieces)
 
 
 def local(block_values, block_columns, row_counts, prolong_blocks, aggregates):
@@ -115,27 +115,27 @@
     coarse_count = CB * panel_total
     me = lax.axis_index("blk")
     group_me = lax.axis_index("grp")
-    received = [(prolong_blocks, aggregates)]
+    share_rows = prolong_blocks.shape[0]
+    local_pairs = (
+        prolong_blocks.reshape(share_rows // 2, 2, block_size, block_size)
+        .transpose(0, 2, 1, 3)
+        .reshape(share_rows // 2, block_size, 2 * block_size)
+    )
+    received = [(local_pairs, aggregates)]
     for k in range(1, group_size):
         received.append(
             lax.ppermute(
-                (prolong_blocks, aggregates),
+                (local_pairs, aggregates),
                 "grp",
                 [(i, (i + k) % group_size) for i in range(group_size)],
             )
         )
-    order = jnp.mod(group_me - jnp.arange(group_size, dtype=jnp.int32), group_size)
-    panel_blocks = jnp.take(
-        jnp.stack([piece[0] for piece in received]), order, axis=0
-    ).reshape(panel_length, block_size, block_size)
-    panel_aggs = jnp.take(
-        jnp.stack([piece[1] for piece in received]), order, axis=0
-    ).reshape(panel_length)
-    paired = (
-        panel_blocks.reshape(panel_length // 2, 2, block_size, block_size)
-        .transpose(0, 2, 1, 3)
-        .reshape(panel_length // 2, block_size, 2 * block_size)
-    )
+    paired = jnp.concatenate([piece[0] for piece in received], axis=0)
+    panel_aggs = jnp.concatenate([piece[1] for piece in received], axis=0)
+
+    def rotated(r):
+        return jnp.mod(group_me - r // share_rows, group_size) * share_rows + r % share_rows
+
     lower = []
     upper = []
     going_down = (paired, panel_aggs)
@@ -150,20 +150,26 @@
     wanted = block_columns.reshape(slot_total)
     column_panel = wanted // panel_length
     distance = jnp.mod(column_panel - me + 2, panel_total)
-    local_rows = distance * panel_length + wanted % panel_length
+    local_rows = distance * panel_length + rotated(wanted % panel_length)
+    own_pos = rotated(jnp.arange(panel_length, dtype=jnp.int32))
     fetched_aggs = jnp.take(window_aggs, local_rows, axis=0)
     slot_ids = lax.axis_index("grp") * slots_here + jnp.arange(slots_here, dtype=jnp.int32)
     live = (slot_ids[None, :] < row_counts[:, None]).astype(jnp.int32).reshape(slot_total)
-    local_coarse = panel_aggs - me * CB
+    local_coarse = jnp.take(panel_aggs, own_pos, axis=0) - me * CB
     target = fetched_aggs * CB + jnp.broadcast_to(
         local_coarse[:, None], (panel_length, slots_here)
     ).reshape(slot_total)
-    own_t = jnp.swapaxes(panel_blocks, 1, 2)
+    own_t = (
+        paired.reshape(panel_length // 2, block_size, 2, block_size)
+        .transpose(0, 2, 3, 1)
+        .reshape(panel_length, block_size, block_size)
+    )
     summed = coarse_partial(
         (local_rows // 2).astype(jnp.int32),
         (local_rows % 2).astype(jnp.int32),
         target.astype(jnp.int32),
         live,
+        own_pos,
         block_values,
         own_t,
         [piece[0] for piece in pieces],

time: 235 us -> 182 us (0.77)
  waiting for transfers between devices: 120 us -> 62.7 us
    ppermute x8, waiting for transfers between devices: 64.1 us -> 28 us  [passed_along(): return lax.ppermute(block, axis, route)]
    ppermute x6, waiting for transfers between devices: 33.8 us -> 11.7 us  [local(): lax.ppermute((local_pairs, aggregates), 'grp', [(i, (i + k) % group_size)...]
    gather x5 -> x1, local copies, waits for them, and re-layouts: 10.7 us -> 1.61 us  [local(): local_coarse = jnp.take(panel_aggs, own_pos, axis=0) - me * CB]
    transpose x0 -> x1, other arithmetic: none -> 8.21 us  [local(): own_t = paired.reshape(panel_length // 2, block_size, 2, block_size).tran...]
    select_n x3 -> x1, other arithmetic: 6.58 us -> 0.02 us  [local(): local_coarse = jnp.take(panel_aggs, own_pos, axis=0) - me * CB]
    transpose x0 -> x1, local copies, waits for them, and re-layouts: none -> 5.74 us  [local(): own_t = paired.reshape(panel_length // 2, block_size, 2, block_size).tran...]
    concatenate x0 -> x4, local copies, waits for them, and re-layouts: none -> 3.79 us  [local(): paired = jnp.concatenate([piece[0] for piece in received], axis=0)]
    unnamed x7 -> x12, local copies, waits for them, and re-layouts: 17 us -> 18.2 us
  transfers between devices with their start and end apart: 17 -> 17, of which waited for: 6 -> 7; matrix products, arithmetic and copies ran while one was open for 13% -> 26% of each run, Pallas kernels for 0% -> 0%
where the time goes in v4:
time: 182 us; the launch traced here: 179 us
  waiting for transfers between devices  62.7 us (34%)
  Pallas kernels  44.5 us (24%)
  local copies, waits for them, and re-layouts  38.3 us (21%)
  starting transfers between devices  17.6 us (10%)
  other arithmetic  15.4 us (8%)
    pallas_call x1, Pallas kernels, coarse_partial(): pl.pallas_call(coarse_kernel, out_shape=jax.ShapeDtypeStruct((n_targets /...  44.5 us
    ppermute x8, waiting for transfers between devices, passed_along(): return lax.ppermute(block, axis, route)  28 us
    ppermute x3, waiting for transfers between devices, local(): lax.ppermute(outgoing, 'grp', [(i, (i + k) % group_size) for i in range(g...  23 us
    unnamed x12, local copies, waits for them, and re-layouts  18.2 us
    ppermute x6, waiting for transfers between devices, local(): lax.ppermute((local_pairs, aggregates), 'grp', [(i, (i + k) % group_size)...  11.7 us
    transpose x1, other arithmetic, local(): own_t = paired.reshape(panel_length // 2, block_size, 2, block_size).tran...  8.21 us
    ppermute x6, starting transfers between devices, local(): lax.ppermute((local_pairs, aggregates), 'grp', [(i, (i + k) % group_size)...  7.92 us
    ppermute x8, starting transfers between devices, passed_along(): return lax.ppermute(block, axis, route)  7.11 us
  transfers between devices with their start and end apart: 17, of which 7 were waited for; matrix products, arithmetic and copies ran while one was open for 26% of the time, Pallas kernels for 0%

profile of v4, /device:TPU:26, one launch (start us, length us, event | category | flops | bytes accessed | tf_op | source)
XLA Modules:
  0.0 178.8 jit_solution(18405252877573084384)
XLA Ops:
  0.0 2.0 %copy.19 = bf16[24,2,64,64]{3,1,2,0:T(2,128)(2,1)S(1)} copy(bf16[24,2,64,64]{3,2,1,0:T(8,128)(2,1)} %bitcast.27) | data formatting | bytes 786432 | tf_op jit(solution)/shard_map/reshape | solution.py:120
  2.0 1.1 reshape.358
  3.1 1.5 collective-permute-start.7
  4.6 0.5 collective-permute-start.8
  5.1 1.5 collective-permute-start.9
  6.6 1.4 collective-permute-start
  8.0 1.5 collective-permute-start.1
  9.5 1.0 constant_dynamic-update-slice_fusion.3
  10.5 4.7 %collective-permute-done.7 = bf16[24,64,128]{2,1,0:T(8,128)(2,1)S(1)} collective-permute-done((bf16[24,64,128]{2,1,0:T(8,128)(2,1)}, bf16[24,64,128]{2,1,0:T(8,128)(2,1)S(1)}, u32[]{:S(2)}, u32[]{:S(2)}) %collective-permute-start.7) | collective-permute-done | bytes 393248 | tf_op jit(solution)/shard_map/ppermute | solution.py:127
  15.3 1.5 collective-permute-start.2
  16.7 0.1 constant_dynamic-update-slice_fusion.2
  16.8 7.0 %collective-permute-done.8 = bf16[24,64,128]{2,1,0:T(8,128)(2,1)S(1)} collective-permute-done((bf16[24,64,128]{2,1,0:T(8,128)(2,1)}, bf16[24,64,128]{2,1,0:T(8,128)(2,1)S(1)}, u32[]{:S(2)}, u32[]{:S(2)}) %collective-permute-start.8) | collective-permute-done | bytes 393248 | tf_op jit(solution)/shard_map/ppermute | solution.py:127
  23.8 0.1 constant_dynamic-update-slice_fusion.1
  23.9 0.0 collective-permute-done.9
  23.9 0.1 constant_dynamic-update-slice_fusion.rest_2_
  23.9 0.1 collective-permute-start.10
  24.0 1.7 collective-permute-start.12
  25.8 0.1 copy.11
  25.9 0.1 div.70
  26.0 0.1 div.65
  26.1 0.1 copy.10
  26.2 0.1 rem.290
  26.4 0.1 rem.264
  26.5 0.2 copy.9
  26.6 0.1 ne.303
  26.8 0.1 ne.293
  27.0 0.6 fusion.24.own_pos_ref
  27.6 0.1 fusion.14
  27.7 0.8 compare_convert_fusion
  28.5 0.0 collective-permute-done
  28.5 0.0 collective-permute-done.2
  28.5 0.6 pad_add_fusion
  29.1 0.0 collective-permute-start.3
  29.1 1.7 collective-permute-start.5
  30.9 0.7 reshape.425.live_ref
  31.6 17.0 %copy.17.values_ref = bf16[192,4,64,64]{3,2,1,0:T(8,128)(2,1)} copy(bf16[192,4,64,64]{0,3,2,1:T(8,128)(2,1)} %param.7) | data formatting | bytes 12582912 | tf_op args[0]
  48.6 1.6 gather_fusion.1
  50.2 10.6 %collective-permute-done.3 = s32[192]{0:T(256)S(1)} collective-permute-done((s32[192]{0:T(256)S(1)}, s32[192]{0:T(256)S(1)}, u32[]{:S(2)}, u32[]{:S(2)}) %collective-permute-start.3) | collective-permute-done | bytes 800 | tf_op jit(solution)/shard_map/ppermute | solution.py:17
  60.8 1.7 collective-permute-start.6
  62.6 0.1 broadcast_in_dim.31
  62.7 0.1 reshape.356
  62.8 1.0 collective-permute-done.4
  63.8 0.1 collective-permute-done.6
  63.9 0.6 concatenate.23
  64.5 3.2 %gather_fusion = s32[768]{0:T(1024)S(1)} fusion(s32[960]{0:T(1024)S(1)} %concatenate.23, s32[1024]{0:T(1024)S(1)} %pad_clamp_fusion.1), kind=kCustom, calls=%fused_computation | custom fusion | bytes 9216 | tf_op jit(solution)/shard_map/jit(_take)/gather | solution.py:155
  67.7 1.8 %collective-permute-start.11 = (bf16[96,64,128]{2,1,0:T(8,128)(2,1)}, bf16[96,64,128]{2,1,0:T(8,128)(2,1)}, u32[]{:S(2)}, u32[]{:S(2)}) collective-permute-start(bf16[96,64,128]{2,1,0:T(8,128)(2,1)} %collective-permute-done.10.rest_1_), channel_id=1, source_target_pairs={{28,0},{0,4},{4,8},{8,12},{12,16},{16,20},{20,24},{24,28},{29,1},{... | collective-permute-start | bytes 4718600 | tf_op jit(solution)/shard_map/ppermute | solution.py:17
  69.5 0.6 multiply_add_fusion
  70.2 0.6 add_select_fusion.1
  70.8 1.3 concatenate.24
  72.0 1.3 concatenate.25
  73.3 1.2 concatenate.26
  74.5 8.2 %maximum_bitcast_fusion = bf16[96,2,64,64]{2,1,3,0:T(2,128)(2,1)S(1)} fusion(bf16[24,64,2,64]{3,2,1,0:T(2,128)(2,1)} %concatenate.26, bf16[24,64,2,64]{3,2,1,0:T(2,128)(2,1)} %concatenate.25, bf16[24,64,2,64]{3,2,1,0:T(2,128)(2,1)} %concatenate.24, bf16[24,64,2,64]{3,2,1,0:T(2,128)(2,1)} %bitcast.26), kind=kLoop, calls=%fused_computation.2 | loop fusion | flops 2359296 | bytes 3145728 | tf_op jit(solution)/shard_map/transpose | solution.py:164
  82.7 5.7 %copy.16 = bf16[96,2,64,64]{3,2,1,0:T(8,128)(2,1)} copy(bf16[96,2,64,64]{2,1,3,0:T(2,128)(2,1)S(1)} %maximum_bitcast_fusion) | data formatting | bytes 3145728 | tf_op jit(solution)/shard_map/transpose | solution.py:164
  88.5 16.3 %collective-permute-done.11.rest_0_ = bf16[96,64,128]{2,1,0:T(8,128)(2,1)} collective-permute-done((bf16[96,64,128]{2,1,0:T(8,128)(2,1)}, bf16[96,64,128]{2,1,0:T(8,128)(2,1)}, u32[]{:S(2)}, u32[]{:S(2)}) %collective-permute-start.11) | collective-permute-done | bytes 1572896 | tf_op jit(solution)/shard_map/ppermute | solution.py:17
  104.8 44.5 %shard_map.55 = f32[64,64,128]{2,1,0:T(8,128)} custom-call(s32[768]{0:T(1024)} %get-tuple-element.25.pair_ref, s32[768]{0:T(1024)} %get-tuple-element.24.half_ref, s32[768]{0:T(1024)} %get-tuple-element.17.target_ref, s32[768]{0:T(1024)} %reshape.425.live_ref, s32[192]{0:T(256)} %fusion.24.own_pos_ref, bf16[192,4,64,64]{3,2,1,0:T(8,128)(2,1)} %copy.17.values_ref, ...), custom_call_target="tpu_custom_call" | custom-call | tf_op jit(solution)/shard_map/pallas_call | solution.py:83
  149.3 1.5 select_bitcast_fusion.2
  150.7 1.2 collective-permute-start.14
  152.0 0.5 collective-permute-start.15
  152.5 0.8 collective-permute-start.16
  153.3 12.3 %collective-permute-done.14 = f32[8,2,64,128]{3,2,1,0:T(8,128)S(1)} collective-permute-done((f32[8,2,64,128]{3,2,1,0:T(8,128)S(1)}, f32[8,2,64,128]{3,2,1,0:T(8,128)S(1)}, u32[]{:S(2)}, u32[]{:S(2)}) %collective-permute-start.14) | collective-permute-done | bytes 524320 | tf_op jit(solution)/shard_map/ppermute | solution.py:183
  165.6 10.8 %collective-permute-done.15 = f32[8,2,64,128]{3,2,1,0:T(8,128)S(1)} collective-permute-done((f32[8,2,64,128]{3,2,1,0:T(8,128)S(1)}, f32[8,2,64,128]{3,2,1,0:T(8,128)S(1)}, u32[]{:S(2)}, u32[]{:S(2)}) %collective-permute-start.15) | collective-permute-done | bytes 524320 | tf_op jit(solution)/shard_map/ppermute | solution.py:183
  176.4 1.2 fusion.1
  177.6 0.2 fusion.33
  177.8 1.1 pad_maximum_fusion
  (23 shorter events, 0.1 us)
Async XLA Ops:
  0.0 6.6 %copy-start.3 = (s32[48]{0:T(128)S(1)}, s32[48]{0:T(128)}, u32[]{:S(2)}) copy-start(s32[48]{0:T(128)} %param.11) | copy-start | bytes 580
  2.0 21.9 %copy-start = (bf16[24,2,64,64]{3,1,2,0:T(2,128)(2,1)}, bf16[24,2,64,64]{3,1,2,0:T(2,128)(2,1)S(1)}, u32[]{:S(2)}) copy-start(bf16[24,2,64,64]{3,1,2,0:T(2,128)(2,1)S(1)} %copy.19) | copy-start | bytes 1179652
  3.1 22.7 %copy-start.2 = (s32[192,4]{0,1:T(4,128)S(1)}, s32[192,4]{0,1:T(4,128)}, u32[]{:S(2)}) copy-start(s32[192,4]{0,1:T(4,128)} %param.8) | copy-start | bytes 9220
  3.1 12.2 %collective-permute-start.7 = (bf16[24,64,128]{2,1,0:T(8,128)(2,1)}, bf16[24,64,128]{2,1,0:T(8,128)(2,1)S(1)}, u32[]{:S(2)}, u32[]{:S(2)}) collective-permute-start(bf16[24,64,128]{2,1,0:T(8,128)(2,1)} %reshape.358), channel_id=1, source_target_pairs={{0,1},{1,2},{2,3},{3,0},{4,5},{5,6},{6,7},{7,4},{8,9},{9,10},{10,1... | collective-permute-start | bytes 1179656 | tf_op jit(solution)/shard_map/ppermute | solution.py:127
  4.6 19.2 %collective-permute-start.8 = (bf16[24,64,128]{2,1,0:T(8,128)(2,1)}, bf16[24,64,128]{2,1,0:T(8,128)(2,1)S(1)}, u32[]{:S(2)}, u32[]{:S(2)}) collective-permute-start(bf16[24,64,128]{2,1,0:T(8,128)(2,1)} %reshape.358), channel_id=1, source_target_pairs={{0,2},{1,3},{2,0},{3,1},{4,6},{5,7},{6,4},{7,5},{8,10},{9,11},{10,... | collective-permute-start | bytes 1179656 | tf_op jit(solution)/shard_map/ppermute | solution.py:127
  5.1 18.8 %collective-permute-start.9 = (bf16[24,64,128]{2,1,0:T(8,128)(2,1)}, bf16[24,64,128]{2,1,0:T(8,128)(2,1)S(1)}, u32[]{:S(2)}, u32[]{:S(2)}) collective-permute-start(bf16[24,64,128]{2,1,0:T(8,128)(2,1)} %reshape.358), channel_id=1, source_target_pairs={{0,3},{1,0},{2,1},{3,2},{4,7},{5,4},{6,5},{7,6},{8,11},{9,8},{10,9... | collective-permute-start | bytes 1179656 | tf_op jit(solution)/shard_map/ppermute | solution.py:127
  6.6 21.8 %collective-permute-start = (s32[48]{0:T(128)S(1)}, s32[48]{0:T(128)S(1)}, u32[]{:S(2)}, u32[]{:S(2)}) collective-permute-start(s32[48]{0:T(128)S(1)} %copy-done.3), channel_id=1, source_target_pairs={{0,1},{1,2},{2,3},{3,0},{4,5},{5,6},{6,7},{7,4},{8,9},{9,10},{10,1... | collective-permute-start | bytes 584 | tf_op jit(solution)/shard_map/ppermute | solution.py:127
  8.0 20.5 %collective-permute-start.1 = (s32[48]{0:T(128)S(1)}, s32[48]{0:T(128)S(1)}, u32[]{:S(2)}, u32[]{:S(2)}) collective-permute-start(s32[48]{0:T(128)S(1)} %copy-done.3), channel_id=1, source_target_pairs={{0,2},{1,3},{2,0},{3,1},{4,6},{5,7},{6,4},{7,5},{8,10},{9,11},{10,... | collective-permute-start | bytes 584 | tf_op jit(solution)/shard_map/ppermute | solution.py:127
  15.3 13.2 %collective-permute-start.2 = (s32[48]{0:T(128)S(1)}, s32[48]{0:T(128)}, u32[]{:S(2)}, u32[]{:S(2)}) collective-permute-start(s32[48]{0:T(128)S(1)} %copy-done.3), channel_id=1, source_target_pairs={{0,3},{1,0},{2,1},{3,2},{4,7},{5,4},{6,5},{7,6},{8,11},{9,8},{10,9... | collective-permute-start | bytes 584 | tf_op jit(solution)/shard_map/ppermute | solution.py:127
  23.9 24.7 %copy-start.1 = (bf16[96,64,128]{2,1,0:T(8,128)(2,1)}, bf16[96,64,128]{2,1,0:T(8,128)(2,1)S(1)}, u32[]{:S(2)}) copy-start(bf16[96,64,128]{2,1,0:T(8,128)(2,1)S(1)} %constant_dynamic-update-slice_fusion.rest_2_) | copy-start | bytes 4718596
  23.9 43.8 %collective-permute-start.10 = (bf16[96,64,128]{2,1,0:T(8,128)(2,1)S(1)}, bf16[96,64,128]{2,1,0:T(8,128)(2,1)}, u32[]{:S(2)}, u32[]{:S(2)}) collective-permute-start(bf16[96,64,128]{2,1,0:T(8,128)(2,1)S(1)} %constant_dynamic-update-slice_fusion.rest_2_), channel_id=1, source_target_pairs={{28,0},{0,4},{4,8},{8,12},{12,16},{16,20},{20,24},{24,28},{29,1},{... | collective-permute-start | bytes 4718600 | tf_op jit(solution)/shard_map/ppermute | solution.py:17
  24.0 45.5 %collective-permute-start.12 = (bf16[96,64,128]{2,1,0:T(8,128)(2,1)S(1)}, bf16[96,64,128]{2,1,0:T(8,128)(2,1)}, u32[]{:S(2)}, u32[]{:S(2)}) collective-permute-start(bf16[96,64,128]{2,1,0:T(8,128)(2,1)S(1)} %constant_dynamic-update-slice_fusion.rest_2_), channel_id=1, source_target_pairs={{4,0},{8,4},{12,8},{16,12},{20,16},{24,20},{28,24},{0,28},{5,1},{9... | collective-permute-start | bytes 4718600 | tf_op jit(solution)/shard_map/ppermute | solution.py:17
  29.1 31.7 %collective-permute-start.3 = (s32[192]{0:T(256)S(1)}, s32[192]{0:T(256)S(1)}, u32[]{:S(2)}, u32[]{:S(2)}) collective-permute-start(s32[192]{0:T(256)S(1)} %pad_add_fusion), channel_id=1, source_target_pairs={{28,0},{0,4},{4,8},{8,12},{12,16},{16,20},{20,24},{24,28},{29,1},{... | collective-permute-start | bytes 2312 | tf_op jit(solution)/shard_map/ppermute | solution.py:17
  29.1 31.7 %collective-permute-start.5 = (s32[192]{0:T(256)S(1)}, s32[192]{0:T(256)S(1)}, u32[]{:S(2)}, u32[]{:S(2)}) collective-permute-start(s32[192]{0:T(256)S(1)} %pad_add_fusion), channel_id=1, source_target_pairs={{4,0},{8,4},{12,8},{16,12},{20,16},{24,20},{28,24},{0,28},{5,1},{9... | collective-permute-start | bytes 2312 | tf_op jit(solution)/shard_map/ppermute | solution.py:17
  60.8 3.0 %collective-permute-start.4 = (s32[192]{0:T(256)S(1)}, s32[192]{0:T(256)S(1)}, u32[]{:S(2)}, u32[]{:S(2)}) collective-permute-start(s32[192]{0:T(256)S(1)} %collective-permute-done.3), channel_id=1, source_target_pairs={{28,0},{0,4},{4,8},{8,12},{12,16},{16,20},{20,24},{24,28},{29,1},{... | collective-permute-start | bytes 2312 | tf_op jit(solution)/shard_map/ppermute | solution.py:17
  60.8 3.0 %collective-permute-start.6 = (s32[192]{0:T(256)S(1)}, s32[192]{0:T(256)S(1)}, u32[]{:S(2)}, u32[]{:S(2)}) collective-permute-start(s32[192]{0:T(256)S(1)} %collective-permute-done.5), channel_id=1, source_target_pairs={{4,0},{8,4},{12,8},{16,12},{20,16},{24,20},{28,24},{0,28},{5,1},{9... | collective-permute-start | bytes 2312 | tf_op jit(solution)/shard_map/ppermute | solution.py:17
  67.7 37.1 %collective-permute-start.11 = (bf16[96,64,128]{2,1,0:T(8,128)(2,1)}, bf16[96,64,128]{2,1,0:T(8,128)(2,1)}, u32[]{:S(2)}, u32[]{:S(2)}) collective-permute-start(bf16[96,64,128]{2,1,0:T(8,128)(2,1)} %collective-permute-done.10.rest_1_), channel_id=1, source_target_pairs={{28,0},{0,4},{4,8},{8,12},{12,16},{16,20},{20,24},{24,28},{29,1},{... | collective-permute-start | bytes 4718600 | tf_op jit(solution)/shard_map/ppermute | solution.py:17
  69.5 35.2 %collective-permute-start.13 = (bf16[96,64,128]{2,1,0:T(8,128)(2,1)}, bf16[96,64,128]{2,1,0:T(8,128)(2,1)}, u32[]{:S(2)}, u32[]{:S(2)}) collective-permute-start(bf16[96,64,128]{2,1,0:T(8,128)(2,1)} %collective-permute-done.12.rest_3_), channel_id=1, source_target_pairs={{4,0},{8,4},{12,8},{16,12},{20,16},{24,20},{28,24},{0,28},{5,1},{9... | collective-permute-start | bytes 4718600 | tf_op jit(solution)/shard_map/ppermute | solution.py:17
  150.7 14.8 %collective-permute-start.14 = (f32[8,2,64,128]{3,2,1,0:T(8,128)S(1)}, f32[8,2,64,128]{3,2,1,0:T(8,128)S(1)}, u32[]{:S(2)}, u32[]{:S(2)}) collective-permute-start(f32[8,2,64,128]{3,2,1,0:T(8,128)S(1)} %get-tuple-element.19), channel_id=1, source_target_pairs={{0,1},{1,2},{2,3},{3,0},{4,5},{5,6},{6,7},{7,4},{8,9},{9,10},{10,1... | collective-permute-start | bytes 1572872 | tf_op jit(solution)/shard_map/ppermute | solution.py:183
  152.0 24.4 %collective-permute-start.15 = (f32[8,2,64,128]{3,2,1,0:T(8,128)S(1)}, f32[8,2,64,128]{3,2,1,0:T(8,128)S(1)}, u32[]{:S(2)}, u32[]{:S(2)}) collective-permute-start(f32[8,2,64,128]{3,2,1,0:T(8,128)S(1)} %get-tuple-element.21), channel_id=1, source_target_pairs={{0,2},{1,3},{2,0},{3,1},{4,6},{5,7},{6,4},{7,5},{8,10},{9,11},{10,... | collective-permute-start | bytes 1572872 | tf_op jit(solution)/shard_map/ppermute | solution.py:183
  152.5 23.9 %collective-permute-start.16 = (f32[8,2,64,128]{3,2,1,0:T(8,128)S(1)}, f32[8,2,64,128]{3,2,1,0:T(8,128)S(1)}, u32[]{:S(2)}, u32[]{:S(2)}) collective-permute-start(f32[8,2,64,128]{3,2,1,0:T(8,128)S(1)} %get-tuple-element.20), channel_id=1, source_target_pairs={{0,3},{1,0},{2,1},{3,2},{4,7},{5,4},{6,5},{7,6},{8,11},{9,8},{10,9... | collective-permute-start | bytes 1572872 | tf_op jit(solution)/shard_map/ppermute | solution.py:183

commit v5 on v4

--- a/solution.py
+++ b/solution.py
@@ -17,7 +17,7 @@
     return lax.ppermute(block, axis, route)
 
 
-def coarse_kernel(pair_ref, half_ref, target_ref, live_ref, own_pos_ref, values_ref, own_t_ref, *rest):
+def coarse_kernel(pair_ref, half_ref, target_ref, live_ref, own_pos_ref, values_ref, *rest):
     pieces = rest[:5]
     out_ref, acc_ref, window, sems = rest[5:]
     step = pl.program_id(0)
@@ -42,7 +42,10 @@
 
     def row_body(r, carry):
         row = step * rows_here + r
-        own_t = own_t_ref[own_pos_ref[row]]
+        own_pair = window[2 * piece_rows + own_pos_ref[row] // 2].astype(jnp.float32)
+        spread = jnp.concatenate([own_pair, jnp.zeros_like(own_pair)], axis=0).T
+        own_t = jnp.where(row % 2 == 0, spread[:bs], spread[bs:])[:, :bs]
+        own_t = own_t.astype(jnp.bfloat16)
         results = []
         for s in range(slots):
             n = row * slots + s
@@ -75,7 +78,7 @@
         lax.fori_loop(0, out_ref.shape[0], pack, 0)
 
 
-def coarse_partial(pair, half, target, live, own_pos, values, own_t, pieces, n_targets):
+def coarse_partial(pair, half, target, live, own_pos, values, pieces, n_targets):
     panel_length, slots, bs, _ = values.shape
     rows_per_step = min(ROWS_PER_STEP, panel_length)
     grid = (panel_length // rows_per_step,)
@@ -88,7 +91,6 @@
             grid=grid,
             in_specs=[
                 pl.BlockSpec((rows_per_step, slots, bs, bs), lambda i, *_: (i, 0, 0, 0)),
-                pl.BlockSpec(memory_space=pltpu.VMEM),
             ]
             + [pl.BlockSpec(memory_space=pl.ANY)] * 5,
             out_specs=pl.BlockSpec((n_targets // 2, bs, lanes), lambda i, *_: (0, 0, 0)),
@@ -102,7 +104,7 @@
             dimension_semantics=("arbitrary",),
             vmem_limit_bytes=60 * 1024 * 1024,
         ),
-    )(pair, half, target, live, own_pos, values, own_t, *pieces)
+    )(pair, half, target, live, own_pos, values, *pieces)
 
 
 def local(block_values, block_columns, row_counts, prolong_blocks, aggregates):
@@ -159,11 +161,6 @@
     target = fetched_aggs * CB + jnp.broadcast_to(
         local_coarse[:, None], (panel_length, slots_here)
     ).reshape(slot_total)
-    own_t = (
-        paired.reshape(panel_length // 2, block_size, 2, block_size)
-        .transpose(0, 2, 3, 1)
-        .reshape(panel_length, block_size, block_size)
-    )
     summed = coarse_partial(
         (local_rows // 2).astype(jnp.int32),
         (local_rows % 2).astype(jnp.int32),
@@ -171,7 +168,6 @@
         live,
         own_pos,
         block_values,
-        own_t,
         [piece[0] for piece in pieces],
         coarse_count * CB,
     )

time: 182 us -> 181 us (level)
  waiting for transfers between devices: 62.7 us -> 86.6 us
  local copies, waits for them, and re-layouts: 38.3 us -> 26.5 us
  other arithmetic: 15.4 us -> 5.9 us
  starting transfers between devices: 17.6 us -> 15.7 us
    ppermute x8, waiting for transfers between devices: 28 us -> 45.3 us  [passed_along(): return lax.ppermute(block, axis, route)]
    transpose x1 -> x0, other arithmetic: 8.21 us -> none  [local(): own_t = paired.reshape(panel_length // 2, block_size, 2, block_size).tran...]
    transpose x1 -> x0, local copies, waits for them, and re-layouts: 5.74 us -> none  [local(): own_t = paired.reshape(panel_length // 2, block_size, 2, block_size).tran...]
    ppermute x6, waiting for transfers between devices: 11.7 us -> 16.9 us  [local(): lax.ppermute((local_pairs, aggregates), 'grp', [(i, (i + k) % group_size)...]
    concatenate x4 -> x1, local copies, waits for them, and re-layouts: 3.79 us -> 0.05 us  [local(): paired = jnp.concatenate([piece[0] for piece in received], axis=0)]
    unnamed x12 -> x14, local copies, waits for them, and re-layouts: 18.2 us -> 17.2 us
  transfers between devices with their start and end apart: 17 -> 17, of which waited for: 7 -> 7; matrix products, arithmetic and copies ran while one was open for 26% -> 15% of each run, Pallas kernels for 0% -> 0%
where the time goes in v5:
time: 181 us; the launch traced here: 178 us
  waiting for transfers between devices  86.6 us (48%)
  Pallas kernels  43.4 us (24%)
  local copies, waits for them, and re-layouts  26.5 us (15%)
  starting transfers between devices  15.7 us (9%)
  other arithmetic  5.9 us (3%)
    ppermute x8, waiting for transfers between devices, passed_along(): return lax.ppermute(block, axis, route)  45.3 us
    pallas_call x1, Pallas kernels, coarse_partial(): pl.pallas_call(coarse_kernel, out_shape=jax.ShapeDtypeStruct((n_targets /...  43.4 us
    ppermute x3, waiting for transfers between devices, local(): lax.ppermute(outgoing, 'grp', [(i, (i + k) % group_size) for i in range(g...  24.4 us
    unnamed x14, local copies, waits for them, and re-layouts  17.2 us
    ppermute x6, waiting for transfers between devices, local(): lax.ppermute((local_pairs, aggregates), 'grp', [(i, (i + k) % group_size)...  16.9 us
    ppermute x8, starting transfers between devices, passed_along(): return lax.ppermute(block, axis, route)  7.02 us
    ppermute x6, starting transfers between devices, local(): lax.ppermute((local_pairs, aggregates), 'grp', [(i, (i + k) % group_size)...  6.13 us
  transfers between devices with their start and end apart: 17, of which 7 were waited for; matrix products, arithmetic and copies ran while one was open for 15% of the time, Pallas kernels for 0%

profile of v5, /device:TPU:26, one launch (start us, length us, event | category | flops | bytes accessed | tf_op | source)
XLA Modules:
  0.0 178.5 jit_solution(13011001530475385858)
XLA Ops:
  0.0 1.9 %copy.17 = bf16[24,2,64,64]{3,1,2,0:T(2,128)(2,1)S(1)} copy(bf16[24,2,64,64]{3,2,1,0:T(8,128)(2,1)} %bitcast.22) | data formatting | bytes 786432 | tf_op jit(solution)/shard_map/reshape | solution.py:122
  1.9 0.3 reshape.349
  2.3 0.0 copy-start.3
  2.3 0.0 copy-start.2
  2.3 1.5 collective-permute-start.7
  3.9 0.5 collective-permute-start.8
  4.4 1.5 collective-permute-start.9
  5.9 0.0 copy-start.4
  6.0 8.4 %collective-permute-done.7 = bf16[24,64,128]{2,1,0:T(8,128)(2,1)S(1)} collective-permute-done((bf16[24,64,128]{2,1,0:T(8,128)(2,1)S(1)}, bf16[24,64,128]{2,1,0:T(8,128)(2,1)S(1)}, u32[]{:S(2)}, u32[]{:S(2)}) %collective-permute-start.7) | collective-permute-done | bytes 393248 | tf_op jit(solution)/shard_map/ppermute | solution.py:129
  14.4 0.1 constant_dynamic-update-slice_fusion.2
  14.4 8.5 %collective-permute-done.8 = bf16[24,64,128]{2,1,0:T(8,128)(2,1)S(1)} collective-permute-done((bf16[24,64,128]{2,1,0:T(8,128)(2,1)S(1)}, bf16[24,64,128]{2,1,0:T(8,128)(2,1)S(1)}, u32[]{:S(2)}, u32[]{:S(2)}) %collective-permute-start.8) | collective-permute-done | bytes 393248 | tf_op jit(solution)/shard_map/ppermute | solution.py:129
  22.9 0.1 constant_dynamic-update-slice_fusion.1
  22.9 0.0 collective-permute-done.9
  22.9 0.1 constant_dynamic-update-slice_fusion.rest_2_
  23.0 0.1 collective-permute-start.10
  23.1 1.7 collective-permute-start.12
  24.8 1.2 collective-permute-start
  26.0 0.5 collective-permute-start.1
  26.5 0.8 collective-permute-start.2
  27.3 0.1 copy.10
  27.5 0.1 div.70
  27.6 0.1 div.65
  27.7 0.1 copy.9
  27.8 0.1 rem.290
  27.9 0.1 rem.264
  28.1 0.2 copy.8
  28.2 0.1 ne.303
  28.4 0.1 ne.293
  28.5 31.2 %collective-permute-done.10.rest_1_ = bf16[96,64,128]{2,1,0:T(8,128)(2,1)S(1)} collective-permute-done((bf16[96,64,128]{2,1,0:T(8,128)(2,1)S(1)}, bf16[96,64,128]{2,1,0:T(8,128)(2,1)S(1)}, u32[]{:S(2)}, u32[]{:S(2)}) %collective-permute-start.10) | collective-permute-done | bytes 1572896 | tf_op jit(solution)/shard_map/ppermute | solution.py:17
  59.7 0.0 collective-permute-start.11
  59.8 0.0 collective-permute-done.12.rest_3_
  59.8 1.7 collective-permute-start.13
  61.5 0.6 fusion.24.own_pos_ref
  62.1 0.1 fusion.14
  62.2 0.1 compare_convert_fusion
  62.3 0.0 collective-permute-done.1
  62.3 0.0 collective-permute-done.2
  62.4 0.1 pad_add_fusion
  62.4 1.7 collective-permute-start.5
  64.2 0.7 reshape.415.live_ref
  64.9 17.0 %copy.15.values_ref = bf16[192,4,64,64]{3,2,1,0:T(8,128)(2,1)} copy(bf16[192,4,64,64]{0,3,2,1:T(8,128)(2,1)} %param.7) | data formatting | bytes 12582912 | tf_op args[0]
  81.9 1.6 gather_fusion.1
  83.5 13.1 %collective-permute-done.3 = s32[192]{0:T(256)S(1)} collective-permute-done((s32[192]{0:T(256)S(1)}, s32[192]{0:T(256)S(1)}, u32[]{:S(2)}, u32[]{:S(2)}) %collective-permute-start.3) | collective-permute-done | bytes 800 | tf_op jit(solution)/shard_map/ppermute | solution.py:17
  96.6 0.0 collective-permute-start.4
  96.6 0.0 collective-permute-done.5
  96.6 1.7 collective-permute-start.6
  98.3 0.1 broadcast_in_dim.31
  98.4 0.1 reshape.347
  98.5 1.0 collective-permute-done.4
  99.6 0.1 collective-permute-done.6
  99.6 0.1 concatenate.14
  99.7 3.2 %gather_fusion = s32[768]{0:T(1024)S(1)} fusion(s32[960]{0:T(1024)S(1)} %concatenate.14, s32[1024]{0:T(1024)S(1)} %pad_clamp_fusion.1), kind=kCustom, calls=%fused_computation | custom fusion | bytes 9216 | tf_op jit(solution)/shard_map/jit(_take)/gather | solution.py:157
  102.9 0.6 multiply_add_fusion
  103.5 0.6 add_select_fusion.1
  104.1 43.4 %shard_map.55 = f32[64,64,128]{2,1,0:T(8,128)} custom-call(s32[768]{0:T(1024)} %get-tuple-element.25.pair_ref, s32[768]{0:T(1024)} %get-tuple-element.24.half_ref, s32[768]{0:T(1024)} %get-tuple-element.17.target_ref, s32[768]{0:T(1024)} %reshape.415.live_ref, s32[192]{0:T(256)} %fusion.24.own_pos_ref, bf16[192,4,64,64]{3,2,1,0:T(8,128)(2,1)} %copy.15.values_ref, ...), custom_call_target="tpu_custom_call" | custom-call | tf_op jit(solution)/shard_map/pallas_call | solution.py:86
  147.6 1.5 select_bitcast_fusion.2
  149.0 1.2 collective-permute-start.14
  150.3 0.5 collective-permute-start.15
  150.8 0.8 collective-permute-start.16
  151.6 12.3 %collective-permute-done.14 = f32[8,2,64,128]{3,2,1,0:T(8,128)S(1)} collective-permute-done((f32[8,2,64,128]{3,2,1,0:T(8,128)S(1)}, f32[8,2,64,128]{3,2,1,0:T(8,128)S(1)}, u32[]{:S(2)}, u32[]{:S(2)}) %collective-permute-start.14) | collective-permute-done | bytes 524320 | tf_op jit(solution)/shard_map/ppermute | solution.py:179
  163.9 12.1 %collective-permute-done.15 = f32[8,2,64,128]{3,2,1,0:T(8,128)S(1)} collective-permute-done((f32[8,2,64,128]{3,2,1,0:T(8,128)S(1)}, f32[8,2,64,128]{3,2,1,0:T(8,128)S(1)}, u32[]{:S(2)}, u32[]{:S(2)}) %collective-permute-start.15) | collective-permute-done | bytes 524320 | tf_op jit(solution)/shard_map/ppermute | solution.py:179
  176.0 1.2 fusion.1
  177.2 0.2 fusion.33
  177.4 1.1 pad_maximum_fusion
  (20 shorter events, 0.1 us)
Async XLA Ops:
  2.3 22.5 %copy-start.3 = (s32[48]{0:T(128)S(1)}, s32[48]{0:T(128)}, u32[]{:S(2)}) copy-start(s32[48]{0:T(128)} %param.11) | copy-start | bytes 580
  2.3 25.0 %copy-start.2 = (s32[192,4]{0,1:T(4,128)S(1)}, s32[192,4]{0,1:T(4,128)}, u32[]{:S(2)}) copy-start(s32[192,4]{0,1:T(4,128)} %param.8) | copy-start | bytes 9220
  2.3 12.0 %collective-permute-start.7 = (bf16[24,64,128]{2,1,0:T(8,128)(2,1)S(1)}, bf16[24,64,128]{2,1,0:T(8,128)(2,1)S(1)}, u32[]{:S(2)}, u32[]{:S(2)}) collective-permute-start(bf16[24,64,128]{2,1,0:T(8,128)(2,1)S(1)} %reshape.349), channel_id=1, source_target_pairs={{0,1},{1,2},{2,3},{3,0},{4,5},{5,6},{6,7},{7,4},{8,9},{9,10},{10,1... | collective-permute-start | bytes 1179656 | tf_op jit(solution)/shard_map/ppermute | solution.py:129
  3.9 19.0 %collective-permute-start.8 = (bf16[24,64,128]{2,1,0:T(8,128)(2,1)S(1)}, bf16[24,64,128]{2,1,0:T(8,128)(2,1)S(1)}, u32[]{:S(2)}, u32[]{:S(2)}) collective-permute-start(bf16[24,64,128]{2,1,0:T(8,128)(2,1)S(1)} %reshape.349), channel_id=1, source_target_pairs={{0,2},{1,3},{2,0},{3,1},{4,6},{5,7},{6,4},{7,5},{8,10},{9,11},{10,... | collective-permute-start | bytes 1179656 | tf_op jit(solution)/shard_map/ppermute | solution.py:129
  4.4 18.6 %collective-permute-start.9 = (bf16[24,64,128]{2,1,0:T(8,128)(2,1)S(1)}, bf16[24,64,128]{2,1,0:T(8,128)(2,1)S(1)}, u32[]{:S(2)}, u32[]{:S(2)}) collective-permute-start(bf16[24,64,128]{2,1,0:T(8,128)(2,1)S(1)} %reshape.349), channel_id=1, source_target_pairs={{0,3},{1,0},{2,1},{3,2},{4,7},{5,4},{6,5},{7,6},{8,11},{9,8},{10,9... | collective-permute-start | bytes 1179656 | tf_op jit(solution)/shard_map/ppermute | solution.py:129
  5.9 56.3 %copy-start.4 = (s32[192]{0:T(256)S(1)}, s32[192]{0:T(256)}, u32[]{:S(2)}) copy-start(s32[192]{0:T(256)} %param.9) | copy-start | bytes 2308
  23.0 58.9 %copy-start = (bf16[96,64,128]{2,1,0:T(8,128)(2,1)}, bf16[96,64,128]{2,1,0:T(8,128)(2,1)S(1)}, u32[]{:S(2)}) copy-start(bf16[96,64,128]{2,1,0:T(8,128)(2,1)S(1)} %constant_dynamic-update-slice_fusion.rest_2_) | copy-start | bytes 4718596
  23.0 36.7 %collective-permute-start.10 = (bf16[96,64,128]{2,1,0:T(8,128)(2,1)S(1)}, bf16[96,64,128]{2,1,0:T(8,128)(2,1)S(1)}, u32[]{:S(2)}, u32[]{:S(2)}) collective-permute-start(bf16[96,64,128]{2,1,0:T(8,128)(2,1)S(1)} %constant_dynamic-update-slice_fusion.rest_2_), channel_id=1, source_target_pairs={{28,0},{0,4},{4,8},{8,12},{12,16},{16,20},{20,24},{24,28},{29,1},{... | collective-permute-start | bytes 4718600 | tf_op jit(solution)/shard_map/ppermute | solution.py:17
  23.1 36.7 %collective-permute-start.12 = (bf16[96,64,128]{2,1,0:T(8,128)(2,1)S(1)}, bf16[96,64,128]{2,1,0:T(8,128)(2,1)}, u32[]{:S(2)}, u32[]{:S(2)}) collective-permute-start(bf16[96,64,128]{2,1,0:T(8,128)(2,1)S(1)} %constant_dynamic-update-slice_fusion.rest_2_), channel_id=1, source_target_pairs={{4,0},{8,4},{12,8},{16,12},{20,16},{24,20},{28,24},{0,28},{5,1},{9... | collective-permute-start | bytes 4718600 | tf_op jit(solution)/shard_map/ppermute | solution.py:17
  24.8 37.5 %collective-permute-start = (s32[48]{0:T(128)S(1)}, s32[48]{0:T(128)S(1)}, u32[]{:S(2)}, u32[]{:S(2)}) collective-permute-start(s32[48]{0:T(128)S(1)} %copy-done.3), channel_id=1, source_target_pairs={{0,1},{1,2},{2,3},{3,0},{4,5},{5,6},{6,7},{7,4},{8,9},{9,10},{10,1... | collective-permute-start | bytes 584 | tf_op jit(solution)/shard_map/ppermute | solution.py:129
  26.0 36.4 %collective-permute-start.1 = (s32[48]{0:T(128)S(1)}, s32[48]{0:T(128)S(1)}, u32[]{:S(2)}, u32[]{:S(2)}) collective-permute-start(s32[48]{0:T(128)S(1)} %copy-done.3), channel_id=1, source_target_pairs={{0,2},{1,3},{2,0},{3,1},{4,6},{5,7},{6,4},{7,5},{8,10},{9,11},{10,... | collective-permute-start | bytes 584 | tf_op jit(solution)/shard_map/ppermute | solution.py:129
  26.5 35.8 %collective-permute-start.2 = (s32[48]{0:T(128)S(1)}, s32[48]{0:T(128)S(1)}, u32[]{:S(2)}, u32[]{:S(2)}) collective-permute-start(s32[48]{0:T(128)S(1)} %copy-done.3), channel_id=1, source_target_pairs={{0,3},{1,0},{2,1},{3,2},{4,7},{5,4},{6,5},{7,6},{8,11},{9,8},{10,9... | collective-permute-start | bytes 584 | tf_op jit(solution)/shard_map/ppermute | solution.py:129
  59.7 22.1 %copy-start.1 = (bf16[96,64,128]{2,1,0:T(8,128)(2,1)}, bf16[96,64,128]{2,1,0:T(8,128)(2,1)S(1)}, u32[]{:S(2)}) copy-start(bf16[96,64,128]{2,1,0:T(8,128)(2,1)S(1)} %collective-permute-done.10.rest_1_) | copy-start | bytes 4718596
  59.7 44.4 %collective-permute-start.11 = (bf16[96,64,128]{2,1,0:T(8,128)(2,1)S(1)}, bf16[96,64,128]{2,1,0:T(8,128)(2,1)}, u32[]{:S(2)}, u32[]{:S(2)}) collective-permute-start(bf16[96,64,128]{2,1,0:T(8,128)(2,1)S(1)} %collective-permute-done.10.rest_1_), channel_id=1, source_target_pairs={{28,0},{0,4},{4,8},{8,12},{12,16},{16,20},{20,24},{24,28},{29,1},{... | collective-permute-start | bytes 4718600 | tf_op jit(solution)/shard_map/ppermute | solution.py:17
  59.8 44.4 %collective-permute-start.13 = (bf16[96,64,128]{2,1,0:T(8,128)(2,1)}, bf16[96,64,128]{2,1,0:T(8,128)(2,1)}, u32[]{:S(2)}, u32[]{:S(2)}) collective-permute-start(bf16[96,64,128]{2,1,0:T(8,128)(2,1)} %collective-permute-done.12.rest_3_), channel_id=1, source_target_pairs={{4,0},{8,4},{12,8},{16,12},{20,16},{24,20},{28,24},{0,28},{5,1},{9... | collective-permute-start | bytes 4718600 | tf_op jit(solution)/shard_map/ppermute | solution.py:17
  62.4 34.1 %collective-permute-start.3 = (s32[192]{0:T(256)S(1)}, s32[192]{0:T(256)S(1)}, u32[]{:S(2)}, u32[]{:S(2)}) collective-permute-start(s32[192]{0:T(256)S(1)} %pad_add_fusion), channel_id=1, source_target_pairs={{28,0},{0,4},{4,8},{8,12},{12,16},{16,20},{20,24},{24,28},{29,1},{... | collective-permute-start | bytes 2312 | tf_op jit(solution)/shard_map/ppermute | solution.py:17
  62.4 34.1 %collective-permute-start.5 = (s32[192]{0:T(256)S(1)}, s32[192]{0:T(256)S(1)}, u32[]{:S(2)}, u32[]{:S(2)}) collective-permute-start(s32[192]{0:T(256)S(1)} %pad_add_fusion), channel_id=1, source_target_pairs={{4,0},{8,4},{12,8},{16,12},{20,16},{24,20},{28,24},{0,28},{5,1},{9... | collective-permute-start | bytes 2312 | tf_op jit(solution)/shard_map/ppermute | solution.py:17
  96.6 3.0 %collective-permute-start.4 = (s32[192]{0:T(256)S(1)}, s32[192]{0:T(256)S(1)}, u32[]{:S(2)}, u32[]{:S(2)}) collective-permute-start(s32[192]{0:T(256)S(1)} %collective-permute-done.3), channel_id=1, source_target_pairs={{28,0},{0,4},{4,8},{8,12},{12,16},{16,20},{20,24},{24,28},{29,1},{... | collective-permute-start | bytes 2312 | tf_op jit(solution)/shard_map/ppermute | solution.py:17
  96.6 3.0 %collective-permute-start.6 = (s32[192]{0:T(256)S(1)}, s32[192]{0:T(256)S(1)}, u32[]{:S(2)}, u32[]{:S(2)}) collective-permute-start(s32[192]{0:T(256)S(1)} %collective-permute-done.5), channel_id=1, source_target_pairs={{4,0},{8,4},{12,8},{16,12},{20,16},{24,20},{28,24},{0,28},{5,1},{9... | collective-permute-start | bytes 2312 | tf_op jit(solution)/shard_map/ppermute | solution.py:17
  149.0 14.8 %collective-permute-start.14 = (f32[8,2,64,128]{3,2,1,0:T(8,128)S(1)}, f32[8,2,64,128]{3,2,1,0:T(8,128)S(1)}, u32[]{:S(2)}, u32[]{:S(2)}) collective-permute-start(f32[8,2,64,128]{3,2,1,0:T(8,128)S(1)} %get-tuple-element.19), channel_id=1, source_target_pairs={{0,1},{1,2},{2,3},{3,0},{4,5},{5,6},{6,7},{7,4},{8,9},{9,10},{10,1... | collective-permute-start | bytes 1572872 | tf_op jit(solution)/shard_map/ppermute | solution.py:179
  150.3 25.7 %collective-permute-start.15 = (f32[8,2,64,128]{3,2,1,0:T(8,128)S(1)}, f32[8,2,64,128]{3,2,1,0:T(8,128)S(1)}, u32[]{:S(2)}, u32[]{:S(2)}) collective-permute-start(f32[8,2,64,128]{3,2,1,0:T(8,128)S(1)} %get-tuple-element.21), channel_id=1, source_target_pairs={{0,2},{1,3},{2,0},{3,1},{4,6},{5,7},{6,4},{7,5},{8,10},{9,11},{10,... | collective-permute-start | bytes 1572872 | tf_op jit(solution)/shard_map/ppermute | solution.py:179
  150.8 25.2 %collective-permute-start.16 = (f32[8,2,64,128]{3,2,1,0:T(8,128)S(1)}, f32[8,2,64,128]{3,2,1,0:T(8,128)S(1)}, u32[]{:S(2)}, u32[]{:S(2)}) collective-permute-start(f32[8,2,64,128]{3,2,1,0:T(8,128)S(1)} %get-tuple-element.20), channel_id=1, source_target_pairs={{0,3},{1,0},{2,1},{3,2},{4,7},{5,4},{6,5},{7,6},{8,11},{9,8},{10,9... | collective-permute-start | bytes 1572872 | tf_op jit(solution)/shard_map/ppermute | solution.py:179

commit v6 on v5

--- a/solution.py
+++ b/solution.py
@@ -18,8 +18,8 @@
 
 
 def coarse_kernel(pair_ref, half_ref, target_ref, live_ref, own_pos_ref, values_ref, *rest):
-    pieces = rest[:5]
-    out_ref, acc_ref, window, sems = rest[5:]
+    pieces = rest[:-4]
+    out_ref, acc_ref, window, sems = rest[-4:]
     step = pl.program_id(0)
     rows_here, slots, bs, _ = values_ref.shape
     piece_rows = pieces[0].shape[0]
@@ -42,7 +42,7 @@
 
     def row_body(r, carry):
         row = step * rows_here + r
-        own_pair = window[2 * piece_rows + own_pos_ref[row] // 2].astype(jnp.float32)
+        own_pair = window[own_pos_ref[row]].astype(jnp.float32)
         spread = jnp.concatenate([own_pair, jnp.zeros_like(own_pair)], axis=0).T
         own_t = jnp.where(row % 2 == 0, spread[:bs], spread[bs:])[:, :bs]
         own_t = own_t.astype(jnp.bfloat16)
@@ -92,12 +92,12 @@
             in_specs=[
                 pl.BlockSpec((rows_per_step, slots, bs, bs), lambda i, *_: (i, 0, 0, 0)),
             ]
-            + [pl.BlockSpec(memory_space=pl.ANY)] * 5,
+            + [pl.BlockSpec(memory_space=pl.ANY)] * len(pieces),
             out_specs=pl.BlockSpec((n_targets // 2, bs, lanes), lambda i, *_: (0, 0, 0)),
             scratch_shapes=[
                 pltpu.VMEM((n_targets, bs, lanes), jnp.float32),
-                pltpu.VMEM((5 * piece_rows, bs, lanes), jnp.bfloat16),
-                pltpu.SemaphoreType.DMA((5,)),
+                pltpu.VMEM((len(pieces) * piece_rows, bs, lanes), jnp.bfloat16),
+                pltpu.SemaphoreType.DMA((len(pieces),)),
             ],
         ),
         compiler_params=pltpu.CompilerParams(
@@ -123,52 +123,55 @@
         .transpose(0, 2, 1, 3)
         .reshape(share_rows // 2, block_size, 2 * block_size)
     )
-    received = [(local_pairs, aggregates)]
+    agg_row = (
+        jnp.zeros((1, block_size, 2 * block_size), jnp.bfloat16)
+        .at[0, 0, :share_rows]
+        .set(aggregates.astype(jnp.bfloat16))
+    )
+    local_ext = jnp.concatenate([local_pairs, agg_row], axis=0)
+    piece_rows = local_ext.shape[0]
+    received = [local_ext]
     for k in range(1, group_size):
         received.append(
             lax.ppermute(
-                (local_pairs, aggregates),
-                "grp",
-                [(i, (i + k) % group_size) for i in range(group_size)],
+                local_ext, "grp", [(i, (i + k) % group_size) for i in range(group_size)]
             )
         )
-    paired = jnp.concatenate([piece[0] for piece in received], axis=0)
-    panel_aggs = jnp.concatenate([piece[1] for piece in received], axis=0)
-
-    def rotated(r):
-        return jnp.mod(group_me - r // share_rows, group_size) * share_rows + r % share_rows
-
-    lower = []
-    upper = []
-    going_down = (paired, panel_aggs)
-    going_up = (paired, panel_aggs)
-    for hop in range(2):
-        going_down = passed_along((going_down[0], going_down[1]), "blk", 1)
-        lower.insert(0, going_down)
-        going_up = passed_along((going_up[0], going_up[1]), "blk", -1)
-        upper.append(going_up)
-    pieces = lower + [(paired, panel_aggs)] + upper
-    window_aggs = jnp.concatenate([piece[1] for piece in pieces], axis=0)
+    down1 = [passed_along(piece, "blk", 1) for piece in received]
+    up1 = [passed_along(piece, "blk", -1) for piece in received]
+    down2 = [passed_along(piece, "blk", 1) for piece in down1]
+    up2 = [passed_along(piece, "blk", -1) for piece in up1]
+    pieces = down2 + down1 + received + up1 + up2
+    flat_aggs = jnp.stack([piece[share_rows // 2, 0, :share_rows] for piece in pieces])
+    flat_aggs = flat_aggs.astype(jnp.int32).reshape(-1)
+
+    def placed(d, r):
+        k = jnp.mod(group_me - r // share_rows, group_size)
+        return d * group_size + k, r % share_rows
+
     wanted = block_columns.reshape(slot_total)
     column_panel = wanted // panel_length
     distance = jnp.mod(column_panel - me + 2, panel_total)
-    local_rows = distance * panel_length + rotated(wanted % panel_length)
-    own_pos = rotated(jnp.arange(panel_length, dtype=jnp.int32))
-    fetched_aggs = jnp.take(window_aggs, local_rows, axis=0)
+    piece_of, within = placed(distance, wanted % panel_length)
+    window_pair = piece_of * piece_rows + within // 2
+    fetched_aggs = jnp.take(flat_aggs, piece_of * share_rows + within, axis=0)
+    own_piece, own_within = placed(2, jnp.arange(panel_length, dtype=jnp.int32))
+    own_pos = own_piece * piece_rows + own_within // 2
+    own_aggs = jnp.take(flat_aggs, own_piece * share_rows + own_within, axis=0)
     slot_ids = lax.axis_index("grp") * slots_here + jnp.arange(slots_here, dtype=jnp.int32)
     live = (slot_ids[None, :] < row_counts[:, None]).astype(jnp.int32).reshape(slot_total)
-    local_coarse = jnp.take(panel_aggs, own_pos, axis=0) - me * CB
+    local_coarse = own_aggs - me * CB
     target = fetched_aggs * CB + jnp.broadcast_to(
         local_coarse[:, None], (panel_length, slots_here)
     ).reshape(slot_total)
     summed = coarse_partial(
-        (local_rows // 2).astype(jnp.int32),
-        (local_rows % 2).astype(jnp.int32),
+        window_pair.astype(jnp.int32),
+        (within % 2).astype(jnp.int32),
         target.astype(jnp.int32),
         live,
         own_pos,
         block_values,
-        [piece[0] for piece in pieces],
+        pieces,
         coarse_count * CB,
     )
     share = coarse_count // group_size

time: 181 us -> 175 us (0.967)
  waiting for transfers between devices: 86.6 us -> 72.4 us
  starting transfers between devices: 15.7 us -> 23.1 us
    ppermute x6 -> x3, waiting for transfers between devices: 16.9 us -> 0.01 us  [local(): lax.ppermute(local_ext, 'grp', [(i, (i + k) % group_size) for i in range(...]
    ppermute x8 -> x16, starting transfers between devices: 7.02 us -> 16 us  [passed_along(): return lax.ppermute(block, axis, route)]
    ppermute x8 -> x16, waiting for transfers between devices: 45.3 us -> 49.2 us  [passed_along(): return lax.ppermute(block, axis, route)]
    ppermute x6 -> x3, starting transfers between devices: 6.13 us -> 4.5 us  [local(): lax.ppermute(local_ext, 'grp', [(i, (i + k) % group_size) for i in range(...]
    unnamed x14 -> x45, local copies, waits for them, and re-layouts: 17.2 us -> 17.8 us
  transfers between devices with their start and end apart: 17 -> 22, of which waited for: 7 -> 11; matrix products, arithmetic and copies ran while one was open for 15% -> 11% of each run, Pallas kernels for 0% -> 0%
where the time goes in v6:
time: 175 us; the launch traced here: 173 us
  waiting for transfers between devices  72.4 us (41%)
  Pallas kernels  43.6 us (25%)
  local copies, waits for them, and re-layouts  26.8 us (15%)
  starting transfers between devices  23.1 us (13%)
  other arithmetic  6.56 us (4%)
    ppermute x16, waiting for transfers between devices, passed_along(): return lax.ppermute(block, axis, route)  49.2 us
    pallas_call x1, Pallas kernels, coarse_partial(): pl.pallas_call(coarse_kernel, out_shape=jax.ShapeDtypeStruct((n_targets /...  43.6 us
    ppermute x3, waiting for transfers between devices, local(): lax.ppermute(outgoing, 'grp', [(i, (i + k) % group_size) for i in range(g...  23.2 us
    unnamed x45, local copies, waits for them, and re-layouts  17.8 us
    ppermute x16, starting transfers between devices, passed_along(): return lax.ppermute(block, axis, route)  16 us
    ppermute x3, starting transfers between devices, local(): lax.ppermute(local_ext, 'grp', [(i, (i + k) % group_size) for i in range(...  4.5 us
  transfers between devices with their start and end apart: 22, of which 11 were waited for; matrix products, arithmetic and copies ran while one was open for 11% of the time, Pallas kernels for 0%

profile of v6, /device:TPU:26, one launch (start us, length us, event | category | flops | bytes accessed | tf_op | source)
XLA Modules:
  0.0 173.0 jit_solution(3720136598876153005)
XLA Ops:
  0.0 0.7 convert_bitcast_fusion
  0.7 2.0 %copy.17 = bf16[24,2,64,64]{3,1,2,0:T(2,128)(2,1)S(1)} copy(bf16[24,2,64,64]{3,2,1,0:T(8,128)(2,1)} %bitcast.64) | data formatting | bytes 786432 | tf_op jit(solution)/shard_map/reshape | solution.py:122
  2.6 0.3 reshape.388
  3.0 0.6 collective-permute-start.8
  3.6 1.5 collective-permute-start.5
  5.1 2.4 %collective-permute-start.2 = (bf16[25,64,128]{2,1,0:T(8,128)(2,1)S(1)}, bf16[25,64,128]{2,1,0:T(8,128)(2,1)S(1)}, u32[]{:S(2)}, u32[]{:S(2)}) collective-permute-start(bf16[25,64,128]{2,1,0:T(8,128)(2,1)S(1)} %fusion.3.rest_8_), channel_id=1, source_target_pairs={{0,1},{1,2},{2,3},{3,0},{4,5},{5,6},{6,7},{7,4},{8,9},{9,10},{10,1... | collective-permute-start | bytes 1228808 | tf_op jit(solution)/shard_map/ppermute | solution.py:136
  7.5 0.0 collective-permute-start
  7.5 1.7 %collective-permute-start.11 = (bf16[25,64,128]{2,1,0:T(8,128)(2,1)S(1)}, bf16[25,64,128]{2,1,0:T(8,128)(2,1)S(1)}, u32[]{:S(2)}, u32[]{:S(2)}) collective-permute-start(bf16[25,64,128]{2,1,0:T(8,128)(2,1)S(1)} %fusion.3.rest_8_), channel_id=1, source_target_pairs={{4,0},{8,4},{12,8},{16,12},{20,16},{24,20},{28,24},{0,28},{5,1},{9... | collective-permute-start | bytes 1228808 | tf_op jit(solution)/shard_map/ppermute | solution.py:17
  9.3 0.1 copy.9
  9.4 0.1 rem.301
  9.6 0.1 rem.276
  9.7 0.1 copy.10
  9.8 0.1 div.78
  9.9 0.1 div.73
  10.0 0.2 copy.8
  10.2 0.1 ne.313
  10.3 0.1 ne.303
  10.5 0.1 compare_convert_fusion
  10.6 0.7 reshape.456.live_ref
  11.3 16.9 %copy.15.values_ref = bf16[192,4,64,64]{3,2,1,0:T(8,128)(2,1)} copy(bf16[192,4,64,64]{0,3,2,1:T(8,128)(2,1)} %param.9) | data formatting | bytes 12582912 | tf_op args[0]
  28.3 0.6 fusion.32.own_pos_ref
  28.9 0.1 fusion.16
  29.0 0.0 collective-permute-done.8.rest_11_
  29.0 0.1 collective-permute-start.14
  29.1 0.0 collective-permute-done.5.rest_10_
  29.1 0.5 collective-permute-start.13
  29.6 0.1 collective-permute-start.9
  29.7 3.5 %collective-permute-start.6 = (bf16[25,64,128]{2,1,0:T(8,128)(2,1)S(1)}, bf16[25,64,128]{2,1,0:T(8,128)(2,1)S(1)}, u32[]{:S(2)}, u32[]{:S(2)}) collective-permute-start(bf16[25,64,128]{2,1,0:T(8,128)(2,1)S(1)} %collective-permute-done.5.rest_10_), channel_id=1, source_target_pairs={{28,0},{0,4},{4,8},{8,12},{12,16},{16,20},{20,24},{24,28},{29,1},{... | collective-permute-start | bytes 1228808 | tf_op jit(solution)/shard_map/ppermute | solution.py:17
  33.2 0.1 collective-permute-start.3
  33.3 9.4 %collective-permute-done.9.rest_7_ = bf16[25,64,128]{2,1,0:T(8,128)(2,1)S(1)} collective-permute-done((bf16[25,64,128]{2,1,0:T(8,128)(2,1)S(1)}, bf16[25,64,128]{2,1,0:T(8,128)(2,1)S(1)}, u32[]{:S(2)}, u32[]{:S(2)}) %collective-permute-start.9) | collective-permute-done | bytes 409632 | tf_op jit(solution)/shard_map/ppermute | solution.py:17
  42.7 8.8 %collective-permute-done.6.rest_6_ = bf16[25,64,128]{2,1,0:T(8,128)(2,1)S(1)} collective-permute-done((bf16[25,64,128]{2,1,0:T(8,128)(2,1)S(1)}, bf16[25,64,128]{2,1,0:T(8,128)(2,1)S(1)}, u32[]{:S(2)}, u32[]{:S(2)}) %collective-permute-start.6) | collective-permute-done | bytes 409632 | tf_op jit(solution)/shard_map/ppermute | solution.py:17
  51.5 1.7 %collective-permute-start.15 = (bf16[25,64,128]{2,1,0:T(8,128)(2,1)S(1)}, bf16[25,64,128]{2,1,0:T(8,128)(2,1)S(1)}, u32[]{:S(2)}, u32[]{:S(2)}) collective-permute-start(bf16[25,64,128]{2,1,0:T(8,128)(2,1)S(1)} %collective-permute-done.11.rest_12_), channel_id=1, source_target_pairs={{4,0},{8,4},{12,8},{16,12},{20,16},{24,20},{28,24},{0,28},{5,1},{9... | collective-permute-start | bytes 1228808 | tf_op jit(solution)/shard_map/ppermute | solution.py:17
  53.3 0.1 collective-permute-start.18
  53.3 5.7 %collective-permute-done.3.rest_5_ = bf16[25,64,128]{2,1,0:T(8,128)(2,1)S(1)} collective-permute-done((bf16[25,64,128]{2,1,0:T(8,128)(2,1)S(1)}, bf16[25,64,128]{2,1,0:T(8,128)(2,1)S(1)}, u32[]{:S(2)}, u32[]{:S(2)}) %collective-permute-start.3) | collective-permute-done | bytes 409632 | tf_op jit(solution)/shard_map/ppermute | solution.py:17
  59.0 0.5 collective-permute-start.10
  59.5 6.8 %collective-permute-done.1.rest_0_ = bf16[25,64,128]{2,1,0:T(8,128)(2,1)S(1)} collective-permute-done((bf16[25,64,128]{2,1,0:T(8,128)(2,1)S(1)}, bf16[25,64,128]{2,1,0:T(8,128)(2,1)S(1)}, u32[]{:S(2)}, u32[]{:S(2)}) %collective-permute-start.1) | collective-permute-done | bytes 409632 | tf_op jit(solution)/shard_map/ppermute | solution.py:17
  66.3 1.2 collective-permute-start.7
  67.5 4.3 %collective-permute-start.4 = (bf16[25,64,128]{2,1,0:T(8,128)(2,1)S(1)}, bf16[25,64,128]{2,1,0:T(8,128)(2,1)S(1)}, u32[]{:S(2)}, u32[]{:S(2)}) collective-permute-start(bf16[25,64,128]{2,1,0:T(8,128)(2,1)S(1)} %collective-permute-done.3.rest_5_), channel_id=1, source_target_pairs={{28,0},{0,4},{4,8},{8,12},{12,16},{16,20},{20,24},{24,28},{29,1},{... | collective-permute-start | bytes 1228808 | tf_op jit(solution)/shard_map/ppermute | solution.py:17
  71.8 0.1 collective-permute-done.18.rest_19_
  71.9 2.2 %collective-permute-start.16 = (bf16[25,64,128]{2,1,0:T(8,128)(2,1)S(1)}, bf16[25,64,128]{2,1,0:T(8,128)(2,1)S(1)}, u32[]{:S(2)}, u32[]{:S(2)}) collective-permute-start(bf16[25,64,128]{2,1,0:T(8,128)(2,1)S(1)} %collective-permute-done.12.rest_13_), channel_id=1, source_target_pairs={{4,0},{8,4},{12,8},{16,12},{20,16},{24,20},{28,24},{0,28},{5,1},{9... | collective-permute-start | bytes 1228808 | tf_op jit(solution)/shard_map/ppermute | solution.py:17
  74.1 6.6 %collective-permute-done.17.rest_18_ = bf16[25,64,128]{2,1,0:T(8,128)(2,1)S(1)} collective-permute-done((bf16[25,64,128]{2,1,0:T(8,128)(2,1)S(1)}, bf16[25,64,128]{2,1,0:T(8,128)(2,1)S(1)}, u32[]{:S(2)}, u32[]{:S(2)}) %collective-permute-start.17) | collective-permute-done | bytes 409632 | tf_op jit(solution)/shard_map/ppermute | solution.py:17
  80.7 3.2 %collective-permute-done.7.rest_2_ = bf16[25,64,128]{2,1,0:T(8,128)(2,1)S(1)} collective-permute-done((bf16[25,64,128]{2,1,0:T(8,128)(2,1)S(1)}, bf16[25,64,128]{2,1,0:T(8,128)(2,1)S(1)}, u32[]{:S(2)}, u32[]{:S(2)}) %collective-permute-start.7) | collective-permute-done | bytes 409632 | tf_op jit(solution)/shard_map/ppermute | solution.py:17
  83.9 8.8 %collective-permute-done.4.rest_1_ = bf16[25,64,128]{2,1,0:T(8,128)(2,1)S(1)} collective-permute-done((bf16[25,64,128]{2,1,0:T(8,128)(2,1)S(1)}, bf16[25,64,128]{2,1,0:T(8,128)(2,1)S(1)}, u32[]{:S(2)}, u32[]{:S(2)}) %collective-permute-start.4) | collective-permute-done | bytes 409632 | tf_op jit(solution)/shard_map/ppermute | solution.py:17
  92.7 0.7 copy-done.18
  93.4 0.1 copy-done.19
  93.5 0.1 stack.3
  93.6 0.1 reshape.455
  93.7 3.2 %gather_fusion = s32[768]{0:T(1024)S(1)} fusion(s32[960]{0:T(1024)S(1)} %reshape.455, s32[1024]{0:T(1024)S(1)} %pad_clamp_fusion.1), kind=kCustom, calls=%fused_computation | custom fusion | bytes 9216 | tf_op jit(solution)/shard_map/jit(_take)/gather | solution.py:157
  97.0 1.2 gather_fusion.1
  98.2 0.1 broadcast_in_dim.32
  98.3 0.1 reshape.389
  98.4 0.6 multiply_add_fusion
  99.0 0.6 fusion.11.pair_ref
  99.6 43.6 %shard_map.55 = f32[64,64,128]{2,1,0:T(8,128)} custom-call(s32[768]{0:T(1024)} %fusion.11.pair_ref, s32[768]{0:T(1024)} %get-tuple-element.36.half_ref, s32[768]{0:T(1024)} %get-tuple-element.29.target_ref, s32[768]{0:T(1024)} %reshape.456.live_ref, s32[192]{0:T(256)} %fusion.32.own_pos_ref, bf16[192,4,64,64]{3,2,1,0:T(8,128)(2,1)} %copy.15.values_ref, ...), custom_call_target="tpu_custom_call" | custom-call | tf_op jit(solution)/shard_map/pallas_call | solution.py:86
  143.3 1.5 select_bitcast_fusion.2
  144.8 0.1 collective-permute-start.19
  144.9 1.1 collective-permute-start.20
  145.9 1.4 collective-permute-start.21
  147.4 11.9 %collective-permute-done.19 = f32[8,2,64,128]{3,2,1,0:T(8,128)S(1)} collective-permute-done((f32[8,2,64,128]{3,2,1,0:T(8,128)S(1)}, f32[8,2,64,128]{3,2,1,0:T(8,128)S(1)}, u32[]{:S(2)}, u32[]{:S(2)}) %collective-permute-start.19) | collective-permute-done | bytes 524320 | tf_op jit(solution)/shard_map/ppermute | solution.py:182
  159.3 0.2 collective-permute-done.20
  159.5 11.1 %collective-permute-done.21 = f32[8,2,64,128]{3,2,1,0:T(8,128)S(1)} collective-permute-done((f32[8,2,64,128]{3,2,1,0:T(8,128)S(1)}, f32[8,2,64,128]{3,2,1,0:T(8,128)S(1)}, u32[]{:S(2)}, u32[]{:S(2)}) %collective-permute-start.21) | collective-permute-done | bytes 524320 | tf_op jit(solution)/shard_map/ppermute | solution.py:182
  170.6 1.2 fusion.2
  171.8 0.2 fusion.34
  172.0 1.1 pad_maximum_fusion
  (82 shorter events, 0.3 us)
Async XLA Ops:
  0.0 9.3 %copy-start.20 = (s32[192,4]{0,1:T(4,128)S(1)}, s32[192,4]{0,1:T(4,128)}, u32[]{:S(2)}) copy-start(s32[192,4]{0,1:T(4,128)} %param.10) | copy-start | bytes 9220
  0.7 9.9 %copy-start.21 = (s32[192]{0:T(256)S(1)}, s32[192]{0:T(256)}, u32[]{:S(2)}) copy-start(s32[192]{0:T(256)} %param.11) | copy-start | bytes 2308
  3.0 25.2 %copy-start = (bf16[25,64,128]{2,1,0:T(8,128)(2,1)}, bf16[25,64,128]{2,1,0:T(8,128)(2,1)S(1)}, u32[]{:S(2)}) copy-start(bf16[25,64,128]{2,1,0:T(8,128)(2,1)S(1)} %fusion.3.rest_8_) | copy-start | bytes 1228804
  3.0 25.9 %collective-permute-start.8 = (bf16[25,64,128]{2,1,0:T(8,128)(2,1)S(1)}, bf16[25,64,128]{2,1,0:T(8,128)(2,1)S(1)}, u32[]{:S(2)}, u32[]{:S(2)}) collective-permute-start(bf16[25,64,128]{2,1,0:T(8,128)(2,1)S(1)} %fusion.3.rest_8_), channel_id=1, source_target_pairs={{0,3},{1,0},{2,1},{3,2},{4,7},{5,4},{6,5},{7,6},{8,11},{9,8},{10,9... | collective-permute-start | bytes 1228808 | tf_op jit(solution)/shard_map/ppermute | solution.py:136
  3.6 25.4 %collective-permute-start.5 = (bf16[25,64,128]{2,1,0:T(8,128)(2,1)S(1)}, bf16[25,64,128]{2,1,0:T(8,128)(2,1)S(1)}, u32[]{:S(2)}, u32[]{:S(2)}) collective-permute-start(bf16[25,64,128]{2,1,0:T(8,128)(2,1)S(1)} %fusion.3.rest_8_), channel_id=1, source_target_pairs={{0,2},{1,3},{2,0},{3,1},{4,6},{5,7},{6,4},{7,5},{8,10},{9,11},{10,... | collective-permute-start | bytes 1228808 | tf_op jit(solution)/shard_map/ppermute | solution.py:136
  5.1 24.5 %collective-permute-start.2 = (bf16[25,64,128]{2,1,0:T(8,128)(2,1)S(1)}, bf16[25,64,128]{2,1,0:T(8,128)(2,1)S(1)}, u32[]{:S(2)}, u32[]{:S(2)}) collective-permute-start(bf16[25,64,128]{2,1,0:T(8,128)(2,1)S(1)} %fusion.3.rest_8_), channel_id=1, source_target_pairs={{0,1},{1,2},{2,3},{3,0},{4,5},{5,6},{6,7},{7,4},{8,9},{9,10},{10,1... | collective-permute-start | bytes 1228808 | tf_op jit(solution)/shard_map/ppermute | solution.py:136
  7.5 22.2 %collective-permute-start = (bf16[25,64,128]{2,1,0:T(8,128)(2,1)S(1)}, bf16[25,64,128]{2,1,0:T(8,128)(2,1)S(1)}, u32[]{:S(2)}, u32[]{:S(2)}) collective-permute-start(bf16[25,64,128]{2,1,0:T(8,128)(2,1)S(1)} %fusion.3.rest_8_), channel_id=1, source_target_pairs={{28,0},{0,4},{4,8},{8,12},{12,16},{16,20},{20,24},{24,28},{29,1},{... | collective-permute-start | bytes 1228808 | tf_op jit(solution)/shard_map/ppermute | solution.py:17
  7.5 25.6 %collective-permute-start.11 = (bf16[25,64,128]{2,1,0:T(8,128)(2,1)S(1)}, bf16[25,64,128]{2,1,0:T(8,128)(2,1)S(1)}, u32[]{:S(2)}, u32[]{:S(2)}) collective-permute-start(bf16[25,64,128]{2,1,0:T(8,128)(2,1)S(1)} %fusion.3.rest_8_), channel_id=1, source_target_pairs={{4,0},{8,4},{12,8},{16,12},{20,16},{24,20},{28,24},{0,28},{5,1},{9... | collective-permute-start | bytes 1228808 | tf_op jit(solution)/shard_map/ppermute | solution.py:17
  29.0 67.9 %copy-start.1 = (bf16[25,64,128]{2,1,0:T(8,128)(2,1)}, bf16[25,64,128]{2,1,0:T(8,128)(2,1)S(1)}, u32[]{:S(2)}) copy-start(bf16[25,64,128]{2,1,0:T(8,128)(2,1)S(1)} %collective-permute-done.8.rest_11_) | copy-start | bytes 1228804
  29.0 22.5 %collective-permute-start.14 = (bf16[25,64,128]{2,1,0:T(8,128)(2,1)S(1)}, bf16[25,64,128]{2,1,0:T(8,128)(2,1)S(1)}, u32[]{:S(2)}, u32[]{:S(2)}) collective-permute-start(bf16[25,64,128]{2,1,0:T(8,128)(2,1)S(1)} %collective-permute-done.8.rest_11_), channel_id=1, source_target_pairs={{4,0},{8,4},{12,8},{16,12},{20,16},{24,20},{28,24},{0,28},{5,1},{9... | collective-permute-start | bytes 1228808 | tf_op jit(solution)/shard_map/ppermute | solution.py:17
  29.1 67.8 %copy-start.2 = (bf16[25,64,128]{2,1,0:T(8,128)(2,1)}, bf16[25,64,128]{2,1,0:T(8,128)(2,1)S(1)}, u32[]{:S(2)}) copy-start(bf16[25,64,128]{2,1,0:T(8,128)(2,1)S(1)} %collective-permute-done.5.rest_10_) | copy-start | bytes 1228804
  29.1 24.2 %collective-permute-start.13 = (bf16[25,64,128]{2,1,0:T(8,128)(2,1)S(1)}, bf16[25,64,128]{2,1,0:T(8,128)(2,1)S(1)}, u32[]{:S(2)}, u32[]{:S(2)}) collective-permute-start(bf16[25,64,128]{2,1,0:T(8,128)(2,1)S(1)} %collective-permute-done.5.rest_10_), channel_id=1, source_target_pairs={{4,0},{8,4},{12,8},{16,12},{20,16},{24,20},{28,24},{0,28},{5,1},{9... | collective-permute-start | bytes 1228808 | tf_op jit(solution)/shard_map/ppermute | solution.py:17
  29.6 67.3 %copy-start.3 = (bf16[25,64,128]{2,1,0:T(8,128)(2,1)}, bf16[25,64,128]{2,1,0:T(8,128)(2,1)S(1)}, u32[]{:S(2)}) copy-start(bf16[25,64,128]{2,1,0:T(8,128)(2,1)S(1)} %collective-permute-done.2.rest_9_) | copy-start | bytes 1228804
  29.6 13.1 %collective-permute-start.9 = (bf16[25,64,128]{2,1,0:T(8,128)(2,1)S(1)}, bf16[25,64,128]{2,1,0:T(8,128)(2,1)S(1)}, u32[]{:S(2)}, u32[]{:S(2)}) collective-permute-start(bf16[25,64,128]{2,1,0:T(8,128)(2,1)S(1)} %collective-permute-done.8.rest_11_), channel_id=1, source_target_pairs={{28,0},{0,4},{4,8},{8,12},{12,16},{16,20},{20,24},{24,28},{29,1},{... | collective-permute-start | bytes 1228808 | tf_op jit(solution)/shard_map/ppermute | solution.py:17
  29.7 67.2 %copy-start.4 = (bf16[25,64,128]{2,1,0:T(8,128)(2,1)}, bf16[25,64,128]{2,1,0:T(8,128)(2,1)S(1)}, u32[]{:S(2)}) copy-start(bf16[25,64,128]{2,1,0:T(8,128)(2,1)S(1)} %collective-permute-done.rest_4_) | copy-start | bytes 1228804
  29.7 21.8 %collective-permute-start.6 = (bf16[25,64,128]{2,1,0:T(8,128)(2,1)S(1)}, bf16[25,64,128]{2,1,0:T(8,128)(2,1)S(1)}, u32[]{:S(2)}, u32[]{:S(2)}) collective-permute-start(bf16[25,64,128]{2,1,0:T(8,128)(2,1)S(1)} %collective-permute-done.5.rest_10_), channel_id=1, source_target_pairs={{28,0},{0,4},{4,8},{8,12},{12,16},{16,20},{20,24},{24,28},{29,1},{... | collective-permute-start | bytes 1228808 | tf_op jit(solution)/shard_map/ppermute | solution.py:17
  33.2 63.8 %copy-start.5 = (bf16[25,64,128]{2,1,0:T(8,128)(2,1)}, bf16[25,64,128]{2,1,0:T(8,128)(2,1)S(1)}, u32[]{:S(2)}) copy-start(bf16[25,64,128]{2,1,0:T(8,128)(2,1)S(1)} %collective-permute-done.11.rest_12_) | copy-start | bytes 1228804
  33.2 25.8 %collective-permute-start.3 = (bf16[25,64,128]{2,1,0:T(8,128)(2,1)S(1)}, bf16[25,64,128]{2,1,0:T(8,128)(2,1)S(1)}, u32[]{:S(2)}, u32[]{:S(2)}) collective-permute-start(bf16[25,64,128]{2,1,0:T(8,128)(2,1)S(1)} %collective-permute-done.2.rest_9_), channel_id=1, source_target_pairs={{28,0},{0,4},{4,8},{8,12},{12,16},{16,20},{20,24},{24,28},{29,1},{... | collective-permute-start | bytes 1228808 | tf_op jit(solution)/shard_map/ppermute | solution.py:17
  42.7 37.9 %copy-start.8 = (bf16[25,64,128]{2,1,0:T(8,128)(2,1)}, bf16[25,64,128]{2,1,0:T(8,128)(2,1)S(1)}, u32[]{:S(2)}) copy-start(bf16[25,64,128]{2,1,0:T(8,128)(2,1)S(1)} %collective-permute-done.9.rest_7_) | copy-start | bytes 1228804
  42.7 16.3 %collective-permute-start.12 = (bf16[25,64,128]{2,1,0:T(8,128)(2,1)S(1)}, bf16[25,64,128]{2,1,0:T(8,128)(2,1)S(1)}, u32[]{:S(2)}, u32[]{:S(2)}) collective-permute-start(bf16[25,64,128]{2,1,0:T(8,128)(2,1)S(1)} %collective-permute-done.2.rest_9_), channel_id=1, source_target_pairs={{4,0},{8,4},{12,8},{16,12},{20,16},{24,20},{28,24},{0,28},{5,1},{9... | collective-permute-start | bytes 1228808 | tf_op jit(solution)/shard_map/ppermute | solution.py:17
  51.5 29.2 %copy-start.9 = (bf16[25,64,128]{2,1,0:T(8,128)(2,1)}, bf16[25,64,128]{2,1,0:T(8,128)(2,1)S(1)}, u32[]{:S(2)}) copy-start(bf16[25,64,128]{2,1,0:T(8,128)(2,1)S(1)} %collective-permute-done.6.rest_6_) | copy-start | bytes 1228804
  51.5 14.8 %collective-permute-start.1 = (bf16[25,64,128]{2,1,0:T(8,128)(2,1)S(1)}, bf16[25,64,128]{2,1,0:T(8,128)(2,1)S(1)}, u32[]{:S(2)}, u32[]{:S(2)}) collective-permute-start(bf16[25,64,128]{2,1,0:T(8,128)(2,1)S(1)} %collective-permute-done.rest_4_), channel_id=1, source_target_pairs={{28,0},{0,4},{4,8},{8,12},{12,16},{16,20},{20,24},{24,28},{29,1},{... | collective-permute-start | bytes 1228808 | tf_op jit(solution)/shard_map/ppermute | solution.py:17
  51.5 45.5 %copy-start.6 = (bf16[25,64,128]{2,1,0:T(8,128)(2,1)}, bf16[25,64,128]{2,1,0:T(8,128)(2,1)S(1)}, u32[]{:S(2)}) copy-start(bf16[25,64,128]{2,1,0:T(8,128)(2,1)S(1)} %collective-permute-done.14.rest_15_) | copy-start | bytes 1228804
  51.5 16.0 %collective-permute-start.15 = (bf16[25,64,128]{2,1,0:T(8,128)(2,1)S(1)}, bf16[25,64,128]{2,1,0:T(8,128)(2,1)S(1)}, u32[]{:S(2)}, u32[]{:S(2)}) collective-permute-start(bf16[25,64,128]{2,1,0:T(8,128)(2,1)S(1)} %collective-permute-done.11.rest_12_), channel_id=1, source_target_pairs={{4,0},{8,4},{12,8},{16,12},{20,16},{24,20},{28,24},{0,28},{5,1},{9... | collective-permute-start | bytes 1228808 | tf_op jit(solution)/shard_map/ppermute | solution.py:17
  53.2 43.7 %copy-start.7 = (bf16[25,64,128]{2,1,0:T(8,128)(2,1)}, bf16[25,64,128]{2,1,0:T(8,128)(2,1)S(1)}, u32[]{:S(2)}) copy-start(bf16[25,64,128]{2,1,0:T(8,128)(2,1)S(1)} %collective-permute-done.13.rest_14_) | copy-start | bytes 1228804
  53.3 18.6 %collective-permute-start.18 = (bf16[25,64,128]{2,1,0:T(8,128)(2,1)S(1)}, bf16[25,64,128]{2,1,0:T(8,128)(2,1)S(1)}, u32[]{:S(2)}, u32[]{:S(2)}) collective-permute-start(bf16[25,64,128]{2,1,0:T(8,128)(2,1)S(1)} %collective-permute-done.14.rest_15_), channel_id=1, source_target_pairs={{4,0},{8,4},{12,8},{16,12},{20,16},{24,20},{28,24},{0,28},{5,1},{9... | collective-permute-start | bytes 1228808 | tf_op jit(solution)/shard_map/ppermute | solution.py:17
  59.0 38.0 %copy-start.10 = (bf16[25,64,128]{2,1,0:T(8,128)(2,1)}, bf16[25,64,128]{2,1,0:T(8,128)(2,1)S(1)}, u32[]{:S(2)}) copy-start(bf16[25,64,128]{2,1,0:T(8,128)(2,1)S(1)} %collective-permute-done.3.rest_5_) | copy-start | bytes 1228804
  59.0 21.6 %collective-permute-start.17 = (bf16[25,64,128]{2,1,0:T(8,128)(2,1)S(1)}, bf16[25,64,128]{2,1,0:T(8,128)(2,1)S(1)}, u32[]{:S(2)}, u32[]{:S(2)}) collective-permute-start(bf16[25,64,128]{2,1,0:T(8,128)(2,1)S(1)} %collective-permute-done.13.rest_14_), channel_id=1, source_target_pairs={{4,0},{8,4},{12,8},{16,12},{20,16},{24,20},{28,24},{0,28},{5,1},{9... | collective-permute-start | bytes 1228808 | tf_op jit(solution)/shard_map/ppermute | solution.py:17
  59.0 33.6 %copy-start.11 = (bf16[25,64,128]{2,1,0:T(8,128)(2,1)}, bf16[25,64,128]{2,1,0:T(8,128)(2,1)S(1)}, u32[]{:S(2)}) copy-start(bf16[25,64,128]{2,1,0:T(8,128)(2,1)S(1)} %collective-permute-done.12.rest_13_) | copy-start | bytes 1228804
  59.0 21.6 %collective-permute-start.10 = (bf16[25,64,128]{2,1,0:T(8,128)(2,1)S(1)}, bf16[25,64,128]{2,1,0:T(8,128)(2,1)S(1)}, u32[]{:S(2)}, u32[]{:S(2)}) collective-permute-start(bf16[25,64,128]{2,1,0:T(8,128)(2,1)S(1)} %collective-permute-done.9.rest_7_), channel_id=1, source_target_pairs={{28,0},{0,4},{4,8},{8,12},{12,16},{16,20},{20,24},{24,28},{29,1},{... | collective-permute-start | bytes 1228808 | tf_op jit(solution)/shard_map/ppermute | solution.py:17
  66.3 26.4 %copy-start.12 = (bf16[25,64,128]{2,1,0:T(8,128)(2,1)}, bf16[25,64,128]{2,1,0:T(8,128)(2,1)S(1)}, u32[]{:S(2)}) copy-start(bf16[25,64,128]{2,1,0:T(8,128)(2,1)S(1)} %collective-permute-done.1.rest_0_) | copy-start | bytes 1228804
  66.3 17.6 %collective-permute-start.7 = (bf16[25,64,128]{2,1,0:T(8,128)(2,1)S(1)}, bf16[25,64,128]{2,1,0:T(8,128)(2,1)S(1)}, u32[]{:S(2)}, u32[]{:S(2)}) collective-permute-start(bf16[25,64,128]{2,1,0:T(8,128)(2,1)S(1)} %collective-permute-done.6.rest_6_), channel_id=1, source_target_pairs={{28,0},{0,4},{4,8},{8,12},{12,16},{16,20},{20,24},{24,28},{29,1},{... | collective-permute-start | bytes 1228808 | tf_op jit(solution)/shard_map/ppermute | solution.py:17
  67.5 25.2 %copy-start.13 = (bf16[25,64,128]{2,1,0:T(8,128)(2,1)}, bf16[25,64,128]{2,1,0:T(8,128)(2,1)S(1)}, u32[]{:S(2)}) copy-start(bf16[25,64,128]{2,1,0:T(8,128)(2,1)S(1)} %collective-permute-done.15.rest_16_) | copy-start | bytes 1228804
  67.5 25.1 %collective-permute-start.4 = (bf16[25,64,128]{2,1,0:T(8,128)(2,1)S(1)}, bf16[25,64,128]{2,1,0:T(8,128)(2,1)S(1)}, u32[]{:S(2)}, u32[]{:S(2)}) collective-permute-start(bf16[25,64,128]{2,1,0:T(8,128)(2,1)S(1)} %collective-permute-done.3.rest_5_), channel_id=1, source_target_pairs={{28,0},{0,4},{4,8},{8,12},{12,16},{16,20},{20,24},{24,28},{29,1},{... | collective-permute-start | bytes 1228808 | tf_op jit(solution)/shard_map/ppermute | solution.py:17
  71.9 20.8 %copy-start.14 = (bf16[25,64,128]{2,1,0:T(8,128)(2,1)}, bf16[25,64,128]{2,1,0:T(8,128)(2,1)S(1)}, u32[]{:S(2)}) copy-start(bf16[25,64,128]{2,1,0:T(8,128)(2,1)S(1)} %collective-permute-done.18.rest_19_) | copy-start | bytes 1228804
  71.9 20.8 %collective-permute-start.16 = (bf16[25,64,128]{2,1,0:T(8,128)(2,1)S(1)}, bf16[25,64,128]{2,1,0:T(8,128)(2,1)S(1)}, u32[]{:S(2)}, u32[]{:S(2)}) collective-permute-start(bf16[25,64,128]{2,1,0:T(8,128)(2,1)S(1)} %collective-permute-done.12.rest_13_), channel_id=1, source_target_pairs={{4,0},{8,4},{12,8},{16,12},{20,16},{24,20},{28,24},{0,28},{5,1},{9... | collective-permute-start | bytes 1228808 | tf_op jit(solution)/shard_map/ppermute | solution.py:17
  80.7 12.0 %copy-start.15 = (bf16[25,64,128]{2,1,0:T(8,128)(2,1)}, bf16[25,64,128]{2,1,0:T(8,128)(2,1)S(1)}, u32[]{:S(2)}) copy-start(bf16[25,64,128]{2,1,0:T(8,128)(2,1)S(1)} %collective-permute-done.17.rest_18_) | copy-start | bytes 1228804
  80.7 12.0 %copy-start.16 = (bf16[25,64,128]{2,1,0:T(8,128)(2,1)}, bf16[25,64,128]{2,1,0:T(8,128)(2,1)S(1)}, u32[]{:S(2)}) copy-start(bf16[25,64,128]{2,1,0:T(8,128)(2,1)S(1)} %collective-permute-done.10.rest_3_) | copy-start | bytes 1228804
  83.8 8.9 %copy-start.17 = (bf16[25,64,128]{2,1,0:T(8,128)(2,1)}, bf16[25,64,128]{2,1,0:T(8,128)(2,1)S(1)}, u32[]{:S(2)}) copy-start(bf16[25,64,128]{2,1,0:T(8,128)(2,1)S(1)} %collective-permute-done.7.rest_2_) | copy-start | bytes 1228804
  92.6 0.8 copy-start.18
  92.7 0.9 copy-start.19
  144.8 14.5 %collective-permute-start.19 = (f32[8,2,64,128]{3,2,1,0:T(8,128)S(1)}, f32[8,2,64,128]{3,2,1,0:T(8,128)S(1)}, u32[]{:S(2)}, u32[]{:S(2)}) collective-permute-start(f32[8,2,64,128]{3,2,1,0:T(8,128)S(1)} %get-tuple-element.31), channel_id=1, source_target_pairs={{0,1},{1,2},{2,3},{3,0},{4,5},{5,6},{6,7},{7,4},{8,9},{9,10},{10,1... | collective-permute-start | bytes 1572872 | tf_op jit(solution)/shard_map/ppermute | solution.py:182
  144.9 14.6 %collective-permute-start.20 = (f32[8,2,64,128]{3,2,1,0:T(8,128)S(1)}, f32[8,2,64,128]{3,2,1,0:T(8,128)S(1)}, u32[]{:S(2)}, u32[]{:S(2)}) collective-permute-start(f32[8,2,64,128]{3,2,1,0:T(8,128)S(1)} %get-tuple-element.33), channel_id=1, source_target_pairs={{0,2},{1,3},{2,0},{3,1},{4,6},{5,7},{6,4},{7,5},{8,10},{9,11},{10,... | collective-permute-start | bytes 1572872 | tf_op jit(solution)/shard_map/ppermute | solution.py:182
  145.9 24.6 %collective-permute-start.21 = (f32[8,2,64,128]{3,2,1,0:T(8,128)S(1)}, f32[8,2,64,128]{3,2,1,0:T(8,128)S(1)}, u32[]{:S(2)}, u32[]{:S(2)}) collective-permute-start(f32[8,2,64,128]{3,2,1,0:T(8,128)S(1)} %get-tuple-element.32), channel_id=1, source_target_pairs={{0,3},{1,0},{2,1},{3,2},{4,7},{5,4},{6,5},{7,6},{8,11},{9,8},{10,9... | collective-permute-start | bytes 1572872 | tf_op jit(solution)/shard_map/ppermute | solution.py:182

commit v7 on v6

--- a/solution.py
+++ b/solution.py
@@ -17,9 +17,14 @@
     return lax.ppermute(block, axis, route)
 
 
-def coarse_kernel(pair_ref, half_ref, target_ref, live_ref, own_pos_ref, values_ref, *rest):
-    pieces = rest[:-4]
+def coarse_kernel(
+    pair_ref, half_ref, target_ref, live_ref, own_pos_ref, fix_ref, values_ref, *rest
+):
     out_ref, acc_ref, window, sems = rest[-4:]
+    n_pieces = sems.shape[0]
+    groups = n_pieces // 5
+    pieces = rest[:n_pieces]
+    fixed = rest[n_pieces:-4]
     step = pl.program_id(0)
     rows_here, slots, bs, _ = values_ref.shape
     piece_rows = pieces[0].shape[0]
@@ -28,11 +33,26 @@
     @pl.when(step == 0)
     def _():
         copies = []
-        for k, piece in enumerate(pieces):
-            cp = pltpu.make_async_copy(
-                piece, window.at[pl.ds(k * piece_rows, piece_rows)], sems.at[k]
-            )
-            cp.start()
+        for j, piece in enumerate(pieces):
+            dst = window.at[pl.ds(j * piece_rows, piece_rows)]
+            cp = pltpu.make_async_copy(piece, dst, sems.at[j])
+            d, k = divmod(j, groups)
+            if k == 0:
+                cp.start()
+            else:
+                flag = fix_ref[d]
+
+                @pl.when(flag < 0)
+                def _():
+                    cp.start()
+
+                for slot in range(2):
+                    @pl.when(flag == slot)
+                    def _():
+                        pltpu.make_async_copy(
+                            fixed[k - 1].at[slot], dst, sems.at[j]
+                        ).start()
+
             copies.append(cp)
         acc_ref[...] = jnp.zeros_like(acc_ref)
         for cp in copies:
@@ -78,7 +98,7 @@
         lax.fori_loop(0, out_ref.shape[0], pack, 0)
 
 
-def coarse_partial(pair, half, target, live, own_pos, values, pieces, n_targets):
+def coarse_partial(pair, half, target, live, own_pos, fix, values, pieces, fixed, n_targets):
     panel_length, slots, bs, _ = values.shape
     rows_per_step = min(ROWS_PER_STEP, panel_length)
     grid = (panel_length // rows_per_step,)
@@ -87,12 +107,12 @@
         coarse_kernel,
         out_shape=jax.ShapeDtypeStruct((n_targets // 2, bs, lanes), jnp.float32),
         grid_spec=pltpu.PrefetchScalarGridSpec(
-            num_scalar_prefetch=5,
+            num_scalar_prefetch=6,
             grid=grid,
             in_specs=[
                 pl.BlockSpec((rows_per_step, slots, bs, bs), lambda i, *_: (i, 0, 0, 0)),
             ]
-            + [pl.BlockSpec(memory_space=pl.ANY)] * len(pieces),
+            + [pl.BlockSpec(memory_space=pl.ANY)] * (len(pieces) + len(fixed)),
             out_specs=pl.BlockSpec((n_targets // 2, bs, lanes), lambda i, *_: (0, 0, 0)),
             scratch_shapes=[
                 pltpu.VMEM((n_targets, bs, lanes), jnp.float32),
@@ -104,7 +124,7 @@
             dimension_semantics=("arbitrary",),
             vmem_limit_bytes=60 * 1024 * 1024,
         ),
-    )(pair, half, target, live, own_pos, values, *pieces)
+    )(pair, half, target, live, own_pos, fix, values, *pieces, *fixed)
 
 
 def local(block_values, block_columns, row_counts, prolong_blocks, aggregates):
@@ -137,13 +157,58 @@
                 local_ext, "grp", [(i, (i + k) % group_size) for i in range(group_size)]
             )
         )
-    down1 = [passed_along(piece, "blk", 1) for piece in received]
-    up1 = [passed_along(piece, "blk", -1) for piece in received]
-    down2 = [passed_along(piece, "blk", 1) for piece in down1]
-    up2 = [passed_along(piece, "blk", -1) for piece in up1]
+    n = panel_total
+    down_skip = ({(n - 1, 0)}, {(n - 1, 0), (0, 1)})
+    up_skip = ({(0, n - 1)}, {(0, n - 1), (n - 1, n - 2)})
+
+    def ring(piece, step, hop, full):
+        skip = set() if full else (down_skip if step == 1 else up_skip)[hop]
+        route = [((i - step) % n, i) for i in range(n)]
+        route = [pair for pair in route if pair not in skip]
+        return lax.ppermute(piece, "blk", route)
+
+    down1 = [ring(piece, 1, 0, k == 0) for k, piece in enumerate(received)]
+    up1 = [ring(piece, -1, 0, k == 0) for k, piece in enumerate(received)]
+    down2 = [ring(piece, 1, 1, k == 0) for k, piece in enumerate(down1)]
+    up2 = [ring(piece, -1, 1, k == 0) for k, piece in enumerate(up1)]
     pieces = down2 + down1 + received + up1 + up2
-    flat_aggs = jnp.stack([piece[share_rows // 2, 0, :share_rows] for piece in pieces])
-    flat_aggs = flat_aggs.astype(jnp.int32).reshape(-1)
+    low_end = me <= 1
+    fix_first = jnp.where(low_end, down2[0], up2[0])
+    fix_second = jnp.where(me == 0, down1[0], up1[0])
+    fix_src = jnp.stack([fix_first, fix_second])
+    ends = [0, 1, n - 2, n - 1]
+    fixed = []
+    for k in range(1, group_size):
+        route = [
+            (b * group_size + g, b * group_size + (g + k) % group_size)
+            for b in ends
+            for g in range(group_size)
+        ]
+        fixed.append(lax.ppermute(fix_src, ("blk", "grp"), route))
+    minus = jnp.int32(-1)
+    fix = jnp.stack([
+        jnp.where(low_end, 0, minus),
+        jnp.where(me == 0, 1, minus),
+        minus,
+        jnp.where(me == n - 1, 1, minus),
+        jnp.where(me >= n - 2, 0, minus),
+    ]).astype(jnp.int32)
+    agg_rows = []
+    for d in range(5):
+        for k in range(group_size):
+            row = pieces[d * group_size + k][share_rows // 2, 0, :share_rows]
+            if k > 0:
+                row = jnp.where(
+                    fix[d] >= 0,
+                    jnp.where(
+                        fix[d] == 0,
+                        fixed[k - 1][0, share_rows // 2, 0, :share_rows],
+                        fixed[k - 1][1, share_rows // 2, 0, :share_rows],
+                    ),
+                    row,
+                )
+            agg_rows.append(row)
+    flat_aggs = jnp.stack(agg_rows).astype(jnp.int32).reshape(-1)
 
     def placed(d, r):
         k = jnp.mod(group_me - r // share_rows, group_size)
@@ -170,8 +235,10 @@
         target.astype(jnp.int32),
         live,
         own_pos,
+        fix,
         block_values,
         pieces,
+        fixed,
         coarse_count * CB,
     )
     share = coarse_count // group_size

time: 175 us -> 173 us (0.989)
  waiting for transfers between devices: 72.4 us -> 34.9 us
  starting transfers between devices: 23.1 us -> 56.8 us
  local copies, waits for them, and re-layouts: 26.8 us -> 29.3 us
    ppermute x16 -> x19, waiting for transfers between devices: 49.2 us -> 15.2 us  [the longest x3 8.03 us: local(): fixed.append(lax.ppermute(fix_src, ('blk', 'grp'), route))]
    ppermute x16 -> x19, starting transfers between devices: 16 us -> 47.7 us  [the longest x16 38.6 us: ring(): return lax.ppermute(piece, 'blk', route)]
    ppermute x3, waiting for transfers between devices: 23.2 us -> 19.8 us  [local(): lax.ppermute(outgoing, 'grp', [(i, (i + k) % group_size) for i in range(g...]
    another operation x21 -> x10, local copies, waits for them, and re-layouts: 0.34 us -> 2.91 us  [the longest x8 2.12 us: local(): flat_aggs = jnp.stack(agg_rows).astype(jnp.int32).reshape(-1)]
    ppermute x3, starting transfers between devices: 2.58 us -> 4.66 us  [local(): lax.ppermute(outgoing, 'grp', [(i, (i + k) % group_size) for i in range(g...]
  transfers between devices with their start and end apart: 22 -> 25, of which waited for: 11 -> 5; matrix products, arithmetic and copies ran while one was open for 11% -> 13% of each run, Pallas kernels for 0% -> 0%
where the time goes in v7:
time: 173 us; the launch traced here: 172 us
  starting transfers between devices  56.8 us (33%)
  Pallas kernels  43.6 us (25%)
  waiting for transfers between devices  34.9 us (20%)
  local copies, waits for them, and re-layouts  29.3 us (17%)
  other arithmetic  6.72 us (4%)
    pallas_call x1, Pallas kernels, coarse_partial(): pl.pallas_call(coarse_kernel, out_shape=jax.ShapeDtypeStruct((n_targets /...  43.6 us
    ppermute x16, starting transfers between devices, ring(): return lax.ppermute(piece, 'blk', route)  38.6 us
    ppermute x3, waiting for transfers between devices, local(): lax.ppermute(outgoing, 'grp', [(i, (i + k) % group_size) for i in range(g...  19.8 us
    unnamed x45, local copies, waits for them, and re-layouts  17.7 us
    ppermute x3, starting transfers between devices, local(): fixed.append(lax.ppermute(fix_src, ('blk', 'grp'), route))  9.14 us
    ppermute x3, waiting for transfers between devices, local(): fixed.append(lax.ppermute(fix_src, ('blk', 'grp'), route))  8.03 us
    ppermute x16, waiting for transfers between devices, ring(): return lax.ppermute(piece, 'blk', route)  7.14 us
    ppermute x3, starting transfers between devices, local(): lax.ppermute(outgoing, 'grp', [(i, (i + k) % group_size) for i in range(g...  4.66 us
  transfers between devices with their start and end apart: 25, of which 5 were waited for; matrix products, arithmetic and copies ran while one was open for 13% of the time, Pallas kernels for 0%

profile of v7, /device:TPU:26, one launch (start us, length us, event | category | flops | bytes accessed | tf_op | source)
XLA Modules:
  0.0 172.3 jit_solution(8106936753258231173)
XLA Ops:
  0.0 0.7 convert_bitcast_fusion
  0.7 2.0 %copy.17 = bf16[24,2,64,64]{3,1,2,0:T(2,128)(2,1)S(1)} copy(bf16[24,2,64,64]{3,2,1,0:T(8,128)(2,1)} %bitcast.144) | data formatting | bytes 786432 | tf_op jit(solution)/shard_map/reshape | solution.py:142
  2.6 0.3 reshape.739
  3.1 1.7 %collective-permute-start.2 = (bf16[25,64,128]{2,1,0:T(8,128)(2,1)S(1)}, bf16[25,64,128]{2,1,0:T(8,128)(2,1)S(1)}, u32[]{:S(2)}, u32[]{:S(2)}) collective-permute-start(bf16[25,64,128]{2,1,0:T(8,128)(2,1)S(1)} %fusion.3.rest_8_), channel_id=1, source_target_pairs={{4,0},{8,4},{12,8},{16,12},{20,16},{24,20},{28,24},{0,28},{5,1},{9... | collective-permute-start | bytes 1228808 | tf_op jit(solution)/shard_map/ppermute | solution.py:168
  4.8 0.5 collective-permute-start.13
  5.4 1.5 collective-permute-start.9
  6.9 2.4 %collective-permute-start.5 = (bf16[25,64,128]{2,1,0:T(8,128)(2,1)S(1)}, bf16[25,64,128]{2,1,0:T(8,128)(2,1)}, u32[]{:S(2)}, u32[]{:S(2)}) collective-permute-start(bf16[25,64,128]{2,1,0:T(8,128)(2,1)S(1)} %fusion.3.rest_8_), channel_id=1, source_target_pairs={{0,1},{1,2},{2,3},{3,0},{4,5},{5,6},{6,7},{7,4},{8,9},{9,10},{10,1... | collective-permute-start | bytes 1228808 | tf_op jit(solution)/shard_map/ppermute | solution.py:156
  9.3 0.1 copy.9
  9.4 0.1 rem.301
  9.6 0.1 rem.276
  9.7 0.1 copy.10
  9.8 0.1 div.78
  9.9 0.1 div.73
  10.0 0.2 copy.8
  10.2 0.1 ne.313
  10.3 0.1 ne.303
  10.5 0.1 compare_convert_fusion
  10.6 0.7 reshape.807.live_ref
  11.3 17.0 %copy.15.values_ref = bf16[192,4,64,64]{3,2,1,0:T(8,128)(2,1)} copy(bf16[192,4,64,64]{0,3,2,1:T(8,128)(2,1)} %param.9) | data formatting | bytes 12582912 | tf_op args[0]
  28.3 0.6 stack.59.fix_ref
  28.9 0.6 fusion.32.own_pos_ref
  29.5 0.1 fusion.16
  29.7 1.7 collective-permute-start.3
  31.4 2.3 %collective-permute-start.14 = (bf16[25,64,128]{2,1,0:T(8,128)(2,1)}, bf16[25,64,128]{2,1,0:T(8,128)(2,1)S(1)}, u32[]{:S(2)}, u32[]{:S(2)}) collective-permute-start(bf16[25,64,128]{2,1,0:T(8,128)(2,1)} %collective-permute-done.13.rest_11_), channel_id=1, source_target_pairs={{0,4},{4,8},{8,12},{12,16},{16,20},{20,24},{24,28},{1,5},{5,9},{9,... | collective-permute-start | bytes 1228808 | tf_op jit(solution)/shard_map/ppermute | solution.py:168
  33.7 0.7 slice_bitcast_fusion.8
  34.4 3.2 %collective-permute-start.18 = (bf16[25,64,128]{2,1,0:T(8,128)(2,1)}, bf16[25,64,128]{2,1,0:T(8,128)(2,1)S(1)}, u32[]{:S(2)}, u32[]{:S(2)}) collective-permute-start(bf16[25,64,128]{2,1,0:T(8,128)(2,1)} %collective-permute-done.13.rest_11_), channel_id=1, source_target_pairs={{4,0},{8,4},{12,8},{16,12},{20,16},{24,20},{28,24},{5,1},{9,5},{13... | collective-permute-start | bytes 1228808 | tf_op jit(solution)/shard_map/ppermute | solution.py:168
  37.7 4.9 %collective-permute-start.10 = (bf16[25,64,128]{2,1,0:T(8,128)(2,1)}, bf16[25,64,128]{2,1,0:T(8,128)(2,1)S(1)}, u32[]{:S(2)}, u32[]{:S(2)}) collective-permute-start(bf16[25,64,128]{2,1,0:T(8,128)(2,1)} %collective-permute-done.9.rest_10_), channel_id=1, source_target_pairs={{0,4},{4,8},{8,12},{12,16},{16,20},{20,24},{24,28},{1,5},{5,9},{9,... | collective-permute-start | bytes 1228808 | tf_op jit(solution)/shard_map/ppermute | solution.py:168
  42.7 0.1 pad_maximum_fusion.1
  42.8 1.9 %collective-permute-start.12 = (bf16[2,25,64,128]{3,2,1,0:T(8,128)(2,1)S(1)}, bf16[2,25,64,128]{3,2,1,0:T(8,128)(2,1)S(1)}, u32[]{:S(2)}, u32[]{:S(2)}) collective-permute-start(bf16[2,25,64,128]{3,2,1,0:T(8,128)(2,1)S(1)} %pad_maximum_fusion.1), channel_id=1, source_target_pairs={{0,3},{1,0},{2,1},{3,2},{4,7},{5,4},{6,5},{7,6},{24,27},{25,24},{2... | collective-permute-start | bytes 2457608 | tf_op jit(solution)/shard_map/ppermute | solution.py:187
  44.7 0.7 slice_bitcast_fusion.9
  45.4 0.7 slice_bitcast_fusion.10
  46.1 2.5 %collective-permute-start.8 = (bf16[2,25,64,128]{3,2,1,0:T(8,128)(2,1)S(1)}, bf16[2,25,64,128]{3,2,1,0:T(8,128)(2,1)S(1)}, u32[]{:S(2)}, u32[]{:S(2)}) collective-permute-start(bf16[2,25,64,128]{3,2,1,0:T(8,128)(2,1)S(1)} %pad_maximum_fusion.1), channel_id=1, source_target_pairs={{0,2},{1,3},{2,0},{3,1},{4,6},{5,7},{6,4},{7,5},{24,26},{25,27},{2... | collective-permute-start | bytes 2457608 | tf_op jit(solution)/shard_map/ppermute | solution.py:187
  48.6 4.3 %collective-permute-start.15 = (bf16[25,64,128]{2,1,0:T(8,128)(2,1)S(1)}, bf16[25,64,128]{2,1,0:T(8,128)(2,1)S(1)}, u32[]{:S(2)}, u32[]{:S(2)}) collective-permute-start(bf16[25,64,128]{2,1,0:T(8,128)(2,1)S(1)} %collective-permute-done.14.rest_7_), channel_id=1, source_target_pairs={{4,8},{8,12},{12,16},{16,20},{20,24},{24,28},{5,9},{9,13},{13,17},... | collective-permute-start | bytes 1228808 | tf_op jit(solution)/shard_map/ppermute | solution.py:168
  52.9 1.3 collective-permute-start.21
  54.2 4.8 %collective-permute-start.4 = (bf16[2,25,64,128]{3,2,1,0:T(8,128)(2,1)S(1)}, bf16[2,25,64,128]{3,2,1,0:T(8,128)(2,1)S(1)}, u32[]{:S(2)}, u32[]{:S(2)}) collective-permute-start(bf16[2,25,64,128]{3,2,1,0:T(8,128)(2,1)S(1)} %pad_maximum_fusion.1), channel_id=1, source_target_pairs={{0,1},{1,2},{2,3},{3,0},{4,5},{5,6},{6,7},{7,4},{24,25},{25,26},{2... | collective-permute-start | bytes 2457608 | tf_op jit(solution)/shard_map/ppermute | solution.py:187
  59.0 1.9 %collective-permute-start.17 = (bf16[25,64,128]{2,1,0:T(8,128)(2,1)}, bf16[25,64,128]{2,1,0:T(8,128)(2,1)S(1)}, u32[]{:S(2)}, u32[]{:S(2)}) collective-permute-start(bf16[25,64,128]{2,1,0:T(8,128)(2,1)} %collective-permute-done.9.rest_10_), channel_id=1, source_target_pairs={{4,0},{8,4},{12,8},{16,12},{20,16},{24,20},{28,24},{5,1},{9,5},{13... | collective-permute-start | bytes 1228808 | tf_op jit(solution)/shard_map/ppermute | solution.py:168
  61.0 2.4 %collective-permute-start.16 = (bf16[25,64,128]{2,1,0:T(8,128)(2,1)}, bf16[25,64,128]{2,1,0:T(8,128)(2,1)S(1)}, u32[]{:S(2)}, u32[]{:S(2)}) collective-permute-start(bf16[25,64,128]{2,1,0:T(8,128)(2,1)} %collective-permute-done.5.rest_9_), channel_id=1, source_target_pairs={{4,0},{8,4},{12,8},{16,12},{20,16},{24,20},{28,24},{5,1},{9,5},{13... | collective-permute-start | bytes 1228808 | tf_op jit(solution)/shard_map/ppermute | solution.py:168
  63.4 1.7 collective-permute-done.12.rest_22_
  65.1 5.1 %collective-permute-start.6 = (bf16[25,64,128]{2,1,0:T(8,128)(2,1)}, bf16[25,64,128]{2,1,0:T(8,128)(2,1)S(1)}, u32[]{:S(2)}, u32[]{:S(2)}) collective-permute-start(bf16[25,64,128]{2,1,0:T(8,128)(2,1)} %collective-permute-done.5.rest_9_), channel_id=1, source_target_pairs={{0,4},{4,8},{8,12},{12,16},{16,20},{20,24},{24,28},{1,5},{5,9},{9,... | collective-permute-start | bytes 1228808 | tf_op jit(solution)/shard_map/ppermute | solution.py:168
  70.2 1.9 %collective-permute-start.11 = (bf16[25,64,128]{2,1,0:T(8,128)(2,1)S(1)}, bf16[25,64,128]{2,1,0:T(8,128)(2,1)S(1)}, u32[]{:S(2)}, u32[]{:S(2)}) collective-permute-start(bf16[25,64,128]{2,1,0:T(8,128)(2,1)S(1)} %collective-permute-done.10.rest_6_), channel_id=1, source_target_pairs={{4,8},{8,12},{12,16},{16,20},{20,24},{24,28},{5,9},{9,13},{13,17},... | collective-permute-start | bytes 1228808 | tf_op jit(solution)/shard_map/ppermute | solution.py:168
  72.2 3.7 %collective-permute-start.20 = (bf16[25,64,128]{2,1,0:T(8,128)(2,1)S(1)}, bf16[25,64,128]{2,1,0:T(8,128)(2,1)S(1)}, u32[]{:S(2)}, u32[]{:S(2)}) collective-permute-start(bf16[25,64,128]{2,1,0:T(8,128)(2,1)S(1)} %collective-permute-done.17.rest_14_), channel_id=1, source_target_pairs={{4,0},{8,4},{12,8},{16,12},{20,16},{24,20},{5,1},{9,5},{13,9},{17,... | collective-permute-start | bytes 1228808 | tf_op jit(solution)/shard_map/ppermute | solution.py:168
  75.9 1.9 %collective-permute-start.19 = (bf16[25,64,128]{2,1,0:T(8,128)(2,1)S(1)}, bf16[25,64,128]{2,1,0:T(8,128)(2,1)S(1)}, u32[]{:S(2)}, u32[]{:S(2)}) collective-permute-start(bf16[25,64,128]{2,1,0:T(8,128)(2,1)S(1)} %collective-permute-done.16.rest_13_), channel_id=1, source_target_pairs={{4,0},{8,4},{12,8},{16,12},{20,16},{24,20},{5,1},{9,5},{13,9},{17,... | collective-permute-start | bytes 1228808 | tf_op jit(solution)/shard_map/ppermute | solution.py:168
  77.8 6.4 %collective-permute-done.8.rest_21_ = bf16[2,25,64,128]{3,2,1,0:T(8,128)(2,1)S(1)} collective-permute-done((bf16[2,25,64,128]{3,2,1,0:T(8,128)(2,1)S(1)}, bf16[2,25,64,128]{3,2,1,0:T(8,128)(2,1)S(1)}, u32[]{:S(2)}, u32[]{:S(2)}) %collective-permute-start.8) | collective-permute-done | bytes 819232 | tf_op jit(solution)/shard_map/ppermute | solution.py:187
  84.2 2.0 %collective-permute-start.7 = (bf16[25,64,128]{2,1,0:T(8,128)(2,1)S(1)}, bf16[25,64,128]{2,1,0:T(8,128)(2,1)S(1)}, u32[]{:S(2)}, u32[]{:S(2)}) collective-permute-start(bf16[25,64,128]{2,1,0:T(8,128)(2,1)S(1)} %collective-permute-done.6.rest_5_), channel_id=1, source_target_pairs={{4,8},{8,12},{12,16},{16,20},{20,24},{24,28},{5,9},{9,13},{13,17},... | collective-permute-start | bytes 1228808 | tf_op jit(solution)/shard_map/ppermute | solution.py:168
  86.3 7.1 %collective-permute-done.7.rest_1_ = bf16[25,64,128]{2,1,0:T(8,128)(2,1)S(1)} collective-permute-done((bf16[25,64,128]{2,1,0:T(8,128)(2,1)S(1)}, bf16[25,64,128]{2,1,0:T(8,128)(2,1)S(1)}, u32[]{:S(2)}, u32[]{:S(2)}) %collective-permute-start.7) | collective-permute-done | bytes 409632 | tf_op jit(solution)/shard_map/ppermute | solution.py:168
  93.5 0.7 copy-done.19
  94.2 0.1 stack.54
  94.3 0.1 reshape.806
  94.4 3.2 %gather_fusion = s32[768]{0:T(1024)S(1)} fusion(s32[960]{0:T(1024)S(1)} %reshape.806, s32[1024]{0:T(1024)S(1)} %pad_clamp_fusion.1), kind=kCustom, calls=%fused_computation | custom fusion | bytes 9216 | tf_op jit(solution)/shard_map/jit(_take)/gather | solution.py:222
  97.6 1.2 gather_fusion.1
  98.8 0.1 broadcast_in_dim.32
  98.9 0.1 reshape.740
  99.0 0.6 multiply_add_fusion
  99.7 0.6 fusion.11.pair_ref
  100.3 43.6 %shard_map.55 = f32[64,64,128]{2,1,0:T(8,128)} custom-call(s32[768]{0:T(1024)} %fusion.11.pair_ref, s32[768]{0:T(1024)} %get-tuple-element.45.half_ref, s32[768]{0:T(1024)} %get-tuple-element.29.target_ref, s32[768]{0:T(1024)} %reshape.807.live_ref, s32[192]{0:T(256)} %fusion.32.own_pos_ref, s32[5]{0:T(128)} %stack.59.fix_ref, ...), custom_call_target="tpu_custom_call" | custom-call | tf_op jit(solution)/shard_map/pallas_call | solution.py:106
  143.9 1.5 select_bitcast_fusion.2
  145.4 4.0 %collective-permute-start.22 = (f32[8,2,64,128]{3,2,1,0:T(8,128)S(1)}, f32[8,2,64,128]{3,2,1,0:T(8,128)S(1)}, u32[]{:S(2)}, u32[]{:S(2)}) collective-permute-start(f32[8,2,64,128]{3,2,1,0:T(8,128)S(1)} %get-tuple-element.31), channel_id=1, source_target_pairs={{0,1},{1,2},{2,3},{3,0},{4,5},{5,6},{6,7},{7,4},{8,9},{9,10},{10,1... | collective-permute-start | bytes 1572872 | tf_op jit(solution)/shard_map/ppermute | solution.py:249
  149.4 0.5 collective-permute-start.23
  149.9 0.1 collective-permute-start.24
  150.1 11.7 %collective-permute-done.22 = f32[8,2,64,128]{3,2,1,0:T(8,128)S(1)} collective-permute-done((f32[8,2,64,128]{3,2,1,0:T(8,128)S(1)}, f32[8,2,64,128]{3,2,1,0:T(8,128)S(1)}, u32[]{:S(2)}, u32[]{:S(2)}) %collective-permute-start.22) | collective-permute-done | bytes 524320 | tf_op jit(solution)/shard_map/ppermute | solution.py:249
  161.7 8.1 %collective-permute-done.23 = f32[8,2,64,128]{3,2,1,0:T(8,128)S(1)} collective-permute-done((f32[8,2,64,128]{3,2,1,0:T(8,128)S(1)}, f32[8,2,64,128]{3,2,1,0:T(8,128)S(1)}, u32[]{:S(2)}, u32[]{:S(2)}) %collective-permute-start.23) | collective-permute-done | bytes 524320 | tf_op jit(solution)/shard_map/ppermute | solution.py:249
  169.8 1.2 fusion.2
  171.0 0.2 fusion.46
  171.2 1.1 pad_maximum_fusion
  (86 shorter events, 0.5 us)
Async XLA Ops:
  0.0 9.3 %copy-start.20 = (s32[192,4]{0,1:T(4,128)S(1)}, s32[192,4]{0,1:T(4,128)}, u32[]{:S(2)}) copy-start(s32[192,4]{0,1:T(4,128)} %param.10) | copy-start | bytes 9220
  0.7 9.9 %copy-start.21 = (s32[192]{0:T(256)S(1)}, s32[192]{0:T(256)}, u32[]{:S(2)}) copy-start(s32[192]{0:T(256)} %param.11) | copy-start | bytes 2308
  3.0 25.3 %copy-start.4 = (bf16[25,64,128]{2,1,0:T(8,128)(2,1)}, bf16[25,64,128]{2,1,0:T(8,128)(2,1)S(1)}, u32[]{:S(2)}) copy-start(bf16[25,64,128]{2,1,0:T(8,128)(2,1)S(1)} %fusion.3.rest_8_) | copy-start | bytes 1228804
  3.0 26.5 %collective-permute-start = (bf16[25,64,128]{2,1,0:T(8,128)(2,1)S(1)}, bf16[25,64,128]{2,1,0:T(8,128)(2,1)S(1)}, u32[]{:S(2)}, u32[]{:S(2)}) collective-permute-start(bf16[25,64,128]{2,1,0:T(8,128)(2,1)S(1)} %fusion.3.rest_8_), channel_id=1, source_target_pairs={{28,0},{0,4},{4,8},{8,12},{12,16},{16,20},{20,24},{24,28},{29,1},{... | collective-permute-start | bytes 1228808 | tf_op jit(solution)/shard_map/ppermute | solution.py:168
  3.1 26.5 %collective-permute-start.2 = (bf16[25,64,128]{2,1,0:T(8,128)(2,1)S(1)}, bf16[25,64,128]{2,1,0:T(8,128)(2,1)S(1)}, u32[]{:S(2)}, u32[]{:S(2)}) collective-permute-start(bf16[25,64,128]{2,1,0:T(8,128)(2,1)S(1)} %fusion.3.rest_8_), channel_id=1, source_target_pairs={{4,0},{8,4},{12,8},{16,12},{20,16},{24,20},{28,24},{0,28},{5,1},{9... | collective-permute-start | bytes 1228808 | tf_op jit(solution)/shard_map/ppermute | solution.py:168
  4.8 26.6 %collective-permute-start.13 = (bf16[25,64,128]{2,1,0:T(8,128)(2,1)S(1)}, bf16[25,64,128]{2,1,0:T(8,128)(2,1)}, u32[]{:S(2)}, u32[]{:S(2)}) collective-permute-start(bf16[25,64,128]{2,1,0:T(8,128)(2,1)S(1)} %fusion.3.rest_8_), channel_id=1, source_target_pairs={{0,3},{1,0},{2,1},{3,2},{4,7},{5,4},{6,5},{7,6},{8,11},{9,8},{10,9... | collective-permute-start | bytes 1228808 | tf_op jit(solution)/shard_map/ppermute | solution.py:156
  5.4 29.1 %collective-permute-start.9 = (bf16[25,64,128]{2,1,0:T(8,128)(2,1)S(1)}, bf16[25,64,128]{2,1,0:T(8,128)(2,1)}, u32[]{:S(2)}, u32[]{:S(2)}) collective-permute-start(bf16[25,64,128]{2,1,0:T(8,128)(2,1)S(1)} %fusion.3.rest_8_), channel_id=1, source_target_pairs={{0,2},{1,3},{2,0},{3,1},{4,6},{5,7},{6,4},{7,5},{8,10},{9,11},{10,... | collective-permute-start | bytes 1228808 | tf_op jit(solution)/shard_map/ppermute | solution.py:156
  6.9 38.5 %collective-permute-start.5 = (bf16[25,64,128]{2,1,0:T(8,128)(2,1)S(1)}, bf16[25,64,128]{2,1,0:T(8,128)(2,1)}, u32[]{:S(2)}, u32[]{:S(2)}) collective-permute-start(bf16[25,64,128]{2,1,0:T(8,128)(2,1)S(1)} %fusion.3.rest_8_), channel_id=1, source_target_pairs={{0,1},{1,2},{2,3},{3,0},{4,5},{5,6},{6,7},{7,4},{8,9},{9,10},{10,1... | collective-permute-start | bytes 1228808 | tf_op jit(solution)/shard_map/ppermute | solution.py:156
  29.6 64.7 %copy-start = (bf16[25,64,128]{2,1,0:T(8,128)(2,1)}, bf16[25,64,128]{2,1,0:T(8,128)(2,1)S(1)}, u32[]{:S(2)}) copy-start(bf16[25,64,128]{2,1,0:T(8,128)(2,1)S(1)} %collective-permute-done.rest_4_) | copy-start | bytes 1228804
  29.6 8.1 %collective-permute-start.1 = (bf16[25,64,128]{2,1,0:T(8,128)(2,1)S(1)}, bf16[25,64,128]{2,1,0:T(8,128)(2,1)S(1)}, u32[]{:S(2)}, u32[]{:S(2)}) collective-permute-start(bf16[25,64,128]{2,1,0:T(8,128)(2,1)S(1)} %collective-permute-done.rest_4_), channel_id=1, source_target_pairs={{28,0},{0,4},{4,8},{8,12},{12,16},{16,20},{20,24},{24,28},{29,1},{... | collective-permute-start | bytes 1228808 | tf_op jit(solution)/shard_map/ppermute | solution.py:168
  29.7 64.7 %copy-start.1 = (bf16[25,64,128]{2,1,0:T(8,128)(2,1)}, bf16[25,64,128]{2,1,0:T(8,128)(2,1)S(1)}, u32[]{:S(2)}) copy-start(bf16[25,64,128]{2,1,0:T(8,128)(2,1)S(1)} %collective-permute-done.2.rest_12_) | copy-start | bytes 1228804
  29.7 13.0 %collective-permute-start.3 = (bf16[25,64,128]{2,1,0:T(8,128)(2,1)S(1)}, bf16[25,64,128]{2,1,0:T(8,128)(2,1)S(1)}, u32[]{:S(2)}, u32[]{:S(2)}) collective-permute-start(bf16[25,64,128]{2,1,0:T(8,128)(2,1)S(1)} %collective-permute-done.2.rest_12_), channel_id=1, source_target_pairs={{4,0},{8,4},{12,8},{16,12},{20,16},{24,20},{28,24},{0,28},{5,1},{9... | collective-permute-start | bytes 1228808 | tf_op jit(solution)/shard_map/ppermute | solution.py:168
  31.4 17.2 %collective-permute-start.14 = (bf16[25,64,128]{2,1,0:T(8,128)(2,1)}, bf16[25,64,128]{2,1,0:T(8,128)(2,1)S(1)}, u32[]{:S(2)}, u32[]{:S(2)}) collective-permute-start(bf16[25,64,128]{2,1,0:T(8,128)(2,1)} %collective-permute-done.13.rest_11_), channel_id=1, source_target_pairs={{0,4},{4,8},{8,12},{12,16},{16,20},{20,24},{24,28},{1,5},{5,9},{9,... | collective-permute-start | bytes 1228808 | tf_op jit(solution)/shard_map/ppermute | solution.py:168
  34.4 18.4 %collective-permute-start.18 = (bf16[25,64,128]{2,1,0:T(8,128)(2,1)}, bf16[25,64,128]{2,1,0:T(8,128)(2,1)S(1)}, u32[]{:S(2)}, u32[]{:S(2)}) collective-permute-start(bf16[25,64,128]{2,1,0:T(8,128)(2,1)} %collective-permute-done.13.rest_11_), channel_id=1, source_target_pairs={{4,0},{8,4},{12,8},{16,12},{20,16},{24,20},{28,24},{5,1},{9,5},{13... | collective-permute-start | bytes 1228808 | tf_op jit(solution)/shard_map/ppermute | solution.py:168
  37.7 59.9 %copy-start.2 = (bf16[25,64,128]{2,1,0:T(8,128)(2,1)}, bf16[25,64,128]{2,1,0:T(8,128)(2,1)S(1)}, u32[]{:S(2)}) copy-start(bf16[25,64,128]{2,1,0:T(8,128)(2,1)S(1)} %collective-permute-done.1.rest_0_) | copy-start | bytes 1228804
  37.7 16.5 %collective-permute-start.10 = (bf16[25,64,128]{2,1,0:T(8,128)(2,1)}, bf16[25,64,128]{2,1,0:T(8,128)(2,1)S(1)}, u32[]{:S(2)}, u32[]{:S(2)}) collective-permute-start(bf16[25,64,128]{2,1,0:T(8,128)(2,1)} %collective-permute-done.9.rest_10_), channel_id=1, source_target_pairs={{0,4},{4,8},{8,12},{12,16},{16,20},{20,24},{24,28},{1,5},{5,9},{9,... | collective-permute-start | bytes 1228808 | tf_op jit(solution)/shard_map/ppermute | solution.py:168
  42.7 54.9 %copy-start.3 = (bf16[25,64,128]{2,1,0:T(8,128)(2,1)}, bf16[25,64,128]{2,1,0:T(8,128)(2,1)S(1)}, u32[]{:S(2)}) copy-start(bf16[25,64,128]{2,1,0:T(8,128)(2,1)S(1)} %collective-permute-done.3.rest_16_) | copy-start | bytes 1228804
  42.8 22.3 %collective-permute-start.12 = (bf16[2,25,64,128]{3,2,1,0:T(8,128)(2,1)S(1)}, bf16[2,25,64,128]{3,2,1,0:T(8,128)(2,1)S(1)}, u32[]{:S(2)}, u32[]{:S(2)}) collective-permute-start(bf16[2,25,64,128]{3,2,1,0:T(8,128)(2,1)S(1)} %pad_maximum_fusion.1), channel_id=1, source_target_pairs={{0,3},{1,0},{2,1},{3,2},{4,7},{5,4},{6,5},{7,6},{24,27},{25,24},{2... | collective-permute-start | bytes 2457608 | tf_op jit(solution)/shard_map/ppermute | solution.py:187
  46.1 38.1 %collective-permute-start.8 = (bf16[2,25,64,128]{3,2,1,0:T(8,128)(2,1)S(1)}, bf16[2,25,64,128]{3,2,1,0:T(8,128)(2,1)S(1)}, u32[]{:S(2)}, u32[]{:S(2)}) collective-permute-start(bf16[2,25,64,128]{3,2,1,0:T(8,128)(2,1)S(1)} %pad_maximum_fusion.1), channel_id=1, source_target_pairs={{0,2},{1,3},{2,0},{3,1},{4,6},{5,7},{6,4},{7,5},{24,26},{25,27},{2... | collective-permute-start | bytes 2457608 | tf_op jit(solution)/shard_map/ppermute | solution.py:187
  48.6 51.7 %copy-start.8 = (bf16[25,64,128]{2,1,0:T(8,128)(2,1)}, bf16[25,64,128]{2,1,0:T(8,128)(2,1)S(1)}, u32[]{:S(2)}) copy-start(bf16[25,64,128]{2,1,0:T(8,128)(2,1)S(1)} %collective-permute-done.14.rest_7_) | copy-start | bytes 1228804
  48.6 10.4 %collective-permute-start.15 = (bf16[25,64,128]{2,1,0:T(8,128)(2,1)S(1)}, bf16[25,64,128]{2,1,0:T(8,128)(2,1)S(1)}, u32[]{:S(2)}, u32[]{:S(2)}) collective-permute-start(bf16[25,64,128]{2,1,0:T(8,128)(2,1)S(1)} %collective-permute-done.14.rest_7_), channel_id=1, source_target_pairs={{4,8},{8,12},{12,16},{16,20},{20,24},{24,28},{5,9},{9,13},{13,17},... | collective-permute-start | bytes 1228808 | tf_op jit(solution)/shard_map/ppermute | solution.py:168
  52.9 40.6 %copy-start.9 = (bf16[25,64,128]{2,1,0:T(8,128)(2,1)}, bf16[25,64,128]{2,1,0:T(8,128)(2,1)S(1)}, u32[]{:S(2)}) copy-start(bf16[25,64,128]{2,1,0:T(8,128)(2,1)S(1)} %collective-permute-done.18.rest_15_) | copy-start | bytes 1228804
  52.9 8.1 %collective-permute-start.21 = (bf16[25,64,128]{2,1,0:T(8,128)(2,1)S(1)}, bf16[25,64,128]{2,1,0:T(8,128)(2,1)S(1)}, u32[]{:S(2)}, u32[]{:S(2)}) collective-permute-start(bf16[25,64,128]{2,1,0:T(8,128)(2,1)S(1)} %collective-permute-done.18.rest_15_), channel_id=1, source_target_pairs={{4,0},{8,4},{12,8},{16,12},{20,16},{24,20},{5,1},{9,5},{13,9},{17,... | collective-permute-start | bytes 1228808 | tf_op jit(solution)/shard_map/ppermute | solution.py:168
  54.2 39.2 %copy-start.10 = (bf16[25,64,128]{2,1,0:T(8,128)(2,1)}, bf16[25,64,128]{2,1,0:T(8,128)(2,1)S(1)}, u32[]{:S(2)}) copy-start(bf16[25,64,128]{2,1,0:T(8,128)(2,1)S(1)} %collective-permute-done.10.rest_6_) | copy-start | bytes 1228804
  54.2 32.0 %collective-permute-start.4 = (bf16[2,25,64,128]{3,2,1,0:T(8,128)(2,1)S(1)}, bf16[2,25,64,128]{3,2,1,0:T(8,128)(2,1)S(1)}, u32[]{:S(2)}, u32[]{:S(2)}) collective-permute-start(bf16[2,25,64,128]{3,2,1,0:T(8,128)(2,1)S(1)} %pad_maximum_fusion.1), channel_id=1, source_target_pairs={{0,1},{1,2},{2,3},{3,0},{4,5},{5,6},{6,7},{7,4},{24,25},{25,26},{2... | collective-permute-start | bytes 2457608 | tf_op jit(solution)/shard_map/ppermute | solution.py:187
  59.0 41.2 %copy-start.11 = (bf16[25,64,128]{2,1,0:T(8,128)(2,1)}, bf16[25,64,128]{2,1,0:T(8,128)(2,1)S(1)}, u32[]{:S(2)}) copy-start(bf16[25,64,128]{2,1,0:T(8,128)(2,1)S(1)} %collective-permute-done.15.rest_3_) | copy-start | bytes 1228804
  59.0 11.2 %collective-permute-start.17 = (bf16[25,64,128]{2,1,0:T(8,128)(2,1)}, bf16[25,64,128]{2,1,0:T(8,128)(2,1)S(1)}, u32[]{:S(2)}, u32[]{:S(2)}) collective-permute-start(bf16[25,64,128]{2,1,0:T(8,128)(2,1)} %collective-permute-done.9.rest_10_), channel_id=1, source_target_pairs={{4,0},{8,4},{12,8},{16,12},{20,16},{24,20},{28,24},{5,1},{9,5},{13... | collective-permute-start | bytes 1228808 | tf_op jit(solution)/shard_map/ppermute | solution.py:168
  61.0 32.5 %copy-start.12 = (bf16[25,64,128]{2,1,0:T(8,128)(2,1)}, bf16[25,64,128]{2,1,0:T(8,128)(2,1)S(1)}, u32[]{:S(2)}) copy-start(bf16[25,64,128]{2,1,0:T(8,128)(2,1)S(1)} %collective-permute-done.21.rest_19_) | copy-start | bytes 1228804
  61.0 11.2 %collective-permute-start.16 = (bf16[25,64,128]{2,1,0:T(8,128)(2,1)}, bf16[25,64,128]{2,1,0:T(8,128)(2,1)S(1)}, u32[]{:S(2)}, u32[]{:S(2)}) collective-permute-start(bf16[25,64,128]{2,1,0:T(8,128)(2,1)} %collective-permute-done.5.rest_9_), channel_id=1, source_target_pairs={{4,0},{8,4},{12,8},{16,12},{20,16},{24,20},{28,24},{5,1},{9,5},{13... | collective-permute-start | bytes 1228808 | tf_op jit(solution)/shard_map/ppermute | solution.py:168
  65.1 32.5 %copy-start.5 = (bf16[2,25,64,128]{3,2,1,0:T(8,128)(2,1)}, bf16[2,25,64,128]{3,2,1,0:T(8,128)(2,1)S(1)}, u32[]{:S(2)}) copy-start(bf16[2,25,64,128]{3,2,1,0:T(8,128)(2,1)S(1)} %collective-permute-done.12.rest_22_) | copy-start | bytes 2457604
  65.1 10.8 %collective-permute-start.6 = (bf16[25,64,128]{2,1,0:T(8,128)(2,1)}, bf16[25,64,128]{2,1,0:T(8,128)(2,1)S(1)}, u32[]{:S(2)}, u32[]{:S(2)}) collective-permute-start(bf16[25,64,128]{2,1,0:T(8,128)(2,1)} %collective-permute-done.5.rest_9_), channel_id=1, source_target_pairs={{0,4},{4,8},{8,12},{12,16},{16,20},{20,24},{24,28},{1,5},{5,9},{9,... | collective-permute-start | bytes 1228808 | tf_op jit(solution)/shard_map/ppermute | solution.py:168
  70.2 23.3 %copy-start.13 = (bf16[25,64,128]{2,1,0:T(8,128)(2,1)}, bf16[25,64,128]{2,1,0:T(8,128)(2,1)S(1)}, u32[]{:S(2)}) copy-start(bf16[25,64,128]{2,1,0:T(8,128)(2,1)S(1)} %collective-permute-done.17.rest_14_) | copy-start | bytes 1228804
  70.2 16.0 %collective-permute-start.11 = (bf16[25,64,128]{2,1,0:T(8,128)(2,1)S(1)}, bf16[25,64,128]{2,1,0:T(8,128)(2,1)S(1)}, u32[]{:S(2)}, u32[]{:S(2)}) collective-permute-start(bf16[25,64,128]{2,1,0:T(8,128)(2,1)S(1)} %collective-permute-done.10.rest_6_), channel_id=1, source_target_pairs={{4,8},{8,12},{12,16},{16,20},{20,24},{24,28},{5,9},{9,13},{13,17},... | collective-permute-start | bytes 1228808 | tf_op jit(solution)/shard_map/ppermute | solution.py:168
  72.2 21.3 %copy-start.14 = (bf16[25,64,128]{2,1,0:T(8,128)(2,1)}, bf16[25,64,128]{2,1,0:T(8,128)(2,1)S(1)}, u32[]{:S(2)}) copy-start(bf16[25,64,128]{2,1,0:T(8,128)(2,1)S(1)} %collective-permute-done.16.rest_13_) | copy-start | bytes 1228804
  72.2 14.1 %collective-permute-start.20 = (bf16[25,64,128]{2,1,0:T(8,128)(2,1)S(1)}, bf16[25,64,128]{2,1,0:T(8,128)(2,1)S(1)}, u32[]{:S(2)}, u32[]{:S(2)}) collective-permute-start(bf16[25,64,128]{2,1,0:T(8,128)(2,1)S(1)} %collective-permute-done.17.rest_14_), channel_id=1, source_target_pairs={{4,0},{8,4},{12,8},{16,12},{20,16},{24,20},{5,1},{9,5},{13,9},{17,... | collective-permute-start | bytes 1228808 | tf_op jit(solution)/shard_map/ppermute | solution.py:168
  75.9 17.6 %copy-start.15 = (bf16[25,64,128]{2,1,0:T(8,128)(2,1)}, bf16[25,64,128]{2,1,0:T(8,128)(2,1)S(1)}, u32[]{:S(2)}) copy-start(bf16[25,64,128]{2,1,0:T(8,128)(2,1)S(1)} %collective-permute-done.6.rest_5_) | copy-start | bytes 1228804
  75.9 10.4 %collective-permute-start.19 = (bf16[25,64,128]{2,1,0:T(8,128)(2,1)S(1)}, bf16[25,64,128]{2,1,0:T(8,128)(2,1)S(1)}, u32[]{:S(2)}, u32[]{:S(2)}) collective-permute-start(bf16[25,64,128]{2,1,0:T(8,128)(2,1)S(1)} %collective-permute-done.16.rest_13_), channel_id=1, source_target_pairs={{4,0},{8,4},{12,8},{16,12},{20,16},{24,20},{5,1},{9,5},{13,9},{17,... | collective-permute-start | bytes 1228808 | tf_op jit(solution)/shard_map/ppermute | solution.py:168
  84.2 2.1 %copy-start.6 = (bf16[2,25,64,128]{3,2,1,0:T(8,128)(2,1)}, bf16[2,25,64,128]{3,2,1,0:T(8,128)(2,1)S(1)}, u32[]{:S(2)}) copy-start(bf16[2,25,64,128]{3,2,1,0:T(8,128)(2,1)S(1)} %collective-permute-done.8.rest_21_) | copy-start | bytes 2457604
  84.2 9.3 %collective-permute-start.7 = (bf16[25,64,128]{2,1,0:T(8,128)(2,1)S(1)}, bf16[25,64,128]{2,1,0:T(8,128)(2,1)S(1)}, u32[]{:S(2)}, u32[]{:S(2)}) collective-permute-start(bf16[25,64,128]{2,1,0:T(8,128)(2,1)S(1)} %collective-permute-done.6.rest_5_), channel_id=1, source_target_pairs={{4,8},{8,12},{12,16},{16,20},{20,24},{24,28},{5,9},{9,13},{13,17},... | collective-permute-start | bytes 1228808 | tf_op jit(solution)/shard_map/ppermute | solution.py:168
  86.2 7.2 %copy-start.7 = (bf16[2,25,64,128]{3,2,1,0:T(8,128)(2,1)}, bf16[2,25,64,128]{3,2,1,0:T(8,128)(2,1)S(1)}, u32[]{:S(2)}) copy-start(bf16[2,25,64,128]{3,2,1,0:T(8,128)(2,1)S(1)} %collective-permute-done.4.rest_20_) | copy-start | bytes 2457604
  86.3 7.3 %copy-start.16 = (bf16[25,64,128]{2,1,0:T(8,128)(2,1)}, bf16[25,64,128]{2,1,0:T(8,128)(2,1)S(1)}, u32[]{:S(2)}) copy-start(bf16[25,64,128]{2,1,0:T(8,128)(2,1)S(1)} %collective-permute-done.11.rest_2_) | copy-start | bytes 1228804
  86.3 7.2 %copy-start.17 = (bf16[25,64,128]{2,1,0:T(8,128)(2,1)}, bf16[25,64,128]{2,1,0:T(8,128)(2,1)S(1)}, u32[]{:S(2)}) copy-start(bf16[25,64,128]{2,1,0:T(8,128)(2,1)S(1)} %collective-permute-done.20.rest_18_) | copy-start | bytes 1228804
  86.3 7.2 %copy-start.18 = (bf16[25,64,128]{2,1,0:T(8,128)(2,1)}, bf16[25,64,128]{2,1,0:T(8,128)(2,1)S(1)}, u32[]{:S(2)}) copy-start(bf16[25,64,128]{2,1,0:T(8,128)(2,1)S(1)} %collective-permute-done.19.rest_17_) | copy-start | bytes 1228804
  93.4 0.8 copy-start.19
  145.4 16.3 %collective-permute-start.22 = (f32[8,2,64,128]{3,2,1,0:T(8,128)S(1)}, f32[8,2,64,128]{3,2,1,0:T(8,128)S(1)}, u32[]{:S(2)}, u32[]{:S(2)}) collective-permute-start(f32[8,2,64,128]{3,2,1,0:T(8,128)S(1)} %get-tuple-element.31), channel_id=1, source_target_pairs={{0,1},{1,2},{2,3},{3,0},{4,5},{5,6},{6,7},{7,4},{8,9},{9,10},{10,1... | collective-permute-start | bytes 1572872 | tf_op jit(solution)/shard_map/ppermute | solution.py:249
  149.4 20.4 %collective-permute-start.23 = (f32[8,2,64,128]{3,2,1,0:T(8,128)S(1)}, f32[8,2,64,128]{3,2,1,0:T(8,128)S(1)}, u32[]{:S(2)}, u32[]{:S(2)}) collective-permute-start(f32[8,2,64,128]{3,2,1,0:T(8,128)S(1)} %get-tuple-element.33), channel_id=1, source_target_pairs={{0,2},{1,3},{2,0},{3,1},{4,6},{5,7},{6,4},{7,5},{8,10},{9,11},{10,... | collective-permute-start | bytes 1572872 | tf_op jit(solution)/shard_map/ppermute | solution.py:249
  149.9 19.9 %collective-permute-start.24 = (f32[8,2,64,128]{3,2,1,0:T(8,128)S(1)}, f32[8,2,64,128]{3,2,1,0:T(8,128)S(1)}, u32[]{:S(2)}, u32[]{:S(2)}) collective-permute-start(f32[8,2,64,128]{3,2,1,0:T(8,128)S(1)} %get-tuple-element.32), channel_id=1, source_target_pairs={{0,3},{1,0},{2,1},{3,2},{4,7},{5,4},{6,5},{7,6},{8,11},{9,8},{10,9... | collective-permute-start | bytes 1572872 | tf_op jit(solution)/shard_map/ppermute | solution.py:249

commit v8 on v7

--- a/solution.py
+++ b/solution.py
@@ -66,21 +66,35 @@
         spread = jnp.concatenate([own_pair, jnp.zeros_like(own_pair)], axis=0).T
         own_t = jnp.where(row % 2 == 0, spread[:bs], spread[bs:])[:, :bs]
         own_t = own_t.astype(jnp.bfloat16)
-        results = []
-        for s in range(slots):
-            n = row * slots + s
-            pair = window[pair_ref[n]]
-            picked = jnp.where(lane_half == half_ref[n], pair, jnp.zeros_like(pair))
-            product = jnp.dot(
-                values_ref[r, s], picked, preferred_element_type=jnp.float32
-            )
-            product = jnp.where(live_ref[n] > 0, product, 0.0).astype(jnp.bfloat16)
-            results.append(
-                jnp.dot(own_t, product, preferred_element_type=jnp.float32)
-            )
-        for s in range(slots):
-            t = target_ref[row * slots + s]
-            acc_ref[t] = acc_ref[t] + results[s]
+        base = row * slots
+        lhs = values_ref[r].reshape(slots * bs, bs)
+        left_lane = lane_half == 0
+        columns = []
+        for j in range(slots // 2):
+            placed = []
+            for side in range(2):
+                n = base + 2 * j + side
+                pair = window[pair_ref[n]].astype(jnp.float32)
+                swapped = pltpu.roll(pair, bs, 1)
+                placed.append(jnp.where(half_ref[n] == side, pair, swapped))
+            columns.append(jnp.where(left_lane, placed[0], placed[1]))
+        weights = jnp.concatenate(columns, axis=1).astype(jnp.bfloat16)
+        out = jnp.dot(lhs, weights, preferred_element_type=jnp.float32)
+        diagonal = []
+        for j in range(slots // 2):
+            lanes_j = slice(2 * bs * j, 2 * bs * (j + 1))
+            top = out[2 * bs * j : 2 * bs * j + bs, lanes_j]
+            bottom = out[2 * bs * j + bs : 2 * bs * (j + 1), lanes_j]
+            top = jnp.where(live_ref[base + 2 * j] > 0, top, 0.0)
+            bottom = jnp.where(live_ref[base + 2 * j + 1] > 0, bottom, 0.0)
+            diagonal.append(jnp.where(left_lane, top, bottom))
+        product = jnp.concatenate(diagonal, axis=1).astype(jnp.bfloat16)
+        restricted = jnp.dot(own_t, product, preferred_element_type=jnp.float32)
+        for k in range(slots):
+            j, side = divmod(k, 2)
+            part = restricted[:, 2 * bs * j : 2 * bs * (j + 1)]
+            t = target_ref[base + k]
+            acc_ref[t] = acc_ref[t] + jnp.where(lane_half == side, part, 0.0)
         return carry
 
     lax.fori_loop(0, rows_here, row_body, 0, unroll=2)

time: 173 us -> 202 us (1.17)
  Pallas kernels: 43.6 us -> 71.9 us
    pallas_call x1, Pallas kernels: 43.6 us -> 71.9 us  [coarse_partial(): pl.pallas_call(coarse_kernel, out_shape=jax.ShapeDtypeStruct((n_targets /...]
  transfers between devices with their start and end apart: 25 -> 25, of which waited for: 5 -> 5; matrix products, arithmetic and copies ran while one was open for 13% -> 11% of each run, Pallas kernels for 0% -> 0%
where the time goes in v8:
time: 202 us; the launch traced here: 201 us
  Pallas kernels  71.9 us (36%)
  starting transfers between devices  56.8 us (28%)
  waiting for transfers between devices  35 us (17%)
  local copies, waits for them, and re-layouts  29.3 us (15%)
  other arithmetic  6.72 us (3%)
    pallas_call x1, Pallas kernels, coarse_partial(): pl.pallas_call(coarse_kernel, out_shape=jax.ShapeDtypeStruct((n_targets /...  71.9 us
    ppermute x16, starting transfers between devices, ring(): return lax.ppermute(piece, 'blk', route)  38.6 us
    ppermute x3, waiting for transfers between devices, local(): lax.ppermute(outgoing, 'grp', [(i, (i + k) % group_size) for i in range(g...  19.8 us
    unnamed x45, local copies, waits for them, and re-layouts  17.7 us
    ppermute x3, starting transfers between devices, local(): fixed.append(lax.ppermute(fix_src, ('blk', 'grp'), route))  9.14 us
    ppermute x3, waiting for transfers between devices, local(): fixed.append(lax.ppermute(fix_src, ('blk', 'grp'), route))  8.03 us
    ppermute x16, waiting for transfers between devices, ring(): return lax.ppermute(piece, 'blk', route)  7.14 us
    ppermute x3, starting transfers between devices, local(): lax.ppermute(outgoing, 'grp', [(i, (i + k) % group_size) for i in range(g...  4.65 us
  transfers between devices with their start and end apart: 25, of which 5 were waited for; matrix products, arithmetic and copies ran while one was open for 11% of the time, Pallas kernels for 0%

profile of v8, /device:TPU:26, one launch (start us, length us, event | category | flops | bytes accessed | tf_op | source)
XLA Modules:
  0.0 200.6 jit_solution(16303791438759915627)
XLA Ops:
  0.0 0.7 convert_bitcast_fusion
  0.7 2.0 copy.17
  2.6 0.3 reshape.739
  3.1 1.7 collective-permute-start.2
  4.8 0.5 collective-permute-start.13
  5.4 1.5 collective-permute-start.9
  6.9 2.4 %collective-permute-start.5 = (bf16[25,64,128]{2,1,0:T(8,128)(2,1)S(1)}, bf16[25,64,128]{2,1,0:T(8,128)(2,1)}, u32[]{:S(2)}, u32[]{:S(2)}) collective-permute-start(bf16[25,64,128]{2,1,0:T(8,128)(2,1)S(1)} %fusion.3.rest_8_), channel_id=1, source_target_pairs={{0,1},{1,2},{2,3},{3,0},{4,5},{5,6},{6,7},{7,4},{8,9},{9,10},{10,1... | collective-permute-start | bytes 1228808 | tf_op jit(solution)/shard_map/ppermute | solution.py:170
  9.3 0.1 copy.9
  9.4 0.1 rem.301
  9.6 0.1 rem.276
  9.7 0.1 copy.10
  9.8 0.1 div.78
  9.9 0.1 div.73
  10.0 0.2 copy.8
  10.2 0.1 ne.313
  10.3 0.1 ne.303
  10.5 0.1 compare_convert_fusion
  10.6 0.7 reshape.807.live_ref
  11.3 17.0 %copy.15.values_ref = bf16[192,4,64,64]{3,2,1,0:T(8,128)(2,1)} copy(bf16[192,4,64,64]{0,3,2,1:T(8,128)(2,1)} %param.9) | data formatting | bytes 12582912 | tf_op args[0]
  28.3 0.6 stack.59.fix_ref
  28.9 0.6 fusion.32.own_pos_ref
  29.5 0.1 fusion.16
  29.7 1.7 collective-permute-start.3
  31.4 2.3 %collective-permute-start.14 = (bf16[25,64,128]{2,1,0:T(8,128)(2,1)}, bf16[25,64,128]{2,1,0:T(8,128)(2,1)S(1)}, u32[]{:S(2)}, u32[]{:S(2)}) collective-permute-start(bf16[25,64,128]{2,1,0:T(8,128)(2,1)} %collective-permute-done.13.rest_11_), channel_id=1, source_target_pairs={{0,4},{4,8},{8,12},{12,16},{16,20},{20,24},{24,28},{1,5},{5,9},{9,... | collective-permute-start | bytes 1228808 | tf_op jit(solution)/shard_map/ppermute | solution.py:182
  33.7 0.7 slice_bitcast_fusion.8
  34.4 3.2 %collective-permute-start.18 = (bf16[25,64,128]{2,1,0:T(8,128)(2,1)}, bf16[25,64,128]{2,1,0:T(8,128)(2,1)S(1)}, u32[]{:S(2)}, u32[]{:S(2)}) collective-permute-start(bf16[25,64,128]{2,1,0:T(8,128)(2,1)} %collective-permute-done.13.rest_11_), channel_id=1, source_target_pairs={{4,0},{8,4},{12,8},{16,12},{20,16},{24,20},{28,24},{5,1},{9,5},{13... | collective-permute-start | bytes 1228808 | tf_op jit(solution)/shard_map/ppermute | solution.py:182
  37.7 4.9 %collective-permute-start.10 = (bf16[25,64,128]{2,1,0:T(8,128)(2,1)}, bf16[25,64,128]{2,1,0:T(8,128)(2,1)S(1)}, u32[]{:S(2)}, u32[]{:S(2)}) collective-permute-start(bf16[25,64,128]{2,1,0:T(8,128)(2,1)} %collective-permute-done.9.rest_10_), channel_id=1, source_target_pairs={{0,4},{4,8},{8,12},{12,16},{16,20},{20,24},{24,28},{1,5},{5,9},{9,... | collective-permute-start | bytes 1228808 | tf_op jit(solution)/shard_map/ppermute | solution.py:182
  42.7 0.1 pad_maximum_fusion.1
  42.8 1.9 collective-permute-start.12
  44.7 0.7 slice_bitcast_fusion.9
  45.4 0.7 slice_bitcast_fusion.10
  46.1 2.5 %collective-permute-start.8 = (bf16[2,25,64,128]{3,2,1,0:T(8,128)(2,1)S(1)}, bf16[2,25,64,128]{3,2,1,0:T(8,128)(2,1)S(1)}, u32[]{:S(2)}, u32[]{:S(2)}) collective-permute-start(bf16[2,25,64,128]{3,2,1,0:T(8,128)(2,1)S(1)} %pad_maximum_fusion.1), channel_id=1, source_target_pairs={{0,2},{1,3},{2,0},{3,1},{4,6},{5,7},{6,4},{7,5},{24,26},{25,27},{2... | collective-permute-start | bytes 2457608 | tf_op jit(solution)/shard_map/ppermute | solution.py:201
  48.6 4.3 %collective-permute-start.15 = (bf16[25,64,128]{2,1,0:T(8,128)(2,1)S(1)}, bf16[25,64,128]{2,1,0:T(8,128)(2,1)S(1)}, u32[]{:S(2)}, u32[]{:S(2)}) collective-permute-start(bf16[25,64,128]{2,1,0:T(8,128)(2,1)S(1)} %collective-permute-done.14.rest_7_), channel_id=1, source_target_pairs={{4,8},{8,12},{12,16},{16,20},{20,24},{24,28},{5,9},{9,13},{13,17},... | collective-permute-start | bytes 1228808 | tf_op jit(solution)/shard_map/ppermute | solution.py:182
  52.9 1.3 collective-permute-start.21
  54.2 4.8 %collective-permute-start.4 = (bf16[2,25,64,128]{3,2,1,0:T(8,128)(2,1)S(1)}, bf16[2,25,64,128]{3,2,1,0:T(8,128)(2,1)S(1)}, u32[]{:S(2)}, u32[]{:S(2)}) collective-permute-start(bf16[2,25,64,128]{3,2,1,0:T(8,128)(2,1)S(1)} %pad_maximum_fusion.1), channel_id=1, source_target_pairs={{0,1},{1,2},{2,3},{3,0},{4,5},{5,6},{6,7},{7,4},{24,25},{25,26},{2... | collective-permute-start | bytes 2457608 | tf_op jit(solution)/shard_map/ppermute | solution.py:201
  59.0 1.9 collective-permute-start.17
  61.0 2.4 %collective-permute-start.16 = (bf16[25,64,128]{2,1,0:T(8,128)(2,1)}, bf16[25,64,128]{2,1,0:T(8,128)(2,1)S(1)}, u32[]{:S(2)}, u32[]{:S(2)}) collective-permute-start(bf16[25,64,128]{2,1,0:T(8,128)(2,1)} %collective-permute-done.5.rest_9_), channel_id=1, source_target_pairs={{4,0},{8,4},{12,8},{16,12},{20,16},{24,20},{28,24},{5,1},{9,5},{13... | collective-permute-start | bytes 1228808 | tf_op jit(solution)/shard_map/ppermute | solution.py:182
  63.4 1.7 collective-permute-done.12.rest_22_
  65.1 5.1 %collective-permute-start.6 = (bf16[25,64,128]{2,1,0:T(8,128)(2,1)}, bf16[25,64,128]{2,1,0:T(8,128)(2,1)S(1)}, u32[]{:S(2)}, u32[]{:S(2)}) collective-permute-start(bf16[25,64,128]{2,1,0:T(8,128)(2,1)} %collective-permute-done.5.rest_9_), channel_id=1, source_target_pairs={{0,4},{4,8},{8,12},{12,16},{16,20},{20,24},{24,28},{1,5},{5,9},{9,... | collective-permute-start | bytes 1228808 | tf_op jit(solution)/shard_map/ppermute | solution.py:182
  70.2 1.9 collective-permute-start.11
  72.2 3.7 %collective-permute-start.20 = (bf16[25,64,128]{2,1,0:T(8,128)(2,1)S(1)}, bf16[25,64,128]{2,1,0:T(8,128)(2,1)S(1)}, u32[]{:S(2)}, u32[]{:S(2)}) collective-permute-start(bf16[25,64,128]{2,1,0:T(8,128)(2,1)S(1)} %collective-permute-done.17.rest_14_), channel_id=1, source_target_pairs={{4,0},{8,4},{12,8},{16,12},{20,16},{24,20},{5,1},{9,5},{13,9},{17,... | collective-permute-start | bytes 1228808 | tf_op jit(solution)/shard_map/ppermute | solution.py:182
  75.9 1.9 collective-permute-start.19
  77.8 6.4 %collective-permute-done.8.rest_21_ = bf16[2,25,64,128]{3,2,1,0:T(8,128)(2,1)S(1)} collective-permute-done((bf16[2,25,64,128]{3,2,1,0:T(8,128)(2,1)S(1)}, bf16[2,25,64,128]{3,2,1,0:T(8,128)(2,1)S(1)}, u32[]{:S(2)}, u32[]{:S(2)}) %collective-permute-start.8) | collective-permute-done | bytes 819232 | tf_op jit(solution)/shard_map/ppermute | solution.py:201
  84.2 2.0 %collective-permute-start.7 = (bf16[25,64,128]{2,1,0:T(8,128)(2,1)S(1)}, bf16[25,64,128]{2,1,0:T(8,128)(2,1)S(1)}, u32[]{:S(2)}, u32[]{:S(2)}) collective-permute-start(bf16[25,64,128]{2,1,0:T(8,128)(2,1)S(1)} %collective-permute-done.6.rest_5_), channel_id=1, source_target_pairs={{4,8},{8,12},{12,16},{16,20},{20,24},{24,28},{5,9},{9,13},{13,17},... | collective-permute-start | bytes 1228808 | tf_op jit(solution)/shard_map/ppermute | solution.py:182
  86.3 7.1 %collective-permute-done.7.rest_1_ = bf16[25,64,128]{2,1,0:T(8,128)(2,1)S(1)} collective-permute-done((bf16[25,64,128]{2,1,0:T(8,128)(2,1)S(1)}, bf16[25,64,128]{2,1,0:T(8,128)(2,1)S(1)}, u32[]{:S(2)}, u32[]{:S(2)}) %collective-permute-start.7) | collective-permute-done | bytes 409632 | tf_op jit(solution)/shard_map/ppermute | solution.py:182
  93.5 0.7 copy-done.19
  94.2 0.1 stack.54
  94.3 0.1 reshape.806
  94.4 3.2 %gather_fusion = s32[768]{0:T(1024)S(1)} fusion(s32[960]{0:T(1024)S(1)} %reshape.806, s32[1024]{0:T(1024)S(1)} %pad_clamp_fusion.1), kind=kCustom, calls=%fused_computation | custom fusion | bytes 9216 | tf_op jit(solution)/shard_map/jit(_take)/gather | solution.py:236
  97.6 1.2 gather_fusion.1
  98.8 0.1 broadcast_in_dim.32
  98.9 0.1 reshape.740
  99.0 0.6 multiply_add_fusion
  99.7 0.6 fusion.11.pair_ref
  100.3 71.9 %shard_map.55 = f32[64,64,128]{2,1,0:T(8,128)} custom-call(s32[768]{0:T(1024)} %fusion.11.pair_ref, s32[768]{0:T(1024)} %get-tuple-element.45.half_ref, s32[768]{0:T(1024)} %get-tuple-element.29.target_ref, s32[768]{0:T(1024)} %reshape.807.live_ref, s32[192]{0:T(256)} %fusion.32.own_pos_ref, s32[5]{0:T(128)} %stack.59.fix_ref, ...), custom_call_target="tpu_custom_call" | custom-call | tf_op jit(solution)/shard_map/pallas_call | solution.py:120
  172.2 1.5 select_bitcast_fusion.2
  173.7 4.0 %collective-permute-start.22 = (f32[8,2,64,128]{3,2,1,0:T(8,128)S(1)}, f32[8,2,64,128]{3,2,1,0:T(8,128)S(1)}, u32[]{:S(2)}, u32[]{:S(2)}) collective-permute-start(f32[8,2,64,128]{3,2,1,0:T(8,128)S(1)} %get-tuple-element.31), channel_id=1, source_target_pairs={{0,1},{1,2},{2,3},{3,0},{4,5},{5,6},{6,7},{7,4},{8,9},{9,10},{10,1... | collective-permute-start | bytes 1572872 | tf_op jit(solution)/shard_map/ppermute | solution.py:263
  177.7 0.5 collective-permute-start.23
  178.2 0.1 collective-permute-start.24
  178.3 11.7 %collective-permute-done.22 = f32[8,2,64,128]{3,2,1,0:T(8,128)S(1)} collective-permute-done((f32[8,2,64,128]{3,2,1,0:T(8,128)S(1)}, f32[8,2,64,128]{3,2,1,0:T(8,128)S(1)}, u32[]{:S(2)}, u32[]{:S(2)}) %collective-permute-start.22) | collective-permute-done | bytes 524320 | tf_op jit(solution)/shard_map/ppermute | solution.py:263
  190.0 8.1 %collective-permute-done.23 = f32[8,2,64,128]{3,2,1,0:T(8,128)S(1)} collective-permute-done((f32[8,2,64,128]{3,2,1,0:T(8,128)S(1)}, f32[8,2,64,128]{3,2,1,0:T(8,128)S(1)}, u32[]{:S(2)}, u32[]{:S(2)}) %collective-permute-start.23) | collective-permute-done | bytes 524320 | tf_op jit(solution)/shard_map/ppermute | solution.py:263
  198.1 1.2 fusion.2
  199.3 0.2 fusion.46
  199.5 1.1 pad_maximum_fusion
  (86 shorter events, 0.5 us)
Async XLA Ops:
  0.0 9.3 %copy-start.20 = (s32[192,4]{0,1:T(4,128)S(1)}, s32[192,4]{0,1:T(4,128)}, u32[]{:S(2)}) copy-start(s32[192,4]{0,1:T(4,128)} %param.10) | copy-start | bytes 9220
  0.7 9.9 %copy-start.21 = (s32[192]{0:T(256)S(1)}, s32[192]{0:T(256)}, u32[]{:S(2)}) copy-start(s32[192]{0:T(256)} %param.11) | copy-start | bytes 2308
  3.0 25.3 %copy-start.4 = (bf16[25,64,128]{2,1,0:T(8,128)(2,1)}, bf16[25,64,128]{2,1,0:T(8,128)(2,1)S(1)}, u32[]{:S(2)}) copy-start(bf16[25,64,128]{2,1,0:T(8,128)(2,1)S(1)} %fusion.3.rest_8_) | copy-start | bytes 1228804
  3.0 26.5 %collective-permute-start = (bf16[25,64,128]{2,1,0:T(8,128)(2,1)S(1)}, bf16[25,64,128]{2,1,0:T(8,128)(2,1)S(1)}, u32[]{:S(2)}, u32[]{:S(2)}) collective-permute-start(bf16[25,64,128]{2,1,0:T(8,128)(2,1)S(1)} %fusion.3.rest_8_), channel_id=1, source_target_pairs={{28,0},{0,4},{4,8},{8,12},{12,16},{16,20},{20,24},{24,28},{29,1},{... | collective-permute-start | bytes 1228808 | tf_op jit(solution)/shard_map/ppermute | solution.py:182
  3.1 26.5 %collective-permute-start.2 = (bf16[25,64,128]{2,1,0:T(8,128)(2,1)S(1)}, bf16[25,64,128]{2,1,0:T(8,128)(2,1)S(1)}, u32[]{:S(2)}, u32[]{:S(2)}) collective-permute-start(bf16[25,64,128]{2,1,0:T(8,128)(2,1)S(1)} %fusion.3.rest_8_), channel_id=1, source_target_pairs={{4,0},{8,4},{12,8},{16,12},{20,16},{24,20},{28,24},{0,28},{5,1},{9... | collective-permute-start | bytes 1228808 | tf_op jit(solution)/shard_map/ppermute | solution.py:182
  4.8 26.6 %collective-permute-start.13 = (bf16[25,64,128]{2,1,0:T(8,128)(2,1)S(1)}, bf16[25,64,128]{2,1,0:T(8,128)(2,1)}, u32[]{:S(2)}, u32[]{:S(2)}) collective-permute-start(bf16[25,64,128]{2,1,0:T(8,128)(2,1)S(1)} %fusion.3.rest_8_), channel_id=1, source_target_pairs={{0,3},{1,0},{2,1},{3,2},{4,7},{5,4},{6,5},{7,6},{8,11},{9,8},{10,9... | collective-permute-start | bytes 1228808 | tf_op jit(solution)/shard_map/ppermute | solution.py:170
  5.4 29.1 %collective-permute-start.9 = (bf16[25,64,128]{2,1,0:T(8,128)(2,1)S(1)}, bf16[25,64,128]{2,1,0:T(8,128)(2,1)}, u32[]{:S(2)}, u32[]{:S(2)}) collective-permute-start(bf16[25,64,128]{2,1,0:T(8,128)(2,1)S(1)} %fusion.3.rest_8_), channel_id=1, source_target_pairs={{0,2},{1,3},{2,0},{3,1},{4,6},{5,7},{6,4},{7,5},{8,10},{9,11},{10,... | collective-permute-start | bytes 1228808 | tf_op jit(solution)/shard_map/ppermute | solution.py:170
  6.9 38.5 %collective-permute-start.5 = (bf16[25,64,128]{2,1,0:T(8,128)(2,1)S(1)}, bf16[25,64,128]{2,1,0:T(8,128)(2,1)}, u32[]{:S(2)}, u32[]{:S(2)}) collective-permute-start(bf16[25,64,128]{2,1,0:T(8,128)(2,1)S(1)} %fusion.3.rest_8_), channel_id=1, source_target_pairs={{0,1},{1,2},{2,3},{3,0},{4,5},{5,6},{6,7},{7,4},{8,9},{9,10},{10,1... | collective-permute-start | bytes 1228808 | tf_op jit(solution)/shard_map/ppermute | solution.py:170
  29.6 64.7 %copy-start = (bf16[25,64,128]{2,1,0:T(8,128)(2,1)}, bf16[25,64,128]{2,1,0:T(8,128)(2,1)S(1)}, u32[]{:S(2)}) copy-start(bf16[25,64,128]{2,1,0:T(8,128)(2,1)S(1)} %collective-permute-done.rest_4_) | copy-start | bytes 1228804
  29.6 8.1 %collective-permute-start.1 = (bf16[25,64,128]{2,1,0:T(8,128)(2,1)S(1)}, bf16[25,64,128]{2,1,0:T(8,128)(2,1)S(1)}, u32[]{:S(2)}, u32[]{:S(2)}) collective-permute-start(bf16[25,64,128]{2,1,0:T(8,128)(2,1)S(1)} %collective-permute-done.rest_4_), channel_id=1, source_target_pairs={{28,0},{0,4},{4,8},{8,12},{12,16},{16,20},{20,24},{24,28},{29,1},{... | collective-permute-start | bytes 1228808 | tf_op jit(solution)/shard_map/ppermute | solution.py:182
  29.7 64.7 %copy-start.1 = (bf16[25,64,128]{2,1,0:T(8,128)(2,1)}, bf16[25,64,128]{2,1,0:T(8,128)(2,1)S(1)}, u32[]{:S(2)}) copy-start(bf16[25,64,128]{2,1,0:T(8,128)(2,1)S(1)} %collective-permute-done.2.rest_12_) | copy-start | bytes 1228804
  29.7 13.0 %collective-permute-start.3 = (bf16[25,64,128]{2,1,0:T(8,128)(2,1)S(1)}, bf16[25,64,128]{2,1,0:T(8,128)(2,1)S(1)}, u32[]{:S(2)}, u32[]{:S(2)}) collective-permute-start(bf16[25,64,128]{2,1,0:T(8,128)(2,1)S(1)} %collective-permute-done.2.rest_12_), channel_id=1, source_target_pairs={{4,0},{8,4},{12,8},{16,12},{20,16},{24,20},{28,24},{0,28},{5,1},{9... | collective-permute-start | bytes 1228808 | tf_op jit(solution)/shard_map/ppermute | solution.py:182
  31.4 17.2 %collective-permute-start.14 = (bf16[25,64,128]{2,1,0:T(8,128)(2,1)}, bf16[25,64,128]{2,1,0:T(8,128)(2,1)S(1)}, u32[]{:S(2)}, u32[]{:S(2)}) collective-permute-start(bf16[25,64,128]{2,1,0:T(8,128)(2,1)} %collective-permute-done.13.rest_11_), channel_id=1, source_target_pairs={{0,4},{4,8},{8,12},{12,16},{16,20},{20,24},{24,28},{1,5},{5,9},{9,... | collective-permute-start | bytes 1228808 | tf_op jit(solution)/shard_map/ppermute | solution.py:182
  34.4 18.4 %collective-permute-start.18 = (bf16[25,64,128]{2,1,0:T(8,128)(2,1)}, bf16[25,64,128]{2,1,0:T(8,128)(2,1)S(1)}, u32[]{:S(2)}, u32[]{:S(2)}) collective-permute-start(bf16[25,64,128]{2,1,0:T(8,128)(2,1)} %collective-permute-done.13.rest_11_), channel_id=1, source_target_pairs={{4,0},{8,4},{12,8},{16,12},{20,16},{24,20},{28,24},{5,1},{9,5},{13... | collective-permute-start | bytes 1228808 | tf_op jit(solution)/shard_map/ppermute | solution.py:182
  37.7 59.9 %copy-start.2 = (bf16[25,64,128]{2,1,0:T(8,128)(2,1)}, bf16[25,64,128]{2,1,0:T(8,128)(2,1)S(1)}, u32[]{:S(2)}) copy-start(bf16[25,64,128]{2,1,0:T(8,128)(2,1)S(1)} %collective-permute-done.1.rest_0_) | copy-start | bytes 1228804
  37.7 16.5 %collective-permute-start.10 = (bf16[25,64,128]{2,1,0:T(8,128)(2,1)}, bf16[25,64,128]{2,1,0:T(8,128)(2,1)S(1)}, u32[]{:S(2)}, u32[]{:S(2)}) collective-permute-start(bf16[25,64,128]{2,1,0:T(8,128)(2,1)} %collective-permute-done.9.rest_10_), channel_id=1, source_target_pairs={{0,4},{4,8},{8,12},{12,16},{16,20},{20,24},{24,28},{1,5},{5,9},{9,... | collective-permute-start | bytes 1228808 | tf_op jit(solution)/shard_map/ppermute | solution.py:182
  42.7 54.9 %copy-start.3 = (bf16[25,64,128]{2,1,0:T(8,128)(2,1)}, bf16[25,64,128]{2,1,0:T(8,128)(2,1)S(1)}, u32[]{:S(2)}) copy-start(bf16[25,64,128]{2,1,0:T(8,128)(2,1)S(1)} %collective-permute-done.3.rest_16_) | copy-start | bytes 1228804
  42.8 22.3 %collective-permute-start.12 = (bf16[2,25,64,128]{3,2,1,0:T(8,128)(2,1)S(1)}, bf16[2,25,64,128]{3,2,1,0:T(8,128)(2,1)S(1)}, u32[]{:S(2)}, u32[]{:S(2)}) collective-permute-start(bf16[2,25,64,128]{3,2,1,0:T(8,128)(2,1)S(1)} %pad_maximum_fusion.1), channel_id=1, source_target_pairs={{0,3},{1,0},{2,1},{3,2},{4,7},{5,4},{6,5},{7,6},{24,27},{25,24},{2... | collective-permute-start | bytes 2457608 | tf_op jit(solution)/shard_map/ppermute | solution.py:201
  46.1 38.1 %collective-permute-start.8 = (bf16[2,25,64,128]{3,2,1,0:T(8,128)(2,1)S(1)}, bf16[2,25,64,128]{3,2,1,0:T(8,128)(2,1)S(1)}, u32[]{:S(2)}, u32[]{:S(2)}) collective-permute-start(bf16[2,25,64,128]{3,2,1,0:T(8,128)(2,1)S(1)} %pad_maximum_fusion.1), channel_id=1, source_target_pairs={{0,2},{1,3},{2,0},{3,1},{4,6},{5,7},{6,4},{7,5},{24,26},{25,27},{2... | collective-permute-start | bytes 2457608 | tf_op jit(solution)/shard_map/ppermute | solution.py:201
  48.6 51.7 %copy-start.8 = (bf16[25,64,128]{2,1,0:T(8,128)(2,1)}, bf16[25,64,128]{2,1,0:T(8,128)(2,1)S(1)}, u32[]{:S(2)}) copy-start(bf16[25,64,128]{2,1,0:T(8,128)(2,1)S(1)} %collective-permute-done.14.rest_7_) | copy-start | bytes 1228804
  48.6 10.4 %collective-permute-start.15 = (bf16[25,64,128]{2,1,0:T(8,128)(2,1)S(1)}, bf16[25,64,128]{2,1,0:T(8,128)(2,1)S(1)}, u32[]{:S(2)}, u32[]{:S(2)}) collective-permute-start(bf16[25,64,128]{2,1,0:T(8,128)(2,1)S(1)} %collective-permute-done.14.rest_7_), channel_id=1, source_target_pairs={{4,8},{8,12},{12,16},{16,20},{20,24},{24,28},{5,9},{9,13},{13,17},... | collective-permute-start | bytes 1228808 | tf_op jit(solution)/shard_map/ppermute | solution.py:182
  52.9 40.6 %copy-start.9 = (bf16[25,64,128]{2,1,0:T(8,128)(2,1)}, bf16[25,64,128]{2,1,0:T(8,128)(2,1)S(1)}, u32[]{:S(2)}) copy-start(bf16[25,64,128]{2,1,0:T(8,128)(2,1)S(1)} %collective-permute-done.18.rest_15_) | copy-start | bytes 1228804
  52.9 8.1 %collective-permute-start.21 = (bf16[25,64,128]{2,1,0:T(8,128)(2,1)S(1)}, bf16[25,64,128]{2,1,0:T(8,128)(2,1)S(1)}, u32[]{:S(2)}, u32[]{:S(2)}) collective-permute-start(bf16[25,64,128]{2,1,0:T(8,128)(2,1)S(1)} %collective-permute-done.18.rest_15_), channel_id=1, source_target_pairs={{4,0},{8,4},{12,8},{16,12},{20,16},{24,20},{5,1},{9,5},{13,9},{17,... | collective-permute-start | bytes 1228808 | tf_op jit(solution)/shard_map/ppermute | solution.py:182
  54.2 39.2 %copy-start.10 = (bf16[25,64,128]{2,1,0:T(8,128)(2,1)}, bf16[25,64,128]{2,1,0:T(8,128)(2,1)S(1)}, u32[]{:S(2)}) copy-start(bf16[25,64,128]{2,1,0:T(8,128)(2,1)S(1)} %collective-permute-done.10.rest_6_) | copy-start | bytes 1228804
  54.2 32.0 %collective-permute-start.4 = (bf16[2,25,64,128]{3,2,1,0:T(8,128)(2,1)S(1)}, bf16[2,25,64,128]{3,2,1,0:T(8,128)(2,1)S(1)}, u32[]{:S(2)}, u32[]{:S(2)}) collective-permute-start(bf16[2,25,64,128]{3,2,1,0:T(8,128)(2,1)S(1)} %pad_maximum_fusion.1), channel_id=1, source_target_pairs={{0,1},{1,2},{2,3},{3,0},{4,5},{5,6},{6,7},{7,4},{24,25},{25,26},{2... | collective-permute-start | bytes 2457608 | tf_op jit(solution)/shard_map/ppermute | solution.py:201
  59.0 41.2 %copy-start.11 = (bf16[25,64,128]{2,1,0:T(8,128)(2,1)}, bf16[25,64,128]{2,1,0:T(8,128)(2,1)S(1)}, u32[]{:S(2)}) copy-start(bf16[25,64,128]{2,1,0:T(8,128)(2,1)S(1)} %collective-permute-done.15.rest_3_) | copy-start | bytes 1228804
  59.0 11.2 %collective-permute-start.17 = (bf16[25,64,128]{2,1,0:T(8,128)(2,1)}, bf16[25,64,128]{2,1,0:T(8,128)(2,1)S(1)}, u32[]{:S(2)}, u32[]{:S(2)}) collective-permute-start(bf16[25,64,128]{2,1,0:T(8,128)(2,1)} %collective-permute-done.9.rest_10_), channel_id=1, source_target_pairs={{4,0},{8,4},{12,8},{16,12},{20,16},{24,20},{28,24},{5,1},{9,5},{13... | collective-permute-start | bytes 1228808 | tf_op jit(solution)/shard_map/ppermute | solution.py:182
  61.0 32.5 %copy-start.12 = (bf16[25,64,128]{2,1,0:T(8,128)(2,1)}, bf16[25,64,128]{2,1,0:T(8,128)(2,1)S(1)}, u32[]{:S(2)}) copy-start(bf16[25,64,128]{2,1,0:T(8,128)(2,1)S(1)} %collective-permute-done.21.rest_19_) | copy-start | bytes 1228804
  61.0 11.2 %collective-permute-start.16 = (bf16[25,64,128]{2,1,0:T(8,128)(2,1)}, bf16[25,64,128]{2,1,0:T(8,128)(2,1)S(1)}, u32[]{:S(2)}, u32[]{:S(2)}) collective-permute-start(bf16[25,64,128]{2,1,0:T(8,128)(2,1)} %collective-permute-done.5.rest_9_), channel_id=1, source_target_pairs={{4,0},{8,4},{12,8},{16,12},{20,16},{24,20},{28,24},{5,1},{9,5},{13... | collective-permute-start | bytes 1228808 | tf_op jit(solution)/shard_map/ppermute | solution.py:182
  65.1 32.5 %copy-start.5 = (bf16[2,25,64,128]{3,2,1,0:T(8,128)(2,1)}, bf16[2,25,64,128]{3,2,1,0:T(8,128)(2,1)S(1)}, u32[]{:S(2)}) copy-start(bf16[2,25,64,128]{3,2,1,0:T(8,128)(2,1)S(1)} %collective-permute-done.12.rest_22_) | copy-start | bytes 2457604
  65.1 10.8 %collective-permute-start.6 = (bf16[25,64,128]{2,1,0:T(8,128)(2,1)}, bf16[25,64,128]{2,1,0:T(8,128)(2,1)S(1)}, u32[]{:S(2)}, u32[]{:S(2)}) collective-permute-start(bf16[25,64,128]{2,1,0:T(8,128)(2,1)} %collective-permute-done.5.rest_9_), channel_id=1, source_target_pairs={{0,4},{4,8},{8,12},{12,16},{16,20},{20,24},{24,28},{1,5},{5,9},{9,... | collective-permute-start | bytes 1228808 | tf_op jit(solution)/shard_map/ppermute | solution.py:182
  70.2 23.3 %copy-start.13 = (bf16[25,64,128]{2,1,0:T(8,128)(2,1)}, bf16[25,64,128]{2,1,0:T(8,128)(2,1)S(1)}, u32[]{:S(2)}) copy-start(bf16[25,64,128]{2,1,0:T(8,128)(2,1)S(1)} %collective-permute-done.17.rest_14_) | copy-start | bytes 1228804
  70.2 16.0 %collective-permute-start.11 = (bf16[25,64,128]{2,1,0:T(8,128)(2,1)S(1)}, bf16[25,64,128]{2,1,0:T(8,128)(2,1)S(1)}, u32[]{:S(2)}, u32[]{:S(2)}) collective-permute-start(bf16[25,64,128]{2,1,0:T(8,128)(2,1)S(1)} %collective-permute-done.10.rest_6_), channel_id=1, source_target_pairs={{4,8},{8,12},{12,16},{16,20},{20,24},{24,28},{5,9},{9,13},{13,17},... | collective-permute-start | bytes 1228808 | tf_op jit(solution)/shard_map/ppermute | solution.py:182
  72.2 21.3 %copy-start.14 = (bf16[25,64,128]{2,1,0:T(8,128)(2,1)}, bf16[25,64,128]{2,1,0:T(8,128)(2,1)S(1)}, u32[]{:S(2)}) copy-start(bf16[25,64,128]{2,1,0:T(8,128)(2,1)S(1)} %collective-permute-done.16.rest_13_) | copy-start | bytes 1228804
  72.2 14.1 %collective-permute-start.20 = (bf16[25,64,128]{2,1,0:T(8,128)(2,1)S(1)}, bf16[25,64,128]{2,1,0:T(8,128)(2,1)S(1)}, u32[]{:S(2)}, u32[]{:S(2)}) collective-permute-start(bf16[25,64,128]{2,1,0:T(8,128)(2,1)S(1)} %collective-permute-done.17.rest_14_), channel_id=1, source_target_pairs={{4,0},{8,4},{12,8},{16,12},{20,16},{24,20},{5,1},{9,5},{13,9},{17,... | collective-permute-start | bytes 1228808 | tf_op jit(solution)/shard_map/ppermute | solution.py:182
  75.9 17.6 %copy-start.15 = (bf16[25,64,128]{2,1,0:T(8,128)(2,1)}, bf16[25,64,128]{2,1,0:T(8,128)(2,1)S(1)}, u32[]{:S(2)}) copy-start(bf16[25,64,128]{2,1,0:T(8,128)(2,1)S(1)} %collective-permute-done.6.rest_5_) | copy-start | bytes 1228804
  75.9 10.4 %collective-permute-start.19 = (bf16[25,64,128]{2,1,0:T(8,128)(2,1)S(1)}, bf16[25,64,128]{2,1,0:T(8,128)(2,1)S(1)}, u32[]{:S(2)}, u32[]{:S(2)}) collective-permute-start(bf16[25,64,128]{2,1,0:T(8,128)(2,1)S(1)} %collective-permute-done.16.rest_13_), channel_id=1, source_target_pairs={{4,0},{8,4},{12,8},{16,12},{20,16},{24,20},{5,1},{9,5},{13,9},{17,... | collective-permute-start | bytes 1228808 | tf_op jit(solution)/shard_map/ppermute | solution.py:182
  84.2 2.1 %copy-start.6 = (bf16[2,25,64,128]{3,2,1,0:T(8,128)(2,1)}, bf16[2,25,64,128]{3,2,1,0:T(8,128)(2,1)S(1)}, u32[]{:S(2)}) copy-start(bf16[2,25,64,128]{3,2,1,0:T(8,128)(2,1)S(1)} %collective-permute-done.8.rest_21_) | copy-start | bytes 2457604
  84.2 9.3 %collective-permute-start.7 = (bf16[25,64,128]{2,1,0:T(8,128)(2,1)S(1)}, bf16[25,64,128]{2,1,0:T(8,128)(2,1)S(1)}, u32[]{:S(2)}, u32[]{:S(2)}) collective-permute-start(bf16[25,64,128]{2,1,0:T(8,128)(2,1)S(1)} %collective-permute-done.6.rest_5_), channel_id=1, source_target_pairs={{4,8},{8,12},{12,16},{16,20},{20,24},{24,28},{5,9},{9,13},{13,17},... | collective-permute-start | bytes 1228808 | tf_op jit(solution)/shard_map/ppermute | solution.py:182
  86.2 7.2 %copy-start.7 = (bf16[2,25,64,128]{3,2,1,0:T(8,128)(2,1)}, bf16[2,25,64,128]{3,2,1,0:T(8,128)(2,1)S(1)}, u32[]{:S(2)}) copy-start(bf16[2,25,64,128]{3,2,1,0:T(8,128)(2,1)S(1)} %collective-permute-done.4.rest_20_) | copy-start | bytes 2457604
  86.3 7.3 %copy-start.16 = (bf16[25,64,128]{2,1,0:T(8,128)(2,1)}, bf16[25,64,128]{2,1,0:T(8,128)(2,1)S(1)}, u32[]{:S(2)}) copy-start(bf16[25,64,128]{2,1,0:T(8,128)(2,1)S(1)} %collective-permute-done.11.rest_2_) | copy-start | bytes 1228804
  86.3 7.2 %copy-start.17 = (bf16[25,64,128]{2,1,0:T(8,128)(2,1)}, bf16[25,64,128]{2,1,0:T(8,128)(2,1)S(1)}, u32[]{:S(2)}) copy-start(bf16[25,64,128]{2,1,0:T(8,128)(2,1)S(1)} %collective-permute-done.20.rest_18_) | copy-start | bytes 1228804
  86.3 7.2 %copy-start.18 = (bf16[25,64,128]{2,1,0:T(8,128)(2,1)}, bf16[25,64,128]{2,1,0:T(8,128)(2,1)S(1)}, u32[]{:S(2)}) copy-start(bf16[25,64,128]{2,1,0:T(8,128)(2,1)S(1)} %collective-permute-done.19.rest_17_) | copy-start | bytes 1228804
  93.4 0.8 copy-start.19
  173.7 16.3 %collective-permute-start.22 = (f32[8,2,64,128]{3,2,1,0:T(8,128)S(1)}, f32[8,2,64,128]{3,2,1,0:T(8,128)S(1)}, u32[]{:S(2)}, u32[]{:S(2)}) collective-permute-start(f32[8,2,64,128]{3,2,1,0:T(8,128)S(1)} %get-tuple-element.31), channel_id=1, source_target_pairs={{0,1},{1,2},{2,3},{3,0},{4,5},{5,6},{6,7},{7,4},{8,9},{9,10},{10,1... | collective-permute-start | bytes 1572872 | tf_op jit(solution)/shard_map/ppermute | solution.py:263
  177.7 20.4 %collective-permute-start.23 = (f32[8,2,64,128]{3,2,1,0:T(8,128)S(1)}, f32[8,2,64,128]{3,2,1,0:T(8,128)S(1)}, u32[]{:S(2)}, u32[]{:S(2)}) collective-permute-start(f32[8,2,64,128]{3,2,1,0:T(8,128)S(1)} %get-tuple-element.33), channel_id=1, source_target_pairs={{0,2},{1,3},{2,0},{3,1},{4,6},{5,7},{6,4},{7,5},{8,10},{9,11},{10,... | collective-permute-start | bytes 1572872 | tf_op jit(solution)/shard_map/ppermute | solution.py:263
  178.2 19.9 %collective-permute-start.24 = (f32[8,2,64,128]{3,2,1,0:T(8,128)S(1)}, f32[8,2,64,128]{3,2,1,0:T(8,128)S(1)}, u32[]{:S(2)}, u32[]{:S(2)}) collective-permute-start(f32[8,2,64,128]{3,2,1,0:T(8,128)S(1)} %get-tuple-element.32), channel_id=1, source_target_pairs={{0,3},{1,0},{2,1},{3,2},{4,7},{5,4},{6,5},{7,6},{8,11},{9,8},{10,9... | collective-permute-start | bytes 1572872 | tf_op jit(solution)/shard_map/ppermute | solution.py:263

commit v9 on v7

--- a/solution.py
+++ b/solution.py
@@ -20,11 +20,11 @@
 def coarse_kernel(
     pair_ref, half_ref, target_ref, live_ref, own_pos_ref, fix_ref, values_ref, *rest
 ):
-    out_ref, acc_ref, window, sems = rest[-4:]
+    out_ref, acc_ref, window, own_scratch, sems = rest[-5:]
     n_pieces = sems.shape[0]
     groups = n_pieces // 5
     pieces = rest[:n_pieces]
-    fixed = rest[n_pieces:-4]
+    fixed = rest[n_pieces:-5]
     step = pl.program_id(0)
     rows_here, slots, bs, _ = values_ref.shape
     piece_rows = pieces[0].shape[0]
@@ -58,14 +58,20 @@
         for cp in copies:
             cp.wait()
 
+        def transpose_pair(m, carry):
+            own_pair = window[own_pos_ref[2 * m]].astype(jnp.float32)
+            spread = jnp.concatenate([own_pair, jnp.zeros_like(own_pair)], axis=0).T
+            own_scratch[2 * m] = spread[:bs, :bs].astype(jnp.bfloat16)
+            own_scratch[2 * m + 1] = spread[bs:, :bs].astype(jnp.bfloat16)
+            return carry
+
+        lax.fori_loop(0, own_scratch.shape[0] // 2, transpose_pair, 0)
+
     lane_half = lax.broadcasted_iota(jnp.int32, (bs, lanes), 1) // bs
 
     def row_body(r, carry):
         row = step * rows_here + r
-        own_pair = window[own_pos_ref[row]].astype(jnp.float32)
-        spread = jnp.concatenate([own_pair, jnp.zeros_like(own_pair)], axis=0).T
-        own_t = jnp.where(row % 2 == 0, spread[:bs], spread[bs:])[:, :bs]
-        own_t = own_t.astype(jnp.bfloat16)
+        own_t = own_scratch[row]
         results = []
         for s in range(slots):
             n = row * slots + s
@@ -117,6 +123,7 @@
             scratch_shapes=[
                 pltpu.VMEM((n_targets, bs, lanes), jnp.float32),
                 pltpu.VMEM((len(pieces) * piece_rows, bs, lanes), jnp.bfloat16),
+                pltpu.VMEM((panel_length, bs, bs), jnp.bfloat16),
                 pltpu.SemaphoreType.DMA((len(pieces),)),
             ],
         ),

time: 173 us -> 183 us (1.058)
  Pallas kernels: 43.6 us -> 53.4 us
    pallas_call x1, Pallas kernels: 43.6 us -> 53.4 us  [coarse_partial(): pl.pallas_call(coarse_kernel, out_shape=jax.ShapeDtypeStruct((n_targets /...]
  transfers between devices with their start and end apart: 25 -> 25, of which waited for: 5 -> 5; matrix products, arithmetic and copies ran while one was open for 13% -> 12% of each run, Pallas kernels for 0% -> 0%
where the time goes in v9:
time: 183 us; the launch traced here: 182 us
  starting transfers between devices  56.8 us (31%)
  Pallas kernels  53.4 us (29%)
  waiting for transfers between devices  34.9 us (19%)
  local copies, waits for them, and re-layouts  29.3 us (16%)
  other arithmetic  6.72 us (4%)
    pallas_call x1, Pallas kernels, coarse_partial(): pl.pallas_call(coarse_kernel, out_shape=jax.ShapeDtypeStruct((n_targets /...  53.4 us
    ppermute x16, starting transfers between devices, ring(): return lax.ppermute(piece, 'blk', route)  38.6 us
    ppermute x3, waiting for transfers between devices, local(): lax.ppermute(outgoing, 'grp', [(i, (i + k) % group_size) for i in range(g...  19.8 us
    unnamed x45, local copies, waits for them, and re-layouts  17.7 us
    ppermute x3, starting transfers between devices, local(): fixed.append(lax.ppermute(fix_src, ('blk', 'grp'), route))  9.14 us
    ppermute x3, waiting for transfers between devices, local(): fixed.append(lax.ppermute(fix_src, ('blk', 'grp'), route))  8.03 us
    ppermute x16, waiting for transfers between devices, ring(): return lax.ppermute(piece, 'blk', route)  7.14 us
    ppermute x3, starting transfers between devices, local(): lax.ppermute(outgoing, 'grp', [(i, (i + k) % group_size) for i in range(g...  4.67 us
  transfers between devices with their start and end apart: 25, of which 5 were waited for; matrix products, arithmetic and copies ran while one was open for 12% of the time, Pallas kernels for 0%

profile of v9, /device:TPU:26, one launch (start us, length us, event | category | flops | bytes accessed | tf_op | source)
XLA Modules:
  0.0 182.1 jit_solution(3446299486480272970)
XLA Ops:
  0.0 0.7 convert_bitcast_fusion
  0.7 2.0 %copy.17 = bf16[24,2,64,64]{3,1,2,0:T(2,128)(2,1)S(1)} copy(bf16[24,2,64,64]{3,2,1,0:T(8,128)(2,1)} %bitcast.144) | data formatting | bytes 786432 | tf_op jit(solution)/shard_map/reshape | solution.py:149
  2.6 0.3 reshape.739
  3.1 1.7 collective-permute-start.2
  4.8 0.5 collective-permute-start.13
  5.4 1.5 collective-permute-start.9
  6.9 2.4 %collective-permute-start.5 = (bf16[25,64,128]{2,1,0:T(8,128)(2,1)S(1)}, bf16[25,64,128]{2,1,0:T(8,128)(2,1)}, u32[]{:S(2)}, u32[]{:S(2)}) collective-permute-start(bf16[25,64,128]{2,1,0:T(8,128)(2,1)S(1)} %fusion.3.rest_8_), channel_id=1, source_target_pairs={{0,1},{1,2},{2,3},{3,0},{4,5},{5,6},{6,7},{7,4},{8,9},{9,10},{10,1... | collective-permute-start | bytes 1228808 | tf_op jit(solution)/shard_map/ppermute | solution.py:163
  9.3 0.1 copy.9
  9.4 0.1 rem.301
  9.6 0.1 rem.276
  9.7 0.1 copy.10
  9.8 0.1 div.78
  9.9 0.1 div.73
  10.0 0.2 copy.8
  10.2 0.1 ne.313
  10.3 0.1 ne.303
  10.5 0.1 compare_convert_fusion
  10.6 0.7 reshape.807.live_ref
  11.3 17.0 %copy.15.values_ref = bf16[192,4,64,64]{3,2,1,0:T(8,128)(2,1)} copy(bf16[192,4,64,64]{0,3,2,1:T(8,128)(2,1)} %param.9) | data formatting | bytes 12582912 | tf_op args[0]
  28.3 0.6 stack.59.fix_ref
  28.9 0.6 fusion.32.own_pos_ref
  29.5 0.1 fusion.16
  29.7 1.7 collective-permute-start.3
  31.4 2.3 %collective-permute-start.14 = (bf16[25,64,128]{2,1,0:T(8,128)(2,1)}, bf16[25,64,128]{2,1,0:T(8,128)(2,1)S(1)}, u32[]{:S(2)}, u32[]{:S(2)}) collective-permute-start(bf16[25,64,128]{2,1,0:T(8,128)(2,1)} %collective-permute-done.13.rest_11_), channel_id=1, source_target_pairs={{0,4},{4,8},{8,12},{12,16},{16,20},{20,24},{24,28},{1,5},{5,9},{9,... | collective-permute-start | bytes 1228808 | tf_op jit(solution)/shard_map/ppermute | solution.py:175
  33.7 0.7 slice_bitcast_fusion.8
  34.4 3.2 %collective-permute-start.18 = (bf16[25,64,128]{2,1,0:T(8,128)(2,1)}, bf16[25,64,128]{2,1,0:T(8,128)(2,1)S(1)}, u32[]{:S(2)}, u32[]{:S(2)}) collective-permute-start(bf16[25,64,128]{2,1,0:T(8,128)(2,1)} %collective-permute-done.13.rest_11_), channel_id=1, source_target_pairs={{4,0},{8,4},{12,8},{16,12},{20,16},{24,20},{28,24},{5,1},{9,5},{13... | collective-permute-start | bytes 1228808 | tf_op jit(solution)/shard_map/ppermute | solution.py:175
  37.7 4.9 %collective-permute-start.10 = (bf16[25,64,128]{2,1,0:T(8,128)(2,1)}, bf16[25,64,128]{2,1,0:T(8,128)(2,1)S(1)}, u32[]{:S(2)}, u32[]{:S(2)}) collective-permute-start(bf16[25,64,128]{2,1,0:T(8,128)(2,1)} %collective-permute-done.9.rest_10_), channel_id=1, source_target_pairs={{0,4},{4,8},{8,12},{12,16},{16,20},{20,24},{24,28},{1,5},{5,9},{9,... | collective-permute-start | bytes 1228808 | tf_op jit(solution)/shard_map/ppermute | solution.py:175
  42.7 0.1 pad_maximum_fusion.1
  42.8 1.9 %collective-permute-start.12 = (bf16[2,25,64,128]{3,2,1,0:T(8,128)(2,1)S(1)}, bf16[2,25,64,128]{3,2,1,0:T(8,128)(2,1)S(1)}, u32[]{:S(2)}, u32[]{:S(2)}) collective-permute-start(bf16[2,25,64,128]{3,2,1,0:T(8,128)(2,1)S(1)} %pad_maximum_fusion.1), channel_id=1, source_target_pairs={{0,3},{1,0},{2,1},{3,2},{4,7},{5,4},{6,5},{7,6},{24,27},{25,24},{2... | collective-permute-start | bytes 2457608 | tf_op jit(solution)/shard_map/ppermute | solution.py:194
  44.7 0.7 slice_bitcast_fusion.9
  45.4 0.7 slice_bitcast_fusion.10
  46.1 2.5 %collective-permute-start.8 = (bf16[2,25,64,128]{3,2,1,0:T(8,128)(2,1)S(1)}, bf16[2,25,64,128]{3,2,1,0:T(8,128)(2,1)S(1)}, u32[]{:S(2)}, u32[]{:S(2)}) collective-permute-start(bf16[2,25,64,128]{3,2,1,0:T(8,128)(2,1)S(1)} %pad_maximum_fusion.1), channel_id=1, source_target_pairs={{0,2},{1,3},{2,0},{3,1},{4,6},{5,7},{6,4},{7,5},{24,26},{25,27},{2... | collective-permute-start | bytes 2457608 | tf_op jit(solution)/shard_map/ppermute | solution.py:194
  48.6 4.3 %collective-permute-start.15 = (bf16[25,64,128]{2,1,0:T(8,128)(2,1)S(1)}, bf16[25,64,128]{2,1,0:T(8,128)(2,1)S(1)}, u32[]{:S(2)}, u32[]{:S(2)}) collective-permute-start(bf16[25,64,128]{2,1,0:T(8,128)(2,1)S(1)} %collective-permute-done.14.rest_7_), channel_id=1, source_target_pairs={{4,8},{8,12},{12,16},{16,20},{20,24},{24,28},{5,9},{9,13},{13,17},... | collective-permute-start | bytes 1228808 | tf_op jit(solution)/shard_map/ppermute | solution.py:175
  52.9 1.3 collective-permute-start.21
  54.2 4.8 %collective-permute-start.4 = (bf16[2,25,64,128]{3,2,1,0:T(8,128)(2,1)S(1)}, bf16[2,25,64,128]{3,2,1,0:T(8,128)(2,1)S(1)}, u32[]{:S(2)}, u32[]{:S(2)}) collective-permute-start(bf16[2,25,64,128]{3,2,1,0:T(8,128)(2,1)S(1)} %pad_maximum_fusion.1), channel_id=1, source_target_pairs={{0,1},{1,2},{2,3},{3,0},{4,5},{5,6},{6,7},{7,4},{24,25},{25,26},{2... | collective-permute-start | bytes 2457608 | tf_op jit(solution)/shard_map/ppermute | solution.py:194
  59.0 1.9 %collective-permute-start.17 = (bf16[25,64,128]{2,1,0:T(8,128)(2,1)}, bf16[25,64,128]{2,1,0:T(8,128)(2,1)S(1)}, u32[]{:S(2)}, u32[]{:S(2)}) collective-permute-start(bf16[25,64,128]{2,1,0:T(8,128)(2,1)} %collective-permute-done.9.rest_10_), channel_id=1, source_target_pairs={{4,0},{8,4},{12,8},{16,12},{20,16},{24,20},{28,24},{5,1},{9,5},{13... | collective-permute-start | bytes 1228808 | tf_op jit(solution)/shard_map/ppermute | solution.py:175
  61.0 2.4 %collective-permute-start.16 = (bf16[25,64,128]{2,1,0:T(8,128)(2,1)}, bf16[25,64,128]{2,1,0:T(8,128)(2,1)S(1)}, u32[]{:S(2)}, u32[]{:S(2)}) collective-permute-start(bf16[25,64,128]{2,1,0:T(8,128)(2,1)} %collective-permute-done.5.rest_9_), channel_id=1, source_target_pairs={{4,0},{8,4},{12,8},{16,12},{20,16},{24,20},{28,24},{5,1},{9,5},{13... | collective-permute-start | bytes 1228808 | tf_op jit(solution)/shard_map/ppermute | solution.py:175
  63.4 1.7 collective-permute-done.12.rest_22_
  65.1 5.1 %collective-permute-start.6 = (bf16[25,64,128]{2,1,0:T(8,128)(2,1)}, bf16[25,64,128]{2,1,0:T(8,128)(2,1)S(1)}, u32[]{:S(2)}, u32[]{:S(2)}) collective-permute-start(bf16[25,64,128]{2,1,0:T(8,128)(2,1)} %collective-permute-done.5.rest_9_), channel_id=1, source_target_pairs={{0,4},{4,8},{8,12},{12,16},{16,20},{20,24},{24,28},{1,5},{5,9},{9,... | collective-permute-start | bytes 1228808 | tf_op jit(solution)/shard_map/ppermute | solution.py:175
  70.2 1.9 %collective-permute-start.11 = (bf16[25,64,128]{2,1,0:T(8,128)(2,1)S(1)}, bf16[25,64,128]{2,1,0:T(8,128)(2,1)S(1)}, u32[]{:S(2)}, u32[]{:S(2)}) collective-permute-start(bf16[25,64,128]{2,1,0:T(8,128)(2,1)S(1)} %collective-permute-done.10.rest_6_), channel_id=1, source_target_pairs={{4,8},{8,12},{12,16},{16,20},{20,24},{24,28},{5,9},{9,13},{13,17},... | collective-permute-start | bytes 1228808 | tf_op jit(solution)/shard_map/ppermute | solution.py:175
  72.2 3.7 %collective-permute-start.20 = (bf16[25,64,128]{2,1,0:T(8,128)(2,1)S(1)}, bf16[25,64,128]{2,1,0:T(8,128)(2,1)S(1)}, u32[]{:S(2)}, u32[]{:S(2)}) collective-permute-start(bf16[25,64,128]{2,1,0:T(8,128)(2,1)S(1)} %collective-permute-done.17.rest_14_), channel_id=1, source_target_pairs={{4,0},{8,4},{12,8},{16,12},{20,16},{24,20},{5,1},{9,5},{13,9},{17,... | collective-permute-start | bytes 1228808 | tf_op jit(solution)/shard_map/ppermute | solution.py:175
  75.9 1.9 %collective-permute-start.19 = (bf16[25,64,128]{2,1,0:T(8,128)(2,1)S(1)}, bf16[25,64,128]{2,1,0:T(8,128)(2,1)S(1)}, u32[]{:S(2)}, u32[]{:S(2)}) collective-permute-start(bf16[25,64,128]{2,1,0:T(8,128)(2,1)S(1)} %collective-permute-done.16.rest_13_), channel_id=1, source_target_pairs={{4,0},{8,4},{12,8},{16,12},{20,16},{24,20},{5,1},{9,5},{13,9},{17,... | collective-permute-start | bytes 1228808 | tf_op jit(solution)/shard_map/ppermute | solution.py:175
  77.8 6.4 %collective-permute-done.8.rest_21_ = bf16[2,25,64,128]{3,2,1,0:T(8,128)(2,1)S(1)} collective-permute-done((bf16[2,25,64,128]{3,2,1,0:T(8,128)(2,1)S(1)}, bf16[2,25,64,128]{3,2,1,0:T(8,128)(2,1)S(1)}, u32[]{:S(2)}, u32[]{:S(2)}) %collective-permute-start.8) | collective-permute-done | bytes 819232 | tf_op jit(solution)/shard_map/ppermute | solution.py:194
  84.2 2.0 %collective-permute-start.7 = (bf16[25,64,128]{2,1,0:T(8,128)(2,1)S(1)}, bf16[25,64,128]{2,1,0:T(8,128)(2,1)S(1)}, u32[]{:S(2)}, u32[]{:S(2)}) collective-permute-start(bf16[25,64,128]{2,1,0:T(8,128)(2,1)S(1)} %collective-permute-done.6.rest_5_), channel_id=1, source_target_pairs={{4,8},{8,12},{12,16},{16,20},{20,24},{24,28},{5,9},{9,13},{13,17},... | collective-permute-start | bytes 1228808 | tf_op jit(solution)/shard_map/ppermute | solution.py:175
  86.3 7.1 %collective-permute-done.7.rest_1_ = bf16[25,64,128]{2,1,0:T(8,128)(2,1)S(1)} collective-permute-done((bf16[25,64,128]{2,1,0:T(8,128)(2,1)S(1)}, bf16[25,64,128]{2,1,0:T(8,128)(2,1)S(1)}, u32[]{:S(2)}, u32[]{:S(2)}) %collective-permute-start.7) | collective-permute-done | bytes 409632 | tf_op jit(solution)/shard_map/ppermute | solution.py:175
  93.5 0.7 copy-done.19
  94.2 0.1 stack.54
  94.3 0.1 reshape.806
  94.4 3.2 %gather_fusion = s32[768]{0:T(1024)S(1)} fusion(s32[960]{0:T(1024)S(1)} %reshape.806, s32[1024]{0:T(1024)S(1)} %pad_clamp_fusion.1), kind=kCustom, calls=%fused_computation | custom fusion | bytes 9216 | tf_op jit(solution)/shard_map/jit(_take)/gather | solution.py:229
  97.6 1.2 gather_fusion.1
  98.8 0.1 broadcast_in_dim.32
  98.9 0.1 reshape.740
  99.0 0.6 multiply_add_fusion
  99.7 0.6 fusion.11.pair_ref
  100.3 53.4 %shard_map.55 = f32[64,64,128]{2,1,0:T(8,128)} custom-call(s32[768]{0:T(1024)} %fusion.11.pair_ref, s32[768]{0:T(1024)} %get-tuple-element.45.half_ref, s32[768]{0:T(1024)} %get-tuple-element.29.target_ref, s32[768]{0:T(1024)} %reshape.807.live_ref, s32[192]{0:T(256)} %fusion.32.own_pos_ref, s32[5]{0:T(128)} %stack.59.fix_ref, ...), custom_call_target="tpu_custom_call" | custom-call | tf_op jit(solution)/shard_map/pallas_call | solution.py:112
  153.7 1.5 select_bitcast_fusion.2
  155.2 4.0 %collective-permute-start.22 = (f32[8,2,64,128]{3,2,1,0:T(8,128)S(1)}, f32[8,2,64,128]{3,2,1,0:T(8,128)S(1)}, u32[]{:S(2)}, u32[]{:S(2)}) collective-permute-start(f32[8,2,64,128]{3,2,1,0:T(8,128)S(1)} %get-tuple-element.31), channel_id=1, source_target_pairs={{0,1},{1,2},{2,3},{3,0},{4,5},{5,6},{6,7},{7,4},{8,9},{9,10},{10,1... | collective-permute-start | bytes 1572872 | tf_op jit(solution)/shard_map/ppermute | solution.py:256
  159.3 0.5 collective-permute-start.23
  159.8 0.1 collective-permute-start.24
  159.9 11.7 %collective-permute-done.22 = f32[8,2,64,128]{3,2,1,0:T(8,128)S(1)} collective-permute-done((f32[8,2,64,128]{3,2,1,0:T(8,128)S(1)}, f32[8,2,64,128]{3,2,1,0:T(8,128)S(1)}, u32[]{:S(2)}, u32[]{:S(2)}) %collective-permute-start.22) | collective-permute-done | bytes 524320 | tf_op jit(solution)/shard_map/ppermute | solution.py:256
  171.6 8.1 %collective-permute-done.23 = f32[8,2,64,128]{3,2,1,0:T(8,128)S(1)} collective-permute-done((f32[8,2,64,128]{3,2,1,0:T(8,128)S(1)}, f32[8,2,64,128]{3,2,1,0:T(8,128)S(1)}, u32[]{:S(2)}, u32[]{:S(2)}) %collective-permute-start.23) | collective-permute-done | bytes 524320 | tf_op jit(solution)/shard_map/ppermute | solution.py:256
  179.7 1.2 fusion.2
  180.9 0.2 fusion.46
  181.1 1.1 pad_maximum_fusion
  (86 shorter events, 0.5 us)
Async XLA Ops:
  0.0 9.3 %copy-start.20 = (s32[192,4]{0,1:T(4,128)S(1)}, s32[192,4]{0,1:T(4,128)}, u32[]{:S(2)}) copy-start(s32[192,4]{0,1:T(4,128)} %param.10) | copy-start | bytes 9220
  0.7 9.9 %copy-start.21 = (s32[192]{0:T(256)S(1)}, s32[192]{0:T(256)}, u32[]{:S(2)}) copy-start(s32[192]{0:T(256)} %param.11) | copy-start | bytes 2308
  3.0 25.3 %copy-start.4 = (bf16[25,64,128]{2,1,0:T(8,128)(2,1)}, bf16[25,64,128]{2,1,0:T(8,128)(2,1)S(1)}, u32[]{:S(2)}) copy-start(bf16[25,64,128]{2,1,0:T(8,128)(2,1)S(1)} %fusion.3.rest_8_) | copy-start | bytes 1228804
  3.0 26.5 %collective-permute-start = (bf16[25,64,128]{2,1,0:T(8,128)(2,1)S(1)}, bf16[25,64,128]{2,1,0:T(8,128)(2,1)S(1)}, u32[]{:S(2)}, u32[]{:S(2)}) collective-permute-start(bf16[25,64,128]{2,1,0:T(8,128)(2,1)S(1)} %fusion.3.rest_8_), channel_id=1, source_target_pairs={{28,0},{0,4},{4,8},{8,12},{12,16},{16,20},{20,24},{24,28},{29,1},{... | collective-permute-start | bytes 1228808 | tf_op jit(solution)/shard_map/ppermute | solution.py:175
  3.1 26.5 %collective-permute-start.2 = (bf16[25,64,128]{2,1,0:T(8,128)(2,1)S(1)}, bf16[25,64,128]{2,1,0:T(8,128)(2,1)S(1)}, u32[]{:S(2)}, u32[]{:S(2)}) collective-permute-start(bf16[25,64,128]{2,1,0:T(8,128)(2,1)S(1)} %fusion.3.rest_8_), channel_id=1, source_target_pairs={{4,0},{8,4},{12,8},{16,12},{20,16},{24,20},{28,24},{0,28},{5,1},{9... | collective-permute-start | bytes 1228808 | tf_op jit(solution)/shard_map/ppermute | solution.py:175
  4.8 26.6 %collective-permute-start.13 = (bf16[25,64,128]{2,1,0:T(8,128)(2,1)S(1)}, bf16[25,64,128]{2,1,0:T(8,128)(2,1)}, u32[]{:S(2)}, u32[]{:S(2)}) collective-permute-start(bf16[25,64,128]{2,1,0:T(8,128)(2,1)S(1)} %fusion.3.rest_8_), channel_id=1, source_target_pairs={{0,3},{1,0},{2,1},{3,2},{4,7},{5,4},{6,5},{7,6},{8,11},{9,8},{10,9... | collective-permute-start | bytes 1228808 | tf_op jit(solution)/shard_map/ppermute | solution.py:163
  5.4 29.1 %collective-permute-start.9 = (bf16[25,64,128]{2,1,0:T(8,128)(2,1)S(1)}, bf16[25,64,128]{2,1,0:T(8,128)(2,1)}, u32[]{:S(2)}, u32[]{:S(2)}) collective-permute-start(bf16[25,64,128]{2,1,0:T(8,128)(2,1)S(1)} %fusion.3.rest_8_), channel_id=1, source_target_pairs={{0,2},{1,3},{2,0},{3,1},{4,6},{5,7},{6,4},{7,5},{8,10},{9,11},{10,... | collective-permute-start | bytes 1228808 | tf_op jit(solution)/shard_map/ppermute | solution.py:163
  6.9 38.5 %collective-permute-start.5 = (bf16[25,64,128]{2,1,0:T(8,128)(2,1)S(1)}, bf16[25,64,128]{2,1,0:T(8,128)(2,1)}, u32[]{:S(2)}, u32[]{:S(2)}) collective-permute-start(bf16[25,64,128]{2,1,0:T(8,128)(2,1)S(1)} %fusion.3.rest_8_), channel_id=1, source_target_pairs={{0,1},{1,2},{2,3},{3,0},{4,5},{5,6},{6,7},{7,4},{8,9},{9,10},{10,1... | collective-permute-start | bytes 1228808 | tf_op jit(solution)/shard_map/ppermute | solution.py:163
  29.6 64.7 %copy-start = (bf16[25,64,128]{2,1,0:T(8,128)(2,1)}, bf16[25,64,128]{2,1,0:T(8,128)(2,1)S(1)}, u32[]{:S(2)}) copy-start(bf16[25,64,128]{2,1,0:T(8,128)(2,1)S(1)} %collective-permute-done.rest_4_) | copy-start | bytes 1228804
  29.6 8.1 %collective-permute-start.1 = (bf16[25,64,128]{2,1,0:T(8,128)(2,1)S(1)}, bf16[25,64,128]{2,1,0:T(8,128)(2,1)S(1)}, u32[]{:S(2)}, u32[]{:S(2)}) collective-permute-start(bf16[25,64,128]{2,1,0:T(8,128)(2,1)S(1)} %collective-permute-done.rest_4_), channel_id=1, source_target_pairs={{28,0},{0,4},{4,8},{8,12},{12,16},{16,20},{20,24},{24,28},{29,1},{... | collective-permute-start | bytes 1228808 | tf_op jit(solution)/shard_map/ppermute | solution.py:175
  29.7 64.7 %copy-start.1 = (bf16[25,64,128]{2,1,0:T(8,128)(2,1)}, bf16[25,64,128]{2,1,0:T(8,128)(2,1)S(1)}, u32[]{:S(2)}) copy-start(bf16[25,64,128]{2,1,0:T(8,128)(2,1)S(1)} %collective-permute-done.2.rest_12_) | copy-start | bytes 1228804
  29.7 13.0 %collective-permute-start.3 = (bf16[25,64,128]{2,1,0:T(8,128)(2,1)S(1)}, bf16[25,64,128]{2,1,0:T(8,128)(2,1)S(1)}, u32[]{:S(2)}, u32[]{:S(2)}) collective-permute-start(bf16[25,64,128]{2,1,0:T(8,128)(2,1)S(1)} %collective-permute-done.2.rest_12_), channel_id=1, source_target_pairs={{4,0},{8,4},{12,8},{16,12},{20,16},{24,20},{28,24},{0,28},{5,1},{9... | collective-permute-start | bytes 1228808 | tf_op jit(solution)/shard_map/ppermute | solution.py:175
  31.4 17.2 %collective-permute-start.14 = (bf16[25,64,128]{2,1,0:T(8,128)(2,1)}, bf16[25,64,128]{2,1,0:T(8,128)(2,1)S(1)}, u32[]{:S(2)}, u32[]{:S(2)}) collective-permute-start(bf16[25,64,128]{2,1,0:T(8,128)(2,1)} %collective-permute-done.13.rest_11_), channel_id=1, source_target_pairs={{0,4},{4,8},{8,12},{12,16},{16,20},{20,24},{24,28},{1,5},{5,9},{9,... | collective-permute-start | bytes 1228808 | tf_op jit(solution)/shard_map/ppermute | solution.py:175
  34.4 18.4 %collective-permute-start.18 = (bf16[25,64,128]{2,1,0:T(8,128)(2,1)}, bf16[25,64,128]{2,1,0:T(8,128)(2,1)S(1)}, u32[]{:S(2)}, u32[]{:S(2)}) collective-permute-start(bf16[25,64,128]{2,1,0:T(8,128)(2,1)} %collective-permute-done.13.rest_11_), channel_id=1, source_target_pairs={{4,0},{8,4},{12,8},{16,12},{20,16},{24,20},{28,24},{5,1},{9,5},{13... | collective-permute-start | bytes 1228808 | tf_op jit(solution)/shard_map/ppermute | solution.py:175
  37.7 59.9 %copy-start.2 = (bf16[25,64,128]{2,1,0:T(8,128)(2,1)}, bf16[25,64,128]{2,1,0:T(8,128)(2,1)S(1)}, u32[]{:S(2)}) copy-start(bf16[25,64,128]{2,1,0:T(8,128)(2,1)S(1)} %collective-permute-done.1.rest_0_) | copy-start | bytes 1228804
  37.7 16.5 %collective-permute-start.10 = (bf16[25,64,128]{2,1,0:T(8,128)(2,1)}, bf16[25,64,128]{2,1,0:T(8,128)(2,1)S(1)}, u32[]{:S(2)}, u32[]{:S(2)}) collective-permute-start(bf16[25,64,128]{2,1,0:T(8,128)(2,1)} %collective-permute-done.9.rest_10_), channel_id=1, source_target_pairs={{0,4},{4,8},{8,12},{12,16},{16,20},{20,24},{24,28},{1,5},{5,9},{9,... | collective-permute-start | bytes 1228808 | tf_op jit(solution)/shard_map/ppermute | solution.py:175
  42.7 54.9 %copy-start.3 = (bf16[25,64,128]{2,1,0:T(8,128)(2,1)}, bf16[25,64,128]{2,1,0:T(8,128)(2,1)S(1)}, u32[]{:S(2)}) copy-start(bf16[25,64,128]{2,1,0:T(8,128)(2,1)S(1)} %collective-permute-done.3.rest_16_) | copy-start | bytes 1228804
  42.8 22.3 %collective-permute-start.12 = (bf16[2,25,64,128]{3,2,1,0:T(8,128)(2,1)S(1)}, bf16[2,25,64,128]{3,2,1,0:T(8,128)(2,1)S(1)}, u32[]{:S(2)}, u32[]{:S(2)}) collective-permute-start(bf16[2,25,64,128]{3,2,1,0:T(8,128)(2,1)S(1)} %pad_maximum_fusion.1), channel_id=1, source_target_pairs={{0,3},{1,0},{2,1},{3,2},{4,7},{5,4},{6,5},{7,6},{24,27},{25,24},{2... | collective-permute-start | bytes 2457608 | tf_op jit(solution)/shard_map/ppermute | solution.py:194
  46.1 38.1 %collective-permute-start.8 = (bf16[2,25,64,128]{3,2,1,0:T(8,128)(2,1)S(1)}, bf16[2,25,64,128]{3,2,1,0:T(8,128)(2,1)S(1)}, u32[]{:S(2)}, u32[]{:S(2)}) collective-permute-start(bf16[2,25,64,128]{3,2,1,0:T(8,128)(2,1)S(1)} %pad_maximum_fusion.1), channel_id=1, source_target_pairs={{0,2},{1,3},{2,0},{3,1},{4,6},{5,7},{6,4},{7,5},{24,26},{25,27},{2... | collective-permute-start | bytes 2457608 | tf_op jit(solution)/shard_map/ppermute | solution.py:194
  48.6 51.7 %copy-start.8 = (bf16[25,64,128]{2,1,0:T(8,128)(2,1)}, bf16[25,64,128]{2,1,0:T(8,128)(2,1)S(1)}, u32[]{:S(2)}) copy-start(bf16[25,64,128]{2,1,0:T(8,128)(2,1)S(1)} %collective-permute-done.14.rest_7_) | copy-start | bytes 1228804
  48.6 10.4 %collective-permute-start.15 = (bf16[25,64,128]{2,1,0:T(8,128)(2,1)S(1)}, bf16[25,64,128]{2,1,0:T(8,128)(2,1)S(1)}, u32[]{:S(2)}, u32[]{:S(2)}) collective-permute-start(bf16[25,64,128]{2,1,0:T(8,128)(2,1)S(1)} %collective-permute-done.14.rest_7_), channel_id=1, source_target_pairs={{4,8},{8,12},{12,16},{16,20},{20,24},{24,28},{5,9},{9,13},{13,17},... | collective-permute-start | bytes 1228808 | tf_op jit(solution)/shard_map/ppermute | solution.py:175
  52.9 40.6 %copy-start.9 = (bf16[25,64,128]{2,1,0:T(8,128)(2,1)}, bf16[25,64,128]{2,1,0:T(8,128)(2,1)S(1)}, u32[]{:S(2)}) copy-start(bf16[25,64,128]{2,1,0:T(8,128)(2,1)S(1)} %collective-permute-done.18.rest_15_) | copy-start | bytes 1228804
  52.9 8.1 %collective-permute-start.21 = (bf16[25,64,128]{2,1,0:T(8,128)(2,1)S(1)}, bf16[25,64,128]{2,1,0:T(8,128)(2,1)S(1)}, u32[]{:S(2)}, u32[]{:S(2)}) collective-permute-start(bf16[25,64,128]{2,1,0:T(8,128)(2,1)S(1)} %collective-permute-done.18.rest_15_), channel_id=1, source_target_pairs={{4,0},{8,4},{12,8},{16,12},{20,16},{24,20},{5,1},{9,5},{13,9},{17,... | collective-permute-start | bytes 1228808 | tf_op jit(solution)/shard_map/ppermute | solution.py:175
  54.2 39.2 %copy-start.10 = (bf16[25,64,128]{2,1,0:T(8,128)(2,1)}, bf16[25,64,128]{2,1,0:T(8,128)(2,1)S(1)}, u32[]{:S(2)}) copy-start(bf16[25,64,128]{2,1,0:T(8,128)(2,1)S(1)} %collective-permute-done.10.rest_6_) | copy-start | bytes 1228804
  54.2 32.0 %collective-permute-start.4 = (bf16[2,25,64,128]{3,2,1,0:T(8,128)(2,1)S(1)}, bf16[2,25,64,128]{3,2,1,0:T(8,128)(2,1)S(1)}, u32[]{:S(2)}, u32[]{:S(2)}) collective-permute-start(bf16[2,25,64,128]{3,2,1,0:T(8,128)(2,1)S(1)} %pad_maximum_fusion.1), channel_id=1, source_target_pairs={{0,1},{1,2},{2,3},{3,0},{4,5},{5,6},{6,7},{7,4},{24,25},{25,26},{2... | collective-permute-start | bytes 2457608 | tf_op jit(solution)/shard_map/ppermute | solution.py:194
  59.0 41.2 %copy-start.11 = (bf16[25,64,128]{2,1,0:T(8,128)(2,1)}, bf16[25,64,128]{2,1,0:T(8,128)(2,1)S(1)}, u32[]{:S(2)}) copy-start(bf16[25,64,128]{2,1,0:T(8,128)(2,1)S(1)} %collective-permute-done.15.rest_3_) | copy-start | bytes 1228804
  59.0 11.2 %collective-permute-start.17 = (bf16[25,64,128]{2,1,0:T(8,128)(2,1)}, bf16[25,64,128]{2,1,0:T(8,128)(2,1)S(1)}, u32[]{:S(2)}, u32[]{:S(2)}) collective-permute-start(bf16[25,64,128]{2,1,0:T(8,128)(2,1)} %collective-permute-done.9.rest_10_), channel_id=1, source_target_pairs={{4,0},{8,4},{12,8},{16,12},{20,16},{24,20},{28,24},{5,1},{9,5},{13... | collective-permute-start | bytes 1228808 | tf_op jit(solution)/shard_map/ppermute | solution.py:175
  61.0 32.5 %copy-start.12 = (bf16[25,64,128]{2,1,0:T(8,128)(2,1)}, bf16[25,64,128]{2,1,0:T(8,128)(2,1)S(1)}, u32[]{:S(2)}) copy-start(bf16[25,64,128]{2,1,0:T(8,128)(2,1)S(1)} %collective-permute-done.21.rest_19_) | copy-start | bytes 1228804
  61.0 11.2 %collective-permute-start.16 = (bf16[25,64,128]{2,1,0:T(8,128)(2,1)}, bf16[25,64,128]{2,1,0:T(8,128)(2,1)S(1)}, u32[]{:S(2)}, u32[]{:S(2)}) collective-permute-start(bf16[25,64,128]{2,1,0:T(8,128)(2,1)} %collective-permute-done.5.rest_9_), channel_id=1, source_target_pairs={{4,0},{8,4},{12,8},{16,12},{20,16},{24,20},{28,24},{5,1},{9,5},{13... | collective-permute-start | bytes 1228808 | tf_op jit(solution)/shard_map/ppermute | solution.py:175
  65.1 32.5 %copy-start.5 = (bf16[2,25,64,128]{3,2,1,0:T(8,128)(2,1)}, bf16[2,25,64,128]{3,2,1,0:T(8,128)(2,1)S(1)}, u32[]{:S(2)}) copy-start(bf16[2,25,64,128]{3,2,1,0:T(8,128)(2,1)S(1)} %collective-permute-done.12.rest_22_) | copy-start | bytes 2457604
  65.1 10.8 %collective-permute-start.6 = (bf16[25,64,128]{2,1,0:T(8,128)(2,1)}, bf16[25,64,128]{2,1,0:T(8,128)(2,1)S(1)}, u32[]{:S(2)}, u32[]{:S(2)}) collective-permute-start(bf16[25,64,128]{2,1,0:T(8,128)(2,1)} %collective-permute-done.5.rest_9_), channel_id=1, source_target_pairs={{0,4},{4,8},{8,12},{12,16},{16,20},{20,24},{24,28},{1,5},{5,9},{9,... | collective-permute-start | bytes 1228808 | tf_op jit(solution)/shard_map/ppermute | solution.py:175
  70.2 23.3 %copy-start.13 = (bf16[25,64,128]{2,1,0:T(8,128)(2,1)}, bf16[25,64,128]{2,1,0:T(8,128)(2,1)S(1)}, u32[]{:S(2)}) copy-start(bf16[25,64,128]{2,1,0:T(8,128)(2,1)S(1)} %collective-permute-done.17.rest_14_) | copy-start | bytes 1228804
  70.2 16.0 %collective-permute-start.11 = (bf16[25,64,128]{2,1,0:T(8,128)(2,1)S(1)}, bf16[25,64,128]{2,1,0:T(8,128)(2,1)S(1)}, u32[]{:S(2)}, u32[]{:S(2)}) collective-permute-start(bf16[25,64,128]{2,1,0:T(8,128)(2,1)S(1)} %collective-permute-done.10.rest_6_), channel_id=1, source_target_pairs={{4,8},{8,12},{12,16},{16,20},{20,24},{24,28},{5,9},{9,13},{13,17},... | collective-permute-start | bytes 1228808 | tf_op jit(solution)/shard_map/ppermute | solution.py:175
  72.2 21.3 %copy-start.14 = (bf16[25,64,128]{2,1,0:T(8,128)(2,1)}, bf16[25,64,128]{2,1,0:T(8,128)(2,1)S(1)}, u32[]{:S(2)}) copy-start(bf16[25,64,128]{2,1,0:T(8,128)(2,1)S(1)} %collective-permute-done.16.rest_13_) | copy-start | bytes 1228804
  72.2 14.1 %collective-permute-start.20 = (bf16[25,64,128]{2,1,0:T(8,128)(2,1)S(1)}, bf16[25,64,128]{2,1,0:T(8,128)(2,1)S(1)}, u32[]{:S(2)}, u32[]{:S(2)}) collective-permute-start(bf16[25,64,128]{2,1,0:T(8,128)(2,1)S(1)} %collective-permute-done.17.rest_14_), channel_id=1, source_target_pairs={{4,0},{8,4},{12,8},{16,12},{20,16},{24,20},{5,1},{9,5},{13,9},{17,... | collective-permute-start | bytes 1228808 | tf_op jit(solution)/shard_map/ppermute | solution.py:175
  75.9 17.6 %copy-start.15 = (bf16[25,64,128]{2,1,0:T(8,128)(2,1)}, bf16[25,64,128]{2,1,0:T(8,128)(2,1)S(1)}, u32[]{:S(2)}) copy-start(bf16[25,64,128]{2,1,0:T(8,128)(2,1)S(1)} %collective-permute-done.6.rest_5_) | copy-start | bytes 1228804
  75.9 10.4 %collective-permute-start.19 = (bf16[25,64,128]{2,1,0:T(8,128)(2,1)S(1)}, bf16[25,64,128]{2,1,0:T(8,128)(2,1)S(1)}, u32[]{:S(2)}, u32[]{:S(2)}) collective-permute-start(bf16[25,64,128]{2,1,0:T(8,128)(2,1)S(1)} %collective-permute-done.16.rest_13_), channel_id=1, source_target_pairs={{4,0},{8,4},{12,8},{16,12},{20,16},{24,20},{5,1},{9,5},{13,9},{17,... | collective-permute-start | bytes 1228808 | tf_op jit(solution)/shard_map/ppermute | solution.py:175
  84.2 2.1 %copy-start.6 = (bf16[2,25,64,128]{3,2,1,0:T(8,128)(2,1)}, bf16[2,25,64,128]{3,2,1,0:T(8,128)(2,1)S(1)}, u32[]{:S(2)}) copy-start(bf16[2,25,64,128]{3,2,1,0:T(8,128)(2,1)S(1)} %collective-permute-done.8.rest_21_) | copy-start | bytes 2457604
  84.2 9.3 %collective-permute-start.7 = (bf16[25,64,128]{2,1,0:T(8,128)(2,1)S(1)}, bf16[25,64,128]{2,1,0:T(8,128)(2,1)S(1)}, u32[]{:S(2)}, u32[]{:S(2)}) collective-permute-start(bf16[25,64,128]{2,1,0:T(8,128)(2,1)S(1)} %collective-permute-done.6.rest_5_), channel_id=1, source_target_pairs={{4,8},{8,12},{12,16},{16,20},{20,24},{24,28},{5,9},{9,13},{13,17},... | collective-permute-start | bytes 1228808 | tf_op jit(solution)/shard_map/ppermute | solution.py:175
  86.2 7.2 %copy-start.7 = (bf16[2,25,64,128]{3,2,1,0:T(8,128)(2,1)}, bf16[2,25,64,128]{3,2,1,0:T(8,128)(2,1)S(1)}, u32[]{:S(2)}) copy-start(bf16[2,25,64,128]{3,2,1,0:T(8,128)(2,1)S(1)} %collective-permute-done.4.rest_20_) | copy-start | bytes 2457604
  86.3 7.3 %copy-start.16 = (bf16[25,64,128]{2,1,0:T(8,128)(2,1)}, bf16[25,64,128]{2,1,0:T(8,128)(2,1)S(1)}, u32[]{:S(2)}) copy-start(bf16[25,64,128]{2,1,0:T(8,128)(2,1)S(1)} %collective-permute-done.11.rest_2_) | copy-start | bytes 1228804
  86.3 7.2 %copy-start.17 = (bf16[25,64,128]{2,1,0:T(8,128)(2,1)}, bf16[25,64,128]{2,1,0:T(8,128)(2,1)S(1)}, u32[]{:S(2)}) copy-start(bf16[25,64,128]{2,1,0:T(8,128)(2,1)S(1)} %collective-permute-done.20.rest_18_) | copy-start | bytes 1228804
  86.3 7.2 %copy-start.18 = (bf16[25,64,128]{2,1,0:T(8,128)(2,1)}, bf16[25,64,128]{2,1,0:T(8,128)(2,1)S(1)}, u32[]{:S(2)}) copy-start(bf16[25,64,128]{2,1,0:T(8,128)(2,1)S(1)} %collective-permute-done.19.rest_17_) | copy-start | bytes 1228804
  93.4 0.8 copy-start.19
  155.2 16.3 %collective-permute-start.22 = (f32[8,2,64,128]{3,2,1,0:T(8,128)S(1)}, f32[8,2,64,128]{3,2,1,0:T(8,128)S(1)}, u32[]{:S(2)}, u32[]{:S(2)}) collective-permute-start(f32[8,2,64,128]{3,2,1,0:T(8,128)S(1)} %get-tuple-element.31), channel_id=1, source_target_pairs={{0,1},{1,2},{2,3},{3,0},{4,5},{5,6},{6,7},{7,4},{8,9},{9,10},{10,1... | collective-permute-start | bytes 1572872 | tf_op jit(solution)/shard_map/ppermute | solution.py:256
  159.3 20.4 %collective-permute-start.23 = (f32[8,2,64,128]{3,2,1,0:T(8,128)S(1)}, f32[8,2,64,128]{3,2,1,0:T(8,128)S(1)}, u32[]{:S(2)}, u32[]{:S(2)}) collective-permute-start(f32[8,2,64,128]{3,2,1,0:T(8,128)S(1)} %get-tuple-element.33), channel_id=1, source_target_pairs={{0,2},{1,3},{2,0},{3,1},{4,6},{5,7},{6,4},{7,5},{8,10},{9,11},{10,... | collective-permute-start | bytes 1572872 | tf_op jit(solution)/shard_map/ppermute | solution.py:256
  159.8 19.9 %collective-permute-start.24 = (f32[8,2,64,128]{3,2,1,0:T(8,128)S(1)}, f32[8,2,64,128]{3,2,1,0:T(8,128)S(1)}, u32[]{:S(2)}, u32[]{:S(2)}) collective-permute-start(f32[8,2,64,128]{3,2,1,0:T(8,128)S(1)} %get-tuple-element.32), channel_id=1, source_target_pairs={{0,3},{1,0},{2,1},{3,2},{4,7},{5,4},{6,5},{7,6},{8,11},{9,8},{10,9... | collective-permute-start | bytes 1572872 | tf_op jit(solution)/shard_map/ppermute | solution.py:256

commit v10 on v7

--- a/solution.py
+++ b/solution.py
@@ -20,11 +20,14 @@
 def coarse_kernel(
     pair_ref, half_ref, target_ref, live_ref, own_pos_ref, fix_ref, values_ref, *rest
 ):
-    out_ref, acc_ref, window, sems = rest[-4:]
+    window, sems = rest[-2:]
     n_pieces = sems.shape[0]
     groups = n_pieces // 5
     pieces = rest[:n_pieces]
-    fixed = rest[n_pieces:-4]
+    n_fixed = groups - 1
+    fixed = rest[n_pieces : n_pieces + n_fixed]
+    out_ref = rest[n_pieces + n_fixed]
+    accs = rest[n_pieces + n_fixed + 1 : -2]
     step = pl.program_id(0)
     rows_here, slots, bs, _ = values_ref.shape
     piece_rows = pieces[0].shape[0]
@@ -54,7 +57,8 @@
                         ).start()
 
             copies.append(cp)
-        acc_ref[...] = jnp.zeros_like(acc_ref)
+        for acc_ref in accs:
+            acc_ref[...] = jnp.zeros_like(acc_ref)
         for cp in copies:
             cp.wait()
 
@@ -80,7 +84,7 @@
             )
         for s in range(slots):
             t = target_ref[row * slots + s]
-            acc_ref[t] = acc_ref[t] + results[s]
+            accs[s][t] = accs[s][t] + results[s]
         return carry
 
     lax.fori_loop(0, rows_here, row_body, 0, unroll=2)
@@ -88,8 +92,8 @@
     @pl.when(step == pl.num_programs(0) - 1)
     def _():
         def pack(m, carry):
-            first = acc_ref[2 * m]
-            second = acc_ref[2 * m + 1]
+            first = sum(acc_ref[2 * m] for acc_ref in accs)
+            second = sum(acc_ref[2 * m + 1] for acc_ref in accs)
             first = first + pltpu.roll(first, bs, 1)
             second = second + pltpu.roll(second, bs, 1)
             out_ref[m] = jnp.where(lane_half == 0, first, second)
@@ -114,8 +118,8 @@
             ]
             + [pl.BlockSpec(memory_space=pl.ANY)] * (len(pieces) + len(fixed)),
             out_specs=pl.BlockSpec((n_targets // 2, bs, lanes), lambda i, *_: (0, 0, 0)),
-            scratch_shapes=[
-                pltpu.VMEM((n_targets, bs, lanes), jnp.float32),
+            scratch_shapes=[pltpu.VMEM((n_targets, bs, lanes), jnp.float32)] * slots
+            + [
                 pltpu.VMEM((len(pieces) * piece_rows, bs, lanes), jnp.bfloat16),
                 pltpu.SemaphoreType.DMA((len(pieces),)),
             ],

time: 173 us -> 174 us (level)
  no operation moved by 1% of the time
where the time goes in v10:
time: 174 us; the launch traced here: 173 us
  starting transfers between devices  56.8 us (33%)
  Pallas kernels  43.9 us (25%)
  waiting for transfers between devices  34.9 us (20%)
  local copies, waits for them, and re-layouts  29.3 us (17%)
  other arithmetic  6.72 us (4%)
    pallas_call x1, Pallas kernels, coarse_partial(): pl.pallas_call(coarse_kernel, out_shape=jax.ShapeDtypeStruct((n_targets /...  43.9 us
    ppermute x16, starting transfers between devices, ring(): return lax.ppermute(piece, 'blk', route)  38.6 us
    ppermute x3, waiting for transfers between devices, local(): lax.ppermute(outgoing, 'grp', [(i, (i + k) % group_size) for i in range(g...  19.8 us
    unnamed x45, local copies, waits for them, and re-layouts  17.7 us
    ppermute x3, starting transfers between devices, local(): fixed.append(lax.ppermute(fix_src, ('blk', 'grp'), route))  9.14 us
    ppermute x3, waiting for transfers between devices, local(): fixed.append(lax.ppermute(fix_src, ('blk', 'grp'), route))  8.03 us
    ppermute x16, waiting for transfers between devices, ring(): return lax.ppermute(piece, 'blk', route)  7.14 us
    ppermute x3, starting transfers between devices, local(): lax.ppermute(outgoing, 'grp', [(i, (i + k) % group_size) for i in range(g...  4.66 us
  transfers between devices with their start and end apart: 25, of which 5 were waited for; matrix products, arithmetic and copies ran while one was open for 13% of the time, Pallas kernels for 0%

profile of v10, /device:TPU:26, one launch (start us, length us, event | category | flops | bytes accessed | tf_op | source)
XLA Modules:
  0.0 172.5 jit_solution(632928433823067192)
XLA Ops:
  0.0 0.7 convert_bitcast_fusion
  0.7 2.0 %copy.17 = bf16[24,2,64,64]{3,1,2,0:T(2,128)(2,1)S(1)} copy(bf16[24,2,64,64]{3,2,1,0:T(8,128)(2,1)} %bitcast.144) | data formatting | bytes 786432 | tf_op jit(solution)/shard_map/reshape | solution.py:146
  2.6 0.3 reshape.739
  3.1 1.7 %collective-permute-start.2 = (bf16[25,64,128]{2,1,0:T(8,128)(2,1)S(1)}, bf16[25,64,128]{2,1,0:T(8,128)(2,1)S(1)}, u32[]{:S(2)}, u32[]{:S(2)}) collective-permute-start(bf16[25,64,128]{2,1,0:T(8,128)(2,1)S(1)} %fusion.3.rest_8_), channel_id=1, source_target_pairs={{4,0},{8,4},{12,8},{16,12},{20,16},{24,20},{28,24},{0,28},{5,1},{9... | collective-permute-start | bytes 1228808 | tf_op jit(solution)/shard_map/ppermute | solution.py:172
  4.8 0.5 collective-permute-start.13
  5.4 1.5 collective-permute-start.9
  6.9 2.4 %collective-permute-start.5 = (bf16[25,64,128]{2,1,0:T(8,128)(2,1)S(1)}, bf16[25,64,128]{2,1,0:T(8,128)(2,1)}, u32[]{:S(2)}, u32[]{:S(2)}) collective-permute-start(bf16[25,64,128]{2,1,0:T(8,128)(2,1)S(1)} %fusion.3.rest_8_), channel_id=1, source_target_pairs={{0,1},{1,2},{2,3},{3,0},{4,5},{5,6},{6,7},{7,4},{8,9},{9,10},{10,1... | collective-permute-start | bytes 1228808 | tf_op jit(solution)/shard_map/ppermute | solution.py:160
  9.3 0.1 copy.9
  9.4 0.1 rem.301
  9.6 0.1 rem.276
  9.7 0.1 copy.10
  9.8 0.1 div.78
  9.9 0.1 div.73
  10.0 0.2 copy.8
  10.2 0.1 ne.313
  10.3 0.1 ne.303
  10.5 0.1 compare_convert_fusion
  10.6 0.7 reshape.807.live_ref
  11.3 17.0 %copy.15.values_ref = bf16[192,4,64,64]{3,2,1,0:T(8,128)(2,1)} copy(bf16[192,4,64,64]{0,3,2,1:T(8,128)(2,1)} %param.9) | data formatting | bytes 12582912 | tf_op args[0]
  28.3 0.6 stack.59.fix_ref
  28.9 0.6 fusion.32.own_pos_ref
  29.5 0.1 fusion.16
  29.7 1.7 collective-permute-start.3
  31.4 2.3 %collective-permute-start.14 = (bf16[25,64,128]{2,1,0:T(8,128)(2,1)}, bf16[25,64,128]{2,1,0:T(8,128)(2,1)S(1)}, u32[]{:S(2)}, u32[]{:S(2)}) collective-permute-start(bf16[25,64,128]{2,1,0:T(8,128)(2,1)} %collective-permute-done.13.rest_11_), channel_id=1, source_target_pairs={{0,4},{4,8},{8,12},{12,16},{16,20},{20,24},{24,28},{1,5},{5,9},{9,... | collective-permute-start | bytes 1228808 | tf_op jit(solution)/shard_map/ppermute | solution.py:172
  33.7 0.7 slice_bitcast_fusion.8
  34.4 3.2 %collective-permute-start.18 = (bf16[25,64,128]{2,1,0:T(8,128)(2,1)}, bf16[25,64,128]{2,1,0:T(8,128)(2,1)S(1)}, u32[]{:S(2)}, u32[]{:S(2)}) collective-permute-start(bf16[25,64,128]{2,1,0:T(8,128)(2,1)} %collective-permute-done.13.rest_11_), channel_id=1, source_target_pairs={{4,0},{8,4},{12,8},{16,12},{20,16},{24,20},{28,24},{5,1},{9,5},{13... | collective-permute-start | bytes 1228808 | tf_op jit(solution)/shard_map/ppermute | solution.py:172
  37.7 4.9 %collective-permute-start.10 = (bf16[25,64,128]{2,1,0:T(8,128)(2,1)}, bf16[25,64,128]{2,1,0:T(8,128)(2,1)S(1)}, u32[]{:S(2)}, u32[]{:S(2)}) collective-permute-start(bf16[25,64,128]{2,1,0:T(8,128)(2,1)} %collective-permute-done.9.rest_10_), channel_id=1, source_target_pairs={{0,4},{4,8},{8,12},{12,16},{16,20},{20,24},{24,28},{1,5},{5,9},{9,... | collective-permute-start | bytes 1228808 | tf_op jit(solution)/shard_map/ppermute | solution.py:172
  42.7 0.1 pad_maximum_fusion.1
  42.8 1.9 %collective-permute-start.12 = (bf16[2,25,64,128]{3,2,1,0:T(8,128)(2,1)S(1)}, bf16[2,25,64,128]{3,2,1,0:T(8,128)(2,1)S(1)}, u32[]{:S(2)}, u32[]{:S(2)}) collective-permute-start(bf16[2,25,64,128]{3,2,1,0:T(8,128)(2,1)S(1)} %pad_maximum_fusion.1), channel_id=1, source_target_pairs={{0,3},{1,0},{2,1},{3,2},{4,7},{5,4},{6,5},{7,6},{24,27},{25,24},{2... | collective-permute-start | bytes 2457608 | tf_op jit(solution)/shard_map/ppermute | solution.py:191
  44.7 0.7 slice_bitcast_fusion.9
  45.4 0.7 slice_bitcast_fusion.10
  46.1 2.5 %collective-permute-start.8 = (bf16[2,25,64,128]{3,2,1,0:T(8,128)(2,1)S(1)}, bf16[2,25,64,128]{3,2,1,0:T(8,128)(2,1)S(1)}, u32[]{:S(2)}, u32[]{:S(2)}) collective-permute-start(bf16[2,25,64,128]{3,2,1,0:T(8,128)(2,1)S(1)} %pad_maximum_fusion.1), channel_id=1, source_target_pairs={{0,2},{1,3},{2,0},{3,1},{4,6},{5,7},{6,4},{7,5},{24,26},{25,27},{2... | collective-permute-start | bytes 2457608 | tf_op jit(solution)/shard_map/ppermute | solution.py:191
  48.6 4.3 %collective-permute-start.15 = (bf16[25,64,128]{2,1,0:T(8,128)(2,1)S(1)}, bf16[25,64,128]{2,1,0:T(8,128)(2,1)S(1)}, u32[]{:S(2)}, u32[]{:S(2)}) collective-permute-start(bf16[25,64,128]{2,1,0:T(8,128)(2,1)S(1)} %collective-permute-done.14.rest_7_), channel_id=1, source_target_pairs={{4,8},{8,12},{12,16},{16,20},{20,24},{24,28},{5,9},{9,13},{13,17},... | collective-permute-start | bytes 1228808 | tf_op jit(solution)/shard_map/ppermute | solution.py:172
  52.9 1.3 collective-permute-start.21
  54.2 4.8 %collective-permute-start.4 = (bf16[2,25,64,128]{3,2,1,0:T(8,128)(2,1)S(1)}, bf16[2,25,64,128]{3,2,1,0:T(8,128)(2,1)S(1)}, u32[]{:S(2)}, u32[]{:S(2)}) collective-permute-start(bf16[2,25,64,128]{3,2,1,0:T(8,128)(2,1)S(1)} %pad_maximum_fusion.1), channel_id=1, source_target_pairs={{0,1},{1,2},{2,3},{3,0},{4,5},{5,6},{6,7},{7,4},{24,25},{25,26},{2... | collective-permute-start | bytes 2457608 | tf_op jit(solution)/shard_map/ppermute | solution.py:191
  59.0 1.9 %collective-permute-start.17 = (bf16[25,64,128]{2,1,0:T(8,128)(2,1)}, bf16[25,64,128]{2,1,0:T(8,128)(2,1)S(1)}, u32[]{:S(2)}, u32[]{:S(2)}) collective-permute-start(bf16[25,64,128]{2,1,0:T(8,128)(2,1)} %collective-permute-done.9.rest_10_), channel_id=1, source_target_pairs={{4,0},{8,4},{12,8},{16,12},{20,16},{24,20},{28,24},{5,1},{9,5},{13... | collective-permute-start | bytes 1228808 | tf_op jit(solution)/shard_map/ppermute | solution.py:172
  61.0 2.4 %collective-permute-start.16 = (bf16[25,64,128]{2,1,0:T(8,128)(2,1)}, bf16[25,64,128]{2,1,0:T(8,128)(2,1)S(1)}, u32[]{:S(2)}, u32[]{:S(2)}) collective-permute-start(bf16[25,64,128]{2,1,0:T(8,128)(2,1)} %collective-permute-done.5.rest_9_), channel_id=1, source_target_pairs={{4,0},{8,4},{12,8},{16,12},{20,16},{24,20},{28,24},{5,1},{9,5},{13... | collective-permute-start | bytes 1228808 | tf_op jit(solution)/shard_map/ppermute | solution.py:172
  63.4 1.7 collective-permute-done.12.rest_22_
  65.1 5.1 %collective-permute-start.6 = (bf16[25,64,128]{2,1,0:T(8,128)(2,1)}, bf16[25,64,128]{2,1,0:T(8,128)(2,1)S(1)}, u32[]{:S(2)}, u32[]{:S(2)}) collective-permute-start(bf16[25,64,128]{2,1,0:T(8,128)(2,1)} %collective-permute-done.5.rest_9_), channel_id=1, source_target_pairs={{0,4},{4,8},{8,12},{12,16},{16,20},{20,24},{24,28},{1,5},{5,9},{9,... | collective-permute-start | bytes 1228808 | tf_op jit(solution)/shard_map/ppermute | solution.py:172
  70.2 1.9 %collective-permute-start.11 = (bf16[25,64,128]{2,1,0:T(8,128)(2,1)S(1)}, bf16[25,64,128]{2,1,0:T(8,128)(2,1)S(1)}, u32[]{:S(2)}, u32[]{:S(2)}) collective-permute-start(bf16[25,64,128]{2,1,0:T(8,128)(2,1)S(1)} %collective-permute-done.10.rest_6_), channel_id=1, source_target_pairs={{4,8},{8,12},{12,16},{16,20},{20,24},{24,28},{5,9},{9,13},{13,17},... | collective-permute-start | bytes 1228808 | tf_op jit(solution)/shard_map/ppermute | solution.py:172
  72.2 3.7 %collective-permute-start.20 = (bf16[25,64,128]{2,1,0:T(8,128)(2,1)S(1)}, bf16[25,64,128]{2,1,0:T(8,128)(2,1)S(1)}, u32[]{:S(2)}, u32[]{:S(2)}) collective-permute-start(bf16[25,64,128]{2,1,0:T(8,128)(2,1)S(1)} %collective-permute-done.17.rest_14_), channel_id=1, source_target_pairs={{4,0},{8,4},{12,8},{16,12},{20,16},{24,20},{5,1},{9,5},{13,9},{17,... | collective-permute-start | bytes 1228808 | tf_op jit(solution)/shard_map/ppermute | solution.py:172
  75.9 1.9 %collective-permute-start.19 = (bf16[25,64,128]{2,1,0:T(8,128)(2,1)S(1)}, bf16[25,64,128]{2,1,0:T(8,128)(2,1)S(1)}, u32[]{:S(2)}, u32[]{:S(2)}) collective-permute-start(bf16[25,64,128]{2,1,0:T(8,128)(2,1)S(1)} %collective-permute-done.16.rest_13_), channel_id=1, source_target_pairs={{4,0},{8,4},{12,8},{16,12},{20,16},{24,20},{5,1},{9,5},{13,9},{17,... | collective-permute-start | bytes 1228808 | tf_op jit(solution)/shard_map/ppermute | solution.py:172
  77.8 6.4 %collective-permute-done.8.rest_21_ = bf16[2,25,64,128]{3,2,1,0:T(8,128)(2,1)S(1)} collective-permute-done((bf16[2,25,64,128]{3,2,1,0:T(8,128)(2,1)S(1)}, bf16[2,25,64,128]{3,2,1,0:T(8,128)(2,1)S(1)}, u32[]{:S(2)}, u32[]{:S(2)}) %collective-permute-start.8) | collective-permute-done | bytes 819232 | tf_op jit(solution)/shard_map/ppermute | solution.py:191
  84.2 2.0 %collective-permute-start.7 = (bf16[25,64,128]{2,1,0:T(8,128)(2,1)S(1)}, bf16[25,64,128]{2,1,0:T(8,128)(2,1)S(1)}, u32[]{:S(2)}, u32[]{:S(2)}) collective-permute-start(bf16[25,64,128]{2,1,0:T(8,128)(2,1)S(1)} %collective-permute-done.6.rest_5_), channel_id=1, source_target_pairs={{4,8},{8,12},{12,16},{16,20},{20,24},{24,28},{5,9},{9,13},{13,17},... | collective-permute-start | bytes 1228808 | tf_op jit(solution)/shard_map/ppermute | solution.py:172
  86.3 7.1 %collective-permute-done.7.rest_1_ = bf16[25,64,128]{2,1,0:T(8,128)(2,1)S(1)} collective-permute-done((bf16[25,64,128]{2,1,0:T(8,128)(2,1)S(1)}, bf16[25,64,128]{2,1,0:T(8,128)(2,1)S(1)}, u32[]{:S(2)}, u32[]{:S(2)}) %collective-permute-start.7) | collective-permute-done | bytes 409632 | tf_op jit(solution)/shard_map/ppermute | solution.py:172
  93.5 0.7 copy-done.19
  94.2 0.1 stack.54
  94.3 0.1 reshape.806
  94.4 3.2 %gather_fusion = s32[768]{0:T(1024)S(1)} fusion(s32[960]{0:T(1024)S(1)} %reshape.806, s32[1024]{0:T(1024)S(1)} %pad_clamp_fusion.1), kind=kCustom, calls=%fused_computation | custom fusion | bytes 9216 | tf_op jit(solution)/shard_map/jit(_take)/gather | solution.py:226
  97.6 1.2 gather_fusion.1
  98.8 0.1 broadcast_in_dim.32
  98.9 0.1 reshape.740
  99.0 0.6 multiply_add_fusion
  99.7 0.6 fusion.11.pair_ref
  100.3 43.9 %shard_map.55 = f32[64,64,128]{2,1,0:T(8,128)} custom-call(s32[768]{0:T(1024)} %fusion.11.pair_ref, s32[768]{0:T(1024)} %get-tuple-element.45.half_ref, s32[768]{0:T(1024)} %get-tuple-element.29.target_ref, s32[768]{0:T(1024)} %reshape.807.live_ref, s32[192]{0:T(256)} %fusion.32.own_pos_ref, s32[5]{0:T(128)} %stack.59.fix_ref, ...), custom_call_target="tpu_custom_call" | custom-call | tf_op jit(solution)/shard_map/pallas_call | solution.py:110
  144.1 1.5 select_bitcast_fusion.2
  145.6 4.0 %collective-permute-start.22 = (f32[8,2,64,128]{3,2,1,0:T(8,128)S(1)}, f32[8,2,64,128]{3,2,1,0:T(8,128)S(1)}, u32[]{:S(2)}, u32[]{:S(2)}) collective-permute-start(f32[8,2,64,128]{3,2,1,0:T(8,128)S(1)} %get-tuple-element.31), channel_id=1, source_target_pairs={{0,1},{1,2},{2,3},{3,0},{4,5},{5,6},{6,7},{7,4},{8,9},{9,10},{10,1... | collective-permute-start | bytes 1572872 | tf_op jit(solution)/shard_map/ppermute | solution.py:253
  149.7 0.5 collective-permute-start.23
  150.2 0.1 collective-permute-start.24
  150.3 11.7 %collective-permute-done.22 = f32[8,2,64,128]{3,2,1,0:T(8,128)S(1)} collective-permute-done((f32[8,2,64,128]{3,2,1,0:T(8,128)S(1)}, f32[8,2,64,128]{3,2,1,0:T(8,128)S(1)}, u32[]{:S(2)}, u32[]{:S(2)}) %collective-permute-start.22) | collective-permute-done | bytes 524320 | tf_op jit(solution)/shard_map/ppermute | solution.py:253
  162.0 8.1 %collective-permute-done.23 = f32[8,2,64,128]{3,2,1,0:T(8,128)S(1)} collective-permute-done((f32[8,2,64,128]{3,2,1,0:T(8,128)S(1)}, f32[8,2,64,128]{3,2,1,0:T(8,128)S(1)}, u32[]{:S(2)}, u32[]{:S(2)}) %collective-permute-start.23) | collective-permute-done | bytes 524320 | tf_op jit(solution)/shard_map/ppermute | solution.py:253
  170.1 1.2 fusion.2
  171.3 0.2 fusion.46
  171.5 1.1 pad_maximum_fusion
  (86 shorter events, 0.5 us)
Async XLA Ops:
  0.0 9.3 %copy-start.20 = (s32[192,4]{0,1:T(4,128)S(1)}, s32[192,4]{0,1:T(4,128)}, u32[]{:S(2)}) copy-start(s32[192,4]{0,1:T(4,128)} %param.10) | copy-start | bytes 9220
  0.7 9.9 %copy-start.21 = (s32[192]{0:T(256)S(1)}, s32[192]{0:T(256)}, u32[]{:S(2)}) copy-start(s32[192]{0:T(256)} %param.11) | copy-start | bytes 2308
  3.0 25.3 %copy-start.4 = (bf16[25,64,128]{2,1,0:T(8,128)(2,1)}, bf16[25,64,128]{2,1,0:T(8,128)(2,1)S(1)}, u32[]{:S(2)}) copy-start(bf16[25,64,128]{2,1,0:T(8,128)(2,1)S(1)} %fusion.3.rest_8_) | copy-start | bytes 1228804
  3.0 26.5 %collective-permute-start = (bf16[25,64,128]{2,1,0:T(8,128)(2,1)S(1)}, bf16[25,64,128]{2,1,0:T(8,128)(2,1)S(1)}, u32[]{:S(2)}, u32[]{:S(2)}) collective-permute-start(bf16[25,64,128]{2,1,0:T(8,128)(2,1)S(1)} %fusion.3.rest_8_), channel_id=1, source_target_pairs={{28,0},{0,4},{4,8},{8,12},{12,16},{16,20},{20,24},{24,28},{29,1},{... | collective-permute-start | bytes 1228808 | tf_op jit(solution)/shard_map/ppermute | solution.py:172
  3.1 26.5 %collective-permute-start.2 = (bf16[25,64,128]{2,1,0:T(8,128)(2,1)S(1)}, bf16[25,64,128]{2,1,0:T(8,128)(2,1)S(1)}, u32[]{:S(2)}, u32[]{:S(2)}) collective-permute-start(bf16[25,64,128]{2,1,0:T(8,128)(2,1)S(1)} %fusion.3.rest_8_), channel_id=1, source_target_pairs={{4,0},{8,4},{12,8},{16,12},{20,16},{24,20},{28,24},{0,28},{5,1},{9... | collective-permute-start | bytes 1228808 | tf_op jit(solution)/shard_map/ppermute | solution.py:172
  4.8 26.6 %collective-permute-start.13 = (bf16[25,64,128]{2,1,0:T(8,128)(2,1)S(1)}, bf16[25,64,128]{2,1,0:T(8,128)(2,1)}, u32[]{:S(2)}, u32[]{:S(2)}) collective-permute-start(bf16[25,64,128]{2,1,0:T(8,128)(2,1)S(1)} %fusion.3.rest_8_), channel_id=1, source_target_pairs={{0,3},{1,0},{2,1},{3,2},{4,7},{5,4},{6,5},{7,6},{8,11},{9,8},{10,9... | collective-permute-start | bytes 1228808 | tf_op jit(solution)/shard_map/ppermute | solution.py:160
  5.4 29.1 %collective-permute-start.9 = (bf16[25,64,128]{2,1,0:T(8,128)(2,1)S(1)}, bf16[25,64,128]{2,1,0:T(8,128)(2,1)}, u32[]{:S(2)}, u32[]{:S(2)}) collective-permute-start(bf16[25,64,128]{2,1,0:T(8,128)(2,1)S(1)} %fusion.3.rest_8_), channel_id=1, source_target_pairs={{0,2},{1,3},{2,0},{3,1},{4,6},{5,7},{6,4},{7,5},{8,10},{9,11},{10,... | collective-permute-start | bytes 1228808 | tf_op jit(solution)/shard_map/ppermute | solution.py:160
  6.9 38.5 %collective-permute-start.5 = (bf16[25,64,128]{2,1,0:T(8,128)(2,1)S(1)}, bf16[25,64,128]{2,1,0:T(8,128)(2,1)}, u32[]{:S(2)}, u32[]{:S(2)}) collective-permute-start(bf16[25,64,128]{2,1,0:T(8,128)(2,1)S(1)} %fusion.3.rest_8_), channel_id=1, source_target_pairs={{0,1},{1,2},{2,3},{3,0},{4,5},{5,6},{6,7},{7,4},{8,9},{9,10},{10,1... | collective-permute-start | bytes 1228808 | tf_op jit(solution)/shard_map/ppermute | solution.py:160
  29.6 64.7 %copy-start = (bf16[25,64,128]{2,1,0:T(8,128)(2,1)}, bf16[25,64,128]{2,1,0:T(8,128)(2,1)S(1)}, u32[]{:S(2)}) copy-start(bf16[25,64,128]{2,1,0:T(8,128)(2,1)S(1)} %collective-permute-done.rest_4_) | copy-start | bytes 1228804
  29.6 8.1 %collective-permute-start.1 = (bf16[25,64,128]{2,1,0:T(8,128)(2,1)S(1)}, bf16[25,64,128]{2,1,0:T(8,128)(2,1)S(1)}, u32[]{:S(2)}, u32[]{:S(2)}) collective-permute-start(bf16[25,64,128]{2,1,0:T(8,128)(2,1)S(1)} %collective-permute-done.rest_4_), channel_id=1, source_target_pairs={{28,0},{0,4},{4,8},{8,12},{12,16},{16,20},{20,24},{24,28},{29,1},{... | collective-permute-start | bytes 1228808 | tf_op jit(solution)/shard_map/ppermute | solution.py:172
  29.7 64.7 %copy-start.1 = (bf16[25,64,128]{2,1,0:T(8,128)(2,1)}, bf16[25,64,128]{2,1,0:T(8,128)(2,1)S(1)}, u32[]{:S(2)}) copy-start(bf16[25,64,128]{2,1,0:T(8,128)(2,1)S(1)} %collective-permute-done.2.rest_12_) | copy-start | bytes 1228804
  29.7 13.0 %collective-permute-start.3 = (bf16[25,64,128]{2,1,0:T(8,128)(2,1)S(1)}, bf16[25,64,128]{2,1,0:T(8,128)(2,1)S(1)}, u32[]{:S(2)}, u32[]{:S(2)}) collective-permute-start(bf16[25,64,128]{2,1,0:T(8,128)(2,1)S(1)} %collective-permute-done.2.rest_12_), channel_id=1, source_target_pairs={{4,0},{8,4},{12,8},{16,12},{20,16},{24,20},{28,24},{0,28},{5,1},{9... | collective-permute-start | bytes 1228808 | tf_op jit(solution)/shard_map/ppermute | solution.py:172
  31.4 17.2 %collective-permute-start.14 = (bf16[25,64,128]{2,1,0:T(8,128)(2,1)}, bf16[25,64,128]{2,1,0:T(8,128)(2,1)S(1)}, u32[]{:S(2)}, u32[]{:S(2)}) collective-permute-start(bf16[25,64,128]{2,1,0:T(8,128)(2,1)} %collective-permute-done.13.rest_11_), channel_id=1, source_target_pairs={{0,4},{4,8},{8,12},{12,16},{16,20},{20,24},{24,28},{1,5},{5,9},{9,... | collective-permute-start | bytes 1228808 | tf_op jit(solution)/shard_map/ppermute | solution.py:172
  34.4 18.4 %collective-permute-start.18 = (bf16[25,64,128]{2,1,0:T(8,128)(2,1)}, bf16[25,64,128]{2,1,0:T(8,128)(2,1)S(1)}, u32[]{:S(2)}, u32[]{:S(2)}) collective-permute-start(bf16[25,64,128]{2,1,0:T(8,128)(2,1)} %collective-permute-done.13.rest_11_), channel_id=1, source_target_pairs={{4,0},{8,4},{12,8},{16,12},{20,16},{24,20},{28,24},{5,1},{9,5},{13... | collective-permute-start | bytes 1228808 | tf_op jit(solution)/shard_map/ppermute | solution.py:172
  37.7 59.9 %copy-start.2 = (bf16[25,64,128]{2,1,0:T(8,128)(2,1)}, bf16[25,64,128]{2,1,0:T(8,128)(2,1)S(1)}, u32[]{:S(2)}) copy-start(bf16[25,64,128]{2,1,0:T(8,128)(2,1)S(1)} %collective-permute-done.1.rest_0_) | copy-start | bytes 1228804
  37.7 16.5 %collective-permute-start.10 = (bf16[25,64,128]{2,1,0:T(8,128)(2,1)}, bf16[25,64,128]{2,1,0:T(8,128)(2,1)S(1)}, u32[]{:S(2)}, u32[]{:S(2)}) collective-permute-start(bf16[25,64,128]{2,1,0:T(8,128)(2,1)} %collective-permute-done.9.rest_10_), channel_id=1, source_target_pairs={{0,4},{4,8},{8,12},{12,16},{16,20},{20,24},{24,28},{1,5},{5,9},{9,... | collective-permute-start | bytes 1228808 | tf_op jit(solution)/shard_map/ppermute | solution.py:172
  42.7 54.9 %copy-start.3 = (bf16[25,64,128]{2,1,0:T(8,128)(2,1)}, bf16[25,64,128]{2,1,0:T(8,128)(2,1)S(1)}, u32[]{:S(2)}) copy-start(bf16[25,64,128]{2,1,0:T(8,128)(2,1)S(1)} %collective-permute-done.3.rest_16_) | copy-start | bytes 1228804
  42.8 22.3 %collective-permute-start.12 = (bf16[2,25,64,128]{3,2,1,0:T(8,128)(2,1)S(1)}, bf16[2,25,64,128]{3,2,1,0:T(8,128)(2,1)S(1)}, u32[]{:S(2)}, u32[]{:S(2)}) collective-permute-start(bf16[2,25,64,128]{3,2,1,0:T(8,128)(2,1)S(1)} %pad_maximum_fusion.1), channel_id=1, source_target_pairs={{0,3},{1,0},{2,1},{3,2},{4,7},{5,4},{6,5},{7,6},{24,27},{25,24},{2... | collective-permute-start | bytes 2457608 | tf_op jit(solution)/shard_map/ppermute | solution.py:191
  46.1 38.1 %collective-permute-start.8 = (bf16[2,25,64,128]{3,2,1,0:T(8,128)(2,1)S(1)}, bf16[2,25,64,128]{3,2,1,0:T(8,128)(2,1)S(1)}, u32[]{:S(2)}, u32[]{:S(2)}) collective-permute-start(bf16[2,25,64,128]{3,2,1,0:T(8,128)(2,1)S(1)} %pad_maximum_fusion.1), channel_id=1, source_target_pairs={{0,2},{1,3},{2,0},{3,1},{4,6},{5,7},{6,4},{7,5},{24,26},{25,27},{2... | collective-permute-start | bytes 2457608 | tf_op jit(solution)/shard_map/ppermute | solution.py:191
  48.6 51.7 %copy-start.8 = (bf16[25,64,128]{2,1,0:T(8,128)(2,1)}, bf16[25,64,128]{2,1,0:T(8,128)(2,1)S(1)}, u32[]{:S(2)}) copy-start(bf16[25,64,128]{2,1,0:T(8,128)(2,1)S(1)} %collective-permute-done.14.rest_7_) | copy-start | bytes 1228804
  48.6 10.4 %collective-permute-start.15 = (bf16[25,64,128]{2,1,0:T(8,128)(2,1)S(1)}, bf16[25,64,128]{2,1,0:T(8,128)(2,1)S(1)}, u32[]{:S(2)}, u32[]{:S(2)}) collective-permute-start(bf16[25,64,128]{2,1,0:T(8,128)(2,1)S(1)} %collective-permute-done.14.rest_7_), channel_id=1, source_target_pairs={{4,8},{8,12},{12,16},{16,20},{20,24},{24,28},{5,9},{9,13},{13,17},... | collective-permute-start | bytes 1228808 | tf_op jit(solution)/shard_map/ppermute | solution.py:172
  52.9 40.6 %copy-start.9 = (bf16[25,64,128]{2,1,0:T(8,128)(2,1)}, bf16[25,64,128]{2,1,0:T(8,128)(2,1)S(1)}, u32[]{:S(2)}) copy-start(bf16[25,64,128]{2,1,0:T(8,128)(2,1)S(1)} %collective-permute-done.18.rest_15_) | copy-start | bytes 1228804
  52.9 8.1 %collective-permute-start.21 = (bf16[25,64,128]{2,1,0:T(8,128)(2,1)S(1)}, bf16[25,64,128]{2,1,0:T(8,128)(2,1)S(1)}, u32[]{:S(2)}, u32[]{:S(2)}) collective-permute-start(bf16[25,64,128]{2,1,0:T(8,128)(2,1)S(1)} %collective-permute-done.18.rest_15_), channel_id=1, source_target_pairs={{4,0},{8,4},{12,8},{16,12},{20,16},{24,20},{5,1},{9,5},{13,9},{17,... | collective-permute-start | bytes 1228808 | tf_op jit(solution)/shard_map/ppermute | solution.py:172
  54.2 39.2 %copy-start.10 = (bf16[25,64,128]{2,1,0:T(8,128)(2,1)}, bf16[25,64,128]{2,1,0:T(8,128)(2,1)S(1)}, u32[]{:S(2)}) copy-start(bf16[25,64,128]{2,1,0:T(8,128)(2,1)S(1)} %collective-permute-done.10.rest_6_) | copy-start | bytes 1228804
  54.2 32.0 %collective-permute-start.4 = (bf16[2,25,64,128]{3,2,1,0:T(8,128)(2,1)S(1)}, bf16[2,25,64,128]{3,2,1,0:T(8,128)(2,1)S(1)}, u32[]{:S(2)}, u32[]{:S(2)}) collective-permute-start(bf16[2,25,64,128]{3,2,1,0:T(8,128)(2,1)S(1)} %pad_maximum_fusion.1), channel_id=1, source_target_pairs={{0,1},{1,2},{2,3},{3,0},{4,5},{5,6},{6,7},{7,4},{24,25},{25,26},{2... | collective-permute-start | bytes 2457608 | tf_op jit(solution)/shard_map/ppermute | solution.py:191
  59.0 41.2 %copy-start.11 = (bf16[25,64,128]{2,1,0:T(8,128)(2,1)}, bf16[25,64,128]{2,1,0:T(8,128)(2,1)S(1)}, u32[]{:S(2)}) copy-start(bf16[25,64,128]{2,1,0:T(8,128)(2,1)S(1)} %collective-permute-done.15.rest_3_) | copy-start | bytes 1228804
  59.0 11.2 %collective-permute-start.17 = (bf16[25,64,128]{2,1,0:T(8,128)(2,1)}, bf16[25,64,128]{2,1,0:T(8,128)(2,1)S(1)}, u32[]{:S(2)}, u32[]{:S(2)}) collective-permute-start(bf16[25,64,128]{2,1,0:T(8,128)(2,1)} %collective-permute-done.9.rest_10_), channel_id=1, source_target_pairs={{4,0},{8,4},{12,8},{16,12},{20,16},{24,20},{28,24},{5,1},{9,5},{13... | collective-permute-start | bytes 1228808 | tf_op jit(solution)/shard_map/ppermute | solution.py:172
  61.0 32.5 %copy-start.12 = (bf16[25,64,128]{2,1,0:T(8,128)(2,1)}, bf16[25,64,128]{2,1,0:T(8,128)(2,1)S(1)}, u32[]{:S(2)}) copy-start(bf16[25,64,128]{2,1,0:T(8,128)(2,1)S(1)} %collective-permute-done.21.rest_19_) | copy-start | bytes 1228804
  61.0 11.2 %collective-permute-start.16 = (bf16[25,64,128]{2,1,0:T(8,128)(2,1)}, bf16[25,64,128]{2,1,0:T(8,128)(2,1)S(1)}, u32[]{:S(2)}, u32[]{:S(2)}) collective-permute-start(bf16[25,64,128]{2,1,0:T(8,128)(2,1)} %collective-permute-done.5.rest_9_), channel_id=1, source_target_pairs={{4,0},{8,4},{12,8},{16,12},{20,16},{24,20},{28,24},{5,1},{9,5},{13... | collective-permute-start | bytes 1228808 | tf_op jit(solution)/shard_map/ppermute | solution.py:172
  65.1 32.5 %copy-start.5 = (bf16[2,25,64,128]{3,2,1,0:T(8,128)(2,1)}, bf16[2,25,64,128]{3,2,1,0:T(8,128)(2,1)S(1)}, u32[]{:S(2)}) copy-start(bf16[2,25,64,128]{3,2,1,0:T(8,128)(2,1)S(1)} %collective-permute-done.12.rest_22_) | copy-start | bytes 2457604
  65.1 10.8 %collective-permute-start.6 = (bf16[25,64,128]{2,1,0:T(8,128)(2,1)}, bf16[25,64,128]{2,1,0:T(8,128)(2,1)S(1)}, u32[]{:S(2)}, u32[]{:S(2)}) collective-permute-start(bf16[25,64,128]{2,1,0:T(8,128)(2,1)} %collective-permute-done.5.rest_9_), channel_id=1, source_target_pairs={{0,4},{4,8},{8,12},{12,16},{16,20},{20,24},{24,28},{1,5},{5,9},{9,... | collective-permute-start | bytes 1228808 | tf_op jit(solution)/shard_map/ppermute | solution.py:172
  70.2 23.3 %copy-start.13 = (bf16[25,64,128]{2,1,0:T(8,128)(2,1)}, bf16[25,64,128]{2,1,0:T(8,128)(2,1)S(1)}, u32[]{:S(2)}) copy-start(bf16[25,64,128]{2,1,0:T(8,128)(2,1)S(1)} %collective-permute-done.17.rest_14_) | copy-start | bytes 1228804
  70.2 16.0 %collective-permute-start.11 = (bf16[25,64,128]{2,1,0:T(8,128)(2,1)S(1)}, bf16[25,64,128]{2,1,0:T(8,128)(2,1)S(1)}, u32[]{:S(2)}, u32[]{:S(2)}) collective-permute-start(bf16[25,64,128]{2,1,0:T(8,128)(2,1)S(1)} %collective-permute-done.10.rest_6_), channel_id=1, source_target_pairs={{4,8},{8,12},{12,16},{16,20},{20,24},{24,28},{5,9},{9,13},{13,17},... | collective-permute-start | bytes 1228808 | tf_op jit(solution)/shard_map/ppermute | solution.py:172
  72.2 21.3 %copy-start.14 = (bf16[25,64,128]{2,1,0:T(8,128)(2,1)}, bf16[25,64,128]{2,1,0:T(8,128)(2,1)S(1)}, u32[]{:S(2)}) copy-start(bf16[25,64,128]{2,1,0:T(8,128)(2,1)S(1)} %collective-permute-done.16.rest_13_) | copy-start | bytes 1228804
  72.2 14.1 %collective-permute-start.20 = (bf16[25,64,128]{2,1,0:T(8,128)(2,1)S(1)}, bf16[25,64,128]{2,1,0:T(8,128)(2,1)S(1)}, u32[]{:S(2)}, u32[]{:S(2)}) collective-permute-start(bf16[25,64,128]{2,1,0:T(8,128)(2,1)S(1)} %collective-permute-done.17.rest_14_), channel_id=1, source_target_pairs={{4,0},{8,4},{12,8},{16,12},{20,16},{24,20},{5,1},{9,5},{13,9},{17,... | collective-permute-start | bytes 1228808 | tf_op jit(solution)/shard_map/ppermute | solution.py:172
  75.9 17.6 %copy-start.15 = (bf16[25,64,128]{2,1,0:T(8,128)(2,1)}, bf16[25,64,128]{2,1,0:T(8,128)(2,1)S(1)}, u32[]{:S(2)}) copy-start(bf16[25,64,128]{2,1,0:T(8,128)(2,1)S(1)} %collective-permute-done.6.rest_5_) | copy-start | bytes 1228804
  75.9 10.4 %collective-permute-start.19 = (bf16[25,64,128]{2,1,0:T(8,128)(2,1)S(1)}, bf16[25,64,128]{2,1,0:T(8,128)(2,1)S(1)}, u32[]{:S(2)}, u32[]{:S(2)}) collective-permute-start(bf16[25,64,128]{2,1,0:T(8,128)(2,1)S(1)} %collective-permute-done.16.rest_13_), channel_id=1, source_target_pairs={{4,0},{8,4},{12,8},{16,12},{20,16},{24,20},{5,1},{9,5},{13,9},{17,... | collective-permute-start | bytes 1228808 | tf_op jit(solution)/shard_map/ppermute | solution.py:172
  84.2 2.1 %copy-start.6 = (bf16[2,25,64,128]{3,2,1,0:T(8,128)(2,1)}, bf16[2,25,64,128]{3,2,1,0:T(8,128)(2,1)S(1)}, u32[]{:S(2)}) copy-start(bf16[2,25,64,128]{3,2,1,0:T(8,128)(2,1)S(1)} %collective-permute-done.8.rest_21_) | copy-start | bytes 2457604
  84.2 9.3 %collective-permute-start.7 = (bf16[25,64,128]{2,1,0:T(8,128)(2,1)S(1)}, bf16[25,64,128]{2,1,0:T(8,128)(2,1)S(1)}, u32[]{:S(2)}, u32[]{:S(2)}) collective-permute-start(bf16[25,64,128]{2,1,0:T(8,128)(2,1)S(1)} %collective-permute-done.6.rest_5_), channel_id=1, source_target_pairs={{4,8},{8,12},{12,16},{16,20},{20,24},{24,28},{5,9},{9,13},{13,17},... | collective-permute-start | bytes 1228808 | tf_op jit(solution)/shard_map/ppermute | solution.py:172
  86.2 7.2 %copy-start.7 = (bf16[2,25,64,128]{3,2,1,0:T(8,128)(2,1)}, bf16[2,25,64,128]{3,2,1,0:T(8,128)(2,1)S(1)}, u32[]{:S(2)}) copy-start(bf16[2,25,64,128]{3,2,1,0:T(8,128)(2,1)S(1)} %collective-permute-done.4.rest_20_) | copy-start | bytes 2457604
  86.3 7.3 %copy-start.16 = (bf16[25,64,128]{2,1,0:T(8,128)(2,1)}, bf16[25,64,128]{2,1,0:T(8,128)(2,1)S(1)}, u32[]{:S(2)}) copy-start(bf16[25,64,128]{2,1,0:T(8,128)(2,1)S(1)} %collective-permute-done.11.rest_2_) | copy-start | bytes 1228804
  86.3 7.2 %copy-start.17 = (bf16[25,64,128]{2,1,0:T(8,128)(2,1)}, bf16[25,64,128]{2,1,0:T(8,128)(2,1)S(1)}, u32[]{:S(2)}) copy-start(bf16[25,64,128]{2,1,0:T(8,128)(2,1)S(1)} %collective-permute-done.20.rest_18_) | copy-start | bytes 1228804
  86.3 7.2 %copy-start.18 = (bf16[25,64,128]{2,1,0:T(8,128)(2,1)}, bf16[25,64,128]{2,1,0:T(8,128)(2,1)S(1)}, u32[]{:S(2)}) copy-start(bf16[25,64,128]{2,1,0:T(8,128)(2,1)S(1)} %collective-permute-done.19.rest_17_) | copy-start | bytes 1228804
  93.4 0.8 copy-start.19
  145.6 16.3 %collective-permute-start.22 = (f32[8,2,64,128]{3,2,1,0:T(8,128)S(1)}, f32[8,2,64,128]{3,2,1,0:T(8,128)S(1)}, u32[]{:S(2)}, u32[]{:S(2)}) collective-permute-start(f32[8,2,64,128]{3,2,1,0:T(8,128)S(1)} %get-tuple-element.31), channel_id=1, source_target_pairs={{0,1},{1,2},{2,3},{3,0},{4,5},{5,6},{6,7},{7,4},{8,9},{9,10},{10,1... | collective-permute-start | bytes 1572872 | tf_op jit(solution)/shard_map/ppermute | solution.py:253
  149.7 20.4 %collective-permute-start.23 = (f32[8,2,64,128]{3,2,1,0:T(8,128)S(1)}, f32[8,2,64,128]{3,2,1,0:T(8,128)S(1)}, u32[]{:S(2)}, u32[]{:S(2)}) collective-permute-start(f32[8,2,64,128]{3,2,1,0:T(8,128)S(1)} %get-tuple-element.33), channel_id=1, source_target_pairs={{0,2},{1,3},{2,0},{3,1},{4,6},{5,7},{6,4},{7,5},{8,10},{9,11},{10,... | collective-permute-start | bytes 1572872 | tf_op jit(solution)/shard_map/ppermute | solution.py:253
  150.2 19.9 %collective-permute-start.24 = (f32[8,2,64,128]{3,2,1,0:T(8,128)S(1)}, f32[8,2,64,128]{3,2,1,0:T(8,128)S(1)}, u32[]{:S(2)}, u32[]{:S(2)}) collective-permute-start(f32[8,2,64,128]{3,2,1,0:T(8,128)S(1)} %get-tuple-element.32), channel_id=1, source_target_pairs={{0,3},{1,0},{2,1},{3,2},{4,7},{5,4},{6,5},{7,6},{8,11},{9,8},{10,9... | collective-permute-start | bytes 1572872 | tf_op jit(solution)/shard_map/ppermute | solution.py:253

commit v11 on v7

--- a/solution.py
+++ b/solution.py
@@ -246,9 +246,12 @@
     total = jnp.take(summed, group_me, axis=0)
     for k in range(1, group_size):
         outgoing = jnp.take(summed, jnp.mod(group_me + k, group_size), axis=0)
-        total = total + lax.ppermute(
-            outgoing, "grp", [(i, (i + k) % group_size) for i in range(group_size)]
+        incoming = lax.ppermute(
+            outgoing.astype(jnp.bfloat16),
+            "grp",
+            [(i, (i + k) % group_size) for i in range(group_size)],
         )
+        total = total + incoming.astype(jnp.float32)
     total = total.reshape(share, CB // 2, block_size, 2, block_size)
     return total.transpose(0, 1, 3, 2, 4).reshape(share, CB, block_size, block_size)
 

time: 173 us -> 162 us (0.936)
  waiting for transfers between devices: 34.9 us -> 23.7 us
    ppermute x3, waiting for transfers between devices: 19.8 us -> 8.54 us  [local(): lax.ppermute(outgoing.astype(jnp.bfloat16), 'grp', [(i, (i + k) % group_s...]
  transfers between devices with their start and end apart: 25 -> 25, of which waited for: 5 -> 5; matrix products, arithmetic and copies ran while one was open for 13% -> 14% of each run, Pallas kernels for 0% -> 0%
where the time goes in v11:
time: 162 us; the launch traced here: 161 us
  starting transfers between devices  56.8 us (35%)
  Pallas kernels  43.6 us (27%)
  local copies, waits for them, and re-layouts  29.3 us (18%)
  waiting for transfers between devices  23.7 us (15%)
  other arithmetic  6.78 us (4%)
    pallas_call x1, Pallas kernels, coarse_partial(): pl.pallas_call(coarse_kernel, out_shape=jax.ShapeDtypeStruct((n_targets /...  43.6 us
    ppermute x16, starting transfers between devices, ring(): return lax.ppermute(piece, 'blk', route)  38.6 us
    unnamed x45, local copies, waits for them, and re-layouts  17.7 us
    ppermute x3, starting transfers between devices, local(): fixed.append(lax.ppermute(fix_src, ('blk', 'grp'), route))  9.14 us
    ppermute x3, waiting for transfers between devices, local(): lax.ppermute(outgoing.astype(jnp.bfloat16), 'grp', [(i, (i + k) % group_s...  8.54 us
    ppermute x3, waiting for transfers between devices, local(): fixed.append(lax.ppermute(fix_src, ('blk', 'grp'), route))  8.03 us
    ppermute x16, waiting for transfers between devices, ring(): return lax.ppermute(piece, 'blk', route)  7.14 us
    ppermute x3, starting transfers between devices, local(): lax.ppermute(outgoing.astype(jnp.bfloat16), 'grp', [(i, (i + k) % group_s...  4.66 us
  transfers between devices with their start and end apart: 25, of which 5 were waited for; matrix products, arithmetic and copies ran while one was open for 14% of the time, Pallas kernels for 0%

profile of v11, /device:TPU:26, one launch (start us, length us, event | category | flops | bytes accessed | tf_op | source)
XLA Modules:
  0.0 161.1 jit_solution(2914044304141675930)
XLA Ops:
  0.0 0.7 convert_bitcast_fusion
  0.7 2.0 %copy.17 = bf16[24,2,64,64]{3,1,2,0:T(2,128)(2,1)S(1)} copy(bf16[24,2,64,64]{3,2,1,0:T(8,128)(2,1)} %bitcast.144) | data formatting | bytes 786432 | tf_op jit(solution)/shard_map/reshape | solution.py:142
  2.6 0.3 reshape.739
  3.1 1.7 %collective-permute-start.2 = (bf16[25,64,128]{2,1,0:T(8,128)(2,1)S(1)}, bf16[25,64,128]{2,1,0:T(8,128)(2,1)S(1)}, u32[]{:S(2)}, u32[]{:S(2)}) collective-permute-start(bf16[25,64,128]{2,1,0:T(8,128)(2,1)S(1)} %fusion.3.rest_8_), channel_id=1, source_target_pairs={{4,0},{8,4},{12,8},{16,12},{20,16},{24,20},{28,24},{0,28},{5,1},{9... | collective-permute-start | bytes 1228808 | tf_op jit(solution)/shard_map/ppermute | solution.py:168
  4.8 0.5 collective-permute-start.13
  5.4 1.5 collective-permute-start.9
  6.9 2.4 %collective-permute-start.5 = (bf16[25,64,128]{2,1,0:T(8,128)(2,1)S(1)}, bf16[25,64,128]{2,1,0:T(8,128)(2,1)}, u32[]{:S(2)}, u32[]{:S(2)}) collective-permute-start(bf16[25,64,128]{2,1,0:T(8,128)(2,1)S(1)} %fusion.3.rest_8_), channel_id=1, source_target_pairs={{0,1},{1,2},{2,3},{3,0},{4,5},{5,6},{6,7},{7,4},{8,9},{9,10},{10,1... | collective-permute-start | bytes 1228808 | tf_op jit(solution)/shard_map/ppermute | solution.py:156
  9.3 0.1 copy.9
  9.4 0.1 rem.301
  9.6 0.1 rem.276
  9.7 0.1 copy.10
  9.8 0.1 div.78
  9.9 0.1 div.73
  10.0 0.2 copy.8
  10.2 0.1 ne.313
  10.3 0.1 ne.303
  10.5 0.1 compare_convert_fusion
  10.6 0.7 reshape.807.live_ref
  11.3 17.0 %copy.15.values_ref = bf16[192,4,64,64]{3,2,1,0:T(8,128)(2,1)} copy(bf16[192,4,64,64]{0,3,2,1:T(8,128)(2,1)} %param.9) | data formatting | bytes 12582912 | tf_op args[0]
  28.3 0.6 stack.59.fix_ref
  28.9 0.6 fusion.32.own_pos_ref
  29.5 0.1 fusion.16
  29.7 1.7 %collective-permute-start.3 = (bf16[25,64,128]{2,1,0:T(8,128)(2,1)S(1)}, bf16[25,64,128]{2,1,0:T(8,128)(2,1)S(1)}, u32[]{:S(2)}, u32[]{:S(2)}) collective-permute-start(bf16[25,64,128]{2,1,0:T(8,128)(2,1)S(1)} %collective-permute-done.2.rest_12_), channel_id=1, source_target_pairs={{4,0},{8,4},{12,8},{16,12},{20,16},{24,20},{28,24},{0,28},{5,1},{9... | collective-permute-start | bytes 1228808 | tf_op jit(solution)/shard_map/ppermute | solution.py:168
  31.4 2.3 %collective-permute-start.14 = (bf16[25,64,128]{2,1,0:T(8,128)(2,1)}, bf16[25,64,128]{2,1,0:T(8,128)(2,1)S(1)}, u32[]{:S(2)}, u32[]{:S(2)}) collective-permute-start(bf16[25,64,128]{2,1,0:T(8,128)(2,1)} %collective-permute-done.13.rest_11_), channel_id=1, source_target_pairs={{0,4},{4,8},{8,12},{12,16},{16,20},{20,24},{24,28},{1,5},{5,9},{9,... | collective-permute-start | bytes 1228808 | tf_op jit(solution)/shard_map/ppermute | solution.py:168
  33.7 0.7 slice_bitcast_fusion.8
  34.4 3.2 %collective-permute-start.18 = (bf16[25,64,128]{2,1,0:T(8,128)(2,1)}, bf16[25,64,128]{2,1,0:T(8,128)(2,1)S(1)}, u32[]{:S(2)}, u32[]{:S(2)}) collective-permute-start(bf16[25,64,128]{2,1,0:T(8,128)(2,1)} %collective-permute-done.13.rest_11_), channel_id=1, source_target_pairs={{4,0},{8,4},{12,8},{16,12},{20,16},{24,20},{28,24},{5,1},{9,5},{13... | collective-permute-start | bytes 1228808 | tf_op jit(solution)/shard_map/ppermute | solution.py:168
  37.7 4.9 %collective-permute-start.10 = (bf16[25,64,128]{2,1,0:T(8,128)(2,1)}, bf16[25,64,128]{2,1,0:T(8,128)(2,1)S(1)}, u32[]{:S(2)}, u32[]{:S(2)}) collective-permute-start(bf16[25,64,128]{2,1,0:T(8,128)(2,1)} %collective-permute-done.9.rest_10_), channel_id=1, source_target_pairs={{0,4},{4,8},{8,12},{12,16},{16,20},{20,24},{24,28},{1,5},{5,9},{9,... | collective-permute-start | bytes 1228808 | tf_op jit(solution)/shard_map/ppermute | solution.py:168
  42.7 0.1 pad_maximum_fusion.1
  42.8 1.9 %collective-permute-start.12 = (bf16[2,25,64,128]{3,2,1,0:T(8,128)(2,1)S(1)}, bf16[2,25,64,128]{3,2,1,0:T(8,128)(2,1)S(1)}, u32[]{:S(2)}, u32[]{:S(2)}) collective-permute-start(bf16[2,25,64,128]{3,2,1,0:T(8,128)(2,1)S(1)} %pad_maximum_fusion.1), channel_id=1, source_target_pairs={{0,3},{1,0},{2,1},{3,2},{4,7},{5,4},{6,5},{7,6},{24,27},{25,24},{2... | collective-permute-start | bytes 2457608 | tf_op jit(solution)/shard_map/ppermute | solution.py:187
  44.7 0.7 slice_bitcast_fusion.9
  45.4 0.7 slice_bitcast_fusion.10
  46.1 2.5 %collective-permute-start.8 = (bf16[2,25,64,128]{3,2,1,0:T(8,128)(2,1)S(1)}, bf16[2,25,64,128]{3,2,1,0:T(8,128)(2,1)S(1)}, u32[]{:S(2)}, u32[]{:S(2)}) collective-permute-start(bf16[2,25,64,128]{3,2,1,0:T(8,128)(2,1)S(1)} %pad_maximum_fusion.1), channel_id=1, source_target_pairs={{0,2},{1,3},{2,0},{3,1},{4,6},{5,7},{6,4},{7,5},{24,26},{25,27},{2... | collective-permute-start | bytes 2457608 | tf_op jit(solution)/shard_map/ppermute | solution.py:187
  48.6 4.3 %collective-permute-start.15 = (bf16[25,64,128]{2,1,0:T(8,128)(2,1)S(1)}, bf16[25,64,128]{2,1,0:T(8,128)(2,1)S(1)}, u32[]{:S(2)}, u32[]{:S(2)}) collective-permute-start(bf16[25,64,128]{2,1,0:T(8,128)(2,1)S(1)} %collective-permute-done.14.rest_7_), channel_id=1, source_target_pairs={{4,8},{8,12},{12,16},{16,20},{20,24},{24,28},{5,9},{9,13},{13,17},... | collective-permute-start | bytes 1228808 | tf_op jit(solution)/shard_map/ppermute | solution.py:168
  52.9 1.3 collective-permute-start.21
  54.2 4.8 %collective-permute-start.4 = (bf16[2,25,64,128]{3,2,1,0:T(8,128)(2,1)S(1)}, bf16[2,25,64,128]{3,2,1,0:T(8,128)(2,1)S(1)}, u32[]{:S(2)}, u32[]{:S(2)}) collective-permute-start(bf16[2,25,64,128]{3,2,1,0:T(8,128)(2,1)S(1)} %pad_maximum_fusion.1), channel_id=1, source_target_pairs={{0,1},{1,2},{2,3},{3,0},{4,5},{5,6},{6,7},{7,4},{24,25},{25,26},{2... | collective-permute-start | bytes 2457608 | tf_op jit(solution)/shard_map/ppermute | solution.py:187
  59.0 1.9 %collective-permute-start.17 = (bf16[25,64,128]{2,1,0:T(8,128)(2,1)}, bf16[25,64,128]{2,1,0:T(8,128)(2,1)S(1)}, u32[]{:S(2)}, u32[]{:S(2)}) collective-permute-start(bf16[25,64,128]{2,1,0:T(8,128)(2,1)} %collective-permute-done.9.rest_10_), channel_id=1, source_target_pairs={{4,0},{8,4},{12,8},{16,12},{20,16},{24,20},{28,24},{5,1},{9,5},{13... | collective-permute-start | bytes 1228808 | tf_op jit(solution)/shard_map/ppermute | solution.py:168
  61.0 2.4 %collective-permute-start.16 = (bf16[25,64,128]{2,1,0:T(8,128)(2,1)}, bf16[25,64,128]{2,1,0:T(8,128)(2,1)S(1)}, u32[]{:S(2)}, u32[]{:S(2)}) collective-permute-start(bf16[25,64,128]{2,1,0:T(8,128)(2,1)} %collective-permute-done.5.rest_9_), channel_id=1, source_target_pairs={{4,0},{8,4},{12,8},{16,12},{20,16},{24,20},{28,24},{5,1},{9,5},{13... | collective-permute-start | bytes 1228808 | tf_op jit(solution)/shard_map/ppermute | solution.py:168
  63.4 1.7 %collective-permute-done.12.rest_22_ = bf16[2,25,64,128]{3,2,1,0:T(8,128)(2,1)S(1)} collective-permute-done((bf16[2,25,64,128]{3,2,1,0:T(8,128)(2,1)S(1)}, bf16[2,25,64,128]{3,2,1,0:T(8,128)(2,1)S(1)}, u32[]{:S(2)}, u32[]{:S(2)}) %collective-permute-start.12) | collective-permute-done | bytes 819232 | tf_op jit(solution)/shard_map/ppermute | solution.py:187
  65.1 5.1 %collective-permute-start.6 = (bf16[25,64,128]{2,1,0:T(8,128)(2,1)}, bf16[25,64,128]{2,1,0:T(8,128)(2,1)S(1)}, u32[]{:S(2)}, u32[]{:S(2)}) collective-permute-start(bf16[25,64,128]{2,1,0:T(8,128)(2,1)} %collective-permute-done.5.rest_9_), channel_id=1, source_target_pairs={{0,4},{4,8},{8,12},{12,16},{16,20},{20,24},{24,28},{1,5},{5,9},{9,... | collective-permute-start | bytes 1228808 | tf_op jit(solution)/shard_map/ppermute | solution.py:168
  70.2 1.9 %collective-permute-start.11 = (bf16[25,64,128]{2,1,0:T(8,128)(2,1)S(1)}, bf16[25,64,128]{2,1,0:T(8,128)(2,1)S(1)}, u32[]{:S(2)}, u32[]{:S(2)}) collective-permute-start(bf16[25,64,128]{2,1,0:T(8,128)(2,1)S(1)} %collective-permute-done.10.rest_6_), channel_id=1, source_target_pairs={{4,8},{8,12},{12,16},{16,20},{20,24},{24,28},{5,9},{9,13},{13,17},... | collective-permute-start | bytes 1228808 | tf_op jit(solution)/shard_map/ppermute | solution.py:168
  72.2 3.7 %collective-permute-start.20 = (bf16[25,64,128]{2,1,0:T(8,128)(2,1)S(1)}, bf16[25,64,128]{2,1,0:T(8,128)(2,1)S(1)}, u32[]{:S(2)}, u32[]{:S(2)}) collective-permute-start(bf16[25,64,128]{2,1,0:T(8,128)(2,1)S(1)} %collective-permute-done.17.rest_14_), channel_id=1, source_target_pairs={{4,0},{8,4},{12,8},{16,12},{20,16},{24,20},{5,1},{9,5},{13,9},{17,... | collective-permute-start | bytes 1228808 | tf_op jit(solution)/shard_map/ppermute | solution.py:168
  75.9 1.9 %collective-permute-start.19 = (bf16[25,64,128]{2,1,0:T(8,128)(2,1)S(1)}, bf16[25,64,128]{2,1,0:T(8,128)(2,1)S(1)}, u32[]{:S(2)}, u32[]{:S(2)}) collective-permute-start(bf16[25,64,128]{2,1,0:T(8,128)(2,1)S(1)} %collective-permute-done.16.rest_13_), channel_id=1, source_target_pairs={{4,0},{8,4},{12,8},{16,12},{20,16},{24,20},{5,1},{9,5},{13,9},{17,... | collective-permute-start | bytes 1228808 | tf_op jit(solution)/shard_map/ppermute | solution.py:168
  77.8 6.4 %collective-permute-done.8.rest_21_ = bf16[2,25,64,128]{3,2,1,0:T(8,128)(2,1)S(1)} collective-permute-done((bf16[2,25,64,128]{3,2,1,0:T(8,128)(2,1)S(1)}, bf16[2,25,64,128]{3,2,1,0:T(8,128)(2,1)S(1)}, u32[]{:S(2)}, u32[]{:S(2)}) %collective-permute-start.8) | collective-permute-done | bytes 819232 | tf_op jit(solution)/shard_map/ppermute | solution.py:187
  84.2 2.0 %collective-permute-start.7 = (bf16[25,64,128]{2,1,0:T(8,128)(2,1)S(1)}, bf16[25,64,128]{2,1,0:T(8,128)(2,1)S(1)}, u32[]{:S(2)}, u32[]{:S(2)}) collective-permute-start(bf16[25,64,128]{2,1,0:T(8,128)(2,1)S(1)} %collective-permute-done.6.rest_5_), channel_id=1, source_target_pairs={{4,8},{8,12},{12,16},{16,20},{20,24},{24,28},{5,9},{9,13},{13,17},... | collective-permute-start | bytes 1228808 | tf_op jit(solution)/shard_map/ppermute | solution.py:168
  86.3 7.1 %collective-permute-done.7.rest_1_ = bf16[25,64,128]{2,1,0:T(8,128)(2,1)S(1)} collective-permute-done((bf16[25,64,128]{2,1,0:T(8,128)(2,1)S(1)}, bf16[25,64,128]{2,1,0:T(8,128)(2,1)S(1)}, u32[]{:S(2)}, u32[]{:S(2)}) %collective-permute-start.7) | collective-permute-done | bytes 409632 | tf_op jit(solution)/shard_map/ppermute | solution.py:168
  93.5 0.7 copy-done.19
  94.2 0.1 stack.54
  94.3 0.1 reshape.806
  94.4 3.2 %gather_fusion = s32[768]{0:T(1024)S(1)} fusion(s32[960]{0:T(1024)S(1)} %reshape.806, s32[1024]{0:T(1024)S(1)} %pad_clamp_fusion.1), kind=kCustom, calls=%fused_computation | custom fusion | bytes 9216 | tf_op jit(solution)/shard_map/jit(_take)/gather | solution.py:222
  97.6 1.2 gather_fusion.1
  98.8 0.1 broadcast_in_dim.32
  98.9 0.1 reshape.740
  99.0 0.6 multiply_add_fusion
  99.7 0.6 fusion.11.pair_ref
  100.3 43.6 %shard_map.55 = f32[64,64,128]{2,1,0:T(8,128)} custom-call(s32[768]{0:T(1024)} %fusion.11.pair_ref, s32[768]{0:T(1024)} %get-tuple-element.45.half_ref, s32[768]{0:T(1024)} %get-tuple-element.29.target_ref, s32[768]{0:T(1024)} %reshape.807.live_ref, s32[192]{0:T(256)} %fusion.32.own_pos_ref, s32[5]{0:T(128)} %stack.59.fix_ref, ...), custom_call_target="tpu_custom_call" | custom-call | tf_op jit(solution)/shard_map/pallas_call | solution.py:106
  143.9 1.6 bitcast_convert_fusion.2
  145.5 4.0 %collective-permute-start.22 = (bf16[8,2,64,128]{3,2,1,0:T(8,128)(2,1)S(1)}, bf16[8,2,64,128]{3,2,1,0:T(8,128)(2,1)S(1)}, u32[]{:S(2)}, u32[]{:S(2)}) collective-permute-start(bf16[8,2,64,128]{3,2,1,0:T(8,128)(2,1)S(1)} %get-tuple-element.31), channel_id=1, source_target_pairs={{0,1},{1,2},{2,3},{3,0},{4,5},{5,6},{6,7},{7,4},{8,9},{9,10},{10,1... | collective-permute-start | bytes 786440 | tf_op jit(solution)/shard_map/ppermute | solution.py:249
  149.5 0.5 collective-permute-start.23
  150.0 0.1 collective-permute-start.24
  150.1 4.1 %collective-permute-done.22 = bf16[8,2,64,128]{3,2,1,0:T(8,128)(2,1)S(1)} collective-permute-done((bf16[8,2,64,128]{3,2,1,0:T(8,128)(2,1)S(1)}, bf16[8,2,64,128]{3,2,1,0:T(8,128)(2,1)S(1)}, u32[]{:S(2)}, u32[]{:S(2)}) %collective-permute-start.22) | collective-permute-done | bytes 262176 | tf_op jit(solution)/shard_map/ppermute | solution.py:249
  154.3 4.4 %collective-permute-done.23 = bf16[8,2,64,128]{3,2,1,0:T(8,128)(2,1)S(1)} collective-permute-done((bf16[8,2,64,128]{3,2,1,0:T(8,128)(2,1)S(1)}, bf16[8,2,64,128]{3,2,1,0:T(8,128)(2,1)S(1)}, u32[]{:S(2)}, u32[]{:S(2)}) %collective-permute-start.23) | collective-permute-done | bytes 262176 | tf_op jit(solution)/shard_map/ppermute | solution.py:249
  158.7 1.2 fusion.2
  159.9 0.2 fusion.46
  160.1 1.1 pad_maximum_fusion
  (86 shorter events, 0.5 us)
Async XLA Ops:
  0.0 9.3 %copy-start.20 = (s32[192,4]{0,1:T(4,128)S(1)}, s32[192,4]{0,1:T(4,128)}, u32[]{:S(2)}) copy-start(s32[192,4]{0,1:T(4,128)} %param.10) | copy-start | bytes 9220
  0.7 9.9 %copy-start.21 = (s32[192]{0:T(256)S(1)}, s32[192]{0:T(256)}, u32[]{:S(2)}) copy-start(s32[192]{0:T(256)} %param.11) | copy-start | bytes 2308
  3.0 25.3 %copy-start.4 = (bf16[25,64,128]{2,1,0:T(8,128)(2,1)}, bf16[25,64,128]{2,1,0:T(8,128)(2,1)S(1)}, u32[]{:S(2)}) copy-start(bf16[25,64,128]{2,1,0:T(8,128)(2,1)S(1)} %fusion.3.rest_8_) | copy-start | bytes 1228804
  3.0 26.5 %collective-permute-start = (bf16[25,64,128]{2,1,0:T(8,128)(2,1)S(1)}, bf16[25,64,128]{2,1,0:T(8,128)(2,1)S(1)}, u32[]{:S(2)}, u32[]{:S(2)}) collective-permute-start(bf16[25,64,128]{2,1,0:T(8,128)(2,1)S(1)} %fusion.3.rest_8_), channel_id=1, source_target_pairs={{28,0},{0,4},{4,8},{8,12},{12,16},{16,20},{20,24},{24,28},{29,1},{... | collective-permute-start | bytes 1228808 | tf_op jit(solution)/shard_map/ppermute | solution.py:168
  3.1 26.5 %collective-permute-start.2 = (bf16[25,64,128]{2,1,0:T(8,128)(2,1)S(1)}, bf16[25,64,128]{2,1,0:T(8,128)(2,1)S(1)}, u32[]{:S(2)}, u32[]{:S(2)}) collective-permute-start(bf16[25,64,128]{2,1,0:T(8,128)(2,1)S(1)} %fusion.3.rest_8_), channel_id=1, source_target_pairs={{4,0},{8,4},{12,8},{16,12},{20,16},{24,20},{28,24},{0,28},{5,1},{9... | collective-permute-start | bytes 1228808 | tf_op jit(solution)/shard_map/ppermute | solution.py:168
  4.8 26.6 %collective-permute-start.13 = (bf16[25,64,128]{2,1,0:T(8,128)(2,1)S(1)}, bf16[25,64,128]{2,1,0:T(8,128)(2,1)}, u32[]{:S(2)}, u32[]{:S(2)}) collective-permute-start(bf16[25,64,128]{2,1,0:T(8,128)(2,1)S(1)} %fusion.3.rest_8_), channel_id=1, source_target_pairs={{0,3},{1,0},{2,1},{3,2},{4,7},{5,4},{6,5},{7,6},{8,11},{9,8},{10,9... | collective-permute-start | bytes 1228808 | tf_op jit(solution)/shard_map/ppermute | solution.py:156
  5.4 29.1 %collective-permute-start.9 = (bf16[25,64,128]{2,1,0:T(8,128)(2,1)S(1)}, bf16[25,64,128]{2,1,0:T(8,128)(2,1)}, u32[]{:S(2)}, u32[]{:S(2)}) collective-permute-start(bf16[25,64,128]{2,1,0:T(8,128)(2,1)S(1)} %fusion.3.rest_8_), channel_id=1, source_target_pairs={{0,2},{1,3},{2,0},{3,1},{4,6},{5,7},{6,4},{7,5},{8,10},{9,11},{10,... | collective-permute-start | bytes 1228808 | tf_op jit(solution)/shard_map/ppermute | solution.py:156
  6.9 38.5 %collective-permute-start.5 = (bf16[25,64,128]{2,1,0:T(8,128)(2,1)S(1)}, bf16[25,64,128]{2,1,0:T(8,128)(2,1)}, u32[]{:S(2)}, u32[]{:S(2)}) collective-permute-start(bf16[25,64,128]{2,1,0:T(8,128)(2,1)S(1)} %fusion.3.rest_8_), channel_id=1, source_target_pairs={{0,1},{1,2},{2,3},{3,0},{4,5},{5,6},{6,7},{7,4},{8,9},{9,10},{10,1... | collective-permute-start | bytes 1228808 | tf_op jit(solution)/shard_map/ppermute | solution.py:156
  29.6 64.7 %copy-start = (bf16[25,64,128]{2,1,0:T(8,128)(2,1)}, bf16[25,64,128]{2,1,0:T(8,128)(2,1)S(1)}, u32[]{:S(2)}) copy-start(bf16[25,64,128]{2,1,0:T(8,128)(2,1)S(1)} %collective-permute-done.rest_4_) | copy-start | bytes 1228804
  29.6 8.1 %collective-permute-start.1 = (bf16[25,64,128]{2,1,0:T(8,128)(2,1)S(1)}, bf16[25,64,128]{2,1,0:T(8,128)(2,1)S(1)}, u32[]{:S(2)}, u32[]{:S(2)}) collective-permute-start(bf16[25,64,128]{2,1,0:T(8,128)(2,1)S(1)} %collective-permute-done.rest_4_), channel_id=1, source_target_pairs={{28,0},{0,4},{4,8},{8,12},{12,16},{16,20},{20,24},{24,28},{29,1},{... | collective-permute-start | bytes 1228808 | tf_op jit(solution)/shard_map/ppermute | solution.py:168
  29.7 64.7 %copy-start.1 = (bf16[25,64,128]{2,1,0:T(8,128)(2,1)}, bf16[25,64,128]{2,1,0:T(8,128)(2,1)S(1)}, u32[]{:S(2)}) copy-start(bf16[25,64,128]{2,1,0:T(8,128)(2,1)S(1)} %collective-permute-done.2.rest_12_) | copy-start | bytes 1228804
  29.7 13.0 %collective-permute-start.3 = (bf16[25,64,128]{2,1,0:T(8,128)(2,1)S(1)}, bf16[25,64,128]{2,1,0:T(8,128)(2,1)S(1)}, u32[]{:S(2)}, u32[]{:S(2)}) collective-permute-start(bf16[25,64,128]{2,1,0:T(8,128)(2,1)S(1)} %collective-permute-done.2.rest_12_), channel_id=1, source_target_pairs={{4,0},{8,4},{12,8},{16,12},{20,16},{24,20},{28,24},{0,28},{5,1},{9... | collective-permute-start | bytes 1228808 | tf_op jit(solution)/shard_map/ppermute | solution.py:168
  31.4 17.2 %collective-permute-start.14 = (bf16[25,64,128]{2,1,0:T(8,128)(2,1)}, bf16[25,64,128]{2,1,0:T(8,128)(2,1)S(1)}, u32[]{:S(2)}, u32[]{:S(2)}) collective-permute-start(bf16[25,64,128]{2,1,0:T(8,128)(2,1)} %collective-permute-done.13.rest_11_), channel_id=1, source_target_pairs={{0,4},{4,8},{8,12},{12,16},{16,20},{20,24},{24,28},{1,5},{5,9},{9,... | collective-permute-start | bytes 1228808 | tf_op jit(solution)/shard_map/ppermute | solution.py:168
  34.4 18.4 %collective-permute-start.18 = (bf16[25,64,128]{2,1,0:T(8,128)(2,1)}, bf16[25,64,128]{2,1,0:T(8,128)(2,1)S(1)}, u32[]{:S(2)}, u32[]{:S(2)}) collective-permute-start(bf16[25,64,128]{2,1,0:T(8,128)(2,1)} %collective-permute-done.13.rest_11_), channel_id=1, source_target_pairs={{4,0},{8,4},{12,8},{16,12},{20,16},{24,20},{28,24},{5,1},{9,5},{13... | collective-permute-start | bytes 1228808 | tf_op jit(solution)/shard_map/ppermute | solution.py:168
  37.7 59.9 %copy-start.2 = (bf16[25,64,128]{2,1,0:T(8,128)(2,1)}, bf16[25,64,128]{2,1,0:T(8,128)(2,1)S(1)}, u32[]{:S(2)}) copy-start(bf16[25,64,128]{2,1,0:T(8,128)(2,1)S(1)} %collective-permute-done.1.rest_0_) | copy-start | bytes 1228804
  37.7 16.5 %collective-permute-start.10 = (bf16[25,64,128]{2,1,0:T(8,128)(2,1)}, bf16[25,64,128]{2,1,0:T(8,128)(2,1)S(1)}, u32[]{:S(2)}, u32[]{:S(2)}) collective-permute-start(bf16[25,64,128]{2,1,0:T(8,128)(2,1)} %collective-permute-done.9.rest_10_), channel_id=1, source_target_pairs={{0,4},{4,8},{8,12},{12,16},{16,20},{20,24},{24,28},{1,5},{5,9},{9,... | collective-permute-start | bytes 1228808 | tf_op jit(solution)/shard_map/ppermute | solution.py:168
  42.7 54.9 %copy-start.3 = (bf16[25,64,128]{2,1,0:T(8,128)(2,1)}, bf16[25,64,128]{2,1,0:T(8,128)(2,1)S(1)}, u32[]{:S(2)}) copy-start(bf16[25,64,128]{2,1,0:T(8,128)(2,1)S(1)} %collective-permute-done.3.rest_16_) | copy-start | bytes 1228804
  42.8 22.3 %collective-permute-start.12 = (bf16[2,25,64,128]{3,2,1,0:T(8,128)(2,1)S(1)}, bf16[2,25,64,128]{3,2,1,0:T(8,128)(2,1)S(1)}, u32[]{:S(2)}, u32[]{:S(2)}) collective-permute-start(bf16[2,25,64,128]{3,2,1,0:T(8,128)(2,1)S(1)} %pad_maximum_fusion.1), channel_id=1, source_target_pairs={{0,3},{1,0},{2,1},{3,2},{4,7},{5,4},{6,5},{7,6},{24,27},{25,24},{2... | collective-permute-start | bytes 2457608 | tf_op jit(solution)/shard_map/ppermute | solution.py:187
  46.1 38.1 %collective-permute-start.8 = (bf16[2,25,64,128]{3,2,1,0:T(8,128)(2,1)S(1)}, bf16[2,25,64,128]{3,2,1,0:T(8,128)(2,1)S(1)}, u32[]{:S(2)}, u32[]{:S(2)}) collective-permute-start(bf16[2,25,64,128]{3,2,1,0:T(8,128)(2,1)S(1)} %pad_maximum_fusion.1), channel_id=1, source_target_pairs={{0,2},{1,3},{2,0},{3,1},{4,6},{5,7},{6,4},{7,5},{24,26},{25,27},{2... | collective-permute-start | bytes 2457608 | tf_op jit(solution)/shard_map/ppermute | solution.py:187
  48.6 51.7 %copy-start.8 = (bf16[25,64,128]{2,1,0:T(8,128)(2,1)}, bf16[25,64,128]{2,1,0:T(8,128)(2,1)S(1)}, u32[]{:S(2)}) copy-start(bf16[25,64,128]{2,1,0:T(8,128)(2,1)S(1)} %collective-permute-done.14.rest_7_) | copy-start | bytes 1228804
  48.6 10.4 %collective-permute-start.15 = (bf16[25,64,128]{2,1,0:T(8,128)(2,1)S(1)}, bf16[25,64,128]{2,1,0:T(8,128)(2,1)S(1)}, u32[]{:S(2)}, u32[]{:S(2)}) collective-permute-start(bf16[25,64,128]{2,1,0:T(8,128)(2,1)S(1)} %collective-permute-done.14.rest_7_), channel_id=1, source_target_pairs={{4,8},{8,12},{12,16},{16,20},{20,24},{24,28},{5,9},{9,13},{13,17},... | collective-permute-start | bytes 1228808 | tf_op jit(solution)/shard_map/ppermute | solution.py:168
  52.9 40.6 %copy-start.9 = (bf16[25,64,128]{2,1,0:T(8,128)(2,1)}, bf16[25,64,128]{2,1,0:T(8,128)(2,1)S(1)}, u32[]{:S(2)}) copy-start(bf16[25,64,128]{2,1,0:T(8,128)(2,1)S(1)} %collective-permute-done.18.rest_15_) | copy-start | bytes 1228804
  52.9 8.1 %collective-permute-start.21 = (bf16[25,64,128]{2,1,0:T(8,128)(2,1)S(1)}, bf16[25,64,128]{2,1,0:T(8,128)(2,1)S(1)}, u32[]{:S(2)}, u32[]{:S(2)}) collective-permute-start(bf16[25,64,128]{2,1,0:T(8,128)(2,1)S(1)} %collective-permute-done.18.rest_15_), channel_id=1, source_target_pairs={{4,0},{8,4},{12,8},{16,12},{20,16},{24,20},{5,1},{9,5},{13,9},{17,... | collective-permute-start | bytes 1228808 | tf_op jit(solution)/shard_map/ppermute | solution.py:168
  54.2 39.2 %copy-start.10 = (bf16[25,64,128]{2,1,0:T(8,128)(2,1)}, bf16[25,64,128]{2,1,0:T(8,128)(2,1)S(1)}, u32[]{:S(2)}) copy-start(bf16[25,64,128]{2,1,0:T(8,128)(2,1)S(1)} %collective-permute-done.10.rest_6_) | copy-start | bytes 1228804
  54.2 32.0 %collective-permute-start.4 = (bf16[2,25,64,128]{3,2,1,0:T(8,128)(2,1)S(1)}, bf16[2,25,64,128]{3,2,1,0:T(8,128)(2,1)S(1)}, u32[]{:S(2)}, u32[]{:S(2)}) collective-permute-start(bf16[2,25,64,128]{3,2,1,0:T(8,128)(2,1)S(1)} %pad_maximum_fusion.1), channel_id=1, source_target_pairs={{0,1},{1,2},{2,3},{3,0},{4,5},{5,6},{6,7},{7,4},{24,25},{25,26},{2... | collective-permute-start | bytes 2457608 | tf_op jit(solution)/shard_map/ppermute | solution.py:187
  59.0 41.2 %copy-start.11 = (bf16[25,64,128]{2,1,0:T(8,128)(2,1)}, bf16[25,64,128]{2,1,0:T(8,128)(2,1)S(1)}, u32[]{:S(2)}) copy-start(bf16[25,64,128]{2,1,0:T(8,128)(2,1)S(1)} %collective-permute-done.15.rest_3_) | copy-start | bytes 1228804
  59.0 11.2 %collective-permute-start.17 = (bf16[25,64,128]{2,1,0:T(8,128)(2,1)}, bf16[25,64,128]{2,1,0:T(8,128)(2,1)S(1)}, u32[]{:S(2)}, u32[]{:S(2)}) collective-permute-start(bf16[25,64,128]{2,1,0:T(8,128)(2,1)} %collective-permute-done.9.rest_10_), channel_id=1, source_target_pairs={{4,0},{8,4},{12,8},{16,12},{20,16},{24,20},{28,24},{5,1},{9,5},{13... | collective-permute-start | bytes 1228808 | tf_op jit(solution)/shard_map/ppermute | solution.py:168
  61.0 32.5 %copy-start.12 = (bf16[25,64,128]{2,1,0:T(8,128)(2,1)}, bf16[25,64,128]{2,1,0:T(8,128)(2,1)S(1)}, u32[]{:S(2)}) copy-start(bf16[25,64,128]{2,1,0:T(8,128)(2,1)S(1)} %collective-permute-done.21.rest_19_) | copy-start | bytes 1228804
  61.0 11.2 %collective-permute-start.16 = (bf16[25,64,128]{2,1,0:T(8,128)(2,1)}, bf16[25,64,128]{2,1,0:T(8,128)(2,1)S(1)}, u32[]{:S(2)}, u32[]{:S(2)}) collective-permute-start(bf16[25,64,128]{2,1,0:T(8,128)(2,1)} %collective-permute-done.5.rest_9_), channel_id=1, source_target_pairs={{4,0},{8,4},{12,8},{16,12},{20,16},{24,20},{28,24},{5,1},{9,5},{13... | collective-permute-start | bytes 1228808 | tf_op jit(solution)/shard_map/ppermute | solution.py:168
  65.1 32.5 %copy-start.5 = (bf16[2,25,64,128]{3,2,1,0:T(8,128)(2,1)}, bf16[2,25,64,128]{3,2,1,0:T(8,128)(2,1)S(1)}, u32[]{:S(2)}) copy-start(bf16[2,25,64,128]{3,2,1,0:T(8,128)(2,1)S(1)} %collective-permute-done.12.rest_22_) | copy-start | bytes 2457604
  65.1 10.8 %collective-permute-start.6 = (bf16[25,64,128]{2,1,0:T(8,128)(2,1)}, bf16[25,64,128]{2,1,0:T(8,128)(2,1)S(1)}, u32[]{:S(2)}, u32[]{:S(2)}) collective-permute-start(bf16[25,64,128]{2,1,0:T(8,128)(2,1)} %collective-permute-done.5.rest_9_), channel_id=1, source_target_pairs={{0,4},{4,8},{8,12},{12,16},{16,20},{20,24},{24,28},{1,5},{5,9},{9,... | collective-permute-start | bytes 1228808 | tf_op jit(solution)/shard_map/ppermute | solution.py:168
  70.2 23.3 %copy-start.13 = (bf16[25,64,128]{2,1,0:T(8,128)(2,1)}, bf16[25,64,128]{2,1,0:T(8,128)(2,1)S(1)}, u32[]{:S(2)}) copy-start(bf16[25,64,128]{2,1,0:T(8,128)(2,1)S(1)} %collective-permute-done.17.rest_14_) | copy-start | bytes 1228804
  70.2 16.0 %collective-permute-start.11 = (bf16[25,64,128]{2,1,0:T(8,128)(2,1)S(1)}, bf16[25,64,128]{2,1,0:T(8,128)(2,1)S(1)}, u32[]{:S(2)}, u32[]{:S(2)}) collective-permute-start(bf16[25,64,128]{2,1,0:T(8,128)(2,1)S(1)} %collective-permute-done.10.rest_6_), channel_id=1, source_target_pairs={{4,8},{8,12},{12,16},{16,20},{20,24},{24,28},{5,9},{9,13},{13,17},... | collective-permute-start | bytes 1228808 | tf_op jit(solution)/shard_map/ppermute | solution.py:168
  72.2 21.3 %copy-start.14 = (bf16[25,64,128]{2,1,0:T(8,128)(2,1)}, bf16[25,64,128]{2,1,0:T(8,128)(2,1)S(1)}, u32[]{:S(2)}) copy-start(bf16[25,64,128]{2,1,0:T(8,128)(2,1)S(1)} %collective-permute-done.16.rest_13_) | copy-start | bytes 1228804
  72.2 14.1 %collective-permute-start.20 = (bf16[25,64,128]{2,1,0:T(8,128)(2,1)S(1)}, bf16[25,64,128]{2,1,0:T(8,128)(2,1)S(1)}, u32[]{:S(2)}, u32[]{:S(2)}) collective-permute-start(bf16[25,64,128]{2,1,0:T(8,128)(2,1)S(1)} %collective-permute-done.17.rest_14_), channel_id=1, source_target_pairs={{4,0},{8,4},{12,8},{16,12},{20,16},{24,20},{5,1},{9,5},{13,9},{17,... | collective-permute-start | bytes 1228808 | tf_op jit(solution)/shard_map/ppermute | solution.py:168
  75.9 17.6 %copy-start.15 = (bf16[25,64,128]{2,1,0:T(8,128)(2,1)}, bf16[25,64,128]{2,1,0:T(8,128)(2,1)S(1)}, u32[]{:S(2)}) copy-start(bf16[25,64,128]{2,1,0:T(8,128)(2,1)S(1)} %collective-permute-done.6.rest_5_) | copy-start | bytes 1228804
  75.9 10.4 %collective-permute-start.19 = (bf16[25,64,128]{2,1,0:T(8,128)(2,1)S(1)}, bf16[25,64,128]{2,1,0:T(8,128)(2,1)S(1)}, u32[]{:S(2)}, u32[]{:S(2)}) collective-permute-start(bf16[25,64,128]{2,1,0:T(8,128)(2,1)S(1)} %collective-permute-done.16.rest_13_), channel_id=1, source_target_pairs={{4,0},{8,4},{12,8},{16,12},{20,16},{24,20},{5,1},{9,5},{13,9},{17,... | collective-permute-start | bytes 1228808 | tf_op jit(solution)/shard_map/ppermute | solution.py:168
  84.2 2.1 %copy-start.6 = (bf16[2,25,64,128]{3,2,1,0:T(8,128)(2,1)}, bf16[2,25,64,128]{3,2,1,0:T(8,128)(2,1)S(1)}, u32[]{:S(2)}) copy-start(bf16[2,25,64,128]{3,2,1,0:T(8,128)(2,1)S(1)} %collective-permute-done.8.rest_21_) | copy-start | bytes 2457604
  84.2 9.3 %collective-permute-start.7 = (bf16[25,64,128]{2,1,0:T(8,128)(2,1)S(1)}, bf16[25,64,128]{2,1,0:T(8,128)(2,1)S(1)}, u32[]{:S(2)}, u32[]{:S(2)}) collective-permute-start(bf16[25,64,128]{2,1,0:T(8,128)(2,1)S(1)} %collective-permute-done.6.rest_5_), channel_id=1, source_target_pairs={{4,8},{8,12},{12,16},{16,20},{20,24},{24,28},{5,9},{9,13},{13,17},... | collective-permute-start | bytes 1228808 | tf_op jit(solution)/shard_map/ppermute | solution.py:168
  86.2 7.2 %copy-start.7 = (bf16[2,25,64,128]{3,2,1,0:T(8,128)(2,1)}, bf16[2,25,64,128]{3,2,1,0:T(8,128)(2,1)S(1)}, u32[]{:S(2)}) copy-start(bf16[2,25,64,128]{3,2,1,0:T(8,128)(2,1)S(1)} %collective-permute-done.4.rest_20_) | copy-start | bytes 2457604
  86.3 7.3 %copy-start.16 = (bf16[25,64,128]{2,1,0:T(8,128)(2,1)}, bf16[25,64,128]{2,1,0:T(8,128)(2,1)S(1)}, u32[]{:S(2)}) copy-start(bf16[25,64,128]{2,1,0:T(8,128)(2,1)S(1)} %collective-permute-done.11.rest_2_) | copy-start | bytes 1228804
  86.3 7.2 %copy-start.17 = (bf16[25,64,128]{2,1,0:T(8,128)(2,1)}, bf16[25,64,128]{2,1,0:T(8,128)(2,1)S(1)}, u32[]{:S(2)}) copy-start(bf16[25,64,128]{2,1,0:T(8,128)(2,1)S(1)} %collective-permute-done.20.rest_18_) | copy-start | bytes 1228804
  86.3 7.2 %copy-start.18 = (bf16[25,64,128]{2,1,0:T(8,128)(2,1)}, bf16[25,64,128]{2,1,0:T(8,128)(2,1)S(1)}, u32[]{:S(2)}) copy-start(bf16[25,64,128]{2,1,0:T(8,128)(2,1)S(1)} %collective-permute-done.19.rest_17_) | copy-start | bytes 1228804
  93.4 0.8 copy-start.19
  145.5 8.8 %collective-permute-start.22 = (bf16[8,2,64,128]{3,2,1,0:T(8,128)(2,1)S(1)}, bf16[8,2,64,128]{3,2,1,0:T(8,128)(2,1)S(1)}, u32[]{:S(2)}, u32[]{:S(2)}) collective-permute-start(bf16[8,2,64,128]{3,2,1,0:T(8,128)(2,1)S(1)} %get-tuple-element.31), channel_id=1, source_target_pairs={{0,1},{1,2},{2,3},{3,0},{4,5},{5,6},{6,7},{7,4},{8,9},{9,10},{10,1... | collective-permute-start | bytes 786440 | tf_op jit(solution)/shard_map/ppermute | solution.py:249
  149.5 9.2 %collective-permute-start.23 = (bf16[8,2,64,128]{3,2,1,0:T(8,128)(2,1)S(1)}, bf16[8,2,64,128]{3,2,1,0:T(8,128)(2,1)S(1)}, u32[]{:S(2)}, u32[]{:S(2)}) collective-permute-start(bf16[8,2,64,128]{3,2,1,0:T(8,128)(2,1)S(1)} %get-tuple-element.33), channel_id=1, source_target_pairs={{0,2},{1,3},{2,0},{3,1},{4,6},{5,7},{6,4},{7,5},{8,10},{9,11},{10,... | collective-permute-start | bytes 786440 | tf_op jit(solution)/shard_map/ppermute | solution.py:249
  150.0 8.7 %collective-permute-start.24 = (bf16[8,2,64,128]{3,2,1,0:T(8,128)(2,1)S(1)}, bf16[8,2,64,128]{3,2,1,0:T(8,128)(2,1)S(1)}, u32[]{:S(2)}, u32[]{:S(2)}) collective-permute-start(bf16[8,2,64,128]{3,2,1,0:T(8,128)(2,1)S(1)} %get-tuple-element.32), channel_id=1, source_target_pairs={{0,3},{1,0},{2,1},{3,2},{4,7},{5,4},{6,5},{7,6},{8,11},{9,8},{10,9... | collective-permute-start | bytes 786440 | tf_op jit(solution)/shard_map/ppermute | solution.py:249

commit v12 on v11

--- a/solution.py
+++ b/solution.py
@@ -8,7 +8,7 @@
 from jax.sharding import PartitionSpec as P
 
 CB = 4
-ROWS_PER_STEP = 16
+ROWS_PER_STEP = 48
 
 
 def passed_along(block, axis, distance):
@@ -83,7 +83,7 @@
             acc_ref[t] = acc_ref[t] + results[s]
         return carry
 
-    lax.fori_loop(0, rows_here, row_body, 0, unroll=2)
+    lax.fori_loop(0, rows_here, row_body, 0, unroll=4)
 
     @pl.when(step == pl.num_programs(0) - 1)
     def _():

time: 162 us -> 151 us (0.932)
  Pallas kernels: 43.6 us -> 32.1 us
    pallas_call x1, Pallas kernels: 43.6 us -> 32.1 us  [coarse_partial(): pl.pallas_call(coarse_kernel, out_shape=jax.ShapeDtypeStruct((n_targets /...]
  transfers between devices with their start and end apart: 25 -> 25, of which waited for: 5 -> 5; matrix products, arithmetic and copies ran while one was open for 14% -> 15% of each run, Pallas kernels for 0% -> 0%
where the time goes in v12:
time: 151 us; the launch traced here: 150 us
  starting transfers between devices  56.8 us (38%)
  Pallas kernels  32.1 us (21%)
  local copies, waits for them, and re-layouts  29.3 us (19%)
  waiting for transfers between devices  23.7 us (16%)
  other arithmetic  6.78 us (4%)
    ppermute x16, starting transfers between devices, ring(): return lax.ppermute(piece, 'blk', route)  38.6 us
    pallas_call x1, Pallas kernels, coarse_partial(): pl.pallas_call(coarse_kernel, out_shape=jax.ShapeDtypeStruct((n_targets /...  32.1 us
    unnamed x45, local copies, waits for them, and re-layouts  17.7 us
    ppermute x3, starting transfers between devices, local(): fixed.append(lax.ppermute(fix_src, ('blk', 'grp'), route))  9.14 us
    ppermute x3, waiting for transfers between devices, local(): lax.ppermute(outgoing.astype(jnp.bfloat16), 'grp', [(i, (i + k) % group_s...  8.54 us
    ppermute x3, waiting for transfers between devices, local(): fixed.append(lax.ppermute(fix_src, ('blk', 'grp'), route))  8.03 us
    ppermute x16, waiting for transfers between devices, ring(): return lax.ppermute(piece, 'blk', route)  7.14 us
    ppermute x3, starting transfers between devices, local(): lax.ppermute(outgoing.astype(jnp.bfloat16), 'grp', [(i, (i + k) % group_s...  4.66 us
  transfers between devices with their start and end apart: 25, of which 5 were waited for; matrix products, arithmetic and copies ran while one was open for 15% of the time, Pallas kernels for 0%

profile of v12, /device:TPU:26, one launch (start us, length us, event | category | flops | bytes accessed | tf_op | source)
XLA Modules:
  0.0 149.6 jit_solution(7678219350860835655)
XLA Ops:
  0.0 0.7 convert_bitcast_fusion
  0.7 2.0 %copy.17 = bf16[24,2,64,64]{3,1,2,0:T(2,128)(2,1)S(1)} copy(bf16[24,2,64,64]{3,2,1,0:T(8,128)(2,1)} %bitcast.144) | data formatting | bytes 786432 | tf_op jit(solution)/shard_map/reshape | solution.py:142
  2.6 0.3 reshape.739
  3.1 1.7 %collective-permute-start.2 = (bf16[25,64,128]{2,1,0:T(8,128)(2,1)S(1)}, bf16[25,64,128]{2,1,0:T(8,128)(2,1)S(1)}, u32[]{:S(2)}, u32[]{:S(2)}) collective-permute-start(bf16[25,64,128]{2,1,0:T(8,128)(2,1)S(1)} %fusion.3.rest_8_), channel_id=1, source_target_pairs={{4,0},{8,4},{12,8},{16,12},{20,16},{24,20},{28,24},{0,28},{5,1},{9... | collective-permute-start | bytes 1228808 | tf_op jit(solution)/shard_map/ppermute | solution.py:168
  4.8 0.5 collective-permute-start.13
  5.4 1.5 %collective-permute-start.9 = (bf16[25,64,128]{2,1,0:T(8,128)(2,1)S(1)}, bf16[25,64,128]{2,1,0:T(8,128)(2,1)}, u32[]{:S(2)}, u32[]{:S(2)}) collective-permute-start(bf16[25,64,128]{2,1,0:T(8,128)(2,1)S(1)} %fusion.3.rest_8_), channel_id=1, source_target_pairs={{0,2},{1,3},{2,0},{3,1},{4,6},{5,7},{6,4},{7,5},{8,10},{9,11},{10,... | collective-permute-start | bytes 1228808 | tf_op jit(solution)/shard_map/ppermute | solution.py:156
  6.9 2.4 %collective-permute-start.5 = (bf16[25,64,128]{2,1,0:T(8,128)(2,1)S(1)}, bf16[25,64,128]{2,1,0:T(8,128)(2,1)}, u32[]{:S(2)}, u32[]{:S(2)}) collective-permute-start(bf16[25,64,128]{2,1,0:T(8,128)(2,1)S(1)} %fusion.3.rest_8_), channel_id=1, source_target_pairs={{0,1},{1,2},{2,3},{3,0},{4,5},{5,6},{6,7},{7,4},{8,9},{9,10},{10,1... | collective-permute-start | bytes 1228808 | tf_op jit(solution)/shard_map/ppermute | solution.py:156
  9.3 0.1 copy.9
  9.4 0.1 rem.301
  9.6 0.1 rem.276
  9.7 0.1 copy.10
  9.8 0.1 div.78
  9.9 0.1 div.73
  10.0 0.2 copy.8
  10.2 0.1 ne.313
  10.3 0.1 ne.303
  10.5 0.1 compare_convert_fusion
  10.6 0.7 reshape.807.live_ref
  11.3 17.0 %copy.15.values_ref = bf16[192,4,64,64]{3,2,1,0:T(8,128)(2,1)} copy(bf16[192,4,64,64]{0,3,2,1:T(8,128)(2,1)} %param.9) | data formatting | bytes 12582912 | tf_op args[0]
  28.3 0.6 stack.59.fix_ref
  28.9 0.6 fusion.32.own_pos_ref
  29.5 0.1 fusion.16
  29.7 1.7 %collective-permute-start.3 = (bf16[25,64,128]{2,1,0:T(8,128)(2,1)S(1)}, bf16[25,64,128]{2,1,0:T(8,128)(2,1)S(1)}, u32[]{:S(2)}, u32[]{:S(2)}) collective-permute-start(bf16[25,64,128]{2,1,0:T(8,128)(2,1)S(1)} %collective-permute-done.2.rest_12_), channel_id=1, source_target_pairs={{4,0},{8,4},{12,8},{16,12},{20,16},{24,20},{28,24},{0,28},{5,1},{9... | collective-permute-start | bytes 1228808 | tf_op jit(solution)/shard_map/ppermute | solution.py:168
  31.4 2.3 %collective-permute-start.14 = (bf16[25,64,128]{2,1,0:T(8,128)(2,1)}, bf16[25,64,128]{2,1,0:T(8,128)(2,1)S(1)}, u32[]{:S(2)}, u32[]{:S(2)}) collective-permute-start(bf16[25,64,128]{2,1,0:T(8,128)(2,1)} %collective-permute-done.13.rest_11_), channel_id=1, source_target_pairs={{0,4},{4,8},{8,12},{12,16},{16,20},{20,24},{24,28},{1,5},{5,9},{9,... | collective-permute-start | bytes 1228808 | tf_op jit(solution)/shard_map/ppermute | solution.py:168
  33.7 0.7 slice_bitcast_fusion.8
  34.4 3.2 %collective-permute-start.18 = (bf16[25,64,128]{2,1,0:T(8,128)(2,1)}, bf16[25,64,128]{2,1,0:T(8,128)(2,1)S(1)}, u32[]{:S(2)}, u32[]{:S(2)}) collective-permute-start(bf16[25,64,128]{2,1,0:T(8,128)(2,1)} %collective-permute-done.13.rest_11_), channel_id=1, source_target_pairs={{4,0},{8,4},{12,8},{16,12},{20,16},{24,20},{28,24},{5,1},{9,5},{13... | collective-permute-start | bytes 1228808 | tf_op jit(solution)/shard_map/ppermute | solution.py:168
  37.7 4.9 %collective-permute-start.10 = (bf16[25,64,128]{2,1,0:T(8,128)(2,1)}, bf16[25,64,128]{2,1,0:T(8,128)(2,1)S(1)}, u32[]{:S(2)}, u32[]{:S(2)}) collective-permute-start(bf16[25,64,128]{2,1,0:T(8,128)(2,1)} %collective-permute-done.9.rest_10_), channel_id=1, source_target_pairs={{0,4},{4,8},{8,12},{12,16},{16,20},{20,24},{24,28},{1,5},{5,9},{9,... | collective-permute-start | bytes 1228808 | tf_op jit(solution)/shard_map/ppermute | solution.py:168
  42.7 0.1 pad_maximum_fusion.1
  42.8 1.9 %collective-permute-start.12 = (bf16[2,25,64,128]{3,2,1,0:T(8,128)(2,1)S(1)}, bf16[2,25,64,128]{3,2,1,0:T(8,128)(2,1)S(1)}, u32[]{:S(2)}, u32[]{:S(2)}) collective-permute-start(bf16[2,25,64,128]{3,2,1,0:T(8,128)(2,1)S(1)} %pad_maximum_fusion.1), channel_id=1, source_target_pairs={{0,3},{1,0},{2,1},{3,2},{4,7},{5,4},{6,5},{7,6},{24,27},{25,24},{2... | collective-permute-start | bytes 2457608 | tf_op jit(solution)/shard_map/ppermute | solution.py:187
  44.7 0.7 slice_bitcast_fusion.9
  45.4 0.7 slice_bitcast_fusion.10
  46.1 2.5 %collective-permute-start.8 = (bf16[2,25,64,128]{3,2,1,0:T(8,128)(2,1)S(1)}, bf16[2,25,64,128]{3,2,1,0:T(8,128)(2,1)S(1)}, u32[]{:S(2)}, u32[]{:S(2)}) collective-permute-start(bf16[2,25,64,128]{3,2,1,0:T(8,128)(2,1)S(1)} %pad_maximum_fusion.1), channel_id=1, source_target_pairs={{0,2},{1,3},{2,0},{3,1},{4,6},{5,7},{6,4},{7,5},{24,26},{25,27},{2... | collective-permute-start | bytes 2457608 | tf_op jit(solution)/shard_map/ppermute | solution.py:187
  48.6 4.3 %collective-permute-start.15 = (bf16[25,64,128]{2,1,0:T(8,128)(2,1)S(1)}, bf16[25,64,128]{2,1,0:T(8,128)(2,1)S(1)}, u32[]{:S(2)}, u32[]{:S(2)}) collective-permute-start(bf16[25,64,128]{2,1,0:T(8,128)(2,1)S(1)} %collective-permute-done.14.rest_7_), channel_id=1, source_target_pairs={{4,8},{8,12},{12,16},{16,20},{20,24},{24,28},{5,9},{9,13},{13,17},... | collective-permute-start | bytes 1228808 | tf_op jit(solution)/shard_map/ppermute | solution.py:168
  52.9 1.3 collective-permute-start.21
  54.2 4.8 %collective-permute-start.4 = (bf16[2,25,64,128]{3,2,1,0:T(8,128)(2,1)S(1)}, bf16[2,25,64,128]{3,2,1,0:T(8,128)(2,1)S(1)}, u32[]{:S(2)}, u32[]{:S(2)}) collective-permute-start(bf16[2,25,64,128]{3,2,1,0:T(8,128)(2,1)S(1)} %pad_maximum_fusion.1), channel_id=1, source_target_pairs={{0,1},{1,2},{2,3},{3,0},{4,5},{5,6},{6,7},{7,4},{24,25},{25,26},{2... | collective-permute-start | bytes 2457608 | tf_op jit(solution)/shard_map/ppermute | solution.py:187
  59.0 1.9 %collective-permute-start.17 = (bf16[25,64,128]{2,1,0:T(8,128)(2,1)}, bf16[25,64,128]{2,1,0:T(8,128)(2,1)S(1)}, u32[]{:S(2)}, u32[]{:S(2)}) collective-permute-start(bf16[25,64,128]{2,1,0:T(8,128)(2,1)} %collective-permute-done.9.rest_10_), channel_id=1, source_target_pairs={{4,0},{8,4},{12,8},{16,12},{20,16},{24,20},{28,24},{5,1},{9,5},{13... | collective-permute-start | bytes 1228808 | tf_op jit(solution)/shard_map/ppermute | solution.py:168
  61.0 2.4 %collective-permute-start.16 = (bf16[25,64,128]{2,1,0:T(8,128)(2,1)}, bf16[25,64,128]{2,1,0:T(8,128)(2,1)S(1)}, u32[]{:S(2)}, u32[]{:S(2)}) collective-permute-start(bf16[25,64,128]{2,1,0:T(8,128)(2,1)} %collective-permute-done.5.rest_9_), channel_id=1, source_target_pairs={{4,0},{8,4},{12,8},{16,12},{20,16},{24,20},{28,24},{5,1},{9,5},{13... | collective-permute-start | bytes 1228808 | tf_op jit(solution)/shard_map/ppermute | solution.py:168
  63.4 1.7 %collective-permute-done.12.rest_22_ = bf16[2,25,64,128]{3,2,1,0:T(8,128)(2,1)S(1)} collective-permute-done((bf16[2,25,64,128]{3,2,1,0:T(8,128)(2,1)S(1)}, bf16[2,25,64,128]{3,2,1,0:T(8,128)(2,1)S(1)}, u32[]{:S(2)}, u32[]{:S(2)}) %collective-permute-start.12) | collective-permute-done | bytes 819232 | tf_op jit(solution)/shard_map/ppermute | solution.py:187
  65.1 5.1 %collective-permute-start.6 = (bf16[25,64,128]{2,1,0:T(8,128)(2,1)}, bf16[25,64,128]{2,1,0:T(8,128)(2,1)S(1)}, u32[]{:S(2)}, u32[]{:S(2)}) collective-permute-start(bf16[25,64,128]{2,1,0:T(8,128)(2,1)} %collective-permute-done.5.rest_9_), channel_id=1, source_target_pairs={{0,4},{4,8},{8,12},{12,16},{16,20},{20,24},{24,28},{1,5},{5,9},{9,... | collective-permute-start | bytes 1228808 | tf_op jit(solution)/shard_map/ppermute | solution.py:168
  70.2 1.9 %collective-permute-start.11 = (bf16[25,64,128]{2,1,0:T(8,128)(2,1)S(1)}, bf16[25,64,128]{2,1,0:T(8,128)(2,1)S(1)}, u32[]{:S(2)}, u32[]{:S(2)}) collective-permute-start(bf16[25,64,128]{2,1,0:T(8,128)(2,1)S(1)} %collective-permute-done.10.rest_6_), channel_id=1, source_target_pairs={{4,8},{8,12},{12,16},{16,20},{20,24},{24,28},{5,9},{9,13},{13,17},... | collective-permute-start | bytes 1228808 | tf_op jit(solution)/shard_map/ppermute | solution.py:168
  72.2 3.7 %collective-permute-start.20 = (bf16[25,64,128]{2,1,0:T(8,128)(2,1)S(1)}, bf16[25,64,128]{2,1,0:T(8,128)(2,1)S(1)}, u32[]{:S(2)}, u32[]{:S(2)}) collective-permute-start(bf16[25,64,128]{2,1,0:T(8,128)(2,1)S(1)} %collective-permute-done.17.rest_14_), channel_id=1, source_target_pairs={{4,0},{8,4},{12,8},{16,12},{20,16},{24,20},{5,1},{9,5},{13,9},{17,... | collective-permute-start | bytes 1228808 | tf_op jit(solution)/shard_map/ppermute | solution.py:168
  75.9 1.9 %collective-permute-start.19 = (bf16[25,64,128]{2,1,0:T(8,128)(2,1)S(1)}, bf16[25,64,128]{2,1,0:T(8,128)(2,1)S(1)}, u32[]{:S(2)}, u32[]{:S(2)}) collective-permute-start(bf16[25,64,128]{2,1,0:T(8,128)(2,1)S(1)} %collective-permute-done.16.rest_13_), channel_id=1, source_target_pairs={{4,0},{8,4},{12,8},{16,12},{20,16},{24,20},{5,1},{9,5},{13,9},{17,... | collective-permute-start | bytes 1228808 | tf_op jit(solution)/shard_map/ppermute | solution.py:168
  77.8 6.4 %collective-permute-done.8.rest_21_ = bf16[2,25,64,128]{3,2,1,0:T(8,128)(2,1)S(1)} collective-permute-done((bf16[2,25,64,128]{3,2,1,0:T(8,128)(2,1)S(1)}, bf16[2,25,64,128]{3,2,1,0:T(8,128)(2,1)S(1)}, u32[]{:S(2)}, u32[]{:S(2)}) %collective-permute-start.8) | collective-permute-done | bytes 819232 | tf_op jit(solution)/shard_map/ppermute | solution.py:187
  84.2 2.0 %collective-permute-start.7 = (bf16[25,64,128]{2,1,0:T(8,128)(2,1)S(1)}, bf16[25,64,128]{2,1,0:T(8,128)(2,1)S(1)}, u32[]{:S(2)}, u32[]{:S(2)}) collective-permute-start(bf16[25,64,128]{2,1,0:T(8,128)(2,1)S(1)} %collective-permute-done.6.rest_5_), channel_id=1, source_target_pairs={{4,8},{8,12},{12,16},{16,20},{20,24},{24,28},{5,9},{9,13},{13,17},... | collective-permute-start | bytes 1228808 | tf_op jit(solution)/shard_map/ppermute | solution.py:168
  86.3 7.1 %collective-permute-done.7.rest_1_ = bf16[25,64,128]{2,1,0:T(8,128)(2,1)S(1)} collective-permute-done((bf16[25,64,128]{2,1,0:T(8,128)(2,1)S(1)}, bf16[25,64,128]{2,1,0:T(8,128)(2,1)S(1)}, u32[]{:S(2)}, u32[]{:S(2)}) %collective-permute-start.7) | collective-permute-done | bytes 409632 | tf_op jit(solution)/shard_map/ppermute | solution.py:168
  93.5 0.7 copy-done.19
  94.2 0.1 stack.54
  94.3 0.1 reshape.806
  94.4 3.2 %gather_fusion = s32[768]{0:T(1024)S(1)} fusion(s32[960]{0:T(1024)S(1)} %reshape.806, s32[1024]{0:T(1024)S(1)} %pad_clamp_fusion.1), kind=kCustom, calls=%fused_computation | custom fusion | bytes 9216 | tf_op jit(solution)/shard_map/jit(_take)/gather | solution.py:222
  97.6 1.2 gather_fusion.1
  98.8 0.1 broadcast_in_dim.32
  98.9 0.1 reshape.740
  99.0 0.6 multiply_add_fusion
  99.7 0.6 fusion.11.pair_ref
  100.3 32.1 %shard_map.55 = f32[64,64,128]{2,1,0:T(8,128)} custom-call(s32[768]{0:T(1024)} %fusion.11.pair_ref, s32[768]{0:T(1024)} %get-tuple-element.45.half_ref, s32[768]{0:T(1024)} %get-tuple-element.29.target_ref, s32[768]{0:T(1024)} %reshape.807.live_ref, s32[192]{0:T(256)} %fusion.32.own_pos_ref, s32[5]{0:T(128)} %stack.59.fix_ref, ...), custom_call_target="tpu_custom_call" | custom-call | tf_op jit(solution)/shard_map/pallas_call | solution.py:106
  132.3 1.6 %bitcast_convert_fusion.2 = (bf16[8,2,64,128]{3,2,1,0:T(8,128)(2,1)S(1)}, bf16[8,2,64,128]{3,2,1,0:T(8,128)(2,1)S(1)}, bf16[8,2,64,128]{3,2,1,0:T(8,128)(2,1)S(1)}) fusion(f32[4,8,2,64,128]{4,3,2,1,0:T(8,128)} %bitcast.141, s32[]{:T(128)S(6)} %select_n.678, pred[]{:T(512)S(6)} %and.252, s32[]{:T(128)S(6)} %select_n.682, pred[]{:T(512)S(6)} %and.254, ...), kind=kLoop, calls=%fused_computation.9 | loop fusion | flops 393216 | bytes 1572879 | tf_op jit(solution)/shard_map/convert_element_type | solution.py:250
  133.9 4.0 %collective-permute-start.22 = (bf16[8,2,64,128]{3,2,1,0:T(8,128)(2,1)S(1)}, bf16[8,2,64,128]{3,2,1,0:T(8,128)(2,1)S(1)}, u32[]{:S(2)}, u32[]{:S(2)}) collective-permute-start(bf16[8,2,64,128]{3,2,1,0:T(8,128)(2,1)S(1)} %get-tuple-element.31), channel_id=1, source_target_pairs={{0,1},{1,2},{2,3},{3,0},{4,5},{5,6},{6,7},{7,4},{8,9},{9,10},{10,1... | collective-permute-start | bytes 786440 | tf_op jit(solution)/shard_map/ppermute | solution.py:249
  137.9 0.5 collective-permute-start.23
  138.4 0.1 collective-permute-start.24
  138.6 4.1 %collective-permute-done.22 = bf16[8,2,64,128]{3,2,1,0:T(8,128)(2,1)S(1)} collective-permute-done((bf16[8,2,64,128]{3,2,1,0:T(8,128)(2,1)S(1)}, bf16[8,2,64,128]{3,2,1,0:T(8,128)(2,1)S(1)}, u32[]{:S(2)}, u32[]{:S(2)}) %collective-permute-start.22) | collective-permute-done | bytes 262176 | tf_op jit(solution)/shard_map/ppermute | solution.py:249
  142.7 4.4 %collective-permute-done.23 = bf16[8,2,64,128]{3,2,1,0:T(8,128)(2,1)S(1)} collective-permute-done((bf16[8,2,64,128]{3,2,1,0:T(8,128)(2,1)S(1)}, bf16[8,2,64,128]{3,2,1,0:T(8,128)(2,1)S(1)}, u32[]{:S(2)}, u32[]{:S(2)}) %collective-permute-start.23) | collective-permute-done | bytes 262176 | tf_op jit(solution)/shard_map/ppermute | solution.py:249
  147.1 1.2 fusion.2
  148.3 0.2 fusion.46
  148.5 1.1 pad_maximum_fusion
  (86 shorter events, 0.5 us)
Async XLA Ops:
  0.0 9.3 %copy-start.20 = (s32[192,4]{0,1:T(4,128)S(1)}, s32[192,4]{0,1:T(4,128)}, u32[]{:S(2)}) copy-start(s32[192,4]{0,1:T(4,128)} %param.10) | copy-start | bytes 9220
  0.7 9.9 %copy-start.21 = (s32[192]{0:T(256)S(1)}, s32[192]{0:T(256)}, u32[]{:S(2)}) copy-start(s32[192]{0:T(256)} %param.11) | copy-start | bytes 2308
  3.0 25.3 %copy-start.4 = (bf16[25,64,128]{2,1,0:T(8,128)(2,1)}, bf16[25,64,128]{2,1,0:T(8,128)(2,1)S(1)}, u32[]{:S(2)}) copy-start(bf16[25,64,128]{2,1,0:T(8,128)(2,1)S(1)} %fusion.3.rest_8_) | copy-start | bytes 1228804
  3.0 26.5 %collective-permute-start = (bf16[25,64,128]{2,1,0:T(8,128)(2,1)S(1)}, bf16[25,64,128]{2,1,0:T(8,128)(2,1)S(1)}, u32[]{:S(2)}, u32[]{:S(2)}) collective-permute-start(bf16[25,64,128]{2,1,0:T(8,128)(2,1)S(1)} %fusion.3.rest_8_), channel_id=1, source_target_pairs={{28,0},{0,4},{4,8},{8,12},{12,16},{16,20},{20,24},{24,28},{29,1},{... | collective-permute-start | bytes 1228808 | tf_op jit(solution)/shard_map/ppermute | solution.py:168
  3.1 26.5 %collective-permute-start.2 = (bf16[25,64,128]{2,1,0:T(8,128)(2,1)S(1)}, bf16[25,64,128]{2,1,0:T(8,128)(2,1)S(1)}, u32[]{:S(2)}, u32[]{:S(2)}) collective-permute-start(bf16[25,64,128]{2,1,0:T(8,128)(2,1)S(1)} %fusion.3.rest_8_), channel_id=1, source_target_pairs={{4,0},{8,4},{12,8},{16,12},{20,16},{24,20},{28,24},{0,28},{5,1},{9... | collective-permute-start | bytes 1228808 | tf_op jit(solution)/shard_map/ppermute | solution.py:168
  4.8 26.6 %collective-permute-start.13 = (bf16[25,64,128]{2,1,0:T(8,128)(2,1)S(1)}, bf16[25,64,128]{2,1,0:T(8,128)(2,1)}, u32[]{:S(2)}, u32[]{:S(2)}) collective-permute-start(bf16[25,64,128]{2,1,0:T(8,128)(2,1)S(1)} %fusion.3.rest_8_), channel_id=1, source_target_pairs={{0,3},{1,0},{2,1},{3,2},{4,7},{5,4},{6,5},{7,6},{8,11},{9,8},{10,9... | collective-permute-start | bytes 1228808 | tf_op jit(solution)/shard_map/ppermute | solution.py:156
  5.4 29.1 %collective-permute-start.9 = (bf16[25,64,128]{2,1,0:T(8,128)(2,1)S(1)}, bf16[25,64,128]{2,1,0:T(8,128)(2,1)}, u32[]{:S(2)}, u32[]{:S(2)}) collective-permute-start(bf16[25,64,128]{2,1,0:T(8,128)(2,1)S(1)} %fusion.3.rest_8_), channel_id=1, source_target_pairs={{0,2},{1,3},{2,0},{3,1},{4,6},{5,7},{6,4},{7,5},{8,10},{9,11},{10,... | collective-permute-start | bytes 1228808 | tf_op jit(solution)/shard_map/ppermute | solution.py:156
  6.9 38.5 %collective-permute-start.5 = (bf16[25,64,128]{2,1,0:T(8,128)(2,1)S(1)}, bf16[25,64,128]{2,1,0:T(8,128)(2,1)}, u32[]{:S(2)}, u32[]{:S(2)}) collective-permute-start(bf16[25,64,128]{2,1,0:T(8,128)(2,1)S(1)} %fusion.3.rest_8_), channel_id=1, source_target_pairs={{0,1},{1,2},{2,3},{3,0},{4,5},{5,6},{6,7},{7,4},{8,9},{9,10},{10,1... | collective-permute-start | bytes 1228808 | tf_op jit(solution)/shard_map/ppermute | solution.py:156
  29.6 64.7 %copy-start = (bf16[25,64,128]{2,1,0:T(8,128)(2,1)}, bf16[25,64,128]{2,1,0:T(8,128)(2,1)S(1)}, u32[]{:S(2)}) copy-start(bf16[25,64,128]{2,1,0:T(8,128)(2,1)S(1)} %collective-permute-done.rest_4_) | copy-start | bytes 1228804
  29.6 8.1 %collective-permute-start.1 = (bf16[25,64,128]{2,1,0:T(8,128)(2,1)S(1)}, bf16[25,64,128]{2,1,0:T(8,128)(2,1)S(1)}, u32[]{:S(2)}, u32[]{:S(2)}) collective-permute-start(bf16[25,64,128]{2,1,0:T(8,128)(2,1)S(1)} %collective-permute-done.rest_4_), channel_id=1, source_target_pairs={{28,0},{0,4},{4,8},{8,12},{12,16},{16,20},{20,24},{24,28},{29,1},{... | collective-permute-start | bytes 1228808 | tf_op jit(solution)/shard_map/ppermute | solution.py:168
  29.7 64.7 %copy-start.1 = (bf16[25,64,128]{2,1,0:T(8,128)(2,1)}, bf16[25,64,128]{2,1,0:T(8,128)(2,1)S(1)}, u32[]{:S(2)}) copy-start(bf16[25,64,128]{2,1,0:T(8,128)(2,1)S(1)} %collective-permute-done.2.rest_12_) | copy-start | bytes 1228804
  29.7 13.0 %collective-permute-start.3 = (bf16[25,64,128]{2,1,0:T(8,128)(2,1)S(1)}, bf16[25,64,128]{2,1,0:T(8,128)(2,1)S(1)}, u32[]{:S(2)}, u32[]{:S(2)}) collective-permute-start(bf16[25,64,128]{2,1,0:T(8,128)(2,1)S(1)} %collective-permute-done.2.rest_12_), channel_id=1, source_target_pairs={{4,0},{8,4},{12,8},{16,12},{20,16},{24,20},{28,24},{0,28},{5,1},{9... | collective-permute-start | bytes 1228808 | tf_op jit(solution)/shard_map/ppermute | solution.py:168
  31.4 17.2 %collective-permute-start.14 = (bf16[25,64,128]{2,1,0:T(8,128)(2,1)}, bf16[25,64,128]{2,1,0:T(8,128)(2,1)S(1)}, u32[]{:S(2)}, u32[]{:S(2)}) collective-permute-start(bf16[25,64,128]{2,1,0:T(8,128)(2,1)} %collective-permute-done.13.rest_11_), channel_id=1, source_target_pairs={{0,4},{4,8},{8,12},{12,16},{16,20},{20,24},{24,28},{1,5},{5,9},{9,... | collective-permute-start | bytes 1228808 | tf_op jit(solution)/shard_map/ppermute | solution.py:168
  34.4 18.4 %collective-permute-start.18 = (bf16[25,64,128]{2,1,0:T(8,128)(2,1)}, bf16[25,64,128]{2,1,0:T(8,128)(2,1)S(1)}, u32[]{:S(2)}, u32[]{:S(2)}) collective-permute-start(bf16[25,64,128]{2,1,0:T(8,128)(2,1)} %collective-permute-done.13.rest_11_), channel_id=1, source_target_pairs={{4,0},{8,4},{12,8},{16,12},{20,16},{24,20},{28,24},{5,1},{9,5},{13... | collective-permute-start | bytes 1228808 | tf_op jit(solution)/shard_map/ppermute | solution.py:168
  37.7 59.9 %copy-start.2 = (bf16[25,64,128]{2,1,0:T(8,128)(2,1)}, bf16[25,64,128]{2,1,0:T(8,128)(2,1)S(1)}, u32[]{:S(2)}) copy-start(bf16[25,64,128]{2,1,0:T(8,128)(2,1)S(1)} %collective-permute-done.1.rest_0_) | copy-start | bytes 1228804
  37.7 16.5 %collective-permute-start.10 = (bf16[25,64,128]{2,1,0:T(8,128)(2,1)}, bf16[25,64,128]{2,1,0:T(8,128)(2,1)S(1)}, u32[]{:S(2)}, u32[]{:S(2)}) collective-permute-start(bf16[25,64,128]{2,1,0:T(8,128)(2,1)} %collective-permute-done.9.rest_10_), channel_id=1, source_target_pairs={{0,4},{4,8},{8,12},{12,16},{16,20},{20,24},{24,28},{1,5},{5,9},{9,... | collective-permute-start | bytes 1228808 | tf_op jit(solution)/shard_map/ppermute | solution.py:168
  42.7 54.9 %copy-start.3 = (bf16[25,64,128]{2,1,0:T(8,128)(2,1)}, bf16[25,64,128]{2,1,0:T(8,128)(2,1)S(1)}, u32[]{:S(2)}) copy-start(bf16[25,64,128]{2,1,0:T(8,128)(2,1)S(1)} %collective-permute-done.3.rest_16_) | copy-start | bytes 1228804
  42.8 22.3 %collective-permute-start.12 = (bf16[2,25,64,128]{3,2,1,0:T(8,128)(2,1)S(1)}, bf16[2,25,64,128]{3,2,1,0:T(8,128)(2,1)S(1)}, u32[]{:S(2)}, u32[]{:S(2)}) collective-permute-start(bf16[2,25,64,128]{3,2,1,0:T(8,128)(2,1)S(1)} %pad_maximum_fusion.1), channel_id=1, source_target_pairs={{0,3},{1,0},{2,1},{3,2},{4,7},{5,4},{6,5},{7,6},{24,27},{25,24},{2... | collective-permute-start | bytes 2457608 | tf_op jit(solution)/shard_map/ppermute | solution.py:187
  46.1 38.1 %collective-permute-start.8 = (bf16[2,25,64,128]{3,2,1,0:T(8,128)(2,1)S(1)}, bf16[2,25,64,128]{3,2,1,0:T(8,128)(2,1)S(1)}, u32[]{:S(2)}, u32[]{:S(2)}) collective-permute-start(bf16[2,25,64,128]{3,2,1,0:T(8,128)(2,1)S(1)} %pad_maximum_fusion.1), channel_id=1, source_target_pairs={{0,2},{1,3},{2,0},{3,1},{4,6},{5,7},{6,4},{7,5},{24,26},{25,27},{2... | collective-permute-start | bytes 2457608 | tf_op jit(solution)/shard_map/ppermute | solution.py:187
  48.6 51.7 %copy-start.8 = (bf16[25,64,128]{2,1,0:T(8,128)(2,1)}, bf16[25,64,128]{2,1,0:T(8,128)(2,1)S(1)}, u32[]{:S(2)}) copy-start(bf16[25,64,128]{2,1,0:T(8,128)(2,1)S(1)} %collective-permute-done.14.rest_7_) | copy-start | bytes 1228804
  48.6 10.4 %collective-permute-start.15 = (bf16[25,64,128]{2,1,0:T(8,128)(2,1)S(1)}, bf16[25,64,128]{2,1,0:T(8,128)(2,1)S(1)}, u32[]{:S(2)}, u32[]{:S(2)}) collective-permute-start(bf16[25,64,128]{2,1,0:T(8,128)(2,1)S(1)} %collective-permute-done.14.rest_7_), channel_id=1, source_target_pairs={{4,8},{8,12},{12,16},{16,20},{20,24},{24,28},{5,9},{9,13},{13,17},... | collective-permute-start | bytes 1228808 | tf_op jit(solution)/shard_map/ppermute | solution.py:168
  52.9 40.6 %copy-start.9 = (bf16[25,64,128]{2,1,0:T(8,128)(2,1)}, bf16[25,64,128]{2,1,0:T(8,128)(2,1)S(1)}, u32[]{:S(2)}) copy-start(bf16[25,64,128]{2,1,0:T(8,128)(2,1)S(1)} %collective-permute-done.18.rest_15_) | copy-start | bytes 1228804
  52.9 8.1 %collective-permute-start.21 = (bf16[25,64,128]{2,1,0:T(8,128)(2,1)S(1)}, bf16[25,64,128]{2,1,0:T(8,128)(2,1)S(1)}, u32[]{:S(2)}, u32[]{:S(2)}) collective-permute-start(bf16[25,64,128]{2,1,0:T(8,128)(2,1)S(1)} %collective-permute-done.18.rest_15_), channel_id=1, source_target_pairs={{4,0},{8,4},{12,8},{16,12},{20,16},{24,20},{5,1},{9,5},{13,9},{17,... | collective-permute-start | bytes 1228808 | tf_op jit(solution)/shard_map/ppermute | solution.py:168
  54.2 39.2 %copy-start.10 = (bf16[25,64,128]{2,1,0:T(8,128)(2,1)}, bf16[25,64,128]{2,1,0:T(8,128)(2,1)S(1)}, u32[]{:S(2)}) copy-start(bf16[25,64,128]{2,1,0:T(8,128)(2,1)S(1)} %collective-permute-done.10.rest_6_) | copy-start | bytes 1228804
  54.2 32.0 %collective-permute-start.4 = (bf16[2,25,64,128]{3,2,1,0:T(8,128)(2,1)S(1)}, bf16[2,25,64,128]{3,2,1,0:T(8,128)(2,1)S(1)}, u32[]{:S(2)}, u32[]{:S(2)}) collective-permute-start(bf16[2,25,64,128]{3,2,1,0:T(8,128)(2,1)S(1)} %pad_maximum_fusion.1), channel_id=1, source_target_pairs={{0,1},{1,2},{2,3},{3,0},{4,5},{5,6},{6,7},{7,4},{24,25},{25,26},{2... | collective-permute-start | bytes 2457608 | tf_op jit(solution)/shard_map/ppermute | solution.py:187
  59.0 41.2 %copy-start.11 = (bf16[25,64,128]{2,1,0:T(8,128)(2,1)}, bf16[25,64,128]{2,1,0:T(8,128)(2,1)S(1)}, u32[]{:S(2)}) copy-start(bf16[25,64,128]{2,1,0:T(8,128)(2,1)S(1)} %collective-permute-done.15.rest_3_) | copy-start | bytes 1228804
  59.0 11.2 %collective-permute-start.17 = (bf16[25,64,128]{2,1,0:T(8,128)(2,1)}, bf16[25,64,128]{2,1,0:T(8,128)(2,1)S(1)}, u32[]{:S(2)}, u32[]{:S(2)}) collective-permute-start(bf16[25,64,128]{2,1,0:T(8,128)(2,1)} %collective-permute-done.9.rest_10_), channel_id=1, source_target_pairs={{4,0},{8,4},{12,8},{16,12},{20,16},{24,20},{28,24},{5,1},{9,5},{13... | collective-permute-start | bytes 1228808 | tf_op jit(solution)/shard_map/ppermute | solution.py:168
  61.0 32.5 %copy-start.12 = (bf16[25,64,128]{2,1,0:T(8,128)(2,1)}, bf16[25,64,128]{2,1,0:T(8,128)(2,1)S(1)}, u32[]{:S(2)}) copy-start(bf16[25,64,128]{2,1,0:T(8,128)(2,1)S(1)} %collective-permute-done.21.rest_19_) | copy-start | bytes 1228804
  61.0 11.2 %collective-permute-start.16 = (bf16[25,64,128]{2,1,0:T(8,128)(2,1)}, bf16[25,64,128]{2,1,0:T(8,128)(2,1)S(1)}, u32[]{:S(2)}, u32[]{:S(2)}) collective-permute-start(bf16[25,64,128]{2,1,0:T(8,128)(2,1)} %collective-permute-done.5.rest_9_), channel_id=1, source_target_pairs={{4,0},{8,4},{12,8},{16,12},{20,16},{24,20},{28,24},{5,1},{9,5},{13... | collective-permute-start | bytes 1228808 | tf_op jit(solution)/shard_map/ppermute | solution.py:168
  65.1 32.5 %copy-start.5 = (bf16[2,25,64,128]{3,2,1,0:T(8,128)(2,1)}, bf16[2,25,64,128]{3,2,1,0:T(8,128)(2,1)S(1)}, u32[]{:S(2)}) copy-start(bf16[2,25,64,128]{3,2,1,0:T(8,128)(2,1)S(1)} %collective-permute-done.12.rest_22_) | copy-start | bytes 2457604
  65.1 10.8 %collective-permute-start.6 = (bf16[25,64,128]{2,1,0:T(8,128)(2,1)}, bf16[25,64,128]{2,1,0:T(8,128)(2,1)S(1)}, u32[]{:S(2)}, u32[]{:S(2)}) collective-permute-start(bf16[25,64,128]{2,1,0:T(8,128)(2,1)} %collective-permute-done.5.rest_9_), channel_id=1, source_target_pairs={{0,4},{4,8},{8,12},{12,16},{16,20},{20,24},{24,28},{1,5},{5,9},{9,... | collective-permute-start | bytes 1228808 | tf_op jit(solution)/shard_map/ppermute | solution.py:168
  70.2 23.3 %copy-start.13 = (bf16[25,64,128]{2,1,0:T(8,128)(2,1)}, bf16[25,64,128]{2,1,0:T(8,128)(2,1)S(1)}, u32[]{:S(2)}) copy-start(bf16[25,64,128]{2,1,0:T(8,128)(2,1)S(1)} %collective-permute-done.17.rest_14_) | copy-start | bytes 1228804
  70.2 16.0 %collective-permute-start.11 = (bf16[25,64,128]{2,1,0:T(8,128)(2,1)S(1)}, bf16[25,64,128]{2,1,0:T(8,128)(2,1)S(1)}, u32[]{:S(2)}, u32[]{:S(2)}) collective-permute-start(bf16[25,64,128]{2,1,0:T(8,128)(2,1)S(1)} %collective-permute-done.10.rest_6_), channel_id=1, source_target_pairs={{4,8},{8,12},{12,16},{16,20},{20,24},{24,28},{5,9},{9,13},{13,17},... | collective-permute-start | bytes 1228808 | tf_op jit(solution)/shard_map/ppermute | solution.py:168
  72.2 21.3 %copy-start.14 = (bf16[25,64,128]{2,1,0:T(8,128)(2,1)}, bf16[25,64,128]{2,1,0:T(8,128)(2,1)S(1)}, u32[]{:S(2)}) copy-start(bf16[25,64,128]{2,1,0:T(8,128)(2,1)S(1)} %collective-permute-done.16.rest_13_) | copy-start | bytes 1228804
  72.2 14.1 %collective-permute-start.20 = (bf16[25,64,128]{2,1,0:T(8,128)(2,1)S(1)}, bf16[25,64,128]{2,1,0:T(8,128)(2,1)S(1)}, u32[]{:S(2)}, u32[]{:S(2)}) collective-permute-start(bf16[25,64,128]{2,1,0:T(8,128)(2,1)S(1)} %collective-permute-done.17.rest_14_), channel_id=1, source_target_pairs={{4,0},{8,4},{12,8},{16,12},{20,16},{24,20},{5,1},{9,5},{13,9},{17,... | collective-permute-start | bytes 1228808 | tf_op jit(solution)/shard_map/ppermute | solution.py:168
  75.9 17.6 %copy-start.15 = (bf16[25,64,128]{2,1,0:T(8,128)(2,1)}, bf16[25,64,128]{2,1,0:T(8,128)(2,1)S(1)}, u32[]{:S(2)}) copy-start(bf16[25,64,128]{2,1,0:T(8,128)(2,1)S(1)} %collective-permute-done.6.rest_5_) | copy-start | bytes 1228804
  75.9 10.4 %collective-permute-start.19 = (bf16[25,64,128]{2,1,0:T(8,128)(2,1)S(1)}, bf16[25,64,128]{2,1,0:T(8,128)(2,1)S(1)}, u32[]{:S(2)}, u32[]{:S(2)}) collective-permute-start(bf16[25,64,128]{2,1,0:T(8,128)(2,1)S(1)} %collective-permute-done.16.rest_13_), channel_id=1, source_target_pairs={{4,0},{8,4},{12,8},{16,12},{20,16},{24,20},{5,1},{9,5},{13,9},{17,... | collective-permute-start | bytes 1228808 | tf_op jit(solution)/shard_map/ppermute | solution.py:168
  84.2 2.1 %copy-start.6 = (bf16[2,25,64,128]{3,2,1,0:T(8,128)(2,1)}, bf16[2,25,64,128]{3,2,1,0:T(8,128)(2,1)S(1)}, u32[]{:S(2)}) copy-start(bf16[2,25,64,128]{3,2,1,0:T(8,128)(2,1)S(1)} %collective-permute-done.8.rest_21_) | copy-start | bytes 2457604
  84.2 9.3 %collective-permute-start.7 = (bf16[25,64,128]{2,1,0:T(8,128)(2,1)S(1)}, bf16[25,64,128]{2,1,0:T(8,128)(2,1)S(1)}, u32[]{:S(2)}, u32[]{:S(2)}) collective-permute-start(bf16[25,64,128]{2,1,0:T(8,128)(2,1)S(1)} %collective-permute-done.6.rest_5_), channel_id=1, source_target_pairs={{4,8},{8,12},{12,16},{16,20},{20,24},{24,28},{5,9},{9,13},{13,17},... | collective-permute-start | bytes 1228808 | tf_op jit(solution)/shard_map/ppermute | solution.py:168
  86.2 7.2 %copy-start.7 = (bf16[2,25,64,128]{3,2,1,0:T(8,128)(2,1)}, bf16[2,25,64,128]{3,2,1,0:T(8,128)(2,1)S(1)}, u32[]{:S(2)}) copy-start(bf16[2,25,64,128]{3,2,1,0:T(8,128)(2,1)S(1)} %collective-permute-done.4.rest_20_) | copy-start | bytes 2457604
  86.3 7.3 %copy-start.16 = (bf16[25,64,128]{2,1,0:T(8,128)(2,1)}, bf16[25,64,128]{2,1,0:T(8,128)(2,1)S(1)}, u32[]{:S(2)}) copy-start(bf16[25,64,128]{2,1,0:T(8,128)(2,1)S(1)} %collective-permute-done.11.rest_2_) | copy-start | bytes 1228804
  86.3 7.2 %copy-start.17 = (bf16[25,64,128]{2,1,0:T(8,128)(2,1)}, bf16[25,64,128]{2,1,0:T(8,128)(2,1)S(1)}, u32[]{:S(2)}) copy-start(bf16[25,64,128]{2,1,0:T(8,128)(2,1)S(1)} %collective-permute-done.20.rest_18_) | copy-start | bytes 1228804
  86.3 7.2 %copy-start.18 = (bf16[25,64,128]{2,1,0:T(8,128)(2,1)}, bf16[25,64,128]{2,1,0:T(8,128)(2,1)S(1)}, u32[]{:S(2)}) copy-start(bf16[25,64,128]{2,1,0:T(8,128)(2,1)S(1)} %collective-permute-done.19.rest_17_) | copy-start | bytes 1228804
  93.4 0.8 copy-start.19
  133.9 8.8 %collective-permute-start.22 = (bf16[8,2,64,128]{3,2,1,0:T(8,128)(2,1)S(1)}, bf16[8,2,64,128]{3,2,1,0:T(8,128)(2,1)S(1)}, u32[]{:S(2)}, u32[]{:S(2)}) collective-permute-start(bf16[8,2,64,128]{3,2,1,0:T(8,128)(2,1)S(1)} %get-tuple-element.31), channel_id=1, source_target_pairs={{0,1},{1,2},{2,3},{3,0},{4,5},{5,6},{6,7},{7,4},{8,9},{9,10},{10,1... | collective-permute-start | bytes 786440 | tf_op jit(solution)/shard_map/ppermute | solution.py:249
  137.9 9.2 %collective-permute-start.23 = (bf16[8,2,64,128]{3,2,1,0:T(8,128)(2,1)S(1)}, bf16[8,2,64,128]{3,2,1,0:T(8,128)(2,1)S(1)}, u32[]{:S(2)}, u32[]{:S(2)}) collective-permute-start(bf16[8,2,64,128]{3,2,1,0:T(8,128)(2,1)S(1)} %get-tuple-element.33), channel_id=1, source_target_pairs={{0,2},{1,3},{2,0},{3,1},{4,6},{5,7},{6,4},{7,5},{8,10},{9,11},{10,... | collective-permute-start | bytes 786440 | tf_op jit(solution)/shard_map/ppermute | solution.py:249
  138.4 8.7 %collective-permute-start.24 = (bf16[8,2,64,128]{3,2,1,0:T(8,128)(2,1)S(1)}, bf16[8,2,64,128]{3,2,1,0:T(8,128)(2,1)S(1)}, u32[]{:S(2)}, u32[]{:S(2)}) collective-permute-start(bf16[8,2,64,128]{3,2,1,0:T(8,128)(2,1)S(1)} %get-tuple-element.32), channel_id=1, source_target_pairs={{0,3},{1,0},{2,1},{3,2},{4,7},{5,4},{6,5},{7,6},{8,11},{9,8},{10,9... | collective-permute-start | bytes 786440 | tf_op jit(solution)/shard_map/ppermute | solution.py:249

commit v13 on v12

--- a/solution.py
+++ b/solution.py
@@ -83,7 +83,7 @@
             acc_ref[t] = acc_ref[t] + results[s]
         return carry
 
-    lax.fori_loop(0, rows_here, row_body, 0, unroll=4)
+    lax.fori_loop(0, rows_here, row_body, 0, unroll=8)
 
     @pl.when(step == pl.num_programs(0) - 1)
     def _():

time: 151 us -> 145 us (0.960)
  Pallas kernels: 32.1 us -> 26.1 us
    pallas_call x1, Pallas kernels: 32.1 us -> 26.1 us  [coarse_partial(): pl.pallas_call(coarse_kernel, out_shape=jax.ShapeDtypeStruct((n_targets /...]
  transfers between devices with their start and end apart: 25 -> 25, of which waited for: 5 -> 5; matrix products, arithmetic and copies ran while one was open for 15% -> 16% of each run, Pallas kernels for 0% -> 0%
where the time goes in v13:
time: 145 us; the launch traced here: 144 us
  starting transfers between devices  56.8 us (39%)
  local copies, waits for them, and re-layouts  29.3 us (20%)
  Pallas kernels  26.1 us (18%)
  waiting for transfers between devices  23.7 us (16%)
  other arithmetic  6.78 us (5%)
    ppermute x16, starting transfers between devices, ring(): return lax.ppermute(piece, 'blk', route)  38.6 us
    pallas_call x1, Pallas kernels, coarse_partial(): pl.pallas_call(coarse_kernel, out_shape=jax.ShapeDtypeStruct((n_targets /...  26.1 us
    unnamed x45, local copies, waits for them, and re-layouts  17.7 us
    ppermute x3, starting transfers between devices, local(): fixed.append(lax.ppermute(fix_src, ('blk', 'grp'), route))  9.14 us
    ppermute x3, waiting for transfers between devices, local(): lax.ppermute(outgoing.astype(jnp.bfloat16), 'grp', [(i, (i + k) % group_s...  8.54 us
    ppermute x3, waiting for transfers between devices, local(): fixed.append(lax.ppermute(fix_src, ('blk', 'grp'), route))  8.03 us
    ppermute x16, waiting for transfers between devices, ring(): return lax.ppermute(piece, 'blk', route)  7.14 us
    ppermute x3, starting transfers between devices, local(): lax.ppermute(outgoing.astype(jnp.bfloat16), 'grp', [(i, (i + k) % group_s...  4.66 us
  transfers between devices with their start and end apart: 25, of which 5 were waited for; matrix products, arithmetic and copies ran while one was open for 16% of the time, Pallas kernels for 0%

profile of v13, /device:TPU:26, one launch (start us, length us, event | category | flops | bytes accessed | tf_op | source)
XLA Modules:
  0.0 143.6 jit_solution(8134267752569832387)
XLA Ops:
  0.0 0.7 convert_bitcast_fusion
  0.7 2.0 %copy.17 = bf16[24,2,64,64]{3,1,2,0:T(2,128)(2,1)S(1)} copy(bf16[24,2,64,64]{3,2,1,0:T(8,128)(2,1)} %bitcast.144) | data formatting | bytes 786432 | tf_op jit(solution)/shard_map/reshape | solution.py:142
  2.6 0.3 reshape.739
  3.1 1.7 %collective-permute-start.2 = (bf16[25,64,128]{2,1,0:T(8,128)(2,1)S(1)}, bf16[25,64,128]{2,1,0:T(8,128)(2,1)S(1)}, u32[]{:S(2)}, u32[]{:S(2)}) collective-permute-start(bf16[25,64,128]{2,1,0:T(8,128)(2,1)S(1)} %fusion.3.rest_8_), channel_id=1, source_target_pairs={{4,0},{8,4},{12,8},{16,12},{20,16},{24,20},{28,24},{0,28},{5,1},{9... | collective-permute-start | bytes 1228808 | tf_op jit(solution)/shard_map/ppermute | solution.py:168
  4.8 0.5 collective-permute-start.13
  5.4 1.5 %collective-permute-start.9 = (bf16[25,64,128]{2,1,0:T(8,128)(2,1)S(1)}, bf16[25,64,128]{2,1,0:T(8,128)(2,1)}, u32[]{:S(2)}, u32[]{:S(2)}) collective-permute-start(bf16[25,64,128]{2,1,0:T(8,128)(2,1)S(1)} %fusion.3.rest_8_), channel_id=1, source_target_pairs={{0,2},{1,3},{2,0},{3,1},{4,6},{5,7},{6,4},{7,5},{8,10},{9,11},{10,... | collective-permute-start | bytes 1228808 | tf_op jit(solution)/shard_map/ppermute | solution.py:156
  6.9 2.4 %collective-permute-start.5 = (bf16[25,64,128]{2,1,0:T(8,128)(2,1)S(1)}, bf16[25,64,128]{2,1,0:T(8,128)(2,1)}, u32[]{:S(2)}, u32[]{:S(2)}) collective-permute-start(bf16[25,64,128]{2,1,0:T(8,128)(2,1)S(1)} %fusion.3.rest_8_), channel_id=1, source_target_pairs={{0,1},{1,2},{2,3},{3,0},{4,5},{5,6},{6,7},{7,4},{8,9},{9,10},{10,1... | collective-permute-start | bytes 1228808 | tf_op jit(solution)/shard_map/ppermute | solution.py:156
  9.3 0.1 copy.9
  9.4 0.1 rem.301
  9.6 0.1 rem.276
  9.7 0.1 copy.10
  9.8 0.1 div.78
  9.9 0.1 div.73
  10.0 0.2 copy.8
  10.2 0.1 ne.313
  10.3 0.1 ne.303
  10.5 0.1 compare_convert_fusion
  10.6 0.7 reshape.807.live_ref
  11.3 17.0 %copy.15.values_ref = bf16[192,4,64,64]{3,2,1,0:T(8,128)(2,1)} copy(bf16[192,4,64,64]{0,3,2,1:T(8,128)(2,1)} %param.9) | data formatting | bytes 12582912 | tf_op args[0]
  28.3 0.6 stack.59.fix_ref
  28.9 0.6 fusion.32.own_pos_ref
  29.5 0.1 fusion.16
  29.7 1.7 %collective-permute-start.3 = (bf16[25,64,128]{2,1,0:T(8,128)(2,1)S(1)}, bf16[25,64,128]{2,1,0:T(8,128)(2,1)S(1)}, u32[]{:S(2)}, u32[]{:S(2)}) collective-permute-start(bf16[25,64,128]{2,1,0:T(8,128)(2,1)S(1)} %collective-permute-done.2.rest_12_), channel_id=1, source_target_pairs={{4,0},{8,4},{12,8},{16,12},{20,16},{24,20},{28,24},{0,28},{5,1},{9... | collective-permute-start | bytes 1228808 | tf_op jit(solution)/shard_map/ppermute | solution.py:168
  31.4 2.3 %collective-permute-start.14 = (bf16[25,64,128]{2,1,0:T(8,128)(2,1)}, bf16[25,64,128]{2,1,0:T(8,128)(2,1)S(1)}, u32[]{:S(2)}, u32[]{:S(2)}) collective-permute-start(bf16[25,64,128]{2,1,0:T(8,128)(2,1)} %collective-permute-done.13.rest_11_), channel_id=1, source_target_pairs={{0,4},{4,8},{8,12},{12,16},{16,20},{20,24},{24,28},{1,5},{5,9},{9,... | collective-permute-start | bytes 1228808 | tf_op jit(solution)/shard_map/ppermute | solution.py:168
  33.7 0.7 slice_bitcast_fusion.8
  34.4 3.2 %collective-permute-start.18 = (bf16[25,64,128]{2,1,0:T(8,128)(2,1)}, bf16[25,64,128]{2,1,0:T(8,128)(2,1)S(1)}, u32[]{:S(2)}, u32[]{:S(2)}) collective-permute-start(bf16[25,64,128]{2,1,0:T(8,128)(2,1)} %collective-permute-done.13.rest_11_), channel_id=1, source_target_pairs={{4,0},{8,4},{12,8},{16,12},{20,16},{24,20},{28,24},{5,1},{9,5},{13... | collective-permute-start | bytes 1228808 | tf_op jit(solution)/shard_map/ppermute | solution.py:168
  37.7 4.9 %collective-permute-start.10 = (bf16[25,64,128]{2,1,0:T(8,128)(2,1)}, bf16[25,64,128]{2,1,0:T(8,128)(2,1)S(1)}, u32[]{:S(2)}, u32[]{:S(2)}) collective-permute-start(bf16[25,64,128]{2,1,0:T(8,128)(2,1)} %collective-permute-done.9.rest_10_), channel_id=1, source_target_pairs={{0,4},{4,8},{8,12},{12,16},{16,20},{20,24},{24,28},{1,5},{5,9},{9,... | collective-permute-start | bytes 1228808 | tf_op jit(solution)/shard_map/ppermute | solution.py:168
  42.7 0.1 pad_maximum_fusion.1
  42.8 1.9 %collective-permute-start.12 = (bf16[2,25,64,128]{3,2,1,0:T(8,128)(2,1)S(1)}, bf16[2,25,64,128]{3,2,1,0:T(8,128)(2,1)S(1)}, u32[]{:S(2)}, u32[]{:S(2)}) collective-permute-start(bf16[2,25,64,128]{3,2,1,0:T(8,128)(2,1)S(1)} %pad_maximum_fusion.1), channel_id=1, source_target_pairs={{0,3},{1,0},{2,1},{3,2},{4,7},{5,4},{6,5},{7,6},{24,27},{25,24},{2... | collective-permute-start | bytes 2457608 | tf_op jit(solution)/shard_map/ppermute | solution.py:187
  44.7 0.7 slice_bitcast_fusion.9
  45.4 0.7 slice_bitcast_fusion.10
  46.1 2.5 %collective-permute-start.8 = (bf16[2,25,64,128]{3,2,1,0:T(8,128)(2,1)S(1)}, bf16[2,25,64,128]{3,2,1,0:T(8,128)(2,1)S(1)}, u32[]{:S(2)}, u32[]{:S(2)}) collective-permute-start(bf16[2,25,64,128]{3,2,1,0:T(8,128)(2,1)S(1)} %pad_maximum_fusion.1), channel_id=1, source_target_pairs={{0,2},{1,3},{2,0},{3,1},{4,6},{5,7},{6,4},{7,5},{24,26},{25,27},{2... | collective-permute-start | bytes 2457608 | tf_op jit(solution)/shard_map/ppermute | solution.py:187
  48.6 4.3 %collective-permute-start.15 = (bf16[25,64,128]{2,1,0:T(8,128)(2,1)S(1)}, bf16[25,64,128]{2,1,0:T(8,128)(2,1)S(1)}, u32[]{:S(2)}, u32[]{:S(2)}) collective-permute-start(bf16[25,64,128]{2,1,0:T(8,128)(2,1)S(1)} %collective-permute-done.14.rest_7_), channel_id=1, source_target_pairs={{4,8},{8,12},{12,16},{16,20},{20,24},{24,28},{5,9},{9,13},{13,17},... | collective-permute-start | bytes 1228808 | tf_op jit(solution)/shard_map/ppermute | solution.py:168
  52.9 1.3 collective-permute-start.21
  54.2 4.8 %collective-permute-start.4 = (bf16[2,25,64,128]{3,2,1,0:T(8,128)(2,1)S(1)}, bf16[2,25,64,128]{3,2,1,0:T(8,128)(2,1)S(1)}, u32[]{:S(2)}, u32[]{:S(2)}) collective-permute-start(bf16[2,25,64,128]{3,2,1,0:T(8,128)(2,1)S(1)} %pad_maximum_fusion.1), channel_id=1, source_target_pairs={{0,1},{1,2},{2,3},{3,0},{4,5},{5,6},{6,7},{7,4},{24,25},{25,26},{2... | collective-permute-start | bytes 2457608 | tf_op jit(solution)/shard_map/ppermute | solution.py:187
  59.0 1.9 %collective-permute-start.17 = (bf16[25,64,128]{2,1,0:T(8,128)(2,1)}, bf16[25,64,128]{2,1,0:T(8,128)(2,1)S(1)}, u32[]{:S(2)}, u32[]{:S(2)}) collective-permute-start(bf16[25,64,128]{2,1,0:T(8,128)(2,1)} %collective-permute-done.9.rest_10_), channel_id=1, source_target_pairs={{4,0},{8,4},{12,8},{16,12},{20,16},{24,20},{28,24},{5,1},{9,5},{13... | collective-permute-start | bytes 1228808 | tf_op jit(solution)/shard_map/ppermute | solution.py:168
  61.0 2.4 %collective-permute-start.16 = (bf16[25,64,128]{2,1,0:T(8,128)(2,1)}, bf16[25,64,128]{2,1,0:T(8,128)(2,1)S(1)}, u32[]{:S(2)}, u32[]{:S(2)}) collective-permute-start(bf16[25,64,128]{2,1,0:T(8,128)(2,1)} %collective-permute-done.5.rest_9_), channel_id=1, source_target_pairs={{4,0},{8,4},{12,8},{16,12},{20,16},{24,20},{28,24},{5,1},{9,5},{13... | collective-permute-start | bytes 1228808 | tf_op jit(solution)/shard_map/ppermute | solution.py:168
  63.4 1.7 %collective-permute-done.12.rest_22_ = bf16[2,25,64,128]{3,2,1,0:T(8,128)(2,1)S(1)} collective-permute-done((bf16[2,25,64,128]{3,2,1,0:T(8,128)(2,1)S(1)}, bf16[2,25,64,128]{3,2,1,0:T(8,128)(2,1)S(1)}, u32[]{:S(2)}, u32[]{:S(2)}) %collective-permute-start.12) | collective-permute-done | bytes 819232 | tf_op jit(solution)/shard_map/ppermute | solution.py:187
  65.1 5.1 %collective-permute-start.6 = (bf16[25,64,128]{2,1,0:T(8,128)(2,1)}, bf16[25,64,128]{2,1,0:T(8,128)(2,1)S(1)}, u32[]{:S(2)}, u32[]{:S(2)}) collective-permute-start(bf16[25,64,128]{2,1,0:T(8,128)(2,1)} %collective-permute-done.5.rest_9_), channel_id=1, source_target_pairs={{0,4},{4,8},{8,12},{12,16},{16,20},{20,24},{24,28},{1,5},{5,9},{9,... | collective-permute-start | bytes 1228808 | tf_op jit(solution)/shard_map/ppermute | solution.py:168
  70.2 1.9 %collective-permute-start.11 = (bf16[25,64,128]{2,1,0:T(8,128)(2,1)S(1)}, bf16[25,64,128]{2,1,0:T(8,128)(2,1)S(1)}, u32[]{:S(2)}, u32[]{:S(2)}) collective-permute-start(bf16[25,64,128]{2,1,0:T(8,128)(2,1)S(1)} %collective-permute-done.10.rest_6_), channel_id=1, source_target_pairs={{4,8},{8,12},{12,16},{16,20},{20,24},{24,28},{5,9},{9,13},{13,17},... | collective-permute-start | bytes 1228808 | tf_op jit(solution)/shard_map/ppermute | solution.py:168
  72.2 3.7 %collective-permute-start.20 = (bf16[25,64,128]{2,1,0:T(8,128)(2,1)S(1)}, bf16[25,64,128]{2,1,0:T(8,128)(2,1)S(1)}, u32[]{:S(2)}, u32[]{:S(2)}) collective-permute-start(bf16[25,64,128]{2,1,0:T(8,128)(2,1)S(1)} %collective-permute-done.17.rest_14_), channel_id=1, source_target_pairs={{4,0},{8,4},{12,8},{16,12},{20,16},{24,20},{5,1},{9,5},{13,9},{17,... | collective-permute-start | bytes 1228808 | tf_op jit(solution)/shard_map/ppermute | solution.py:168
  75.9 1.9 %collective-permute-start.19 = (bf16[25,64,128]{2,1,0:T(8,128)(2,1)S(1)}, bf16[25,64,128]{2,1,0:T(8,128)(2,1)S(1)}, u32[]{:S(2)}, u32[]{:S(2)}) collective-permute-start(bf16[25,64,128]{2,1,0:T(8,128)(2,1)S(1)} %collective-permute-done.16.rest_13_), channel_id=1, source_target_pairs={{4,0},{8,4},{12,8},{16,12},{20,16},{24,20},{5,1},{9,5},{13,9},{17,... | collective-permute-start | bytes 1228808 | tf_op jit(solution)/shard_map/ppermute | solution.py:168
  77.8 6.4 %collective-permute-done.8.rest_21_ = bf16[2,25,64,128]{3,2,1,0:T(8,128)(2,1)S(1)} collective-permute-done((bf16[2,25,64,128]{3,2,1,0:T(8,128)(2,1)S(1)}, bf16[2,25,64,128]{3,2,1,0:T(8,128)(2,1)S(1)}, u32[]{:S(2)}, u32[]{:S(2)}) %collective-permute-start.8) | collective-permute-done | bytes 819232 | tf_op jit(solution)/shard_map/ppermute | solution.py:187
  84.2 2.0 %collective-permute-start.7 = (bf16[25,64,128]{2,1,0:T(8,128)(2,1)S(1)}, bf16[25,64,128]{2,1,0:T(8,128)(2,1)S(1)}, u32[]{:S(2)}, u32[]{:S(2)}) collective-permute-start(bf16[25,64,128]{2,1,0:T(8,128)(2,1)S(1)} %collective-permute-done.6.rest_5_), channel_id=1, source_target_pairs={{4,8},{8,12},{12,16},{16,20},{20,24},{24,28},{5,9},{9,13},{13,17},... | collective-permute-start | bytes 1228808 | tf_op jit(solution)/shard_map/ppermute | solution.py:168
  86.3 7.1 %collective-permute-done.7.rest_1_ = bf16[25,64,128]{2,1,0:T(8,128)(2,1)S(1)} collective-permute-done((bf16[25,64,128]{2,1,0:T(8,128)(2,1)S(1)}, bf16[25,64,128]{2,1,0:T(8,128)(2,1)S(1)}, u32[]{:S(2)}, u32[]{:S(2)}) %collective-permute-start.7) | collective-permute-done | bytes 409632 | tf_op jit(solution)/shard_map/ppermute | solution.py:168
  93.5 0.7 copy-done.19
  94.2 0.1 stack.54
  94.3 0.1 reshape.806
  94.4 3.2 %gather_fusion = s32[768]{0:T(1024)S(1)} fusion(s32[960]{0:T(1024)S(1)} %reshape.806, s32[1024]{0:T(1024)S(1)} %pad_clamp_fusion.1), kind=kCustom, calls=%fused_computation | custom fusion | bytes 9216 | tf_op jit(solution)/shard_map/jit(_take)/gather | solution.py:222
  97.6 1.2 gather_fusion.1
  98.8 0.1 broadcast_in_dim.32
  98.9 0.1 reshape.740
  99.0 0.6 multiply_add_fusion
  99.7 0.6 fusion.11.pair_ref
  100.3 26.1 %shard_map.55 = f32[64,64,128]{2,1,0:T(8,128)} custom-call(s32[768]{0:T(1024)} %fusion.11.pair_ref, s32[768]{0:T(1024)} %get-tuple-element.45.half_ref, s32[768]{0:T(1024)} %get-tuple-element.29.target_ref, s32[768]{0:T(1024)} %reshape.807.live_ref, s32[192]{0:T(256)} %fusion.32.own_pos_ref, s32[5]{0:T(128)} %stack.59.fix_ref, ...), custom_call_target="tpu_custom_call" | custom-call | tf_op jit(solution)/shard_map/pallas_call | solution.py:106
  126.4 1.6 %bitcast_convert_fusion.2 = (bf16[8,2,64,128]{3,2,1,0:T(8,128)(2,1)S(1)}, bf16[8,2,64,128]{3,2,1,0:T(8,128)(2,1)S(1)}, bf16[8,2,64,128]{3,2,1,0:T(8,128)(2,1)S(1)}) fusion(f32[4,8,2,64,128]{4,3,2,1,0:T(8,128)} %bitcast.141, s32[]{:T(128)S(6)} %select_n.678, pred[]{:T(512)S(6)} %and.252, s32[]{:T(128)S(6)} %select_n.682, pred[]{:T(512)S(6)} %and.254, ...), kind=kLoop, calls=%fused_computation.9 | loop fusion | flops 393216 | bytes 1572879 | tf_op jit(solution)/shard_map/convert_element_type | solution.py:250
  127.9 4.0 %collective-permute-start.22 = (bf16[8,2,64,128]{3,2,1,0:T(8,128)(2,1)S(1)}, bf16[8,2,64,128]{3,2,1,0:T(8,128)(2,1)S(1)}, u32[]{:S(2)}, u32[]{:S(2)}) collective-permute-start(bf16[8,2,64,128]{3,2,1,0:T(8,128)(2,1)S(1)} %get-tuple-element.31), channel_id=1, source_target_pairs={{0,1},{1,2},{2,3},{3,0},{4,5},{5,6},{6,7},{7,4},{8,9},{9,10},{10,1... | collective-permute-start | bytes 786440 | tf_op jit(solution)/shard_map/ppermute | solution.py:249
  132.0 0.5 collective-permute-start.23
  132.5 0.1 collective-permute-start.24
  132.6 4.1 %collective-permute-done.22 = bf16[8,2,64,128]{3,2,1,0:T(8,128)(2,1)S(1)} collective-permute-done((bf16[8,2,64,128]{3,2,1,0:T(8,128)(2,1)S(1)}, bf16[8,2,64,128]{3,2,1,0:T(8,128)(2,1)S(1)}, u32[]{:S(2)}, u32[]{:S(2)}) %collective-permute-start.22) | collective-permute-done | bytes 262176 | tf_op jit(solution)/shard_map/ppermute | solution.py:249
  136.7 4.4 %collective-permute-done.23 = bf16[8,2,64,128]{3,2,1,0:T(8,128)(2,1)S(1)} collective-permute-done((bf16[8,2,64,128]{3,2,1,0:T(8,128)(2,1)S(1)}, bf16[8,2,64,128]{3,2,1,0:T(8,128)(2,1)S(1)}, u32[]{:S(2)}, u32[]{:S(2)}) %collective-permute-start.23) | collective-permute-done | bytes 262176 | tf_op jit(solution)/shard_map/ppermute | solution.py:249
  141.1 1.2 fusion.2
  142.3 0.2 fusion.46
  142.5 1.1 pad_maximum_fusion
  (86 shorter events, 0.5 us)
Async XLA Ops:
  0.0 9.3 %copy-start.20 = (s32[192,4]{0,1:T(4,128)S(1)}, s32[192,4]{0,1:T(4,128)}, u32[]{:S(2)}) copy-start(s32[192,4]{0,1:T(4,128)} %param.10) | copy-start | bytes 9220
  0.7 9.9 %copy-start.21 = (s32[192]{0:T(256)S(1)}, s32[192]{0:T(256)}, u32[]{:S(2)}) copy-start(s32[192]{0:T(256)} %param.11) | copy-start | bytes 2308
  3.0 25.3 %copy-start.4 = (bf16[25,64,128]{2,1,0:T(8,128)(2,1)}, bf16[25,64,128]{2,1,0:T(8,128)(2,1)S(1)}, u32[]{:S(2)}) copy-start(bf16[25,64,128]{2,1,0:T(8,128)(2,1)S(1)} %fusion.3.rest_8_) | copy-start | bytes 1228804
  3.0 26.5 %collective-permute-start = (bf16[25,64,128]{2,1,0:T(8,128)(2,1)S(1)}, bf16[25,64,128]{2,1,0:T(8,128)(2,1)S(1)}, u32[]{:S(2)}, u32[]{:S(2)}) collective-permute-start(bf16[25,64,128]{2,1,0:T(8,128)(2,1)S(1)} %fusion.3.rest_8_), channel_id=1, source_target_pairs={{28,0},{0,4},{4,8},{8,12},{12,16},{16,20},{20,24},{24,28},{29,1},{... | collective-permute-start | bytes 1228808 | tf_op jit(solution)/shard_map/ppermute | solution.py:168
  3.1 26.5 %collective-permute-start.2 = (bf16[25,64,128]{2,1,0:T(8,128)(2,1)S(1)}, bf16[25,64,128]{2,1,0:T(8,128)(2,1)S(1)}, u32[]{:S(2)}, u32[]{:S(2)}) collective-permute-start(bf16[25,64,128]{2,1,0:T(8,128)(2,1)S(1)} %fusion.3.rest_8_), channel_id=1, source_target_pairs={{4,0},{8,4},{12,8},{16,12},{20,16},{24,20},{28,24},{0,28},{5,1},{9... | collective-permute-start | bytes 1228808 | tf_op jit(solution)/shard_map/ppermute | solution.py:168
  4.8 26.6 %collective-permute-start.13 = (bf16[25,64,128]{2,1,0:T(8,128)(2,1)S(1)}, bf16[25,64,128]{2,1,0:T(8,128)(2,1)}, u32[]{:S(2)}, u32[]{:S(2)}) collective-permute-start(bf16[25,64,128]{2,1,0:T(8,128)(2,1)S(1)} %fusion.3.rest_8_), channel_id=1, source_target_pairs={{0,3},{1,0},{2,1},{3,2},{4,7},{5,4},{6,5},{7,6},{8,11},{9,8},{10,9... | collective-permute-start | bytes 1228808 | tf_op jit(solution)/shard_map/ppermute | solution.py:156
  5.4 29.1 %collective-permute-start.9 = (bf16[25,64,128]{2,1,0:T(8,128)(2,1)S(1)}, bf16[25,64,128]{2,1,0:T(8,128)(2,1)}, u32[]{:S(2)}, u32[]{:S(2)}) collective-permute-start(bf16[25,64,128]{2,1,0:T(8,128)(2,1)S(1)} %fusion.3.rest_8_), channel_id=1, source_target_pairs={{0,2},{1,3},{2,0},{3,1},{4,6},{5,7},{6,4},{7,5},{8,10},{9,11},{10,... | collective-permute-start | bytes 1228808 | tf_op jit(solution)/shard_map/ppermute | solution.py:156
  6.9 38.5 %collective-permute-start.5 = (bf16[25,64,128]{2,1,0:T(8,128)(2,1)S(1)}, bf16[25,64,128]{2,1,0:T(8,128)(2,1)}, u32[]{:S(2)}, u32[]{:S(2)}) collective-permute-start(bf16[25,64,128]{2,1,0:T(8,128)(2,1)S(1)} %fusion.3.rest_8_), channel_id=1, source_target_pairs={{0,1},{1,2},{2,3},{3,0},{4,5},{5,6},{6,7},{7,4},{8,9},{9,10},{10,1... | collective-permute-start | bytes 1228808 | tf_op jit(solution)/shard_map/ppermute | solution.py:156
  29.6 64.7 %copy-start = (bf16[25,64,128]{2,1,0:T(8,128)(2,1)}, bf16[25,64,128]{2,1,0:T(8,128)(2,1)S(1)}, u32[]{:S(2)}) copy-start(bf16[25,64,128]{2,1,0:T(8,128)(2,1)S(1)} %collective-permute-done.rest_4_) | copy-start | bytes 1228804
  29.6 8.1 %collective-permute-start.1 = (bf16[25,64,128]{2,1,0:T(8,128)(2,1)S(1)}, bf16[25,64,128]{2,1,0:T(8,128)(2,1)S(1)}, u32[]{:S(2)}, u32[]{:S(2)}) collective-permute-start(bf16[25,64,128]{2,1,0:T(8,128)(2,1)S(1)} %collective-permute-done.rest_4_), channel_id=1, source_target_pairs={{28,0},{0,4},{4,8},{8,12},{12,16},{16,20},{20,24},{24,28},{29,1},{... | collective-permute-start | bytes 1228808 | tf_op jit(solution)/shard_map/ppermute | solution.py:168
  29.7 64.7 %copy-start.1 = (bf16[25,64,128]{2,1,0:T(8,128)(2,1)}, bf16[25,64,128]{2,1,0:T(8,128)(2,1)S(1)}, u32[]{:S(2)}) copy-start(bf16[25,64,128]{2,1,0:T(8,128)(2,1)S(1)} %collective-permute-done.2.rest_12_) | copy-start | bytes 1228804
  29.7 13.0 %collective-permute-start.3 = (bf16[25,64,128]{2,1,0:T(8,128)(2,1)S(1)}, bf16[25,64,128]{2,1,0:T(8,128)(2,1)S(1)}, u32[]{:S(2)}, u32[]{:S(2)}) collective-permute-start(bf16[25,64,128]{2,1,0:T(8,128)(2,1)S(1)} %collective-permute-done.2.rest_12_), channel_id=1, source_target_pairs={{4,0},{8,4},{12,8},{16,12},{20,16},{24,20},{28,24},{0,28},{5,1},{9... | collective-permute-start | bytes 1228808 | tf_op jit(solution)/shard_map/ppermute | solution.py:168
  31.4 17.2 %collective-permute-start.14 = (bf16[25,64,128]{2,1,0:T(8,128)(2,1)}, bf16[25,64,128]{2,1,0:T(8,128)(2,1)S(1)}, u32[]{:S(2)}, u32[]{:S(2)}) collective-permute-start(bf16[25,64,128]{2,1,0:T(8,128)(2,1)} %collective-permute-done.13.rest_11_), channel_id=1, source_target_pairs={{0,4},{4,8},{8,12},{12,16},{16,20},{20,24},{24,28},{1,5},{5,9},{9,... | collective-permute-start | bytes 1228808 | tf_op jit(solution)/shard_map/ppermute | solution.py:168
  34.4 18.4 %collective-permute-start.18 = (bf16[25,64,128]{2,1,0:T(8,128)(2,1)}, bf16[25,64,128]{2,1,0:T(8,128)(2,1)S(1)}, u32[]{:S(2)}, u32[]{:S(2)}) collective-permute-start(bf16[25,64,128]{2,1,0:T(8,128)(2,1)} %collective-permute-done.13.rest_11_), channel_id=1, source_target_pairs={{4,0},{8,4},{12,8},{16,12},{20,16},{24,20},{28,24},{5,1},{9,5},{13... | collective-permute-start | bytes 1228808 | tf_op jit(solution)/shard_map/ppermute | solution.py:168
  37.7 59.9 %copy-start.2 = (bf16[25,64,128]{2,1,0:T(8,128)(2,1)}, bf16[25,64,128]{2,1,0:T(8,128)(2,1)S(1)}, u32[]{:S(2)}) copy-start(bf16[25,64,128]{2,1,0:T(8,128)(2,1)S(1)} %collective-permute-done.1.rest_0_) | copy-start | bytes 1228804
  37.7 16.5 %collective-permute-start.10 = (bf16[25,64,128]{2,1,0:T(8,128)(2,1)}, bf16[25,64,128]{2,1,0:T(8,128)(2,1)S(1)}, u32[]{:S(2)}, u32[]{:S(2)}) collective-permute-start(bf16[25,64,128]{2,1,0:T(8,128)(2,1)} %collective-permute-done.9.rest_10_), channel_id=1, source_target_pairs={{0,4},{4,8},{8,12},{12,16},{16,20},{20,24},{24,28},{1,5},{5,9},{9,... | collective-permute-start | bytes 1228808 | tf_op jit(solution)/shard_map/ppermute | solution.py:168
  42.7 54.9 %copy-start.3 = (bf16[25,64,128]{2,1,0:T(8,128)(2,1)}, bf16[25,64,128]{2,1,0:T(8,128)(2,1)S(1)}, u32[]{:S(2)}) copy-start(bf16[25,64,128]{2,1,0:T(8,128)(2,1)S(1)} %collective-permute-done.3.rest_16_) | copy-start | bytes 1228804
  42.8 22.3 %collective-permute-start.12 = (bf16[2,25,64,128]{3,2,1,0:T(8,128)(2,1)S(1)}, bf16[2,25,64,128]{3,2,1,0:T(8,128)(2,1)S(1)}, u32[]{:S(2)}, u32[]{:S(2)}) collective-permute-start(bf16[2,25,64,128]{3,2,1,0:T(8,128)(2,1)S(1)} %pad_maximum_fusion.1), channel_id=1, source_target_pairs={{0,3},{1,0},{2,1},{3,2},{4,7},{5,4},{6,5},{7,6},{24,27},{25,24},{2... | collective-permute-start | bytes 2457608 | tf_op jit(solution)/shard_map/ppermute | solution.py:187
  46.1 38.1 %collective-permute-start.8 = (bf16[2,25,64,128]{3,2,1,0:T(8,128)(2,1)S(1)}, bf16[2,25,64,128]{3,2,1,0:T(8,128)(2,1)S(1)}, u32[]{:S(2)}, u32[]{:S(2)}) collective-permute-start(bf16[2,25,64,128]{3,2,1,0:T(8,128)(2,1)S(1)} %pad_maximum_fusion.1), channel_id=1, source_target_pairs={{0,2},{1,3},{2,0},{3,1},{4,6},{5,7},{6,4},{7,5},{24,26},{25,27},{2... | collective-permute-start | bytes 2457608 | tf_op jit(solution)/shard_map/ppermute | solution.py:187
  48.6 51.7 %copy-start.8 = (bf16[25,64,128]{2,1,0:T(8,128)(2,1)}, bf16[25,64,128]{2,1,0:T(8,128)(2,1)S(1)}, u32[]{:S(2)}) copy-start(bf16[25,64,128]{2,1,0:T(8,128)(2,1)S(1)} %collective-permute-done.14.rest_7_) | copy-start | bytes 1228804
  48.6 10.4 %collective-permute-start.15 = (bf16[25,64,128]{2,1,0:T(8,128)(2,1)S(1)}, bf16[25,64,128]{2,1,0:T(8,128)(2,1)S(1)}, u32[]{:S(2)}, u32[]{:S(2)}) collective-permute-start(bf16[25,64,128]{2,1,0:T(8,128)(2,1)S(1)} %collective-permute-done.14.rest_7_), channel_id=1, source_target_pairs={{4,8},{8,12},{12,16},{16,20},{20,24},{24,28},{5,9},{9,13},{13,17},... | collective-permute-start | bytes 1228808 | tf_op jit(solution)/shard_map/ppermute | solution.py:168
  52.9 40.6 %copy-start.9 = (bf16[25,64,128]{2,1,0:T(8,128)(2,1)}, bf16[25,64,128]{2,1,0:T(8,128)(2,1)S(1)}, u32[]{:S(2)}) copy-start(bf16[25,64,128]{2,1,0:T(8,128)(2,1)S(1)} %collective-permute-done.18.rest_15_) | copy-start | bytes 1228804
  52.9 8.1 %collective-permute-start.21 = (bf16[25,64,128]{2,1,0:T(8,128)(2,1)S(1)}, bf16[25,64,128]{2,1,0:T(8,128)(2,1)S(1)}, u32[]{:S(2)}, u32[]{:S(2)}) collective-permute-start(bf16[25,64,128]{2,1,0:T(8,128)(2,1)S(1)} %collective-permute-done.18.rest_15_), channel_id=1, source_target_pairs={{4,0},{8,4},{12,8},{16,12},{20,16},{24,20},{5,1},{9,5},{13,9},{17,... | collective-permute-start | bytes 1228808 | tf_op jit(solution)/shard_map/ppermute | solution.py:168
  54.2 39.2 %copy-start.10 = (bf16[25,64,128]{2,1,0:T(8,128)(2,1)}, bf16[25,64,128]{2,1,0:T(8,128)(2,1)S(1)}, u32[]{:S(2)}) copy-start(bf16[25,64,128]{2,1,0:T(8,128)(2,1)S(1)} %collective-permute-done.10.rest_6_) | copy-start | bytes 1228804
  54.2 32.0 %collective-permute-start.4 = (bf16[2,25,64,128]{3,2,1,0:T(8,128)(2,1)S(1)}, bf16[2,25,64,128]{3,2,1,0:T(8,128)(2,1)S(1)}, u32[]{:S(2)}, u32[]{:S(2)}) collective-permute-start(bf16[2,25,64,128]{3,2,1,0:T(8,128)(2,1)S(1)} %pad_maximum_fusion.1), channel_id=1, source_target_pairs={{0,1},{1,2},{2,3},{3,0},{4,5},{5,6},{6,7},{7,4},{24,25},{25,26},{2... | collective-permute-start | bytes 2457608 | tf_op jit(solution)/shard_map/ppermute | solution.py:187
  59.0 41.2 %copy-start.11 = (bf16[25,64,128]{2,1,0:T(8,128)(2,1)}, bf16[25,64,128]{2,1,0:T(8,128)(2,1)S(1)}, u32[]{:S(2)}) copy-start(bf16[25,64,128]{2,1,0:T(8,128)(2,1)S(1)} %collective-permute-done.15.rest_3_) | copy-start | bytes 1228804
  59.0 11.2 %collective-permute-start.17 = (bf16[25,64,128]{2,1,0:T(8,128)(2,1)}, bf16[25,64,128]{2,1,0:T(8,128)(2,1)S(1)}, u32[]{:S(2)}, u32[]{:S(2)}) collective-permute-start(bf16[25,64,128]{2,1,0:T(8,128)(2,1)} %collective-permute-done.9.rest_10_), channel_id=1, source_target_pairs={{4,0},{8,4},{12,8},{16,12},{20,16},{24,20},{28,24},{5,1},{9,5},{13... | collective-permute-start | bytes 1228808 | tf_op jit(solution)/shard_map/ppermute | solution.py:168
  61.0 32.5 %copy-start.12 = (bf16[25,64,128]{2,1,0:T(8,128)(2,1)}, bf16[25,64,128]{2,1,0:T(8,128)(2,1)S(1)}, u32[]{:S(2)}) copy-start(bf16[25,64,128]{2,1,0:T(8,128)(2,1)S(1)} %collective-permute-done.21.rest_19_) | copy-start | bytes 1228804
  61.0 11.2 %collective-permute-start.16 = (bf16[25,64,128]{2,1,0:T(8,128)(2,1)}, bf16[25,64,128]{2,1,0:T(8,128)(2,1)S(1)}, u32[]{:S(2)}, u32[]{:S(2)}) collective-permute-start(bf16[25,64,128]{2,1,0:T(8,128)(2,1)} %collective-permute-done.5.rest_9_), channel_id=1, source_target_pairs={{4,0},{8,4},{12,8},{16,12},{20,16},{24,20},{28,24},{5,1},{9,5},{13... | collective-permute-start | bytes 1228808 | tf_op jit(solution)/shard_map/ppermute | solution.py:168
  65.1 32.5 %copy-start.5 = (bf16[2,25,64,128]{3,2,1,0:T(8,128)(2,1)}, bf16[2,25,64,128]{3,2,1,0:T(8,128)(2,1)S(1)}, u32[]{:S(2)}) copy-start(bf16[2,25,64,128]{3,2,1,0:T(8,128)(2,1)S(1)} %collective-permute-done.12.rest_22_) | copy-start | bytes 2457604
  65.1 10.8 %collective-permute-start.6 = (bf16[25,64,128]{2,1,0:T(8,128)(2,1)}, bf16[25,64,128]{2,1,0:T(8,128)(2,1)S(1)}, u32[]{:S(2)}, u32[]{:S(2)}) collective-permute-start(bf16[25,64,128]{2,1,0:T(8,128)(2,1)} %collective-permute-done.5.rest_9_), channel_id=1, source_target_pairs={{0,4},{4,8},{8,12},{12,16},{16,20},{20,24},{24,28},{1,5},{5,9},{9,... | collective-permute-start | bytes 1228808 | tf_op jit(solution)/shard_map/ppermute | solution.py:168
  70.2 23.3 %copy-start.13 = (bf16[25,64,128]{2,1,0:T(8,128)(2,1)}, bf16[25,64,128]{2,1,0:T(8,128)(2,1)S(1)}, u32[]{:S(2)}) copy-start(bf16[25,64,128]{2,1,0:T(8,128)(2,1)S(1)} %collective-permute-done.17.rest_14_) | copy-start | bytes 1228804
  70.2 16.0 %collective-permute-start.11 = (bf16[25,64,128]{2,1,0:T(8,128)(2,1)S(1)}, bf16[25,64,128]{2,1,0:T(8,128)(2,1)S(1)}, u32[]{:S(2)}, u32[]{:S(2)}) collective-permute-start(bf16[25,64,128]{2,1,0:T(8,128)(2,1)S(1)} %collective-permute-done.10.rest_6_), channel_id=1, source_target_pairs={{4,8},{8,12},{12,16},{16,20},{20,24},{24,28},{5,9},{9,13},{13,17},... | collective-permute-start | bytes 1228808 | tf_op jit(solution)/shard_map/ppermute | solution.py:168
  72.2 21.3 %copy-start.14 = (bf16[25,64,128]{2,1,0:T(8,128)(2,1)}, bf16[25,64,128]{2,1,0:T(8,128)(2,1)S(1)}, u32[]{:S(2)}) copy-start(bf16[25,64,128]{2,1,0:T(8,128)(2,1)S(1)} %collective-permute-done.16.rest_13_) | copy-start | bytes 1228804
  72.2 14.1 %collective-permute-start.20 = (bf16[25,64,128]{2,1,0:T(8,128)(2,1)S(1)}, bf16[25,64,128]{2,1,0:T(8,128)(2,1)S(1)}, u32[]{:S(2)}, u32[]{:S(2)}) collective-permute-start(bf16[25,64,128]{2,1,0:T(8,128)(2,1)S(1)} %collective-permute-done.17.rest_14_), channel_id=1, source_target_pairs={{4,0},{8,4},{12,8},{16,12},{20,16},{24,20},{5,1},{9,5},{13,9},{17,... | collective-permute-start | bytes 1228808 | tf_op jit(solution)/shard_map/ppermute | solution.py:168
  75.9 17.6 %copy-start.15 = (bf16[25,64,128]{2,1,0:T(8,128)(2,1)}, bf16[25,64,128]{2,1,0:T(8,128)(2,1)S(1)}, u32[]{:S(2)}) copy-start(bf16[25,64,128]{2,1,0:T(8,128)(2,1)S(1)} %collective-permute-done.6.rest_5_) | copy-start | bytes 1228804
  75.9 10.4 %collective-permute-start.19 = (bf16[25,64,128]{2,1,0:T(8,128)(2,1)S(1)}, bf16[25,64,128]{2,1,0:T(8,128)(2,1)S(1)}, u32[]{:S(2)}, u32[]{:S(2)}) collective-permute-start(bf16[25,64,128]{2,1,0:T(8,128)(2,1)S(1)} %collective-permute-done.16.rest_13_), channel_id=1, source_target_pairs={{4,0},{8,4},{12,8},{16,12},{20,16},{24,20},{5,1},{9,5},{13,9},{17,... | collective-permute-start | bytes 1228808 | tf_op jit(solution)/shard_map/ppermute | solution.py:168
  84.2 2.1 %copy-start.6 = (bf16[2,25,64,128]{3,2,1,0:T(8,128)(2,1)}, bf16[2,25,64,128]{3,2,1,0:T(8,128)(2,1)S(1)}, u32[]{:S(2)}) copy-start(bf16[2,25,64,128]{3,2,1,0:T(8,128)(2,1)S(1)} %collective-permute-done.8.rest_21_) | copy-start | bytes 2457604
  84.2 9.3 %collective-permute-start.7 = (bf16[25,64,128]{2,1,0:T(8,128)(2,1)S(1)}, bf16[25,64,128]{2,1,0:T(8,128)(2,1)S(1)}, u32[]{:S(2)}, u32[]{:S(2)}) collective-permute-start(bf16[25,64,128]{2,1,0:T(8,128)(2,1)S(1)} %collective-permute-done.6.rest_5_), channel_id=1, source_target_pairs={{4,8},{8,12},{12,16},{16,20},{20,24},{24,28},{5,9},{9,13},{13,17},... | collective-permute-start | bytes 1228808 | tf_op jit(solution)/shard_map/ppermute | solution.py:168
  86.2 7.2 %copy-start.7 = (bf16[2,25,64,128]{3,2,1,0:T(8,128)(2,1)}, bf16[2,25,64,128]{3,2,1,0:T(8,128)(2,1)S(1)}, u32[]{:S(2)}) copy-start(bf16[2,25,64,128]{3,2,1,0:T(8,128)(2,1)S(1)} %collective-permute-done.4.rest_20_) | copy-start | bytes 2457604
  86.3 7.3 %copy-start.16 = (bf16[25,64,128]{2,1,0:T(8,128)(2,1)}, bf16[25,64,128]{2,1,0:T(8,128)(2,1)S(1)}, u32[]{:S(2)}) copy-start(bf16[25,64,128]{2,1,0:T(8,128)(2,1)S(1)} %collective-permute-done.11.rest_2_) | copy-start | bytes 1228804
  86.3 7.2 %copy-start.17 = (bf16[25,64,128]{2,1,0:T(8,128)(2,1)}, bf16[25,64,128]{2,1,0:T(8,128)(2,1)S(1)}, u32[]{:S(2)}) copy-start(bf16[25,64,128]{2,1,0:T(8,128)(2,1)S(1)} %collective-permute-done.20.rest_18_) | copy-start | bytes 1228804
  86.3 7.2 %copy-start.18 = (bf16[25,64,128]{2,1,0:T(8,128)(2,1)}, bf16[25,64,128]{2,1,0:T(8,128)(2,1)S(1)}, u32[]{:S(2)}) copy-start(bf16[25,64,128]{2,1,0:T(8,128)(2,1)S(1)} %collective-permute-done.19.rest_17_) | copy-start | bytes 1228804
  93.4 0.8 copy-start.19
  127.9 8.8 %collective-permute-start.22 = (bf16[8,2,64,128]{3,2,1,0:T(8,128)(2,1)S(1)}, bf16[8,2,64,128]{3,2,1,0:T(8,128)(2,1)S(1)}, u32[]{:S(2)}, u32[]{:S(2)}) collective-permute-start(bf16[8,2,64,128]{3,2,1,0:T(8,128)(2,1)S(1)} %get-tuple-element.31), channel_id=1, source_target_pairs={{0,1},{1,2},{2,3},{3,0},{4,5},{5,6},{6,7},{7,4},{8,9},{9,10},{10,1... | collective-permute-start | bytes 786440 | tf_op jit(solution)/shard_map/ppermute | solution.py:249
  132.0 9.2 %collective-permute-start.23 = (bf16[8,2,64,128]{3,2,1,0:T(8,128)(2,1)S(1)}, bf16[8,2,64,128]{3,2,1,0:T(8,128)(2,1)S(1)}, u32[]{:S(2)}, u32[]{:S(2)}) collective-permute-start(bf16[8,2,64,128]{3,2,1,0:T(8,128)(2,1)S(1)} %get-tuple-element.33), channel_id=1, source_target_pairs={{0,2},{1,3},{2,0},{3,1},{4,6},{5,7},{6,4},{7,5},{8,10},{9,11},{10,... | collective-permute-start | bytes 786440 | tf_op jit(solution)/shard_map/ppermute | solution.py:249
  132.5 8.7 %collective-permute-start.24 = (bf16[8,2,64,128]{3,2,1,0:T(8,128)(2,1)S(1)}, bf16[8,2,64,128]{3,2,1,0:T(8,128)(2,1)S(1)}, u32[]{:S(2)}, u32[]{:S(2)}) collective-permute-start(bf16[8,2,64,128]{3,2,1,0:T(8,128)(2,1)S(1)} %get-tuple-element.32), channel_id=1, source_target_pairs={{0,3},{1,0},{2,1},{3,2},{4,7},{5,4},{6,5},{7,6},{8,11},{9,8},{10,9... | collective-permute-start | bytes 786440 | tf_op jit(solution)/shard_map/ppermute | solution.py:249

commit v14 on v13

--- a/solution.py
+++ b/solution.py
@@ -83,7 +83,7 @@
             acc_ref[t] = acc_ref[t] + results[s]
         return carry
 
-    lax.fori_loop(0, rows_here, row_body, 0, unroll=8)
+    lax.fori_loop(0, rows_here, row_body, 0, unroll=16)
 
     @pl.when(step == pl.num_programs(0) - 1)
     def _():

time: 145 us -> 142 us (0.979)
  Pallas kernels: 26.1 us -> 23 us
    pallas_call x1, Pallas kernels: 26.1 us -> 23 us  [coarse_partial(): pl.pallas_call(coarse_kernel, out_shape=jax.ShapeDtypeStruct((n_targets /...]
where the time goes in v14:
time: 142 us; the launch traced here: 141 us
  starting transfers between devices  56.8 us (40%)
  local copies, waits for them, and re-layouts  29.3 us (21%)
  waiting for transfers between devices  23.7 us (17%)
  Pallas kernels  23 us (16%)
  other arithmetic  6.78 us (5%)
    ppermute x16, starting transfers between devices, ring(): return lax.ppermute(piece, 'blk', route)  38.6 us
    pallas_call x1, Pallas kernels, coarse_partial(): pl.pallas_call(coarse_kernel, out_shape=jax.ShapeDtypeStruct((n_targets /...  23 us
    unnamed x45, local copies, waits for them, and re-layouts  17.7 us
    ppermute x3, starting transfers between devices, local(): fixed.append(lax.ppermute(fix_src, ('blk', 'grp'), route))  9.14 us
    ppermute x3, waiting for transfers between devices, local(): lax.ppermute(outgoing.astype(jnp.bfloat16), 'grp', [(i, (i + k) % group_s...  8.54 us
    ppermute x3, waiting for transfers between devices, local(): fixed.append(lax.ppermute(fix_src, ('blk', 'grp'), route))  8.03 us
    ppermute x16, waiting for transfers between devices, ring(): return lax.ppermute(piece, 'blk', route)  7.14 us
    ppermute x3, starting transfers between devices, local(): lax.ppermute(outgoing.astype(jnp.bfloat16), 'grp', [(i, (i + k) % group_s...  4.66 us
  transfers between devices with their start and end apart: 25, of which 5 were waited for; matrix products, arithmetic and copies ran while one was open for 16% of the time, Pallas kernels for 0%

profile of v14, /device:TPU:26, one launch (start us, length us, event | category | flops | bytes accessed | tf_op | source)
XLA Modules:
  0.0 140.5 jit_solution(3437958878880744323)
XLA Ops:
  0.0 0.7 convert_bitcast_fusion
  0.7 2.0 %copy.17 = bf16[24,2,64,64]{3,1,2,0:T(2,128)(2,1)S(1)} copy(bf16[24,2,64,64]{3,2,1,0:T(8,128)(2,1)} %bitcast.144) | data formatting | bytes 786432 | tf_op jit(solution)/shard_map/reshape | solution.py:142
  2.6 0.3 reshape.739
  3.1 1.7 %collective-permute-start.2 = (bf16[25,64,128]{2,1,0:T(8,128)(2,1)S(1)}, bf16[25,64,128]{2,1,0:T(8,128)(2,1)S(1)}, u32[]{:S(2)}, u32[]{:S(2)}) collective-permute-start(bf16[25,64,128]{2,1,0:T(8,128)(2,1)S(1)} %fusion.3.rest_8_), channel_id=1, source_target_pairs={{4,0},{8,4},{12,8},{16,12},{20,16},{24,20},{28,24},{0,28},{5,1},{9... | collective-permute-start | bytes 1228808 | tf_op jit(solution)/shard_map/ppermute | solution.py:168
  4.8 0.5 collective-permute-start.13
  5.4 1.5 %collective-permute-start.9 = (bf16[25,64,128]{2,1,0:T(8,128)(2,1)S(1)}, bf16[25,64,128]{2,1,0:T(8,128)(2,1)}, u32[]{:S(2)}, u32[]{:S(2)}) collective-permute-start(bf16[25,64,128]{2,1,0:T(8,128)(2,1)S(1)} %fusion.3.rest_8_), channel_id=1, source_target_pairs={{0,2},{1,3},{2,0},{3,1},{4,6},{5,7},{6,4},{7,5},{8,10},{9,11},{10,... | collective-permute-start | bytes 1228808 | tf_op jit(solution)/shard_map/ppermute | solution.py:156
  6.9 2.4 %collective-permute-start.5 = (bf16[25,64,128]{2,1,0:T(8,128)(2,1)S(1)}, bf16[25,64,128]{2,1,0:T(8,128)(2,1)}, u32[]{:S(2)}, u32[]{:S(2)}) collective-permute-start(bf16[25,64,128]{2,1,0:T(8,128)(2,1)S(1)} %fusion.3.rest_8_), channel_id=1, source_target_pairs={{0,1},{1,2},{2,3},{3,0},{4,5},{5,6},{6,7},{7,4},{8,9},{9,10},{10,1... | collective-permute-start | bytes 1228808 | tf_op jit(solution)/shard_map/ppermute | solution.py:156
  9.3 0.1 copy.9
  9.4 0.1 rem.301
  9.6 0.1 rem.276
  9.7 0.1 copy.10
  9.8 0.1 div.78
  9.9 0.1 div.73
  10.0 0.2 copy.8
  10.2 0.1 ne.313
  10.3 0.1 ne.303
  10.5 0.1 compare_convert_fusion
  10.6 0.7 reshape.807.live_ref
  11.3 17.0 %copy.15.values_ref = bf16[192,4,64,64]{3,2,1,0:T(8,128)(2,1)} copy(bf16[192,4,64,64]{0,3,2,1:T(8,128)(2,1)} %param.9) | data formatting | bytes 12582912 | tf_op args[0]
  28.3 0.6 stack.59.fix_ref
  28.9 0.6 fusion.32.own_pos_ref
  29.5 0.1 fusion.16
  29.7 1.7 %collective-permute-start.3 = (bf16[25,64,128]{2,1,0:T(8,128)(2,1)S(1)}, bf16[25,64,128]{2,1,0:T(8,128)(2,1)S(1)}, u32[]{:S(2)}, u32[]{:S(2)}) collective-permute-start(bf16[25,64,128]{2,1,0:T(8,128)(2,1)S(1)} %collective-permute-done.2.rest_12_), channel_id=1, source_target_pairs={{4,0},{8,4},{12,8},{16,12},{20,16},{24,20},{28,24},{0,28},{5,1},{9... | collective-permute-start | bytes 1228808 | tf_op jit(solution)/shard_map/ppermute | solution.py:168
  31.4 2.3 %collective-permute-start.14 = (bf16[25,64,128]{2,1,0:T(8,128)(2,1)}, bf16[25,64,128]{2,1,0:T(8,128)(2,1)S(1)}, u32[]{:S(2)}, u32[]{:S(2)}) collective-permute-start(bf16[25,64,128]{2,1,0:T(8,128)(2,1)} %collective-permute-done.13.rest_11_), channel_id=1, source_target_pairs={{0,4},{4,8},{8,12},{12,16},{16,20},{20,24},{24,28},{1,5},{5,9},{9,... | collective-permute-start | bytes 1228808 | tf_op jit(solution)/shard_map/ppermute | solution.py:168
  33.7 0.7 slice_bitcast_fusion.8
  34.4 3.2 %collective-permute-start.18 = (bf16[25,64,128]{2,1,0:T(8,128)(2,1)}, bf16[25,64,128]{2,1,0:T(8,128)(2,1)S(1)}, u32[]{:S(2)}, u32[]{:S(2)}) collective-permute-start(bf16[25,64,128]{2,1,0:T(8,128)(2,1)} %collective-permute-done.13.rest_11_), channel_id=1, source_target_pairs={{4,0},{8,4},{12,8},{16,12},{20,16},{24,20},{28,24},{5,1},{9,5},{13... | collective-permute-start | bytes 1228808 | tf_op jit(solution)/shard_map/ppermute | solution.py:168
  37.7 4.9 %collective-permute-start.10 = (bf16[25,64,128]{2,1,0:T(8,128)(2,1)}, bf16[25,64,128]{2,1,0:T(8,128)(2,1)S(1)}, u32[]{:S(2)}, u32[]{:S(2)}) collective-permute-start(bf16[25,64,128]{2,1,0:T(8,128)(2,1)} %collective-permute-done.9.rest_10_), channel_id=1, source_target_pairs={{0,4},{4,8},{8,12},{12,16},{16,20},{20,24},{24,28},{1,5},{5,9},{9,... | collective-permute-start | bytes 1228808 | tf_op jit(solution)/shard_map/ppermute | solution.py:168
  42.7 0.1 pad_maximum_fusion.1
  42.8 1.9 %collective-permute-start.12 = (bf16[2,25,64,128]{3,2,1,0:T(8,128)(2,1)S(1)}, bf16[2,25,64,128]{3,2,1,0:T(8,128)(2,1)S(1)}, u32[]{:S(2)}, u32[]{:S(2)}) collective-permute-start(bf16[2,25,64,128]{3,2,1,0:T(8,128)(2,1)S(1)} %pad_maximum_fusion.1), channel_id=1, source_target_pairs={{0,3},{1,0},{2,1},{3,2},{4,7},{5,4},{6,5},{7,6},{24,27},{25,24},{2... | collective-permute-start | bytes 2457608 | tf_op jit(solution)/shard_map/ppermute | solution.py:187
  44.7 0.7 slice_bitcast_fusion.9
  45.4 0.7 slice_bitcast_fusion.10
  46.1 2.5 %collective-permute-start.8 = (bf16[2,25,64,128]{3,2,1,0:T(8,128)(2,1)S(1)}, bf16[2,25,64,128]{3,2,1,0:T(8,128)(2,1)S(1)}, u32[]{:S(2)}, u32[]{:S(2)}) collective-permute-start(bf16[2,25,64,128]{3,2,1,0:T(8,128)(2,1)S(1)} %pad_maximum_fusion.1), channel_id=1, source_target_pairs={{0,2},{1,3},{2,0},{3,1},{4,6},{5,7},{6,4},{7,5},{24,26},{25,27},{2... | collective-permute-start | bytes 2457608 | tf_op jit(solution)/shard_map/ppermute | solution.py:187
  48.6 4.3 %collective-permute-start.15 = (bf16[25,64,128]{2,1,0:T(8,128)(2,1)S(1)}, bf16[25,64,128]{2,1,0:T(8,128)(2,1)S(1)}, u32[]{:S(2)}, u32[]{:S(2)}) collective-permute-start(bf16[25,64,128]{2,1,0:T(8,128)(2,1)S(1)} %collective-permute-done.14.rest_7_), channel_id=1, source_target_pairs={{4,8},{8,12},{12,16},{16,20},{20,24},{24,28},{5,9},{9,13},{13,17},... | collective-permute-start | bytes 1228808 | tf_op jit(solution)/shard_map/ppermute | solution.py:168
  52.9 1.3 collective-permute-start.21
  54.2 4.8 %collective-permute-start.4 = (bf16[2,25,64,128]{3,2,1,0:T(8,128)(2,1)S(1)}, bf16[2,25,64,128]{3,2,1,0:T(8,128)(2,1)S(1)}, u32[]{:S(2)}, u32[]{:S(2)}) collective-permute-start(bf16[2,25,64,128]{3,2,1,0:T(8,128)(2,1)S(1)} %pad_maximum_fusion.1), channel_id=1, source_target_pairs={{0,1},{1,2},{2,3},{3,0},{4,5},{5,6},{6,7},{7,4},{24,25},{25,26},{2... | collective-permute-start | bytes 2457608 | tf_op jit(solution)/shard_map/ppermute | solution.py:187
  59.0 1.9 %collective-permute-start.17 = (bf16[25,64,128]{2,1,0:T(8,128)(2,1)}, bf16[25,64,128]{2,1,0:T(8,128)(2,1)S(1)}, u32[]{:S(2)}, u32[]{:S(2)}) collective-permute-start(bf16[25,64,128]{2,1,0:T(8,128)(2,1)} %collective-permute-done.9.rest_10_), channel_id=1, source_target_pairs={{4,0},{8,4},{12,8},{16,12},{20,16},{24,20},{28,24},{5,1},{9,5},{13... | collective-permute-start | bytes 1228808 | tf_op jit(solution)/shard_map/ppermute | solution.py:168
  61.0 2.4 %collective-permute-start.16 = (bf16[25,64,128]{2,1,0:T(8,128)(2,1)}, bf16[25,64,128]{2,1,0:T(8,128)(2,1)S(1)}, u32[]{:S(2)}, u32[]{:S(2)}) collective-permute-start(bf16[25,64,128]{2,1,0:T(8,128)(2,1)} %collective-permute-done.5.rest_9_), channel_id=1, source_target_pairs={{4,0},{8,4},{12,8},{16,12},{20,16},{24,20},{28,24},{5,1},{9,5},{13... | collective-permute-start | bytes 1228808 | tf_op jit(solution)/shard_map/ppermute | solution.py:168
  63.4 1.7 %collective-permute-done.12.rest_22_ = bf16[2,25,64,128]{3,2,1,0:T(8,128)(2,1)S(1)} collective-permute-done((bf16[2,25,64,128]{3,2,1,0:T(8,128)(2,1)S(1)}, bf16[2,25,64,128]{3,2,1,0:T(8,128)(2,1)S(1)}, u32[]{:S(2)}, u32[]{:S(2)}) %collective-permute-start.12) | collective-permute-done | bytes 819232 | tf_op jit(solution)/shard_map/ppermute | solution.py:187
  65.1 5.1 %collective-permute-start.6 = (bf16[25,64,128]{2,1,0:T(8,128)(2,1)}, bf16[25,64,128]{2,1,0:T(8,128)(2,1)S(1)}, u32[]{:S(2)}, u32[]{:S(2)}) collective-permute-start(bf16[25,64,128]{2,1,0:T(8,128)(2,1)} %collective-permute-done.5.rest_9_), channel_id=1, source_target_pairs={{0,4},{4,8},{8,12},{12,16},{16,20},{20,24},{24,28},{1,5},{5,9},{9,... | collective-permute-start | bytes 1228808 | tf_op jit(solution)/shard_map/ppermute | solution.py:168
  70.2 1.9 %collective-permute-start.11 = (bf16[25,64,128]{2,1,0:T(8,128)(2,1)S(1)}, bf16[25,64,128]{2,1,0:T(8,128)(2,1)S(1)}, u32[]{:S(2)}, u32[]{:S(2)}) collective-permute-start(bf16[25,64,128]{2,1,0:T(8,128)(2,1)S(1)} %collective-permute-done.10.rest_6_), channel_id=1, source_target_pairs={{4,8},{8,12},{12,16},{16,20},{20,24},{24,28},{5,9},{9,13},{13,17},... | collective-permute-start | bytes 1228808 | tf_op jit(solution)/shard_map/ppermute | solution.py:168
  72.2 3.7 %collective-permute-start.20 = (bf16[25,64,128]{2,1,0:T(8,128)(2,1)S(1)}, bf16[25,64,128]{2,1,0:T(8,128)(2,1)S(1)}, u32[]{:S(2)}, u32[]{:S(2)}) collective-permute-start(bf16[25,64,128]{2,1,0:T(8,128)(2,1)S(1)} %collective-permute-done.17.rest_14_), channel_id=1, source_target_pairs={{4,0},{8,4},{12,8},{16,12},{20,16},{24,20},{5,1},{9,5},{13,9},{17,... | collective-permute-start | bytes 1228808 | tf_op jit(solution)/shard_map/ppermute | solution.py:168
  75.9 1.9 %collective-permute-start.19 = (bf16[25,64,128]{2,1,0:T(8,128)(2,1)S(1)}, bf16[25,64,128]{2,1,0:T(8,128)(2,1)S(1)}, u32[]{:S(2)}, u32[]{:S(2)}) collective-permute-start(bf16[25,64,128]{2,1,0:T(8,128)(2,1)S(1)} %collective-permute-done.16.rest_13_), channel_id=1, source_target_pairs={{4,0},{8,4},{12,8},{16,12},{20,16},{24,20},{5,1},{9,5},{13,9},{17,... | collective-permute-start | bytes 1228808 | tf_op jit(solution)/shard_map/ppermute | solution.py:168
  77.8 6.4 %collective-permute-done.8.rest_21_ = bf16[2,25,64,128]{3,2,1,0:T(8,128)(2,1)S(1)} collective-permute-done((bf16[2,25,64,128]{3,2,1,0:T(8,128)(2,1)S(1)}, bf16[2,25,64,128]{3,2,1,0:T(8,128)(2,1)S(1)}, u32[]{:S(2)}, u32[]{:S(2)}) %collective-permute-start.8) | collective-permute-done | bytes 819232 | tf_op jit(solution)/shard_map/ppermute | solution.py:187
  84.2 2.0 %collective-permute-start.7 = (bf16[25,64,128]{2,1,0:T(8,128)(2,1)S(1)}, bf16[25,64,128]{2,1,0:T(8,128)(2,1)S(1)}, u32[]{:S(2)}, u32[]{:S(2)}) collective-permute-start(bf16[25,64,128]{2,1,0:T(8,128)(2,1)S(1)} %collective-permute-done.6.rest_5_), channel_id=1, source_target_pairs={{4,8},{8,12},{12,16},{16,20},{20,24},{24,28},{5,9},{9,13},{13,17},... | collective-permute-start | bytes 1228808 | tf_op jit(solution)/shard_map/ppermute | solution.py:168
  86.3 7.1 %collective-permute-done.7.rest_1_ = bf16[25,64,128]{2,1,0:T(8,128)(2,1)S(1)} collective-permute-done((bf16[25,64,128]{2,1,0:T(8,128)(2,1)S(1)}, bf16[25,64,128]{2,1,0:T(8,128)(2,1)S(1)}, u32[]{:S(2)}, u32[]{:S(2)}) %collective-permute-start.7) | collective-permute-done | bytes 409632 | tf_op jit(solution)/shard_map/ppermute | solution.py:168
  93.5 0.7 copy-done.19
  94.2 0.1 stack.54
  94.3 0.1 reshape.806
  94.4 3.2 %gather_fusion = s32[768]{0:T(1024)S(1)} fusion(s32[960]{0:T(1024)S(1)} %reshape.806, s32[1024]{0:T(1024)S(1)} %pad_clamp_fusion.1), kind=kCustom, calls=%fused_computation | custom fusion | bytes 9216 | tf_op jit(solution)/shard_map/jit(_take)/gather | solution.py:222
  97.6 1.2 gather_fusion.1
  98.8 0.1 broadcast_in_dim.32
  98.9 0.1 reshape.740
  99.0 0.6 multiply_add_fusion
  99.7 0.6 fusion.11.pair_ref
  100.3 23.0 %shard_map.55 = f32[64,64,128]{2,1,0:T(8,128)} custom-call(s32[768]{0:T(1024)} %fusion.11.pair_ref, s32[768]{0:T(1024)} %get-tuple-element.45.half_ref, s32[768]{0:T(1024)} %get-tuple-element.29.target_ref, s32[768]{0:T(1024)} %reshape.807.live_ref, s32[192]{0:T(256)} %fusion.32.own_pos_ref, s32[5]{0:T(128)} %stack.59.fix_ref, ...), custom_call_target="tpu_custom_call" | custom-call | tf_op jit(solution)/shard_map/pallas_call | solution.py:106
  123.3 1.6 %bitcast_convert_fusion.2 = (bf16[8,2,64,128]{3,2,1,0:T(8,128)(2,1)S(1)}, bf16[8,2,64,128]{3,2,1,0:T(8,128)(2,1)S(1)}, bf16[8,2,64,128]{3,2,1,0:T(8,128)(2,1)S(1)}) fusion(f32[4,8,2,64,128]{4,3,2,1,0:T(8,128)} %bitcast.141, s32[]{:T(128)S(6)} %select_n.678, pred[]{:T(512)S(6)} %and.252, s32[]{:T(128)S(6)} %select_n.682, pred[]{:T(512)S(6)} %and.254, ...), kind=kLoop, calls=%fused_computation.9 | loop fusion | flops 393216 | bytes 1572879 | tf_op jit(solution)/shard_map/convert_element_type | solution.py:250
  124.8 4.0 %collective-permute-start.22 = (bf16[8,2,64,128]{3,2,1,0:T(8,128)(2,1)S(1)}, bf16[8,2,64,128]{3,2,1,0:T(8,128)(2,1)S(1)}, u32[]{:S(2)}, u32[]{:S(2)}) collective-permute-start(bf16[8,2,64,128]{3,2,1,0:T(8,128)(2,1)S(1)} %get-tuple-element.31), channel_id=1, source_target_pairs={{0,1},{1,2},{2,3},{3,0},{4,5},{5,6},{6,7},{7,4},{8,9},{9,10},{10,1... | collective-permute-start | bytes 786440 | tf_op jit(solution)/shard_map/ppermute | solution.py:249
  128.9 0.5 collective-permute-start.23
  129.4 0.1 collective-permute-start.24
  129.5 4.1 %collective-permute-done.22 = bf16[8,2,64,128]{3,2,1,0:T(8,128)(2,1)S(1)} collective-permute-done((bf16[8,2,64,128]{3,2,1,0:T(8,128)(2,1)S(1)}, bf16[8,2,64,128]{3,2,1,0:T(8,128)(2,1)S(1)}, u32[]{:S(2)}, u32[]{:S(2)}) %collective-permute-start.22) | collective-permute-done | bytes 262176 | tf_op jit(solution)/shard_map/ppermute | solution.py:249
  133.6 4.4 %collective-permute-done.23 = bf16[8,2,64,128]{3,2,1,0:T(8,128)(2,1)S(1)} collective-permute-done((bf16[8,2,64,128]{3,2,1,0:T(8,128)(2,1)S(1)}, bf16[8,2,64,128]{3,2,1,0:T(8,128)(2,1)S(1)}, u32[]{:S(2)}, u32[]{:S(2)}) %collective-permute-start.23) | collective-permute-done | bytes 262176 | tf_op jit(solution)/shard_map/ppermute | solution.py:249
  138.1 1.2 fusion.2
  139.2 0.2 fusion.46
  139.5 1.1 pad_maximum_fusion
  (86 shorter events, 0.5 us)
Async XLA Ops:
  0.0 9.3 %copy-start.20 = (s32[192,4]{0,1:T(4,128)S(1)}, s32[192,4]{0,1:T(4,128)}, u32[]{:S(2)}) copy-start(s32[192,4]{0,1:T(4,128)} %param.10) | copy-start | bytes 9220
  0.7 9.9 %copy-start.21 = (s32[192]{0:T(256)S(1)}, s32[192]{0:T(256)}, u32[]{:S(2)}) copy-start(s32[192]{0:T(256)} %param.11) | copy-start | bytes 2308
  3.0 25.3 %copy-start.4 = (bf16[25,64,128]{2,1,0:T(8,128)(2,1)}, bf16[25,64,128]{2,1,0:T(8,128)(2,1)S(1)}, u32[]{:S(2)}) copy-start(bf16[25,64,128]{2,1,0:T(8,128)(2,1)S(1)} %fusion.3.rest_8_) | copy-start | bytes 1228804
  3.0 26.5 %collective-permute-start = (bf16[25,64,128]{2,1,0:T(8,128)(2,1)S(1)}, bf16[25,64,128]{2,1,0:T(8,128)(2,1)S(1)}, u32[]{:S(2)}, u32[]{:S(2)}) collective-permute-start(bf16[25,64,128]{2,1,0:T(8,128)(2,1)S(1)} %fusion.3.rest_8_), channel_id=1, source_target_pairs={{28,0},{0,4},{4,8},{8,12},{12,16},{16,20},{20,24},{24,28},{29,1},{... | collective-permute-start | bytes 1228808 | tf_op jit(solution)/shard_map/ppermute | solution.py:168
  3.1 26.5 %collective-permute-start.2 = (bf16[25,64,128]{2,1,0:T(8,128)(2,1)S(1)}, bf16[25,64,128]{2,1,0:T(8,128)(2,1)S(1)}, u32[]{:S(2)}, u32[]{:S(2)}) collective-permute-start(bf16[25,64,128]{2,1,0:T(8,128)(2,1)S(1)} %fusion.3.rest_8_), channel_id=1, source_target_pairs={{4,0},{8,4},{12,8},{16,12},{20,16},{24,20},{28,24},{0,28},{5,1},{9... | collective-permute-start | bytes 1228808 | tf_op jit(solution)/shard_map/ppermute | solution.py:168
  4.8 26.6 %collective-permute-start.13 = (bf16[25,64,128]{2,1,0:T(8,128)(2,1)S(1)}, bf16[25,64,128]{2,1,0:T(8,128)(2,1)}, u32[]{:S(2)}, u32[]{:S(2)}) collective-permute-start(bf16[25,64,128]{2,1,0:T(8,128)(2,1)S(1)} %fusion.3.rest_8_), channel_id=1, source_target_pairs={{0,3},{1,0},{2,1},{3,2},{4,7},{5,4},{6,5},{7,6},{8,11},{9,8},{10,9... | collective-permute-start | bytes 1228808 | tf_op jit(solution)/shard_map/ppermute | solution.py:156
  5.4 29.1 %collective-permute-start.9 = (bf16[25,64,128]{2,1,0:T(8,128)(2,1)S(1)}, bf16[25,64,128]{2,1,0:T(8,128)(2,1)}, u32[]{:S(2)}, u32[]{:S(2)}) collective-permute-start(bf16[25,64,128]{2,1,0:T(8,128)(2,1)S(1)} %fusion.3.rest_8_), channel_id=1, source_target_pairs={{0,2},{1,3},{2,0},{3,1},{4,6},{5,7},{6,4},{7,5},{8,10},{9,11},{10,... | collective-permute-start | bytes 1228808 | tf_op jit(solution)/shard_map/ppermute | solution.py:156
  6.9 38.5 %collective-permute-start.5 = (bf16[25,64,128]{2,1,0:T(8,128)(2,1)S(1)}, bf16[25,64,128]{2,1,0:T(8,128)(2,1)}, u32[]{:S(2)}, u32[]{:S(2)}) collective-permute-start(bf16[25,64,128]{2,1,0:T(8,128)(2,1)S(1)} %fusion.3.rest_8_), channel_id=1, source_target_pairs={{0,1},{1,2},{2,3},{3,0},{4,5},{5,6},{6,7},{7,4},{8,9},{9,10},{10,1... | collective-permute-start | bytes 1228808 | tf_op jit(solution)/shard_map/ppermute | solution.py:156
  29.6 64.7 %copy-start = (bf16[25,64,128]{2,1,0:T(8,128)(2,1)}, bf16[25,64,128]{2,1,0:T(8,128)(2,1)S(1)}, u32[]{:S(2)}) copy-start(bf16[25,64,128]{2,1,0:T(8,128)(2,1)S(1)} %collective-permute-done.rest_4_) | copy-start | bytes 1228804
  29.6 8.1 %collective-permute-start.1 = (bf16[25,64,128]{2,1,0:T(8,128)(2,1)S(1)}, bf16[25,64,128]{2,1,0:T(8,128)(2,1)S(1)}, u32[]{:S(2)}, u32[]{:S(2)}) collective-permute-start(bf16[25,64,128]{2,1,0:T(8,128)(2,1)S(1)} %collective-permute-done.rest_4_), channel_id=1, source_target_pairs={{28,0},{0,4},{4,8},{8,12},{12,16},{16,20},{20,24},{24,28},{29,1},{... | collective-permute-start | bytes 1228808 | tf_op jit(solution)/shard_map/ppermute | solution.py:168
  29.7 64.7 %copy-start.1 = (bf16[25,64,128]{2,1,0:T(8,128)(2,1)}, bf16[25,64,128]{2,1,0:T(8,128)(2,1)S(1)}, u32[]{:S(2)}) copy-start(bf16[25,64,128]{2,1,0:T(8,128)(2,1)S(1)} %collective-permute-done.2.rest_12_) | copy-start | bytes 1228804
  29.7 13.0 %collective-permute-start.3 = (bf16[25,64,128]{2,1,0:T(8,128)(2,1)S(1)}, bf16[25,64,128]{2,1,0:T(8,128)(2,1)S(1)}, u32[]{:S(2)}, u32[]{:S(2)}) collective-permute-start(bf16[25,64,128]{2,1,0:T(8,128)(2,1)S(1)} %collective-permute-done.2.rest_12_), channel_id=1, source_target_pairs={{4,0},{8,4},{12,8},{16,12},{20,16},{24,20},{28,24},{0,28},{5,1},{9... | collective-permute-start | bytes 1228808 | tf_op jit(solution)/shard_map/ppermute | solution.py:168
  31.4 17.2 %collective-permute-start.14 = (bf16[25,64,128]{2,1,0:T(8,128)(2,1)}, bf16[25,64,128]{2,1,0:T(8,128)(2,1)S(1)}, u32[]{:S(2)}, u32[]{:S(2)}) collective-permute-start(bf16[25,64,128]{2,1,0:T(8,128)(2,1)} %collective-permute-done.13.rest_11_), channel_id=1, source_target_pairs={{0,4},{4,8},{8,12},{12,16},{16,20},{20,24},{24,28},{1,5},{5,9},{9,... | collective-permute-start | bytes 1228808 | tf_op jit(solution)/shard_map/ppermute | solution.py:168
  34.4 18.4 %collective-permute-start.18 = (bf16[25,64,128]{2,1,0:T(8,128)(2,1)}, bf16[25,64,128]{2,1,0:T(8,128)(2,1)S(1)}, u32[]{:S(2)}, u32[]{:S(2)}) collective-permute-start(bf16[25,64,128]{2,1,0:T(8,128)(2,1)} %collective-permute-done.13.rest_11_), channel_id=1, source_target_pairs={{4,0},{8,4},{12,8},{16,12},{20,16},{24,20},{28,24},{5,1},{9,5},{13... | collective-permute-start | bytes 1228808 | tf_op jit(solution)/shard_map/ppermute | solution.py:168
  37.7 59.9 %copy-start.2 = (bf16[25,64,128]{2,1,0:T(8,128)(2,1)}, bf16[25,64,128]{2,1,0:T(8,128)(2,1)S(1)}, u32[]{:S(2)}) copy-start(bf16[25,64,128]{2,1,0:T(8,128)(2,1)S(1)} %collective-permute-done.1.rest_0_) | copy-start | bytes 1228804
  37.7 16.5 %collective-permute-start.10 = (bf16[25,64,128]{2,1,0:T(8,128)(2,1)}, bf16[25,64,128]{2,1,0:T(8,128)(2,1)S(1)}, u32[]{:S(2)}, u32[]{:S(2)}) collective-permute-start(bf16[25,64,128]{2,1,0:T(8,128)(2,1)} %collective-permute-done.9.rest_10_), channel_id=1, source_target_pairs={{0,4},{4,8},{8,12},{12,16},{16,20},{20,24},{24,28},{1,5},{5,9},{9,... | collective-permute-start | bytes 1228808 | tf_op jit(solution)/shard_map/ppermute | solution.py:168
  42.7 54.9 %copy-start.3 = (bf16[25,64,128]{2,1,0:T(8,128)(2,1)}, bf16[25,64,128]{2,1,0:T(8,128)(2,1)S(1)}, u32[]{:S(2)}) copy-start(bf16[25,64,128]{2,1,0:T(8,128)(2,1)S(1)} %collective-permute-done.3.rest_16_) | copy-start | bytes 1228804
  42.8 22.3 %collective-permute-start.12 = (bf16[2,25,64,128]{3,2,1,0:T(8,128)(2,1)S(1)}, bf16[2,25,64,128]{3,2,1,0:T(8,128)(2,1)S(1)}, u32[]{:S(2)}, u32[]{:S(2)}) collective-permute-start(bf16[2,25,64,128]{3,2,1,0:T(8,128)(2,1)S(1)} %pad_maximum_fusion.1), channel_id=1, source_target_pairs={{0,3},{1,0},{2,1},{3,2},{4,7},{5,4},{6,5},{7,6},{24,27},{25,24},{2... | collective-permute-start | bytes 2457608 | tf_op jit(solution)/shard_map/ppermute | solution.py:187
  46.1 38.1 %collective-permute-start.8 = (bf16[2,25,64,128]{3,2,1,0:T(8,128)(2,1)S(1)}, bf16[2,25,64,128]{3,2,1,0:T(8,128)(2,1)S(1)}, u32[]{:S(2)}, u32[]{:S(2)}) collective-permute-start(bf16[2,25,64,128]{3,2,1,0:T(8,128)(2,1)S(1)} %pad_maximum_fusion.1), channel_id=1, source_target_pairs={{0,2},{1,3},{2,0},{3,1},{4,6},{5,7},{6,4},{7,5},{24,26},{25,27},{2... | collective-permute-start | bytes 2457608 | tf_op jit(solution)/shard_map/ppermute | solution.py:187
  48.6 51.7 %copy-start.8 = (bf16[25,64,128]{2,1,0:T(8,128)(2,1)}, bf16[25,64,128]{2,1,0:T(8,128)(2,1)S(1)}, u32[]{:S(2)}) copy-start(bf16[25,64,128]{2,1,0:T(8,128)(2,1)S(1)} %collective-permute-done.14.rest_7_) | copy-start | bytes 1228804
  48.6 10.4 %collective-permute-start.15 = (bf16[25,64,128]{2,1,0:T(8,128)(2,1)S(1)}, bf16[25,64,128]{2,1,0:T(8,128)(2,1)S(1)}, u32[]{:S(2)}, u32[]{:S(2)}) collective-permute-start(bf16[25,64,128]{2,1,0:T(8,128)(2,1)S(1)} %collective-permute-done.14.rest_7_), channel_id=1, source_target_pairs={{4,8},{8,12},{12,16},{16,20},{20,24},{24,28},{5,9},{9,13},{13,17},... | collective-permute-start | bytes 1228808 | tf_op jit(solution)/shard_map/ppermute | solution.py:168
  52.9 40.6 %copy-start.9 = (bf16[25,64,128]{2,1,0:T(8,128)(2,1)}, bf16[25,64,128]{2,1,0:T(8,128)(2,1)S(1)}, u32[]{:S(2)}) copy-start(bf16[25,64,128]{2,1,0:T(8,128)(2,1)S(1)} %collective-permute-done.18.rest_15_) | copy-start | bytes 1228804
  52.9 8.1 %collective-permute-start.21 = (bf16[25,64,128]{2,1,0:T(8,128)(2,1)S(1)}, bf16[25,64,128]{2,1,0:T(8,128)(2,1)S(1)}, u32[]{:S(2)}, u32[]{:S(2)}) collective-permute-start(bf16[25,64,128]{2,1,0:T(8,128)(2,1)S(1)} %collective-permute-done.18.rest_15_), channel_id=1, source_target_pairs={{4,0},{8,4},{12,8},{16,12},{20,16},{24,20},{5,1},{9,5},{13,9},{17,... | collective-permute-start | bytes 1228808 | tf_op jit(solution)/shard_map/ppermute | solution.py:168
  54.2 39.2 %copy-start.10 = (bf16[25,64,128]{2,1,0:T(8,128)(2,1)}, bf16[25,64,128]{2,1,0:T(8,128)(2,1)S(1)}, u32[]{:S(2)}) copy-start(bf16[25,64,128]{2,1,0:T(8,128)(2,1)S(1)} %collective-permute-done.10.rest_6_) | copy-start | bytes 1228804
  54.2 32.0 %collective-permute-start.4 = (bf16[2,25,64,128]{3,2,1,0:T(8,128)(2,1)S(1)}, bf16[2,25,64,128]{3,2,1,0:T(8,128)(2,1)S(1)}, u32[]{:S(2)}, u32[]{:S(2)}) collective-permute-start(bf16[2,25,64,128]{3,2,1,0:T(8,128)(2,1)S(1)} %pad_maximum_fusion.1), channel_id=1, source_target_pairs={{0,1},{1,2},{2,3},{3,0},{4,5},{5,6},{6,7},{7,4},{24,25},{25,26},{2... | collective-permute-start | bytes 2457608 | tf_op jit(solution)/shard_map/ppermute | solution.py:187
  59.0 41.2 %copy-start.11 = (bf16[25,64,128]{2,1,0:T(8,128)(2,1)}, bf16[25,64,128]{2,1,0:T(8,128)(2,1)S(1)}, u32[]{:S(2)}) copy-start(bf16[25,64,128]{2,1,0:T(8,128)(2,1)S(1)} %collective-permute-done.15.rest_3_) | copy-start | bytes 1228804
  59.0 11.2 %collective-permute-start.17 = (bf16[25,64,128]{2,1,0:T(8,128)(2,1)}, bf16[25,64,128]{2,1,0:T(8,128)(2,1)S(1)}, u32[]{:S(2)}, u32[]{:S(2)}) collective-permute-start(bf16[25,64,128]{2,1,0:T(8,128)(2,1)} %collective-permute-done.9.rest_10_), channel_id=1, source_target_pairs={{4,0},{8,4},{12,8},{16,12},{20,16},{24,20},{28,24},{5,1},{9,5},{13... | collective-permute-start | bytes 1228808 | tf_op jit(solution)/shard_map/ppermute | solution.py:168
  61.0 32.5 %copy-start.12 = (bf16[25,64,128]{2,1,0:T(8,128)(2,1)}, bf16[25,64,128]{2,1,0:T(8,128)(2,1)S(1)}, u32[]{:S(2)}) copy-start(bf16[25,64,128]{2,1,0:T(8,128)(2,1)S(1)} %collective-permute-done.21.rest_19_) | copy-start | bytes 1228804
  61.0 11.2 %collective-permute-start.16 = (bf16[25,64,128]{2,1,0:T(8,128)(2,1)}, bf16[25,64,128]{2,1,0:T(8,128)(2,1)S(1)}, u32[]{:S(2)}, u32[]{:S(2)}) collective-permute-start(bf16[25,64,128]{2,1,0:T(8,128)(2,1)} %collective-permute-done.5.rest_9_), channel_id=1, source_target_pairs={{4,0},{8,4},{12,8},{16,12},{20,16},{24,20},{28,24},{5,1},{9,5},{13... | collective-permute-start | bytes 1228808 | tf_op jit(solution)/shard_map/ppermute | solution.py:168
  65.1 32.5 %copy-start.5 = (bf16[2,25,64,128]{3,2,1,0:T(8,128)(2,1)}, bf16[2,25,64,128]{3,2,1,0:T(8,128)(2,1)S(1)}, u32[]{:S(2)}) copy-start(bf16[2,25,64,128]{3,2,1,0:T(8,128)(2,1)S(1)} %collective-permute-done.12.rest_22_) | copy-start | bytes 2457604
  65.1 10.8 %collective-permute-start.6 = (bf16[25,64,128]{2,1,0:T(8,128)(2,1)}, bf16[25,64,128]{2,1,0:T(8,128)(2,1)S(1)}, u32[]{:S(2)}, u32[]{:S(2)}) collective-permute-start(bf16[25,64,128]{2,1,0:T(8,128)(2,1)} %collective-permute-done.5.rest_9_), channel_id=1, source_target_pairs={{0,4},{4,8},{8,12},{12,16},{16,20},{20,24},{24,28},{1,5},{5,9},{9,... | collective-permute-start | bytes 1228808 | tf_op jit(solution)/shard_map/ppermute | solution.py:168
  70.2 23.3 %copy-start.13 = (bf16[25,64,128]{2,1,0:T(8,128)(2,1)}, bf16[25,64,128]{2,1,0:T(8,128)(2,1)S(1)}, u32[]{:S(2)}) copy-start(bf16[25,64,128]{2,1,0:T(8,128)(2,1)S(1)} %collective-permute-done.17.rest_14_) | copy-start | bytes 1228804
  70.2 16.0 %collective-permute-start.11 = (bf16[25,64,128]{2,1,0:T(8,128)(2,1)S(1)}, bf16[25,64,128]{2,1,0:T(8,128)(2,1)S(1)}, u32[]{:S(2)}, u32[]{:S(2)}) collective-permute-start(bf16[25,64,128]{2,1,0:T(8,128)(2,1)S(1)} %collective-permute-done.10.rest_6_), channel_id=1, source_target_pairs={{4,8},{8,12},{12,16},{16,20},{20,24},{24,28},{5,9},{9,13},{13,17},... | collective-permute-start | bytes 1228808 | tf_op jit(solution)/shard_map/ppermute | solution.py:168
  72.2 21.3 %copy-start.14 = (bf16[25,64,128]{2,1,0:T(8,128)(2,1)}, bf16[25,64,128]{2,1,0:T(8,128)(2,1)S(1)}, u32[]{:S(2)}) copy-start(bf16[25,64,128]{2,1,0:T(8,128)(2,1)S(1)} %collective-permute-done.16.rest_13_) | copy-start | bytes 1228804
  72.2 14.1 %collective-permute-start.20 = (bf16[25,64,128]{2,1,0:T(8,128)(2,1)S(1)}, bf16[25,64,128]{2,1,0:T(8,128)(2,1)S(1)}, u32[]{:S(2)}, u32[]{:S(2)}) collective-permute-start(bf16[25,64,128]{2,1,0:T(8,128)(2,1)S(1)} %collective-permute-done.17.rest_14_), channel_id=1, source_target_pairs={{4,0},{8,4},{12,8},{16,12},{20,16},{24,20},{5,1},{9,5},{13,9},{17,... | collective-permute-start | bytes 1228808 | tf_op jit(solution)/shard_map/ppermute | solution.py:168
  75.9 17.6 %copy-start.15 = (bf16[25,64,128]{2,1,0:T(8,128)(2,1)}, bf16[25,64,128]{2,1,0:T(8,128)(2,1)S(1)}, u32[]{:S(2)}) copy-start(bf16[25,64,128]{2,1,0:T(8,128)(2,1)S(1)} %collective-permute-done.6.rest_5_) | copy-start | bytes 1228804
  75.9 10.4 %collective-permute-start.19 = (bf16[25,64,128]{2,1,0:T(8,128)(2,1)S(1)}, bf16[25,64,128]{2,1,0:T(8,128)(2,1)S(1)}, u32[]{:S(2)}, u32[]{:S(2)}) collective-permute-start(bf16[25,64,128]{2,1,0:T(8,128)(2,1)S(1)} %collective-permute-done.16.rest_13_), channel_id=1, source_target_pairs={{4,0},{8,4},{12,8},{16,12},{20,16},{24,20},{5,1},{9,5},{13,9},{17,... | collective-permute-start | bytes 1228808 | tf_op jit(solution)/shard_map/ppermute | solution.py:168
  84.2 2.1 %copy-start.6 = (bf16[2,25,64,128]{3,2,1,0:T(8,128)(2,1)}, bf16[2,25,64,128]{3,2,1,0:T(8,128)(2,1)S(1)}, u32[]{:S(2)}) copy-start(bf16[2,25,64,128]{3,2,1,0:T(8,128)(2,1)S(1)} %collective-permute-done.8.rest_21_) | copy-start | bytes 2457604
  84.2 9.3 %collective-permute-start.7 = (bf16[25,64,128]{2,1,0:T(8,128)(2,1)S(1)}, bf16[25,64,128]{2,1,0:T(8,128)(2,1)S(1)}, u32[]{:S(2)}, u32[]{:S(2)}) collective-permute-start(bf16[25,64,128]{2,1,0:T(8,128)(2,1)S(1)} %collective-permute-done.6.rest_5_), channel_id=1, source_target_pairs={{4,8},{8,12},{12,16},{16,20},{20,24},{24,28},{5,9},{9,13},{13,17},... | collective-permute-start | bytes 1228808 | tf_op jit(solution)/shard_map/ppermute | solution.py:168
  86.2 7.2 %copy-start.7 = (bf16[2,25,64,128]{3,2,1,0:T(8,128)(2,1)}, bf16[2,25,64,128]{3,2,1,0:T(8,128)(2,1)S(1)}, u32[]{:S(2)}) copy-start(bf16[2,25,64,128]{3,2,1,0:T(8,128)(2,1)S(1)} %collective-permute-done.4.rest_20_) | copy-start | bytes 2457604
  86.3 7.3 %copy-start.16 = (bf16[25,64,128]{2,1,0:T(8,128)(2,1)}, bf16[25,64,128]{2,1,0:T(8,128)(2,1)S(1)}, u32[]{:S(2)}) copy-start(bf16[25,64,128]{2,1,0:T(8,128)(2,1)S(1)} %collective-permute-done.11.rest_2_) | copy-start | bytes 1228804
  86.3 7.2 %copy-start.17 = (bf16[25,64,128]{2,1,0:T(8,128)(2,1)}, bf16[25,64,128]{2,1,0:T(8,128)(2,1)S(1)}, u32[]{:S(2)}) copy-start(bf16[25,64,128]{2,1,0:T(8,128)(2,1)S(1)} %collective-permute-done.20.rest_18_) | copy-start | bytes 1228804
  86.3 7.2 %copy-start.18 = (bf16[25,64,128]{2,1,0:T(8,128)(2,1)}, bf16[25,64,128]{2,1,0:T(8,128)(2,1)S(1)}, u32[]{:S(2)}) copy-start(bf16[25,64,128]{2,1,0:T(8,128)(2,1)S(1)} %collective-permute-done.19.rest_17_) | copy-start | bytes 1228804
  93.4 0.8 copy-start.19
  124.8 8.8 %collective-permute-start.22 = (bf16[8,2,64,128]{3,2,1,0:T(8,128)(2,1)S(1)}, bf16[8,2,64,128]{3,2,1,0:T(8,128)(2,1)S(1)}, u32[]{:S(2)}, u32[]{:S(2)}) collective-permute-start(bf16[8,2,64,128]{3,2,1,0:T(8,128)(2,1)S(1)} %get-tuple-element.31), channel_id=1, source_target_pairs={{0,1},{1,2},{2,3},{3,0},{4,5},{5,6},{6,7},{7,4},{8,9},{9,10},{10,1... | collective-permute-start | bytes 786440 | tf_op jit(solution)/shard_map/ppermute | solution.py:249
  128.9 9.2 %collective-permute-start.23 = (bf16[8,2,64,128]{3,2,1,0:T(8,128)(2,1)S(1)}, bf16[8,2,64,128]{3,2,1,0:T(8,128)(2,1)S(1)}, u32[]{:S(2)}, u32[]{:S(2)}) collective-permute-start(bf16[8,2,64,128]{3,2,1,0:T(8,128)(2,1)S(1)} %get-tuple-element.33), channel_id=1, source_target_pairs={{0,2},{1,3},{2,0},{3,1},{4,6},{5,7},{6,4},{7,5},{8,10},{9,11},{10,... | collective-permute-start | bytes 786440 | tf_op jit(solution)/shard_map/ppermute | solution.py:249
  129.4 8.7 %collective-permute-start.24 = (bf16[8,2,64,128]{3,2,1,0:T(8,128)(2,1)S(1)}, bf16[8,2,64,128]{3,2,1,0:T(8,128)(2,1)S(1)}, u32[]{:S(2)}, u32[]{:S(2)}) collective-permute-start(bf16[8,2,64,128]{3,2,1,0:T(8,128)(2,1)S(1)} %get-tuple-element.32), channel_id=1, source_target_pairs={{0,3},{1,0},{2,1},{3,2},{4,7},{5,4},{6,5},{7,6},{8,11},{9,8},{10,9... | collective-permute-start | bytes 786440 | tf_op jit(solution)/shard_map/ppermute | solution.py:249

commit v15 on v10

--- a/solution.py
+++ b/solution.py
@@ -8,7 +8,7 @@
 from jax.sharding import PartitionSpec as P
 
 CB = 4
-ROWS_PER_STEP = 16
+ROWS_PER_STEP = 48
 
 
 def passed_along(block, axis, distance):
@@ -87,7 +87,7 @@
             accs[s][t] = accs[s][t] + results[s]
         return carry
 
-    lax.fori_loop(0, rows_here, row_body, 0, unroll=2)
+    lax.fori_loop(0, rows_here, row_body, 0, unroll=16)
 
     @pl.when(step == pl.num_programs(0) - 1)
     def _():
@@ -250,9 +250,12 @@
     total = jnp.take(summed, group_me, axis=0)
     for k in range(1, group_size):
         outgoing = jnp.take(summed, jnp.mod(group_me + k, group_size), axis=0)
-        total = total + lax.ppermute(
-            outgoing, "grp", [(i, (i + k) % group_size) for i in range(group_size)]
+        incoming = lax.ppermute(
+            outgoing.astype(jnp.bfloat16),
+            "grp",
+            [(i, (i + k) % group_size) for i in range(group_size)],
         )
+        total = total + incoming.astype(jnp.float32)
     total = total.reshape(share, CB // 2, block_size, 2, block_size)
     return total.transpose(0, 1, 3, 2, 4).reshape(share, CB, block_size, block_size)
 

time: 174 us -> 142 us (0.82)
  Pallas kernels: 43.9 us -> 23.2 us
  waiting for transfers between devices: 34.9 us -> 23.7 us
    pallas_call x1, Pallas kernels: 43.9 us -> 23.2 us  [coarse_partial(): pl.pallas_call(coarse_kernel, out_shape=jax.ShapeDtypeStruct((n_targets /...]
    ppermute x3, waiting for transfers between devices: 19.8 us -> 8.54 us  [local(): lax.ppermute(outgoing.astype(jnp.bfloat16), 'grp', [(i, (i + k) % group_s...]
  transfers between devices with their start and end apart: 25 -> 25, of which waited for: 5 -> 5; matrix products, arithmetic and copies ran while one was open for 13% -> 16% of each run, Pallas kernels for 0% -> 0%
where the time goes in v15:
time: 142 us; the launch traced here: 141 us
  starting transfers between devices  56.8 us (40%)
  local copies, waits for them, and re-layouts  29.3 us (21%)
  waiting for transfers between devices  23.7 us (17%)
  Pallas kernels  23.2 us (16%)
  other arithmetic  6.78 us (5%)
    ppermute x16, starting transfers between devices, ring(): return lax.ppermute(piece, 'blk', route)  38.6 us
    pallas_call x1, Pallas kernels, coarse_partial(): pl.pallas_call(coarse_kernel, out_shape=jax.ShapeDtypeStruct((n_targets /...  23.2 us
    unnamed x45, local copies, waits for them, and re-layouts  17.7 us
    ppermute x3, starting transfers between devices, local(): fixed.append(lax.ppermute(fix_src, ('blk', 'grp'), route))  9.14 us
    ppermute x3, waiting for transfers between devices, local(): lax.ppermute(outgoing.astype(jnp.bfloat16), 'grp', [(i, (i + k) % group_s...  8.54 us
    ppermute x3, waiting for transfers between devices, local(): fixed.append(lax.ppermute(fix_src, ('blk', 'grp'), route))  8.03 us
    ppermute x16, waiting for transfers between devices, ring(): return lax.ppermute(piece, 'blk', route)  7.14 us
    ppermute x3, starting transfers between devices, local(): lax.ppermute(outgoing.astype(jnp.bfloat16), 'grp', [(i, (i + k) % group_s...  4.67 us
  transfers between devices with their start and end apart: 25, of which 5 were waited for; matrix products, arithmetic and copies ran while one was open for 16% of the time, Pallas kernels for 0%

profile of v15, /device:TPU:26, one launch (start us, length us, event | category | flops | bytes accessed | tf_op | source)
XLA Modules:
  0.0 140.7 jit_solution(854030020869226703)
XLA Ops:
  0.0 0.7 convert_bitcast_fusion
  0.7 2.0 %copy.17 = bf16[24,2,64,64]{3,1,2,0:T(2,128)(2,1)S(1)} copy(bf16[24,2,64,64]{3,2,1,0:T(8,128)(2,1)} %bitcast.144) | data formatting | bytes 786432 | tf_op jit(solution)/shard_map/reshape | solution.py:146
  2.6 0.3 reshape.739
  3.1 1.7 %collective-permute-start.2 = (bf16[25,64,128]{2,1,0:T(8,128)(2,1)S(1)}, bf16[25,64,128]{2,1,0:T(8,128)(2,1)S(1)}, u32[]{:S(2)}, u32[]{:S(2)}) collective-permute-start(bf16[25,64,128]{2,1,0:T(8,128)(2,1)S(1)} %fusion.3.rest_8_), channel_id=1, source_target_pairs={{4,0},{8,4},{12,8},{16,12},{20,16},{24,20},{28,24},{0,28},{5,1},{9... | collective-permute-start | bytes 1228808 | tf_op jit(solution)/shard_map/ppermute | solution.py:172
  4.8 0.5 collective-permute-start.13
  5.4 1.5 %collective-permute-start.9 = (bf16[25,64,128]{2,1,0:T(8,128)(2,1)S(1)}, bf16[25,64,128]{2,1,0:T(8,128)(2,1)}, u32[]{:S(2)}, u32[]{:S(2)}) collective-permute-start(bf16[25,64,128]{2,1,0:T(8,128)(2,1)S(1)} %fusion.3.rest_8_), channel_id=1, source_target_pairs={{0,2},{1,3},{2,0},{3,1},{4,6},{5,7},{6,4},{7,5},{8,10},{9,11},{10,... | collective-permute-start | bytes 1228808 | tf_op jit(solution)/shard_map/ppermute | solution.py:160
  6.9 2.4 %collective-permute-start.5 = (bf16[25,64,128]{2,1,0:T(8,128)(2,1)S(1)}, bf16[25,64,128]{2,1,0:T(8,128)(2,1)}, u32[]{:S(2)}, u32[]{:S(2)}) collective-permute-start(bf16[25,64,128]{2,1,0:T(8,128)(2,1)S(1)} %fusion.3.rest_8_), channel_id=1, source_target_pairs={{0,1},{1,2},{2,3},{3,0},{4,5},{5,6},{6,7},{7,4},{8,9},{9,10},{10,1... | collective-permute-start | bytes 1228808 | tf_op jit(solution)/shard_map/ppermute | solution.py:160
  9.3 0.1 copy.9
  9.4 0.1 rem.301
  9.6 0.1 rem.276
  9.7 0.1 copy.10
  9.8 0.1 div.78
  9.9 0.1 div.73
  10.0 0.2 copy.8
  10.2 0.1 ne.313
  10.3 0.1 ne.303
  10.5 0.1 compare_convert_fusion
  10.6 0.7 reshape.807.live_ref
  11.3 17.0 %copy.15.values_ref = bf16[192,4,64,64]{3,2,1,0:T(8,128)(2,1)} copy(bf16[192,4,64,64]{0,3,2,1:T(8,128)(2,1)} %param.9) | data formatting | bytes 12582912 | tf_op args[0]
  28.3 0.6 stack.59.fix_ref
  28.9 0.6 fusion.32.own_pos_ref
  29.5 0.1 fusion.16
  29.7 1.7 %collective-permute-start.3 = (bf16[25,64,128]{2,1,0:T(8,128)(2,1)S(1)}, bf16[25,64,128]{2,1,0:T(8,128)(2,1)S(1)}, u32[]{:S(2)}, u32[]{:S(2)}) collective-permute-start(bf16[25,64,128]{2,1,0:T(8,128)(2,1)S(1)} %collective-permute-done.2.rest_12_), channel_id=1, source_target_pairs={{4,0},{8,4},{12,8},{16,12},{20,16},{24,20},{28,24},{0,28},{5,1},{9... | collective-permute-start | bytes 1228808 | tf_op jit(solution)/shard_map/ppermute | solution.py:172
  31.4 2.3 %collective-permute-start.14 = (bf16[25,64,128]{2,1,0:T(8,128)(2,1)}, bf16[25,64,128]{2,1,0:T(8,128)(2,1)S(1)}, u32[]{:S(2)}, u32[]{:S(2)}) collective-permute-start(bf16[25,64,128]{2,1,0:T(8,128)(2,1)} %collective-permute-done.13.rest_11_), channel_id=1, source_target_pairs={{0,4},{4,8},{8,12},{12,16},{16,20},{20,24},{24,28},{1,5},{5,9},{9,... | collective-permute-start | bytes 1228808 | tf_op jit(solution)/shard_map/ppermute | solution.py:172
  33.7 0.7 slice_bitcast_fusion.8
  34.4 3.2 %collective-permute-start.18 = (bf16[25,64,128]{2,1,0:T(8,128)(2,1)}, bf16[25,64,128]{2,1,0:T(8,128)(2,1)S(1)}, u32[]{:S(2)}, u32[]{:S(2)}) collective-permute-start(bf16[25,64,128]{2,1,0:T(8,128)(2,1)} %collective-permute-done.13.rest_11_), channel_id=1, source_target_pairs={{4,0},{8,4},{12,8},{16,12},{20,16},{24,20},{28,24},{5,1},{9,5},{13... | collective-permute-start | bytes 1228808 | tf_op jit(solution)/shard_map/ppermute | solution.py:172
  37.7 4.9 %collective-permute-start.10 = (bf16[25,64,128]{2,1,0:T(8,128)(2,1)}, bf16[25,64,128]{2,1,0:T(8,128)(2,1)S(1)}, u32[]{:S(2)}, u32[]{:S(2)}) collective-permute-start(bf16[25,64,128]{2,1,0:T(8,128)(2,1)} %collective-permute-done.9.rest_10_), channel_id=1, source_target_pairs={{0,4},{4,8},{8,12},{12,16},{16,20},{20,24},{24,28},{1,5},{5,9},{9,... | collective-permute-start | bytes 1228808 | tf_op jit(solution)/shard_map/ppermute | solution.py:172
  42.7 0.1 pad_maximum_fusion.1
  42.8 1.9 %collective-permute-start.12 = (bf16[2,25,64,128]{3,2,1,0:T(8,128)(2,1)S(1)}, bf16[2,25,64,128]{3,2,1,0:T(8,128)(2,1)S(1)}, u32[]{:S(2)}, u32[]{:S(2)}) collective-permute-start(bf16[2,25,64,128]{3,2,1,0:T(8,128)(2,1)S(1)} %pad_maximum_fusion.1), channel_id=1, source_target_pairs={{0,3},{1,0},{2,1},{3,2},{4,7},{5,4},{6,5},{7,6},{24,27},{25,24},{2... | collective-permute-start | bytes 2457608 | tf_op jit(solution)/shard_map/ppermute | solution.py:191
  44.7 0.7 slice_bitcast_fusion.9
  45.4 0.7 slice_bitcast_fusion.10
  46.1 2.5 %collective-permute-start.8 = (bf16[2,25,64,128]{3,2,1,0:T(8,128)(2,1)S(1)}, bf16[2,25,64,128]{3,2,1,0:T(8,128)(2,1)S(1)}, u32[]{:S(2)}, u32[]{:S(2)}) collective-permute-start(bf16[2,25,64,128]{3,2,1,0:T(8,128)(2,1)S(1)} %pad_maximum_fusion.1), channel_id=1, source_target_pairs={{0,2},{1,3},{2,0},{3,1},{4,6},{5,7},{6,4},{7,5},{24,26},{25,27},{2... | collective-permute-start | bytes 2457608 | tf_op jit(solution)/shard_map/ppermute | solution.py:191
  48.6 4.3 %collective-permute-start.15 = (bf16[25,64,128]{2,1,0:T(8,128)(2,1)S(1)}, bf16[25,64,128]{2,1,0:T(8,128)(2,1)S(1)}, u32[]{:S(2)}, u32[]{:S(2)}) collective-permute-start(bf16[25,64,128]{2,1,0:T(8,128)(2,1)S(1)} %collective-permute-done.14.rest_7_), channel_id=1, source_target_pairs={{4,8},{8,12},{12,16},{16,20},{20,24},{24,28},{5,9},{9,13},{13,17},... | collective-permute-start | bytes 1228808 | tf_op jit(solution)/shard_map/ppermute | solution.py:172
  52.9 1.3 collective-permute-start.21
  54.2 4.8 %collective-permute-start.4 = (bf16[2,25,64,128]{3,2,1,0:T(8,128)(2,1)S(1)}, bf16[2,25,64,128]{3,2,1,0:T(8,128)(2,1)S(1)}, u32[]{:S(2)}, u32[]{:S(2)}) collective-permute-start(bf16[2,25,64,128]{3,2,1,0:T(8,128)(2,1)S(1)} %pad_maximum_fusion.1), channel_id=1, source_target_pairs={{0,1},{1,2},{2,3},{3,0},{4,5},{5,6},{6,7},{7,4},{24,25},{25,26},{2... | collective-permute-start | bytes 2457608 | tf_op jit(solution)/shard_map/ppermute | solution.py:191
  59.0 1.9 %collective-permute-start.17 = (bf16[25,64,128]{2,1,0:T(8,128)(2,1)}, bf16[25,64,128]{2,1,0:T(8,128)(2,1)S(1)}, u32[]{:S(2)}, u32[]{:S(2)}) collective-permute-start(bf16[25,64,128]{2,1,0:T(8,128)(2,1)} %collective-permute-done.9.rest_10_), channel_id=1, source_target_pairs={{4,0},{8,4},{12,8},{16,12},{20,16},{24,20},{28,24},{5,1},{9,5},{13... | collective-permute-start | bytes 1228808 | tf_op jit(solution)/shard_map/ppermute | solution.py:172
  61.0 2.4 %collective-permute-start.16 = (bf16[25,64,128]{2,1,0:T(8,128)(2,1)}, bf16[25,64,128]{2,1,0:T(8,128)(2,1)S(1)}, u32[]{:S(2)}, u32[]{:S(2)}) collective-permute-start(bf16[25,64,128]{2,1,0:T(8,128)(2,1)} %collective-permute-done.5.rest_9_), channel_id=1, source_target_pairs={{4,0},{8,4},{12,8},{16,12},{20,16},{24,20},{28,24},{5,1},{9,5},{13... | collective-permute-start | bytes 1228808 | tf_op jit(solution)/shard_map/ppermute | solution.py:172
  63.4 1.7 %collective-permute-done.12.rest_22_ = bf16[2,25,64,128]{3,2,1,0:T(8,128)(2,1)S(1)} collective-permute-done((bf16[2,25,64,128]{3,2,1,0:T(8,128)(2,1)S(1)}, bf16[2,25,64,128]{3,2,1,0:T(8,128)(2,1)S(1)}, u32[]{:S(2)}, u32[]{:S(2)}) %collective-permute-start.12) | collective-permute-done | bytes 819232 | tf_op jit(solution)/shard_map/ppermute | solution.py:191
  65.1 5.1 %collective-permute-start.6 = (bf16[25,64,128]{2,1,0:T(8,128)(2,1)}, bf16[25,64,128]{2,1,0:T(8,128)(2,1)S(1)}, u32[]{:S(2)}, u32[]{:S(2)}) collective-permute-start(bf16[25,64,128]{2,1,0:T(8,128)(2,1)} %collective-permute-done.5.rest_9_), channel_id=1, source_target_pairs={{0,4},{4,8},{8,12},{12,16},{16,20},{20,24},{24,28},{1,5},{5,9},{9,... | collective-permute-start | bytes 1228808 | tf_op jit(solution)/shard_map/ppermute | solution.py:172
  70.2 1.9 %collective-permute-start.11 = (bf16[25,64,128]{2,1,0:T(8,128)(2,1)S(1)}, bf16[25,64,128]{2,1,0:T(8,128)(2,1)S(1)}, u32[]{:S(2)}, u32[]{:S(2)}) collective-permute-start(bf16[25,64,128]{2,1,0:T(8,128)(2,1)S(1)} %collective-permute-done.10.rest_6_), channel_id=1, source_target_pairs={{4,8},{8,12},{12,16},{16,20},{20,24},{24,28},{5,9},{9,13},{13,17},... | collective-permute-start | bytes 1228808 | tf_op jit(solution)/shard_map/ppermute | solution.py:172
  72.2 3.7 %collective-permute-start.20 = (bf16[25,64,128]{2,1,0:T(8,128)(2,1)S(1)}, bf16[25,64,128]{2,1,0:T(8,128)(2,1)S(1)}, u32[]{:S(2)}, u32[]{:S(2)}) collective-permute-start(bf16[25,64,128]{2,1,0:T(8,128)(2,1)S(1)} %collective-permute-done.17.rest_14_), channel_id=1, source_target_pairs={{4,0},{8,4},{12,8},{16,12},{20,16},{24,20},{5,1},{9,5},{13,9},{17,... | collective-permute-start | bytes 1228808 | tf_op jit(solution)/shard_map/ppermute | solution.py:172
  75.9 1.9 %collective-permute-start.19 = (bf16[25,64,128]{2,1,0:T(8,128)(2,1)S(1)}, bf16[25,64,128]{2,1,0:T(8,128)(2,1)S(1)}, u32[]{:S(2)}, u32[]{:S(2)}) collective-permute-start(bf16[25,64,128]{2,1,0:T(8,128)(2,1)S(1)} %collective-permute-done.16.rest_13_), channel_id=1, source_target_pairs={{4,0},{8,4},{12,8},{16,12},{20,16},{24,20},{5,1},{9,5},{13,9},{17,... | collective-permute-start | bytes 1228808 | tf_op jit(solution)/shard_map/ppermute | solution.py:172
  77.8 6.4 %collective-permute-done.8.rest_21_ = bf16[2,25,64,128]{3,2,1,0:T(8,128)(2,1)S(1)} collective-permute-done((bf16[2,25,64,128]{3,2,1,0:T(8,128)(2,1)S(1)}, bf16[2,25,64,128]{3,2,1,0:T(8,128)(2,1)S(1)}, u32[]{:S(2)}, u32[]{:S(2)}) %collective-permute-start.8) | collective-permute-done | bytes 819232 | tf_op jit(solution)/shard_map/ppermute | solution.py:191
  84.2 2.0 %collective-permute-start.7 = (bf16[25,64,128]{2,1,0:T(8,128)(2,1)S(1)}, bf16[25,64,128]{2,1,0:T(8,128)(2,1)S(1)}, u32[]{:S(2)}, u32[]{:S(2)}) collective-permute-start(bf16[25,64,128]{2,1,0:T(8,128)(2,1)S(1)} %collective-permute-done.6.rest_5_), channel_id=1, source_target_pairs={{4,8},{8,12},{12,16},{16,20},{20,24},{24,28},{5,9},{9,13},{13,17},... | collective-permute-start | bytes 1228808 | tf_op jit(solution)/shard_map/ppermute | solution.py:172
  86.3 7.1 %collective-permute-done.7.rest_1_ = bf16[25,64,128]{2,1,0:T(8,128)(2,1)S(1)} collective-permute-done((bf16[25,64,128]{2,1,0:T(8,128)(2,1)S(1)}, bf16[25,64,128]{2,1,0:T(8,128)(2,1)S(1)}, u32[]{:S(2)}, u32[]{:S(2)}) %collective-permute-start.7) | collective-permute-done | bytes 409632 | tf_op jit(solution)/shard_map/ppermute | solution.py:172
  93.5 0.7 copy-done.19
  94.2 0.1 stack.54
  94.3 0.1 reshape.806
  94.4 3.2 %gather_fusion = s32[768]{0:T(1024)S(1)} fusion(s32[960]{0:T(1024)S(1)} %reshape.806, s32[1024]{0:T(1024)S(1)} %pad_clamp_fusion.1), kind=kCustom, calls=%fused_computation | custom fusion | bytes 9216 | tf_op jit(solution)/shard_map/jit(_take)/gather | solution.py:226
  97.6 1.2 gather_fusion.1
  98.8 0.1 broadcast_in_dim.32
  98.9 0.1 reshape.740
  99.0 0.6 multiply_add_fusion
  99.7 0.6 fusion.11.pair_ref
  100.3 23.2 %shard_map.55 = f32[64,64,128]{2,1,0:T(8,128)} custom-call(s32[768]{0:T(1024)} %fusion.11.pair_ref, s32[768]{0:T(1024)} %get-tuple-element.45.half_ref, s32[768]{0:T(1024)} %get-tuple-element.29.target_ref, s32[768]{0:T(1024)} %reshape.807.live_ref, s32[192]{0:T(256)} %fusion.32.own_pos_ref, s32[5]{0:T(128)} %stack.59.fix_ref, ...), custom_call_target="tpu_custom_call" | custom-call | tf_op jit(solution)/shard_map/pallas_call | solution.py:110
  123.5 1.6 %bitcast_convert_fusion.2 = (bf16[8,2,64,128]{3,2,1,0:T(8,128)(2,1)S(1)}, bf16[8,2,64,128]{3,2,1,0:T(8,128)(2,1)S(1)}, bf16[8,2,64,128]{3,2,1,0:T(8,128)(2,1)S(1)}) fusion(f32[4,8,2,64,128]{4,3,2,1,0:T(8,128)} %bitcast.141, s32[]{:T(128)S(6)} %select_n.678, pred[]{:T(512)S(6)} %and.252, s32[]{:T(128)S(6)} %select_n.682, pred[]{:T(512)S(6)} %and.254, ...), kind=kLoop, calls=%fused_computation.9 | loop fusion | flops 393216 | bytes 1572879 | tf_op jit(solution)/shard_map/convert_element_type | solution.py:254
  125.1 4.0 %collective-permute-start.22 = (bf16[8,2,64,128]{3,2,1,0:T(8,128)(2,1)S(1)}, bf16[8,2,64,128]{3,2,1,0:T(8,128)(2,1)S(1)}, u32[]{:S(2)}, u32[]{:S(2)}) collective-permute-start(bf16[8,2,64,128]{3,2,1,0:T(8,128)(2,1)S(1)} %get-tuple-element.31), channel_id=1, source_target_pairs={{0,1},{1,2},{2,3},{3,0},{4,5},{5,6},{6,7},{7,4},{8,9},{9,10},{10,1... | collective-permute-start | bytes 786440 | tf_op jit(solution)/shard_map/ppermute | solution.py:253
  129.1 0.5 collective-permute-start.23
  129.6 0.1 collective-permute-start.24
  129.7 4.1 %collective-permute-done.22 = bf16[8,2,64,128]{3,2,1,0:T(8,128)(2,1)S(1)} collective-permute-done((bf16[8,2,64,128]{3,2,1,0:T(8,128)(2,1)S(1)}, bf16[8,2,64,128]{3,2,1,0:T(8,128)(2,1)S(1)}, u32[]{:S(2)}, u32[]{:S(2)}) %collective-permute-start.22) | collective-permute-done | bytes 262176 | tf_op jit(solution)/shard_map/ppermute | solution.py:253
  133.9 4.4 %collective-permute-done.23 = bf16[8,2,64,128]{3,2,1,0:T(8,128)(2,1)S(1)} collective-permute-done((bf16[8,2,64,128]{3,2,1,0:T(8,128)(2,1)S(1)}, bf16[8,2,64,128]{3,2,1,0:T(8,128)(2,1)S(1)}, u32[]{:S(2)}, u32[]{:S(2)}) %collective-permute-start.23) | collective-permute-done | bytes 262176 | tf_op jit(solution)/shard_map/ppermute | solution.py:253
  138.3 1.2 fusion.2
  139.5 0.2 fusion.46
  139.7 1.1 pad_maximum_fusion
  (86 shorter events, 0.5 us)
Async XLA Ops:
  0.0 9.3 %copy-start.20 = (s32[192,4]{0,1:T(4,128)S(1)}, s32[192,4]{0,1:T(4,128)}, u32[]{:S(2)}) copy-start(s32[192,4]{0,1:T(4,128)} %param.10) | copy-start | bytes 9220
  0.7 9.9 %copy-start.21 = (s32[192]{0:T(256)S(1)}, s32[192]{0:T(256)}, u32[]{:S(2)}) copy-start(s32[192]{0:T(256)} %param.11) | copy-start | bytes 2308
  3.0 25.3 %copy-start.4 = (bf16[25,64,128]{2,1,0:T(8,128)(2,1)}, bf16[25,64,128]{2,1,0:T(8,128)(2,1)S(1)}, u32[]{:S(2)}) copy-start(bf16[25,64,128]{2,1,0:T(8,128)(2,1)S(1)} %fusion.3.rest_8_) | copy-start | bytes 1228804
  3.0 26.5 %collective-permute-start = (bf16[25,64,128]{2,1,0:T(8,128)(2,1)S(1)}, bf16[25,64,128]{2,1,0:T(8,128)(2,1)S(1)}, u32[]{:S(2)}, u32[]{:S(2)}) collective-permute-start(bf16[25,64,128]{2,1,0:T(8,128)(2,1)S(1)} %fusion.3.rest_8_), channel_id=1, source_target_pairs={{28,0},{0,4},{4,8},{8,12},{12,16},{16,20},{20,24},{24,28},{29,1},{... | collective-permute-start | bytes 1228808 | tf_op jit(solution)/shard_map/ppermute | solution.py:172
  3.1 26.5 %collective-permute-start.2 = (bf16[25,64,128]{2,1,0:T(8,128)(2,1)S(1)}, bf16[25,64,128]{2,1,0:T(8,128)(2,1)S(1)}, u32[]{:S(2)}, u32[]{:S(2)}) collective-permute-start(bf16[25,64,128]{2,1,0:T(8,128)(2,1)S(1)} %fusion.3.rest_8_), channel_id=1, source_target_pairs={{4,0},{8,4},{12,8},{16,12},{20,16},{24,20},{28,24},{0,28},{5,1},{9... | collective-permute-start | bytes 1228808 | tf_op jit(solution)/shard_map/ppermute | solution.py:172
  4.8 26.6 %collective-permute-start.13 = (bf16[25,64,128]{2,1,0:T(8,128)(2,1)S(1)}, bf16[25,64,128]{2,1,0:T(8,128)(2,1)}, u32[]{:S(2)}, u32[]{:S(2)}) collective-permute-start(bf16[25,64,128]{2,1,0:T(8,128)(2,1)S(1)} %fusion.3.rest_8_), channel_id=1, source_target_pairs={{0,3},{1,0},{2,1},{3,2},{4,7},{5,4},{6,5},{7,6},{8,11},{9,8},{10,9... | collective-permute-start | bytes 1228808 | tf_op jit(solution)/shard_map/ppermute | solution.py:160
  5.4 29.1 %collective-permute-start.9 = (bf16[25,64,128]{2,1,0:T(8,128)(2,1)S(1)}, bf16[25,64,128]{2,1,0:T(8,128)(2,1)}, u32[]{:S(2)}, u32[]{:S(2)}) collective-permute-start(bf16[25,64,128]{2,1,0:T(8,128)(2,1)S(1)} %fusion.3.rest_8_), channel_id=1, source_target_pairs={{0,2},{1,3},{2,0},{3,1},{4,6},{5,7},{6,4},{7,5},{8,10},{9,11},{10,... | collective-permute-start | bytes 1228808 | tf_op jit(solution)/shard_map/ppermute | solution.py:160
  6.9 38.5 %collective-permute-start.5 = (bf16[25,64,128]{2,1,0:T(8,128)(2,1)S(1)}, bf16[25,64,128]{2,1,0:T(8,128)(2,1)}, u32[]{:S(2)}, u32[]{:S(2)}) collective-permute-start(bf16[25,64,128]{2,1,0:T(8,128)(2,1)S(1)} %fusion.3.rest_8_), channel_id=1, source_target_pairs={{0,1},{1,2},{2,3},{3,0},{4,5},{5,6},{6,7},{7,4},{8,9},{9,10},{10,1... | collective-permute-start | bytes 1228808 | tf_op jit(solution)/shard_map/ppermute | solution.py:160
  29.6 64.7 %copy-start = (bf16[25,64,128]{2,1,0:T(8,128)(2,1)}, bf16[25,64,128]{2,1,0:T(8,128)(2,1)S(1)}, u32[]{:S(2)}) copy-start(bf16[25,64,128]{2,1,0:T(8,128)(2,1)S(1)} %collective-permute-done.rest_4_) | copy-start | bytes 1228804
  29.6 8.1 %collective-permute-start.1 = (bf16[25,64,128]{2,1,0:T(8,128)(2,1)S(1)}, bf16[25,64,128]{2,1,0:T(8,128)(2,1)S(1)}, u32[]{:S(2)}, u32[]{:S(2)}) collective-permute-start(bf16[25,64,128]{2,1,0:T(8,128)(2,1)S(1)} %collective-permute-done.rest_4_), channel_id=1, source_target_pairs={{28,0},{0,4},{4,8},{8,12},{12,16},{16,20},{20,24},{24,28},{29,1},{... | collective-permute-start | bytes 1228808 | tf_op jit(solution)/shard_map/ppermute | solution.py:172
  29.7 64.7 %copy-start.1 = (bf16[25,64,128]{2,1,0:T(8,128)(2,1)}, bf16[25,64,128]{2,1,0:T(8,128)(2,1)S(1)}, u32[]{:S(2)}) copy-start(bf16[25,64,128]{2,1,0:T(8,128)(2,1)S(1)} %collective-permute-done.2.rest_12_) | copy-start | bytes 1228804
  29.7 13.0 %collective-permute-start.3 = (bf16[25,64,128]{2,1,0:T(8,128)(2,1)S(1)}, bf16[25,64,128]{2,1,0:T(8,128)(2,1)S(1)}, u32[]{:S(2)}, u32[]{:S(2)}) collective-permute-start(bf16[25,64,128]{2,1,0:T(8,128)(2,1)S(1)} %collective-permute-done.2.rest_12_), channel_id=1, source_target_pairs={{4,0},{8,4},{12,8},{16,12},{20,16},{24,20},{28,24},{0,28},{5,1},{9... | collective-permute-start | bytes 1228808 | tf_op jit(solution)/shard_map/ppermute | solution.py:172
  31.4 17.2 %collective-permute-start.14 = (bf16[25,64,128]{2,1,0:T(8,128)(2,1)}, bf16[25,64,128]{2,1,0:T(8,128)(2,1)S(1)}, u32[]{:S(2)}, u32[]{:S(2)}) collective-permute-start(bf16[25,64,128]{2,1,0:T(8,128)(2,1)} %collective-permute-done.13.rest_11_), channel_id=1, source_target_pairs={{0,4},{4,8},{8,12},{12,16},{16,20},{20,24},{24,28},{1,5},{5,9},{9,... | collective-permute-start | bytes 1228808 | tf_op jit(solution)/shard_map/ppermute | solution.py:172
  34.4 18.4 %collective-permute-start.18 = (bf16[25,64,128]{2,1,0:T(8,128)(2,1)}, bf16[25,64,128]{2,1,0:T(8,128)(2,1)S(1)}, u32[]{:S(2)}, u32[]{:S(2)}) collective-permute-start(bf16[25,64,128]{2,1,0:T(8,128)(2,1)} %collective-permute-done.13.rest_11_), channel_id=1, source_target_pairs={{4,0},{8,4},{12,8},{16,12},{20,16},{24,20},{28,24},{5,1},{9,5},{13... | collective-permute-start | bytes 1228808 | tf_op jit(solution)/shard_map/ppermute | solution.py:172
  37.7 59.9 %copy-start.2 = (bf16[25,64,128]{2,1,0:T(8,128)(2,1)}, bf16[25,64,128]{2,1,0:T(8,128)(2,1)S(1)}, u32[]{:S(2)}) copy-start(bf16[25,64,128]{2,1,0:T(8,128)(2,1)S(1)} %collective-permute-done.1.rest_0_) | copy-start | bytes 1228804
  37.7 16.5 %collective-permute-start.10 = (bf16[25,64,128]{2,1,0:T(8,128)(2,1)}, bf16[25,64,128]{2,1,0:T(8,128)(2,1)S(1)}, u32[]{:S(2)}, u32[]{:S(2)}) collective-permute-start(bf16[25,64,128]{2,1,0:T(8,128)(2,1)} %collective-permute-done.9.rest_10_), channel_id=1, source_target_pairs={{0,4},{4,8},{8,12},{12,16},{16,20},{20,24},{24,28},{1,5},{5,9},{9,... | collective-permute-start | bytes 1228808 | tf_op jit(solution)/shard_map/ppermute | solution.py:172
  42.7 54.9 %copy-start.3 = (bf16[25,64,128]{2,1,0:T(8,128)(2,1)}, bf16[25,64,128]{2,1,0:T(8,128)(2,1)S(1)}, u32[]{:S(2)}) copy-start(bf16[25,64,128]{2,1,0:T(8,128)(2,1)S(1)} %collective-permute-done.3.rest_16_) | copy-start | bytes 1228804
  42.8 22.3 %collective-permute-start.12 = (bf16[2,25,64,128]{3,2,1,0:T(8,128)(2,1)S(1)}, bf16[2,25,64,128]{3,2,1,0:T(8,128)(2,1)S(1)}, u32[]{:S(2)}, u32[]{:S(2)}) collective-permute-start(bf16[2,25,64,128]{3,2,1,0:T(8,128)(2,1)S(1)} %pad_maximum_fusion.1), channel_id=1, source_target_pairs={{0,3},{1,0},{2,1},{3,2},{4,7},{5,4},{6,5},{7,6},{24,27},{25,24},{2... | collective-permute-start | bytes 2457608 | tf_op jit(solution)/shard_map/ppermute | solution.py:191
  46.1 38.1 %collective-permute-start.8 = (bf16[2,25,64,128]{3,2,1,0:T(8,128)(2,1)S(1)}, bf16[2,25,64,128]{3,2,1,0:T(8,128)(2,1)S(1)}, u32[]{:S(2)}, u32[]{:S(2)}) collective-permute-start(bf16[2,25,64,128]{3,2,1,0:T(8,128)(2,1)S(1)} %pad_maximum_fusion.1), channel_id=1, source_target_pairs={{0,2},{1,3},{2,0},{3,1},{4,6},{5,7},{6,4},{7,5},{24,26},{25,27},{2... | collective-permute-start | bytes 2457608 | tf_op jit(solution)/shard_map/ppermute | solution.py:191
  48.6 51.7 %copy-start.8 = (bf16[25,64,128]{2,1,0:T(8,128)(2,1)}, bf16[25,64,128]{2,1,0:T(8,128)(2,1)S(1)}, u32[]{:S(2)}) copy-start(bf16[25,64,128]{2,1,0:T(8,128)(2,1)S(1)} %collective-permute-done.14.rest_7_) | copy-start | bytes 1228804
  48.6 10.4 %collective-permute-start.15 = (bf16[25,64,128]{2,1,0:T(8,128)(2,1)S(1)}, bf16[25,64,128]{2,1,0:T(8,128)(2,1)S(1)}, u32[]{:S(2)}, u32[]{:S(2)}) collective-permute-start(bf16[25,64,128]{2,1,0:T(8,128)(2,1)S(1)} %collective-permute-done.14.rest_7_), channel_id=1, source_target_pairs={{4,8},{8,12},{12,16},{16,20},{20,24},{24,28},{5,9},{9,13},{13,17},... | collective-permute-start | bytes 1228808 | tf_op jit(solution)/shard_map/ppermute | solution.py:172
  52.9 40.6 %copy-start.9 = (bf16[25,64,128]{2,1,0:T(8,128)(2,1)}, bf16[25,64,128]{2,1,0:T(8,128)(2,1)S(1)}, u32[]{:S(2)}) copy-start(bf16[25,64,128]{2,1,0:T(8,128)(2,1)S(1)} %collective-permute-done.18.rest_15_) | copy-start | bytes 1228804
  52.9 8.1 %collective-permute-start.21 = (bf16[25,64,128]{2,1,0:T(8,128)(2,1)S(1)}, bf16[25,64,128]{2,1,0:T(8,128)(2,1)S(1)}, u32[]{:S(2)}, u32[]{:S(2)}) collective-permute-start(bf16[25,64,128]{2,1,0:T(8,128)(2,1)S(1)} %collective-permute-done.18.rest_15_), channel_id=1, source_target_pairs={{4,0},{8,4},{12,8},{16,12},{20,16},{24,20},{5,1},{9,5},{13,9},{17,... | collective-permute-start | bytes 1228808 | tf_op jit(solution)/shard_map/ppermute | solution.py:172
  54.2 39.2 %copy-start.10 = (bf16[25,64,128]{2,1,0:T(8,128)(2,1)}, bf16[25,64,128]{2,1,0:T(8,128)(2,1)S(1)}, u32[]{:S(2)}) copy-start(bf16[25,64,128]{2,1,0:T(8,128)(2,1)S(1)} %collective-permute-done.10.rest_6_) | copy-start | bytes 1228804
  54.2 32.0 %collective-permute-start.4 = (bf16[2,25,64,128]{3,2,1,0:T(8,128)(2,1)S(1)}, bf16[2,25,64,128]{3,2,1,0:T(8,128)(2,1)S(1)}, u32[]{:S(2)}, u32[]{:S(2)}) collective-permute-start(bf16[2,25,64,128]{3,2,1,0:T(8,128)(2,1)S(1)} %pad_maximum_fusion.1), channel_id=1, source_target_pairs={{0,1},{1,2},{2,3},{3,0},{4,5},{5,6},{6,7},{7,4},{24,25},{25,26},{2... | collective-permute-start | bytes 2457608 | tf_op jit(solution)/shard_map/ppermute | solution.py:191
  59.0 41.2 %copy-start.11 = (bf16[25,64,128]{2,1,0:T(8,128)(2,1)}, bf16[25,64,128]{2,1,0:T(8,128)(2,1)S(1)}, u32[]{:S(2)}) copy-start(bf16[25,64,128]{2,1,0:T(8,128)(2,1)S(1)} %collective-permute-done.15.rest_3_) | copy-start | bytes 1228804
  59.0 11.2 %collective-permute-start.17 = (bf16[25,64,128]{2,1,0:T(8,128)(2,1)}, bf16[25,64,128]{2,1,0:T(8,128)(2,1)S(1)}, u32[]{:S(2)}, u32[]{:S(2)}) collective-permute-start(bf16[25,64,128]{2,1,0:T(8,128)(2,1)} %collective-permute-done.9.rest_10_), channel_id=1, source_target_pairs={{4,0},{8,4},{12,8},{16,12},{20,16},{24,20},{28,24},{5,1},{9,5},{13... | collective-permute-start | bytes 1228808 | tf_op jit(solution)/shard_map/ppermute | solution.py:172
  61.0 32.5 %copy-start.12 = (bf16[25,64,128]{2,1,0:T(8,128)(2,1)}, bf16[25,64,128]{2,1,0:T(8,128)(2,1)S(1)}, u32[]{:S(2)}) copy-start(bf16[25,64,128]{2,1,0:T(8,128)(2,1)S(1)} %collective-permute-done.21.rest_19_) | copy-start | bytes 1228804
  61.0 11.2 %collective-permute-start.16 = (bf16[25,64,128]{2,1,0:T(8,128)(2,1)}, bf16[25,64,128]{2,1,0:T(8,128)(2,1)S(1)}, u32[]{:S(2)}, u32[]{:S(2)}) collective-permute-start(bf16[25,64,128]{2,1,0:T(8,128)(2,1)} %collective-permute-done.5.rest_9_), channel_id=1, source_target_pairs={{4,0},{8,4},{12,8},{16,12},{20,16},{24,20},{28,24},{5,1},{9,5},{13... | collective-permute-start | bytes 1228808 | tf_op jit(solution)/shard_map/ppermute | solution.py:172
  65.1 32.5 %copy-start.5 = (bf16[2,25,64,128]{3,2,1,0:T(8,128)(2,1)}, bf16[2,25,64,128]{3,2,1,0:T(8,128)(2,1)S(1)}, u32[]{:S(2)}) copy-start(bf16[2,25,64,128]{3,2,1,0:T(8,128)(2,1)S(1)} %collective-permute-done.12.rest_22_) | copy-start | bytes 2457604
  65.1 10.8 %collective-permute-start.6 = (bf16[25,64,128]{2,1,0:T(8,128)(2,1)}, bf16[25,64,128]{2,1,0:T(8,128)(2,1)S(1)}, u32[]{:S(2)}, u32[]{:S(2)}) collective-permute-start(bf16[25,64,128]{2,1,0:T(8,128)(2,1)} %collective-permute-done.5.rest_9_), channel_id=1, source_target_pairs={{0,4},{4,8},{8,12},{12,16},{16,20},{20,24},{24,28},{1,5},{5,9},{9,... | collective-permute-start | bytes 1228808 | tf_op jit(solution)/shard_map/ppermute | solution.py:172
  70.2 23.3 %copy-start.13 = (bf16[25,64,128]{2,1,0:T(8,128)(2,1)}, bf16[25,64,128]{2,1,0:T(8,128)(2,1)S(1)}, u32[]{:S(2)}) copy-start(bf16[25,64,128]{2,1,0:T(8,128)(2,1)S(1)} %collective-permute-done.17.rest_14_) | copy-start | bytes 1228804
  70.2 16.0 %collective-permute-start.11 = (bf16[25,64,128]{2,1,0:T(8,128)(2,1)S(1)}, bf16[25,64,128]{2,1,0:T(8,128)(2,1)S(1)}, u32[]{:S(2)}, u32[]{:S(2)}) collective-permute-start(bf16[25,64,128]{2,1,0:T(8,128)(2,1)S(1)} %collective-permute-done.10.rest_6_), channel_id=1, source_target_pairs={{4,8},{8,12},{12,16},{16,20},{20,24},{24,28},{5,9},{9,13},{13,17},... | collective-permute-start | bytes 1228808 | tf_op jit(solution)/shard_map/ppermute | solution.py:172
  72.2 21.3 %copy-start.14 = (bf16[25,64,128]{2,1,0:T(8,128)(2,1)}, bf16[25,64,128]{2,1,0:T(8,128)(2,1)S(1)}, u32[]{:S(2)}) copy-start(bf16[25,64,128]{2,1,0:T(8,128)(2,1)S(1)} %collective-permute-done.16.rest_13_) | copy-start | bytes 1228804
  72.2 14.1 %collective-permute-start.20 = (bf16[25,64,128]{2,1,0:T(8,128)(2,1)S(1)}, bf16[25,64,128]{2,1,0:T(8,128)(2,1)S(1)}, u32[]{:S(2)}, u32[]{:S(2)}) collective-permute-start(bf16[25,64,128]{2,1,0:T(8,128)(2,1)S(1)} %collective-permute-done.17.rest_14_), channel_id=1, source_target_pairs={{4,0},{8,4},{12,8},{16,12},{20,16},{24,20},{5,1},{9,5},{13,9},{17,... | collective-permute-start | bytes 1228808 | tf_op jit(solution)/shard_map/ppermute | solution.py:172
  75.9 17.6 %copy-start.15 = (bf16[25,64,128]{2,1,0:T(8,128)(2,1)}, bf16[25,64,128]{2,1,0:T(8,128)(2,1)S(1)}, u32[]{:S(2)}) copy-start(bf16[25,64,128]{2,1,0:T(8,128)(2,1)S(1)} %collective-permute-done.6.rest_5_) | copy-start | bytes 1228804
  75.9 10.4 %collective-permute-start.19 = (bf16[25,64,128]{2,1,0:T(8,128)(2,1)S(1)}, bf16[25,64,128]{2,1,0:T(8,128)(2,1)S(1)}, u32[]{:S(2)}, u32[]{:S(2)}) collective-permute-start(bf16[25,64,128]{2,1,0:T(8,128)(2,1)S(1)} %collective-permute-done.16.rest_13_), channel_id=1, source_target_pairs={{4,0},{8,4},{12,8},{16,12},{20,16},{24,20},{5,1},{9,5},{13,9},{17,... | collective-permute-start | bytes 1228808 | tf_op jit(solution)/shard_map/ppermute | solution.py:172
  84.2 2.1 %copy-start.6 = (bf16[2,25,64,128]{3,2,1,0:T(8,128)(2,1)}, bf16[2,25,64,128]{3,2,1,0:T(8,128)(2,1)S(1)}, u32[]{:S(2)}) copy-start(bf16[2,25,64,128]{3,2,1,0:T(8,128)(2,1)S(1)} %collective-permute-done.8.rest_21_) | copy-start | bytes 2457604
  84.2 9.3 %collective-permute-start.7 = (bf16[25,64,128]{2,1,0:T(8,128)(2,1)S(1)}, bf16[25,64,128]{2,1,0:T(8,128)(2,1)S(1)}, u32[]{:S(2)}, u32[]{:S(2)}) collective-permute-start(bf16[25,64,128]{2,1,0:T(8,128)(2,1)S(1)} %collective-permute-done.6.rest_5_), channel_id=1, source_target_pairs={{4,8},{8,12},{12,16},{16,20},{20,24},{24,28},{5,9},{9,13},{13,17},... | collective-permute-start | bytes 1228808 | tf_op jit(solution)/shard_map/ppermute | solution.py:172
  86.2 7.2 %copy-start.7 = (bf16[2,25,64,128]{3,2,1,0:T(8,128)(2,1)}, bf16[2,25,64,128]{3,2,1,0:T(8,128)(2,1)S(1)}, u32[]{:S(2)}) copy-start(bf16[2,25,64,128]{3,2,1,0:T(8,128)(2,1)S(1)} %collective-permute-done.4.rest_20_) | copy-start | bytes 2457604
  86.3 7.3 %copy-start.16 = (bf16[25,64,128]{2,1,0:T(8,128)(2,1)}, bf16[25,64,128]{2,1,0:T(8,128)(2,1)S(1)}, u32[]{:S(2)}) copy-start(bf16[25,64,128]{2,1,0:T(8,128)(2,1)S(1)} %collective-permute-done.11.rest_2_) | copy-start | bytes 1228804
  86.3 7.2 %copy-start.17 = (bf16[25,64,128]{2,1,0:T(8,128)(2,1)}, bf16[25,64,128]{2,1,0:T(8,128)(2,1)S(1)}, u32[]{:S(2)}) copy-start(bf16[25,64,128]{2,1,0:T(8,128)(2,1)S(1)} %collective-permute-done.20.rest_18_) | copy-start | bytes 1228804
  86.3 7.2 %copy-start.18 = (bf16[25,64,128]{2,1,0:T(8,128)(2,1)}, bf16[25,64,128]{2,1,0:T(8,128)(2,1)S(1)}, u32[]{:S(2)}) copy-start(bf16[25,64,128]{2,1,0:T(8,128)(2,1)S(1)} %collective-permute-done.19.rest_17_) | copy-start | bytes 1228804
  93.4 0.8 copy-start.19
  125.1 8.8 %collective-permute-start.22 = (bf16[8,2,64,128]{3,2,1,0:T(8,128)(2,1)S(1)}, bf16[8,2,64,128]{3,2,1,0:T(8,128)(2,1)S(1)}, u32[]{:S(2)}, u32[]{:S(2)}) collective-permute-start(bf16[8,2,64,128]{3,2,1,0:T(8,128)(2,1)S(1)} %get-tuple-element.31), channel_id=1, source_target_pairs={{0,1},{1,2},{2,3},{3,0},{4,5},{5,6},{6,7},{7,4},{8,9},{9,10},{10,1... | collective-permute-start | bytes 786440 | tf_op jit(solution)/shard_map/ppermute | solution.py:253
  129.1 9.2 %collective-permute-start.23 = (bf16[8,2,64,128]{3,2,1,0:T(8,128)(2,1)S(1)}, bf16[8,2,64,128]{3,2,1,0:T(8,128)(2,1)S(1)}, u32[]{:S(2)}, u32[]{:S(2)}) collective-permute-start(bf16[8,2,64,128]{3,2,1,0:T(8,128)(2,1)S(1)} %get-tuple-element.33), channel_id=1, source_target_pairs={{0,2},{1,3},{2,0},{3,1},{4,6},{5,7},{6,4},{7,5},{8,10},{9,11},{10,... | collective-permute-start | bytes 786440 | tf_op jit(solution)/shard_map/ppermute | solution.py:253
  129.6 8.7 %collective-permute-start.24 = (bf16[8,2,64,128]{3,2,1,0:T(8,128)(2,1)S(1)}, bf16[8,2,64,128]{3,2,1,0:T(8,128)(2,1)S(1)}, u32[]{:S(2)}, u32[]{:S(2)}) collective-permute-start(bf16[8,2,64,128]{3,2,1,0:T(8,128)(2,1)S(1)} %get-tuple-element.32), channel_id=1, source_target_pairs={{0,3},{1,0},{2,1},{3,2},{4,7},{5,4},{6,5},{7,6},{8,11},{9,8},{10,9... | collective-permute-start | bytes 786440 | tf_op jit(solution)/shard_map/ppermute | solution.py:253

commit v16 on v15

--- a/solution.py
+++ b/solution.py
@@ -233,6 +233,7 @@
     target = fetched_aggs * CB + jnp.broadcast_to(
         local_coarse[:, None], (panel_length, slots_here)
     ).reshape(slot_total)
+    block_values, _ = lax.optimization_barrier((block_values, down1[-1]))
     summed = coarse_partial(
         window_pair.astype(jnp.int32),
         (within % 2).astype(jnp.int32),

time: 142 us -> 142 us (level)
  the two profiles are of different devices: /device:TPU:26 before, /device:TPU:19 now
where the time goes in v16:
time: 142 us; the launch traced here: 141 us
  starting transfers between devices  52.6 us (37%)
  local copies, waits for them, and re-layouts  29.8 us (21%)
  waiting for transfers between devices  24.5 us (17%)
  Pallas kernels  23.2 us (16%)
  other arithmetic  9.73 us (7%)
    ppermute x16, starting transfers between devices, ring(): return lax.ppermute(piece, 'blk', route)  43.3 us
    pallas_call x1, Pallas kernels, coarse_partial(): pl.pallas_call(coarse_kernel, out_shape=jax.ShapeDtypeStruct((n_targets /...  23.2 us
    optimization_barrier x1, local copies, waits for them, and re-layouts, local(): block_values, _ = lax.optimization_barrier((block_values, down1[-1]))  17.1 us
    ppermute x16, waiting for transfers between devices, ring(): return lax.ppermute(piece, 'blk', route)  11.6 us
    ppermute x3, waiting for transfers between devices, local(): lax.ppermute(outgoing.astype(jnp.bfloat16), 'grp', [(i, (i + k) % group_s...  10.8 us
    ppermute x3, starting transfers between devices, local(): lax.ppermute(local_ext, 'grp', [(i, (i + k) % group_size) for i in range(...  3.6 us
    gather x1, local copies, waits for them, and re-layouts, local(): fetched_aggs = jnp.take(flat_aggs, piece_of * share_rows + within, axis=0)  3.18 us
    ppermute x3, starting transfers between devices, local(): fixed.append(lax.ppermute(fix_src, ('blk', 'grp'), route))  2.98 us
  transfers between devices with their start and end apart: 25, of which 8 were waited for; matrix products, arithmetic and copies ran while one was open for 18% of the time, Pallas kernels for 0%

profile of v16, /device:TPU:19, one launch (start us, length us, event | category | flops | bytes accessed | tf_op | source)
XLA Modules:
  0.0 140.5 jit_solution(16860434801053375208)
XLA Ops:
  0.0 0.7 convert_bitcast_fusion
  0.7 2.0 %copy.17 = bf16[24,2,64,64]{3,1,2,0:T(2,128)(2,1)S(1)} copy(bf16[24,2,64,64]{3,2,1,0:T(8,128)(2,1)} %bitcast.144) | data formatting | bytes 786432 | tf_op jit(solution)/shard_map/reshape | solution.py:146
  2.6 0.3 reshape.739
  3.0 1.9 %collective-permute-start = (bf16[25,64,128]{2,1,0:T(8,128)(2,1)S(1)}, bf16[25,64,128]{2,1,0:T(8,128)(2,1)S(1)}, u32[]{:S(2)}, u32[]{:S(2)}) collective-permute-start(bf16[25,64,128]{2,1,0:T(8,128)(2,1)S(1)} %fusion.3.rest_8_), channel_id=1, source_target_pairs={{28,0},{0,4},{4,8},{8,12},{12,16},{16,20},{20,24},{24,28},{29,1},{... | collective-permute-start | bytes 1228808 | tf_op jit(solution)/shard_map/ppermute | solution.py:172
  5.0 0.3 collective-permute-start.13
  5.2 1.2 collective-permute-start.9
  6.4 2.1 %collective-permute-start.5 = (bf16[25,64,128]{2,1,0:T(8,128)(2,1)S(1)}, bf16[25,64,128]{2,1,0:T(8,128)(2,1)}, u32[]{:S(2)}, u32[]{:S(2)}) collective-permute-start(bf16[25,64,128]{2,1,0:T(8,128)(2,1)S(1)} %fusion.3.rest_8_), channel_id=1, source_target_pairs={{0,1},{1,2},{2,3},{3,0},{4,5},{5,6},{6,7},{7,4},{8,9},{9,10},{10,1... | collective-permute-start | bytes 1228808 | tf_op jit(solution)/shard_map/ppermute | solution.py:160
  8.6 0.1 copy.9
  8.7 0.1 rem.301
  8.9 0.1 copy.10
  9.1 0.1 div.78
  9.3 0.2 copy.8
  9.4 0.1 ne.313
  9.6 0.1 ne.303
  9.9 0.7 reshape.807.live_ref
  10.6 0.7 stack.59.fix_ref
  11.3 0.6 fusion.32.own_pos_ref
  12.0 4.7 %collective-permute-start.1 = (bf16[25,64,128]{2,1,0:T(8,128)(2,1)S(1)}, bf16[25,64,128]{2,1,0:T(8,128)(2,1)S(1)}, u32[]{:S(2)}, u32[]{:S(2)}) collective-permute-start(bf16[25,64,128]{2,1,0:T(8,128)(2,1)S(1)} %collective-permute-done.rest_4_), channel_id=1, source_target_pairs={{28,0},{0,4},{4,8},{8,12},{12,16},{16,20},{20,24},{24,28},{29,1},{... | collective-permute-start | bytes 1228808 | tf_op jit(solution)/shard_map/ppermute | solution.py:172
  16.8 5.2 %collective-permute-start.14 = (bf16[25,64,128]{2,1,0:T(8,128)(2,1)}, bf16[25,64,128]{2,1,0:T(8,128)(2,1)S(1)}, u32[]{:S(2)}, u32[]{:S(2)}) collective-permute-start(bf16[25,64,128]{2,1,0:T(8,128)(2,1)} %collective-permute-done.13.rest_11_), channel_id=1, source_target_pairs={{0,4},{4,8},{8,12},{12,16},{16,20},{20,24},{24,28},{1,5},{5,9},{9,... | collective-permute-start | bytes 1228808 | tf_op jit(solution)/shard_map/ppermute | solution.py:172
  21.9 0.7 slice_bitcast_fusion.8
  22.7 2.2 %collective-permute-done.9.rest_10_ = bf16[25,64,128]{2,1,0:T(8,128)(2,1)} collective-permute-done((bf16[25,64,128]{2,1,0:T(8,128)(2,1)S(1)}, bf16[25,64,128]{2,1,0:T(8,128)(2,1)}, u32[]{:S(2)}, u32[]{:S(2)}) %collective-permute-start.9) | collective-permute-done | bytes 409632 | tf_op jit(solution)/shard_map/ppermute | solution.py:160
  24.8 3.0 %collective-permute-start.18 = (bf16[25,64,128]{2,1,0:T(8,128)(2,1)}, bf16[25,64,128]{2,1,0:T(8,128)(2,1)}, u32[]{:S(2)}, u32[]{:S(2)}) collective-permute-start(bf16[25,64,128]{2,1,0:T(8,128)(2,1)} %collective-permute-done.13.rest_11_), channel_id=1, source_target_pairs={{4,0},{8,4},{12,8},{16,12},{20,16},{24,20},{28,24},{5,1},{9,5},{13... | collective-permute-start | bytes 1228808 | tf_op jit(solution)/shard_map/ppermute | solution.py:172
  27.9 2.5 %collective-permute-start.10 = (bf16[25,64,128]{2,1,0:T(8,128)(2,1)}, bf16[25,64,128]{2,1,0:T(8,128)(2,1)}, u32[]{:S(2)}, u32[]{:S(2)}) collective-permute-start(bf16[25,64,128]{2,1,0:T(8,128)(2,1)} %collective-permute-done.9.rest_10_), channel_id=1, source_target_pairs={{0,4},{4,8},{8,12},{12,16},{16,20},{20,24},{24,28},{1,5},{5,9},{9,... | collective-permute-start | bytes 1228808 | tf_op jit(solution)/shard_map/ppermute | solution.py:172
  30.5 1.0 pad_maximum_fusion.1
  31.5 0.7 collective-permute-start.12
  32.2 0.7 slice_bitcast_fusion.9
  32.8 0.7 slice_bitcast_fusion.10
  33.5 1.6 %collective-permute-start.8 = (bf16[2,25,64,128]{3,2,1,0:T(8,128)(2,1)}, bf16[2,25,64,128]{3,2,1,0:T(8,128)(2,1)}, u32[]{:S(2)}, u32[]{:S(2)}) collective-permute-start(bf16[2,25,64,128]{3,2,1,0:T(8,128)(2,1)} %pad_maximum_fusion.1), channel_id=1, source_target_pairs={{0,2},{1,3},{2,0},{3,1},{4,6},{5,7},{6,4},{7,5},{24,26},{25,27},{2... | collective-permute-start | bytes 2457608 | tf_op jit(solution)/shard_map/ppermute | solution.py:191
  35.1 17.1 %copy.15.values_ref = bf16[192,4,64,64]{3,2,1,0:T(8,128)(2,1)} copy(bf16[192,4,64,64]{0,3,2,1:T(8,128)(2,1)} %param.9) | data formatting | bytes 12582912 | tf_op jit(solution)/shard_map/optimization_barrier | solution.py:236
  52.2 7.1 %collective-permute-start.15 = (bf16[25,64,128]{2,1,0:T(8,128)(2,1)S(1)}, bf16[25,64,128]{2,1,0:T(8,128)(2,1)S(1)}, u32[]{:S(2)}, u32[]{:S(2)}) collective-permute-start(bf16[25,64,128]{2,1,0:T(8,128)(2,1)S(1)} %collective-permute-done.14.rest_7_), channel_id=1, source_target_pairs={{4,8},{8,12},{12,16},{16,20},{20,24},{24,28},{5,9},{9,13},{13,17},... | collective-permute-start | bytes 1228808 | tf_op jit(solution)/shard_map/ppermute | solution.py:172
  59.4 1.9 %collective-permute-start.21 = (bf16[25,64,128]{2,1,0:T(8,128)(2,1)}, bf16[25,64,128]{2,1,0:T(8,128)(2,1)S(1)}, u32[]{:S(2)}, u32[]{:S(2)}) collective-permute-start(bf16[25,64,128]{2,1,0:T(8,128)(2,1)} %collective-permute-done.18.rest_15_), channel_id=1, source_target_pairs={{4,0},{8,4},{12,8},{16,12},{20,16},{24,20},{5,1},{9,5},{13,9},{17,... | collective-permute-start | bytes 1228808 | tf_op jit(solution)/shard_map/ppermute | solution.py:172
  61.3 0.7 collective-permute-start.4
  62.1 2.2 %collective-permute-done.15.rest_3_ = bf16[25,64,128]{2,1,0:T(8,128)(2,1)S(1)} collective-permute-done((bf16[25,64,128]{2,1,0:T(8,128)(2,1)S(1)}, bf16[25,64,128]{2,1,0:T(8,128)(2,1)S(1)}, u32[]{:S(2)}, u32[]{:S(2)}) %collective-permute-start.15) | collective-permute-done | bytes 409632 | tf_op jit(solution)/shard_map/ppermute | solution.py:172
  64.2 1.9 %collective-permute-start.17 = (bf16[25,64,128]{2,1,0:T(8,128)(2,1)}, bf16[25,64,128]{2,1,0:T(8,128)(2,1)S(1)}, u32[]{:S(2)}, u32[]{:S(2)}) collective-permute-start(bf16[25,64,128]{2,1,0:T(8,128)(2,1)} %collective-permute-done.9.rest_10_), channel_id=1, source_target_pairs={{4,0},{8,4},{12,8},{16,12},{20,16},{24,20},{28,24},{5,1},{9,5},{13... | collective-permute-start | bytes 1228808 | tf_op jit(solution)/shard_map/ppermute | solution.py:172
  66.1 2.7 %collective-permute-done.21.rest_19_ = bf16[25,64,128]{2,1,0:T(8,128)(2,1)S(1)} collective-permute-done((bf16[25,64,128]{2,1,0:T(8,128)(2,1)}, bf16[25,64,128]{2,1,0:T(8,128)(2,1)S(1)}, u32[]{:S(2)}, u32[]{:S(2)}) %collective-permute-start.21) | collective-permute-done | bytes 409632 | tf_op jit(solution)/shard_map/ppermute | solution.py:172
  68.8 1.9 %collective-permute-start.16 = (bf16[25,64,128]{2,1,0:T(8,128)(2,1)}, bf16[25,64,128]{2,1,0:T(8,128)(2,1)S(1)}, u32[]{:S(2)}, u32[]{:S(2)}) collective-permute-start(bf16[25,64,128]{2,1,0:T(8,128)(2,1)} %collective-permute-done.5.rest_9_), channel_id=1, source_target_pairs={{4,0},{8,4},{12,8},{16,12},{20,16},{24,20},{28,24},{5,1},{9,5},{13... | collective-permute-start | bytes 1228808 | tf_op jit(solution)/shard_map/ppermute | solution.py:172
  70.8 3.6 %collective-permute-start.6 = (bf16[25,64,128]{2,1,0:T(8,128)(2,1)}, bf16[25,64,128]{2,1,0:T(8,128)(2,1)S(1)}, u32[]{:S(2)}, u32[]{:S(2)}) collective-permute-start(bf16[25,64,128]{2,1,0:T(8,128)(2,1)} %collective-permute-done.5.rest_9_), channel_id=1, source_target_pairs={{0,4},{4,8},{8,12},{12,16},{16,20},{20,24},{24,28},{1,5},{5,9},{9,... | collective-permute-start | bytes 1228808 | tf_op jit(solution)/shard_map/ppermute | solution.py:172
  74.5 0.7 broadcast_select_fusion.3
  75.2 1.9 %collective-permute-start.11 = (bf16[25,64,128]{2,1,0:T(8,128)(2,1)}, bf16[25,64,128]{2,1,0:T(8,128)(2,1)S(1)}, u32[]{:S(2)}, u32[]{:S(2)}) collective-permute-start(bf16[25,64,128]{2,1,0:T(8,128)(2,1)} %collective-permute-done.10.rest_6_), channel_id=1, source_target_pairs={{4,8},{8,12},{12,16},{16,20},{20,24},{24,28},{5,9},{9,13},{13,17},... | collective-permute-start | bytes 1228808 | tf_op jit(solution)/shard_map/ppermute | solution.py:172
  77.1 2.0 %collective-permute-done.16.rest_13_ = bf16[25,64,128]{2,1,0:T(8,128)(2,1)S(1)} collective-permute-done((bf16[25,64,128]{2,1,0:T(8,128)(2,1)}, bf16[25,64,128]{2,1,0:T(8,128)(2,1)S(1)}, u32[]{:S(2)}, u32[]{:S(2)}) %collective-permute-start.16) | collective-permute-done | bytes 409632 | tf_op jit(solution)/shard_map/ppermute | solution.py:172
  79.1 1.9 %collective-permute-start.20 = (bf16[25,64,128]{2,1,0:T(8,128)(2,1)S(1)}, bf16[25,64,128]{2,1,0:T(8,128)(2,1)S(1)}, u32[]{:S(2)}, u32[]{:S(2)}) collective-permute-start(bf16[25,64,128]{2,1,0:T(8,128)(2,1)S(1)} %collective-permute-done.17.rest_14_), channel_id=1, source_target_pairs={{4,0},{8,4},{12,8},{16,12},{20,16},{24,20},{5,1},{9,5},{13,9},{17,... | collective-permute-start | bytes 1228808 | tf_op jit(solution)/shard_map/ppermute | solution.py:172
  81.1 1.9 %collective-permute-start.19 = (bf16[25,64,128]{2,1,0:T(8,128)(2,1)S(1)}, bf16[25,64,128]{2,1,0:T(8,128)(2,1)S(1)}, u32[]{:S(2)}, u32[]{:S(2)}) collective-permute-start(bf16[25,64,128]{2,1,0:T(8,128)(2,1)S(1)} %collective-permute-done.16.rest_13_), channel_id=1, source_target_pairs={{4,0},{8,4},{12,8},{16,12},{20,16},{24,20},{5,1},{9,5},{13,9},{17,... | collective-permute-start | bytes 1228808 | tf_op jit(solution)/shard_map/ppermute | solution.py:172
  83.0 3.7 %collective-permute-start.7 = (bf16[25,64,128]{2,1,0:T(8,128)(2,1)S(1)}, bf16[25,64,128]{2,1,0:T(8,128)(2,1)S(1)}, u32[]{:S(2)}, u32[]{:S(2)}) collective-permute-start(bf16[25,64,128]{2,1,0:T(8,128)(2,1)S(1)} %collective-permute-done.6.rest_5_), channel_id=1, source_target_pairs={{4,8},{8,12},{12,16},{16,20},{20,24},{24,28},{5,9},{9,13},{13,17},... | collective-permute-start | bytes 1228808 | tf_op jit(solution)/shard_map/ppermute | solution.py:172
  86.7 0.7 broadcast_select_fusion.16
  87.4 1.3 collective-permute-done.20.rest_18_
  88.7 0.7 broadcast_select_fusion.4
  89.4 3.4 %collective-permute-done.19.rest_17_ = bf16[25,64,128]{2,1,0:T(8,128)(2,1)S(1)} collective-permute-done((bf16[25,64,128]{2,1,0:T(8,128)(2,1)S(1)}, bf16[25,64,128]{2,1,0:T(8,128)(2,1)S(1)}, u32[]{:S(2)}, u32[]{:S(2)}) %collective-permute-start.19) | collective-permute-done | bytes 409632 | tf_op jit(solution)/shard_map/ppermute | solution.py:172
  92.8 0.7 copy-done.15
  93.5 0.1 copy-done.16
  93.8 3.2 %gather_fusion = s32[768]{0:T(1024)S(1)} fusion(s32[960]{0:T(1024)S(1)} %reshape.806, s32[1024]{0:T(1024)S(1)} %pad_clamp_fusion.1), kind=kCustom, calls=%fused_computation | custom fusion | bytes 9216 | tf_op jit(solution)/shard_map/jit(_take)/gather | solution.py:226
  97.1 1.2 gather_fusion.1
  98.4 0.1 reshape.740
  98.5 0.6 multiply_add_fusion
  99.1 0.6 fusion.11.pair_ref
  99.7 23.2 %shard_map.55 = f32[64,64,128]{2,1,0:T(8,128)} custom-call(s32[768]{0:T(1024)} %fusion.11.pair_ref, s32[768]{0:T(1024)} %get-tuple-element.47.half_ref, s32[768]{0:T(1024)} %get-tuple-element.31.target_ref, s32[768]{0:T(1024)} %reshape.807.live_ref, s32[192]{0:T(256)} %fusion.32.own_pos_ref, s32[5]{0:T(128)} %stack.59.fix_ref, ...), custom_call_target="tpu_custom_call" | custom-call | tf_op jit(solution)/shard_map/pallas_call | solution.py:110
  123.0 1.6 %bitcast_convert_fusion.2 = (bf16[8,2,64,128]{3,2,1,0:T(8,128)(2,1)S(1)}, bf16[8,2,64,128]{3,2,1,0:T(8,128)(2,1)S(1)}, bf16[8,2,64,128]{3,2,1,0:T(8,128)(2,1)S(1)}) fusion(f32[4,8,2,64,128]{4,3,2,1,0:T(8,128)} %bitcast.141, s32[]{:T(128)S(6)} %select_n.678, pred[]{:T(512)S(6)} %and.252, s32[]{:T(128)S(6)} %select_n.682, pred[]{:T(512)S(6)} %and.254, ...), kind=kLoop, calls=%fused_computation.9 | loop fusion | flops 393216 | bytes 1572879 | tf_op jit(solution)/shard_map/convert_element_type | solution.py:255
  124.5 1.3 collective-permute-start.22
  125.8 0.2 collective-permute-start.23
  126.0 1.3 collective-permute-start.24
  127.3 5.6 %collective-permute-done.22 = bf16[8,2,64,128]{3,2,1,0:T(8,128)(2,1)S(1)} collective-permute-done((bf16[8,2,64,128]{3,2,1,0:T(8,128)(2,1)S(1)}, bf16[8,2,64,128]{3,2,1,0:T(8,128)(2,1)S(1)}, u32[]{:S(2)}, u32[]{:S(2)}) %collective-permute-start.22) | collective-permute-done | bytes 262176 | tf_op jit(solution)/shard_map/ppermute | solution.py:254
  132.9 5.1 %collective-permute-done.23 = bf16[8,2,64,128]{3,2,1,0:T(8,128)(2,1)S(1)} collective-permute-done((bf16[8,2,64,128]{3,2,1,0:T(8,128)(2,1)S(1)}, bf16[8,2,64,128]{3,2,1,0:T(8,128)(2,1)S(1)}, u32[]{:S(2)}, u32[]{:S(2)}) %collective-permute-start.23) | collective-permute-done | bytes 262176 | tf_op jit(solution)/shard_map/ppermute | solution.py:254
  138.1 1.2 fusion.2
  139.2 0.2 fusion.46
  139.5 1.1 pad_maximum_fusion
  (80 shorter events, 1.0 us)
Async XLA Ops:
  0.0 8.6 %copy-start.17 = (s32[192,4]{0,1:T(4,128)S(1)}, s32[192,4]{0,1:T(4,128)}, u32[]{:S(2)}) copy-start(s32[192,4]{0,1:T(4,128)} %param.10) | copy-start | bytes 9220
  0.7 9.1 %copy-start.18 = (s32[192]{0:T(256)S(1)}, s32[192]{0:T(256)}, u32[]{:S(2)}) copy-start(s32[192]{0:T(256)} %param.11) | copy-start | bytes 2308
  3.0 28.4 %copy-start.4 = (bf16[25,64,128]{2,1,0:T(8,128)(2,1)}, bf16[25,64,128]{2,1,0:T(8,128)(2,1)S(1)}, u32[]{:S(2)}) copy-start(bf16[25,64,128]{2,1,0:T(8,128)(2,1)S(1)} %fusion.3.rest_8_) | copy-start | bytes 1228804
  3.0 8.9 %collective-permute-start = (bf16[25,64,128]{2,1,0:T(8,128)(2,1)S(1)}, bf16[25,64,128]{2,1,0:T(8,128)(2,1)S(1)}, u32[]{:S(2)}, u32[]{:S(2)}) collective-permute-start(bf16[25,64,128]{2,1,0:T(8,128)(2,1)S(1)} %fusion.3.rest_8_), channel_id=1, source_target_pairs={{28,0},{0,4},{4,8},{8,12},{12,16},{16,20},{20,24},{24,28},{29,1},{... | collective-permute-start | bytes 1228808 | tf_op jit(solution)/shard_map/ppermute | solution.py:172
  4.9 11.8 %collective-permute-start.2 = (bf16[25,64,128]{2,1,0:T(8,128)(2,1)S(1)}, bf16[25,64,128]{2,1,0:T(8,128)(2,1)S(1)}, u32[]{:S(2)}, u32[]{:S(2)}) collective-permute-start(bf16[25,64,128]{2,1,0:T(8,128)(2,1)S(1)} %fusion.3.rest_8_), channel_id=1, source_target_pairs={{4,0},{8,4},{12,8},{16,12},{20,16},{24,20},{28,24},{0,28},{5,1},{9... | collective-permute-start | bytes 1228808 | tf_op jit(solution)/shard_map/ppermute | solution.py:172
  5.0 11.8 %collective-permute-start.13 = (bf16[25,64,128]{2,1,0:T(8,128)(2,1)S(1)}, bf16[25,64,128]{2,1,0:T(8,128)(2,1)}, u32[]{:S(2)}, u32[]{:S(2)}) collective-permute-start(bf16[25,64,128]{2,1,0:T(8,128)(2,1)S(1)} %fusion.3.rest_8_), channel_id=1, source_target_pairs={{0,3},{1,0},{2,1},{3,2},{4,7},{5,4},{6,5},{7,6},{8,11},{9,8},{10,9... | collective-permute-start | bytes 1228808 | tf_op jit(solution)/shard_map/ppermute | solution.py:160
  5.2 19.6 %collective-permute-start.9 = (bf16[25,64,128]{2,1,0:T(8,128)(2,1)S(1)}, bf16[25,64,128]{2,1,0:T(8,128)(2,1)}, u32[]{:S(2)}, u32[]{:S(2)}) collective-permute-start(bf16[25,64,128]{2,1,0:T(8,128)(2,1)S(1)} %fusion.3.rest_8_), channel_id=1, source_target_pairs={{0,2},{1,3},{2,0},{3,1},{4,6},{5,7},{6,4},{7,5},{8,10},{9,11},{10,... | collective-permute-start | bytes 1228808 | tf_op jit(solution)/shard_map/ppermute | solution.py:160
  6.4 26.4 %collective-permute-start.5 = (bf16[25,64,128]{2,1,0:T(8,128)(2,1)S(1)}, bf16[25,64,128]{2,1,0:T(8,128)(2,1)}, u32[]{:S(2)}, u32[]{:S(2)}) collective-permute-start(bf16[25,64,128]{2,1,0:T(8,128)(2,1)S(1)} %fusion.3.rest_8_), channel_id=1, source_target_pairs={{0,1},{1,2},{2,3},{3,0},{4,5},{5,6},{6,7},{7,4},{8,9},{9,10},{10,1... | collective-permute-start | bytes 1228808 | tf_op jit(solution)/shard_map/ppermute | solution.py:160
  12.0 40.3 %copy-start = (bf16[25,64,128]{2,1,0:T(8,128)(2,1)}, bf16[25,64,128]{2,1,0:T(8,128)(2,1)S(1)}, u32[]{:S(2)}) copy-start(bf16[25,64,128]{2,1,0:T(8,128)(2,1)S(1)} %collective-permute-done.rest_4_) | copy-start | bytes 1228804
  12.0 15.9 %collective-permute-start.1 = (bf16[25,64,128]{2,1,0:T(8,128)(2,1)S(1)}, bf16[25,64,128]{2,1,0:T(8,128)(2,1)S(1)}, u32[]{:S(2)}, u32[]{:S(2)}) collective-permute-start(bf16[25,64,128]{2,1,0:T(8,128)(2,1)S(1)} %collective-permute-done.rest_4_), channel_id=1, source_target_pairs={{28,0},{0,4},{4,8},{8,12},{12,16},{16,20},{20,24},{24,28},{29,1},{... | collective-permute-start | bytes 1228808 | tf_op jit(solution)/shard_map/ppermute | solution.py:172
  16.7 35.5 %copy-start.1 = (bf16[25,64,128]{2,1,0:T(8,128)(2,1)}, bf16[25,64,128]{2,1,0:T(8,128)(2,1)S(1)}, u32[]{:S(2)}) copy-start(bf16[25,64,128]{2,1,0:T(8,128)(2,1)S(1)} %collective-permute-done.2.rest_12_) | copy-start | bytes 1228804
  16.7 13.7 %collective-permute-start.3 = (bf16[25,64,128]{2,1,0:T(8,128)(2,1)S(1)}, bf16[25,64,128]{2,1,0:T(8,128)(2,1)S(1)}, u32[]{:S(2)}, u32[]{:S(2)}) collective-permute-start(bf16[25,64,128]{2,1,0:T(8,128)(2,1)S(1)} %collective-permute-done.2.rest_12_), channel_id=1, source_target_pairs={{4,0},{8,4},{12,8},{16,12},{20,16},{24,20},{28,24},{0,28},{5,1},{9... | collective-permute-start | bytes 1228808 | tf_op jit(solution)/shard_map/ppermute | solution.py:172
  16.8 18.3 %collective-permute-start.14 = (bf16[25,64,128]{2,1,0:T(8,128)(2,1)}, bf16[25,64,128]{2,1,0:T(8,128)(2,1)S(1)}, u32[]{:S(2)}, u32[]{:S(2)}) collective-permute-start(bf16[25,64,128]{2,1,0:T(8,128)(2,1)} %collective-permute-done.13.rest_11_), channel_id=1, source_target_pairs={{0,4},{4,8},{8,12},{12,16},{16,20},{20,24},{24,28},{1,5},{5,9},{9,... | collective-permute-start | bytes 1228808 | tf_op jit(solution)/shard_map/ppermute | solution.py:172
  24.8 34.5 %collective-permute-start.18 = (bf16[25,64,128]{2,1,0:T(8,128)(2,1)}, bf16[25,64,128]{2,1,0:T(8,128)(2,1)}, u32[]{:S(2)}, u32[]{:S(2)}) collective-permute-start(bf16[25,64,128]{2,1,0:T(8,128)(2,1)} %collective-permute-done.13.rest_11_), channel_id=1, source_target_pairs={{4,0},{8,4},{12,8},{16,12},{20,16},{24,20},{28,24},{5,1},{9,5},{13... | collective-permute-start | bytes 1228808 | tf_op jit(solution)/shard_map/ppermute | solution.py:172
  27.9 33.4 %copy-start.2 = (bf16[25,64,128]{2,1,0:T(8,128)(2,1)}, bf16[25,64,128]{2,1,0:T(8,128)(2,1)S(1)}, u32[]{:S(2)}) copy-start(bf16[25,64,128]{2,1,0:T(8,128)(2,1)S(1)} %collective-permute-done.1.rest_0_) | copy-start | bytes 1228804
  27.9 33.4 %collective-permute-start.10 = (bf16[25,64,128]{2,1,0:T(8,128)(2,1)}, bf16[25,64,128]{2,1,0:T(8,128)(2,1)}, u32[]{:S(2)}, u32[]{:S(2)}) collective-permute-start(bf16[25,64,128]{2,1,0:T(8,128)(2,1)} %collective-permute-done.9.rest_10_), channel_id=1, source_target_pairs={{0,4},{4,8},{8,12},{12,16},{16,20},{20,24},{24,28},{1,5},{5,9},{9,... | collective-permute-start | bytes 1228808 | tf_op jit(solution)/shard_map/ppermute | solution.py:172
  30.4 31.6 %copy-start.3 = (bf16[25,64,128]{2,1,0:T(8,128)(2,1)}, bf16[25,64,128]{2,1,0:T(8,128)(2,1)S(1)}, u32[]{:S(2)}) copy-start(bf16[25,64,128]{2,1,0:T(8,128)(2,1)S(1)} %collective-permute-done.3.rest_16_) | copy-start | bytes 1228804
  31.5 39.3 %collective-permute-start.12 = (bf16[2,25,64,128]{3,2,1,0:T(8,128)(2,1)}, bf16[2,25,64,128]{3,2,1,0:T(8,128)(2,1)S(1)}, u32[]{:S(2)}, u32[]{:S(2)}) collective-permute-start(bf16[2,25,64,128]{3,2,1,0:T(8,128)(2,1)} %pad_maximum_fusion.1), channel_id=1, source_target_pairs={{0,3},{1,0},{2,1},{3,2},{4,7},{5,4},{6,5},{7,6},{24,27},{25,24},{2... | collective-permute-start | bytes 2457608 | tf_op jit(solution)/shard_map/ppermute | solution.py:191
  33.5 49.5 %collective-permute-start.8 = (bf16[2,25,64,128]{3,2,1,0:T(8,128)(2,1)}, bf16[2,25,64,128]{3,2,1,0:T(8,128)(2,1)}, u32[]{:S(2)}, u32[]{:S(2)}) collective-permute-start(bf16[2,25,64,128]{3,2,1,0:T(8,128)(2,1)} %pad_maximum_fusion.1), channel_id=1, source_target_pairs={{0,2},{1,3},{2,0},{3,1},{4,6},{5,7},{6,4},{7,5},{24,26},{25,27},{2... | collective-permute-start | bytes 2457608 | tf_op jit(solution)/shard_map/ppermute | solution.py:191
  35.1 39.3 %copy-start.7 = (bf16[25,64,128]{2,1,0:T(8,128)(2,1)}, bf16[25,64,128]{2,1,0:T(8,128)(2,1)S(1)}, u32[]{:S(2)}) copy-start(bf16[25,64,128]{2,1,0:T(8,128)(2,1)S(1)} %collective-permute-done.14.rest_7_) | copy-start | bytes 1228804
  52.2 12.0 %collective-permute-start.15 = (bf16[25,64,128]{2,1,0:T(8,128)(2,1)S(1)}, bf16[25,64,128]{2,1,0:T(8,128)(2,1)S(1)}, u32[]{:S(2)}, u32[]{:S(2)}) collective-permute-start(bf16[25,64,128]{2,1,0:T(8,128)(2,1)S(1)} %collective-permute-done.14.rest_7_), channel_id=1, source_target_pairs={{4,8},{8,12},{12,16},{16,20},{20,24},{24,28},{5,9},{9,13},{13,17},... | collective-permute-start | bytes 1228808 | tf_op jit(solution)/shard_map/ppermute | solution.py:172
  59.4 9.5 %collective-permute-start.21 = (bf16[25,64,128]{2,1,0:T(8,128)(2,1)}, bf16[25,64,128]{2,1,0:T(8,128)(2,1)S(1)}, u32[]{:S(2)}, u32[]{:S(2)}) collective-permute-start(bf16[25,64,128]{2,1,0:T(8,128)(2,1)} %collective-permute-done.18.rest_15_), channel_id=1, source_target_pairs={{4,0},{8,4},{12,8},{16,12},{20,16},{24,20},{5,1},{9,5},{13,9},{17,... | collective-permute-start | bytes 1228808 | tf_op jit(solution)/shard_map/ppermute | solution.py:172
  61.3 26.0 %collective-permute-start.4 = (bf16[2,25,64,128]{3,2,1,0:T(8,128)(2,1)}, bf16[2,25,64,128]{3,2,1,0:T(8,128)(2,1)S(1)}, u32[]{:S(2)}, u32[]{:S(2)}) collective-permute-start(bf16[2,25,64,128]{3,2,1,0:T(8,128)(2,1)} %pad_maximum_fusion.1), channel_id=1, source_target_pairs={{0,1},{1,2},{2,3},{3,0},{4,5},{5,6},{6,7},{7,4},{24,25},{25,26},{2... | collective-permute-start | bytes 2457608 | tf_op jit(solution)/shard_map/ppermute | solution.py:191
  64.2 32.8 %copy-start.8 = (bf16[25,64,128]{2,1,0:T(8,128)(2,1)}, bf16[25,64,128]{2,1,0:T(8,128)(2,1)S(1)}, u32[]{:S(2)}) copy-start(bf16[25,64,128]{2,1,0:T(8,128)(2,1)S(1)} %collective-permute-done.15.rest_3_) | copy-start | bytes 1228804
  64.2 10.9 %collective-permute-start.17 = (bf16[25,64,128]{2,1,0:T(8,128)(2,1)}, bf16[25,64,128]{2,1,0:T(8,128)(2,1)S(1)}, u32[]{:S(2)}, u32[]{:S(2)}) collective-permute-start(bf16[25,64,128]{2,1,0:T(8,128)(2,1)} %collective-permute-done.9.rest_10_), channel_id=1, source_target_pairs={{4,0},{8,4},{12,8},{16,12},{20,16},{24,20},{28,24},{5,1},{9,5},{13... | collective-permute-start | bytes 1228808 | tf_op jit(solution)/shard_map/ppermute | solution.py:172
  68.8 18.5 %copy-start.9 = (bf16[25,64,128]{2,1,0:T(8,128)(2,1)}, bf16[25,64,128]{2,1,0:T(8,128)(2,1)S(1)}, u32[]{:S(2)}) copy-start(bf16[25,64,128]{2,1,0:T(8,128)(2,1)S(1)} %collective-permute-done.21.rest_19_) | copy-start | bytes 1228804
  68.8 10.3 %collective-permute-start.16 = (bf16[25,64,128]{2,1,0:T(8,128)(2,1)}, bf16[25,64,128]{2,1,0:T(8,128)(2,1)S(1)}, u32[]{:S(2)}, u32[]{:S(2)}) collective-permute-start(bf16[25,64,128]{2,1,0:T(8,128)(2,1)} %collective-permute-done.5.rest_9_), channel_id=1, source_target_pairs={{4,0},{8,4},{12,8},{16,12},{20,16},{24,20},{28,24},{5,1},{9,5},{13... | collective-permute-start | bytes 1228808 | tf_op jit(solution)/shard_map/ppermute | solution.py:172
  70.8 26.3 %copy-start.5 = (bf16[2,25,64,128]{3,2,1,0:T(8,128)(2,1)}, bf16[2,25,64,128]{3,2,1,0:T(8,128)(2,1)S(1)}, u32[]{:S(2)}) copy-start(bf16[2,25,64,128]{3,2,1,0:T(8,128)(2,1)S(1)} %collective-permute-done.12.rest_22_) | copy-start | bytes 2457604
  70.8 10.3 %collective-permute-start.6 = (bf16[25,64,128]{2,1,0:T(8,128)(2,1)}, bf16[25,64,128]{2,1,0:T(8,128)(2,1)S(1)}, u32[]{:S(2)}, u32[]{:S(2)}) collective-permute-start(bf16[25,64,128]{2,1,0:T(8,128)(2,1)} %collective-permute-done.5.rest_9_), channel_id=1, source_target_pairs={{0,4},{4,8},{8,12},{12,16},{16,20},{20,24},{24,28},{1,5},{5,9},{9,... | collective-permute-start | bytes 1228808 | tf_op jit(solution)/shard_map/ppermute | solution.py:172
  75.2 21.9 %copy-start.10 = (bf16[25,64,128]{2,1,0:T(8,128)(2,1)}, bf16[25,64,128]{2,1,0:T(8,128)(2,1)S(1)}, u32[]{:S(2)}) copy-start(bf16[25,64,128]{2,1,0:T(8,128)(2,1)S(1)} %collective-permute-done.17.rest_14_) | copy-start | bytes 1228804
  75.2 12.2 %collective-permute-start.11 = (bf16[25,64,128]{2,1,0:T(8,128)(2,1)}, bf16[25,64,128]{2,1,0:T(8,128)(2,1)S(1)}, u32[]{:S(2)}, u32[]{:S(2)}) collective-permute-start(bf16[25,64,128]{2,1,0:T(8,128)(2,1)} %collective-permute-done.10.rest_6_), channel_id=1, source_target_pairs={{4,8},{8,12},{12,16},{16,20},{20,24},{24,28},{5,9},{9,13},{13,17},... | collective-permute-start | bytes 1228808 | tf_op jit(solution)/shard_map/ppermute | solution.py:172
  79.1 17.9 %copy-start.11 = (bf16[25,64,128]{2,1,0:T(8,128)(2,1)}, bf16[25,64,128]{2,1,0:T(8,128)(2,1)S(1)}, u32[]{:S(2)}) copy-start(bf16[25,64,128]{2,1,0:T(8,128)(2,1)S(1)} %collective-permute-done.16.rest_13_) | copy-start | bytes 1228804
  79.1 9.6 %collective-permute-start.20 = (bf16[25,64,128]{2,1,0:T(8,128)(2,1)S(1)}, bf16[25,64,128]{2,1,0:T(8,128)(2,1)S(1)}, u32[]{:S(2)}, u32[]{:S(2)}) collective-permute-start(bf16[25,64,128]{2,1,0:T(8,128)(2,1)S(1)} %collective-permute-done.17.rest_14_), channel_id=1, source_target_pairs={{4,0},{8,4},{12,8},{16,12},{20,16},{24,20},{5,1},{9,5},{13,9},{17,... | collective-permute-start | bytes 1228808 | tf_op jit(solution)/shard_map/ppermute | solution.py:172
  81.1 11.7 %copy-start.12 = (bf16[25,64,128]{2,1,0:T(8,128)(2,1)}, bf16[25,64,128]{2,1,0:T(8,128)(2,1)S(1)}, u32[]{:S(2)}) copy-start(bf16[25,64,128]{2,1,0:T(8,128)(2,1)S(1)} %collective-permute-done.6.rest_5_) | copy-start | bytes 1228804
  81.1 11.7 %collective-permute-start.19 = (bf16[25,64,128]{2,1,0:T(8,128)(2,1)S(1)}, bf16[25,64,128]{2,1,0:T(8,128)(2,1)S(1)}, u32[]{:S(2)}, u32[]{:S(2)}) collective-permute-start(bf16[25,64,128]{2,1,0:T(8,128)(2,1)S(1)} %collective-permute-done.16.rest_13_), channel_id=1, source_target_pairs={{4,0},{8,4},{12,8},{16,12},{20,16},{24,20},{5,1},{9,5},{13,9},{17,... | collective-permute-start | bytes 1228808 | tf_op jit(solution)/shard_map/ppermute | solution.py:172
  83.0 9.8 %collective-permute-start.7 = (bf16[25,64,128]{2,1,0:T(8,128)(2,1)S(1)}, bf16[25,64,128]{2,1,0:T(8,128)(2,1)S(1)}, u32[]{:S(2)}, u32[]{:S(2)}) collective-permute-start(bf16[25,64,128]{2,1,0:T(8,128)(2,1)S(1)} %collective-permute-done.6.rest_5_), channel_id=1, source_target_pairs={{4,8},{8,12},{12,16},{16,20},{20,24},{24,28},{5,9},{9,13},{13,17},... | collective-permute-start | bytes 1228808 | tf_op jit(solution)/shard_map/ppermute | solution.py:172
  87.4 9.7 %copy-start.6 = (bf16[2,25,64,128]{3,2,1,0:T(8,128)(2,1)}, bf16[2,25,64,128]{3,2,1,0:T(8,128)(2,1)S(1)}, u32[]{:S(2)}) copy-start(bf16[2,25,64,128]{3,2,1,0:T(8,128)(2,1)S(1)} %collective-permute-done.4.rest_20_) | copy-start | bytes 2457604
  87.4 9.7 %copy-start.13 = (bf16[25,64,128]{2,1,0:T(8,128)(2,1)}, bf16[25,64,128]{2,1,0:T(8,128)(2,1)S(1)}, u32[]{:S(2)}) copy-start(bf16[25,64,128]{2,1,0:T(8,128)(2,1)S(1)} %collective-permute-done.11.rest_2_) | copy-start | bytes 1228804
  88.7 4.1 %copy-start.14 = (bf16[25,64,128]{2,1,0:T(8,128)(2,1)}, bf16[25,64,128]{2,1,0:T(8,128)(2,1)S(1)}, u32[]{:S(2)}) copy-start(bf16[25,64,128]{2,1,0:T(8,128)(2,1)S(1)} %collective-permute-done.20.rest_18_) | copy-start | bytes 1228804
  92.8 0.8 copy-start.15
  92.8 0.9 copy-start.16
  124.5 8.4 %collective-permute-start.22 = (bf16[8,2,64,128]{3,2,1,0:T(8,128)(2,1)S(1)}, bf16[8,2,64,128]{3,2,1,0:T(8,128)(2,1)S(1)}, u32[]{:S(2)}, u32[]{:S(2)}) collective-permute-start(bf16[8,2,64,128]{3,2,1,0:T(8,128)(2,1)S(1)} %get-tuple-element.33), channel_id=1, source_target_pairs={{0,1},{1,2},{2,3},{3,0},{4,5},{5,6},{6,7},{7,4},{8,9},{9,10},{10,1... | collective-permute-start | bytes 786440 | tf_op jit(solution)/shard_map/ppermute | solution.py:254
  125.8 12.2 %collective-permute-start.23 = (bf16[8,2,64,128]{3,2,1,0:T(8,128)(2,1)S(1)}, bf16[8,2,64,128]{3,2,1,0:T(8,128)(2,1)S(1)}, u32[]{:S(2)}, u32[]{:S(2)}) collective-permute-start(bf16[8,2,64,128]{3,2,1,0:T(8,128)(2,1)S(1)} %get-tuple-element.35), channel_id=1, source_target_pairs={{0,2},{1,3},{2,0},{3,1},{4,6},{5,7},{6,4},{7,5},{8,10},{9,11},{10,... | collective-permute-start | bytes 786440 | tf_op jit(solution)/shard_map/ppermute | solution.py:254
  126.0 12.0 %collective-permute-start.24 = (bf16[8,2,64,128]{3,2,1,0:T(8,128)(2,1)S(1)}, bf16[8,2,64,128]{3,2,1,0:T(8,128)(2,1)S(1)}, u32[]{:S(2)}, u32[]{:S(2)}) collective-permute-start(bf16[8,2,64,128]{3,2,1,0:T(8,128)(2,1)S(1)} %get-tuple-element.34), channel_id=1, source_target_pairs={{0,3},{1,0},{2,1},{3,2},{4,7},{5,4},{6,5},{7,6},{8,11},{9,8},{10,9... | collective-permute-start | bytes 786440 | tf_op jit(solution)/shard_map/ppermute | solution.py:254

commit v17 on v16

--- a/solution.py
+++ b/solution.py
@@ -18,7 +18,8 @@
 
 
 def coarse_kernel(
-    pair_ref, half_ref, target_ref, live_ref, own_pos_ref, fix_ref, values_ref, *rest
+    pair_ref, half_ref, agg_at_ref, own_agg_at_ref, aggs_ref, base_ref, live_ref,
+    own_pos_ref, fix_ref, values_ref, *rest
 ):
     window, sems = rest[-2:]
     n_pieces = sems.shape[0]
@@ -82,8 +83,9 @@
             results.append(
                 jnp.dot(own_t, product, preferred_element_type=jnp.float32)
             )
+        own_coarse = aggs_ref[own_agg_at_ref[row]] - base_ref[0]
         for s in range(slots):
-            t = target_ref[row * slots + s]
+            t = aggs_ref[agg_at_ref[row * slots + s]] * CB + own_coarse
             accs[s][t] = accs[s][t] + results[s]
         return carry
 
@@ -102,7 +104,7 @@
         lax.fori_loop(0, out_ref.shape[0], pack, 0)
 
 
-def coarse_partial(pair, half, target, live, own_pos, fix, values, pieces, fixed, n_targets):
+def coarse_partial(pair, half, agg_at, own_agg_at, aggs, base, live, own_pos, fix, values, pieces, fixed, n_targets):
     panel_length, slots, bs, _ = values.shape
     rows_per_step = min(ROWS_PER_STEP, panel_length)
     grid = (panel_length // rows_per_step,)
@@ -111,7 +113,7 @@
         coarse_kernel,
         out_shape=jax.ShapeDtypeStruct((n_targets // 2, bs, lanes), jnp.float32),
         grid_spec=pltpu.PrefetchScalarGridSpec(
-            num_scalar_prefetch=6,
+            num_scalar_prefetch=9,
             grid=grid,
             in_specs=[
                 pl.BlockSpec((rows_per_step, slots, bs, bs), lambda i, *_: (i, 0, 0, 0)),
@@ -128,7 +130,7 @@
             dimension_semantics=("arbitrary",),
             vmem_limit_bytes=60 * 1024 * 1024,
         ),
-    )(pair, half, target, live, own_pos, fix, values, *pieces, *fixed)
+    )(pair, half, agg_at, own_agg_at, aggs, base, live, own_pos, fix, values, *pieces, *fixed)
 
 
 def local(block_values, block_columns, row_counts, prolong_blocks, aggregates):
@@ -223,21 +225,18 @@
     distance = jnp.mod(column_panel - me + 2, panel_total)
     piece_of, within = placed(distance, wanted % panel_length)
     window_pair = piece_of * piece_rows + within // 2
-    fetched_aggs = jnp.take(flat_aggs, piece_of * share_rows + within, axis=0)
     own_piece, own_within = placed(2, jnp.arange(panel_length, dtype=jnp.int32))
     own_pos = own_piece * piece_rows + own_within // 2
-    own_aggs = jnp.take(flat_aggs, own_piece * share_rows + own_within, axis=0)
     slot_ids = lax.axis_index("grp") * slots_here + jnp.arange(slots_here, dtype=jnp.int32)
     live = (slot_ids[None, :] < row_counts[:, None]).astype(jnp.int32).reshape(slot_total)
-    local_coarse = own_aggs - me * CB
-    target = fetched_aggs * CB + jnp.broadcast_to(
-        local_coarse[:, None], (panel_length, slots_here)
-    ).reshape(slot_total)
     block_values, _ = lax.optimization_barrier((block_values, down1[-1]))
     summed = coarse_partial(
         window_pair.astype(jnp.int32),
         (within % 2).astype(jnp.int32),
-        target.astype(jnp.int32),
+        (piece_of * share_rows + within).astype(jnp.int32),
+        (own_piece * share_rows + own_within).astype(jnp.int32),
+        flat_aggs,
+        jnp.reshape(me * CB, (1,)).astype(jnp.int32),
         live,
         own_pos,
         fix,

time: 142 us -> 137 us (0.965)
  local copies, waits for them, and re-layouts: 29.8 us -> 25.4 us
    gather x2 -> x0, local copies, waits for them, and re-layouts: 4.36 us -> none  [the longest x1 3.18 us: local(): fetched_aggs = jnp.take(flat_aggs, piece_of * share_rows + within, axis=0)]
  transfers between devices with their start and end apart: 25 -> 25, of which waited for: 8 -> 8; matrix products, arithmetic and copies ran while one was open for 18% -> 19% of each run, Pallas kernels for 0% -> 0%
where the time goes in v17:
time: 137 us; the launch traced here: 135 us
  starting transfers between devices  52 us (38%)
  local copies, waits for them, and re-layouts  25.4 us (19%)
  waiting for transfers between devices  24.6 us (18%)
  Pallas kernels  23.4 us (17%)
  other arithmetic  9.52 us (7%)
    ppermute x16, starting transfers between devices, ring(): return lax.ppermute(piece, 'blk', route)  42.7 us
    pallas_call x1, Pallas kernels, coarse_partial(): pl.pallas_call(coarse_kernel, out_shape=jax.ShapeDtypeStruct((n_targets /...  23.4 us
    optimization_barrier x1, local copies, waits for them, and re-layouts, local(): block_values, _ = lax.optimization_barrier((block_values, down1[-1]))  17.1 us
    ppermute x16, waiting for transfers between devices, ring(): return lax.ppermute(piece, 'blk', route)  11.6 us
    ppermute x3, waiting for transfers between devices, local(): lax.ppermute(outgoing.astype(jnp.bfloat16), 'grp', [(i, (i + k) % group_s...  10.8 us
    ppermute x3, starting transfers between devices, local(): lax.ppermute(local_ext, 'grp', [(i, (i + k) % group_size) for i in range(...  3.6 us
    ppermute x3, starting transfers between devices, local(): fixed.append(lax.ppermute(fix_src, ('blk', 'grp'), route))  2.97 us
    ppermute x3, starting transfers between devices, local(): lax.ppermute(outgoing.astype(jnp.bfloat16), 'grp', [(i, (i + k) % group_s...  2.76 us
  transfers between devices with their start and end apart: 25, of which 8 were waited for; matrix products, arithmetic and copies ran while one was open for 19% of the time, Pallas kernels for 0%

profile of v17, /device:TPU:19, one launch (start us, length us, event | category | flops | bytes accessed | tf_op | source)
XLA Modules:
  0.0 135.4 jit_solution(15941248841828688478)
XLA Ops:
  0.0 0.7 convert_bitcast_fusion
  0.7 2.0 %copy.14 = bf16[24,2,64,64]{3,1,2,0:T(2,128)(2,1)S(1)} copy(bf16[24,2,64,64]{3,2,1,0:T(8,128)(2,1)} %bitcast.144) | data formatting | bytes 786432 | tf_op jit(solution)/shard_map/reshape | solution.py:148
  2.6 0.3 reshape.425
  3.0 1.9 %collective-permute-start = (bf16[25,64,128]{2,1,0:T(8,128)(2,1)S(1)}, bf16[25,64,128]{2,1,0:T(8,128)(2,1)S(1)}, u32[]{:S(2)}, u32[]{:S(2)}) collective-permute-start(bf16[25,64,128]{2,1,0:T(8,128)(2,1)S(1)} %fusion.3.rest_8_), channel_id=1, source_target_pairs={{28,0},{0,4},{4,8},{8,12},{12,16},{16,20},{20,24},{24,28},{29,1},{... | collective-permute-start | bytes 1228808 | tf_op jit(solution)/shard_map/ppermute | solution.py:174
  5.0 0.3 collective-permute-start.13
  5.2 1.2 collective-permute-start.9
  6.4 2.1 %collective-permute-start.5 = (bf16[25,64,128]{2,1,0:T(8,128)(2,1)S(1)}, bf16[25,64,128]{2,1,0:T(8,128)(2,1)}, u32[]{:S(2)}, u32[]{:S(2)}) collective-permute-start(bf16[25,64,128]{2,1,0:T(8,128)(2,1)S(1)} %fusion.3.rest_8_), channel_id=1, source_target_pairs={{0,1},{1,2},{2,3},{3,0},{4,5},{5,6},{6,7},{7,4},{8,9},{9,10},{10,1... | collective-permute-start | bytes 1228808 | tf_op jit(solution)/shard_map/ppermute | solution.py:162
  8.6 0.6 fusion.20
  9.1 0.1 copy.9
  9.3 0.1 rem.165
  9.4 0.1 copy.10
  9.5 0.1 div.36
  9.6 0.2 copy.8
  9.8 0.1 ne.114
  9.9 0.1 compare_convert_fusion
  10.0 0.7 reshape.493.live_ref
  10.7 0.6 stack.59.fix_ref
  11.4 0.6 multiply_add_fusion
  12.0 0.6 fusion.11.pair_ref
  12.6 4.1 %collective-permute-start.1 = (bf16[25,64,128]{2,1,0:T(8,128)(2,1)S(1)}, bf16[25,64,128]{2,1,0:T(8,128)(2,1)S(1)}, u32[]{:S(2)}, u32[]{:S(2)}) collective-permute-start(bf16[25,64,128]{2,1,0:T(8,128)(2,1)S(1)} %collective-permute-done.rest_4_), channel_id=1, source_target_pairs={{28,0},{0,4},{4,8},{8,12},{12,16},{16,20},{20,24},{24,28},{29,1},{... | collective-permute-start | bytes 1228808 | tf_op jit(solution)/shard_map/ppermute | solution.py:174
  16.8 5.2 %collective-permute-start.14 = (bf16[25,64,128]{2,1,0:T(8,128)(2,1)}, bf16[25,64,128]{2,1,0:T(8,128)(2,1)S(1)}, u32[]{:S(2)}, u32[]{:S(2)}) collective-permute-start(bf16[25,64,128]{2,1,0:T(8,128)(2,1)} %collective-permute-done.13.rest_11_), channel_id=1, source_target_pairs={{0,4},{4,8},{8,12},{12,16},{16,20},{20,24},{24,28},{1,5},{5,9},{9,... | collective-permute-start | bytes 1228808 | tf_op jit(solution)/shard_map/ppermute | solution.py:174
  21.9 0.7 slice_bitcast_fusion.8
  22.7 2.2 %collective-permute-done.9.rest_10_ = bf16[25,64,128]{2,1,0:T(8,128)(2,1)} collective-permute-done((bf16[25,64,128]{2,1,0:T(8,128)(2,1)S(1)}, bf16[25,64,128]{2,1,0:T(8,128)(2,1)}, u32[]{:S(2)}, u32[]{:S(2)}) %collective-permute-start.9) | collective-permute-done | bytes 409632 | tf_op jit(solution)/shard_map/ppermute | solution.py:162
  24.8 3.0 %collective-permute-start.18 = (bf16[25,64,128]{2,1,0:T(8,128)(2,1)}, bf16[25,64,128]{2,1,0:T(8,128)(2,1)}, u32[]{:S(2)}, u32[]{:S(2)}) collective-permute-start(bf16[25,64,128]{2,1,0:T(8,128)(2,1)} %collective-permute-done.13.rest_11_), channel_id=1, source_target_pairs={{4,0},{8,4},{12,8},{16,12},{20,16},{24,20},{28,24},{5,1},{9,5},{13... | collective-permute-start | bytes 1228808 | tf_op jit(solution)/shard_map/ppermute | solution.py:174
  27.9 2.5 %collective-permute-start.10 = (bf16[25,64,128]{2,1,0:T(8,128)(2,1)}, bf16[25,64,128]{2,1,0:T(8,128)(2,1)}, u32[]{:S(2)}, u32[]{:S(2)}) collective-permute-start(bf16[25,64,128]{2,1,0:T(8,128)(2,1)} %collective-permute-done.9.rest_10_), channel_id=1, source_target_pairs={{0,4},{4,8},{8,12},{12,16},{16,20},{20,24},{24,28},{1,5},{5,9},{9,... | collective-permute-start | bytes 1228808 | tf_op jit(solution)/shard_map/ppermute | solution.py:174
  30.5 1.0 pad_maximum_fusion.1
  31.5 0.7 collective-permute-start.12
  32.2 0.7 slice_bitcast_fusion.9
  32.9 0.7 slice_bitcast_fusion.10
  33.5 1.6 %collective-permute-start.8 = (bf16[2,25,64,128]{3,2,1,0:T(8,128)(2,1)}, bf16[2,25,64,128]{3,2,1,0:T(8,128)(2,1)}, u32[]{:S(2)}, u32[]{:S(2)}) collective-permute-start(bf16[2,25,64,128]{3,2,1,0:T(8,128)(2,1)} %pad_maximum_fusion.1), channel_id=1, source_target_pairs={{0,2},{1,3},{2,0},{3,1},{4,6},{5,7},{6,4},{7,5},{24,26},{25,27},{2... | collective-permute-start | bytes 2457608 | tf_op jit(solution)/shard_map/ppermute | solution.py:193
  35.1 17.1 %copy.12.values_ref = bf16[192,4,64,64]{3,2,1,0:T(8,128)(2,1)} copy(bf16[192,4,64,64]{0,3,2,1:T(8,128)(2,1)} %param.9) | data formatting | bytes 12582912 | tf_op jit(solution)/shard_map/optimization_barrier | solution.py:232
  52.2 7.1 %collective-permute-start.15 = (bf16[25,64,128]{2,1,0:T(8,128)(2,1)S(1)}, bf16[25,64,128]{2,1,0:T(8,128)(2,1)S(1)}, u32[]{:S(2)}, u32[]{:S(2)}) collective-permute-start(bf16[25,64,128]{2,1,0:T(8,128)(2,1)S(1)} %collective-permute-done.14.rest_7_), channel_id=1, source_target_pairs={{4,8},{8,12},{12,16},{16,20},{20,24},{24,28},{5,9},{9,13},{13,17},... | collective-permute-start | bytes 1228808 | tf_op jit(solution)/shard_map/ppermute | solution.py:174
  59.4 1.9 %collective-permute-start.21 = (bf16[25,64,128]{2,1,0:T(8,128)(2,1)}, bf16[25,64,128]{2,1,0:T(8,128)(2,1)S(1)}, u32[]{:S(2)}, u32[]{:S(2)}) collective-permute-start(bf16[25,64,128]{2,1,0:T(8,128)(2,1)} %collective-permute-done.18.rest_15_), channel_id=1, source_target_pairs={{4,0},{8,4},{12,8},{16,12},{20,16},{24,20},{5,1},{9,5},{13,9},{17,... | collective-permute-start | bytes 1228808 | tf_op jit(solution)/shard_map/ppermute | solution.py:174
  61.3 0.7 collective-permute-start.4
  62.1 2.2 %collective-permute-done.15.rest_3_ = bf16[25,64,128]{2,1,0:T(8,128)(2,1)S(1)} collective-permute-done((bf16[25,64,128]{2,1,0:T(8,128)(2,1)S(1)}, bf16[25,64,128]{2,1,0:T(8,128)(2,1)S(1)}, u32[]{:S(2)}, u32[]{:S(2)}) %collective-permute-start.15) | collective-permute-done | bytes 409632 | tf_op jit(solution)/shard_map/ppermute | solution.py:174
  64.2 1.9 %collective-permute-start.17 = (bf16[25,64,128]{2,1,0:T(8,128)(2,1)}, bf16[25,64,128]{2,1,0:T(8,128)(2,1)S(1)}, u32[]{:S(2)}, u32[]{:S(2)}) collective-permute-start(bf16[25,64,128]{2,1,0:T(8,128)(2,1)} %collective-permute-done.9.rest_10_), channel_id=1, source_target_pairs={{4,0},{8,4},{12,8},{16,12},{20,16},{24,20},{28,24},{5,1},{9,5},{13... | collective-permute-start | bytes 1228808 | tf_op jit(solution)/shard_map/ppermute | solution.py:174
  66.2 2.7 %collective-permute-done.21.rest_19_ = bf16[25,64,128]{2,1,0:T(8,128)(2,1)S(1)} collective-permute-done((bf16[25,64,128]{2,1,0:T(8,128)(2,1)}, bf16[25,64,128]{2,1,0:T(8,128)(2,1)S(1)}, u32[]{:S(2)}, u32[]{:S(2)}) %collective-permute-start.21) | collective-permute-done | bytes 409632 | tf_op jit(solution)/shard_map/ppermute | solution.py:174
  68.9 1.9 %collective-permute-start.16 = (bf16[25,64,128]{2,1,0:T(8,128)(2,1)}, bf16[25,64,128]{2,1,0:T(8,128)(2,1)S(1)}, u32[]{:S(2)}, u32[]{:S(2)}) collective-permute-start(bf16[25,64,128]{2,1,0:T(8,128)(2,1)} %collective-permute-done.5.rest_9_), channel_id=1, source_target_pairs={{4,0},{8,4},{12,8},{16,12},{20,16},{24,20},{28,24},{5,1},{9,5},{13... | collective-permute-start | bytes 1228808 | tf_op jit(solution)/shard_map/ppermute | solution.py:174
  70.8 3.6 %collective-permute-start.6 = (bf16[25,64,128]{2,1,0:T(8,128)(2,1)}, bf16[25,64,128]{2,1,0:T(8,128)(2,1)S(1)}, u32[]{:S(2)}, u32[]{:S(2)}) collective-permute-start(bf16[25,64,128]{2,1,0:T(8,128)(2,1)} %collective-permute-done.5.rest_9_), channel_id=1, source_target_pairs={{0,4},{4,8},{8,12},{12,16},{16,20},{20,24},{24,28},{1,5},{5,9},{9,... | collective-permute-start | bytes 1228808 | tf_op jit(solution)/shard_map/ppermute | solution.py:174
  74.5 0.7 broadcast_select_fusion.3
  75.2 1.9 %collective-permute-start.11 = (bf16[25,64,128]{2,1,0:T(8,128)(2,1)}, bf16[25,64,128]{2,1,0:T(8,128)(2,1)S(1)}, u32[]{:S(2)}, u32[]{:S(2)}) collective-permute-start(bf16[25,64,128]{2,1,0:T(8,128)(2,1)} %collective-permute-done.10.rest_6_), channel_id=1, source_target_pairs={{4,8},{8,12},{12,16},{16,20},{20,24},{24,28},{5,9},{9,13},{13,17},... | collective-permute-start | bytes 1228808 | tf_op jit(solution)/shard_map/ppermute | solution.py:174
  77.1 2.0 %collective-permute-done.16.rest_13_ = bf16[25,64,128]{2,1,0:T(8,128)(2,1)S(1)} collective-permute-done((bf16[25,64,128]{2,1,0:T(8,128)(2,1)}, bf16[25,64,128]{2,1,0:T(8,128)(2,1)S(1)}, u32[]{:S(2)}, u32[]{:S(2)}) %collective-permute-start.16) | collective-permute-done | bytes 409632 | tf_op jit(solution)/shard_map/ppermute | solution.py:174
  79.1 1.9 %collective-permute-start.20 = (bf16[25,64,128]{2,1,0:T(8,128)(2,1)S(1)}, bf16[25,64,128]{2,1,0:T(8,128)(2,1)S(1)}, u32[]{:S(2)}, u32[]{:S(2)}) collective-permute-start(bf16[25,64,128]{2,1,0:T(8,128)(2,1)S(1)} %collective-permute-done.17.rest_14_), channel_id=1, source_target_pairs={{4,0},{8,4},{12,8},{16,12},{20,16},{24,20},{5,1},{9,5},{13,9},{17,... | collective-permute-start | bytes 1228808 | tf_op jit(solution)/shard_map/ppermute | solution.py:174
  81.1 1.9 %collective-permute-start.19 = (bf16[25,64,128]{2,1,0:T(8,128)(2,1)S(1)}, bf16[25,64,128]{2,1,0:T(8,128)(2,1)S(1)}, u32[]{:S(2)}, u32[]{:S(2)}) collective-permute-start(bf16[25,64,128]{2,1,0:T(8,128)(2,1)S(1)} %collective-permute-done.16.rest_13_), channel_id=1, source_target_pairs={{4,0},{8,4},{12,8},{16,12},{20,16},{24,20},{5,1},{9,5},{13,9},{17,... | collective-permute-start | bytes 1228808 | tf_op jit(solution)/shard_map/ppermute | solution.py:174
  83.0 3.7 %collective-permute-start.7 = (bf16[25,64,128]{2,1,0:T(8,128)(2,1)S(1)}, bf16[25,64,128]{2,1,0:T(8,128)(2,1)S(1)}, u32[]{:S(2)}, u32[]{:S(2)}) collective-permute-start(bf16[25,64,128]{2,1,0:T(8,128)(2,1)S(1)} %collective-permute-done.6.rest_5_), channel_id=1, source_target_pairs={{4,8},{8,12},{12,16},{16,20},{20,24},{24,28},{5,9},{9,13},{13,17},... | collective-permute-start | bytes 1228808 | tf_op jit(solution)/shard_map/ppermute | solution.py:174
  86.7 0.7 broadcast_select_fusion.16
  87.4 0.0 copy-start.6
  87.4 1.3 collective-permute-done.20.rest_18_
  88.7 0.6 broadcast_select_fusion.4
  89.3 3.5 %collective-permute-done.19.rest_17_ = bf16[25,64,128]{2,1,0:T(8,128)(2,1)S(1)} collective-permute-done((bf16[25,64,128]{2,1,0:T(8,128)(2,1)S(1)}, bf16[25,64,128]{2,1,0:T(8,128)(2,1)S(1)}, u32[]{:S(2)}, u32[]{:S(2)}) %collective-permute-start.19) | collective-permute-done | bytes 409632 | tf_op jit(solution)/shard_map/ppermute | solution.py:174
  92.8 0.7 copy-done.15
  93.6 0.1 copy-done.16
  93.7 0.1 stack.54
  93.8 0.7 reshape.492.aggs_ref
  94.5 23.4 %shard_map.55 = f32[64,64,128]{2,1,0:T(8,128)} custom-call(s32[768]{0:T(1024)} %fusion.11.pair_ref, s32[768]{0:T(1024)} %get-tuple-element.47.half_ref, s32[768]{0:T(1024)} %get-tuple-element.31.agg_at_ref, s32[192]{0:T(256)} %get-tuple-element.53.own_agg_at_ref, s32[960]{0:T(1024)} %reshape.492.aggs_ref, s32[1]{0:T(128)} %bitcast.37.base_ref, ...), custom_call_target="tpu_custom_call" | custom-call | tf_op jit(solution)/shard_map/pallas_call | solution.py:112
  117.8 1.6 %bitcast_convert_fusion.2 = (bf16[8,2,64,128]{3,2,1,0:T(8,128)(2,1)S(1)}, bf16[8,2,64,128]{3,2,1,0:T(8,128)(2,1)S(1)}, bf16[8,2,64,128]{3,2,1,0:T(8,128)(2,1)S(1)}) fusion(f32[4,8,2,64,128]{4,3,2,1,0:T(8,128)} %bitcast.141, s32[]{:T(128)S(6)} %select_n.510, pred[]{:T(512)S(6)} %and.92, s32[]{:T(128)S(6)} %select_n.514, pred[]{:T(512)S(6)} %and.94, ...), kind=kLoop, calls=%fused_computation.7 | loop fusion | flops 393216 | bytes 1572879 | tf_op jit(solution)/shard_map/convert_element_type | solution.py:254
  119.4 1.3 collective-permute-start.22
  120.7 0.2 collective-permute-start.23
  120.9 1.3 collective-permute-start.24
  122.2 5.6 %collective-permute-done.22 = bf16[8,2,64,128]{3,2,1,0:T(8,128)(2,1)S(1)} collective-permute-done((bf16[8,2,64,128]{3,2,1,0:T(8,128)(2,1)S(1)}, bf16[8,2,64,128]{3,2,1,0:T(8,128)(2,1)S(1)}, u32[]{:S(2)}, u32[]{:S(2)}) %collective-permute-start.22) | collective-permute-done | bytes 262176 | tf_op jit(solution)/shard_map/ppermute | solution.py:253
  127.8 5.1 %collective-permute-done.23 = bf16[8,2,64,128]{3,2,1,0:T(8,128)(2,1)S(1)} collective-permute-done((bf16[8,2,64,128]{3,2,1,0:T(8,128)(2,1)S(1)}, bf16[8,2,64,128]{3,2,1,0:T(8,128)(2,1)S(1)}, u32[]{:S(2)}, u32[]{:S(2)}) %collective-permute-start.23) | collective-permute-done | bytes 262176 | tf_op jit(solution)/shard_map/ppermute | solution.py:253
  132.9 1.2 fusion.2
  134.1 0.2 fusion.34
  134.3 1.1 pad_maximum_fusion
  (68 shorter events, 0.3 us)
Async XLA Ops:
  0.0 8.6 %copy-start.17 = (s32[192,4]{0,1:T(4,128)S(1)}, s32[192,4]{0,1:T(4,128)}, u32[]{:S(2)}) copy-start(s32[192,4]{0,1:T(4,128)} %param.10) | copy-start | bytes 9220
  0.7 9.2 %copy-start.18 = (s32[192]{0:T(256)S(1)}, s32[192]{0:T(256)}, u32[]{:S(2)}) copy-start(s32[192]{0:T(256)} %param.11) | copy-start | bytes 2308
  3.0 28.4 %copy-start.4 = (bf16[25,64,128]{2,1,0:T(8,128)(2,1)}, bf16[25,64,128]{2,1,0:T(8,128)(2,1)S(1)}, u32[]{:S(2)}) copy-start(bf16[25,64,128]{2,1,0:T(8,128)(2,1)S(1)} %fusion.3.rest_8_) | copy-start | bytes 1228804
  3.0 9.5 %collective-permute-start = (bf16[25,64,128]{2,1,0:T(8,128)(2,1)S(1)}, bf16[25,64,128]{2,1,0:T(8,128)(2,1)S(1)}, u32[]{:S(2)}, u32[]{:S(2)}) collective-permute-start(bf16[25,64,128]{2,1,0:T(8,128)(2,1)S(1)} %fusion.3.rest_8_), channel_id=1, source_target_pairs={{28,0},{0,4},{4,8},{8,12},{12,16},{16,20},{20,24},{24,28},{29,1},{... | collective-permute-start | bytes 1228808 | tf_op jit(solution)/shard_map/ppermute | solution.py:174
  4.9 11.8 %collective-permute-start.2 = (bf16[25,64,128]{2,1,0:T(8,128)(2,1)S(1)}, bf16[25,64,128]{2,1,0:T(8,128)(2,1)S(1)}, u32[]{:S(2)}, u32[]{:S(2)}) collective-permute-start(bf16[25,64,128]{2,1,0:T(8,128)(2,1)S(1)} %fusion.3.rest_8_), channel_id=1, source_target_pairs={{4,0},{8,4},{12,8},{16,12},{20,16},{24,20},{28,24},{0,28},{5,1},{9... | collective-permute-start | bytes 1228808 | tf_op jit(solution)/shard_map/ppermute | solution.py:174
  5.0 11.8 %collective-permute-start.13 = (bf16[25,64,128]{2,1,0:T(8,128)(2,1)S(1)}, bf16[25,64,128]{2,1,0:T(8,128)(2,1)}, u32[]{:S(2)}, u32[]{:S(2)}) collective-permute-start(bf16[25,64,128]{2,1,0:T(8,128)(2,1)S(1)} %fusion.3.rest_8_), channel_id=1, source_target_pairs={{0,3},{1,0},{2,1},{3,2},{4,7},{5,4},{6,5},{7,6},{8,11},{9,8},{10,9... | collective-permute-start | bytes 1228808 | tf_op jit(solution)/shard_map/ppermute | solution.py:162
  5.2 19.6 %collective-permute-start.9 = (bf16[25,64,128]{2,1,0:T(8,128)(2,1)S(1)}, bf16[25,64,128]{2,1,0:T(8,128)(2,1)}, u32[]{:S(2)}, u32[]{:S(2)}) collective-permute-start(bf16[25,64,128]{2,1,0:T(8,128)(2,1)S(1)} %fusion.3.rest_8_), channel_id=1, source_target_pairs={{0,2},{1,3},{2,0},{3,1},{4,6},{5,7},{6,4},{7,5},{8,10},{9,11},{10,... | collective-permute-start | bytes 1228808 | tf_op jit(solution)/shard_map/ppermute | solution.py:162
  6.4 26.4 %collective-permute-start.5 = (bf16[25,64,128]{2,1,0:T(8,128)(2,1)S(1)}, bf16[25,64,128]{2,1,0:T(8,128)(2,1)}, u32[]{:S(2)}, u32[]{:S(2)}) collective-permute-start(bf16[25,64,128]{2,1,0:T(8,128)(2,1)S(1)} %fusion.3.rest_8_), channel_id=1, source_target_pairs={{0,1},{1,2},{2,3},{3,0},{4,5},{5,6},{6,7},{7,4},{8,9},{9,10},{10,1... | collective-permute-start | bytes 1228808 | tf_op jit(solution)/shard_map/ppermute | solution.py:162
  12.6 39.7 %copy-start = (bf16[25,64,128]{2,1,0:T(8,128)(2,1)}, bf16[25,64,128]{2,1,0:T(8,128)(2,1)S(1)}, u32[]{:S(2)}) copy-start(bf16[25,64,128]{2,1,0:T(8,128)(2,1)S(1)} %collective-permute-done.rest_4_) | copy-start | bytes 1228804
  12.6 15.3 %collective-permute-start.1 = (bf16[25,64,128]{2,1,0:T(8,128)(2,1)S(1)}, bf16[25,64,128]{2,1,0:T(8,128)(2,1)S(1)}, u32[]{:S(2)}, u32[]{:S(2)}) collective-permute-start(bf16[25,64,128]{2,1,0:T(8,128)(2,1)S(1)} %collective-permute-done.rest_4_), channel_id=1, source_target_pairs={{28,0},{0,4},{4,8},{8,12},{12,16},{16,20},{20,24},{24,28},{29,1},{... | collective-permute-start | bytes 1228808 | tf_op jit(solution)/shard_map/ppermute | solution.py:174
  16.7 35.5 %copy-start.1 = (bf16[25,64,128]{2,1,0:T(8,128)(2,1)}, bf16[25,64,128]{2,1,0:T(8,128)(2,1)S(1)}, u32[]{:S(2)}) copy-start(bf16[25,64,128]{2,1,0:T(8,128)(2,1)S(1)} %collective-permute-done.2.rest_12_) | copy-start | bytes 1228804
  16.7 13.7 %collective-permute-start.3 = (bf16[25,64,128]{2,1,0:T(8,128)(2,1)S(1)}, bf16[25,64,128]{2,1,0:T(8,128)(2,1)S(1)}, u32[]{:S(2)}, u32[]{:S(2)}) collective-permute-start(bf16[25,64,128]{2,1,0:T(8,128)(2,1)S(1)} %collective-permute-done.2.rest_12_), channel_id=1, source_target_pairs={{4,0},{8,4},{12,8},{16,12},{20,16},{24,20},{28,24},{0,28},{5,1},{9... | collective-permute-start | bytes 1228808 | tf_op jit(solution)/shard_map/ppermute | solution.py:174
  16.8 18.3 %collective-permute-start.14 = (bf16[25,64,128]{2,1,0:T(8,128)(2,1)}, bf16[25,64,128]{2,1,0:T(8,128)(2,1)S(1)}, u32[]{:S(2)}, u32[]{:S(2)}) collective-permute-start(bf16[25,64,128]{2,1,0:T(8,128)(2,1)} %collective-permute-done.13.rest_11_), channel_id=1, source_target_pairs={{0,4},{4,8},{8,12},{12,16},{16,20},{20,24},{24,28},{1,5},{5,9},{9,... | collective-permute-start | bytes 1228808 | tf_op jit(solution)/shard_map/ppermute | solution.py:174
  24.8 34.5 %collective-permute-start.18 = (bf16[25,64,128]{2,1,0:T(8,128)(2,1)}, bf16[25,64,128]{2,1,0:T(8,128)(2,1)}, u32[]{:S(2)}, u32[]{:S(2)}) collective-permute-start(bf16[25,64,128]{2,1,0:T(8,128)(2,1)} %collective-permute-done.13.rest_11_), channel_id=1, source_target_pairs={{4,0},{8,4},{12,8},{16,12},{20,16},{24,20},{28,24},{5,1},{9,5},{13... | collective-permute-start | bytes 1228808 | tf_op jit(solution)/shard_map/ppermute | solution.py:174
  27.9 33.4 %copy-start.2 = (bf16[25,64,128]{2,1,0:T(8,128)(2,1)}, bf16[25,64,128]{2,1,0:T(8,128)(2,1)S(1)}, u32[]{:S(2)}) copy-start(bf16[25,64,128]{2,1,0:T(8,128)(2,1)S(1)} %collective-permute-done.1.rest_0_) | copy-start | bytes 1228804
  27.9 33.4 %collective-permute-start.10 = (bf16[25,64,128]{2,1,0:T(8,128)(2,1)}, bf16[25,64,128]{2,1,0:T(8,128)(2,1)}, u32[]{:S(2)}, u32[]{:S(2)}) collective-permute-start(bf16[25,64,128]{2,1,0:T(8,128)(2,1)} %collective-permute-done.9.rest_10_), channel_id=1, source_target_pairs={{0,4},{4,8},{8,12},{12,16},{16,20},{20,24},{24,28},{1,5},{5,9},{9,... | collective-permute-start | bytes 1228808 | tf_op jit(solution)/shard_map/ppermute | solution.py:174
  30.4 31.6 %copy-start.3 = (bf16[25,64,128]{2,1,0:T(8,128)(2,1)}, bf16[25,64,128]{2,1,0:T(8,128)(2,1)S(1)}, u32[]{:S(2)}) copy-start(bf16[25,64,128]{2,1,0:T(8,128)(2,1)S(1)} %collective-permute-done.3.rest_16_) | copy-start | bytes 1228804
  31.5 39.3 %collective-permute-start.12 = (bf16[2,25,64,128]{3,2,1,0:T(8,128)(2,1)}, bf16[2,25,64,128]{3,2,1,0:T(8,128)(2,1)S(1)}, u32[]{:S(2)}, u32[]{:S(2)}) collective-permute-start(bf16[2,25,64,128]{3,2,1,0:T(8,128)(2,1)} %pad_maximum_fusion.1), channel_id=1, source_target_pairs={{0,3},{1,0},{2,1},{3,2},{4,7},{5,4},{6,5},{7,6},{24,27},{25,24},{2... | collective-permute-start | bytes 2457608 | tf_op jit(solution)/shard_map/ppermute | solution.py:193
  33.5 49.5 %collective-permute-start.8 = (bf16[2,25,64,128]{3,2,1,0:T(8,128)(2,1)}, bf16[2,25,64,128]{3,2,1,0:T(8,128)(2,1)}, u32[]{:S(2)}, u32[]{:S(2)}) collective-permute-start(bf16[2,25,64,128]{3,2,1,0:T(8,128)(2,1)} %pad_maximum_fusion.1), channel_id=1, source_target_pairs={{0,2},{1,3},{2,0},{3,1},{4,6},{5,7},{6,4},{7,5},{24,26},{25,27},{2... | collective-permute-start | bytes 2457608 | tf_op jit(solution)/shard_map/ppermute | solution.py:193
  35.1 39.3 %copy-start.7 = (bf16[25,64,128]{2,1,0:T(8,128)(2,1)}, bf16[25,64,128]{2,1,0:T(8,128)(2,1)S(1)}, u32[]{:S(2)}) copy-start(bf16[25,64,128]{2,1,0:T(8,128)(2,1)S(1)} %collective-permute-done.14.rest_7_) | copy-start | bytes 1228804
  52.2 12.0 %collective-permute-start.15 = (bf16[25,64,128]{2,1,0:T(8,128)(2,1)S(1)}, bf16[25,64,128]{2,1,0:T(8,128)(2,1)S(1)}, u32[]{:S(2)}, u32[]{:S(2)}) collective-permute-start(bf16[25,64,128]{2,1,0:T(8,128)(2,1)S(1)} %collective-permute-done.14.rest_7_), channel_id=1, source_target_pairs={{4,8},{8,12},{12,16},{16,20},{20,24},{24,28},{5,9},{9,13},{13,17},... | collective-permute-start | bytes 1228808 | tf_op jit(solution)/shard_map/ppermute | solution.py:174
  59.4 9.5 %collective-permute-start.21 = (bf16[25,64,128]{2,1,0:T(8,128)(2,1)}, bf16[25,64,128]{2,1,0:T(8,128)(2,1)S(1)}, u32[]{:S(2)}, u32[]{:S(2)}) collective-permute-start(bf16[25,64,128]{2,1,0:T(8,128)(2,1)} %collective-permute-done.18.rest_15_), channel_id=1, source_target_pairs={{4,0},{8,4},{12,8},{16,12},{20,16},{24,20},{5,1},{9,5},{13,9},{17,... | collective-permute-start | bytes 1228808 | tf_op jit(solution)/shard_map/ppermute | solution.py:174
  61.3 26.0 %collective-permute-start.4 = (bf16[2,25,64,128]{3,2,1,0:T(8,128)(2,1)}, bf16[2,25,64,128]{3,2,1,0:T(8,128)(2,1)S(1)}, u32[]{:S(2)}, u32[]{:S(2)}) collective-permute-start(bf16[2,25,64,128]{3,2,1,0:T(8,128)(2,1)} %pad_maximum_fusion.1), channel_id=1, source_target_pairs={{0,1},{1,2},{2,3},{3,0},{4,5},{5,6},{6,7},{7,4},{24,25},{25,26},{2... | collective-permute-start | bytes 2457608 | tf_op jit(solution)/shard_map/ppermute | solution.py:193
  64.2 30.2 %copy-start.8 = (bf16[25,64,128]{2,1,0:T(8,128)(2,1)}, bf16[25,64,128]{2,1,0:T(8,128)(2,1)S(1)}, u32[]{:S(2)}) copy-start(bf16[25,64,128]{2,1,0:T(8,128)(2,1)S(1)} %collective-permute-done.15.rest_3_) | copy-start | bytes 1228804
  64.2 10.9 %collective-permute-start.17 = (bf16[25,64,128]{2,1,0:T(8,128)(2,1)}, bf16[25,64,128]{2,1,0:T(8,128)(2,1)S(1)}, u32[]{:S(2)}, u32[]{:S(2)}) collective-permute-start(bf16[25,64,128]{2,1,0:T(8,128)(2,1)} %collective-permute-done.9.rest_10_), channel_id=1, source_target_pairs={{4,0},{8,4},{12,8},{16,12},{20,16},{24,20},{28,24},{5,1},{9,5},{13... | collective-permute-start | bytes 1228808 | tf_op jit(solution)/shard_map/ppermute | solution.py:174
  68.9 18.5 %copy-start.9 = (bf16[25,64,128]{2,1,0:T(8,128)(2,1)}, bf16[25,64,128]{2,1,0:T(8,128)(2,1)S(1)}, u32[]{:S(2)}) copy-start(bf16[25,64,128]{2,1,0:T(8,128)(2,1)S(1)} %collective-permute-done.21.rest_19_) | copy-start | bytes 1228804
  68.9 10.3 %collective-permute-start.16 = (bf16[25,64,128]{2,1,0:T(8,128)(2,1)}, bf16[25,64,128]{2,1,0:T(8,128)(2,1)S(1)}, u32[]{:S(2)}, u32[]{:S(2)}) collective-permute-start(bf16[25,64,128]{2,1,0:T(8,128)(2,1)} %collective-permute-done.5.rest_9_), channel_id=1, source_target_pairs={{4,0},{8,4},{12,8},{16,12},{20,16},{24,20},{28,24},{5,1},{9,5},{13... | collective-permute-start | bytes 1228808 | tf_op jit(solution)/shard_map/ppermute | solution.py:174
  70.8 23.7 %copy-start.5 = (bf16[2,25,64,128]{3,2,1,0:T(8,128)(2,1)}, bf16[2,25,64,128]{3,2,1,0:T(8,128)(2,1)S(1)}, u32[]{:S(2)}) copy-start(bf16[2,25,64,128]{3,2,1,0:T(8,128)(2,1)S(1)} %collective-permute-done.12.rest_22_) | copy-start | bytes 2457604
  70.8 10.3 %collective-permute-start.6 = (bf16[25,64,128]{2,1,0:T(8,128)(2,1)}, bf16[25,64,128]{2,1,0:T(8,128)(2,1)S(1)}, u32[]{:S(2)}, u32[]{:S(2)}) collective-permute-start(bf16[25,64,128]{2,1,0:T(8,128)(2,1)} %collective-permute-done.5.rest_9_), channel_id=1, source_target_pairs={{0,4},{4,8},{8,12},{12,16},{16,20},{20,24},{24,28},{1,5},{5,9},{9,... | collective-permute-start | bytes 1228808 | tf_op jit(solution)/shard_map/ppermute | solution.py:174
  75.2 19.3 %copy-start.10 = (bf16[25,64,128]{2,1,0:T(8,128)(2,1)}, bf16[25,64,128]{2,1,0:T(8,128)(2,1)S(1)}, u32[]{:S(2)}) copy-start(bf16[25,64,128]{2,1,0:T(8,128)(2,1)S(1)} %collective-permute-done.17.rest_14_) | copy-start | bytes 1228804
  75.2 12.2 %collective-permute-start.11 = (bf16[25,64,128]{2,1,0:T(8,128)(2,1)}, bf16[25,64,128]{2,1,0:T(8,128)(2,1)S(1)}, u32[]{:S(2)}, u32[]{:S(2)}) collective-permute-start(bf16[25,64,128]{2,1,0:T(8,128)(2,1)} %collective-permute-done.10.rest_6_), channel_id=1, source_target_pairs={{4,8},{8,12},{12,16},{16,20},{20,24},{24,28},{5,9},{9,13},{13,17},... | collective-permute-start | bytes 1228808 | tf_op jit(solution)/shard_map/ppermute | solution.py:174
  79.1 15.3 %copy-start.11 = (bf16[25,64,128]{2,1,0:T(8,128)(2,1)}, bf16[25,64,128]{2,1,0:T(8,128)(2,1)S(1)}, u32[]{:S(2)}) copy-start(bf16[25,64,128]{2,1,0:T(8,128)(2,1)S(1)} %collective-permute-done.16.rest_13_) | copy-start | bytes 1228804
  79.1 9.6 %collective-permute-start.20 = (bf16[25,64,128]{2,1,0:T(8,128)(2,1)S(1)}, bf16[25,64,128]{2,1,0:T(8,128)(2,1)S(1)}, u32[]{:S(2)}, u32[]{:S(2)}) collective-permute-start(bf16[25,64,128]{2,1,0:T(8,128)(2,1)S(1)} %collective-permute-done.17.rest_14_), channel_id=1, source_target_pairs={{4,0},{8,4},{12,8},{16,12},{20,16},{24,20},{5,1},{9,5},{13,9},{17,... | collective-permute-start | bytes 1228808 | tf_op jit(solution)/shard_map/ppermute | solution.py:174
  81.1 11.7 %copy-start.12 = (bf16[25,64,128]{2,1,0:T(8,128)(2,1)}, bf16[25,64,128]{2,1,0:T(8,128)(2,1)S(1)}, u32[]{:S(2)}) copy-start(bf16[25,64,128]{2,1,0:T(8,128)(2,1)S(1)} %collective-permute-done.6.rest_5_) | copy-start | bytes 1228804
  81.1 11.7 %collective-permute-start.19 = (bf16[25,64,128]{2,1,0:T(8,128)(2,1)S(1)}, bf16[25,64,128]{2,1,0:T(8,128)(2,1)S(1)}, u32[]{:S(2)}, u32[]{:S(2)}) collective-permute-start(bf16[25,64,128]{2,1,0:T(8,128)(2,1)S(1)} %collective-permute-done.16.rest_13_), channel_id=1, source_target_pairs={{4,0},{8,4},{12,8},{16,12},{20,16},{24,20},{5,1},{9,5},{13,9},{17,... | collective-permute-start | bytes 1228808 | tf_op jit(solution)/shard_map/ppermute | solution.py:174
  83.0 9.8 %collective-permute-start.7 = (bf16[25,64,128]{2,1,0:T(8,128)(2,1)S(1)}, bf16[25,64,128]{2,1,0:T(8,128)(2,1)S(1)}, u32[]{:S(2)}, u32[]{:S(2)}) collective-permute-start(bf16[25,64,128]{2,1,0:T(8,128)(2,1)S(1)} %collective-permute-done.6.rest_5_), channel_id=1, source_target_pairs={{4,8},{8,12},{12,16},{16,20},{20,24},{24,28},{5,9},{9,13},{13,17},... | collective-permute-start | bytes 1228808 | tf_op jit(solution)/shard_map/ppermute | solution.py:174
  87.4 7.1 %copy-start.6 = (bf16[2,25,64,128]{3,2,1,0:T(8,128)(2,1)}, bf16[2,25,64,128]{3,2,1,0:T(8,128)(2,1)S(1)}, u32[]{:S(2)}) copy-start(bf16[2,25,64,128]{3,2,1,0:T(8,128)(2,1)S(1)} %collective-permute-done.4.rest_20_) | copy-start | bytes 2457604
  87.4 7.0 %copy-start.13 = (bf16[25,64,128]{2,1,0:T(8,128)(2,1)}, bf16[25,64,128]{2,1,0:T(8,128)(2,1)S(1)}, u32[]{:S(2)}) copy-start(bf16[25,64,128]{2,1,0:T(8,128)(2,1)S(1)} %collective-permute-done.11.rest_2_) | copy-start | bytes 1228804
  88.7 4.1 %copy-start.14 = (bf16[25,64,128]{2,1,0:T(8,128)(2,1)}, bf16[25,64,128]{2,1,0:T(8,128)(2,1)S(1)}, u32[]{:S(2)}) copy-start(bf16[25,64,128]{2,1,0:T(8,128)(2,1)S(1)} %collective-permute-done.20.rest_18_) | copy-start | bytes 1228804
  92.8 0.8 copy-start.15
  92.8 0.9 copy-start.16
  119.4 8.4 %collective-permute-start.22 = (bf16[8,2,64,128]{3,2,1,0:T(8,128)(2,1)S(1)}, bf16[8,2,64,128]{3,2,1,0:T(8,128)(2,1)S(1)}, u32[]{:S(2)}, u32[]{:S(2)}) collective-permute-start(bf16[8,2,64,128]{3,2,1,0:T(8,128)(2,1)S(1)} %get-tuple-element.33), channel_id=1, source_target_pairs={{0,1},{1,2},{2,3},{3,0},{4,5},{5,6},{6,7},{7,4},{8,9},{9,10},{10,1... | collective-permute-start | bytes 786440 | tf_op jit(solution)/shard_map/ppermute | solution.py:253
  120.7 12.3 %collective-permute-start.23 = (bf16[8,2,64,128]{3,2,1,0:T(8,128)(2,1)S(1)}, bf16[8,2,64,128]{3,2,1,0:T(8,128)(2,1)S(1)}, u32[]{:S(2)}, u32[]{:S(2)}) collective-permute-start(bf16[8,2,64,128]{3,2,1,0:T(8,128)(2,1)S(1)} %get-tuple-element.35), channel_id=1, source_target_pairs={{0,2},{1,3},{2,0},{3,1},{4,6},{5,7},{6,4},{7,5},{8,10},{9,11},{10,... | collective-permute-start | bytes 786440 | tf_op jit(solution)/shard_map/ppermute | solution.py:253
  120.9 12.0 %collective-permute-start.24 = (bf16[8,2,64,128]{3,2,1,0:T(8,128)(2,1)S(1)}, bf16[8,2,64,128]{3,2,1,0:T(8,128)(2,1)S(1)}, u32[]{:S(2)}, u32[]{:S(2)}) collective-permute-start(bf16[8,2,64,128]{3,2,1,0:T(8,128)(2,1)S(1)} %get-tuple-element.34), channel_id=1, source_target_pairs={{0,3},{1,0},{2,1},{3,2},{4,7},{5,4},{6,5},{7,6},{8,11},{9,8},{10,9... | collective-permute-start | bytes 786440 | tf_op jit(solution)/shard_map/ppermute | solution.py:253

commit v18 on v17

--- a/solution.py
+++ b/solution.py
@@ -8,7 +8,7 @@
 from jax.sharding import PartitionSpec as P
 
 CB = 4
-ROWS_PER_STEP = 48
+ROWS_PER_STEP = 96
 
 
 def passed_along(block, axis, distance):

time: 137 us -> 138 us (level)
  Pallas kernels: 23.4 us -> 24.9 us
    pallas_call x1, Pallas kernels: 23.4 us -> 24.9 us  [coarse_partial(): pl.pallas_call(coarse_kernel, out_shape=jax.ShapeDtypeStruct((n_targets /...]
where the time goes in v18:
time: 138 us; the launch traced here: 137 us
  starting transfers between devices  52 us (38%)
  local copies, waits for them, and re-layouts  25.4 us (18%)
  Pallas kernels  24.9 us (18%)
  waiting for transfers between devices  24.6 us (18%)
  other arithmetic  9.52 us (7%)
    ppermute x16, starting transfers between devices, ring(): return lax.ppermute(piece, 'blk', route)  42.7 us
    pallas_call x1, Pallas kernels, coarse_partial(): pl.pallas_call(coarse_kernel, out_shape=jax.ShapeDtypeStruct((n_targets /...  24.9 us
    optimization_barrier x1, local copies, waits for them, and re-layouts, local(): block_values, _ = lax.optimization_barrier((block_values, down1[-1]))  17.1 us
    ppermute x16, waiting for transfers between devices, ring(): return lax.ppermute(piece, 'blk', route)  11.6 us
    ppermute x3, waiting for transfers between devices, local(): lax.ppermute(outgoing.astype(jnp.bfloat16), 'grp', [(i, (i + k) % group_s...  10.8 us
    ppermute x3, starting transfers between devices, local(): lax.ppermute(local_ext, 'grp', [(i, (i + k) % group_size) for i in range(...  3.6 us
    ppermute x3, starting transfers between devices, local(): fixed.append(lax.ppermute(fix_src, ('blk', 'grp'), route))  2.97 us
  transfers between devices with their start and end apart: 25, of which 8 were waited for; matrix products, arithmetic and copies ran while one was open for 19% of the time, Pallas kernels for 0%

profile of v18, /device:TPU:19, one launch (start us, length us, event | category | flops | bytes accessed | tf_op | source)
XLA Modules:
  0.0 137.0 jit_solution(8370382656856453801)
XLA Ops:
  0.0 0.7 convert_bitcast_fusion
  0.7 2.0 %copy.14 = bf16[24,2,64,64]{3,1,2,0:T(2,128)(2,1)S(1)} copy(bf16[24,2,64,64]{3,2,1,0:T(8,128)(2,1)} %bitcast.144) | data formatting | bytes 786432 | tf_op jit(solution)/shard_map/reshape | solution.py:148
  2.6 0.3 reshape.425
  3.0 1.9 %collective-permute-start = (bf16[25,64,128]{2,1,0:T(8,128)(2,1)S(1)}, bf16[25,64,128]{2,1,0:T(8,128)(2,1)S(1)}, u32[]{:S(2)}, u32[]{:S(2)}) collective-permute-start(bf16[25,64,128]{2,1,0:T(8,128)(2,1)S(1)} %fusion.3.rest_8_), channel_id=1, source_target_pairs={{28,0},{0,4},{4,8},{8,12},{12,16},{16,20},{20,24},{24,28},{29,1},{... | collective-permute-start | bytes 1228808 | tf_op jit(solution)/shard_map/ppermute | solution.py:174
  5.0 0.3 collective-permute-start.13
  5.2 1.2 collective-permute-start.9
  6.4 2.1 %collective-permute-start.5 = (bf16[25,64,128]{2,1,0:T(8,128)(2,1)S(1)}, bf16[25,64,128]{2,1,0:T(8,128)(2,1)}, u32[]{:S(2)}, u32[]{:S(2)}) collective-permute-start(bf16[25,64,128]{2,1,0:T(8,128)(2,1)S(1)} %fusion.3.rest_8_), channel_id=1, source_target_pairs={{0,1},{1,2},{2,3},{3,0},{4,5},{5,6},{6,7},{7,4},{8,9},{9,10},{10,1... | collective-permute-start | bytes 1228808 | tf_op jit(solution)/shard_map/ppermute | solution.py:162
  8.6 0.6 fusion.20
  9.1 0.1 copy.9
  9.3 0.1 rem.165
  9.4 0.1 copy.10
  9.5 0.1 div.36
  9.6 0.2 copy.8
  9.8 0.1 ne.114
  9.9 0.1 compare_convert_fusion
  10.0 0.7 reshape.493.live_ref
  10.7 0.6 stack.59.fix_ref
  11.4 0.6 multiply_add_fusion
  12.0 0.6 fusion.11.pair_ref
  12.6 4.1 %collective-permute-start.1 = (bf16[25,64,128]{2,1,0:T(8,128)(2,1)S(1)}, bf16[25,64,128]{2,1,0:T(8,128)(2,1)S(1)}, u32[]{:S(2)}, u32[]{:S(2)}) collective-permute-start(bf16[25,64,128]{2,1,0:T(8,128)(2,1)S(1)} %collective-permute-done.rest_4_), channel_id=1, source_target_pairs={{28,0},{0,4},{4,8},{8,12},{12,16},{16,20},{20,24},{24,28},{29,1},{... | collective-permute-start | bytes 1228808 | tf_op jit(solution)/shard_map/ppermute | solution.py:174
  16.8 5.2 %collective-permute-start.14 = (bf16[25,64,128]{2,1,0:T(8,128)(2,1)}, bf16[25,64,128]{2,1,0:T(8,128)(2,1)S(1)}, u32[]{:S(2)}, u32[]{:S(2)}) collective-permute-start(bf16[25,64,128]{2,1,0:T(8,128)(2,1)} %collective-permute-done.13.rest_11_), channel_id=1, source_target_pairs={{0,4},{4,8},{8,12},{12,16},{16,20},{20,24},{24,28},{1,5},{5,9},{9,... | collective-permute-start | bytes 1228808 | tf_op jit(solution)/shard_map/ppermute | solution.py:174
  21.9 0.7 slice_bitcast_fusion.8
  22.7 2.2 %collective-permute-done.9.rest_10_ = bf16[25,64,128]{2,1,0:T(8,128)(2,1)} collective-permute-done((bf16[25,64,128]{2,1,0:T(8,128)(2,1)S(1)}, bf16[25,64,128]{2,1,0:T(8,128)(2,1)}, u32[]{:S(2)}, u32[]{:S(2)}) %collective-permute-start.9) | collective-permute-done | bytes 409632 | tf_op jit(solution)/shard_map/ppermute | solution.py:162
  24.8 3.0 %collective-permute-start.18 = (bf16[25,64,128]{2,1,0:T(8,128)(2,1)}, bf16[25,64,128]{2,1,0:T(8,128)(2,1)}, u32[]{:S(2)}, u32[]{:S(2)}) collective-permute-start(bf16[25,64,128]{2,1,0:T(8,128)(2,1)} %collective-permute-done.13.rest_11_), channel_id=1, source_target_pairs={{4,0},{8,4},{12,8},{16,12},{20,16},{24,20},{28,24},{5,1},{9,5},{13... | collective-permute-start | bytes 1228808 | tf_op jit(solution)/shard_map/ppermute | solution.py:174
  27.9 2.5 %collective-permute-start.10 = (bf16[25,64,128]{2,1,0:T(8,128)(2,1)}, bf16[25,64,128]{2,1,0:T(8,128)(2,1)}, u32[]{:S(2)}, u32[]{:S(2)}) collective-permute-start(bf16[25,64,128]{2,1,0:T(8,128)(2,1)} %collective-permute-done.9.rest_10_), channel_id=1, source_target_pairs={{0,4},{4,8},{8,12},{12,16},{16,20},{20,24},{24,28},{1,5},{5,9},{9,... | collective-permute-start | bytes 1228808 | tf_op jit(solution)/shard_map/ppermute | solution.py:174
  30.5 1.0 pad_maximum_fusion.1
  31.5 0.7 collective-permute-start.12
  32.2 0.7 slice_bitcast_fusion.9
  32.9 0.7 slice_bitcast_fusion.10
  33.5 1.6 %collective-permute-start.8 = (bf16[2,25,64,128]{3,2,1,0:T(8,128)(2,1)}, bf16[2,25,64,128]{3,2,1,0:T(8,128)(2,1)}, u32[]{:S(2)}, u32[]{:S(2)}) collective-permute-start(bf16[2,25,64,128]{3,2,1,0:T(8,128)(2,1)} %pad_maximum_fusion.1), channel_id=1, source_target_pairs={{0,2},{1,3},{2,0},{3,1},{4,6},{5,7},{6,4},{7,5},{24,26},{25,27},{2... | collective-permute-start | bytes 2457608 | tf_op jit(solution)/shard_map/ppermute | solution.py:193
  35.1 17.1 %copy.12.values_ref = bf16[192,4,64,64]{3,2,1,0:T(8,128)(2,1)} copy(bf16[192,4,64,64]{0,3,2,1:T(8,128)(2,1)} %param.9) | data formatting | bytes 12582912 | tf_op jit(solution)/shard_map/optimization_barrier | solution.py:232
  52.2 7.1 %collective-permute-start.15 = (bf16[25,64,128]{2,1,0:T(8,128)(2,1)S(1)}, bf16[25,64,128]{2,1,0:T(8,128)(2,1)S(1)}, u32[]{:S(2)}, u32[]{:S(2)}) collective-permute-start(bf16[25,64,128]{2,1,0:T(8,128)(2,1)S(1)} %collective-permute-done.14.rest_7_), channel_id=1, source_target_pairs={{4,8},{8,12},{12,16},{16,20},{20,24},{24,28},{5,9},{9,13},{13,17},... | collective-permute-start | bytes 1228808 | tf_op jit(solution)/shard_map/ppermute | solution.py:174
  59.4 1.9 %collective-permute-start.21 = (bf16[25,64,128]{2,1,0:T(8,128)(2,1)}, bf16[25,64,128]{2,1,0:T(8,128)(2,1)S(1)}, u32[]{:S(2)}, u32[]{:S(2)}) collective-permute-start(bf16[25,64,128]{2,1,0:T(8,128)(2,1)} %collective-permute-done.18.rest_15_), channel_id=1, source_target_pairs={{4,0},{8,4},{12,8},{16,12},{20,16},{24,20},{5,1},{9,5},{13,9},{17,... | collective-permute-start | bytes 1228808 | tf_op jit(solution)/shard_map/ppermute | solution.py:174
  61.3 0.7 collective-permute-start.4
  62.1 2.2 %collective-permute-done.15.rest_3_ = bf16[25,64,128]{2,1,0:T(8,128)(2,1)S(1)} collective-permute-done((bf16[25,64,128]{2,1,0:T(8,128)(2,1)S(1)}, bf16[25,64,128]{2,1,0:T(8,128)(2,1)S(1)}, u32[]{:S(2)}, u32[]{:S(2)}) %collective-permute-start.15) | collective-permute-done | bytes 409632 | tf_op jit(solution)/shard_map/ppermute | solution.py:174
  64.2 1.9 %collective-permute-start.17 = (bf16[25,64,128]{2,1,0:T(8,128)(2,1)}, bf16[25,64,128]{2,1,0:T(8,128)(2,1)S(1)}, u32[]{:S(2)}, u32[]{:S(2)}) collective-permute-start(bf16[25,64,128]{2,1,0:T(8,128)(2,1)} %collective-permute-done.9.rest_10_), channel_id=1, source_target_pairs={{4,0},{8,4},{12,8},{16,12},{20,16},{24,20},{28,24},{5,1},{9,5},{13... | collective-permute-start | bytes 1228808 | tf_op jit(solution)/shard_map/ppermute | solution.py:174
  66.2 2.7 %collective-permute-done.21.rest_19_ = bf16[25,64,128]{2,1,0:T(8,128)(2,1)S(1)} collective-permute-done((bf16[25,64,128]{2,1,0:T(8,128)(2,1)}, bf16[25,64,128]{2,1,0:T(8,128)(2,1)S(1)}, u32[]{:S(2)}, u32[]{:S(2)}) %collective-permute-start.21) | collective-permute-done | bytes 409632 | tf_op jit(solution)/shard_map/ppermute | solution.py:174
  68.9 1.9 %collective-permute-start.16 = (bf16[25,64,128]{2,1,0:T(8,128)(2,1)}, bf16[25,64,128]{2,1,0:T(8,128)(2,1)S(1)}, u32[]{:S(2)}, u32[]{:S(2)}) collective-permute-start(bf16[25,64,128]{2,1,0:T(8,128)(2,1)} %collective-permute-done.5.rest_9_), channel_id=1, source_target_pairs={{4,0},{8,4},{12,8},{16,12},{20,16},{24,20},{28,24},{5,1},{9,5},{13... | collective-permute-start | bytes 1228808 | tf_op jit(solution)/shard_map/ppermute | solution.py:174
  70.8 3.6 %collective-permute-start.6 = (bf16[25,64,128]{2,1,0:T(8,128)(2,1)}, bf16[25,64,128]{2,1,0:T(8,128)(2,1)S(1)}, u32[]{:S(2)}, u32[]{:S(2)}) collective-permute-start(bf16[25,64,128]{2,1,0:T(8,128)(2,1)} %collective-permute-done.5.rest_9_), channel_id=1, source_target_pairs={{0,4},{4,8},{8,12},{12,16},{16,20},{20,24},{24,28},{1,5},{5,9},{9,... | collective-permute-start | bytes 1228808 | tf_op jit(solution)/shard_map/ppermute | solution.py:174
  74.5 0.7 broadcast_select_fusion.3
  75.2 1.9 %collective-permute-start.11 = (bf16[25,64,128]{2,1,0:T(8,128)(2,1)}, bf16[25,64,128]{2,1,0:T(8,128)(2,1)S(1)}, u32[]{:S(2)}, u32[]{:S(2)}) collective-permute-start(bf16[25,64,128]{2,1,0:T(8,128)(2,1)} %collective-permute-done.10.rest_6_), channel_id=1, source_target_pairs={{4,8},{8,12},{12,16},{16,20},{20,24},{24,28},{5,9},{9,13},{13,17},... | collective-permute-start | bytes 1228808 | tf_op jit(solution)/shard_map/ppermute | solution.py:174
  77.1 2.0 %collective-permute-done.16.rest_13_ = bf16[25,64,128]{2,1,0:T(8,128)(2,1)S(1)} collective-permute-done((bf16[25,64,128]{2,1,0:T(8,128)(2,1)}, bf16[25,64,128]{2,1,0:T(8,128)(2,1)S(1)}, u32[]{:S(2)}, u32[]{:S(2)}) %collective-permute-start.16) | collective-permute-done | bytes 409632 | tf_op jit(solution)/shard_map/ppermute | solution.py:174
  79.1 1.9 %collective-permute-start.20 = (bf16[25,64,128]{2,1,0:T(8,128)(2,1)S(1)}, bf16[25,64,128]{2,1,0:T(8,128)(2,1)S(1)}, u32[]{:S(2)}, u32[]{:S(2)}) collective-permute-start(bf16[25,64,128]{2,1,0:T(8,128)(2,1)S(1)} %collective-permute-done.17.rest_14_), channel_id=1, source_target_pairs={{4,0},{8,4},{12,8},{16,12},{20,16},{24,20},{5,1},{9,5},{13,9},{17,... | collective-permute-start | bytes 1228808 | tf_op jit(solution)/shard_map/ppermute | solution.py:174
  81.1 1.9 %collective-permute-start.19 = (bf16[25,64,128]{2,1,0:T(8,128)(2,1)S(1)}, bf16[25,64,128]{2,1,0:T(8,128)(2,1)S(1)}, u32[]{:S(2)}, u32[]{:S(2)}) collective-permute-start(bf16[25,64,128]{2,1,0:T(8,128)(2,1)S(1)} %collective-permute-done.16.rest_13_), channel_id=1, source_target_pairs={{4,0},{8,4},{12,8},{16,12},{20,16},{24,20},{5,1},{9,5},{13,9},{17,... | collective-permute-start | bytes 1228808 | tf_op jit(solution)/shard_map/ppermute | solution.py:174
  83.0 3.7 %collective-permute-start.7 = (bf16[25,64,128]{2,1,0:T(8,128)(2,1)S(1)}, bf16[25,64,128]{2,1,0:T(8,128)(2,1)S(1)}, u32[]{:S(2)}, u32[]{:S(2)}) collective-permute-start(bf16[25,64,128]{2,1,0:T(8,128)(2,1)S(1)} %collective-permute-done.6.rest_5_), channel_id=1, source_target_pairs={{4,8},{8,12},{12,16},{16,20},{20,24},{24,28},{5,9},{9,13},{13,17},... | collective-permute-start | bytes 1228808 | tf_op jit(solution)/shard_map/ppermute | solution.py:174
  86.7 0.7 broadcast_select_fusion.16
  87.4 0.0 copy-start.6
  87.4 1.3 collective-permute-done.20.rest_18_
  88.7 0.6 broadcast_select_fusion.4
  89.3 3.5 %collective-permute-done.19.rest_17_ = bf16[25,64,128]{2,1,0:T(8,128)(2,1)S(1)} collective-permute-done((bf16[25,64,128]{2,1,0:T(8,128)(2,1)S(1)}, bf16[25,64,128]{2,1,0:T(8,128)(2,1)S(1)}, u32[]{:S(2)}, u32[]{:S(2)}) %collective-permute-start.19) | collective-permute-done | bytes 409632 | tf_op jit(solution)/shard_map/ppermute | solution.py:174
  92.8 0.7 copy-done.15
  93.6 0.1 copy-done.16
  93.7 0.1 stack.54
  93.8 0.7 reshape.492.aggs_ref
  94.5 24.9 %shard_map.55 = f32[64,64,128]{2,1,0:T(8,128)} custom-call(s32[768]{0:T(1024)} %fusion.11.pair_ref, s32[768]{0:T(1024)} %get-tuple-element.47.half_ref, s32[768]{0:T(1024)} %get-tuple-element.31.agg_at_ref, s32[192]{0:T(256)} %get-tuple-element.53.own_agg_at_ref, s32[960]{0:T(1024)} %reshape.492.aggs_ref, s32[1]{0:T(128)} %bitcast.37.base_ref, ...), custom_call_target="tpu_custom_call" | custom-call | tf_op jit(solution)/shard_map/pallas_call | solution.py:112
  119.4 1.6 %bitcast_convert_fusion.2 = (bf16[8,2,64,128]{3,2,1,0:T(8,128)(2,1)S(1)}, bf16[8,2,64,128]{3,2,1,0:T(8,128)(2,1)S(1)}, bf16[8,2,64,128]{3,2,1,0:T(8,128)(2,1)S(1)}) fusion(f32[4,8,2,64,128]{4,3,2,1,0:T(8,128)} %bitcast.141, s32[]{:T(128)S(6)} %select_n.510, pred[]{:T(512)S(6)} %and.92, s32[]{:T(128)S(6)} %select_n.514, pred[]{:T(512)S(6)} %and.94, ...), kind=kLoop, calls=%fused_computation.7 | loop fusion | flops 393216 | bytes 1572879 | tf_op jit(solution)/shard_map/convert_element_type | solution.py:254
  121.0 1.3 collective-permute-start.22
  122.3 0.2 collective-permute-start.23
  122.5 1.3 collective-permute-start.24
  123.8 5.6 %collective-permute-done.22 = bf16[8,2,64,128]{3,2,1,0:T(8,128)(2,1)S(1)} collective-permute-done((bf16[8,2,64,128]{3,2,1,0:T(8,128)(2,1)S(1)}, bf16[8,2,64,128]{3,2,1,0:T(8,128)(2,1)S(1)}, u32[]{:S(2)}, u32[]{:S(2)}) %collective-permute-start.22) | collective-permute-done | bytes 262176 | tf_op jit(solution)/shard_map/ppermute | solution.py:253
  129.4 5.1 %collective-permute-done.23 = bf16[8,2,64,128]{3,2,1,0:T(8,128)(2,1)S(1)} collective-permute-done((bf16[8,2,64,128]{3,2,1,0:T(8,128)(2,1)S(1)}, bf16[8,2,64,128]{3,2,1,0:T(8,128)(2,1)S(1)}, u32[]{:S(2)}, u32[]{:S(2)}) %collective-permute-start.23) | collective-permute-done | bytes 262176 | tf_op jit(solution)/shard_map/ppermute | solution.py:253
  134.5 1.2 fusion.2
  135.7 0.2 fusion.34
  135.9 1.1 pad_maximum_fusion
  (68 shorter events, 0.3 us)
Async XLA Ops:
  0.0 8.6 %copy-start.17 = (s32[192,4]{0,1:T(4,128)S(1)}, s32[192,4]{0,1:T(4,128)}, u32[]{:S(2)}) copy-start(s32[192,4]{0,1:T(4,128)} %param.10) | copy-start | bytes 9220
  0.7 9.2 %copy-start.18 = (s32[192]{0:T(256)S(1)}, s32[192]{0:T(256)}, u32[]{:S(2)}) copy-start(s32[192]{0:T(256)} %param.11) | copy-start | bytes 2308
  3.0 28.4 %copy-start.4 = (bf16[25,64,128]{2,1,0:T(8,128)(2,1)}, bf16[25,64,128]{2,1,0:T(8,128)(2,1)S(1)}, u32[]{:S(2)}) copy-start(bf16[25,64,128]{2,1,0:T(8,128)(2,1)S(1)} %fusion.3.rest_8_) | copy-start | bytes 1228804
  3.0 9.5 %collective-permute-start = (bf16[25,64,128]{2,1,0:T(8,128)(2,1)S(1)}, bf16[25,64,128]{2,1,0:T(8,128)(2,1)S(1)}, u32[]{:S(2)}, u32[]{:S(2)}) collective-permute-start(bf16[25,64,128]{2,1,0:T(8,128)(2,1)S(1)} %fusion.3.rest_8_), channel_id=1, source_target_pairs={{28,0},{0,4},{4,8},{8,12},{12,16},{16,20},{20,24},{24,28},{29,1},{... | collective-permute-start | bytes 1228808 | tf_op jit(solution)/shard_map/ppermute | solution.py:174
  4.9 11.8 %collective-permute-start.2 = (bf16[25,64,128]{2,1,0:T(8,128)(2,1)S(1)}, bf16[25,64,128]{2,1,0:T(8,128)(2,1)S(1)}, u32[]{:S(2)}, u32[]{:S(2)}) collective-permute-start(bf16[25,64,128]{2,1,0:T(8,128)(2,1)S(1)} %fusion.3.rest_8_), channel_id=1, source_target_pairs={{4,0},{8,4},{12,8},{16,12},{20,16},{24,20},{28,24},{0,28},{5,1},{9... | collective-permute-start | bytes 1228808 | tf_op jit(solution)/shard_map/ppermute | solution.py:174
  5.0 11.8 %collective-permute-start.13 = (bf16[25,64,128]{2,1,0:T(8,128)(2,1)S(1)}, bf16[25,64,128]{2,1,0:T(8,128)(2,1)}, u32[]{:S(2)}, u32[]{:S(2)}) collective-permute-start(bf16[25,64,128]{2,1,0:T(8,128)(2,1)S(1)} %fusion.3.rest_8_), channel_id=1, source_target_pairs={{0,3},{1,0},{2,1},{3,2},{4,7},{5,4},{6,5},{7,6},{8,11},{9,8},{10,9... | collective-permute-start | bytes 1228808 | tf_op jit(solution)/shard_map/ppermute | solution.py:162
  5.2 19.6 %collective-permute-start.9 = (bf16[25,64,128]{2,1,0:T(8,128)(2,1)S(1)}, bf16[25,64,128]{2,1,0:T(8,128)(2,1)}, u32[]{:S(2)}, u32[]{:S(2)}) collective-permute-start(bf16[25,64,128]{2,1,0:T(8,128)(2,1)S(1)} %fusion.3.rest_8_), channel_id=1, source_target_pairs={{0,2},{1,3},{2,0},{3,1},{4,6},{5,7},{6,4},{7,5},{8,10},{9,11},{10,... | collective-permute-start | bytes 1228808 | tf_op jit(solution)/shard_map/ppermute | solution.py:162
  6.4 26.4 %collective-permute-start.5 = (bf16[25,64,128]{2,1,0:T(8,128)(2,1)S(1)}, bf16[25,64,128]{2,1,0:T(8,128)(2,1)}, u32[]{:S(2)}, u32[]{:S(2)}) collective-permute-start(bf16[25,64,128]{2,1,0:T(8,128)(2,1)S(1)} %fusion.3.rest_8_), channel_id=1, source_target_pairs={{0,1},{1,2},{2,3},{3,0},{4,5},{5,6},{6,7},{7,4},{8,9},{9,10},{10,1... | collective-permute-start | bytes 1228808 | tf_op jit(solution)/shard_map/ppermute | solution.py:162
  12.6 39.7 %copy-start = (bf16[25,64,128]{2,1,0:T(8,128)(2,1)}, bf16[25,64,128]{2,1,0:T(8,128)(2,1)S(1)}, u32[]{:S(2)}) copy-start(bf16[25,64,128]{2,1,0:T(8,128)(2,1)S(1)} %collective-permute-done.rest_4_) | copy-start | bytes 1228804
  12.6 15.3 %collective-permute-start.1 = (bf16[25,64,128]{2,1,0:T(8,128)(2,1)S(1)}, bf16[25,64,128]{2,1,0:T(8,128)(2,1)S(1)}, u32[]{:S(2)}, u32[]{:S(2)}) collective-permute-start(bf16[25,64,128]{2,1,0:T(8,128)(2,1)S(1)} %collective-permute-done.rest_4_), channel_id=1, source_target_pairs={{28,0},{0,4},{4,8},{8,12},{12,16},{16,20},{20,24},{24,28},{29,1},{... | collective-permute-start | bytes 1228808 | tf_op jit(solution)/shard_map/ppermute | solution.py:174
  16.7 35.5 %copy-start.1 = (bf16[25,64,128]{2,1,0:T(8,128)(2,1)}, bf16[25,64,128]{2,1,0:T(8,128)(2,1)S(1)}, u32[]{:S(2)}) copy-start(bf16[25,64,128]{2,1,0:T(8,128)(2,1)S(1)} %collective-permute-done.2.rest_12_) | copy-start | bytes 1228804
  16.7 13.7 %collective-permute-start.3 = (bf16[25,64,128]{2,1,0:T(8,128)(2,1)S(1)}, bf16[25,64,128]{2,1,0:T(8,128)(2,1)S(1)}, u32[]{:S(2)}, u32[]{:S(2)}) collective-permute-start(bf16[25,64,128]{2,1,0:T(8,128)(2,1)S(1)} %collective-permute-done.2.rest_12_), channel_id=1, source_target_pairs={{4,0},{8,4},{12,8},{16,12},{20,16},{24,20},{28,24},{0,28},{5,1},{9... | collective-permute-start | bytes 1228808 | tf_op jit(solution)/shard_map/ppermute | solution.py:174
  16.8 18.3 %collective-permute-start.14 = (bf16[25,64,128]{2,1,0:T(8,128)(2,1)}, bf16[25,64,128]{2,1,0:T(8,128)(2,1)S(1)}, u32[]{:S(2)}, u32[]{:S(2)}) collective-permute-start(bf16[25,64,128]{2,1,0:T(8,128)(2,1)} %collective-permute-done.13.rest_11_), channel_id=1, source_target_pairs={{0,4},{4,8},{8,12},{12,16},{16,20},{20,24},{24,28},{1,5},{5,9},{9,... | collective-permute-start | bytes 1228808 | tf_op jit(solution)/shard_map/ppermute | solution.py:174
  24.8 34.5 %collective-permute-start.18 = (bf16[25,64,128]{2,1,0:T(8,128)(2,1)}, bf16[25,64,128]{2,1,0:T(8,128)(2,1)}, u32[]{:S(2)}, u32[]{:S(2)}) collective-permute-start(bf16[25,64,128]{2,1,0:T(8,128)(2,1)} %collective-permute-done.13.rest_11_), channel_id=1, source_target_pairs={{4,0},{8,4},{12,8},{16,12},{20,16},{24,20},{28,24},{5,1},{9,5},{13... | collective-permute-start | bytes 1228808 | tf_op jit(solution)/shard_map/ppermute | solution.py:174
  27.9 33.4 %copy-start.2 = (bf16[25,64,128]{2,1,0:T(8,128)(2,1)}, bf16[25,64,128]{2,1,0:T(8,128)(2,1)S(1)}, u32[]{:S(2)}) copy-start(bf16[25,64,128]{2,1,0:T(8,128)(2,1)S(1)} %collective-permute-done.1.rest_0_) | copy-start | bytes 1228804
  27.9 33.4 %collective-permute-start.10 = (bf16[25,64,128]{2,1,0:T(8,128)(2,1)}, bf16[25,64,128]{2,1,0:T(8,128)(2,1)}, u32[]{:S(2)}, u32[]{:S(2)}) collective-permute-start(bf16[25,64,128]{2,1,0:T(8,128)(2,1)} %collective-permute-done.9.rest_10_), channel_id=1, source_target_pairs={{0,4},{4,8},{8,12},{12,16},{16,20},{20,24},{24,28},{1,5},{5,9},{9,... | collective-permute-start | bytes 1228808 | tf_op jit(solution)/shard_map/ppermute | solution.py:174
  30.4 31.6 %copy-start.3 = (bf16[25,64,128]{2,1,0:T(8,128)(2,1)}, bf16[25,64,128]{2,1,0:T(8,128)(2,1)S(1)}, u32[]{:S(2)}) copy-start(bf16[25,64,128]{2,1,0:T(8,128)(2,1)S(1)} %collective-permute-done.3.rest_16_) | copy-start | bytes 1228804
  31.5 39.3 %collective-permute-start.12 = (bf16[2,25,64,128]{3,2,1,0:T(8,128)(2,1)}, bf16[2,25,64,128]{3,2,1,0:T(8,128)(2,1)S(1)}, u32[]{:S(2)}, u32[]{:S(2)}) collective-permute-start(bf16[2,25,64,128]{3,2,1,0:T(8,128)(2,1)} %pad_maximum_fusion.1), channel_id=1, source_target_pairs={{0,3},{1,0},{2,1},{3,2},{4,7},{5,4},{6,5},{7,6},{24,27},{25,24},{2... | collective-permute-start | bytes 2457608 | tf_op jit(solution)/shard_map/ppermute | solution.py:193
  33.5 49.5 %collective-permute-start.8 = (bf16[2,25,64,128]{3,2,1,0:T(8,128)(2,1)}, bf16[2,25,64,128]{3,2,1,0:T(8,128)(2,1)}, u32[]{:S(2)}, u32[]{:S(2)}) collective-permute-start(bf16[2,25,64,128]{3,2,1,0:T(8,128)(2,1)} %pad_maximum_fusion.1), channel_id=1, source_target_pairs={{0,2},{1,3},{2,0},{3,1},{4,6},{5,7},{6,4},{7,5},{24,26},{25,27},{2... | collective-permute-start | bytes 2457608 | tf_op jit(solution)/shard_map/ppermute | solution.py:193
  35.1 39.3 %copy-start.7 = (bf16[25,64,128]{2,1,0:T(8,128)(2,1)}, bf16[25,64,128]{2,1,0:T(8,128)(2,1)S(1)}, u32[]{:S(2)}) copy-start(bf16[25,64,128]{2,1,0:T(8,128)(2,1)S(1)} %collective-permute-done.14.rest_7_) | copy-start | bytes 1228804
  52.2 12.0 %collective-permute-start.15 = (bf16[25,64,128]{2,1,0:T(8,128)(2,1)S(1)}, bf16[25,64,128]{2,1,0:T(8,128)(2,1)S(1)}, u32[]{:S(2)}, u32[]{:S(2)}) collective-permute-start(bf16[25,64,128]{2,1,0:T(8,128)(2,1)S(1)} %collective-permute-done.14.rest_7_), channel_id=1, source_target_pairs={{4,8},{8,12},{12,16},{16,20},{20,24},{24,28},{5,9},{9,13},{13,17},... | collective-permute-start | bytes 1228808 | tf_op jit(solution)/shard_map/ppermute | solution.py:174
  59.4 9.5 %collective-permute-start.21 = (bf16[25,64,128]{2,1,0:T(8,128)(2,1)}, bf16[25,64,128]{2,1,0:T(8,128)(2,1)S(1)}, u32[]{:S(2)}, u32[]{:S(2)}) collective-permute-start(bf16[25,64,128]{2,1,0:T(8,128)(2,1)} %collective-permute-done.18.rest_15_), channel_id=1, source_target_pairs={{4,0},{8,4},{12,8},{16,12},{20,16},{24,20},{5,1},{9,5},{13,9},{17,... | collective-permute-start | bytes 1228808 | tf_op jit(solution)/shard_map/ppermute | solution.py:174
  61.3 26.0 %collective-permute-start.4 = (bf16[2,25,64,128]{3,2,1,0:T(8,128)(2,1)}, bf16[2,25,64,128]{3,2,1,0:T(8,128)(2,1)S(1)}, u32[]{:S(2)}, u32[]{:S(2)}) collective-permute-start(bf16[2,25,64,128]{3,2,1,0:T(8,128)(2,1)} %pad_maximum_fusion.1), channel_id=1, source_target_pairs={{0,1},{1,2},{2,3},{3,0},{4,5},{5,6},{6,7},{7,4},{24,25},{25,26},{2... | collective-permute-start | bytes 2457608 | tf_op jit(solution)/shard_map/ppermute | solution.py:193
  64.2 30.2 %copy-start.8 = (bf16[25,64,128]{2,1,0:T(8,128)(2,1)}, bf16[25,64,128]{2,1,0:T(8,128)(2,1)S(1)}, u32[]{:S(2)}) copy-start(bf16[25,64,128]{2,1,0:T(8,128)(2,1)S(1)} %collective-permute-done.15.rest_3_) | copy-start | bytes 1228804
  64.2 10.9 %collective-permute-start.17 = (bf16[25,64,128]{2,1,0:T(8,128)(2,1)}, bf16[25,64,128]{2,1,0:T(8,128)(2,1)S(1)}, u32[]{:S(2)}, u32[]{:S(2)}) collective-permute-start(bf16[25,64,128]{2,1,0:T(8,128)(2,1)} %collective-permute-done.9.rest_10_), channel_id=1, source_target_pairs={{4,0},{8,4},{12,8},{16,12},{20,16},{24,20},{28,24},{5,1},{9,5},{13... | collective-permute-start | bytes 1228808 | tf_op jit(solution)/shard_map/ppermute | solution.py:174
  68.9 18.5 %copy-start.9 = (bf16[25,64,128]{2,1,0:T(8,128)(2,1)}, bf16[25,64,128]{2,1,0:T(8,128)(2,1)S(1)}, u32[]{:S(2)}) copy-start(bf16[25,64,128]{2,1,0:T(8,128)(2,1)S(1)} %collective-permute-done.21.rest_19_) | copy-start | bytes 1228804
  68.9 10.3 %collective-permute-start.16 = (bf16[25,64,128]{2,1,0:T(8,128)(2,1)}, bf16[25,64,128]{2,1,0:T(8,128)(2,1)S(1)}, u32[]{:S(2)}, u32[]{:S(2)}) collective-permute-start(bf16[25,64,128]{2,1,0:T(8,128)(2,1)} %collective-permute-done.5.rest_9_), channel_id=1, source_target_pairs={{4,0},{8,4},{12,8},{16,12},{20,16},{24,20},{28,24},{5,1},{9,5},{13... | collective-permute-start | bytes 1228808 | tf_op jit(solution)/shard_map/ppermute | solution.py:174
  70.8 23.7 %copy-start.5 = (bf16[2,25,64,128]{3,2,1,0:T(8,128)(2,1)}, bf16[2,25,64,128]{3,2,1,0:T(8,128)(2,1)S(1)}, u32[]{:S(2)}) copy-start(bf16[2,25,64,128]{3,2,1,0:T(8,128)(2,1)S(1)} %collective-permute-done.12.rest_22_) | copy-start | bytes 2457604
  70.8 10.3 %collective-permute-start.6 = (bf16[25,64,128]{2,1,0:T(8,128)(2,1)}, bf16[25,64,128]{2,1,0:T(8,128)(2,1)S(1)}, u32[]{:S(2)}, u32[]{:S(2)}) collective-permute-start(bf16[25,64,128]{2,1,0:T(8,128)(2,1)} %collective-permute-done.5.rest_9_), channel_id=1, source_target_pairs={{0,4},{4,8},{8,12},{12,16},{16,20},{20,24},{24,28},{1,5},{5,9},{9,... | collective-permute-start | bytes 1228808 | tf_op jit(solution)/shard_map/ppermute | solution.py:174
  75.2 19.3 %copy-start.10 = (bf16[25,64,128]{2,1,0:T(8,128)(2,1)}, bf16[25,64,128]{2,1,0:T(8,128)(2,1)S(1)}, u32[]{:S(2)}) copy-start(bf16[25,64,128]{2,1,0:T(8,128)(2,1)S(1)} %collective-permute-done.17.rest_14_) | copy-start | bytes 1228804
  75.2 12.2 %collective-permute-start.11 = (bf16[25,64,128]{2,1,0:T(8,128)(2,1)}, bf16[25,64,128]{2,1,0:T(8,128)(2,1)S(1)}, u32[]{:S(2)}, u32[]{:S(2)}) collective-permute-start(bf16[25,64,128]{2,1,0:T(8,128)(2,1)} %collective-permute-done.10.rest_6_), channel_id=1, source_target_pairs={{4,8},{8,12},{12,16},{16,20},{20,24},{24,28},{5,9},{9,13},{13,17},... | collective-permute-start | bytes 1228808 | tf_op jit(solution)/shard_map/ppermute | solution.py:174
  79.1 15.3 %copy-start.11 = (bf16[25,64,128]{2,1,0:T(8,128)(2,1)}, bf16[25,64,128]{2,1,0:T(8,128)(2,1)S(1)}, u32[]{:S(2)}) copy-start(bf16[25,64,128]{2,1,0:T(8,128)(2,1)S(1)} %collective-permute-done.16.rest_13_) | copy-start | bytes 1228804
  79.1 9.6 %collective-permute-start.20 = (bf16[25,64,128]{2,1,0:T(8,128)(2,1)S(1)}, bf16[25,64,128]{2,1,0:T(8,128)(2,1)S(1)}, u32[]{:S(2)}, u32[]{:S(2)}) collective-permute-start(bf16[25,64,128]{2,1,0:T(8,128)(2,1)S(1)} %collective-permute-done.17.rest_14_), channel_id=1, source_target_pairs={{4,0},{8,4},{12,8},{16,12},{20,16},{24,20},{5,1},{9,5},{13,9},{17,... | collective-permute-start | bytes 1228808 | tf_op jit(solution)/shard_map/ppermute | solution.py:174
  81.1 11.7 %copy-start.12 = (bf16[25,64,128]{2,1,0:T(8,128)(2,1)}, bf16[25,64,128]{2,1,0:T(8,128)(2,1)S(1)}, u32[]{:S(2)}) copy-start(bf16[25,64,128]{2,1,0:T(8,128)(2,1)S(1)} %collective-permute-done.6.rest_5_) | copy-start | bytes 1228804
  81.1 11.7 %collective-permute-start.19 = (bf16[25,64,128]{2,1,0:T(8,128)(2,1)S(1)}, bf16[25,64,128]{2,1,0:T(8,128)(2,1)S(1)}, u32[]{:S(2)}, u32[]{:S(2)}) collective-permute-start(bf16[25,64,128]{2,1,0:T(8,128)(2,1)S(1)} %collective-permute-done.16.rest_13_), channel_id=1, source_target_pairs={{4,0},{8,4},{12,8},{16,12},{20,16},{24,20},{5,1},{9,5},{13,9},{17,... | collective-permute-start | bytes 1228808 | tf_op jit(solution)/shard_map/ppermute | solution.py:174
  83.0 9.8 %collective-permute-start.7 = (bf16[25,64,128]{2,1,0:T(8,128)(2,1)S(1)}, bf16[25,64,128]{2,1,0:T(8,128)(2,1)S(1)}, u32[]{:S(2)}, u32[]{:S(2)}) collective-permute-start(bf16[25,64,128]{2,1,0:T(8,128)(2,1)S(1)} %collective-permute-done.6.rest_5_), channel_id=1, source_target_pairs={{4,8},{8,12},{12,16},{16,20},{20,24},{24,28},{5,9},{9,13},{13,17},... | collective-permute-start | bytes 1228808 | tf_op jit(solution)/shard_map/ppermute | solution.py:174
  87.4 7.1 %copy-start.6 = (bf16[2,25,64,128]{3,2,1,0:T(8,128)(2,1)}, bf16[2,25,64,128]{3,2,1,0:T(8,128)(2,1)S(1)}, u32[]{:S(2)}) copy-start(bf16[2,25,64,128]{3,2,1,0:T(8,128)(2,1)S(1)} %collective-permute-done.4.rest_20_) | copy-start | bytes 2457604
  87.4 7.0 %copy-start.13 = (bf16[25,64,128]{2,1,0:T(8,128)(2,1)}, bf16[25,64,128]{2,1,0:T(8,128)(2,1)S(1)}, u32[]{:S(2)}) copy-start(bf16[25,64,128]{2,1,0:T(8,128)(2,1)S(1)} %collective-permute-done.11.rest_2_) | copy-start | bytes 1228804
  88.7 4.1 %copy-start.14 = (bf16[25,64,128]{2,1,0:T(8,128)(2,1)}, bf16[25,64,128]{2,1,0:T(8,128)(2,1)S(1)}, u32[]{:S(2)}) copy-start(bf16[25,64,128]{2,1,0:T(8,128)(2,1)S(1)} %collective-permute-done.20.rest_18_) | copy-start | bytes 1228804
  92.8 0.8 copy-start.15
  92.8 0.9 copy-start.16
  121.0 8.4 %collective-permute-start.22 = (bf16[8,2,64,128]{3,2,1,0:T(8,128)(2,1)S(1)}, bf16[8,2,64,128]{3,2,1,0:T(8,128)(2,1)S(1)}, u32[]{:S(2)}, u32[]{:S(2)}) collective-permute-start(bf16[8,2,64,128]{3,2,1,0:T(8,128)(2,1)S(1)} %get-tuple-element.33), channel_id=1, source_target_pairs={{0,1},{1,2},{2,3},{3,0},{4,5},{5,6},{6,7},{7,4},{8,9},{9,10},{10,1... | collective-permute-start | bytes 786440 | tf_op jit(solution)/shard_map/ppermute | solution.py:253
  122.3 12.3 %collective-permute-start.23 = (bf16[8,2,64,128]{3,2,1,0:T(8,128)(2,1)S(1)}, bf16[8,2,64,128]{3,2,1,0:T(8,128)(2,1)S(1)}, u32[]{:S(2)}, u32[]{:S(2)}) collective-permute-start(bf16[8,2,64,128]{3,2,1,0:T(8,128)(2,1)S(1)} %get-tuple-element.35), channel_id=1, source_target_pairs={{0,2},{1,3},{2,0},{3,1},{4,6},{5,7},{6,4},{7,5},{8,10},{9,11},{10,... | collective-permute-start | bytes 786440 | tf_op jit(solution)/shard_map/ppermute | solution.py:253
  122.5 12.0 %collective-permute-start.24 = (bf16[8,2,64,128]{3,2,1,0:T(8,128)(2,1)S(1)}, bf16[8,2,64,128]{3,2,1,0:T(8,128)(2,1)S(1)}, u32[]{:S(2)}, u32[]{:S(2)}) collective-permute-start(bf16[8,2,64,128]{3,2,1,0:T(8,128)(2,1)S(1)} %get-tuple-element.34), channel_id=1, source_target_pairs={{0,3},{1,0},{2,1},{3,2},{4,7},{5,4},{6,5},{7,6},{8,11},{9,8},{10,9... | collective-permute-start | bytes 786440 | tf_op jit(solution)/shard_map/ppermute | solution.py:253

commit v19 on v17

--- a/solution.py
+++ b/solution.py
@@ -89,7 +89,7 @@
             accs[s][t] = accs[s][t] + results[s]
         return carry
 
-    lax.fori_loop(0, rows_here, row_body, 0, unroll=16)
+    lax.fori_loop(0, rows_here, row_body, 0, unroll=rows_here)
 
     @pl.when(step == pl.num_programs(0) - 1)
     def _():

time: 137 us -> 135 us (0.985)
  Pallas kernels: 23.4 us -> 21.3 us
    pallas_call x1, Pallas kernels: 23.4 us -> 21.3 us  [coarse_partial(): pl.pallas_call(coarse_kernel, out_shape=jax.ShapeDtypeStruct((n_targets /...]
  transfers between devices with their start and end apart: 25 -> 25, of which waited for: 8 -> 8; matrix products, arithmetic and copies ran while one was open for 19% -> 20% of each run, Pallas kernels for 0% -> 0%
where the time goes in v19:
time: 135 us; the launch traced here: 133 us
  starting transfers between devices  52 us (39%)
  local copies, waits for them, and re-layouts  25.4 us (19%)
  waiting for transfers between devices  24.6 us (18%)
  Pallas kernels  21.3 us (16%)
  other arithmetic  9.52 us (7%)
    ppermute x16, starting transfers between devices, ring(): return lax.ppermute(piece, 'blk', route)  42.7 us
    pallas_call x1, Pallas kernels, coarse_partial(): pl.pallas_call(coarse_kernel, out_shape=jax.ShapeDtypeStruct((n_targets /...  21.3 us
    optimization_barrier x1, local copies, waits for them, and re-layouts, local(): block_values, _ = lax.optimization_barrier((block_values, down1[-1]))  17.1 us
    ppermute x16, waiting for transfers between devices, ring(): return lax.ppermute(piece, 'blk', route)  11.6 us
    ppermute x3, waiting for transfers between devices, local(): lax.ppermute(outgoing.astype(jnp.bfloat16), 'grp', [(i, (i + k) % group_s...  10.8 us
    ppermute x3, starting transfers between devices, local(): lax.ppermute(local_ext, 'grp', [(i, (i + k) % group_size) for i in range(...  3.6 us
    ppermute x3, starting transfers between devices, local(): fixed.append(lax.ppermute(fix_src, ('blk', 'grp'), route))  2.97 us
    ppermute x3, starting transfers between devices, local(): lax.ppermute(outgoing.astype(jnp.bfloat16), 'grp', [(i, (i + k) % group_s...  2.76 us
  transfers between devices with their start and end apart: 25, of which 8 were waited for; matrix products, arithmetic and copies ran while one was open for 20% of the time, Pallas kernels for 0%

profile of v19, /device:TPU:19, one launch (start us, length us, event | category | flops | bytes accessed | tf_op | source)
XLA Modules:
  0.0 133.3 jit_solution(18316928590861113241)
XLA Ops:
  0.0 0.7 convert_bitcast_fusion
  0.7 2.0 %copy.14 = bf16[24,2,64,64]{3,1,2,0:T(2,128)(2,1)S(1)} copy(bf16[24,2,64,64]{3,2,1,0:T(8,128)(2,1)} %bitcast.144) | data formatting | bytes 786432 | tf_op jit(solution)/shard_map/reshape | solution.py:148
  2.6 0.3 reshape.425
  3.0 1.9 %collective-permute-start = (bf16[25,64,128]{2,1,0:T(8,128)(2,1)S(1)}, bf16[25,64,128]{2,1,0:T(8,128)(2,1)S(1)}, u32[]{:S(2)}, u32[]{:S(2)}) collective-permute-start(bf16[25,64,128]{2,1,0:T(8,128)(2,1)S(1)} %fusion.3.rest_8_), channel_id=1, source_target_pairs={{28,0},{0,4},{4,8},{8,12},{12,16},{16,20},{20,24},{24,28},{29,1},{... | collective-permute-start | bytes 1228808 | tf_op jit(solution)/shard_map/ppermute | solution.py:174
  5.0 0.3 collective-permute-start.13
  5.2 1.2 collective-permute-start.9
  6.4 2.1 %collective-permute-start.5 = (bf16[25,64,128]{2,1,0:T(8,128)(2,1)S(1)}, bf16[25,64,128]{2,1,0:T(8,128)(2,1)}, u32[]{:S(2)}, u32[]{:S(2)}) collective-permute-start(bf16[25,64,128]{2,1,0:T(8,128)(2,1)S(1)} %fusion.3.rest_8_), channel_id=1, source_target_pairs={{0,1},{1,2},{2,3},{3,0},{4,5},{5,6},{6,7},{7,4},{8,9},{9,10},{10,1... | collective-permute-start | bytes 1228808 | tf_op jit(solution)/shard_map/ppermute | solution.py:162
  8.6 0.6 fusion.20
  9.1 0.1 copy.9
  9.3 0.1 rem.165
  9.4 0.1 copy.10
  9.5 0.1 div.36
  9.6 0.2 copy.8
  9.8 0.1 ne.114
  9.9 0.1 compare_convert_fusion
  10.0 0.7 reshape.493.live_ref
  10.7 0.6 stack.59.fix_ref
  11.4 0.6 multiply_add_fusion
  12.0 0.6 fusion.11.pair_ref
  12.6 4.1 %collective-permute-start.1 = (bf16[25,64,128]{2,1,0:T(8,128)(2,1)S(1)}, bf16[25,64,128]{2,1,0:T(8,128)(2,1)S(1)}, u32[]{:S(2)}, u32[]{:S(2)}) collective-permute-start(bf16[25,64,128]{2,1,0:T(8,128)(2,1)S(1)} %collective-permute-done.rest_4_), channel_id=1, source_target_pairs={{28,0},{0,4},{4,8},{8,12},{12,16},{16,20},{20,24},{24,28},{29,1},{... | collective-permute-start | bytes 1228808 | tf_op jit(solution)/shard_map/ppermute | solution.py:174
  16.8 5.2 %collective-permute-start.14 = (bf16[25,64,128]{2,1,0:T(8,128)(2,1)}, bf16[25,64,128]{2,1,0:T(8,128)(2,1)S(1)}, u32[]{:S(2)}, u32[]{:S(2)}) collective-permute-start(bf16[25,64,128]{2,1,0:T(8,128)(2,1)} %collective-permute-done.13.rest_11_), channel_id=1, source_target_pairs={{0,4},{4,8},{8,12},{12,16},{16,20},{20,24},{24,28},{1,5},{5,9},{9,... | collective-permute-start | bytes 1228808 | tf_op jit(solution)/shard_map/ppermute | solution.py:174
  21.9 0.7 slice_bitcast_fusion.8
  22.7 2.2 %collective-permute-done.9.rest_10_ = bf16[25,64,128]{2,1,0:T(8,128)(2,1)} collective-permute-done((bf16[25,64,128]{2,1,0:T(8,128)(2,1)S(1)}, bf16[25,64,128]{2,1,0:T(8,128)(2,1)}, u32[]{:S(2)}, u32[]{:S(2)}) %collective-permute-start.9) | collective-permute-done | bytes 409632 | tf_op jit(solution)/shard_map/ppermute | solution.py:162
  24.8 3.0 %collective-permute-start.18 = (bf16[25,64,128]{2,1,0:T(8,128)(2,1)}, bf16[25,64,128]{2,1,0:T(8,128)(2,1)}, u32[]{:S(2)}, u32[]{:S(2)}) collective-permute-start(bf16[25,64,128]{2,1,0:T(8,128)(2,1)} %collective-permute-done.13.rest_11_), channel_id=1, source_target_pairs={{4,0},{8,4},{12,8},{16,12},{20,16},{24,20},{28,24},{5,1},{9,5},{13... | collective-permute-start | bytes 1228808 | tf_op jit(solution)/shard_map/ppermute | solution.py:174
  27.9 2.5 %collective-permute-start.10 = (bf16[25,64,128]{2,1,0:T(8,128)(2,1)}, bf16[25,64,128]{2,1,0:T(8,128)(2,1)}, u32[]{:S(2)}, u32[]{:S(2)}) collective-permute-start(bf16[25,64,128]{2,1,0:T(8,128)(2,1)} %collective-permute-done.9.rest_10_), channel_id=1, source_target_pairs={{0,4},{4,8},{8,12},{12,16},{16,20},{20,24},{24,28},{1,5},{5,9},{9,... | collective-permute-start | bytes 1228808 | tf_op jit(solution)/shard_map/ppermute | solution.py:174
  30.5 1.0 pad_maximum_fusion.1
  31.5 0.7 collective-permute-start.12
  32.2 0.7 slice_bitcast_fusion.9
  32.9 0.7 slice_bitcast_fusion.10
  33.5 1.6 %collective-permute-start.8 = (bf16[2,25,64,128]{3,2,1,0:T(8,128)(2,1)}, bf16[2,25,64,128]{3,2,1,0:T(8,128)(2,1)}, u32[]{:S(2)}, u32[]{:S(2)}) collective-permute-start(bf16[2,25,64,128]{3,2,1,0:T(8,128)(2,1)} %pad_maximum_fusion.1), channel_id=1, source_target_pairs={{0,2},{1,3},{2,0},{3,1},{4,6},{5,7},{6,4},{7,5},{24,26},{25,27},{2... | collective-permute-start | bytes 2457608 | tf_op jit(solution)/shard_map/ppermute | solution.py:193
  35.1 17.1 %copy.12.values_ref = bf16[192,4,64,64]{3,2,1,0:T(8,128)(2,1)} copy(bf16[192,4,64,64]{0,3,2,1:T(8,128)(2,1)} %param.9) | data formatting | bytes 12582912 | tf_op jit(solution)/shard_map/optimization_barrier | solution.py:232
  52.2 7.1 %collective-permute-start.15 = (bf16[25,64,128]{2,1,0:T(8,128)(2,1)S(1)}, bf16[25,64,128]{2,1,0:T(8,128)(2,1)S(1)}, u32[]{:S(2)}, u32[]{:S(2)}) collective-permute-start(bf16[25,64,128]{2,1,0:T(8,128)(2,1)S(1)} %collective-permute-done.14.rest_7_), channel_id=1, source_target_pairs={{4,8},{8,12},{12,16},{16,20},{20,24},{24,28},{5,9},{9,13},{13,17},... | collective-permute-start | bytes 1228808 | tf_op jit(solution)/shard_map/ppermute | solution.py:174
  59.4 1.9 %collective-permute-start.21 = (bf16[25,64,128]{2,1,0:T(8,128)(2,1)}, bf16[25,64,128]{2,1,0:T(8,128)(2,1)S(1)}, u32[]{:S(2)}, u32[]{:S(2)}) collective-permute-start(bf16[25,64,128]{2,1,0:T(8,128)(2,1)} %collective-permute-done.18.rest_15_), channel_id=1, source_target_pairs={{4,0},{8,4},{12,8},{16,12},{20,16},{24,20},{5,1},{9,5},{13,9},{17,... | collective-permute-start | bytes 1228808 | tf_op jit(solution)/shard_map/ppermute | solution.py:174
  61.3 0.7 collective-permute-start.4
  62.1 2.2 %collective-permute-done.15.rest_3_ = bf16[25,64,128]{2,1,0:T(8,128)(2,1)S(1)} collective-permute-done((bf16[25,64,128]{2,1,0:T(8,128)(2,1)S(1)}, bf16[25,64,128]{2,1,0:T(8,128)(2,1)S(1)}, u32[]{:S(2)}, u32[]{:S(2)}) %collective-permute-start.15) | collective-permute-done | bytes 409632 | tf_op jit(solution)/shard_map/ppermute | solution.py:174
  64.2 1.9 %collective-permute-start.17 = (bf16[25,64,128]{2,1,0:T(8,128)(2,1)}, bf16[25,64,128]{2,1,0:T(8,128)(2,1)S(1)}, u32[]{:S(2)}, u32[]{:S(2)}) collective-permute-start(bf16[25,64,128]{2,1,0:T(8,128)(2,1)} %collective-permute-done.9.rest_10_), channel_id=1, source_target_pairs={{4,0},{8,4},{12,8},{16,12},{20,16},{24,20},{28,24},{5,1},{9,5},{13... | collective-permute-start | bytes 1228808 | tf_op jit(solution)/shard_map/ppermute | solution.py:174
  66.2 2.7 %collective-permute-done.21.rest_19_ = bf16[25,64,128]{2,1,0:T(8,128)(2,1)S(1)} collective-permute-done((bf16[25,64,128]{2,1,0:T(8,128)(2,1)}, bf16[25,64,128]{2,1,0:T(8,128)(2,1)S(1)}, u32[]{:S(2)}, u32[]{:S(2)}) %collective-permute-start.21) | collective-permute-done | bytes 409632 | tf_op jit(solution)/shard_map/ppermute | solution.py:174
  68.9 1.9 %collective-permute-start.16 = (bf16[25,64,128]{2,1,0:T(8,128)(2,1)}, bf16[25,64,128]{2,1,0:T(8,128)(2,1)S(1)}, u32[]{:S(2)}, u32[]{:S(2)}) collective-permute-start(bf16[25,64,128]{2,1,0:T(8,128)(2,1)} %collective-permute-done.5.rest_9_), channel_id=1, source_target_pairs={{4,0},{8,4},{12,8},{16,12},{20,16},{24,20},{28,24},{5,1},{9,5},{13... | collective-permute-start | bytes 1228808 | tf_op jit(solution)/shard_map/ppermute | solution.py:174
  70.8 3.6 %collective-permute-start.6 = (bf16[25,64,128]{2,1,0:T(8,128)(2,1)}, bf16[25,64,128]{2,1,0:T(8,128)(2,1)S(1)}, u32[]{:S(2)}, u32[]{:S(2)}) collective-permute-start(bf16[25,64,128]{2,1,0:T(8,128)(2,1)} %collective-permute-done.5.rest_9_), channel_id=1, source_target_pairs={{0,4},{4,8},{8,12},{12,16},{16,20},{20,24},{24,28},{1,5},{5,9},{9,... | collective-permute-start | bytes 1228808 | tf_op jit(solution)/shard_map/ppermute | solution.py:174
  74.5 0.7 broadcast_select_fusion.3
  75.2 1.9 %collective-permute-start.11 = (bf16[25,64,128]{2,1,0:T(8,128)(2,1)}, bf16[25,64,128]{2,1,0:T(8,128)(2,1)S(1)}, u32[]{:S(2)}, u32[]{:S(2)}) collective-permute-start(bf16[25,64,128]{2,1,0:T(8,128)(2,1)} %collective-permute-done.10.rest_6_), channel_id=1, source_target_pairs={{4,8},{8,12},{12,16},{16,20},{20,24},{24,28},{5,9},{9,13},{13,17},... | collective-permute-start | bytes 1228808 | tf_op jit(solution)/shard_map/ppermute | solution.py:174
  77.1 2.0 %collective-permute-done.16.rest_13_ = bf16[25,64,128]{2,1,0:T(8,128)(2,1)S(1)} collective-permute-done((bf16[25,64,128]{2,1,0:T(8,128)(2,1)}, bf16[25,64,128]{2,1,0:T(8,128)(2,1)S(1)}, u32[]{:S(2)}, u32[]{:S(2)}) %collective-permute-start.16) | collective-permute-done | bytes 409632 | tf_op jit(solution)/shard_map/ppermute | solution.py:174
  79.1 1.9 %collective-permute-start.20 = (bf16[25,64,128]{2,1,0:T(8,128)(2,1)S(1)}, bf16[25,64,128]{2,1,0:T(8,128)(2,1)S(1)}, u32[]{:S(2)}, u32[]{:S(2)}) collective-permute-start(bf16[25,64,128]{2,1,0:T(8,128)(2,1)S(1)} %collective-permute-done.17.rest_14_), channel_id=1, source_target_pairs={{4,0},{8,4},{12,8},{16,12},{20,16},{24,20},{5,1},{9,5},{13,9},{17,... | collective-permute-start | bytes 1228808 | tf_op jit(solution)/shard_map/ppermute | solution.py:174
  81.1 1.9 %collective-permute-start.19 = (bf16[25,64,128]{2,1,0:T(8,128)(2,1)S(1)}, bf16[25,64,128]{2,1,0:T(8,128)(2,1)S(1)}, u32[]{:S(2)}, u32[]{:S(2)}) collective-permute-start(bf16[25,64,128]{2,1,0:T(8,128)(2,1)S(1)} %collective-permute-done.16.rest_13_), channel_id=1, source_target_pairs={{4,0},{8,4},{12,8},{16,12},{20,16},{24,20},{5,1},{9,5},{13,9},{17,... | collective-permute-start | bytes 1228808 | tf_op jit(solution)/shard_map/ppermute | solution.py:174
  83.0 3.7 %collective-permute-start.7 = (bf16[25,64,128]{2,1,0:T(8,128)(2,1)S(1)}, bf16[25,64,128]{2,1,0:T(8,128)(2,1)S(1)}, u32[]{:S(2)}, u32[]{:S(2)}) collective-permute-start(bf16[25,64,128]{2,1,0:T(8,128)(2,1)S(1)} %collective-permute-done.6.rest_5_), channel_id=1, source_target_pairs={{4,8},{8,12},{12,16},{16,20},{20,24},{24,28},{5,9},{9,13},{13,17},... | collective-permute-start | bytes 1228808 | tf_op jit(solution)/shard_map/ppermute | solution.py:174
  86.7 0.7 broadcast_select_fusion.16
  87.4 0.0 copy-start.6
  87.4 1.3 collective-permute-done.20.rest_18_
  88.7 0.6 broadcast_select_fusion.4
  89.3 3.5 %collective-permute-done.19.rest_17_ = bf16[25,64,128]{2,1,0:T(8,128)(2,1)S(1)} collective-permute-done((bf16[25,64,128]{2,1,0:T(8,128)(2,1)S(1)}, bf16[25,64,128]{2,1,0:T(8,128)(2,1)S(1)}, u32[]{:S(2)}, u32[]{:S(2)}) %collective-permute-start.19) | collective-permute-done | bytes 409632 | tf_op jit(solution)/shard_map/ppermute | solution.py:174
  92.8 0.7 copy-done.15
  93.6 0.1 copy-done.16
  93.7 0.1 stack.54
  93.8 0.7 reshape.492.aggs_ref
  94.5 21.3 %shard_map.55 = f32[64,64,128]{2,1,0:T(8,128)} custom-call(s32[768]{0:T(1024)} %fusion.11.pair_ref, s32[768]{0:T(1024)} %get-tuple-element.47.half_ref, s32[768]{0:T(1024)} %get-tuple-element.31.agg_at_ref, s32[192]{0:T(256)} %get-tuple-element.53.own_agg_at_ref, s32[960]{0:T(1024)} %reshape.492.aggs_ref, s32[1]{0:T(128)} %bitcast.37.base_ref, ...), custom_call_target="tpu_custom_call" | custom-call | tf_op jit(solution)/shard_map/pallas_call | solution.py:112
  115.8 1.6 %bitcast_convert_fusion.2 = (bf16[8,2,64,128]{3,2,1,0:T(8,128)(2,1)S(1)}, bf16[8,2,64,128]{3,2,1,0:T(8,128)(2,1)S(1)}, bf16[8,2,64,128]{3,2,1,0:T(8,128)(2,1)S(1)}) fusion(f32[4,8,2,64,128]{4,3,2,1,0:T(8,128)} %bitcast.141, s32[]{:T(128)S(6)} %select_n.510, pred[]{:T(512)S(6)} %and.92, s32[]{:T(128)S(6)} %select_n.514, pred[]{:T(512)S(6)} %and.94, ...), kind=kLoop, calls=%fused_computation.7 | loop fusion | flops 393216 | bytes 1572879 | tf_op jit(solution)/shard_map/convert_element_type | solution.py:254
  117.3 1.3 collective-permute-start.22
  118.6 0.2 collective-permute-start.23
  118.8 1.3 collective-permute-start.24
  120.1 5.6 %collective-permute-done.22 = bf16[8,2,64,128]{3,2,1,0:T(8,128)(2,1)S(1)} collective-permute-done((bf16[8,2,64,128]{3,2,1,0:T(8,128)(2,1)S(1)}, bf16[8,2,64,128]{3,2,1,0:T(8,128)(2,1)S(1)}, u32[]{:S(2)}, u32[]{:S(2)}) %collective-permute-start.22) | collective-permute-done | bytes 262176 | tf_op jit(solution)/shard_map/ppermute | solution.py:253
  125.7 5.1 %collective-permute-done.23 = bf16[8,2,64,128]{3,2,1,0:T(8,128)(2,1)S(1)} collective-permute-done((bf16[8,2,64,128]{3,2,1,0:T(8,128)(2,1)S(1)}, bf16[8,2,64,128]{3,2,1,0:T(8,128)(2,1)S(1)}, u32[]{:S(2)}, u32[]{:S(2)}) %collective-permute-start.23) | collective-permute-done | bytes 262176 | tf_op jit(solution)/shard_map/ppermute | solution.py:253
  130.9 1.2 fusion.2
  132.1 0.2 fusion.34
  132.3 1.1 pad_maximum_fusion
  (68 shorter events, 0.3 us)
Async XLA Ops:
  0.0 8.6 %copy-start.17 = (s32[192,4]{0,1:T(4,128)S(1)}, s32[192,4]{0,1:T(4,128)}, u32[]{:S(2)}) copy-start(s32[192,4]{0,1:T(4,128)} %param.10) | copy-start | bytes 9220
  0.7 9.2 %copy-start.18 = (s32[192]{0:T(256)S(1)}, s32[192]{0:T(256)}, u32[]{:S(2)}) copy-start(s32[192]{0:T(256)} %param.11) | copy-start | bytes 2308
  3.0 28.4 %copy-start.4 = (bf16[25,64,128]{2,1,0:T(8,128)(2,1)}, bf16[25,64,128]{2,1,0:T(8,128)(2,1)S(1)}, u32[]{:S(2)}) copy-start(bf16[25,64,128]{2,1,0:T(8,128)(2,1)S(1)} %fusion.3.rest_8_) | copy-start | bytes 1228804
  3.0 9.5 %collective-permute-start = (bf16[25,64,128]{2,1,0:T(8,128)(2,1)S(1)}, bf16[25,64,128]{2,1,0:T(8,128)(2,1)S(1)}, u32[]{:S(2)}, u32[]{:S(2)}) collective-permute-start(bf16[25,64,128]{2,1,0:T(8,128)(2,1)S(1)} %fusion.3.rest_8_), channel_id=1, source_target_pairs={{28,0},{0,4},{4,8},{8,12},{12,16},{16,20},{20,24},{24,28},{29,1},{... | collective-permute-start | bytes 1228808 | tf_op jit(solution)/shard_map/ppermute | solution.py:174
  4.9 11.8 %collective-permute-start.2 = (bf16[25,64,128]{2,1,0:T(8,128)(2,1)S(1)}, bf16[25,64,128]{2,1,0:T(8,128)(2,1)S(1)}, u32[]{:S(2)}, u32[]{:S(2)}) collective-permute-start(bf16[25,64,128]{2,1,0:T(8,128)(2,1)S(1)} %fusion.3.rest_8_), channel_id=1, source_target_pairs={{4,0},{8,4},{12,8},{16,12},{20,16},{24,20},{28,24},{0,28},{5,1},{9... | collective-permute-start | bytes 1228808 | tf_op jit(solution)/shard_map/ppermute | solution.py:174
  5.0 11.8 %collective-permute-start.13 = (bf16[25,64,128]{2,1,0:T(8,128)(2,1)S(1)}, bf16[25,64,128]{2,1,0:T(8,128)(2,1)}, u32[]{:S(2)}, u32[]{:S(2)}) collective-permute-start(bf16[25,64,128]{2,1,0:T(8,128)(2,1)S(1)} %fusion.3.rest_8_), channel_id=1, source_target_pairs={{0,3},{1,0},{2,1},{3,2},{4,7},{5,4},{6,5},{7,6},{8,11},{9,8},{10,9... | collective-permute-start | bytes 1228808 | tf_op jit(solution)/shard_map/ppermute | solution.py:162
  5.2 19.6 %collective-permute-start.9 = (bf16[25,64,128]{2,1,0:T(8,128)(2,1)S(1)}, bf16[25,64,128]{2,1,0:T(8,128)(2,1)}, u32[]{:S(2)}, u32[]{:S(2)}) collective-permute-start(bf16[25,64,128]{2,1,0:T(8,128)(2,1)S(1)} %fusion.3.rest_8_), channel_id=1, source_target_pairs={{0,2},{1,3},{2,0},{3,1},{4,6},{5,7},{6,4},{7,5},{8,10},{9,11},{10,... | collective-permute-start | bytes 1228808 | tf_op jit(solution)/shard_map/ppermute | solution.py:162
  6.4 26.4 %collective-permute-start.5 = (bf16[25,64,128]{2,1,0:T(8,128)(2,1)S(1)}, bf16[25,64,128]{2,1,0:T(8,128)(2,1)}, u32[]{:S(2)}, u32[]{:S(2)}) collective-permute-start(bf16[25,64,128]{2,1,0:T(8,128)(2,1)S(1)} %fusion.3.rest_8_), channel_id=1, source_target_pairs={{0,1},{1,2},{2,3},{3,0},{4,5},{5,6},{6,7},{7,4},{8,9},{9,10},{10,1... | collective-permute-start | bytes 1228808 | tf_op jit(solution)/shard_map/ppermute | solution.py:162
  12.6 39.7 %copy-start = (bf16[25,64,128]{2,1,0:T(8,128)(2,1)}, bf16[25,64,128]{2,1,0:T(8,128)(2,1)S(1)}, u32[]{:S(2)}) copy-start(bf16[25,64,128]{2,1,0:T(8,128)(2,1)S(1)} %collective-permute-done.rest_4_) | copy-start | bytes 1228804
  12.6 15.3 %collective-permute-start.1 = (bf16[25,64,128]{2,1,0:T(8,128)(2,1)S(1)}, bf16[25,64,128]{2,1,0:T(8,128)(2,1)S(1)}, u32[]{:S(2)}, u32[]{:S(2)}) collective-permute-start(bf16[25,64,128]{2,1,0:T(8,128)(2,1)S(1)} %collective-permute-done.rest_4_), channel_id=1, source_target_pairs={{28,0},{0,4},{4,8},{8,12},{12,16},{16,20},{20,24},{24,28},{29,1},{... | collective-permute-start | bytes 1228808 | tf_op jit(solution)/shard_map/ppermute | solution.py:174
  16.7 35.5 %copy-start.1 = (bf16[25,64,128]{2,1,0:T(8,128)(2,1)}, bf16[25,64,128]{2,1,0:T(8,128)(2,1)S(1)}, u32[]{:S(2)}) copy-start(bf16[25,64,128]{2,1,0:T(8,128)(2,1)S(1)} %collective-permute-done.2.rest_12_) | copy-start | bytes 1228804
  16.7 13.7 %collective-permute-start.3 = (bf16[25,64,128]{2,1,0:T(8,128)(2,1)S(1)}, bf16[25,64,128]{2,1,0:T(8,128)(2,1)S(1)}, u32[]{:S(2)}, u32[]{:S(2)}) collective-permute-start(bf16[25,64,128]{2,1,0:T(8,128)(2,1)S(1)} %collective-permute-done.2.rest_12_), channel_id=1, source_target_pairs={{4,0},{8,4},{12,8},{16,12},{20,16},{24,20},{28,24},{0,28},{5,1},{9... | collective-permute-start | bytes 1228808 | tf_op jit(solution)/shard_map/ppermute | solution.py:174
  16.8 18.3 %collective-permute-start.14 = (bf16[25,64,128]{2,1,0:T(8,128)(2,1)}, bf16[25,64,128]{2,1,0:T(8,128)(2,1)S(1)}, u32[]{:S(2)}, u32[]{:S(2)}) collective-permute-start(bf16[25,64,128]{2,1,0:T(8,128)(2,1)} %collective-permute-done.13.rest_11_), channel_id=1, source_target_pairs={{0,4},{4,8},{8,12},{12,16},{16,20},{20,24},{24,28},{1,5},{5,9},{9,... | collective-permute-start | bytes 1228808 | tf_op jit(solution)/shard_map/ppermute | solution.py:174
  24.8 34.5 %collective-permute-start.18 = (bf16[25,64,128]{2,1,0:T(8,128)(2,1)}, bf16[25,64,128]{2,1,0:T(8,128)(2,1)}, u32[]{:S(2)}, u32[]{:S(2)}) collective-permute-start(bf16[25,64,128]{2,1,0:T(8,128)(2,1)} %collective-permute-done.13.rest_11_), channel_id=1, source_target_pairs={{4,0},{8,4},{12,8},{16,12},{20,16},{24,20},{28,24},{5,1},{9,5},{13... | collective-permute-start | bytes 1228808 | tf_op jit(solution)/shard_map/ppermute | solution.py:174
  27.9 33.4 %copy-start.2 = (bf16[25,64,128]{2,1,0:T(8,128)(2,1)}, bf16[25,64,128]{2,1,0:T(8,128)(2,1)S(1)}, u32[]{:S(2)}) copy-start(bf16[25,64,128]{2,1,0:T(8,128)(2,1)S(1)} %collective-permute-done.1.rest_0_) | copy-start | bytes 1228804
  27.9 33.4 %collective-permute-start.10 = (bf16[25,64,128]{2,1,0:T(8,128)(2,1)}, bf16[25,64,128]{2,1,0:T(8,128)(2,1)}, u32[]{:S(2)}, u32[]{:S(2)}) collective-permute-start(bf16[25,64,128]{2,1,0:T(8,128)(2,1)} %collective-permute-done.9.rest_10_), channel_id=1, source_target_pairs={{0,4},{4,8},{8,12},{12,16},{16,20},{20,24},{24,28},{1,5},{5,9},{9,... | collective-permute-start | bytes 1228808 | tf_op jit(solution)/shard_map/ppermute | solution.py:174
  30.4 31.6 %copy-start.3 = (bf16[25,64,128]{2,1,0:T(8,128)(2,1)}, bf16[25,64,128]{2,1,0:T(8,128)(2,1)S(1)}, u32[]{:S(2)}) copy-start(bf16[25,64,128]{2,1,0:T(8,128)(2,1)S(1)} %collective-permute-done.3.rest_16_) | copy-start | bytes 1228804
  31.5 39.3 %collective-permute-start.12 = (bf16[2,25,64,128]{3,2,1,0:T(8,128)(2,1)}, bf16[2,25,64,128]{3,2,1,0:T(8,128)(2,1)S(1)}, u32[]{:S(2)}, u32[]{:S(2)}) collective-permute-start(bf16[2,25,64,128]{3,2,1,0:T(8,128)(2,1)} %pad_maximum_fusion.1), channel_id=1, source_target_pairs={{0,3},{1,0},{2,1},{3,2},{4,7},{5,4},{6,5},{7,6},{24,27},{25,24},{2... | collective-permute-start | bytes 2457608 | tf_op jit(solution)/shard_map/ppermute | solution.py:193
  33.5 49.5 %collective-permute-start.8 = (bf16[2,25,64,128]{3,2,1,0:T(8,128)(2,1)}, bf16[2,25,64,128]{3,2,1,0:T(8,128)(2,1)}, u32[]{:S(2)}, u32[]{:S(2)}) collective-permute-start(bf16[2,25,64,128]{3,2,1,0:T(8,128)(2,1)} %pad_maximum_fusion.1), channel_id=1, source_target_pairs={{0,2},{1,3},{2,0},{3,1},{4,6},{5,7},{6,4},{7,5},{24,26},{25,27},{2... | collective-permute-start | bytes 2457608 | tf_op jit(solution)/shard_map/ppermute | solution.py:193
  35.1 39.3 %copy-start.7 = (bf16[25,64,128]{2,1,0:T(8,128)(2,1)}, bf16[25,64,128]{2,1,0:T(8,128)(2,1)S(1)}, u32[]{:S(2)}) copy-start(bf16[25,64,128]{2,1,0:T(8,128)(2,1)S(1)} %collective-permute-done.14.rest_7_) | copy-start | bytes 1228804
  52.2 12.0 %collective-permute-start.15 = (bf16[25,64,128]{2,1,0:T(8,128)(2,1)S(1)}, bf16[25,64,128]{2,1,0:T(8,128)(2,1)S(1)}, u32[]{:S(2)}, u32[]{:S(2)}) collective-permute-start(bf16[25,64,128]{2,1,0:T(8,128)(2,1)S(1)} %collective-permute-done.14.rest_7_), channel_id=1, source_target_pairs={{4,8},{8,12},{12,16},{16,20},{20,24},{24,28},{5,9},{9,13},{13,17},... | collective-permute-start | bytes 1228808 | tf_op jit(solution)/shard_map/ppermute | solution.py:174
  59.4 9.5 %collective-permute-start.21 = (bf16[25,64,128]{2,1,0:T(8,128)(2,1)}, bf16[25,64,128]{2,1,0:T(8,128)(2,1)S(1)}, u32[]{:S(2)}, u32[]{:S(2)}) collective-permute-start(bf16[25,64,128]{2,1,0:T(8,128)(2,1)} %collective-permute-done.18.rest_15_), channel_id=1, source_target_pairs={{4,0},{8,4},{12,8},{16,12},{20,16},{24,20},{5,1},{9,5},{13,9},{17,... | collective-permute-start | bytes 1228808 | tf_op jit(solution)/shard_map/ppermute | solution.py:174
  61.3 26.0 %collective-permute-start.4 = (bf16[2,25,64,128]{3,2,1,0:T(8,128)(2,1)}, bf16[2,25,64,128]{3,2,1,0:T(8,128)(2,1)S(1)}, u32[]{:S(2)}, u32[]{:S(2)}) collective-permute-start(bf16[2,25,64,128]{3,2,1,0:T(8,128)(2,1)} %pad_maximum_fusion.1), channel_id=1, source_target_pairs={{0,1},{1,2},{2,3},{3,0},{4,5},{5,6},{6,7},{7,4},{24,25},{25,26},{2... | collective-permute-start | bytes 2457608 | tf_op jit(solution)/shard_map/ppermute | solution.py:193
  64.2 30.2 %copy-start.8 = (bf16[25,64,128]{2,1,0:T(8,128)(2,1)}, bf16[25,64,128]{2,1,0:T(8,128)(2,1)S(1)}, u32[]{:S(2)}) copy-start(bf16[25,64,128]{2,1,0:T(8,128)(2,1)S(1)} %collective-permute-done.15.rest_3_) | copy-start | bytes 1228804
  64.2 10.9 %collective-permute-start.17 = (bf16[25,64,128]{2,1,0:T(8,128)(2,1)}, bf16[25,64,128]{2,1,0:T(8,128)(2,1)S(1)}, u32[]{:S(2)}, u32[]{:S(2)}) collective-permute-start(bf16[25,64,128]{2,1,0:T(8,128)(2,1)} %collective-permute-done.9.rest_10_), channel_id=1, source_target_pairs={{4,0},{8,4},{12,8},{16,12},{20,16},{24,20},{28,24},{5,1},{9,5},{13... | collective-permute-start | bytes 1228808 | tf_op jit(solution)/shard_map/ppermute | solution.py:174
  68.9 18.5 %copy-start.9 = (bf16[25,64,128]{2,1,0:T(8,128)(2,1)}, bf16[25,64,128]{2,1,0:T(8,128)(2,1)S(1)}, u32[]{:S(2)}) copy-start(bf16[25,64,128]{2,1,0:T(8,128)(2,1)S(1)} %collective-permute-done.21.rest_19_) | copy-start | bytes 1228804
  68.9 10.3 %collective-permute-start.16 = (bf16[25,64,128]{2,1,0:T(8,128)(2,1)}, bf16[25,64,128]{2,1,0:T(8,128)(2,1)S(1)}, u32[]{:S(2)}, u32[]{:S(2)}) collective-permute-start(bf16[25,64,128]{2,1,0:T(8,128)(2,1)} %collective-permute-done.5.rest_9_), channel_id=1, source_target_pairs={{4,0},{8,4},{12,8},{16,12},{20,16},{24,20},{28,24},{5,1},{9,5},{13... | collective-permute-start | bytes 1228808 | tf_op jit(solution)/shard_map/ppermute | solution.py:174
  70.8 23.7 %copy-start.5 = (bf16[2,25,64,128]{3,2,1,0:T(8,128)(2,1)}, bf16[2,25,64,128]{3,2,1,0:T(8,128)(2,1)S(1)}, u32[]{:S(2)}) copy-start(bf16[2,25,64,128]{3,2,1,0:T(8,128)(2,1)S(1)} %collective-permute-done.12.rest_22_) | copy-start | bytes 2457604
  70.8 10.3 %collective-permute-start.6 = (bf16[25,64,128]{2,1,0:T(8,128)(2,1)}, bf16[25,64,128]{2,1,0:T(8,128)(2,1)S(1)}, u32[]{:S(2)}, u32[]{:S(2)}) collective-permute-start(bf16[25,64,128]{2,1,0:T(8,128)(2,1)} %collective-permute-done.5.rest_9_), channel_id=1, source_target_pairs={{0,4},{4,8},{8,12},{12,16},{16,20},{20,24},{24,28},{1,5},{5,9},{9,... | collective-permute-start | bytes 1228808 | tf_op jit(solution)/shard_map/ppermute | solution.py:174
  75.2 19.3 %copy-start.10 = (bf16[25,64,128]{2,1,0:T(8,128)(2,1)}, bf16[25,64,128]{2,1,0:T(8,128)(2,1)S(1)}, u32[]{:S(2)}) copy-start(bf16[25,64,128]{2,1,0:T(8,128)(2,1)S(1)} %collective-permute-done.17.rest_14_) | copy-start | bytes 1228804
  75.2 12.2 %collective-permute-start.11 = (bf16[25,64,128]{2,1,0:T(8,128)(2,1)}, bf16[25,64,128]{2,1,0:T(8,128)(2,1)S(1)}, u32[]{:S(2)}, u32[]{:S(2)}) collective-permute-start(bf16[25,64,128]{2,1,0:T(8,128)(2,1)} %collective-permute-done.10.rest_6_), channel_id=1, source_target_pairs={{4,8},{8,12},{12,16},{16,20},{20,24},{24,28},{5,9},{9,13},{13,17},... | collective-permute-start | bytes 1228808 | tf_op jit(solution)/shard_map/ppermute | solution.py:174
  79.1 15.3 %copy-start.11 = (bf16[25,64,128]{2,1,0:T(8,128)(2,1)}, bf16[25,64,128]{2,1,0:T(8,128)(2,1)S(1)}, u32[]{:S(2)}) copy-start(bf16[25,64,128]{2,1,0:T(8,128)(2,1)S(1)} %collective-permute-done.16.rest_13_) | copy-start | bytes 1228804
  79.1 9.6 %collective-permute-start.20 = (bf16[25,64,128]{2,1,0:T(8,128)(2,1)S(1)}, bf16[25,64,128]{2,1,0:T(8,128)(2,1)S(1)}, u32[]{:S(2)}, u32[]{:S(2)}) collective-permute-start(bf16[25,64,128]{2,1,0:T(8,128)(2,1)S(1)} %collective-permute-done.17.rest_14_), channel_id=1, source_target_pairs={{4,0},{8,4},{12,8},{16,12},{20,16},{24,20},{5,1},{9,5},{13,9},{17,... | collective-permute-start | bytes 1228808 | tf_op jit(solution)/shard_map/ppermute | solution.py:174
  81.1 11.7 %copy-start.12 = (bf16[25,64,128]{2,1,0:T(8,128)(2,1)}, bf16[25,64,128]{2,1,0:T(8,128)(2,1)S(1)}, u32[]{:S(2)}) copy-start(bf16[25,64,128]{2,1,0:T(8,128)(2,1)S(1)} %collective-permute-done.6.rest_5_) | copy-start | bytes 1228804
  81.1 11.7 %collective-permute-start.19 = (bf16[25,64,128]{2,1,0:T(8,128)(2,1)S(1)}, bf16[25,64,128]{2,1,0:T(8,128)(2,1)S(1)}, u32[]{:S(2)}, u32[]{:S(2)}) collective-permute-start(bf16[25,64,128]{2,1,0:T(8,128)(2,1)S(1)} %collective-permute-done.16.rest_13_), channel_id=1, source_target_pairs={{4,0},{8,4},{12,8},{16,12},{20,16},{24,20},{5,1},{9,5},{13,9},{17,... | collective-permute-start | bytes 1228808 | tf_op jit(solution)/shard_map/ppermute | solution.py:174
  83.0 9.8 %collective-permute-start.7 = (bf16[25,64,128]{2,1,0:T(8,128)(2,1)S(1)}, bf16[25,64,128]{2,1,0:T(8,128)(2,1)S(1)}, u32[]{:S(2)}, u32[]{:S(2)}) collective-permute-start(bf16[25,64,128]{2,1,0:T(8,128)(2,1)S(1)} %collective-permute-done.6.rest_5_), channel_id=1, source_target_pairs={{4,8},{8,12},{12,16},{16,20},{20,24},{24,28},{5,9},{9,13},{13,17},... | collective-permute-start | bytes 1228808 | tf_op jit(solution)/shard_map/ppermute | solution.py:174
  87.4 7.1 %copy-start.6 = (bf16[2,25,64,128]{3,2,1,0:T(8,128)(2,1)}, bf16[2,25,64,128]{3,2,1,0:T(8,128)(2,1)S(1)}, u32[]{:S(2)}) copy-start(bf16[2,25,64,128]{3,2,1,0:T(8,128)(2,1)S(1)} %collective-permute-done.4.rest_20_) | copy-start | bytes 2457604
  87.4 7.0 %copy-start.13 = (bf16[25,64,128]{2,1,0:T(8,128)(2,1)}, bf16[25,64,128]{2,1,0:T(8,128)(2,1)S(1)}, u32[]{:S(2)}) copy-start(bf16[25,64,128]{2,1,0:T(8,128)(2,1)S(1)} %collective-permute-done.11.rest_2_) | copy-start | bytes 1228804
  88.7 4.1 %copy-start.14 = (bf16[25,64,128]{2,1,0:T(8,128)(2,1)}, bf16[25,64,128]{2,1,0:T(8,128)(2,1)S(1)}, u32[]{:S(2)}) copy-start(bf16[25,64,128]{2,1,0:T(8,128)(2,1)S(1)} %collective-permute-done.20.rest_18_) | copy-start | bytes 1228804
  92.8 0.8 copy-start.15
  92.8 0.9 copy-start.16
  117.3 8.4 %collective-permute-start.22 = (bf16[8,2,64,128]{3,2,1,0:T(8,128)(2,1)S(1)}, bf16[8,2,64,128]{3,2,1,0:T(8,128)(2,1)S(1)}, u32[]{:S(2)}, u32[]{:S(2)}) collective-permute-start(bf16[8,2,64,128]{3,2,1,0:T(8,128)(2,1)S(1)} %get-tuple-element.33), channel_id=1, source_target_pairs={{0,1},{1,2},{2,3},{3,0},{4,5},{5,6},{6,7},{7,4},{8,9},{9,10},{10,1... | collective-permute-start | bytes 786440 | tf_op jit(solution)/shard_map/ppermute | solution.py:253
  118.6 12.3 %collective-permute-start.23 = (bf16[8,2,64,128]{3,2,1,0:T(8,128)(2,1)S(1)}, bf16[8,2,64,128]{3,2,1,0:T(8,128)(2,1)S(1)}, u32[]{:S(2)}, u32[]{:S(2)}) collective-permute-start(bf16[8,2,64,128]{3,2,1,0:T(8,128)(2,1)S(1)} %get-tuple-element.35), channel_id=1, source_target_pairs={{0,2},{1,3},{2,0},{3,1},{4,6},{5,7},{6,4},{7,5},{8,10},{9,11},{10,... | collective-permute-start | bytes 786440 | tf_op jit(solution)/shard_map/ppermute | solution.py:253
  118.8 12.0 %collective-permute-start.24 = (bf16[8,2,64,128]{3,2,1,0:T(8,128)(2,1)S(1)}, bf16[8,2,64,128]{3,2,1,0:T(8,128)(2,1)S(1)}, u32[]{:S(2)}, u32[]{:S(2)}) collective-permute-start(bf16[8,2,64,128]{3,2,1,0:T(8,128)(2,1)S(1)} %get-tuple-element.34), channel_id=1, source_target_pairs={{0,3},{1,0},{2,1},{3,2},{4,7},{5,4},{6,5},{7,6},{8,11},{9,8},{10,9... | collective-permute-start | bytes 786440 | tf_op jit(solution)/shard_map/ppermute | solution.py:253

commit v20 on v19

--- a/solution.py
+++ b/solution.py
@@ -8,7 +8,7 @@
 from jax.sharding import PartitionSpec as P
 
 CB = 4
-ROWS_PER_STEP = 48
+ROWS_PER_STEP = 64
 
 
 def passed_along(block, axis, distance):

time: 135 us -> 135 us (level)
  no operation moved by 1% of the time
where the time goes in v20:
time: 135 us; the launch traced here: 134 us
  starting transfers between devices  52 us (39%)
  local copies, waits for them, and re-layouts  25.4 us (19%)
  waiting for transfers between devices  24.6 us (18%)
  Pallas kernels  21.5 us (16%)
  other arithmetic  9.52 us (7%)
    ppermute x16, starting transfers between devices, ring(): return lax.ppermute(piece, 'blk', route)  42.7 us
    pallas_call x1, Pallas kernels, coarse_partial(): pl.pallas_call(coarse_kernel, out_shape=jax.ShapeDtypeStruct((n_targets /...  21.5 us
    optimization_barrier x1, local copies, waits for them, and re-layouts, local(): block_values, _ = lax.optimization_barrier((block_values, down1[-1]))  17.1 us
    ppermute x16, waiting for transfers between devices, ring(): return lax.ppermute(piece, 'blk', route)  11.6 us
    ppermute x3, waiting for transfers between devices, local(): lax.ppermute(outgoing.astype(jnp.bfloat16), 'grp', [(i, (i + k) % group_s...  10.8 us
    ppermute x3, starting transfers between devices, local(): lax.ppermute(local_ext, 'grp', [(i, (i + k) % group_size) for i in range(...  3.6 us
    ppermute x3, starting transfers between devices, local(): fixed.append(lax.ppermute(fix_src, ('blk', 'grp'), route))  2.97 us
    ppermute x3, starting transfers between devices, local(): lax.ppermute(outgoing.astype(jnp.bfloat16), 'grp', [(i, (i + k) % group_s...  2.76 us
  transfers between devices with their start and end apart: 25, of which 8 were waited for; matrix products, arithmetic and copies ran while one was open for 20% of the time, Pallas kernels for 0%

profile of v20, /device:TPU:19, one launch (start us, length us, event | category | flops | bytes accessed | tf_op | source)
XLA Modules:
  0.0 133.6 jit_solution(18143249733063417732)
XLA Ops:
  0.0 0.7 convert_bitcast_fusion
  0.7 2.0 %copy.14 = bf16[24,2,64,64]{3,1,2,0:T(2,128)(2,1)S(1)} copy(bf16[24,2,64,64]{3,2,1,0:T(8,128)(2,1)} %bitcast.144) | data formatting | bytes 786432 | tf_op jit(solution)/shard_map/reshape | solution.py:148
  2.6 0.3 reshape.425
  3.0 1.9 %collective-permute-start = (bf16[25,64,128]{2,1,0:T(8,128)(2,1)S(1)}, bf16[25,64,128]{2,1,0:T(8,128)(2,1)S(1)}, u32[]{:S(2)}, u32[]{:S(2)}) collective-permute-start(bf16[25,64,128]{2,1,0:T(8,128)(2,1)S(1)} %fusion.3.rest_8_), channel_id=1, source_target_pairs={{28,0},{0,4},{4,8},{8,12},{12,16},{16,20},{20,24},{24,28},{29,1},{... | collective-permute-start | bytes 1228808 | tf_op jit(solution)/shard_map/ppermute | solution.py:174
  5.0 0.3 collective-permute-start.13
  5.2 1.2 collective-permute-start.9
  6.4 2.1 %collective-permute-start.5 = (bf16[25,64,128]{2,1,0:T(8,128)(2,1)S(1)}, bf16[25,64,128]{2,1,0:T(8,128)(2,1)}, u32[]{:S(2)}, u32[]{:S(2)}) collective-permute-start(bf16[25,64,128]{2,1,0:T(8,128)(2,1)S(1)} %fusion.3.rest_8_), channel_id=1, source_target_pairs={{0,1},{1,2},{2,3},{3,0},{4,5},{5,6},{6,7},{7,4},{8,9},{9,10},{10,1... | collective-permute-start | bytes 1228808 | tf_op jit(solution)/shard_map/ppermute | solution.py:162
  8.6 0.6 fusion.20
  9.1 0.1 copy.9
  9.3 0.1 rem.165
  9.4 0.1 copy.10
  9.5 0.1 div.36
  9.6 0.2 copy.8
  9.8 0.1 ne.114
  9.9 0.1 compare_convert_fusion
  10.0 0.7 reshape.493.live_ref
  10.7 0.6 stack.59.fix_ref
  11.4 0.6 multiply_add_fusion
  12.0 0.6 fusion.11.pair_ref
  12.6 4.1 %collective-permute-start.1 = (bf16[25,64,128]{2,1,0:T(8,128)(2,1)S(1)}, bf16[25,64,128]{2,1,0:T(8,128)(2,1)S(1)}, u32[]{:S(2)}, u32[]{:S(2)}) collective-permute-start(bf16[25,64,128]{2,1,0:T(8,128)(2,1)S(1)} %collective-permute-done.rest_4_), channel_id=1, source_target_pairs={{28,0},{0,4},{4,8},{8,12},{12,16},{16,20},{20,24},{24,28},{29,1},{... | collective-permute-start | bytes 1228808 | tf_op jit(solution)/shard_map/ppermute | solution.py:174
  16.8 5.2 %collective-permute-start.14 = (bf16[25,64,128]{2,1,0:T(8,128)(2,1)}, bf16[25,64,128]{2,1,0:T(8,128)(2,1)S(1)}, u32[]{:S(2)}, u32[]{:S(2)}) collective-permute-start(bf16[25,64,128]{2,1,0:T(8,128)(2,1)} %collective-permute-done.13.rest_11_), channel_id=1, source_target_pairs={{0,4},{4,8},{8,12},{12,16},{16,20},{20,24},{24,28},{1,5},{5,9},{9,... | collective-permute-start | bytes 1228808 | tf_op jit(solution)/shard_map/ppermute | solution.py:174
  21.9 0.7 slice_bitcast_fusion.8
  22.7 2.2 %collective-permute-done.9.rest_10_ = bf16[25,64,128]{2,1,0:T(8,128)(2,1)} collective-permute-done((bf16[25,64,128]{2,1,0:T(8,128)(2,1)S(1)}, bf16[25,64,128]{2,1,0:T(8,128)(2,1)}, u32[]{:S(2)}, u32[]{:S(2)}) %collective-permute-start.9) | collective-permute-done | bytes 409632 | tf_op jit(solution)/shard_map/ppermute | solution.py:162
  24.8 3.0 %collective-permute-start.18 = (bf16[25,64,128]{2,1,0:T(8,128)(2,1)}, bf16[25,64,128]{2,1,0:T(8,128)(2,1)}, u32[]{:S(2)}, u32[]{:S(2)}) collective-permute-start(bf16[25,64,128]{2,1,0:T(8,128)(2,1)} %collective-permute-done.13.rest_11_), channel_id=1, source_target_pairs={{4,0},{8,4},{12,8},{16,12},{20,16},{24,20},{28,24},{5,1},{9,5},{13... | collective-permute-start | bytes 1228808 | tf_op jit(solution)/shard_map/ppermute | solution.py:174
  27.9 2.5 %collective-permute-start.10 = (bf16[25,64,128]{2,1,0:T(8,128)(2,1)}, bf16[25,64,128]{2,1,0:T(8,128)(2,1)}, u32[]{:S(2)}, u32[]{:S(2)}) collective-permute-start(bf16[25,64,128]{2,1,0:T(8,128)(2,1)} %collective-permute-done.9.rest_10_), channel_id=1, source_target_pairs={{0,4},{4,8},{8,12},{12,16},{16,20},{20,24},{24,28},{1,5},{5,9},{9,... | collective-permute-start | bytes 1228808 | tf_op jit(solution)/shard_map/ppermute | solution.py:174
  30.5 1.0 pad_maximum_fusion.1
  31.5 0.7 collective-permute-start.12
  32.2 0.7 slice_bitcast_fusion.9
  32.9 0.7 slice_bitcast_fusion.10
  33.5 1.6 %collective-permute-start.8 = (bf16[2,25,64,128]{3,2,1,0:T(8,128)(2,1)}, bf16[2,25,64,128]{3,2,1,0:T(8,128)(2,1)}, u32[]{:S(2)}, u32[]{:S(2)}) collective-permute-start(bf16[2,25,64,128]{3,2,1,0:T(8,128)(2,1)} %pad_maximum_fusion.1), channel_id=1, source_target_pairs={{0,2},{1,3},{2,0},{3,1},{4,6},{5,7},{6,4},{7,5},{24,26},{25,27},{2... | collective-permute-start | bytes 2457608 | tf_op jit(solution)/shard_map/ppermute | solution.py:193
  35.1 17.1 %copy.12.values_ref = bf16[192,4,64,64]{3,2,1,0:T(8,128)(2,1)} copy(bf16[192,4,64,64]{0,3,2,1:T(8,128)(2,1)} %param.9) | data formatting | bytes 12582912 | tf_op jit(solution)/shard_map/optimization_barrier | solution.py:232
  52.2 7.1 %collective-permute-start.15 = (bf16[25,64,128]{2,1,0:T(8,128)(2,1)S(1)}, bf16[25,64,128]{2,1,0:T(8,128)(2,1)S(1)}, u32[]{:S(2)}, u32[]{:S(2)}) collective-permute-start(bf16[25,64,128]{2,1,0:T(8,128)(2,1)S(1)} %collective-permute-done.14.rest_7_), channel_id=1, source_target_pairs={{4,8},{8,12},{12,16},{16,20},{20,24},{24,28},{5,9},{9,13},{13,17},... | collective-permute-start | bytes 1228808 | tf_op jit(solution)/shard_map/ppermute | solution.py:174
  59.4 1.9 %collective-permute-start.21 = (bf16[25,64,128]{2,1,0:T(8,128)(2,1)}, bf16[25,64,128]{2,1,0:T(8,128)(2,1)S(1)}, u32[]{:S(2)}, u32[]{:S(2)}) collective-permute-start(bf16[25,64,128]{2,1,0:T(8,128)(2,1)} %collective-permute-done.18.rest_15_), channel_id=1, source_target_pairs={{4,0},{8,4},{12,8},{16,12},{20,16},{24,20},{5,1},{9,5},{13,9},{17,... | collective-permute-start | bytes 1228808 | tf_op jit(solution)/shard_map/ppermute | solution.py:174
  61.3 0.7 collective-permute-start.4
  62.1 2.2 %collective-permute-done.15.rest_3_ = bf16[25,64,128]{2,1,0:T(8,128)(2,1)S(1)} collective-permute-done((bf16[25,64,128]{2,1,0:T(8,128)(2,1)S(1)}, bf16[25,64,128]{2,1,0:T(8,128)(2,1)S(1)}, u32[]{:S(2)}, u32[]{:S(2)}) %collective-permute-start.15) | collective-permute-done | bytes 409632 | tf_op jit(solution)/shard_map/ppermute | solution.py:174
  64.2 1.9 %collective-permute-start.17 = (bf16[25,64,128]{2,1,0:T(8,128)(2,1)}, bf16[25,64,128]{2,1,0:T(8,128)(2,1)S(1)}, u32[]{:S(2)}, u32[]{:S(2)}) collective-permute-start(bf16[25,64,128]{2,1,0:T(8,128)(2,1)} %collective-permute-done.9.rest_10_), channel_id=1, source_target_pairs={{4,0},{8,4},{12,8},{16,12},{20,16},{24,20},{28,24},{5,1},{9,5},{13... | collective-permute-start | bytes 1228808 | tf_op jit(solution)/shard_map/ppermute | solution.py:174
  66.2 2.7 %collective-permute-done.21.rest_19_ = bf16[25,64,128]{2,1,0:T(8,128)(2,1)S(1)} collective-permute-done((bf16[25,64,128]{2,1,0:T(8,128)(2,1)}, bf16[25,64,128]{2,1,0:T(8,128)(2,1)S(1)}, u32[]{:S(2)}, u32[]{:S(2)}) %collective-permute-start.21) | collective-permute-done | bytes 409632 | tf_op jit(solution)/shard_map/ppermute | solution.py:174
  68.9 1.9 %collective-permute-start.16 = (bf16[25,64,128]{2,1,0:T(8,128)(2,1)}, bf16[25,64,128]{2,1,0:T(8,128)(2,1)S(1)}, u32[]{:S(2)}, u32[]{:S(2)}) collective-permute-start(bf16[25,64,128]{2,1,0:T(8,128)(2,1)} %collective-permute-done.5.rest_9_), channel_id=1, source_target_pairs={{4,0},{8,4},{12,8},{16,12},{20,16},{24,20},{28,24},{5,1},{9,5},{13... | collective-permute-start | bytes 1228808 | tf_op jit(solution)/shard_map/ppermute | solution.py:174
  70.8 3.6 %collective-permute-start.6 = (bf16[25,64,128]{2,1,0:T(8,128)(2,1)}, bf16[25,64,128]{2,1,0:T(8,128)(2,1)S(1)}, u32[]{:S(2)}, u32[]{:S(2)}) collective-permute-start(bf16[25,64,128]{2,1,0:T(8,128)(2,1)} %collective-permute-done.5.rest_9_), channel_id=1, source_target_pairs={{0,4},{4,8},{8,12},{12,16},{16,20},{20,24},{24,28},{1,5},{5,9},{9,... | collective-permute-start | bytes 1228808 | tf_op jit(solution)/shard_map/ppermute | solution.py:174
  74.5 0.7 broadcast_select_fusion.3
  75.2 1.9 %collective-permute-start.11 = (bf16[25,64,128]{2,1,0:T(8,128)(2,1)}, bf16[25,64,128]{2,1,0:T(8,128)(2,1)S(1)}, u32[]{:S(2)}, u32[]{:S(2)}) collective-permute-start(bf16[25,64,128]{2,1,0:T(8,128)(2,1)} %collective-permute-done.10.rest_6_), channel_id=1, source_target_pairs={{4,8},{8,12},{12,16},{16,20},{20,24},{24,28},{5,9},{9,13},{13,17},... | collective-permute-start | bytes 1228808 | tf_op jit(solution)/shard_map/ppermute | solution.py:174
  77.1 2.0 %collective-permute-done.16.rest_13_ = bf16[25,64,128]{2,1,0:T(8,128)(2,1)S(1)} collective-permute-done((bf16[25,64,128]{2,1,0:T(8,128)(2,1)}, bf16[25,64,128]{2,1,0:T(8,128)(2,1)S(1)}, u32[]{:S(2)}, u32[]{:S(2)}) %collective-permute-start.16) | collective-permute-done | bytes 409632 | tf_op jit(solution)/shard_map/ppermute | solution.py:174
  79.1 1.9 %collective-permute-start.20 = (bf16[25,64,128]{2,1,0:T(8,128)(2,1)S(1)}, bf16[25,64,128]{2,1,0:T(8,128)(2,1)S(1)}, u32[]{:S(2)}, u32[]{:S(2)}) collective-permute-start(bf16[25,64,128]{2,1,0:T(8,128)(2,1)S(1)} %collective-permute-done.17.rest_14_), channel_id=1, source_target_pairs={{4,0},{8,4},{12,8},{16,12},{20,16},{24,20},{5,1},{9,5},{13,9},{17,... | collective-permute-start | bytes 1228808 | tf_op jit(solution)/shard_map/ppermute | solution.py:174
  81.1 1.9 %collective-permute-start.19 = (bf16[25,64,128]{2,1,0:T(8,128)(2,1)S(1)}, bf16[25,64,128]{2,1,0:T(8,128)(2,1)S(1)}, u32[]{:S(2)}, u32[]{:S(2)}) collective-permute-start(bf16[25,64,128]{2,1,0:T(8,128)(2,1)S(1)} %collective-permute-done.16.rest_13_), channel_id=1, source_target_pairs={{4,0},{8,4},{12,8},{16,12},{20,16},{24,20},{5,1},{9,5},{13,9},{17,... | collective-permute-start | bytes 1228808 | tf_op jit(solution)/shard_map/ppermute | solution.py:174
  83.0 3.7 %collective-permute-start.7 = (bf16[25,64,128]{2,1,0:T(8,128)(2,1)S(1)}, bf16[25,64,128]{2,1,0:T(8,128)(2,1)S(1)}, u32[]{:S(2)}, u32[]{:S(2)}) collective-permute-start(bf16[25,64,128]{2,1,0:T(8,128)(2,1)S(1)} %collective-permute-done.6.rest_5_), channel_id=1, source_target_pairs={{4,8},{8,12},{12,16},{16,20},{20,24},{24,28},{5,9},{9,13},{13,17},... | collective-permute-start | bytes 1228808 | tf_op jit(solution)/shard_map/ppermute | solution.py:174
  86.7 0.7 broadcast_select_fusion.16
  87.4 0.0 copy-start.6
  87.4 1.3 collective-permute-done.20.rest_18_
  88.7 0.6 broadcast_select_fusion.4
  89.3 3.5 %collective-permute-done.19.rest_17_ = bf16[25,64,128]{2,1,0:T(8,128)(2,1)S(1)} collective-permute-done((bf16[25,64,128]{2,1,0:T(8,128)(2,1)S(1)}, bf16[25,64,128]{2,1,0:T(8,128)(2,1)S(1)}, u32[]{:S(2)}, u32[]{:S(2)}) %collective-permute-start.19) | collective-permute-done | bytes 409632 | tf_op jit(solution)/shard_map/ppermute | solution.py:174
  92.8 0.7 copy-done.15
  93.6 0.1 copy-done.16
  93.7 0.1 stack.54
  93.8 0.7 reshape.492.aggs_ref
  94.5 21.5 %shard_map.55 = f32[64,64,128]{2,1,0:T(8,128)} custom-call(s32[768]{0:T(1024)} %fusion.11.pair_ref, s32[768]{0:T(1024)} %get-tuple-element.47.half_ref, s32[768]{0:T(1024)} %get-tuple-element.31.agg_at_ref, s32[192]{0:T(256)} %get-tuple-element.53.own_agg_at_ref, s32[960]{0:T(1024)} %reshape.492.aggs_ref, s32[1]{0:T(128)} %bitcast.37.base_ref, ...), custom_call_target="tpu_custom_call" | custom-call | tf_op jit(solution)/shard_map/pallas_call | solution.py:112
  116.0 1.6 %bitcast_convert_fusion.2 = (bf16[8,2,64,128]{3,2,1,0:T(8,128)(2,1)S(1)}, bf16[8,2,64,128]{3,2,1,0:T(8,128)(2,1)S(1)}, bf16[8,2,64,128]{3,2,1,0:T(8,128)(2,1)S(1)}) fusion(f32[4,8,2,64,128]{4,3,2,1,0:T(8,128)} %bitcast.141, s32[]{:T(128)S(6)} %select_n.510, pred[]{:T(512)S(6)} %and.92, s32[]{:T(128)S(6)} %select_n.514, pred[]{:T(512)S(6)} %and.94, ...), kind=kLoop, calls=%fused_computation.7 | loop fusion | flops 393216 | bytes 1572879 | tf_op jit(solution)/shard_map/convert_element_type | solution.py:254
  117.6 1.3 collective-permute-start.22
  118.9 0.2 collective-permute-start.23
  119.1 1.3 collective-permute-start.24
  120.4 5.6 %collective-permute-done.22 = bf16[8,2,64,128]{3,2,1,0:T(8,128)(2,1)S(1)} collective-permute-done((bf16[8,2,64,128]{3,2,1,0:T(8,128)(2,1)S(1)}, bf16[8,2,64,128]{3,2,1,0:T(8,128)(2,1)S(1)}, u32[]{:S(2)}, u32[]{:S(2)}) %collective-permute-start.22) | collective-permute-done | bytes 262176 | tf_op jit(solution)/shard_map/ppermute | solution.py:253
  126.0 5.1 %collective-permute-done.23 = bf16[8,2,64,128]{3,2,1,0:T(8,128)(2,1)S(1)} collective-permute-done((bf16[8,2,64,128]{3,2,1,0:T(8,128)(2,1)S(1)}, bf16[8,2,64,128]{3,2,1,0:T(8,128)(2,1)S(1)}, u32[]{:S(2)}, u32[]{:S(2)}) %collective-permute-start.23) | collective-permute-done | bytes 262176 | tf_op jit(solution)/shard_map/ppermute | solution.py:253
  131.1 1.2 fusion.2
  132.3 0.2 fusion.34
  132.5 1.1 pad_maximum_fusion
  (68 shorter events, 0.3 us)
Async XLA Ops:
  0.0 8.6 %copy-start.17 = (s32[192,4]{0,1:T(4,128)S(1)}, s32[192,4]{0,1:T(4,128)}, u32[]{:S(2)}) copy-start(s32[192,4]{0,1:T(4,128)} %param.10) | copy-start | bytes 9220
  0.7 9.2 %copy-start.18 = (s32[192]{0:T(256)S(1)}, s32[192]{0:T(256)}, u32[]{:S(2)}) copy-start(s32[192]{0:T(256)} %param.11) | copy-start | bytes 2308
  3.0 28.4 %copy-start.4 = (bf16[25,64,128]{2,1,0:T(8,128)(2,1)}, bf16[25,64,128]{2,1,0:T(8,128)(2,1)S(1)}, u32[]{:S(2)}) copy-start(bf16[25,64,128]{2,1,0:T(8,128)(2,1)S(1)} %fusion.3.rest_8_) | copy-start | bytes 1228804
  3.0 9.5 %collective-permute-start = (bf16[25,64,128]{2,1,0:T(8,128)(2,1)S(1)}, bf16[25,64,128]{2,1,0:T(8,128)(2,1)S(1)}, u32[]{:S(2)}, u32[]{:S(2)}) collective-permute-start(bf16[25,64,128]{2,1,0:T(8,128)(2,1)S(1)} %fusion.3.rest_8_), channel_id=1, source_target_pairs={{28,0},{0,4},{4,8},{8,12},{12,16},{16,20},{20,24},{24,28},{29,1},{... | collective-permute-start | bytes 1228808 | tf_op jit(solution)/shard_map/ppermute | solution.py:174
  4.9 11.8 %collective-permute-start.2 = (bf16[25,64,128]{2,1,0:T(8,128)(2,1)S(1)}, bf16[25,64,128]{2,1,0:T(8,128)(2,1)S(1)}, u32[]{:S(2)}, u32[]{:S(2)}) collective-permute-start(bf16[25,64,128]{2,1,0:T(8,128)(2,1)S(1)} %fusion.3.rest_8_), channel_id=1, source_target_pairs={{4,0},{8,4},{12,8},{16,12},{20,16},{24,20},{28,24},{0,28},{5,1},{9... | collective-permute-start | bytes 1228808 | tf_op jit(solution)/shard_map/ppermute | solution.py:174
  5.0 11.8 %collective-permute-start.13 = (bf16[25,64,128]{2,1,0:T(8,128)(2,1)S(1)}, bf16[25,64,128]{2,1,0:T(8,128)(2,1)}, u32[]{:S(2)}, u32[]{:S(2)}) collective-permute-start(bf16[25,64,128]{2,1,0:T(8,128)(2,1)S(1)} %fusion.3.rest_8_), channel_id=1, source_target_pairs={{0,3},{1,0},{2,1},{3,2},{4,7},{5,4},{6,5},{7,6},{8,11},{9,8},{10,9... | collective-permute-start | bytes 1228808 | tf_op jit(solution)/shard_map/ppermute | solution.py:162
  5.2 19.6 %collective-permute-start.9 = (bf16[25,64,128]{2,1,0:T(8,128)(2,1)S(1)}, bf16[25,64,128]{2,1,0:T(8,128)(2,1)}, u32[]{:S(2)}, u32[]{:S(2)}) collective-permute-start(bf16[25,64,128]{2,1,0:T(8,128)(2,1)S(1)} %fusion.3.rest_8_), channel_id=1, source_target_pairs={{0,2},{1,3},{2,0},{3,1},{4,6},{5,7},{6,4},{7,5},{8,10},{9,11},{10,... | collective-permute-start | bytes 1228808 | tf_op jit(solution)/shard_map/ppermute | solution.py:162
  6.4 26.4 %collective-permute-start.5 = (bf16[25,64,128]{2,1,0:T(8,128)(2,1)S(1)}, bf16[25,64,128]{2,1,0:T(8,128)(2,1)}, u32[]{:S(2)}, u32[]{:S(2)}) collective-permute-start(bf16[25,64,128]{2,1,0:T(8,128)(2,1)S(1)} %fusion.3.rest_8_), channel_id=1, source_target_pairs={{0,1},{1,2},{2,3},{3,0},{4,5},{5,6},{6,7},{7,4},{8,9},{9,10},{10,1... | collective-permute-start | bytes 1228808 | tf_op jit(solution)/shard_map/ppermute | solution.py:162
  12.6 39.7 %copy-start = (bf16[25,64,128]{2,1,0:T(8,128)(2,1)}, bf16[25,64,128]{2,1,0:T(8,128)(2,1)S(1)}, u32[]{:S(2)}) copy-start(bf16[25,64,128]{2,1,0:T(8,128)(2,1)S(1)} %collective-permute-done.rest_4_) | copy-start | bytes 1228804
  12.6 15.3 %collective-permute-start.1 = (bf16[25,64,128]{2,1,0:T(8,128)(2,1)S(1)}, bf16[25,64,128]{2,1,0:T(8,128)(2,1)S(1)}, u32[]{:S(2)}, u32[]{:S(2)}) collective-permute-start(bf16[25,64,128]{2,1,0:T(8,128)(2,1)S(1)} %collective-permute-done.rest_4_), channel_id=1, source_target_pairs={{28,0},{0,4},{4,8},{8,12},{12,16},{16,20},{20,24},{24,28},{29,1},{... | collective-permute-start | bytes 1228808 | tf_op jit(solution)/shard_map/ppermute | solution.py:174
  16.7 35.5 %copy-start.1 = (bf16[25,64,128]{2,1,0:T(8,128)(2,1)}, bf16[25,64,128]{2,1,0:T(8,128)(2,1)S(1)}, u32[]{:S(2)}) copy-start(bf16[25,64,128]{2,1,0:T(8,128)(2,1)S(1)} %collective-permute-done.2.rest_12_) | copy-start | bytes 1228804
  16.7 13.7 %collective-permute-start.3 = (bf16[25,64,128]{2,1,0:T(8,128)(2,1)S(1)}, bf16[25,64,128]{2,1,0:T(8,128)(2,1)S(1)}, u32[]{:S(2)}, u32[]{:S(2)}) collective-permute-start(bf16[25,64,128]{2,1,0:T(8,128)(2,1)S(1)} %collective-permute-done.2.rest_12_), channel_id=1, source_target_pairs={{4,0},{8,4},{12,8},{16,12},{20,16},{24,20},{28,24},{0,28},{5,1},{9... | collective-permute-start | bytes 1228808 | tf_op jit(solution)/shard_map/ppermute | solution.py:174
  16.8 18.3 %collective-permute-start.14 = (bf16[25,64,128]{2,1,0:T(8,128)(2,1)}, bf16[25,64,128]{2,1,0:T(8,128)(2,1)S(1)}, u32[]{:S(2)}, u32[]{:S(2)}) collective-permute-start(bf16[25,64,128]{2,1,0:T(8,128)(2,1)} %collective-permute-done.13.rest_11_), channel_id=1, source_target_pairs={{0,4},{4,8},{8,12},{12,16},{16,20},{20,24},{24,28},{1,5},{5,9},{9,... | collective-permute-start | bytes 1228808 | tf_op jit(solution)/shard_map/ppermute | solution.py:174
  24.8 34.5 %collective-permute-start.18 = (bf16[25,64,128]{2,1,0:T(8,128)(2,1)}, bf16[25,64,128]{2,1,0:T(8,128)(2,1)}, u32[]{:S(2)}, u32[]{:S(2)}) collective-permute-start(bf16[25,64,128]{2,1,0:T(8,128)(2,1)} %collective-permute-done.13.rest_11_), channel_id=1, source_target_pairs={{4,0},{8,4},{12,8},{16,12},{20,16},{24,20},{28,24},{5,1},{9,5},{13... | collective-permute-start | bytes 1228808 | tf_op jit(solution)/shard_map/ppermute | solution.py:174
  27.9 33.4 %copy-start.2 = (bf16[25,64,128]{2,1,0:T(8,128)(2,1)}, bf16[25,64,128]{2,1,0:T(8,128)(2,1)S(1)}, u32[]{:S(2)}) copy-start(bf16[25,64,128]{2,1,0:T(8,128)(2,1)S(1)} %collective-permute-done.1.rest_0_) | copy-start | bytes 1228804
  27.9 33.4 %collective-permute-start.10 = (bf16[25,64,128]{2,1,0:T(8,128)(2,1)}, bf16[25,64,128]{2,1,0:T(8,128)(2,1)}, u32[]{:S(2)}, u32[]{:S(2)}) collective-permute-start(bf16[25,64,128]{2,1,0:T(8,128)(2,1)} %collective-permute-done.9.rest_10_), channel_id=1, source_target_pairs={{0,4},{4,8},{8,12},{12,16},{16,20},{20,24},{24,28},{1,5},{5,9},{9,... | collective-permute-start | bytes 1228808 | tf_op jit(solution)/shard_map/ppermute | solution.py:174
  30.4 31.6 %copy-start.3 = (bf16[25,64,128]{2,1,0:T(8,128)(2,1)}, bf16[25,64,128]{2,1,0:T(8,128)(2,1)S(1)}, u32[]{:S(2)}) copy-start(bf16[25,64,128]{2,1,0:T(8,128)(2,1)S(1)} %collective-permute-done.3.rest_16_) | copy-start | bytes 1228804
  31.5 39.3 %collective-permute-start.12 = (bf16[2,25,64,128]{3,2,1,0:T(8,128)(2,1)}, bf16[2,25,64,128]{3,2,1,0:T(8,128)(2,1)S(1)}, u32[]{:S(2)}, u32[]{:S(2)}) collective-permute-start(bf16[2,25,64,128]{3,2,1,0:T(8,128)(2,1)} %pad_maximum_fusion.1), channel_id=1, source_target_pairs={{0,3},{1,0},{2,1},{3,2},{4,7},{5,4},{6,5},{7,6},{24,27},{25,24},{2... | collective-permute-start | bytes 2457608 | tf_op jit(solution)/shard_map/ppermute | solution.py:193
  33.5 49.5 %collective-permute-start.8 = (bf16[2,25,64,128]{3,2,1,0:T(8,128)(2,1)}, bf16[2,25,64,128]{3,2,1,0:T(8,128)(2,1)}, u32[]{:S(2)}, u32[]{:S(2)}) collective-permute-start(bf16[2,25,64,128]{3,2,1,0:T(8,128)(2,1)} %pad_maximum_fusion.1), channel_id=1, source_target_pairs={{0,2},{1,3},{2,0},{3,1},{4,6},{5,7},{6,4},{7,5},{24,26},{25,27},{2... | collective-permute-start | bytes 2457608 | tf_op jit(solution)/shard_map/ppermute | solution.py:193
  35.1 39.3 %copy-start.7 = (bf16[25,64,128]{2,1,0:T(8,128)(2,1)}, bf16[25,64,128]{2,1,0:T(8,128)(2,1)S(1)}, u32[]{:S(2)}) copy-start(bf16[25,64,128]{2,1,0:T(8,128)(2,1)S(1)} %collective-permute-done.14.rest_7_) | copy-start | bytes 1228804
  52.2 12.0 %collective-permute-start.15 = (bf16[25,64,128]{2,1,0:T(8,128)(2,1)S(1)}, bf16[25,64,128]{2,1,0:T(8,128)(2,1)S(1)}, u32[]{:S(2)}, u32[]{:S(2)}) collective-permute-start(bf16[25,64,128]{2,1,0:T(8,128)(2,1)S(1)} %collective-permute-done.14.rest_7_), channel_id=1, source_target_pairs={{4,8},{8,12},{12,16},{16,20},{20,24},{24,28},{5,9},{9,13},{13,17},... | collective-permute-start | bytes 1228808 | tf_op jit(solution)/shard_map/ppermute | solution.py:174
  59.4 9.5 %collective-permute-start.21 = (bf16[25,64,128]{2,1,0:T(8,128)(2,1)}, bf16[25,64,128]{2,1,0:T(8,128)(2,1)S(1)}, u32[]{:S(2)}, u32[]{:S(2)}) collective-permute-start(bf16[25,64,128]{2,1,0:T(8,128)(2,1)} %collective-permute-done.18.rest_15_), channel_id=1, source_target_pairs={{4,0},{8,4},{12,8},{16,12},{20,16},{24,20},{5,1},{9,5},{13,9},{17,... | collective-permute-start | bytes 1228808 | tf_op jit(solution)/shard_map/ppermute | solution.py:174
  61.3 26.0 %collective-permute-start.4 = (bf16[2,25,64,128]{3,2,1,0:T(8,128)(2,1)}, bf16[2,25,64,128]{3,2,1,0:T(8,128)(2,1)S(1)}, u32[]{:S(2)}, u32[]{:S(2)}) collective-permute-start(bf16[2,25,64,128]{3,2,1,0:T(8,128)(2,1)} %pad_maximum_fusion.1), channel_id=1, source_target_pairs={{0,1},{1,2},{2,3},{3,0},{4,5},{5,6},{6,7},{7,4},{24,25},{25,26},{2... | collective-permute-start | bytes 2457608 | tf_op jit(solution)/shard_map/ppermute | solution.py:193
  64.2 30.2 %copy-start.8 = (bf16[25,64,128]{2,1,0:T(8,128)(2,1)}, bf16[25,64,128]{2,1,0:T(8,128)(2,1)S(1)}, u32[]{:S(2)}) copy-start(bf16[25,64,128]{2,1,0:T(8,128)(2,1)S(1)} %collective-permute-done.15.rest_3_) | copy-start | bytes 1228804
  64.2 10.9 %collective-permute-start.17 = (bf16[25,64,128]{2,1,0:T(8,128)(2,1)}, bf16[25,64,128]{2,1,0:T(8,128)(2,1)S(1)}, u32[]{:S(2)}, u32[]{:S(2)}) collective-permute-start(bf16[25,64,128]{2,1,0:T(8,128)(2,1)} %collective-permute-done.9.rest_10_), channel_id=1, source_target_pairs={{4,0},{8,4},{12,8},{16,12},{20,16},{24,20},{28,24},{5,1},{9,5},{13... | collective-permute-start | bytes 1228808 | tf_op jit(solution)/shard_map/ppermute | solution.py:174
  68.9 18.5 %copy-start.9 = (bf16[25,64,128]{2,1,0:T(8,128)(2,1)}, bf16[25,64,128]{2,1,0:T(8,128)(2,1)S(1)}, u32[]{:S(2)}) copy-start(bf16[25,64,128]{2,1,0:T(8,128)(2,1)S(1)} %collective-permute-done.21.rest_19_) | copy-start | bytes 1228804
  68.9 10.3 %collective-permute-start.16 = (bf16[25,64,128]{2,1,0:T(8,128)(2,1)}, bf16[25,64,128]{2,1,0:T(8,128)(2,1)S(1)}, u32[]{:S(2)}, u32[]{:S(2)}) collective-permute-start(bf16[25,64,128]{2,1,0:T(8,128)(2,1)} %collective-permute-done.5.rest_9_), channel_id=1, source_target_pairs={{4,0},{8,4},{12,8},{16,12},{20,16},{24,20},{28,24},{5,1},{9,5},{13... | collective-permute-start | bytes 1228808 | tf_op jit(solution)/shard_map/ppermute | solution.py:174
  70.8 23.7 %copy-start.5 = (bf16[2,25,64,128]{3,2,1,0:T(8,128)(2,1)}, bf16[2,25,64,128]{3,2,1,0:T(8,128)(2,1)S(1)}, u32[]{:S(2)}) copy-start(bf16[2,25,64,128]{3,2,1,0:T(8,128)(2,1)S(1)} %collective-permute-done.12.rest_22_) | copy-start | bytes 2457604
  70.8 10.3 %collective-permute-start.6 = (bf16[25,64,128]{2,1,0:T(8,128)(2,1)}, bf16[25,64,128]{2,1,0:T(8,128)(2,1)S(1)}, u32[]{:S(2)}, u32[]{:S(2)}) collective-permute-start(bf16[25,64,128]{2,1,0:T(8,128)(2,1)} %collective-permute-done.5.rest_9_), channel_id=1, source_target_pairs={{0,4},{4,8},{8,12},{12,16},{16,20},{20,24},{24,28},{1,5},{5,9},{9,... | collective-permute-start | bytes 1228808 | tf_op jit(solution)/shard_map/ppermute | solution.py:174
  75.2 19.3 %copy-start.10 = (bf16[25,64,128]{2,1,0:T(8,128)(2,1)}, bf16[25,64,128]{2,1,0:T(8,128)(2,1)S(1)}, u32[]{:S(2)}) copy-start(bf16[25,64,128]{2,1,0:T(8,128)(2,1)S(1)} %collective-permute-done.17.rest_14_) | copy-start | bytes 1228804
  75.2 12.2 %collective-permute-start.11 = (bf16[25,64,128]{2,1,0:T(8,128)(2,1)}, bf16[25,64,128]{2,1,0:T(8,128)(2,1)S(1)}, u32[]{:S(2)}, u32[]{:S(2)}) collective-permute-start(bf16[25,64,128]{2,1,0:T(8,128)(2,1)} %collective-permute-done.10.rest_6_), channel_id=1, source_target_pairs={{4,8},{8,12},{12,16},{16,20},{20,24},{24,28},{5,9},{9,13},{13,17},... | collective-permute-start | bytes 1228808 | tf_op jit(solution)/shard_map/ppermute | solution.py:174
  79.1 15.3 %copy-start.11 = (bf16[25,64,128]{2,1,0:T(8,128)(2,1)}, bf16[25,64,128]{2,1,0:T(8,128)(2,1)S(1)}, u32[]{:S(2)}) copy-start(bf16[25,64,128]{2,1,0:T(8,128)(2,1)S(1)} %collective-permute-done.16.rest_13_) | copy-start | bytes 1228804
  79.1 9.6 %collective-permute-start.20 = (bf16[25,64,128]{2,1,0:T(8,128)(2,1)S(1)}, bf16[25,64,128]{2,1,0:T(8,128)(2,1)S(1)}, u32[]{:S(2)}, u32[]{:S(2)}) collective-permute-start(bf16[25,64,128]{2,1,0:T(8,128)(2,1)S(1)} %collective-permute-done.17.rest_14_), channel_id=1, source_target_pairs={{4,0},{8,4},{12,8},{16,12},{20,16},{24,20},{5,1},{9,5},{13,9},{17,... | collective-permute-start | bytes 1228808 | tf_op jit(solution)/shard_map/ppermute | solution.py:174
  81.1 11.7 %copy-start.12 = (bf16[25,64,128]{2,1,0:T(8,128)(2,1)}, bf16[25,64,128]{2,1,0:T(8,128)(2,1)S(1)}, u32[]{:S(2)}) copy-start(bf16[25,64,128]{2,1,0:T(8,128)(2,1)S(1)} %collective-permute-done.6.rest_5_) | copy-start | bytes 1228804
  81.1 11.7 %collective-permute-start.19 = (bf16[25,64,128]{2,1,0:T(8,128)(2,1)S(1)}, bf16[25,64,128]{2,1,0:T(8,128)(2,1)S(1)}, u32[]{:S(2)}, u32[]{:S(2)}) collective-permute-start(bf16[25,64,128]{2,1,0:T(8,128)(2,1)S(1)} %collective-permute-done.16.rest_13_), channel_id=1, source_target_pairs={{4,0},{8,4},{12,8},{16,12},{20,16},{24,20},{5,1},{9,5},{13,9},{17,... | collective-permute-start | bytes 1228808 | tf_op jit(solution)/shard_map/ppermute | solution.py:174
  83.0 9.8 %collective-permute-start.7 = (bf16[25,64,128]{2,1,0:T(8,128)(2,1)S(1)}, bf16[25,64,128]{2,1,0:T(8,128)(2,1)S(1)}, u32[]{:S(2)}, u32[]{:S(2)}) collective-permute-start(bf16[25,64,128]{2,1,0:T(8,128)(2,1)S(1)} %collective-permute-done.6.rest_5_), channel_id=1, source_target_pairs={{4,8},{8,12},{12,16},{16,20},{20,24},{24,28},{5,9},{9,13},{13,17},... | collective-permute-start | bytes 1228808 | tf_op jit(solution)/shard_map/ppermute | solution.py:174
  87.4 7.1 %copy-start.6 = (bf16[2,25,64,128]{3,2,1,0:T(8,128)(2,1)}, bf16[2,25,64,128]{3,2,1,0:T(8,128)(2,1)S(1)}, u32[]{:S(2)}) copy-start(bf16[2,25,64,128]{3,2,1,0:T(8,128)(2,1)S(1)} %collective-permute-done.4.rest_20_) | copy-start | bytes 2457604
  87.4 7.0 %copy-start.13 = (bf16[25,64,128]{2,1,0:T(8,128)(2,1)}, bf16[25,64,128]{2,1,0:T(8,128)(2,1)S(1)}, u32[]{:S(2)}) copy-start(bf16[25,64,128]{2,1,0:T(8,128)(2,1)S(1)} %collective-permute-done.11.rest_2_) | copy-start | bytes 1228804
  88.7 4.1 %copy-start.14 = (bf16[25,64,128]{2,1,0:T(8,128)(2,1)}, bf16[25,64,128]{2,1,0:T(8,128)(2,1)S(1)}, u32[]{:S(2)}) copy-start(bf16[25,64,128]{2,1,0:T(8,128)(2,1)S(1)} %collective-permute-done.20.rest_18_) | copy-start | bytes 1228804
  92.8 0.8 copy-start.15
  92.8 0.9 copy-start.16
  117.6 8.4 %collective-permute-start.22 = (bf16[8,2,64,128]{3,2,1,0:T(8,128)(2,1)S(1)}, bf16[8,2,64,128]{3,2,1,0:T(8,128)(2,1)S(1)}, u32[]{:S(2)}, u32[]{:S(2)}) collective-permute-start(bf16[8,2,64,128]{3,2,1,0:T(8,128)(2,1)S(1)} %get-tuple-element.33), channel_id=1, source_target_pairs={{0,1},{1,2},{2,3},{3,0},{4,5},{5,6},{6,7},{7,4},{8,9},{9,10},{10,1... | collective-permute-start | bytes 786440 | tf_op jit(solution)/shard_map/ppermute | solution.py:253
  118.9 12.3 %collective-permute-start.23 = (bf16[8,2,64,128]{3,2,1,0:T(8,128)(2,1)S(1)}, bf16[8,2,64,128]{3,2,1,0:T(8,128)(2,1)S(1)}, u32[]{:S(2)}, u32[]{:S(2)}) collective-permute-start(bf16[8,2,64,128]{3,2,1,0:T(8,128)(2,1)S(1)} %get-tuple-element.35), channel_id=1, source_target_pairs={{0,2},{1,3},{2,0},{3,1},{4,6},{5,7},{6,4},{7,5},{8,10},{9,11},{10,... | collective-permute-start | bytes 786440 | tf_op jit(solution)/shard_map/ppermute | solution.py:253
  119.1 12.0 %collective-permute-start.24 = (bf16[8,2,64,128]{3,2,1,0:T(8,128)(2,1)S(1)}, bf16[8,2,64,128]{3,2,1,0:T(8,128)(2,1)S(1)}, u32[]{:S(2)}, u32[]{:S(2)}) collective-permute-start(bf16[8,2,64,128]{3,2,1,0:T(8,128)(2,1)S(1)} %get-tuple-element.34), channel_id=1, source_target_pairs={{0,3},{1,0},{2,1},{3,2},{4,7},{5,4},{6,5},{7,6},{8,11},{9,8},{10,9... | collective-permute-start | bytes 786440 | tf_op jit(solution)/shard_map/ppermute | solution.py:253

commit v21 on v19

--- a/solution.py
+++ b/solution.py
@@ -75,11 +75,11 @@
         for s in range(slots):
             n = row * slots + s
             pair = window[pair_ref[n]]
-            picked = jnp.where(lane_half == half_ref[n], pair, jnp.zeros_like(pair))
+            keep = (lane_half == half_ref[n]) & (live_ref[n] > 0)
+            picked = jnp.where(keep, pair, jnp.zeros_like(pair))
             product = jnp.dot(
                 values_ref[r, s], picked, preferred_element_type=jnp.float32
-            )
-            product = jnp.where(live_ref[n] > 0, product, 0.0).astype(jnp.bfloat16)
+            ).astype(jnp.bfloat16)
             results.append(
                 jnp.dot(own_t, product, preferred_element_type=jnp.float32)
             )

time: 135 us -> 135 us (level)
  no operation moved by 1% of the time
where the time goes in v21:
time: 135 us; the launch traced here: 133 us
  starting transfers between devices  52 us (39%)
  local copies, waits for them, and re-layouts  25.4 us (19%)
  waiting for transfers between devices  24.6 us (18%)
  Pallas kernels  21.3 us (16%)
  other arithmetic  9.52 us (7%)
    ppermute x16, starting transfers between devices, ring(): return lax.ppermute(piece, 'blk', route)  42.7 us
    pallas_call x1, Pallas kernels, coarse_partial(): pl.pallas_call(coarse_kernel, out_shape=jax.ShapeDtypeStruct((n_targets /...  21.3 us
    optimization_barrier x1, local copies, waits for them, and re-layouts, local(): block_values, _ = lax.optimization_barrier((block_values, down1[-1]))  17.1 us
    ppermute x16, waiting for transfers between devices, ring(): return lax.ppermute(piece, 'blk', route)  11.6 us
    ppermute x3, waiting for transfers between devices, local(): lax.ppermute(outgoing.astype(jnp.bfloat16), 'grp', [(i, (i + k) % group_s...  10.8 us
    ppermute x3, starting transfers between devices, local(): lax.ppermute(local_ext, 'grp', [(i, (i + k) % group_size) for i in range(...  3.6 us
    ppermute x3, starting transfers between devices, local(): fixed.append(lax.ppermute(fix_src, ('blk', 'grp'), route))  2.97 us
    ppermute x3, starting transfers between devices, local(): lax.ppermute(outgoing.astype(jnp.bfloat16), 'grp', [(i, (i + k) % group_s...  2.76 us
  transfers between devices with their start and end apart: 25, of which 8 were waited for; matrix products, arithmetic and copies ran while one was open for 20% of the time, Pallas kernels for 0%

profile of v21, /device:TPU:19, one launch (start us, length us, event | category | flops | bytes accessed | tf_op | source)
XLA Modules:
  0.0 133.3 jit_solution(9963110091041653602)
XLA Ops:
  0.0 0.7 convert_bitcast_fusion
  0.7 2.0 %copy.14 = bf16[24,2,64,64]{3,1,2,0:T(2,128)(2,1)S(1)} copy(bf16[24,2,64,64]{3,2,1,0:T(8,128)(2,1)} %bitcast.144) | data formatting | bytes 786432 | tf_op jit(solution)/shard_map/reshape | solution.py:148
  2.6 0.3 reshape.425
  3.0 1.9 %collective-permute-start = (bf16[25,64,128]{2,1,0:T(8,128)(2,1)S(1)}, bf16[25,64,128]{2,1,0:T(8,128)(2,1)S(1)}, u32[]{:S(2)}, u32[]{:S(2)}) collective-permute-start(bf16[25,64,128]{2,1,0:T(8,128)(2,1)S(1)} %fusion.3.rest_8_), channel_id=1, source_target_pairs={{28,0},{0,4},{4,8},{8,12},{12,16},{16,20},{20,24},{24,28},{29,1},{... | collective-permute-start | bytes 1228808 | tf_op jit(solution)/shard_map/ppermute | solution.py:174
  5.0 0.3 collective-permute-start.13
  5.2 1.2 collective-permute-start.9
  6.4 2.1 %collective-permute-start.5 = (bf16[25,64,128]{2,1,0:T(8,128)(2,1)S(1)}, bf16[25,64,128]{2,1,0:T(8,128)(2,1)}, u32[]{:S(2)}, u32[]{:S(2)}) collective-permute-start(bf16[25,64,128]{2,1,0:T(8,128)(2,1)S(1)} %fusion.3.rest_8_), channel_id=1, source_target_pairs={{0,1},{1,2},{2,3},{3,0},{4,5},{5,6},{6,7},{7,4},{8,9},{9,10},{10,1... | collective-permute-start | bytes 1228808 | tf_op jit(solution)/shard_map/ppermute | solution.py:162
  8.6 0.6 fusion.20
  9.1 0.1 copy.9
  9.3 0.1 rem.165
  9.4 0.1 copy.10
  9.5 0.1 div.36
  9.6 0.2 copy.8
  9.8 0.1 ne.114
  9.9 0.1 compare_convert_fusion
  10.0 0.7 reshape.493.live_ref
  10.7 0.6 stack.59.fix_ref
  11.4 0.6 multiply_add_fusion
  12.0 0.6 fusion.11.pair_ref
  12.6 4.1 %collective-permute-start.1 = (bf16[25,64,128]{2,1,0:T(8,128)(2,1)S(1)}, bf16[25,64,128]{2,1,0:T(8,128)(2,1)S(1)}, u32[]{:S(2)}, u32[]{:S(2)}) collective-permute-start(bf16[25,64,128]{2,1,0:T(8,128)(2,1)S(1)} %collective-permute-done.rest_4_), channel_id=1, source_target_pairs={{28,0},{0,4},{4,8},{8,12},{12,16},{16,20},{20,24},{24,28},{29,1},{... | collective-permute-start | bytes 1228808 | tf_op jit(solution)/shard_map/ppermute | solution.py:174
  16.8 5.2 %collective-permute-start.14 = (bf16[25,64,128]{2,1,0:T(8,128)(2,1)}, bf16[25,64,128]{2,1,0:T(8,128)(2,1)S(1)}, u32[]{:S(2)}, u32[]{:S(2)}) collective-permute-start(bf16[25,64,128]{2,1,0:T(8,128)(2,1)} %collective-permute-done.13.rest_11_), channel_id=1, source_target_pairs={{0,4},{4,8},{8,12},{12,16},{16,20},{20,24},{24,28},{1,5},{5,9},{9,... | collective-permute-start | bytes 1228808 | tf_op jit(solution)/shard_map/ppermute | solution.py:174
  21.9 0.7 slice_bitcast_fusion.8
  22.7 2.2 %collective-permute-done.9.rest_10_ = bf16[25,64,128]{2,1,0:T(8,128)(2,1)} collective-permute-done((bf16[25,64,128]{2,1,0:T(8,128)(2,1)S(1)}, bf16[25,64,128]{2,1,0:T(8,128)(2,1)}, u32[]{:S(2)}, u32[]{:S(2)}) %collective-permute-start.9) | collective-permute-done | bytes 409632 | tf_op jit(solution)/shard_map/ppermute | solution.py:162
  24.8 3.0 %collective-permute-start.18 = (bf16[25,64,128]{2,1,0:T(8,128)(2,1)}, bf16[25,64,128]{2,1,0:T(8,128)(2,1)}, u32[]{:S(2)}, u32[]{:S(2)}) collective-permute-start(bf16[25,64,128]{2,1,0:T(8,128)(2,1)} %collective-permute-done.13.rest_11_), channel_id=1, source_target_pairs={{4,0},{8,4},{12,8},{16,12},{20,16},{24,20},{28,24},{5,1},{9,5},{13... | collective-permute-start | bytes 1228808 | tf_op jit(solution)/shard_map/ppermute | solution.py:174
  27.9 2.5 %collective-permute-start.10 = (bf16[25,64,128]{2,1,0:T(8,128)(2,1)}, bf16[25,64,128]{2,1,0:T(8,128)(2,1)}, u32[]{:S(2)}, u32[]{:S(2)}) collective-permute-start(bf16[25,64,128]{2,1,0:T(8,128)(2,1)} %collective-permute-done.9.rest_10_), channel_id=1, source_target_pairs={{0,4},{4,8},{8,12},{12,16},{16,20},{20,24},{24,28},{1,5},{5,9},{9,... | collective-permute-start | bytes 1228808 | tf_op jit(solution)/shard_map/ppermute | solution.py:174
  30.5 1.0 pad_maximum_fusion.1
  31.5 0.7 collective-permute-start.12
  32.2 0.7 slice_bitcast_fusion.9
  32.9 0.7 slice_bitcast_fusion.10
  33.5 1.6 %collective-permute-start.8 = (bf16[2,25,64,128]{3,2,1,0:T(8,128)(2,1)}, bf16[2,25,64,128]{3,2,1,0:T(8,128)(2,1)}, u32[]{:S(2)}, u32[]{:S(2)}) collective-permute-start(bf16[2,25,64,128]{3,2,1,0:T(8,128)(2,1)} %pad_maximum_fusion.1), channel_id=1, source_target_pairs={{0,2},{1,3},{2,0},{3,1},{4,6},{5,7},{6,4},{7,5},{24,26},{25,27},{2... | collective-permute-start | bytes 2457608 | tf_op jit(solution)/shard_map/ppermute | solution.py:193
  35.1 17.1 %copy.12.values_ref = bf16[192,4,64,64]{3,2,1,0:T(8,128)(2,1)} copy(bf16[192,4,64,64]{0,3,2,1:T(8,128)(2,1)} %param.9) | data formatting | bytes 12582912 | tf_op jit(solution)/shard_map/optimization_barrier | solution.py:232
  52.2 7.1 %collective-permute-start.15 = (bf16[25,64,128]{2,1,0:T(8,128)(2,1)S(1)}, bf16[25,64,128]{2,1,0:T(8,128)(2,1)S(1)}, u32[]{:S(2)}, u32[]{:S(2)}) collective-permute-start(bf16[25,64,128]{2,1,0:T(8,128)(2,1)S(1)} %collective-permute-done.14.rest_7_), channel_id=1, source_target_pairs={{4,8},{8,12},{12,16},{16,20},{20,24},{24,28},{5,9},{9,13},{13,17},... | collective-permute-start | bytes 1228808 | tf_op jit(solution)/shard_map/ppermute | solution.py:174
  59.4 1.9 %collective-permute-start.21 = (bf16[25,64,128]{2,1,0:T(8,128)(2,1)}, bf16[25,64,128]{2,1,0:T(8,128)(2,1)S(1)}, u32[]{:S(2)}, u32[]{:S(2)}) collective-permute-start(bf16[25,64,128]{2,1,0:T(8,128)(2,1)} %collective-permute-done.18.rest_15_), channel_id=1, source_target_pairs={{4,0},{8,4},{12,8},{16,12},{20,16},{24,20},{5,1},{9,5},{13,9},{17,... | collective-permute-start | bytes 1228808 | tf_op jit(solution)/shard_map/ppermute | solution.py:174
  61.3 0.7 collective-permute-start.4
  62.1 2.2 %collective-permute-done.15.rest_3_ = bf16[25,64,128]{2,1,0:T(8,128)(2,1)S(1)} collective-permute-done((bf16[25,64,128]{2,1,0:T(8,128)(2,1)S(1)}, bf16[25,64,128]{2,1,0:T(8,128)(2,1)S(1)}, u32[]{:S(2)}, u32[]{:S(2)}) %collective-permute-start.15) | collective-permute-done | bytes 409632 | tf_op jit(solution)/shard_map/ppermute | solution.py:174
  64.2 1.9 %collective-permute-start.17 = (bf16[25,64,128]{2,1,0:T(8,128)(2,1)}, bf16[25,64,128]{2,1,0:T(8,128)(2,1)S(1)}, u32[]{:S(2)}, u32[]{:S(2)}) collective-permute-start(bf16[25,64,128]{2,1,0:T(8,128)(2,1)} %collective-permute-done.9.rest_10_), channel_id=1, source_target_pairs={{4,0},{8,4},{12,8},{16,12},{20,16},{24,20},{28,24},{5,1},{9,5},{13... | collective-permute-start | bytes 1228808 | tf_op jit(solution)/shard_map/ppermute | solution.py:174
  66.2 2.7 %collective-permute-done.21.rest_19_ = bf16[25,64,128]{2,1,0:T(8,128)(2,1)S(1)} collective-permute-done((bf16[25,64,128]{2,1,0:T(8,128)(2,1)}, bf16[25,64,128]{2,1,0:T(8,128)(2,1)S(1)}, u32[]{:S(2)}, u32[]{:S(2)}) %collective-permute-start.21) | collective-permute-done | bytes 409632 | tf_op jit(solution)/shard_map/ppermute | solution.py:174
  68.9 1.9 %collective-permute-start.16 = (bf16[25,64,128]{2,1,0:T(8,128)(2,1)}, bf16[25,64,128]{2,1,0:T(8,128)(2,1)S(1)}, u32[]{:S(2)}, u32[]{:S(2)}) collective-permute-start(bf16[25,64,128]{2,1,0:T(8,128)(2,1)} %collective-permute-done.5.rest_9_), channel_id=1, source_target_pairs={{4,0},{8,4},{12,8},{16,12},{20,16},{24,20},{28,24},{5,1},{9,5},{13... | collective-permute-start | bytes 1228808 | tf_op jit(solution)/shard_map/ppermute | solution.py:174
  70.8 3.6 %collective-permute-start.6 = (bf16[25,64,128]{2,1,0:T(8,128)(2,1)}, bf16[25,64,128]{2,1,0:T(8,128)(2,1)S(1)}, u32[]{:S(2)}, u32[]{:S(2)}) collective-permute-start(bf16[25,64,128]{2,1,0:T(8,128)(2,1)} %collective-permute-done.5.rest_9_), channel_id=1, source_target_pairs={{0,4},{4,8},{8,12},{12,16},{16,20},{20,24},{24,28},{1,5},{5,9},{9,... | collective-permute-start | bytes 1228808 | tf_op jit(solution)/shard_map/ppermute | solution.py:174
  74.5 0.7 broadcast_select_fusion.3
  75.2 1.9 %collective-permute-start.11 = (bf16[25,64,128]{2,1,0:T(8,128)(2,1)}, bf16[25,64,128]{2,1,0:T(8,128)(2,1)S(1)}, u32[]{:S(2)}, u32[]{:S(2)}) collective-permute-start(bf16[25,64,128]{2,1,0:T(8,128)(2,1)} %collective-permute-done.10.rest_6_), channel_id=1, source_target_pairs={{4,8},{8,12},{12,16},{16,20},{20,24},{24,28},{5,9},{9,13},{13,17},... | collective-permute-start | bytes 1228808 | tf_op jit(solution)/shard_map/ppermute | solution.py:174
  77.1 2.0 %collective-permute-done.16.rest_13_ = bf16[25,64,128]{2,1,0:T(8,128)(2,1)S(1)} collective-permute-done((bf16[25,64,128]{2,1,0:T(8,128)(2,1)}, bf16[25,64,128]{2,1,0:T(8,128)(2,1)S(1)}, u32[]{:S(2)}, u32[]{:S(2)}) %collective-permute-start.16) | collective-permute-done | bytes 409632 | tf_op jit(solution)/shard_map/ppermute | solution.py:174
  79.1 1.9 %collective-permute-start.20 = (bf16[25,64,128]{2,1,0:T(8,128)(2,1)S(1)}, bf16[25,64,128]{2,1,0:T(8,128)(2,1)S(1)}, u32[]{:S(2)}, u32[]{:S(2)}) collective-permute-start(bf16[25,64,128]{2,1,0:T(8,128)(2,1)S(1)} %collective-permute-done.17.rest_14_), channel_id=1, source_target_pairs={{4,0},{8,4},{12,8},{16,12},{20,16},{24,20},{5,1},{9,5},{13,9},{17,... | collective-permute-start | bytes 1228808 | tf_op jit(solution)/shard_map/ppermute | solution.py:174
  81.1 1.9 %collective-permute-start.19 = (bf16[25,64,128]{2,1,0:T(8,128)(2,1)S(1)}, bf16[25,64,128]{2,1,0:T(8,128)(2,1)S(1)}, u32[]{:S(2)}, u32[]{:S(2)}) collective-permute-start(bf16[25,64,128]{2,1,0:T(8,128)(2,1)S(1)} %collective-permute-done.16.rest_13_), channel_id=1, source_target_pairs={{4,0},{8,4},{12,8},{16,12},{20,16},{24,20},{5,1},{9,5},{13,9},{17,... | collective-permute-start | bytes 1228808 | tf_op jit(solution)/shard_map/ppermute | solution.py:174
  83.0 3.7 %collective-permute-start.7 = (bf16[25,64,128]{2,1,0:T(8,128)(2,1)S(1)}, bf16[25,64,128]{2,1,0:T(8,128)(2,1)S(1)}, u32[]{:S(2)}, u32[]{:S(2)}) collective-permute-start(bf16[25,64,128]{2,1,0:T(8,128)(2,1)S(1)} %collective-permute-done.6.rest_5_), channel_id=1, source_target_pairs={{4,8},{8,12},{12,16},{16,20},{20,24},{24,28},{5,9},{9,13},{13,17},... | collective-permute-start | bytes 1228808 | tf_op jit(solution)/shard_map/ppermute | solution.py:174
  86.7 0.7 broadcast_select_fusion.16
  87.4 0.0 copy-start.6
  87.4 1.3 collective-permute-done.20.rest_18_
  88.7 0.6 broadcast_select_fusion.4
  89.3 3.5 %collective-permute-done.19.rest_17_ = bf16[25,64,128]{2,1,0:T(8,128)(2,1)S(1)} collective-permute-done((bf16[25,64,128]{2,1,0:T(8,128)(2,1)S(1)}, bf16[25,64,128]{2,1,0:T(8,128)(2,1)S(1)}, u32[]{:S(2)}, u32[]{:S(2)}) %collective-permute-start.19) | collective-permute-done | bytes 409632 | tf_op jit(solution)/shard_map/ppermute | solution.py:174
  92.8 0.7 copy-done.15
  93.6 0.1 copy-done.16
  93.7 0.1 stack.54
  93.8 0.7 reshape.492.aggs_ref
  94.5 21.3 %shard_map.55 = f32[64,64,128]{2,1,0:T(8,128)} custom-call(s32[768]{0:T(1024)} %fusion.11.pair_ref, s32[768]{0:T(1024)} %get-tuple-element.47.half_ref, s32[768]{0:T(1024)} %get-tuple-element.31.agg_at_ref, s32[192]{0:T(256)} %get-tuple-element.53.own_agg_at_ref, s32[960]{0:T(1024)} %reshape.492.aggs_ref, s32[1]{0:T(128)} %bitcast.37.base_ref, ...), custom_call_target="tpu_custom_call" | custom-call | tf_op jit(solution)/shard_map/pallas_call | solution.py:112
  115.8 1.6 %bitcast_convert_fusion.2 = (bf16[8,2,64,128]{3,2,1,0:T(8,128)(2,1)S(1)}, bf16[8,2,64,128]{3,2,1,0:T(8,128)(2,1)S(1)}, bf16[8,2,64,128]{3,2,1,0:T(8,128)(2,1)S(1)}) fusion(f32[4,8,2,64,128]{4,3,2,1,0:T(8,128)} %bitcast.141, s32[]{:T(128)S(6)} %select_n.510, pred[]{:T(512)S(6)} %and.92, s32[]{:T(128)S(6)} %select_n.514, pred[]{:T(512)S(6)} %and.94, ...), kind=kLoop, calls=%fused_computation.7 | loop fusion | flops 393216 | bytes 1572879 | tf_op jit(solution)/shard_map/convert_element_type | solution.py:254
  117.4 1.3 collective-permute-start.22
  118.6 0.2 collective-permute-start.23
  118.8 1.3 collective-permute-start.24
  120.1 5.6 %collective-permute-done.22 = bf16[8,2,64,128]{3,2,1,0:T(8,128)(2,1)S(1)} collective-permute-done((bf16[8,2,64,128]{3,2,1,0:T(8,128)(2,1)S(1)}, bf16[8,2,64,128]{3,2,1,0:T(8,128)(2,1)S(1)}, u32[]{:S(2)}, u32[]{:S(2)}) %collective-permute-start.22) | collective-permute-done | bytes 262176 | tf_op jit(solution)/shard_map/ppermute | solution.py:253
  125.7 5.1 %collective-permute-done.23 = bf16[8,2,64,128]{3,2,1,0:T(8,128)(2,1)S(1)} collective-permute-done((bf16[8,2,64,128]{3,2,1,0:T(8,128)(2,1)S(1)}, bf16[8,2,64,128]{3,2,1,0:T(8,128)(2,1)S(1)}, u32[]{:S(2)}, u32[]{:S(2)}) %collective-permute-start.23) | collective-permute-done | bytes 262176 | tf_op jit(solution)/shard_map/ppermute | solution.py:253
  130.9 1.2 fusion.2
  132.1 0.2 fusion.34
  132.3 1.1 pad_maximum_fusion
  (68 shorter events, 0.3 us)
Async XLA Ops:
  0.0 8.6 %copy-start.17 = (s32[192,4]{0,1:T(4,128)S(1)}, s32[192,4]{0,1:T(4,128)}, u32[]{:S(2)}) copy-start(s32[192,4]{0,1:T(4,128)} %param.10) | copy-start | bytes 9220
  0.7 9.2 %copy-start.18 = (s32[192]{0:T(256)S(1)}, s32[192]{0:T(256)}, u32[]{:S(2)}) copy-start(s32[192]{0:T(256)} %param.11) | copy-start | bytes 2308
  3.0 28.4 %copy-start.4 = (bf16[25,64,128]{2,1,0:T(8,128)(2,1)}, bf16[25,64,128]{2,1,0:T(8,128)(2,1)S(1)}, u32[]{:S(2)}) copy-start(bf16[25,64,128]{2,1,0:T(8,128)(2,1)S(1)} %fusion.3.rest_8_) | copy-start | bytes 1228804
  3.0 9.5 %collective-permute-start = (bf16[25,64,128]{2,1,0:T(8,128)(2,1)S(1)}, bf16[25,64,128]{2,1,0:T(8,128)(2,1)S(1)}, u32[]{:S(2)}, u32[]{:S(2)}) collective-permute-start(bf16[25,64,128]{2,1,0:T(8,128)(2,1)S(1)} %fusion.3.rest_8_), channel_id=1, source_target_pairs={{28,0},{0,4},{4,8},{8,12},{12,16},{16,20},{20,24},{24,28},{29,1},{... | collective-permute-start | bytes 1228808 | tf_op jit(solution)/shard_map/ppermute | solution.py:174
  4.9 11.8 %collective-permute-start.2 = (bf16[25,64,128]{2,1,0:T(8,128)(2,1)S(1)}, bf16[25,64,128]{2,1,0:T(8,128)(2,1)S(1)}, u32[]{:S(2)}, u32[]{:S(2)}) collective-permute-start(bf16[25,64,128]{2,1,0:T(8,128)(2,1)S(1)} %fusion.3.rest_8_), channel_id=1, source_target_pairs={{4,0},{8,4},{12,8},{16,12},{20,16},{24,20},{28,24},{0,28},{5,1},{9... | collective-permute-start | bytes 1228808 | tf_op jit(solution)/shard_map/ppermute | solution.py:174
  5.0 11.8 %collective-permute-start.13 = (bf16[25,64,128]{2,1,0:T(8,128)(2,1)S(1)}, bf16[25,64,128]{2,1,0:T(8,128)(2,1)}, u32[]{:S(2)}, u32[]{:S(2)}) collective-permute-start(bf16[25,64,128]{2,1,0:T(8,128)(2,1)S(1)} %fusion.3.rest_8_), channel_id=1, source_target_pairs={{0,3},{1,0},{2,1},{3,2},{4,7},{5,4},{6,5},{7,6},{8,11},{9,8},{10,9... | collective-permute-start | bytes 1228808 | tf_op jit(solution)/shard_map/ppermute | solution.py:162
  5.2 19.6 %collective-permute-start.9 = (bf16[25,64,128]{2,1,0:T(8,128)(2,1)S(1)}, bf16[25,64,128]{2,1,0:T(8,128)(2,1)}, u32[]{:S(2)}, u32[]{:S(2)}) collective-permute-start(bf16[25,64,128]{2,1,0:T(8,128)(2,1)S(1)} %fusion.3.rest_8_), channel_id=1, source_target_pairs={{0,2},{1,3},{2,0},{3,1},{4,6},{5,7},{6,4},{7,5},{8,10},{9,11},{10,... | collective-permute-start | bytes 1228808 | tf_op jit(solution)/shard_map/ppermute | solution.py:162
  6.4 26.4 %collective-permute-start.5 = (bf16[25,64,128]{2,1,0:T(8,128)(2,1)S(1)}, bf16[25,64,128]{2,1,0:T(8,128)(2,1)}, u32[]{:S(2)}, u32[]{:S(2)}) collective-permute-start(bf16[25,64,128]{2,1,0:T(8,128)(2,1)S(1)} %fusion.3.rest_8_), channel_id=1, source_target_pairs={{0,1},{1,2},{2,3},{3,0},{4,5},{5,6},{6,7},{7,4},{8,9},{9,10},{10,1... | collective-permute-start | bytes 1228808 | tf_op jit(solution)/shard_map/ppermute | solution.py:162
  12.6 39.7 %copy-start = (bf16[25,64,128]{2,1,0:T(8,128)(2,1)}, bf16[25,64,128]{2,1,0:T(8,128)(2,1)S(1)}, u32[]{:S(2)}) copy-start(bf16[25,64,128]{2,1,0:T(8,128)(2,1)S(1)} %collective-permute-done.rest_4_) | copy-start | bytes 1228804
  12.6 15.3 %collective-permute-start.1 = (bf16[25,64,128]{2,1,0:T(8,128)(2,1)S(1)}, bf16[25,64,128]{2,1,0:T(8,128)(2,1)S(1)}, u32[]{:S(2)}, u32[]{:S(2)}) collective-permute-start(bf16[25,64,128]{2,1,0:T(8,128)(2,1)S(1)} %collective-permute-done.rest_4_), channel_id=1, source_target_pairs={{28,0},{0,4},{4,8},{8,12},{12,16},{16,20},{20,24},{24,28},{29,1},{... | collective-permute-start | bytes 1228808 | tf_op jit(solution)/shard_map/ppermute | solution.py:174
  16.7 35.5 %copy-start.1 = (bf16[25,64,128]{2,1,0:T(8,128)(2,1)}, bf16[25,64,128]{2,1,0:T(8,128)(2,1)S(1)}, u32[]{:S(2)}) copy-start(bf16[25,64,128]{2,1,0:T(8,128)(2,1)S(1)} %collective-permute-done.2.rest_12_) | copy-start | bytes 1228804
  16.7 13.7 %collective-permute-start.3 = (bf16[25,64,128]{2,1,0:T(8,128)(2,1)S(1)}, bf16[25,64,128]{2,1,0:T(8,128)(2,1)S(1)}, u32[]{:S(2)}, u32[]{:S(2)}) collective-permute-start(bf16[25,64,128]{2,1,0:T(8,128)(2,1)S(1)} %collective-permute-done.2.rest_12_), channel_id=1, source_target_pairs={{4,0},{8,4},{12,8},{16,12},{20,16},{24,20},{28,24},{0,28},{5,1},{9... | collective-permute-start | bytes 1228808 | tf_op jit(solution)/shard_map/ppermute | solution.py:174
  16.8 18.3 %collective-permute-start.14 = (bf16[25,64,128]{2,1,0:T(8,128)(2,1)}, bf16[25,64,128]{2,1,0:T(8,128)(2,1)S(1)}, u32[]{:S(2)}, u32[]{:S(2)}) collective-permute-start(bf16[25,64,128]{2,1,0:T(8,128)(2,1)} %collective-permute-done.13.rest_11_), channel_id=1, source_target_pairs={{0,4},{4,8},{8,12},{12,16},{16,20},{20,24},{24,28},{1,5},{5,9},{9,... | collective-permute-start | bytes 1228808 | tf_op jit(solution)/shard_map/ppermute | solution.py:174
  24.8 34.5 %collective-permute-start.18 = (bf16[25,64,128]{2,1,0:T(8,128)(2,1)}, bf16[25,64,128]{2,1,0:T(8,128)(2,1)}, u32[]{:S(2)}, u32[]{:S(2)}) collective-permute-start(bf16[25,64,128]{2,1,0:T(8,128)(2,1)} %collective-permute-done.13.rest_11_), channel_id=1, source_target_pairs={{4,0},{8,4},{12,8},{16,12},{20,16},{24,20},{28,24},{5,1},{9,5},{13... | collective-permute-start | bytes 1228808 | tf_op jit(solution)/shard_map/ppermute | solution.py:174
  27.9 33.4 %copy-start.2 = (bf16[25,64,128]{2,1,0:T(8,128)(2,1)}, bf16[25,64,128]{2,1,0:T(8,128)(2,1)S(1)}, u32[]{:S(2)}) copy-start(bf16[25,64,128]{2,1,0:T(8,128)(2,1)S(1)} %collective-permute-done.1.rest_0_) | copy-start | bytes 1228804
  27.9 33.4 %collective-permute-start.10 = (bf16[25,64,128]{2,1,0:T(8,128)(2,1)}, bf16[25,64,128]{2,1,0:T(8,128)(2,1)}, u32[]{:S(2)}, u32[]{:S(2)}) collective-permute-start(bf16[25,64,128]{2,1,0:T(8,128)(2,1)} %collective-permute-done.9.rest_10_), channel_id=1, source_target_pairs={{0,4},{4,8},{8,12},{12,16},{16,20},{20,24},{24,28},{1,5},{5,9},{9,... | collective-permute-start | bytes 1228808 | tf_op jit(solution)/shard_map/ppermute | solution.py:174
  30.4 31.6 %copy-start.3 = (bf16[25,64,128]{2,1,0:T(8,128)(2,1)}, bf16[25,64,128]{2,1,0:T(8,128)(2,1)S(1)}, u32[]{:S(2)}) copy-start(bf16[25,64,128]{2,1,0:T(8,128)(2,1)S(1)} %collective-permute-done.3.rest_16_) | copy-start | bytes 1228804
  31.5 39.3 %collective-permute-start.12 = (bf16[2,25,64,128]{3,2,1,0:T(8,128)(2,1)}, bf16[2,25,64,128]{3,2,1,0:T(8,128)(2,1)S(1)}, u32[]{:S(2)}, u32[]{:S(2)}) collective-permute-start(bf16[2,25,64,128]{3,2,1,0:T(8,128)(2,1)} %pad_maximum_fusion.1), channel_id=1, source_target_pairs={{0,3},{1,0},{2,1},{3,2},{4,7},{5,4},{6,5},{7,6},{24,27},{25,24},{2... | collective-permute-start | bytes 2457608 | tf_op jit(solution)/shard_map/ppermute | solution.py:193
  33.5 49.5 %collective-permute-start.8 = (bf16[2,25,64,128]{3,2,1,0:T(8,128)(2,1)}, bf16[2,25,64,128]{3,2,1,0:T(8,128)(2,1)}, u32[]{:S(2)}, u32[]{:S(2)}) collective-permute-start(bf16[2,25,64,128]{3,2,1,0:T(8,128)(2,1)} %pad_maximum_fusion.1), channel_id=1, source_target_pairs={{0,2},{1,3},{2,0},{3,1},{4,6},{5,7},{6,4},{7,5},{24,26},{25,27},{2... | collective-permute-start | bytes 2457608 | tf_op jit(solution)/shard_map/ppermute | solution.py:193
  35.1 39.3 %copy-start.7 = (bf16[25,64,128]{2,1,0:T(8,128)(2,1)}, bf16[25,64,128]{2,1,0:T(8,128)(2,1)S(1)}, u32[]{:S(2)}) copy-start(bf16[25,64,128]{2,1,0:T(8,128)(2,1)S(1)} %collective-permute-done.14.rest_7_) | copy-start | bytes 1228804
  52.2 12.0 %collective-permute-start.15 = (bf16[25,64,128]{2,1,0:T(8,128)(2,1)S(1)}, bf16[25,64,128]{2,1,0:T(8,128)(2,1)S(1)}, u32[]{:S(2)}, u32[]{:S(2)}) collective-permute-start(bf16[25,64,128]{2,1,0:T(8,128)(2,1)S(1)} %collective-permute-done.14.rest_7_), channel_id=1, source_target_pairs={{4,8},{8,12},{12,16},{16,20},{20,24},{24,28},{5,9},{9,13},{13,17},... | collective-permute-start | bytes 1228808 | tf_op jit(solution)/shard_map/ppermute | solution.py:174
  59.4 9.5 %collective-permute-start.21 = (bf16[25,64,128]{2,1,0:T(8,128)(2,1)}, bf16[25,64,128]{2,1,0:T(8,128)(2,1)S(1)}, u32[]{:S(2)}, u32[]{:S(2)}) collective-permute-start(bf16[25,64,128]{2,1,0:T(8,128)(2,1)} %collective-permute-done.18.rest_15_), channel_id=1, source_target_pairs={{4,0},{8,4},{12,8},{16,12},{20,16},{24,20},{5,1},{9,5},{13,9},{17,... | collective-permute-start | bytes 1228808 | tf_op jit(solution)/shard_map/ppermute | solution.py:174
  61.3 26.0 %collective-permute-start.4 = (bf16[2,25,64,128]{3,2,1,0:T(8,128)(2,1)}, bf16[2,25,64,128]{3,2,1,0:T(8,128)(2,1)S(1)}, u32[]{:S(2)}, u32[]{:S(2)}) collective-permute-start(bf16[2,25,64,128]{3,2,1,0:T(8,128)(2,1)} %pad_maximum_fusion.1), channel_id=1, source_target_pairs={{0,1},{1,2},{2,3},{3,0},{4,5},{5,6},{6,7},{7,4},{24,25},{25,26},{2... | collective-permute-start | bytes 2457608 | tf_op jit(solution)/shard_map/ppermute | solution.py:193
  64.2 30.2 %copy-start.8 = (bf16[25,64,128]{2,1,0:T(8,128)(2,1)}, bf16[25,64,128]{2,1,0:T(8,128)(2,1)S(1)}, u32[]{:S(2)}) copy-start(bf16[25,64,128]{2,1,0:T(8,128)(2,1)S(1)} %collective-permute-done.15.rest_3_) | copy-start | bytes 1228804
  64.2 10.9 %collective-permute-start.17 = (bf16[25,64,128]{2,1,0:T(8,128)(2,1)}, bf16[25,64,128]{2,1,0:T(8,128)(2,1)S(1)}, u32[]{:S(2)}, u32[]{:S(2)}) collective-permute-start(bf16[25,64,128]{2,1,0:T(8,128)(2,1)} %collective-permute-done.9.rest_10_), channel_id=1, source_target_pairs={{4,0},{8,4},{12,8},{16,12},{20,16},{24,20},{28,24},{5,1},{9,5},{13... | collective-permute-start | bytes 1228808 | tf_op jit(solution)/shard_map/ppermute | solution.py:174
  68.9 18.5 %copy-start.9 = (bf16[25,64,128]{2,1,0:T(8,128)(2,1)}, bf16[25,64,128]{2,1,0:T(8,128)(2,1)S(1)}, u32[]{:S(2)}) copy-start(bf16[25,64,128]{2,1,0:T(8,128)(2,1)S(1)} %collective-permute-done.21.rest_19_) | copy-start | bytes 1228804
  68.9 10.3 %collective-permute-start.16 = (bf16[25,64,128]{2,1,0:T(8,128)(2,1)}, bf16[25,64,128]{2,1,0:T(8,128)(2,1)S(1)}, u32[]{:S(2)}, u32[]{:S(2)}) collective-permute-start(bf16[25,64,128]{2,1,0:T(8,128)(2,1)} %collective-permute-done.5.rest_9_), channel_id=1, source_target_pairs={{4,0},{8,4},{12,8},{16,12},{20,16},{24,20},{28,24},{5,1},{9,5},{13... | collective-permute-start | bytes 1228808 | tf_op jit(solution)/shard_map/ppermute | solution.py:174
  70.8 23.7 %copy-start.5 = (bf16[2,25,64,128]{3,2,1,0:T(8,128)(2,1)}, bf16[2,25,64,128]{3,2,1,0:T(8,128)(2,1)S(1)}, u32[]{:S(2)}) copy-start(bf16[2,25,64,128]{3,2,1,0:T(8,128)(2,1)S(1)} %collective-permute-done.12.rest_22_) | copy-start | bytes 2457604
  70.8 10.3 %collective-permute-start.6 = (bf16[25,64,128]{2,1,0:T(8,128)(2,1)}, bf16[25,64,128]{2,1,0:T(8,128)(2,1)S(1)}, u32[]{:S(2)}, u32[]{:S(2)}) collective-permute-start(bf16[25,64,128]{2,1,0:T(8,128)(2,1)} %collective-permute-done.5.rest_9_), channel_id=1, source_target_pairs={{0,4},{4,8},{8,12},{12,16},{16,20},{20,24},{24,28},{1,5},{5,9},{9,... | collective-permute-start | bytes 1228808 | tf_op jit(solution)/shard_map/ppermute | solution.py:174
  75.2 19.3 %copy-start.10 = (bf16[25,64,128]{2,1,0:T(8,128)(2,1)}, bf16[25,64,128]{2,1,0:T(8,128)(2,1)S(1)}, u32[]{:S(2)}) copy-start(bf16[25,64,128]{2,1,0:T(8,128)(2,1)S(1)} %collective-permute-done.17.rest_14_) | copy-start | bytes 1228804
  75.2 12.2 %collective-permute-start.11 = (bf16[25,64,128]{2,1,0:T(8,128)(2,1)}, bf16[25,64,128]{2,1,0:T(8,128)(2,1)S(1)}, u32[]{:S(2)}, u32[]{:S(2)}) collective-permute-start(bf16[25,64,128]{2,1,0:T(8,128)(2,1)} %collective-permute-done.10.rest_6_), channel_id=1, source_target_pairs={{4,8},{8,12},{12,16},{16,20},{20,24},{24,28},{5,9},{9,13},{13,17},... | collective-permute-start | bytes 1228808 | tf_op jit(solution)/shard_map/ppermute | solution.py:174
  79.1 15.3 %copy-start.11 = (bf16[25,64,128]{2,1,0:T(8,128)(2,1)}, bf16[25,64,128]{2,1,0:T(8,128)(2,1)S(1)}, u32[]{:S(2)}) copy-start(bf16[25,64,128]{2,1,0:T(8,128)(2,1)S(1)} %collective-permute-done.16.rest_13_) | copy-start | bytes 1228804
  79.1 9.6 %collective-permute-start.20 = (bf16[25,64,128]{2,1,0:T(8,128)(2,1)S(1)}, bf16[25,64,128]{2,1,0:T(8,128)(2,1)S(1)}, u32[]{:S(2)}, u32[]{:S(2)}) collective-permute-start(bf16[25,64,128]{2,1,0:T(8,128)(2,1)S(1)} %collective-permute-done.17.rest_14_), channel_id=1, source_target_pairs={{4,0},{8,4},{12,8},{16,12},{20,16},{24,20},{5,1},{9,5},{13,9},{17,... | collective-permute-start | bytes 1228808 | tf_op jit(solution)/shard_map/ppermute | solution.py:174
  81.1 11.7 %copy-start.12 = (bf16[25,64,128]{2,1,0:T(8,128)(2,1)}, bf16[25,64,128]{2,1,0:T(8,128)(2,1)S(1)}, u32[]{:S(2)}) copy-start(bf16[25,64,128]{2,1,0:T(8,128)(2,1)S(1)} %collective-permute-done.6.rest_5_) | copy-start | bytes 1228804
  81.1 11.7 %collective-permute-start.19 = (bf16[25,64,128]{2,1,0:T(8,128)(2,1)S(1)}, bf16[25,64,128]{2,1,0:T(8,128)(2,1)S(1)}, u32[]{:S(2)}, u32[]{:S(2)}) collective-permute-start(bf16[25,64,128]{2,1,0:T(8,128)(2,1)S(1)} %collective-permute-done.16.rest_13_), channel_id=1, source_target_pairs={{4,0},{8,4},{12,8},{16,12},{20,16},{24,20},{5,1},{9,5},{13,9},{17,... | collective-permute-start | bytes 1228808 | tf_op jit(solution)/shard_map/ppermute | solution.py:174
  83.0 9.8 %collective-permute-start.7 = (bf16[25,64,128]{2,1,0:T(8,128)(2,1)S(1)}, bf16[25,64,128]{2,1,0:T(8,128)(2,1)S(1)}, u32[]{:S(2)}, u32[]{:S(2)}) collective-permute-start(bf16[25,64,128]{2,1,0:T(8,128)(2,1)S(1)} %collective-permute-done.6.rest_5_), channel_id=1, source_target_pairs={{4,8},{8,12},{12,16},{16,20},{20,24},{24,28},{5,9},{9,13},{13,17},... | collective-permute-start | bytes 1228808 | tf_op jit(solution)/shard_map/ppermute | solution.py:174
  87.4 7.1 %copy-start.6 = (bf16[2,25,64,128]{3,2,1,0:T(8,128)(2,1)}, bf16[2,25,64,128]{3,2,1,0:T(8,128)(2,1)S(1)}, u32[]{:S(2)}) copy-start(bf16[2,25,64,128]{3,2,1,0:T(8,128)(2,1)S(1)} %collective-permute-done.4.rest_20_) | copy-start | bytes 2457604
  87.4 7.0 %copy-start.13 = (bf16[25,64,128]{2,1,0:T(8,128)(2,1)}, bf16[25,64,128]{2,1,0:T(8,128)(2,1)S(1)}, u32[]{:S(2)}) copy-start(bf16[25,64,128]{2,1,0:T(8,128)(2,1)S(1)} %collective-permute-done.11.rest_2_) | copy-start | bytes 1228804
  88.7 4.1 %copy-start.14 = (bf16[25,64,128]{2,1,0:T(8,128)(2,1)}, bf16[25,64,128]{2,1,0:T(8,128)(2,1)S(1)}, u32[]{:S(2)}) copy-start(bf16[25,64,128]{2,1,0:T(8,128)(2,1)S(1)} %collective-permute-done.20.rest_18_) | copy-start | bytes 1228804
  92.8 0.8 copy-start.15
  92.8 0.9 copy-start.16
  117.4 8.4 %collective-permute-start.22 = (bf16[8,2,64,128]{3,2,1,0:T(8,128)(2,1)S(1)}, bf16[8,2,64,128]{3,2,1,0:T(8,128)(2,1)S(1)}, u32[]{:S(2)}, u32[]{:S(2)}) collective-permute-start(bf16[8,2,64,128]{3,2,1,0:T(8,128)(2,1)S(1)} %get-tuple-element.33), channel_id=1, source_target_pairs={{0,1},{1,2},{2,3},{3,0},{4,5},{5,6},{6,7},{7,4},{8,9},{9,10},{10,1... | collective-permute-start | bytes 786440 | tf_op jit(solution)/shard_map/ppermute | solution.py:253
  118.6 12.3 %collective-permute-start.23 = (bf16[8,2,64,128]{3,2,1,0:T(8,128)(2,1)S(1)}, bf16[8,2,64,128]{3,2,1,0:T(8,128)(2,1)S(1)}, u32[]{:S(2)}, u32[]{:S(2)}) collective-permute-start(bf16[8,2,64,128]{3,2,1,0:T(8,128)(2,1)S(1)} %get-tuple-element.35), channel_id=1, source_target_pairs={{0,2},{1,3},{2,0},{3,1},{4,6},{5,7},{6,4},{7,5},{8,10},{9,11},{10,... | collective-permute-start | bytes 786440 | tf_op jit(solution)/shard_map/ppermute | solution.py:253
  118.8 12.0 %collective-permute-start.24 = (bf16[8,2,64,128]{3,2,1,0:T(8,128)(2,1)S(1)}, bf16[8,2,64,128]{3,2,1,0:T(8,128)(2,1)S(1)}, u32[]{:S(2)}, u32[]{:S(2)}) collective-permute-start(bf16[8,2,64,128]{3,2,1,0:T(8,128)(2,1)S(1)} %get-tuple-element.34), channel_id=1, source_target_pairs={{0,3},{1,0},{2,1},{3,2},{4,7},{5,4},{6,5},{7,6},{8,11},{9,8},{10,9... | collective-permute-start | bytes 786440 | tf_op jit(solution)/shard_map/ppermute | solution.py:253
